TPU v7x, 32 devices: a whole 2x2x4 slice. The times are simulated.
32 devices in a mesh: groups: 2 (over x), seq: 16 (over z, y, core).
Axes of the slice: x: 2, y: 2, z: 4, core: 2. Of those that a mesh axis runs over, the one named last changes fastest.
Arguments:
- query: bfloat16 [4096, 1024], P(('groups', 'seq')), parts along dimension 0, as said below
- keys: bfloat16 [4096, 1024], P(('groups', 'seq')), parts along dimension 0, as said below
- values: bfloat16 [4096, 1024], P(('groups', 'seq')), parts along dimension 0, may hold values from -6 to 6
- out_weight: bfloat16 [1024, 2048], P('seq'), may hold values from -0.1875 to 0.1875
- grad_out: bfloat16 [4096, 2048], P(('groups', 'seq')), parts along dimension 0, may hold values from -6 to 6
- global_blocks: int32 [4], P('groups'), parts along dimension 0, may hold values from 0 to 15
- random_blocks: int32 [32, 3], P(('groups', 'seq')), parts along dimension 0, may hold values from 0 to 15, as said below
Outputs:
- layer_out: bfloat16 [4096, 2048], P(('groups', 'seq')), parts along dimension 0
- grad_query: bfloat16 [4096, 1024], P(('groups', 'seq')), parts along dimension 0
- grad_keys: bfloat16 [4096, 1024], P(('groups', 'seq')), parts along dimension 0
- grad_values: bfloat16 [4096, 1024], P(('groups', 'seq')), parts along dimension 0
- grad_weight: float32 [2048, 2048], P(('groups', 'seq')), parts along dimension 0
There are 2 independent parts, one for each index of `groups`. A program takes and returns all parts, laid end to end along the dimension named above; an argument that names none is the same for every part. Nothing has to cross between parts.
Inputs may be any that keep to these rules, and one draw needn't show every extreme that they name: `random_blocks`: random block r of query block b lies on the device that holds b or on a device beside it: it is at least max(b - 1, 0) * 1 and below min(b + 2, 16). `query`: entries lie between -12 and 12. `keys`: entries lie between -6 and 6.
All inputs are finite; a program needn't handle non-finite values.
Results may differ from a plain program's by a relative error of at most 0.012.
Values may be sent and summed in bfloat16 or wider, within the bound.
No kernel may reach another device: no remote copies, remote signals or barrier semaphores. Data moves between devices by JAX's collectives and lax.ppermute only.
A program may use at most 128 MiB of HBM per device.

v0:
```python
import math

import jax
import jax.numpy as jnp
from jax import lax
from jax.sharding import PartitionSpec as P

H = 8
BLK = 128


NEG_FILL = -1e30


def extended_2(shard, sides, width):
    for axis, dim in sides:
        count, length = (lax.axis_size(axis), shard.shape[dim])
        up = [(i, (i + 1) % count) for i in range(count - 1)]
        down = [(j, i) for i, j in up]
        last = lax.slice_in_dim(shard, length - width, length, axis=dim)
        initial = lax.slice_in_dim(shard, 0, width, axis=dim)
        before = lax.ppermute(last, axis, up)
        after = lax.ppermute(initial, axis, down)
        shard = jnp.concatenate([before, shard, after], axis=dim)
    return shard


def spread(shard, axis, root):
    mine = lax.axis_index(axis) == root
    return lax.psum(jnp.where(mine, shard, jnp.zeros_like(shard)), axis)


def window_and_random(random_rows, device, blocks_dev, total_blocks):
    local_ids = jnp.arange(blocks_dev, dtype=jnp.int32)
    global_ids = device * blocks_dev + local_ids
    offsets = jnp.array([-1, 0, 1], dtype=jnp.int32)
    neighbour_ids = global_ids[:, None] + offsets[None, :]
    window_index = local_ids[:, None] + blocks_dev + offsets[None, :]
    window_live = (neighbour_ids >= 0) & (neighbour_ids < total_blocks)
    random_index = random_rows - (device - 1) * blocks_dev
    ext_index = jnp.concatenate([window_index, random_index], axis=1)
    live_local = jnp.concatenate(
        [window_live, jnp.ones(random_rows.shape, dtype=jnp.bool_)], axis=1
    )
    return (ext_index, live_local)


def choose_blocks(extended, global_kv, ext_index, live_local, blocks_dev):
    feature_count = extended.shape[2]
    ext_blocks = extended.reshape(2, 3 * blocks_dev, BLK, feature_count)
    local_sel = jnp.take(ext_blocks, ext_index, axis=1)
    global_count = global_kv.shape[0]
    global_sel = jnp.swapaxes(global_kv, 0, 1)[:, None]
    chosen = jnp.concatenate([local_sel, global_sel], axis=2)
    listed = chosen.shape[2]
    chosen = chosen.reshape(2, blocks_dev, listed * BLK, H, feature_count // H)
    live = jnp.concatenate(
        [live_local, jnp.ones((blocks_dev, global_count), dtype=jnp.bool_)], axis=1
    )
    live_rows = jnp.repeat(live, BLK, axis=1)
    return (chosen[0], chosen[1], live_rows)


def attend_blocks(query_blocks, chosen_keys, chosen_values, live_rows):
    score_scale = 1.0 / math.sqrt(query_blocks.shape[-1])
    scores = (
        jnp.einsum("qihd,qjhd->qhij", query_blocks, chosen_keys, preferred_element_type=jnp.float32)
        * score_scale
    )
    scores = jnp.where(live_rows[:, None, None, :], scores, NEG_FILL)
    row_top = jnp.max(scores, axis=-1, keepdims=True)
    raised = jnp.exp(scores - row_top)
    soft_weights = raised / jnp.sum(raised, axis=-1, keepdims=True)
    rounded_weights = soft_weights.astype(jnp.bfloat16)
    mixed_out = jnp.einsum(
        "qhij,qjhd->qihd", rounded_weights, chosen_values, preferred_element_type=jnp.float32
    )
    return (soft_weights, rounded_weights, mixed_out.astype(jnp.bfloat16))


def attend_backward(
    query_blocks, chosen_keys, chosen_values, soft_weights, rounded_weights, upstream_blocks
):
    score_scale = 1.0 / math.sqrt(query_blocks.shape[-1])
    grad_chosen_values = jnp.einsum(
        "qhij,qihd->qjhd", rounded_weights, upstream_blocks, preferred_element_type=jnp.float32
    )
    grad_weights = jnp.einsum(
        "qihd,qjhd->qhij", upstream_blocks, chosen_values, preferred_element_type=jnp.float32
    )
    row_delta = jnp.sum(soft_weights * grad_weights, axis=-1, keepdims=True)
    grad_scores = (score_scale * soft_weights * (grad_weights - row_delta)).astype(jnp.bfloat16)
    grad_query_blocks = jnp.einsum(
        "qhij,qjhd->qihd", grad_scores, chosen_keys, preferred_element_type=jnp.float32
    )
    grad_chosen_keys = jnp.einsum(
        "qhij,qihd->qjhd", grad_scores, query_blocks, preferred_element_type=jnp.float32
    )
    return (grad_query_blocks, grad_chosen_keys, grad_chosen_values)


def fold_gradients(grad_chosen_keys, grad_chosen_values, ext_index, blocks_dev):
    stacked = jnp.stack([grad_chosen_keys, grad_chosen_values])
    listed_local = ext_index.shape[1]
    feature_count = stacked.shape[3] * stacked.shape[4]
    stacked = stacked.reshape(2, blocks_dev, -1, BLK * feature_count)
    local_part = stacked[:, :, :listed_local].reshape(
        2, blocks_dev * listed_local, BLK * feature_count
    )
    one_hot = (
        ext_index.reshape(-1)[:, None] == jnp.arange(3 * blocks_dev, dtype=jnp.int32)[None, :]
    ).astype(jnp.float32)
    grad_ext = jnp.einsum("sj,ksx->kjx", one_hot, local_part, precision=lax.Precision.HIGHEST)
    grad_ext = grad_ext.reshape(2, 3 * blocks_dev * BLK, feature_count)
    grad_global = jnp.sum(stacked[:, :, listed_local:], axis=1).reshape(2, -1, BLK, feature_count)
    return (grad_ext, grad_global)


def local(query, keys, values, out_weight, grad_out, global_blocks, random_blocks):
    tok_rows = query.shape[0]
    feature_count = query.shape[1]
    blocks_dev = tok_rows // BLK
    device = lax.axis_index("seq")
    total_blocks = blocks_dev * lax.axis_size("seq")
    paired = jnp.stack([keys, values])
    extended = extended_2(paired, (("seq", 1),), tok_rows)
    fetched = []
    for global_slot in range(global_blocks.shape[0]):
        block_id = global_blocks[global_slot]
        owner_index = block_id // blocks_dev
        fetched.append(spread(paired, "seq", owner_index))
    global_kv = jnp.stack(fetched)
    ext_index, live_local = window_and_random(random_blocks, device, blocks_dev, total_blocks)
    chosen_keys, chosen_values, live_rows = choose_blocks(
        extended, global_kv, ext_index, live_local, blocks_dev
    )
    query_blocks = query.reshape(blocks_dev, BLK, H, feature_count // H)
    soft_weights, rounded_weights, mixed_out = attend_blocks(
        query_blocks, chosen_keys, chosen_values, live_rows
    )
    attn_out = mixed_out.reshape(tok_rows, feature_count)
    columns = attn_out
    layer_sum = jnp.dot(
        columns,
        lax.all_gather(out_weight, "seq", axis=0, tiled=True),
        preferred_element_type=jnp.float32,
    )
    upstream_sum = lax.dot_general(
        grad_out,
        lax.all_gather(out_weight, "seq", axis=0, tiled=True),
        (((1,), (1,)), ((), ())),
        preferred_element_type=jnp.float32,
    )
    layer_out = layer_sum.astype(jnp.bfloat16)
    upstream_blocks = upstream_sum.astype(jnp.bfloat16).reshape(
        blocks_dev, BLK, H, feature_count // H
    )
    columns = attn_out
    grad_weight = lax.psum_scatter(
        lax.dot_general(
            columns, grad_out, (((0,), (0,)), ((), ())), preferred_element_type=jnp.float32
        ),
        "seq",
        scatter_dimension=0,
        tiled=True,
    )
    grad_query_blocks, grad_chosen_keys, grad_chosen_values = attend_backward(
        query_blocks, chosen_keys, chosen_values, soft_weights, rounded_weights, upstream_blocks
    )
    grad_ext, grad_global = fold_gradients(
        grad_chosen_keys, grad_chosen_values, ext_index, blocks_dev
    )
    rim_grads = jnp.concatenate(
        [grad_ext[:, :tok_rows], grad_ext[:, 2 * tok_rows :]], axis=1
    ).astype(jnp.bfloat16)
    arrived = extended_2(rim_grads, (("seq", 1),), tok_rows)
    global_total = lax.psum(grad_global, "seq")
    owned_mask = (
        global_blocks[:, None]
        == device * blocks_dev + jnp.arange(blocks_dev, dtype=jnp.int32)[None, :]
    ).astype(jnp.float32)
    owned_sum = jnp.einsum(
        "gj,kgx->kjx",
        owned_mask,
        global_total.reshape(2, owned_mask.shape[0], -1),
        precision=lax.Precision.HIGHEST,
    )
    grad_paired = grad_ext[:, tok_rows : 2 * tok_rows] + arrived[:, :tok_rows].astype(jnp.float32)
    grad_paired = grad_paired + arrived[:, 3 * tok_rows :].astype(jnp.float32)
    grad_paired = grad_paired + owned_sum.reshape(2, tok_rows, feature_count)
    grad_paired = grad_paired.astype(jnp.bfloat16)
    grad_query = grad_query_blocks.reshape(tok_rows, feature_count).astype(jnp.bfloat16)
    return (layer_out, grad_query, grad_paired[0], grad_paired[1], grad_weight)


def solution(mesh):
    placed = (
        P(("groups", "seq"), None),
        P(("groups", "seq"), None),
        P(("groups", "seq"), None),
        P("seq", None),
        P(("groups", "seq"), None),
        P("groups"),
        P(("groups", "seq"), None),
    )
    return jax.shard_map(
        local,
        mesh=mesh,
        in_specs=placed,
        out_specs=(
            P(("groups", "seq"), None),
            P(("groups", "seq"), None),
            P(("groups", "seq"), None),
            P(("groups", "seq"), None),
            P(("groups", "seq"), None),
        ),
        check_vma=False,
    )
```

profile of v0, /device:TPU:11, one launch (start us, length us, event | category | flops | bytes accessed | tf_op | source)
XLA Modules:
  0.0 427.6 jit_solution(10546698557166395422)
XLA Ops:
  7.3 1.4 fusion.36
  10.0 2.1 select_bitcast_fusion.1
  12.1 0.7 all-gather.2.cloned.1.call-update
  12.9 2.6 collective-permute-start.1
  15.5 3.0 collective-permute-start
  18.9 12.4 %collective-permute-done.1 = bf16[2,128,1024]{2,1,0:T(8,128)(2,1)S(1)} collective-permute-done((bf16[2,128,1024]{2,1,0:T(8,128)(2,1)S(1)}, bf16[2,128,1024]{2,1,0:T(8,128)(2,1)S(1)}, u32[]{:S(2)}, u32[]{:S(2)}) %collective-permute-start.1) | collective-permute-done | bytes 524320 | tf_op jit(solution)/shard_map/ppermute | solution.py:23
  31.3 1.2 pad_maximum_fusion.2
  32.5 2.5 gather_fusion
  35.0 74.2 %all-reduce.6.cloned.1.call-done = (bf16[1,2,128,1024]{3,2,1,0:T(8,128)(2,1)}, bf16[1,2,128,1024]{3,2,1,0:T(8,128)(2,1)}) async-done(((bf16[1,2,128,1024]{3,2,1,0:T(8,128)(2,1)}, bf16[1,2,128,1024]{3,2,1,0:T(8,128)(2,1)}), (bf16[1,2,128,1024]{3,2,1,0:T(8,128)(2,1)}, bf16[1,2,128,1024]{3,2,1,0:T(8,128)(2,1)})) %all-reduce.6.cloned.1.call-update) | async-done | bytes 1048592 | tf_op jit(solution)/shard_map/psum | solution.py:30
  109.2 1.3 maximum_bitcast_fusion.2
  110.5 2.3 bitcast_select_fusion
  112.7 1.6 pad_maximum_fusion.1
  114.3 0.6 copy.57
  114.9 3.0 copy.52
  117.9 3.5 copy.58
  121.5 3.3 copy.34
  124.8 0.8 fusion.22
  125.6 3.4 fusion.37
  129.0 33.9 %all-gather.2.cloned.1.call-done = bf16[1024,2048]{1,0:T(8,128)(2,1)} async-done(((bf16[64,2048]{1,0:T(8,128)(2,1)}), bf16[1024,2048]{1,0:T(8,128)(2,1)}) %all-gather.2.cloned.1.call-update) | async-done | bytes 4194320 | tf_op jit(solution)/shard_map/all_gather | solution.py:145
  162.9 3.7 convolution_convert_fusion.3
  166.8 5.0 %convolution_bitcast_fusion.1 = f32[1,1024,8,128]{1,3,2,0:T(8,128)} fusion(bf16[128,8,128]{0,2,1:T(8,128)(2,1)S(1)} %bitcast.154, f32[8,128,1024]{1,2,0:T(8,128)} %get-tuple-element.29, f32[8,128]{1,0:T(8,128)S(1)} %get-tuple-element.28), kind=kOutput, calls=%fused_computation.19 | convolution fusion | flops 270532608 | bytes 8654848 | tf_op jit(solution)/shard_map/qhij,qihd->qjhd/dot_general | solution.py:85
  171.8 3.1 multiply_reduce_fusion
  174.9 5.4 %copy.40 = f32[1,1024,8,128]{3,2,1,0:T(8,128)} copy(f32[1,1024,8,128]{1,3,2,0:T(8,128)} %convolution_bitcast_fusion.1) | data formatting | bytes 8388608 | tf_op jit(solution)/shard_map/qhij,qihd->qjhd/transpose | solution.py:85
  180.2 4.9 %stack.34 = f32[1,1,8,131072]{3,2,1,0:T(8,128)} reshape(f32[1,1024,8,128]{3,2,1,0:T(8,128)} %copy.40) | data formatting | bytes 8388608 | tf_op jit(solution)/shard_map/stack | solution.py:103
  185.1 4.2 multiply_convert_fusion
  189.3 0.7 convolution_bitcast_fusion.2
  190.0 0.6 copy-done.1
  190.6 4.4 %copy.37 = f32[1,1024,8,128]{3,2,1,0:T(8,128)} copy(f32[1,1024,8,128]{3,1,2,0:T(8,128)S(1)} %convolution_bitcast_fusion.2) | data formatting | bytes 8388608 | tf_op jit(solution)/shard_map/qhij,qihd->qjhd/transpose | solution.py:96
  195.0 4.9 %stack.33 = f32[1,1,8,131072]{3,2,1,0:T(8,128)} reshape(f32[1,1024,8,128]{3,2,1,0:T(8,128)} %copy.37) | data formatting | bytes 8388608 | tf_op jit(solution)/shard_map/stack | solution.py:103
  199.9 5.7 %fusion.10 = f32[2,131072,2]{1,2,0:T(2,128)} fusion(f32[1,1,8,131072]{3,2,0,1:T(8,128)} %bitcast.138, f32[1,1,8,131072]{3,2,0,1:T(8,128)} %bitcast.140), kind=kLoop, calls=%fused_computation.23 | loop fusion | flops 524288 | bytes 10485760 | tf_op jit(solution)/shard_map/gj,kgx->kjx/dot_general | solution.py:182
  205.6 4.0 dot_general.56
  209.7 0.3 reduce-scatter.2.cloned.1.call-start
  209.9 3.5 convolution_convert_fusion.2
  213.5 4.5 %fusion.38 = f32[1024,2048]{1,0:T(8,128)} fusion(bf16[128,1024]{0,1:T(8,128)(2,1)S(1)} %bitcast.147, bf16[128,2048]{1,0:T(8,128)(2,1)S(1)} %copy-done), kind=kOutput, calls=%fused_computation.75 | convolution fusion | flops 536870912 | bytes 9175040 | tf_op jit(solution)/shard_map/dot_general | solution.py:160
  218.0 0.6 copy-done.10
  218.7 2.3 convolution_convert_fusion.1
  221.0 0.9 copy.43
  221.8 9.8 %convolution_bitcast_fusion = f32[2,3,131072]{2,1,0:T(4,128)} fusion(f32[1,1,8,131072]{3,2,0,1:T(8,128)} %bitcast.139, f32[1,1,8,131072]{3,2,0,1:T(8,128)} %bitcast.141, s32[6]{0:T(128)S(1)} %add_bitcast_fusion), kind=kOutput, calls=%fused_computation.2 | convolution fusion | flops 58195984 | bytes 11534360 | tf_op jit(solution)/shard_map/sj,ksx->kjx/dot_general | solution.py:113
  231.6 5.1 %reshape.362 = f32[2,384,1024]{2,1,0:T(8,128)} reshape(f32[2,3,131072]{2,1,0:T(4,128)} %convolution_bitcast_fusion) | data formatting | bytes 6291456 | tf_op jit(solution)/shard_map/reshape | solution.py:114
  236.7 2.3 convert.6
  239.1 2.2 collective-permute-start.3
  241.3 3.7 collective-permute-start.2
  245.0 1.5 convolution_convert_fusion
  246.5 64.4 %all-reduce.4.cloned.1.call-done = f32[2,128,1024,2]{2,1,3,0:T(8,128)} async-done(((f32[2,128,1024,2]{2,1,3,0:T(8,128)}), f32[2,128,1024,2]{2,1,3,0:T(8,128)}) %all-reduce.4.cloned.1.call-update) | async-done | bytes 2097168 | tf_op jit(solution)/shard_map/psum | solution.py:177
  310.9 6.6 %fusion.13 = f32[1,2,128,1024]{3,0,2,1:T(1,128)S(1)} fusion(f32[2,128,1024,2]{2,1,3,0:T(8,128)} %all-reduce.4.cloned.1.call-done, s32[2]{0:T(128)S(1)} %copy-done.8, s32[]{:T(128)S(6)} %axis_index.8), kind=kOutput, calls=%fused_computation.28 | convolution fusion | flops 6291458 | bytes 3145740 | tf_op jit(solution)/shard_map/gj,kgx->kjx/dot_general | solution.py:182
  317.5 1.7 fusion.18
  319.2 0.8 slice_bitcast_fusion
  320.0 101.1 %reduce-scatter.2.cloned.1.call-done = f32[64,2048]{1,0:T(8,128)} async-done(((f32[1024,2048]{1,0:T(8,128)}), f32[64,2048]{1,0:T(8,128)}) %reduce-scatter.2.cloned.1.call-update) | async-done | bytes 524304 | tf_op jit(solution)/shard_map/reduce_scatter | solution.py:159
  (48 shorter events, 0.9 us)
Async XLA Ops:
  7.2 155.7 %copy-start = (bf16[128,2048]{1,0:T(8,128)(2,1)S(1)}, bf16[128,2048]{1,0:T(8,128)(2,1)}, u32[]{:S(2)}) copy-start(bf16[128,2048]{1,0:T(8,128)(2,1)} %param.12) | copy-start | bytes 1572868
  7.2 11.4 %copy-start.12 = (s32[1,3,1]{1,2,0:T(1,128)S(1)}, s32[1,3,1]{1,2,0:T(1,128)}, u32[]{:S(2)}) copy-start(s32[1,3,1]{1,2,0:T(1,128)} %constant.63) | copy-start | bytes 40
  7.2 11.4 %copy-start.11 = (s32[3]{0:T(128)S(1)}, s32[3]{0:T(128)}, u32[]{:S(2)}) copy-start(s32[3]{0:T(128)} %constant.60.clone) | copy-start | bytes 40
  7.2 24.1 %copy-start.6 = (bf16[128,1024]{1,0:T(8,128)(2,1)S(1)}, bf16[128,1024]{1,0:T(8,128)(2,1)}, u32[]{:S(2)}) copy-start(bf16[128,1024]{1,0:T(8,128)(2,1)} %param.10) | copy-start | bytes 786436
  7.2 24.1 %copy-start.7 = (bf16[128,1024]{1,0:T(8,128)(2,1)S(1)}, bf16[128,1024]{1,0:T(8,128)(2,1)}, u32[]{:S(2)}) copy-start(bf16[128,1024]{1,0:T(8,128)(2,1)} %param.9) | copy-start | bytes 786436
  7.2 11.3 %copy-start.9 = (s32[1,3]{1,0:T(1,128)S(1)}, s32[1,3]{1,0:T(1,128)}, u32[]{:S(2)}) copy-start(s32[1,3]{1,0:T(1,128)} %param.14) | copy-start | bytes 40
  7.2 101.9 %all-reduce.6.cloned.1.call-start = ((), (), s32[]{:S(2)}) async-start(), calls=%async_computation.4 | async-start | bytes 2097152 | tf_op jit(solution)/shard_map/psum | solution.py:30
  12.1 150.8 %all-gather.2.cloned.1.call-start = ((), (), s32[]{:S(2)}) async-start(), calls=%async_computation.1 | async-start | bytes 4456448 | tf_op jit(solution)/shard_map/all_gather | solution.py:145
  12.8 298.1 %all-reduce.4.cloned.1.call-start = ((), (), s32[]{:S(2)}) async-start(), calls=%async_computation.2 | async-start | bytes 4194304 | tf_op jit(solution)/shard_map/psum | solution.py:177
  12.9 18.4 %collective-permute-start.1 = (bf16[2,128,1024]{2,1,0:T(8,128)(2,1)S(1)}, bf16[2,128,1024]{2,1,0:T(8,128)(2,1)S(1)}, u32[]{:S(2)}, u32[]{:S(2)}) collective-permute-start(bf16[2,128,1024]{2,1,0:T(8,128)(2,1)S(1)} %get-tuple-element.25), channel_id=1, source_target_pairs={{1,0},{2,1},{3,2},{4,3},{5,4},{6,5},{7,6},{8,7},{9,8},{10,9},{11,1... | collective-permute-start | bytes 1572872 | tf_op jit(solution)/shard_map/ppermute | solution.py:23
  15.5 15.8 %collective-permute-start = (bf16[2,128,1024]{2,1,0:T(8,128)(2,1)S(1)}, bf16[2,128,1024]{2,1,0:T(8,128)(2,1)}, u32[]{:S(2)}, u32[]{:S(2)}) collective-permute-start(bf16[2,128,1024]{2,1,0:T(8,128)(2,1)S(1)} %get-tuple-element.25), channel_id=1, source_target_pairs={{0,1},{1,2},{2,3},{3,4},{4,5},{5,6},{6,7},{7,8},{8,9},{9,10},{10,1... | collective-permute-start | bytes 1572872 | tf_op jit(solution)/shard_map/ppermute | solution.py:22
  121.5 3.3 copy-start.5
  166.8 5.0 %copy-start.3 = (f32[8,128,1024]{1,2,0:T(8,128)S(1)}, f32[8,128,1024]{1,2,0:T(8,128)}, u32[]{:S(2)}) copy-start(f32[8,128,1024]{1,2,0:T(8,128)} %get-tuple-element.29) | copy-start | bytes 12582916
  166.8 5.0 %copy-start.4 = (bf16[1024,8,128]{0,2,1:T(8,128)(2,1)S(1)}, bf16[1024,8,128]{0,2,1:T(8,128)(2,1)}, u32[]{:S(2)}) copy-start(bf16[1024,8,128]{0,2,1:T(8,128)(2,1)} %copy.52) | copy-start | bytes 6291460
  189.2 1.4 copy-start.1
  209.7 211.4 %reduce-scatter.2.cloned.1.call-start = ((), (), s32[]{:S(2)}) async-start(), calls=%async_computation.3 | async-start | bytes 8912896 | tf_op jit(solution)/shard_map/reduce_scatter | solution.py:159
  217.9 0.7 copy-start.10
  236.7 8.2 %copy-start.2 = (bf16[1024,2048]{1,0:T(8,128)(2,1)S(1)}, bf16[1024,2048]{1,0:T(8,128)(2,1)}, u32[]{:S(2)}) copy-start(bf16[1024,2048]{1,0:T(8,128)(2,1)} %all-gather.2.cloned.1.call-done) | copy-start | bytes 12582916
  239.0 71.9 %copy-start.8 = (s32[2]{0:T(128)S(1)}, s32[2]{0:T(128)}, u32[]{:S(2)}) copy-start(s32[2]{0:T(128)} %param.13) | copy-start | bytes 28
  239.1 78.4 %collective-permute-start.3 = (bf16[2,128,1024]{2,1,0:T(8,128)(2,1)S(1)}, bf16[2,128,1024]{2,1,0:T(8,128)(2,1)S(1)}, u32[]{:S(2)}, u32[]{:S(2)}) collective-permute-start(bf16[2,128,1024]{2,1,0:T(8,128)(2,1)S(1)} %get-tuple-element.20), channel_id=1, source_target_pairs={{1,0},{2,1},{3,2},{4,3},{5,4},{6,5},{7,6},{8,7},{9,8},{10,9},{11,1... | collective-permute-start | bytes 1572872 | tf_op jit(solution)/shard_map/ppermute | solution.py:23
  241.3 76.2 %collective-permute-start.2 = (bf16[2,128,1024]{2,1,0:T(8,128)(2,1)S(1)}, bf16[2,128,1024]{2,1,0:T(8,128)(2,1)S(1)}, u32[]{:S(2)}, u32[]{:S(2)}) collective-permute-start(bf16[2,128,1024]{2,1,0:T(8,128)(2,1)S(1)} %get-tuple-element.19), channel_id=1, source_target_pairs={{0,1},{1,2},{2,3},{3,4},{4,5},{5,6},{6,7},{7,8},{8,9},{9,10},{10,1... | collective-permute-start | bytes 1572872 | tf_op jit(solution)/shard_map/ppermute | solution.py:22
Sparse Core Ops, SparseCore 0:
  12.2 96.9 all-reduce.5
  111.3 51.5 all-gather.1
  209.8 101.0 all-reduce.3
  315.9 105.1 reduce-scatter.1
where the time goes:
time: 430 us; the launch traced here: 428 us
  waiting for transfers between devices  287 us (67%)
  local copies, waits for them, and re-layouts  46.4 us (11%)
  matrix products  41.4 us (10%)
  other arithmetic  26 us (6%)
  between operations  15.4 us (4%)
  starting transfers between devices  11.8 us (3%)
    reduce_scatter x1, waiting for transfers between devices, local(): lax.psum_scatter(lax.dot_general(columns, grad_out, (((0,), (0,)), ((), (...  101 us
    psum x1, waiting for transfers between devices, spread(): return lax.psum(jnp.where(mine, shard, jnp.zeros_like(shard)), axis)  74.2 us
    psum x1, waiting for transfers between devices, local(): global_total = lax.psum(grad_global, 'seq')  64.4 us
    all_gather x1, waiting for transfers between devices, local(): lax.all_gather(out_weight, 'seq', axis=0, tiled=True)  33.9 us
    ppermute x2, waiting for transfers between devices, extended_2(): after = lax.ppermute(initial, axis, down)  12.4 us
    dot_general x1, matrix products, fold_gradients(): jnp.einsum('sj,ksx->kjx', one_hot, local_part, precision=lax.Precision.HI...  9.76 us
    another operation x2, local copies, waits for them, and re-layouts, fold_gradients(): stacked = jnp.stack([grad_chosen_keys, grad_chosen_values])  9.74 us
  transfers between devices with their start and end apart: 8, of which 5 were waited for; matrix products, arithmetic and copies ran while one was open for 15% of the time, Pallas kernels for 0%

commit v1 on v0

v1 whole, which is shorter than its diff:
```python
import math

import jax
import jax.numpy as jnp
from jax import lax
from jax.sharding import Mesh
from jax.sharding import PartitionSpec as P

H = 8
BLK = 128
SEQ = ("chip", "core")


NEG_FILL = -1e30


def flat_index():
    return lax.axis_index("chip") * lax.axis_size("core") + lax.axis_index("core")


def xor_swap(x, level):
    if level == 0:
        n = lax.axis_size("core")
        return lax.ppermute(x, "core", [(i, i ^ 1) for i in range(n)])
    n = lax.axis_size("chip")
    m = 1 << (level - 1)
    return lax.ppermute(x, "chip", [(i, i ^ m) for i in range(n)])


def butterfly_sum(x):
    count = lax.axis_size("chip") * lax.axis_size("core")
    levels = count.bit_length() - 1
    shape = x.shape
    flat = x.reshape(count, -1)
    d = flat_index()
    parts = flat
    for k in range(levels):
        half = parts.shape[0] // 2
        lo, hi = parts[:half], parts[half:]
        upper = ((d >> k) & 1) == 1
        send = jnp.where(upper, lo, hi)
        keep = jnp.where(upper, hi, lo)
        parts = keep + xor_swap(send, k)
    for k in reversed(range(levels)):
        upper = ((d >> k) & 1) == 1
        other = xor_swap(parts, k)
        parts = jnp.where(
            upper, jnp.concatenate([other, parts]), jnp.concatenate([parts, other])
        )
    return parts.reshape(shape)


def halo(shard):
    count = lax.axis_size("chip") * lax.axis_size("core")
    up = [(i, i + 1) for i in range(count - 1)]
    down = [(j, i) for i, j in up]
    before = lax.ppermute(shard, SEQ, up)
    after = lax.ppermute(shard, SEQ, down)
    return before, after


def attend(q, k, v, live, up):
    scale = 1.0 / math.sqrt(q.shape[-1])
    scores = jnp.einsum("ihd,jhd->hij", q, k, preferred_element_type=jnp.float32) * scale
    scores = jnp.where(live[None, None, :], scores, NEG_FILL)
    top = jnp.max(scores, axis=-1, keepdims=True)
    raised = jnp.exp(scores - top)
    probs = raised / jnp.sum(raised, axis=-1, keepdims=True)
    probs_b = probs.astype(jnp.bfloat16)
    attn = jnp.einsum("hij,jhd->ihd", probs_b, v, preferred_element_type=jnp.float32)
    attn = attn.astype(jnp.bfloat16)
    return probs, probs_b, attn


def attend_back(q, k, v, probs, probs_b, up):
    scale = 1.0 / math.sqrt(q.shape[-1])
    dv = jnp.einsum("hij,ihd->jhd", probs_b, up, preferred_element_type=jnp.float32)
    dprobs = jnp.einsum("ihd,jhd->hij", up, v, preferred_element_type=jnp.float32)
    rowdot = jnp.sum(probs * dprobs, axis=-1, keepdims=True)
    dscores = (scale * probs * (dprobs - rowdot)).astype(jnp.bfloat16)
    dq = jnp.einsum("hij,jhd->ihd", dscores, k, preferred_element_type=jnp.float32)
    dk = jnp.einsum("hij,ihd->jhd", dscores, q, preferred_element_type=jnp.float32)
    return dq, dk, dv


def local(query, keys, values, out_weight, grad_out, global_blocks, random_blocks):
    tok_rows, feature_count = query.shape
    hd = feature_count // H
    blocks_dev = tok_rows // BLK
    count = lax.axis_size("chip") * lax.axis_size("core")
    total_blocks = blocks_dev * count
    device = flat_index()

    grad_out_all = lax.all_gather(grad_out, SEQ, axis=0, tiled=True)
    weight_all = lax.all_gather(out_weight, SEQ, axis=0, tiled=True)

    paired = jnp.stack([keys, values])
    before, after = halo(paired)
    extended = jnp.concatenate([before, paired, after], axis=1)

    slots = global_blocks.shape[0]
    owners = global_blocks // blocks_dev
    masked = []
    for g in range(slots):
        start = (global_blocks[g] % blocks_dev) * BLK
        block = lax.dynamic_slice_in_dim(paired, start, BLK, axis=1)
        masked.append(jnp.where(owners[g] == device, block, jnp.zeros_like(block)))
    global_kv = butterfly_sum(jnp.stack(masked))

    local_ids = jnp.arange(blocks_dev, dtype=jnp.int32)
    global_ids = device * blocks_dev + local_ids
    offsets = jnp.array([-1, 0, 1], dtype=jnp.int32)
    neighbour_ids = global_ids[:, None] + offsets[None, :]
    window_index = local_ids[:, None] + blocks_dev + offsets[None, :]
    window_live = (neighbour_ids >= 0) & (neighbour_ids < total_blocks)
    random_index = random_blocks - (device - 1) * blocks_dev
    ext_index = jnp.concatenate([window_index, random_index], axis=1)
    n_local = ext_index.shape[1]
    live = jnp.concatenate(
        [window_live, jnp.ones(random_blocks.shape, jnp.bool_), jnp.ones((blocks_dev, slots), jnp.bool_)],
        axis=1,
    )

    upstream = lax.dot_general(
        grad_out, weight_all, (((1,), (1,)), ((), ())), preferred_element_type=jnp.float32
    ).astype(jnp.bfloat16)

    attn_rows, dq_rows, dk_ext, dv_ext = [], [], [], []
    grad_ext = jnp.zeros((2, 3 * blocks_dev * BLK, feature_count), jnp.float32)
    global_terms = []
    for b in range(blocks_dev):
        chosen = [
            lax.dynamic_slice_in_dim(extended, ext_index[b, j] * BLK, BLK, axis=1)
            for j in range(n_local)
        ]
        chosen += [global_kv[g] for g in range(slots)]
        chosen = jnp.concatenate(chosen, axis=1).reshape(2, -1, H, hd)
        live_rows = jnp.repeat(live[b], BLK)
        q = query[b * BLK : (b + 1) * BLK].reshape(BLK, H, hd)
        up = upstream[b * BLK : (b + 1) * BLK].reshape(BLK, H, hd)
        probs, probs_b, attn = attend(q, chosen[0], chosen[1], live_rows, up)
        dq, dk, dv = attend_back(q, chosen[0], chosen[1], probs, probs_b, up)
        attn_rows.append(attn.reshape(BLK, feature_count))
        dq_rows.append(dq.reshape(BLK, feature_count).astype(jnp.bfloat16))
        dkv = jnp.stack([dk, dv]).reshape(2, -1, BLK, feature_count)
        for j in range(n_local):
            start = ext_index[b, j] * BLK
            cur = lax.dynamic_slice_in_dim(grad_ext, start, BLK, axis=1)
            grad_ext = lax.dynamic_update_slice_in_dim(grad_ext, cur + dkv[:, j], start, axis=1)
        global_terms.append(dkv[:, n_local:])
    global_local = global_terms[0]
    for t in global_terms[1:]:
        global_local = global_local + t
    global_total = butterfly_sum(jnp.swapaxes(global_local, 0, 1))

    attn_out = jnp.concatenate(attn_rows, axis=0)
    layer_out = jnp.dot(attn_out, weight_all, preferred_element_type=jnp.float32).astype(
        jnp.bfloat16
    )
    w_rows = out_weight.shape[0]
    attn_cols = lax.all_to_all(
        attn_out.reshape(tok_rows, count, w_rows), SEQ, 1, 0, tiled=False
    ).reshape(count * tok_rows, w_rows)
    grad_weight = lax.dot_general(
        attn_cols, grad_out_all, (((0,), (0,)), ((), ())), preferred_element_type=jnp.float32
    )

    rims = jnp.concatenate(
        [grad_ext[:, : blocks_dev * BLK], grad_ext[:, 2 * blocks_dev * BLK :]], axis=1
    ).astype(jnp.bfloat16)
    from_prev, from_next = halo(rims)
    own = grad_ext[:, blocks_dev * BLK : 2 * blocks_dev * BLK]
    own = own + from_prev[:, blocks_dev * BLK :].astype(jnp.float32)
    own = own + from_next[:, : blocks_dev * BLK].astype(jnp.float32)
    for g in range(slots):
        start = (global_blocks[g] % blocks_dev) * BLK
        add = jnp.where(owners[g] == device, global_total[g], jnp.zeros_like(global_total[g]))
        cur = lax.dynamic_slice_in_dim(own, start, BLK, axis=1)
        own = lax.dynamic_update_slice_in_dim(own, cur + add, start, axis=1)
    own = own.astype(jnp.bfloat16)
    grad_query = jnp.concatenate(dq_rows, axis=0)
    return (layer_out, grad_query, own[0], own[1], grad_weight)


def solution(mesh):
    groups, seq = mesh.devices.shape
    split = Mesh(mesh.devices.reshape(groups, seq // 2, 2), ("groups",) + SEQ)
    rows = P(("groups",) + SEQ, None)
    placed = (rows, rows, rows, P(SEQ, None), rows, P("groups"), rows)
    return jax.shard_map(
        local,
        mesh=split,
        in_specs=placed,
        out_specs=(rows, rows, rows, rows, rows),
        check_vma=False,
    )
```

time: 430 us -> 298 us (0.69)
  waiting for transfers between devices: 287 us -> 111 us
  starting transfers between devices: 11.8 us -> 64.1 us
  matrix products: 41.4 us -> 23.4 us
  local copies, waits for them, and re-layouts: 46.4 us -> 50.9 us
    psum x2 -> x0, waiting for transfers between devices: 139 us -> none  [the longest x1 74.2 us: spread(): return lax.psum(jnp.where(mine, shard, jnp.zeros_like(shard)), axis)]
    reduce_scatter x1 -> x0, waiting for transfers between devices: 101 us -> none  [local(): lax.psum_scatter(lax.dot_general(columns, grad_out, (((0,), (0,)), ((), (...]
    ppermute x4 -> x20, waiting for transfers between devices: 12.4 us -> 92 us  [the longest x12 63.4 us: xor_swap(): return lax.ppermute(x, 'chip', [(i, i ^ m) for i in range(n)])]
    ppermute x4 -> x20, starting transfers between devices: 11.5 us -> 56.9 us  [the longest x12 25.2 us: xor_swap(): return lax.ppermute(x, 'chip', [(i, i ^ m) for i in range(n)])]
    all_gather x1 -> x2, waiting for transfers between devices: 33.9 us -> 9.63 us  [the longest x1 9.63 us: local(): grad_out_all = lax.all_gather(grad_out, SEQ, axis=0, tiled=True)]
    dot_general x11 -> x9, matrix products: 41.4 us -> 23.4 us  [the longest x1 5.89 us: local(): lax.dot_general(attn_cols, grad_out_all, (((0,), (0,)), ((), ())), prefer...]
    slice x2 -> x7, local copies, waits for them, and re-layouts: 1.43 us -> 11.5 us  [the longest x3 9.43 us: local(): probs, probs_b, attn = attend(q, chosen[0], chosen[1], live_rows, up)]
    all_to_all x0 -> x1, waiting for transfers between devices: none -> 9.34 us  [local(): lax.all_to_all(attn_out.reshape(tok_rows, count, w_rows), SEQ, 1, 0, tile...]
  transfers between devices with their start and end apart: 8 -> 23, of which waited for: 5 -> 15; matrix products, arithmetic and copies ran while one was open for 15% -> 17% of each run, Pallas kernels for 0% -> 0%
where the time goes in v1:
time: 298 us; the launch traced here: 297 us
  waiting for transfers between devices  111 us (37%)
  starting transfers between devices  64.1 us (22%)
  local copies, waits for them, and re-layouts  50.9 us (17%)
  other arithmetic  29.5 us (10%)
  matrix products  23.4 us (8%)
  between operations  17.8 us (6%)
    ppermute x12, waiting for transfers between devices, xor_swap(): return lax.ppermute(x, 'chip', [(i, i ^ m) for i in range(n)])  63.4 us
    ppermute x12, starting transfers between devices, xor_swap(): return lax.ppermute(x, 'chip', [(i, i ^ m) for i in range(n)])  25.2 us
    ppermute x2, waiting for transfers between devices, halo(): after = lax.ppermute(shard, SEQ, down)  21 us
    ppermute x4, starting transfers between devices, xor_swap(): return lax.ppermute(x, 'core', [(i, i ^ 1) for i in range(n)])  19 us
    unnamed x42, local copies, waits for them, and re-layouts  13.6 us
    another operation x2, local copies, waits for them, and re-layouts, local(): dkv = jnp.stack([dk, dv]).reshape(2, -1, BLK, feature_count)  10.3 us
    all_gather x1, waiting for transfers between devices, local(): grad_out_all = lax.all_gather(grad_out, SEQ, axis=0, tiled=True)  9.63 us
    slice x3, local copies, waits for them, and re-layouts, local(): probs, probs_b, attn = attend(q, chosen[0], chosen[1], live_rows, up)  9.43 us
  transfers between devices with their start and end apart: 23, of which 15 were waited for; matrix products, arithmetic and copies ran while one was open for 17% of the time, Pallas kernels for 0%

profile of v1, /device:TPU:11, one launch (start us, length us, event | category | flops | bytes accessed | tf_op | source)
XLA Modules:
  0.0 296.7 jit_solution(14538599541132574064)
XLA Ops:
  8.3 3.7 %collective-permute-start = (bf16[2,128,1024]{2,1,0:T(8,128)(2,1)S(1)}, bf16[2,128,1024]{2,1,0:T(8,128)(2,1)S(1)}, u32[]{:S(2)}, u32[]{:S(2)}) collective-permute-start(bf16[2,128,1024]{2,1,0:T(8,128)(2,1)S(1)} %pad_maximum_fusion.3), channel_id=1, source_target_pairs={{0,1},{1,2},{2,3},{3,4},{4,5},{5,6},{6,7},{7,8},{8,9},{9,10},{10,1... | collective-permute-start | bytes 1572872 | tf_op jit(solution)/shard_map/ppermute | solution.py:57
  14.7 3.5 %collective-permute-done = bf16[2,128,1024]{2,1,0:T(8,128)(2,1)S(1)} collective-permute-done((bf16[2,128,1024]{2,1,0:T(8,128)(2,1)S(1)}, bf16[2,128,1024]{2,1,0:T(8,128)(2,1)S(1)}, u32[]{:S(2)}, u32[]{:S(2)}) %collective-permute-start) | collective-permute-done | bytes 524320 | tf_op jit(solution)/shard_map/ppermute | solution.py:57
  19.0 2.2 broadcast_select_fusion.2
  22.2 2.3 collective-permute-start.2
  27.0 7.2 %collective-permute-done.3 = bf16[4,32768]{1,0:T(4,128)(2,1)S(1)} collective-permute-done((bf16[4,32768]{1,0:T(4,128)(2,1)S(1)}, bf16[4,32768]{1,0:T(4,128)(2,1)S(1)}, u32[]{:S(2)}, u32[]{:S(2)}) %collective-permute-start.3) | collective-permute-done | bytes 262176 | tf_op jit(solution)/shard_map/ppermute | solution.py:27
  34.7 3.1 %collective-permute-start.1 = (bf16[2,128,1024]{2,1,0:T(8,128)(2,1)S(1)}, bf16[2,128,1024]{2,1,0:T(8,128)(2,1)S(1)}, u32[]{:S(2)}, u32[]{:S(2)}) collective-permute-start(bf16[2,128,1024]{2,1,0:T(8,128)(2,1)S(1)} %pad_maximum_fusion.3), channel_id=1, source_target_pairs={{1,0},{2,1},{3,2},{4,3},{5,4},{6,5},{7,6},{8,7},{9,8},{10,9},{11,1... | collective-permute-start | bytes 1572872 | tf_op jit(solution)/shard_map/ppermute | solution.py:58
  39.0 2.4 collective-permute-start.5
  41.4 3.7 %collective-permute-done.5 = bf16[1,32768]{1,0:T(2,128)(2,1)S(1)} collective-permute-done((bf16[1,32768]{1,0:T(2,128)(2,1)S(1)}, bf16[1,32768]{1,0:T(2,128)(2,1)S(1)}, u32[]{:S(2)}, u32[]{:S(2)}) %collective-permute-start.5) | collective-permute-done | bytes 65568 | tf_op jit(solution)/shard_map/ppermute | solution.py:27
  45.4 4.2 %collective-permute-start.6 = (bf16[1,32768]{1,0:T(2,128)(2,1)S(1)}, bf16[1,32768]{1,0:T(2,128)(2,1)S(1)}, u32[]{:S(2)}, u32[]{:S(2)}) collective-permute-start(bf16[1,32768]{1,0:T(2,128)(2,1)S(1)} %fusion.33), channel_id=1, source_target_pairs={{0,8},{2,10},{4,12},{6,14},{8,0},{10,2},{12,4},{14,6},{1,9},{3,11}... | collective-permute-start | bytes 196616 | tf_op jit(solution)/shard_map/ppermute | solution.py:27
  49.6 5.3 %collective-permute-done.6 = bf16[1,32768]{1,0:T(2,128)(2,1)S(1)} collective-permute-done((bf16[1,32768]{1,0:T(2,128)(2,1)S(1)}, bf16[1,32768]{1,0:T(2,128)(2,1)S(1)}, u32[]{:S(2)}, u32[]{:S(2)}) %collective-permute-start.6) | collective-permute-done | bytes 65568 | tf_op jit(solution)/shard_map/ppermute | solution.py:27
  55.5 9.8 %collective-permute-start.7 = (bf16[2,32768]{1,0:T(2,128)(2,1)S(1)}, bf16[2,32768]{1,0:T(2,128)(2,1)S(1)}, u32[]{:S(2)}, u32[]{:S(2)}) collective-permute-start(bf16[2,32768]{1,0:T(2,128)(2,1)S(1)} %broadcast_select_fusion.12), channel_id=1, source_target_pairs={{0,4},{2,6},{4,0},{6,2},{8,12},{10,14},{12,8},{14,10},{1,5},{3,7},... | collective-permute-start | bytes 393224 | tf_op jit(solution)/shard_map/ppermute | solution.py:27
  69.5 6.5 %collective-permute-done.8 = bf16[4,32768]{1,0:T(4,128)(2,1)S(1)} collective-permute-done((bf16[4,32768]{1,0:T(4,128)(2,1)S(1)}, bf16[4,32768]{1,0:T(4,128)(2,1)S(1)}, u32[]{:S(2)}, u32[]{:S(2)}) %collective-permute-start.8) | collective-permute-done | bytes 262176 | tf_op jit(solution)/shard_map/ppermute | solution.py:27
  76.5 13.4 %collective-permute-start.9 = (bf16[8,32768]{1,0:T(8,128)(2,1)S(1)}, bf16[8,32768]{1,0:T(8,128)(2,1)S(1)}, u32[]{:S(2)}, u32[]{:S(2)}) collective-permute-start(bf16[8,32768]{1,0:T(8,128)(2,1)S(1)} %maximum_select_fusion.3), channel_id=1, source_target_pairs={{0,1},{1,0},{2,3},{3,2},{4,5},{5,4},{6,7},{7,6},{8,9},{9,8},{10,11... | collective-permute-start | bytes 1572872 | tf_op jit(solution)/shard_map/ppermute | solution.py:24
  94.9 4.0 %fusion.39 = (bf16[1,1024,1024]{2,1,0:T(8,128)(2,1)}, bf16[1,1024,1024]{2,1,0:T(8,128)(2,1)S(1)}) fusion(bf16[2,1024,1024]{2,1,0:T(8,128)(2,1)} %constant_dynamic-update-slice_fusion), kind=kLoop, calls=%fused_computation.102 | loop fusion | bytes 8388608 | tf_op jit(solution)/shard_map/slice | solution.py:141
  98.9 2.5 copy.71
  101.5 2.9 copy.72
  105.2 3.4 %fusion.44 = (f32[8,128]{1,0:T(8,128)S(1)}, f32[8,128,1024]{1,2,0:T(8,128)}) fusion(f32[8,1024,128]{2,1,0:T(8,128)S(1)} %fusion.29, pred[1024]{0:T(1024)(128)(4,1)S(1)} %broadcast_bitcast_fusion), kind=kOutput, calls=%fused_computation.107 | output fusion | flops 6292479 | bytes 8393728 | tf_op jit(solution)/shard_map/sub | solution.py:67
  108.6 3.7 %convolution_convert_fusion.3 = bf16[128,1024]{1,0:T(8,128)(2,1)S(1)} fusion(bf16[128,2048]{1,0:T(8,128)(2,1)S(1)} %copy-done.12, bf16[1024,2048]{1,0:T(8,128)(2,1)} %all-gather.3.cloned.1.call-done), kind=kOutput, calls=%fused_computation.20 | convolution fusion | flops 537001984 | bytes 4980736 | tf_op jit(solution)/shard_map/dot_general | solution.py:124
  112.5 3.1 %fusion.22 = f32[8,128,1024]{2,1,0:T(8,128)S(1)} fusion(bf16[128,8,128]{0,2,1:T(8,128)(2,1)S(1)} %bitcast.158, f32[8,128,1024]{1,2,0:T(8,128)} %get-tuple-element.46, f32[8,128]{1,0:T(8,128)S(1)} %get-tuple-element.45), kind=kOutput, calls=%fused_computation.46 | convolution fusion | flops 270532608 | bytes 8654848 | tf_op jit(solution)/shard_map/hij,ihd->jhd/dot_general | solution.py:77
  116.6 3.1 %multiply_reduce_fusion = (f32[8,128]{1,0:T(8,128)S(1)}, f32[8,128,1024]{1,2,0:T(8,128)}) fusion(f32[8,128,1024]{1,2,0:T(8,128)S(1)} %copy-done.8, f32[8,128]{1,0:T(8,128)S(1)} %get-tuple-element.45, bf16[128,8,128]{0,2,1:T(8,128)(2,1)S(1)} %bitcast.159, bf16[1024,8,128]{0,2,1:T(8,128)(2,1)S(1)} %bitcast.154), kind=kOutput, calls=%fused_computation.6 | convolution fusion | flops 271580160 | bytes 10756096 | tf_op jit(solution)/shard_map/ihd,jhd->hij/dot_general | solution.py:78
  119.8 3.0 %copy.107 = f32[128,8,8,128]{3,2,1,0:T(8,128)} copy(f32[128,8,8,128]{3,1,2,0:T(8,128)S(1)} %bitcast.146) | data formatting | bytes 8388608
  122.7 5.4 %copy.85 = f32[1,8,128,1024]{3,2,1,0:T(8,128)} copy(f32[1,8,128,1024]{2,1,3,0:T(8,128)} %bitcast.145) | data formatting | bytes 8388608 | tf_op jit(solution)/shard_map/stack | solution.py:145
  128.1 4.2 %multiply_convert_fusion = bf16[8,128,1024]{1,2,0:T(8,128)(2,1)S(1)} fusion(f32[8,128,1024]{1,2,0:T(8,128)} %get-tuple-element.48, f32[8,128]{1,0:T(8,128)S(1)} %get-tuple-element.47, f32[8,128,1024]{1,2,0:T(8,128)} %get-tuple-element.46, f32[8,128]{1,0:T(8,128)S(1)} %get-tuple-element.45), kind=kLoop, calls=%fused_computation.5 | loop fusion | flops 5242880 | bytes 10493952 | tf_op jit(solution)/shard_map/convert_element_type | solution.py:80
  134.4 4.5 %copy.82 = f32[1024,8,128]{2,1,0:T(8,128)} copy(f32[1024,8,128]{2,0,1:T(8,128)S(1)} %convolution_bitcast_fusion) | data formatting | bytes 8388608 | tf_op jit(solution)/shard_map/hij,ihd->jhd/transpose | solution.py:82
  138.8 4.9 %stack.24 = f32[1,8,128,1024]{3,2,1,0:T(8,128)} reshape(f32[1024,8,128]{2,1,0:T(8,128)} %copy.82) | data formatting | bytes 8388608 | tf_op jit(solution)/shard_map/stack | solution.py:145
  143.8 1.7 fusion.5
  147.2 2.6 collective-permute-done.12
  150.1 13.4 %collective-permute-done.13 = f32[4,32768]{1,0:T(4,128)S(1)} collective-permute-done((f32[4,32768]{1,0:T(4,128)S(1)}, f32[4,32768]{1,0:T(4,128)S(1)}, u32[]{:S(2)}, u32[]{:S(2)}) %collective-permute-start.13) | collective-permute-done | bytes 524320 | tf_op jit(solution)/shard_map/ppermute | solution.py:27
  163.8 2.7 collective-permute-start.14
  166.5 5.7 %collective-permute-done.14 = f32[2,32768]{1,0:T(2,128)S(1)} collective-permute-done((f32[2,32768]{1,0:T(2,128)S(1)}, f32[2,32768]{1,0:T(2,128)S(1)}, u32[]{:S(2)}, u32[]{:S(2)}) %collective-permute-start.14) | collective-permute-done | bytes 262176 | tf_op jit(solution)/shard_map/ppermute | solution.py:27
  172.7 1.5 convolution_convert_fusion.2
  174.2 7.1 %all-to-all-start = ((bf16[1,128,16,64]{1,3,0,2:T(8,128)(2,1)}), bf16[1,128,16,64]{1,3,0,2:T(8,128)(2,1)S(1)}, u32[]{:S(2)}, u32[]{:S(2)}) async-start(bf16[1,128,16,64]{1,3,0,2:T(8,128)(2,1)} %bitcast.29), calls=%async_computation | async-start | bytes 524288 | tf_op jit(solution)/shard_map/all_to_all | solution.py:161
  181.5 2.2 collective-permute-start.16
  183.7 9.3 %all-to-all-done = bf16[1,128,16,64]{1,3,0,2:T(8,128)(2,1)S(1)} async-done(((bf16[1,128,16,64]{1,3,0,2:T(8,128)(2,1)}), bf16[1,128,16,64]{1,3,0,2:T(8,128)(2,1)S(1)}, u32[]{:S(2)}, u32[]{:S(2)}) %all-to-all-start) | async-done | bytes 262176 | tf_op jit(solution)/shard_map/all_to_all | solution.py:161
  194.3 2.0 collective-permute-start.17
  200.4 11.7 %collective-permute-done.17 = f32[2,32768]{1,0:T(2,128)S(1)} collective-permute-done((f32[2,32768]{1,0:T(2,128)S(1)}, f32[2,32768]{1,0:T(2,128)S(1)}, u32[]{:S(2)}, u32[]{:S(2)}) %collective-permute-start.17) | collective-permute-done | bytes 262176 | tf_op jit(solution)/shard_map/ppermute | solution.py:27
  215.1 9.3 %collective-permute-done.18 = f32[4,32768]{1,0:T(4,128)S(1)} collective-permute-done((f32[4,32768]{1,0:T(4,128)S(1)}, f32[4,32768]{1,0:T(4,128)S(1)}, u32[]{:S(2)}, u32[]{:S(2)}) %collective-permute-start.18) | collective-permute-done | bytes 524320 | tf_op jit(solution)/shard_map/ppermute | solution.py:27
  225.7 3.3 %collective-permute-start.19 = (f32[8,32768]{1,0:T(8,128)}, f32[8,32768]{1,0:T(8,128)}, u32[]{:S(2)}, u32[]{:S(2)}) collective-permute-start(f32[8,32768]{1,0:T(8,128)} %maximum_select_fusion.2), channel_id=1, source_target_pairs={{0,1},{1,0},{2,3},{3,2},{4,5},{5,4},{6,7},{7,6},{8,9},{9,8},{10,11... | collective-permute-start | bytes 3145736 | tf_op jit(solution)/shard_map/ppermute | solution.py:24
  230.2 1.9 collective-permute-start.11
  232.1 4.0 %collective-permute-start.10 = (bf16[2,256,1024]{2,1,0:T(8,128)(2,1)}, bf16[2,256,1024]{2,1,0:T(8,128)(2,1)}, u32[]{:S(2)}, u32[]{:S(2)}) collective-permute-start(bf16[2,256,1024]{2,1,0:T(8,128)(2,1)} %pad_maximum_fusion.2), channel_id=1, source_target_pairs={{0,1},{1,2},{2,3},{3,4},{4,5},{5,6},{6,7},{7,8},{8,9},{9,10},{10,1... | collective-permute-start | bytes 3145736 | tf_op jit(solution)/shard_map/ppermute | solution.py:57
  237.7 3.9 %convolution_convert_fusion = bf16[128,2048]{1,0:T(8,128)(2,1)} fusion(bf16[128,1024]{0,1:T(8,128)(2,1)} %bitcast.14, bf16[1024,2048]{1,0:T(8,128)(2,1)} %all-gather.3.cloned.1.call-done), kind=kOutput, calls=%fused_computation.8 | convolution fusion | flops 537133056 | bytes 4980736 | tf_op jit(solution)/shard_map/dot_general | solution.py:157
  241.6 2.5 maximum_select_fusion
  245.5 2.4 select_n.294
  247.9 2.4 select_n.291
  250.3 21.0 %collective-permute-done.11 = bf16[2,256,1024]{2,1,0:T(8,128)(2,1)} collective-permute-done((bf16[2,256,1024]{2,1,0:T(8,128)(2,1)}, bf16[2,256,1024]{2,1,0:T(8,128)(2,1)}, u32[]{:S(2)}, u32[]{:S(2)}) %collective-permute-start.11) | collective-permute-done | bytes 1048608 | tf_op jit(solution)/shard_map/ppermute | solution.py:58
  271.3 2.3 fusion.12
  274.4 9.6 %all-gather.5.cloned.1.call-done = bf16[2048,2048]{1,0:T(8,128)(2,1)} async-done(((bf16[128,2048]{1,0:T(8,128)(2,1)}), bf16[2048,2048]{1,0:T(8,128)(2,1)}) %all-gather.5.cloned.1.call-update) | async-done | bytes 8388624 | tf_op jit(solution)/shard_map/all_gather | solution.py:94
  284.0 5.9 %fusion.25 = f32[64,2048]{1,0:T(8,128)} fusion(bf16[2048,2048]{1,0:T(8,128)(2,1)} %all-gather.5.cloned.1.call-done, bf16[8,8,16,128]{3,2,1,0:T(8,128)(2,1)} %bitcast.153), kind=kOutput, calls=%fused_computation.63 | convolution fusion | flops 536870912 | bytes 9175040 | tf_op jit(solution)/shard_map/dot_general | solution.py:164
  (119 shorter events, 38.8 us)
Async XLA Ops:
  7.2 97.2 %copy-start = (bf16[128,1024]{1,0:T(8,128)(2,1)S(1)}, bf16[128,1024]{1,0:T(8,128)(2,1)}, u32[]{:S(2)}) copy-start(bf16[128,1024]{1,0:T(8,128)(2,1)} %param.8) | copy-start | bytes 786436
  7.2 101.4 %all-gather.3.cloned.1.call-start = ((), (), s32[]{:S(2)}) async-start(), calls=%async_computation.1 | async-start | bytes 4456448 | tf_op jit(solution)/shard_map/all_gather | solution.py:95
  8.3 9.8 %collective-permute-start = (bf16[2,128,1024]{2,1,0:T(8,128)(2,1)S(1)}, bf16[2,128,1024]{2,1,0:T(8,128)(2,1)S(1)}, u32[]{:S(2)}, u32[]{:S(2)}) collective-permute-start(bf16[2,128,1024]{2,1,0:T(8,128)(2,1)S(1)} %pad_maximum_fusion.3), channel_id=1, source_target_pairs={{0,1},{1,2},{2,3},{3,4},{4,5},{5,6},{6,7},{7,8},{8,9},{9,10},{10,1... | collective-permute-start | bytes 1572872 | tf_op jit(solution)/shard_map/ppermute | solution.py:57
  19.0 22.4 %copy-start.16 = (s32[3]{0:T(128)S(1)}, s32[3]{0:T(128)}, u32[]{:S(2)}) copy-start(s32[3]{0:T(128)} %constant.74.clone) | copy-start | bytes 40
  21.2 28.4 %copy-start.15 = (s32[1,3]{1,0:T(1,128)S(1)}, s32[1,3]{1,0:T(1,128)}, u32[]{:S(2)}) copy-start(s32[1,3]{1,0:T(1,128)} %param.14) | copy-start | bytes 40
  22.2 4.0 %collective-permute-start.2 = (bf16[8,32768]{1,0:T(8,128)(2,1)}, bf16[8,32768]{1,0:T(8,128)(2,1)S(1)}, u32[]{:S(2)}, u32[]{:S(2)}) collective-permute-start(bf16[8,32768]{1,0:T(8,128)(2,1)} %select_n.261), channel_id=1, source_target_pairs={{0,1},{1,0},{2,3},{3,2},{4,5},{5,4},{6,7},{7,6},{8,9},{9,8},{10,11... | collective-permute-start | bytes 1572872 | tf_op jit(solution)/shard_map/ppermute | solution.py:24
  24.7 65.1 %copy-start.10 = (bf16[128,1024]{1,0:T(8,128)(2,1)S(1)}, bf16[128,1024]{1,0:T(8,128)(2,1)}, u32[]{:S(2)}) copy-start(bf16[128,1024]{1,0:T(8,128)(2,1)} %param.10) | copy-start | bytes 786436
  24.7 65.1 %copy-start.11 = (bf16[128,1024]{1,0:T(8,128)(2,1)S(1)}, bf16[128,1024]{1,0:T(8,128)(2,1)}, u32[]{:S(2)}) copy-start(bf16[128,1024]{1,0:T(8,128)(2,1)} %param.9) | copy-start | bytes 786436
  26.6 7.6 %collective-permute-start.3 = (bf16[4,32768]{1,0:T(4,128)(2,1)S(1)}, bf16[4,32768]{1,0:T(4,128)(2,1)S(1)}, u32[]{:S(2)}, u32[]{:S(2)}) collective-permute-start(bf16[4,32768]{1,0:T(4,128)(2,1)S(1)} %broadcast_select_fusion.4), channel_id=1, source_target_pairs={{0,2},{2,0},{4,6},{6,4},{8,10},{10,8},{12,14},{14,12},{1,3},{3,1},... | collective-permute-start | bytes 786440 | tf_op jit(solution)/shard_map/ppermute | solution.py:27
  34.6 3.9 %collective-permute-start.4 = (bf16[2,32768]{1,0:T(2,128)(2,1)S(1)}, bf16[2,32768]{1,0:T(2,128)(2,1)S(1)}, u32[]{:S(2)}, u32[]{:S(2)}) collective-permute-start(bf16[2,32768]{1,0:T(2,128)(2,1)S(1)} %broadcast_select_fusion.6), channel_id=1, source_target_pairs={{0,4},{2,6},{4,0},{6,2},{8,12},{10,14},{12,8},{14,10},{1,5},{3,7},... | collective-permute-start | bytes 393224 | tf_op jit(solution)/shard_map/ppermute | solution.py:27
  34.7 34.0 %collective-permute-start.1 = (bf16[2,128,1024]{2,1,0:T(8,128)(2,1)S(1)}, bf16[2,128,1024]{2,1,0:T(8,128)(2,1)S(1)}, u32[]{:S(2)}, u32[]{:S(2)}) collective-permute-start(bf16[2,128,1024]{2,1,0:T(8,128)(2,1)S(1)} %pad_maximum_fusion.3), channel_id=1, source_target_pairs={{1,0},{2,1},{3,2},{4,3},{5,4},{6,5},{7,6},{8,7},{9,8},{10,9},{11,1... | collective-permute-start | bytes 1572872 | tf_op jit(solution)/shard_map/ppermute | solution.py:58
  39.0 6.1 %collective-permute-start.5 = (bf16[1,32768]{1,0:T(2,128)(2,1)S(1)}, bf16[1,32768]{1,0:T(2,128)(2,1)S(1)}, u32[]{:S(2)}, u32[]{:S(2)}) collective-permute-start(bf16[1,32768]{1,0:T(2,128)(2,1)S(1)} %broadcast_select_fusion.10), channel_id=1, source_target_pairs={{0,8},{2,10},{4,12},{6,14},{8,0},{10,2},{12,4},{14,6},{1,9},{3,11}... | collective-permute-start | bytes 196616 | tf_op jit(solution)/shard_map/ppermute | solution.py:27
  45.4 9.5 %collective-permute-start.6 = (bf16[1,32768]{1,0:T(2,128)(2,1)S(1)}, bf16[1,32768]{1,0:T(2,128)(2,1)S(1)}, u32[]{:S(2)}, u32[]{:S(2)}) collective-permute-start(bf16[1,32768]{1,0:T(2,128)(2,1)S(1)} %fusion.33), channel_id=1, source_target_pairs={{0,8},{2,10},{4,12},{6,14},{8,0},{10,2},{12,4},{14,6},{1,9},{3,11}... | collective-permute-start | bytes 196616 | tf_op jit(solution)/shard_map/ppermute | solution.py:27
  55.5 12.5 %collective-permute-start.7 = (bf16[2,32768]{1,0:T(2,128)(2,1)S(1)}, bf16[2,32768]{1,0:T(2,128)(2,1)S(1)}, u32[]{:S(2)}, u32[]{:S(2)}) collective-permute-start(bf16[2,32768]{1,0:T(2,128)(2,1)S(1)} %broadcast_select_fusion.12), channel_id=1, source_target_pairs={{0,4},{2,6},{4,0},{6,2},{8,12},{10,14},{12,8},{14,10},{1,5},{3,7},... | collective-permute-start | bytes 393224 | tf_op jit(solution)/shard_map/ppermute | solution.py:27
  68.5 7.5 %collective-permute-start.8 = (bf16[4,32768]{1,0:T(4,128)(2,1)S(1)}, bf16[4,32768]{1,0:T(4,128)(2,1)S(1)}, u32[]{:S(2)}, u32[]{:S(2)}) collective-permute-start(bf16[4,32768]{1,0:T(4,128)(2,1)S(1)} %maximum_select_fusion.5), channel_id=1, source_target_pairs={{0,2},{2,0},{4,6},{6,4},{8,10},{10,8},{12,14},{14,12},{1,3},{3,1},... | collective-permute-start | bytes 786440 | tf_op jit(solution)/shard_map/ppermute | solution.py:27
  76.5 16.0 %collective-permute-start.9 = (bf16[8,32768]{1,0:T(8,128)(2,1)S(1)}, bf16[8,32768]{1,0:T(8,128)(2,1)S(1)}, u32[]{:S(2)}, u32[]{:S(2)}) collective-permute-start(bf16[8,32768]{1,0:T(8,128)(2,1)S(1)} %maximum_select_fusion.3), channel_id=1, source_target_pairs={{0,1},{1,0},{2,3},{3,2},{4,5},{5,4},{6,7},{7,6},{8,9},{9,8},{10,11... | collective-permute-start | bytes 1572872 | tf_op jit(solution)/shard_map/ppermute | solution.py:24
  104.4 4.3 %copy-start.4 = (bf16[1,1024,1024]{1,2,0:T(8,128)(2,1)}, bf16[1,1024,1024]{1,2,0:T(8,128)(2,1)S(1)}, u32[]{:S(2)}) copy-start(bf16[1,1024,1024]{1,2,0:T(8,128)(2,1)S(1)} %copy.72) | copy-start | bytes 6291460
  105.2 3.4 %copy-start.12 = (bf16[128,2048]{1,0:T(8,128)(2,1)S(1)}, bf16[128,2048]{1,0:T(8,128)(2,1)}, u32[]{:S(2)}) copy-start(bf16[128,2048]{1,0:T(8,128)(2,1)} %param.12) | copy-start | bytes 1572868
  112.5 3.5 %copy-start.8 = (f32[8,128,1024]{1,2,0:T(8,128)S(1)}, f32[8,128,1024]{1,2,0:T(8,128)}, u32[]{:S(2)}) copy-start(f32[8,128,1024]{1,2,0:T(8,128)} %get-tuple-element.46) | copy-start | bytes 12582916
  112.5 4.1 %copy-start.13 = (bf16[1,1024,1024]{1,2,0:T(8,128)(2,1)S(1)}, bf16[1,1024,1024]{1,2,0:T(8,128)(2,1)}, u32[]{:S(2)}) copy-start(bf16[1,1024,1024]{1,2,0:T(8,128)(2,1)} %copy.71) | copy-start | bytes 6291460
  132.3 1.4 copy-start.6
  146.9 2.9 collective-permute-start.12
  147.1 25.5 %copy-start.9 = (f32[8,128,1024]{1,2,0:T(8,128)S(1)}, f32[8,128,1024]{1,2,0:T(8,128)}, u32[]{:S(2)}) copy-start(f32[8,128,1024]{1,2,0:T(8,128)} %get-tuple-element.46) | copy-start | bytes 12582916
  147.1 25.5 %copy-start.14 = (bf16[1,1024,1024]{1,2,0:T(8,128)(2,1)S(1)}, bf16[1,1024,1024]{1,2,0:T(8,128)(2,1)}, u32[]{:S(2)}) copy-start(bf16[1,1024,1024]{1,2,0:T(8,128)(2,1)} %copy.71) | copy-start | bytes 6291460
  150.0 13.4 %collective-permute-start.13 = (f32[4,32768]{1,0:T(4,128)S(1)}, f32[4,32768]{1,0:T(4,128)S(1)}, u32[]{:S(2)}, u32[]{:S(2)}) collective-permute-start(f32[4,32768]{1,0:T(4,128)S(1)} %slice_select_fusion.4), channel_id=1, source_target_pairs={{0,2},{2,0},{4,6},{6,4},{8,10},{10,8},{12,14},{14,12},{1,3},{3,1},... | collective-permute-start | bytes 1572872 | tf_op jit(solution)/shard_map/ppermute | solution.py:27
  163.8 8.4 %collective-permute-start.14 = (f32[2,32768]{1,0:T(2,128)S(1)}, f32[2,32768]{1,0:T(2,128)S(1)}, u32[]{:S(2)}, u32[]{:S(2)}) collective-permute-start(f32[2,32768]{1,0:T(2,128)S(1)} %broadcast_select_fusion.5), channel_id=1, source_target_pairs={{0,4},{2,6},{4,0},{6,2},{8,12},{10,14},{12,8},{14,10},{1,5},{3,7},... | collective-permute-start | bytes 786440 | tf_op jit(solution)/shard_map/ppermute | solution.py:27
  172.6 8.7 %collective-permute-start.15 = (f32[1,32768]{1,0:T(1,128)S(1)}, f32[1,32768]{1,0:T(1,128)S(1)}, u32[]{:S(2)}, u32[]{:S(2)}) collective-permute-start(f32[1,32768]{1,0:T(1,128)S(1)} %broadcast_select_fusion.8), channel_id=1, source_target_pairs={{0,8},{2,10},{4,12},{6,14},{8,0},{10,2},{12,4},{14,6},{1,9},{3,11}... | collective-permute-start | bytes 393224 | tf_op jit(solution)/shard_map/ppermute | solution.py:27
  174.2 18.9 %all-to-all-start = ((bf16[1,128,16,64]{1,3,0,2:T(8,128)(2,1)}), bf16[1,128,16,64]{1,3,0,2:T(8,128)(2,1)S(1)}, u32[]{:S(2)}, u32[]{:S(2)}) async-start(bf16[1,128,16,64]{1,3,0,2:T(8,128)(2,1)} %bitcast.29), calls=%async_computation | async-start | bytes 524288 | tf_op jit(solution)/shard_map/all_to_all | solution.py:161
  181.3 102.7 %all-gather.5.cloned.1.call-start = ((), (), s32[]{:S(2)}) async-start(), calls=%async_computation.2 | async-start | bytes 8912896 | tf_op jit(solution)/shard_map/all_gather | solution.py:94
  181.5 12.4 %collective-permute-start.16 = (f32[1,32768]{1,0:T(1,128)S(1)}, f32[1,32768]{1,0:T(1,128)S(1)}, u32[]{:S(2)}, u32[]{:S(2)}) collective-permute-start(f32[1,32768]{1,0:T(1,128)S(1)} %fusion.34), channel_id=1, source_target_pairs={{0,8},{2,10},{4,12},{6,14},{8,0},{10,2},{12,4},{14,6},{1,9},{3,11}... | collective-permute-start | bytes 393224 | tf_op jit(solution)/shard_map/ppermute | solution.py:27
  194.3 17.8 %collective-permute-start.17 = (f32[2,32768]{1,0:T(2,128)S(1)}, f32[2,32768]{1,0:T(2,128)S(1)}, u32[]{:S(2)}, u32[]{:S(2)}) collective-permute-start(f32[2,32768]{1,0:T(2,128)S(1)} %maximum_select_fusion.6), channel_id=1, source_target_pairs={{0,4},{2,6},{4,0},{6,2},{8,12},{10,14},{12,8},{14,10},{1,5},{3,7},... | collective-permute-start | bytes 786440 | tf_op jit(solution)/shard_map/ppermute | solution.py:27
  196.3 2.5 copy-start.3
  197.7 2.6 copy-start.2
  212.5 11.9 %collective-permute-start.18 = (f32[4,32768]{1,0:T(4,128)S(1)}, f32[4,32768]{1,0:T(4,128)S(1)}, u32[]{:S(2)}, u32[]{:S(2)}) collective-permute-start(f32[4,32768]{1,0:T(4,128)S(1)} %maximum_select_fusion.4), channel_id=1, source_target_pairs={{0,2},{2,0},{4,6},{6,4},{8,10},{10,8},{12,14},{14,12},{1,3},{3,1},... | collective-permute-start | bytes 1572872 | tf_op jit(solution)/shard_map/ppermute | solution.py:27
  215.1 21.0 %copy-start.5 = (bf16[1,1024,1024]{1,2,0:T(8,128)(2,1)S(1)}, bf16[1,1024,1024]{1,2,0:T(8,128)(2,1)}, u32[]{:S(2)}) copy-start(bf16[1,1024,1024]{1,2,0:T(8,128)(2,1)} %copy-done.4) | copy-start | bytes 6291460
  215.1 21.0 %copy-start.7 = (bf16[8,128,1024]{1,2,0:T(8,128)(2,1)S(1)}, bf16[8,128,1024]{1,2,0:T(8,128)(2,1)}, u32[]{:S(2)}) copy-start(bf16[8,128,1024]{1,2,0:T(8,128)(2,1)} %copy-done.6) | copy-start | bytes 6291460
  225.7 15.8 %collective-permute-start.19 = (f32[8,32768]{1,0:T(8,128)}, f32[8,32768]{1,0:T(8,128)}, u32[]{:S(2)}, u32[]{:S(2)}) collective-permute-start(f32[8,32768]{1,0:T(8,128)} %maximum_select_fusion.2), channel_id=1, source_target_pairs={{0,1},{1,0},{2,3},{3,2},{4,5},{5,4},{6,7},{7,6},{8,9},{9,8},{10,11... | collective-permute-start | bytes 3145736 | tf_op jit(solution)/shard_map/ppermute | solution.py:24
  230.2 41.1 %collective-permute-start.11 = (bf16[2,256,1024]{2,1,0:T(8,128)(2,1)}, bf16[2,256,1024]{2,1,0:T(8,128)(2,1)}, u32[]{:S(2)}, u32[]{:S(2)}) collective-permute-start(bf16[2,256,1024]{2,1,0:T(8,128)(2,1)} %pad_maximum_fusion.2), channel_id=1, source_target_pairs={{1,0},{2,1},{3,2},{4,3},{5,4},{6,5},{7,6},{8,7},{9,8},{10,9},{11,1... | collective-permute-start | bytes 3145736 | tf_op jit(solution)/shard_map/ppermute | solution.py:58
  232.1 39.2 %collective-permute-start.10 = (bf16[2,256,1024]{2,1,0:T(8,128)(2,1)}, bf16[2,256,1024]{2,1,0:T(8,128)(2,1)}, u32[]{:S(2)}, u32[]{:S(2)}) collective-permute-start(bf16[2,256,1024]{2,1,0:T(8,128)(2,1)} %pad_maximum_fusion.2), channel_id=1, source_target_pairs={{0,1},{1,2},{2,3},{3,4},{4,5},{5,6},{6,7},{7,8},{8,9},{9,10},{10,1... | collective-permute-start | bytes 3145736 | tf_op jit(solution)/shard_map/ppermute | solution.py:57
  284.0 5.9 %copy-start.1 = (bf16[128,1024]{1,0:T(8,128)(2,1)S(1)}, bf16[128,1024]{1,0:T(8,128)(2,1)}, u32[]{:S(2)}) copy-start(bf16[128,1024]{1,0:T(8,128)(2,1)} %param.8) | copy-start | bytes 786436
Sparse Core Ops, SparseCore 0:
  38.0 57.6 all-gather.2
  184.3 99.6 all-gather.4

commit v2 on v1

--- a/solution.py
+++ b/solution.py
@@ -27,7 +27,7 @@
     return lax.ppermute(x, "chip", [(i, i ^ m) for i in range(n)])
 
 
-def butterfly_sum(x):
+def butterfly_sum(x, wire=None):
     count = lax.axis_size("chip") * lax.axis_size("core")
     levels = count.bit_length() - 1
     shape = x.shape
@@ -40,9 +40,13 @@
         upper = ((d >> k) & 1) == 1
         send = jnp.where(upper, lo, hi)
         keep = jnp.where(upper, hi, lo)
-        parts = keep + xor_swap(send, k)
+        if wire is not None:
+            send = send.astype(wire)
+        parts = keep + xor_swap(send, k).astype(keep.dtype)
     for k in reversed(range(levels)):
         upper = ((d >> k) & 1) == 1
+        if wire is not None and k == levels - 1:
+            parts = parts.astype(wire)
         other = xor_swap(parts, k)
         parts = jnp.where(
             upper, jnp.concatenate([other, parts]), jnp.concatenate([parts, other])
@@ -121,9 +125,14 @@
         axis=1,
     )
 
-    upstream = lax.dot_general(
-        grad_out, weight_all, (((1,), (1,)), ((), ())), preferred_element_type=jnp.float32
+    w_rows = out_weight.shape[0]
+    upstream_cols = lax.dot_general(
+        grad_out_all, out_weight, (((1,), (1,)), ((), ())), preferred_element_type=jnp.float32
     ).astype(jnp.bfloat16)
+    upstream = lax.all_to_all(
+        upstream_cols.reshape(count, tok_rows, w_rows), SEQ, 0, 0, tiled=False
+    )
+    upstream = jnp.swapaxes(upstream, 0, 1).reshape(tok_rows, feature_count)
 
     attn_rows, dq_rows, dk_ext, dv_ext = [], [], [], []
     grad_ext = jnp.zeros((2, 3 * blocks_dev * BLK, feature_count), jnp.float32)
@@ -151,13 +160,12 @@
     global_local = global_terms[0]
     for t in global_terms[1:]:
         global_local = global_local + t
-    global_total = butterfly_sum(jnp.swapaxes(global_local, 0, 1))
+    global_total = butterfly_sum(jnp.swapaxes(global_local, 0, 1), jnp.bfloat16)
 
     attn_out = jnp.concatenate(attn_rows, axis=0)
     layer_out = jnp.dot(attn_out, weight_all, preferred_element_type=jnp.float32).astype(
         jnp.bfloat16
     )
-    w_rows = out_weight.shape[0]
     attn_cols = lax.all_to_all(
         attn_out.reshape(tok_rows, count, w_rows), SEQ, 1, 0, tiled=False
     ).reshape(count * tok_rows, w_rows)

time: 298 us -> 278 us (0.933)
  waiting for transfers between devices: 111 us -> 91.1 us
  other arithmetic: 29.5 us -> 23.4 us
    all_to_all x0 -> x1, waiting for transfers between devices: none -> 13.4 us  [local(): lax.all_to_all(upstream_cols.reshape(count, tok_rows, w_rows), SEQ, 0, 0,...]
    ppermute x4, starting transfers between devices: 19 us -> 7.24 us  [xor_swap(): return lax.ppermute(x, 'core', [(i, i ^ 1) for i in range(n)])]
    ppermute x12, starting transfers between devices: 25.2 us -> 36 us  [xor_swap(): return lax.ppermute(x, 'chip', [(i, i ^ m) for i in range(n)])]
    ppermute x12, waiting for transfers between devices: 63.4 us -> 53.6 us  [xor_swap(): return lax.ppermute(x, 'chip', [(i, i ^ m) for i in range(n)])]
    all_gather x1, waiting for transfers between devices: 9.63 us -> 0.02 us  [local(): grad_out_all = lax.all_gather(grad_out, SEQ, axis=0, tiled=True)]
    ppermute x2, waiting for transfers between devices: 21 us -> 12.4 us  [halo(): after = lax.ppermute(shard, SEQ, down)]
    convert_element_type x0 -> x3, local copies, waits for them, and re-layouts: none -> 5.87 us  [the longest x2 4.84 us: local(): own = lax.dynamic_update_slice_in_dim(own, cur + add, start, axis=1)]
    select_n x2 -> x0, local copies, waits for them, and re-layouts: 4.76 us -> none  [local(): jnp.where(owners[g] == device, global_total[g], jnp.zeros_like(global_tot...]
  transfers between devices with their start and end apart: 23 -> 24, of which waited for: 15 -> 18; matrix products, arithmetic and copies ran while one was open for 17% -> 32% of each run, Pallas kernels for 0% -> 0%
where the time goes in v2:
time: 278 us; the launch traced here: 275 us
  waiting for transfers between devices  91.1 us (33%)
  starting transfers between devices  64.9 us (23%)
  local copies, waits for them, and re-layouts  51.5 us (19%)
  matrix products  26.2 us (9%)
  other arithmetic  23.4 us (8%)
  between operations  17.8 us (6%)
    ppermute x12, waiting for transfers between devices, xor_swap(): return lax.ppermute(x, 'chip', [(i, i ^ m) for i in range(n)])  53.6 us
    ppermute x12, starting transfers between devices, xor_swap(): return lax.ppermute(x, 'chip', [(i, i ^ m) for i in range(n)])  36 us
    all_to_all x1, waiting for transfers between devices, local(): lax.all_to_all(upstream_cols.reshape(count, tok_rows, w_rows), SEQ, 0, 0,...  13.4 us
    ppermute x2, waiting for transfers between devices, halo(): after = lax.ppermute(shard, SEQ, down)  12.4 us
    slice x3, local copies, waits for them, and re-layouts, local(): probs, probs_b, attn = attend(q, chosen[0], chosen[1], live_rows, up)  12.3 us
    unnamed x44, local copies, waits for them, and re-layouts  10.6 us
    another operation x2, local copies, waits for them, and re-layouts, local(): dkv = jnp.stack([dk, dv]).reshape(2, -1, BLK, feature_count)  10.5 us
    ppermute x2, starting transfers between devices, halo(): before = lax.ppermute(shard, SEQ, up)  7.35 us
  transfers between devices with their start and end apart: 24, of which 18 were waited for; matrix products, arithmetic and copies ran while one was open for 32% of the time, Pallas kernels for 0%

profile of v2, /device:TPU:11, one launch (start us, length us, event | category | flops | bytes accessed | tf_op | source)
XLA Modules:
  0.0 274.9 jit_solution(16176240918339718600)
XLA Ops:
  8.3 3.7 %collective-permute-start = (bf16[2,128,1024]{2,1,0:T(8,128)(2,1)S(1)}, bf16[2,128,1024]{2,1,0:T(8,128)(2,1)S(1)}, u32[]{:S(2)}, u32[]{:S(2)}) collective-permute-start(bf16[2,128,1024]{2,1,0:T(8,128)(2,1)S(1)} %pad_maximum_fusion.3), channel_id=1, source_target_pairs={{0,1},{1,2},{2,3},{3,4},{4,5},{5,6},{6,7},{7,8},{8,9},{9,10},{10,1... | collective-permute-start | bytes 1572872 | tf_op jit(solution)/shard_map/ppermute | solution.py:61
  14.7 3.5 %collective-permute-done = bf16[2,128,1024]{2,1,0:T(8,128)(2,1)S(1)} collective-permute-done((bf16[2,128,1024]{2,1,0:T(8,128)(2,1)S(1)}, bf16[2,128,1024]{2,1,0:T(8,128)(2,1)S(1)}, u32[]{:S(2)}, u32[]{:S(2)}) %collective-permute-start) | collective-permute-done | bytes 524320 | tf_op jit(solution)/shard_map/ppermute | solution.py:61
  19.0 2.1 broadcast_select_fusion.2
  22.2 2.3 collective-permute-start.2
  26.9 7.2 %collective-permute-done.3 = bf16[4,32768]{1,0:T(4,128)(2,1)S(1)} collective-permute-done((bf16[4,32768]{1,0:T(4,128)(2,1)S(1)}, bf16[4,32768]{1,0:T(4,128)(2,1)S(1)}, u32[]{:S(2)}, u32[]{:S(2)}) %collective-permute-start.3) | collective-permute-done | bytes 262176 | tf_op jit(solution)/shard_map/ppermute | solution.py:27
  34.7 3.1 %collective-permute-start.1 = (bf16[2,128,1024]{2,1,0:T(8,128)(2,1)S(1)}, bf16[2,128,1024]{2,1,0:T(8,128)(2,1)S(1)}, u32[]{:S(2)}, u32[]{:S(2)}) collective-permute-start(bf16[2,128,1024]{2,1,0:T(8,128)(2,1)S(1)} %pad_maximum_fusion.3), channel_id=1, source_target_pairs={{1,0},{2,1},{3,2},{4,3},{5,4},{6,5},{7,6},{8,7},{9,8},{10,9},{11,1... | collective-permute-start | bytes 1572872 | tf_op jit(solution)/shard_map/ppermute | solution.py:62
  37.8 6.2 %collective-permute-done.4 = bf16[2,32768]{1,0:T(2,128)(2,1)S(1)} collective-permute-done((bf16[2,32768]{1,0:T(2,128)(2,1)S(1)}, bf16[2,32768]{1,0:T(2,128)(2,1)S(1)}, u32[]{:S(2)}, u32[]{:S(2)}) %collective-permute-start.4) | collective-permute-done | bytes 131104 | tf_op jit(solution)/shard_map/ppermute | solution.py:27
  44.5 5.2 %collective-permute-start.5 = (bf16[1,32768]{1,0:T(2,128)(2,1)S(1)}, bf16[1,32768]{1,0:T(2,128)(2,1)S(1)}, u32[]{:S(2)}, u32[]{:S(2)}) collective-permute-start(bf16[1,32768]{1,0:T(2,128)(2,1)S(1)} %broadcast_select_fusion.9), channel_id=1, source_target_pairs={{0,8},{2,10},{4,12},{6,14},{8,0},{10,2},{12,4},{14,6},{1,9},{3,11}... | collective-permute-start | bytes 196616 | tf_op jit(solution)/shard_map/ppermute | solution.py:27
  49.7 8.8 %collective-permute-done.5 = bf16[1,32768]{1,0:T(2,128)(2,1)S(1)} collective-permute-done((bf16[1,32768]{1,0:T(2,128)(2,1)S(1)}, bf16[1,32768]{1,0:T(2,128)(2,1)S(1)}, u32[]{:S(2)}, u32[]{:S(2)}) %collective-permute-start.5) | collective-permute-done | bytes 65568 | tf_op jit(solution)/shard_map/ppermute | solution.py:27
  58.9 3.2 %collective-permute-start.6 = (bf16[1,32768]{1,0:T(2,128)(2,1)S(1)}, bf16[1,32768]{1,0:T(2,128)(2,1)S(1)}, u32[]{:S(2)}, u32[]{:S(2)}) collective-permute-start(bf16[1,32768]{1,0:T(2,128)(2,1)S(1)} %fusion.36), channel_id=1, source_target_pairs={{0,8},{2,10},{4,12},{6,14},{8,0},{10,2},{12,4},{14,6},{1,9},{3,11}... | collective-permute-start | bytes 196616 | tf_op jit(solution)/shard_map/ppermute | solution.py:27
  62.0 4.0 %collective-permute-done.6 = bf16[1,32768]{1,0:T(2,128)(2,1)S(1)} collective-permute-done((bf16[1,32768]{1,0:T(2,128)(2,1)S(1)}, bf16[1,32768]{1,0:T(2,128)(2,1)S(1)}, u32[]{:S(2)}, u32[]{:S(2)}) %collective-permute-start.6) | collective-permute-done | bytes 65568 | tf_op jit(solution)/shard_map/ppermute | solution.py:27
  66.7 2.3 collective-permute-start.7
  71.6 4.2 %collective-permute-done.7 = bf16[2,32768]{1,0:T(2,128)(2,1)S(1)} collective-permute-done((bf16[2,32768]{1,0:T(2,128)(2,1)S(1)}, bf16[2,32768]{1,0:T(2,128)(2,1)S(1)}, u32[]{:S(2)}, u32[]{:S(2)}) %collective-permute-start.7) | collective-permute-done | bytes 131104 | tf_op jit(solution)/shard_map/ppermute | solution.py:27
  76.2 9.7 %collective-permute-start.8 = (bf16[4,32768]{1,0:T(4,128)(2,1)S(1)}, bf16[4,32768]{1,0:T(4,128)(2,1)S(1)}, u32[]{:S(2)}, u32[]{:S(2)}) collective-permute-start(bf16[4,32768]{1,0:T(4,128)(2,1)S(1)} %maximum_select_fusion.4), channel_id=1, source_target_pairs={{0,2},{2,0},{4,6},{6,4},{8,10},{10,8},{12,14},{14,12},{1,3},{3,1},... | collective-permute-start | bytes 786440 | tf_op jit(solution)/shard_map/ppermute | solution.py:27
  86.8 9.8 %collective-permute-done.8 = bf16[4,32768]{1,0:T(4,128)(2,1)S(1)} collective-permute-done((bf16[4,32768]{1,0:T(4,128)(2,1)S(1)}, bf16[4,32768]{1,0:T(4,128)(2,1)S(1)}, u32[]{:S(2)}, u32[]{:S(2)}) %collective-permute-start.8) | collective-permute-done | bytes 262176 | tf_op jit(solution)/shard_map/ppermute | solution.py:27
  103.6 4.8 %fusion.44 = (bf16[1,1024,1024]{2,1,0:T(8,128)(2,1)}, bf16[1,1024,1024]{2,1,0:T(8,128)(2,1)}) fusion(bf16[2,1024,1024]{2,1,0:T(8,128)(2,1)} %constant_dynamic-update-slice_fusion), kind=kLoop, calls=%fused_computation.109 | loop fusion | bytes 8388608 | tf_op jit(solution)/shard_map/slice | solution.py:150
  108.4 2.9 %copy.71 = bf16[1,1024,1024]{1,2,0:T(8,128)(2,1)S(1)} copy(bf16[1,1024,1024]{2,1,0:T(8,128)(2,1)} %get-tuple-element.25) | data formatting | bytes 4194304 | tf_op jit(solution)/shard_map/slice | solution.py:150
  111.3 4.6 %copy.70 = bf16[1,1024,1024]{1,2,0:T(8,128)(2,1)} copy(bf16[1,1024,1024]{2,1,0:T(8,128)(2,1)} %get-tuple-element.26) | data formatting | bytes 4194304 | tf_op jit(solution)/shard_map/slice | solution.py:150
  118.3 1.9 convolution_convert_fusion.3
  120.3 4.9 %all-to-all-start.1 = ((bf16[1,128,16,64]{1,3,0,2:T(8,128)(2,1)}), bf16[1,128,16,64]{1,3,0,2:T(8,128)(2,1)S(1)}, u32[]{:S(2)}, u32[]{:S(2)}) async-start(bf16[1,128,16,64]{1,3,0,2:T(8,128)(2,1)} %bitcast.32), calls=%async_computation.1 | async-start | bytes 524288 | tf_op jit(solution)/shard_map/all_to_all | solution.py:169
  125.2 6.1 %fusion.9 = bf16[8,16,8,128]{3,2,1,0:T(8,128)(2,1)S(1)} fusion(bf16[2048,2048]{1,0:T(8,128)(2,1)} %all-gather.5.cloned.1.call-done, bf16[64,2048]{1,0:T(8,128)(2,1)S(1)} %copy-done.15), kind=kOutput, calls=%fused_computation.20 | convolution fusion | flops 537001984 | bytes 8912896 | tf_op jit(solution)/shard_map/dot_general | solution.py:129
  132.1 6.5 %all-to-all-done.1 = bf16[1,128,16,64]{1,3,0,2:T(8,128)(2,1)S(1)} async-done(((bf16[1,128,16,64]{1,3,0,2:T(8,128)(2,1)}), bf16[1,128,16,64]{1,3,0,2:T(8,128)(2,1)S(1)}, u32[]{:S(2)}, u32[]{:S(2)}) %all-to-all-start.1) | async-done | bytes 262176 | tf_op jit(solution)/shard_map/all_to_all | solution.py:169
  138.6 4.3 %all-to-all-start = ((bf16[16,128,64]{1,2,0:T(8,128)(2,1)}), bf16[16,128,64]{1,2,0:T(8,128)(2,1)S(1)}, u32[]{:S(2)}, u32[]{:S(2)}) async-start(bf16[16,128,64]{1,2,0:T(8,128)(2,1)} %bitcast.149), calls=%async_computation | async-start | bytes 524288 | tf_op jit(solution)/shard_map/all_to_all | solution.py:132
  143.8 13.4 %all-to-all-done = bf16[16,128,64]{1,2,0:T(8,128)(2,1)S(1)} async-done(((bf16[16,128,64]{1,2,0:T(8,128)(2,1)}), bf16[16,128,64]{1,2,0:T(8,128)(2,1)S(1)}, u32[]{:S(2)}, u32[]{:S(2)}) %all-to-all-start) | async-done | bytes 262176 | tf_op jit(solution)/shard_map/all_to_all | solution.py:132
  157.2 2.9 %fusion.23 = f32[8,128,1024]{2,1,0:T(8,128)S(1)} fusion(bf16[128,8,128]{0,2,1:T(8,128)(2,1)S(1)} %bitcast.165, f32[8,128,1024]{1,2,0:T(8,128)} %copy-done.8, f32[8,128]{1,0:T(8,128)S(1)} %get-tuple-element.43), kind=kOutput, calls=%fused_computation.46 | convolution fusion | flops 270532608 | bytes 8654848 | tf_op jit(solution)/shard_map/hij,ihd->jhd/dot_general | solution.py:81
  160.1 3.0 %copy.107 = f32[128,8,8,128]{3,2,1,0:T(8,128)} copy(f32[128,8,8,128]{3,1,2,0:T(8,128)S(1)} %bitcast.153) | data formatting | bytes 8388608
  163.2 5.6 %copy.84 = f32[1,8,128,1024]{3,2,1,0:T(8,128)} copy(f32[1,8,128,1024]{2,1,3,0:T(8,128)} %bitcast.152) | data formatting | bytes 8388608 | tf_op jit(solution)/shard_map/stack | solution.py:154
  168.8 3.4 %multiply_reduce_fusion = (f32[8,128]{1,0:T(8,128)S(1)}, f32[8,128,1024]{1,2,0:T(8,128)S(1)}) fusion(f32[8,128,1024]{1,2,0:T(8,128)} %copy-done.8, f32[8,128]{1,0:T(8,128)S(1)} %get-tuple-element.43, bf16[128,8,128]{0,2,1:T(8,128)(2,1)S(1)} %bitcast.166, bf16[1024,8,128]{0,2,1:T(8,128)(2,1)S(1)} %bitcast.162), kind=kOutput, calls=%fused_computation.6 | convolution fusion | flops 271580160 | bytes 10756096 | tf_op jit(solution)/shard_map/ihd,jhd->hij/dot_general | solution.py:82
  175.0 4.5 %copy.82 = f32[1024,8,128]{2,1,0:T(8,128)} copy(f32[1024,8,128]{2,0,1:T(8,128)S(1)} %convolution_bitcast_fusion) | data formatting | bytes 8388608 | tf_op jit(solution)/shard_map/hij,ihd->jhd/transpose | solution.py:86
  179.5 4.9 %stack.24 = f32[1,8,128,1024]{3,2,1,0:T(8,128)} reshape(f32[1024,8,128]{2,1,0:T(8,128)} %copy.82) | data formatting | bytes 8388608 | tf_op jit(solution)/shard_map/stack | solution.py:154
  187.2 3.8 %convolution_convert_fusion = bf16[128,2048]{1,0:T(8,128)(2,1)} fusion(bf16[128,1024]{0,1:T(8,128)(2,1)} %bitcast.14, bf16[1024,2048]{1,0:T(8,128)(2,1)} %all-gather.3.cloned.1.call-done), kind=kOutput, calls=%fused_computation.8 | convolution fusion | flops 537133056 | bytes 4980736 | tf_op jit(solution)/shard_map/dot_general | solution.py:166
  194.4 5.9 %fusion.28 = f32[64,2048]{1,0:T(8,128)} fusion(bf16[2048,2048]{1,0:T(8,128)(2,1)} %all-gather.5.cloned.1.call-done, bf16[8,8,16,128]{3,2,1,0:T(8,128)(2,1)S(1)} %bitcast.160), kind=kOutput, calls=%fused_computation.66 | convolution fusion | flops 536870912 | bytes 9175040 | tf_op jit(solution)/shard_map/dot_general | solution.py:172
  202.1 2.6 collective-permute-done.14
  205.1 3.0 %collective-permute-start.15 = (bf16[1,32768]{1,0:T(2,128)(2,1)S(1)}, bf16[1,32768]{1,0:T(2,128)(2,1)S(1)}, u32[]{:S(2)}, u32[]{:S(2)}) collective-permute-start(bf16[1,32768]{1,0:T(2,128)(2,1)S(1)} %fusion.39), channel_id=1, source_target_pairs={{0,8},{2,10},{4,12},{6,14},{8,0},{10,2},{12,4},{14,6},{1,9},{3,11}... | collective-permute-start | bytes 196616 | tf_op jit(solution)/shard_map/ppermute | solution.py:27
  208.2 2.4 collective-permute-done.15
  210.8 3.7 %collective-permute-start.16 = (bf16[1,32768]{1,0:T(2,128)(2,1)S(1)}, bf16[1,32768]{1,0:T(2,128)(2,1)S(1)}, u32[]{:S(2)}, u32[]{:S(2)}) collective-permute-start(bf16[1,32768]{1,0:T(2,128)(2,1)S(1)} %fusion.38), channel_id=1, source_target_pairs={{0,8},{2,10},{4,12},{6,14},{8,0},{10,2},{12,4},{14,6},{1,9},{3,11}... | collective-permute-start | bytes 196616 | tf_op jit(solution)/shard_map/ppermute | solution.py:27
  214.8 3.1 %collective-permute-done.16 = bf16[1,32768]{1,0:T(2,128)(2,1)S(1)} collective-permute-done((bf16[1,32768]{1,0:T(2,128)(2,1)S(1)}, bf16[1,32768]{1,0:T(2,128)(2,1)S(1)}, u32[]{:S(2)}, u32[]{:S(2)}) %collective-permute-start.16) | collective-permute-done | bytes 65568 | tf_op jit(solution)/shard_map/ppermute | solution.py:27
  218.4 2.5 collective-permute-start.17
  221.2 2.1 collective-permute-done.17
  223.8 3.4 %collective-permute-start.18 = (bf16[4,32768]{1,0:T(4,128)(2,1)S(1)}, bf16[4,32768]{1,0:T(4,128)(2,1)S(1)}, u32[]{:S(2)}, u32[]{:S(2)}) collective-permute-start(bf16[4,32768]{1,0:T(4,128)(2,1)S(1)} %maximum_select_fusion.5), channel_id=1, source_target_pairs={{0,2},{2,0},{4,6},{6,4},{8,10},{10,8},{12,14},{14,12},{1,3},{3,1},... | collective-permute-start | bytes 786440 | tf_op jit(solution)/shard_map/ppermute | solution.py:27
  227.9 3.1 %collective-permute-done.18 = bf16[4,32768]{1,0:T(4,128)(2,1)S(1)} collective-permute-done((bf16[4,32768]{1,0:T(4,128)(2,1)S(1)}, bf16[4,32768]{1,0:T(4,128)(2,1)S(1)}, u32[]{:S(2)}, u32[]{:S(2)}) %collective-permute-start.18) | collective-permute-done | bytes 262176 | tf_op jit(solution)/shard_map/ppermute | solution.py:27
  232.3 3.6 %collective-permute-start.19 = (bf16[8,32768]{1,0:T(8,128)(2,1)}, bf16[8,32768]{1,0:T(8,128)(2,1)}, u32[]{:S(2)}, u32[]{:S(2)}) collective-permute-start(bf16[8,32768]{1,0:T(8,128)(2,1)} %maximum_select_fusion.3), channel_id=1, source_target_pairs={{0,1},{1,0},{2,3},{3,2},{4,5},{5,4},{6,7},{7,6},{8,9},{9,8},{10,11... | collective-permute-start | bytes 1572872 | tf_op jit(solution)/shard_map/ppermute | solution.py:24
  237.0 1.9 collective-permute-start.11
  239.0 3.6 %collective-permute-start.10 = (bf16[2,256,1024]{2,1,0:T(8,128)(2,1)}, bf16[2,256,1024]{2,1,0:T(8,128)(2,1)}, u32[]{:S(2)}, u32[]{:S(2)}) collective-permute-start(bf16[2,256,1024]{2,1,0:T(8,128)(2,1)} %pad_maximum_fusion.2), channel_id=1, source_target_pairs={{0,1},{1,2},{2,3},{3,4},{4,5},{5,6},{6,7},{7,8},{8,9},{9,10},{10,1... | collective-permute-start | bytes 3145736 | tf_op jit(solution)/shard_map/ppermute | solution.py:61
  247.5 2.4 reshape.104
  249.9 2.4 reshape.105
  252.3 12.4 %collective-permute-done.11 = bf16[2,256,1024]{2,1,0:T(8,128)(2,1)} collective-permute-done((bf16[2,256,1024]{2,1,0:T(8,128)(2,1)}, bf16[2,256,1024]{2,1,0:T(8,128)(2,1)}, u32[]{:S(2)}, u32[]{:S(2)}) %collective-permute-start.11) | collective-permute-done | bytes 1048608 | tf_op jit(solution)/shard_map/ppermute | solution.py:62
  265.0 2.3 fusion.13
  (124 shorter events, 43.8 us)
Async XLA Ops:
  7.2 108.8 %copy-start = (bf16[128,1024]{1,0:T(8,128)(2,1)S(1)}, bf16[128,1024]{1,0:T(8,128)(2,1)}, u32[]{:S(2)}) copy-start(bf16[128,1024]{1,0:T(8,128)(2,1)} %param.8) | copy-start | bytes 786436
  7.2 118.0 %all-gather.5.cloned.1.call-start = ((), (), s32[]{:S(2)}) async-start(), calls=%async_computation.3 | async-start | bytes 8912896 | tf_op jit(solution)/shard_map/all_gather | solution.py:98
  8.3 9.8 %collective-permute-start = (bf16[2,128,1024]{2,1,0:T(8,128)(2,1)S(1)}, bf16[2,128,1024]{2,1,0:T(8,128)(2,1)S(1)}, u32[]{:S(2)}, u32[]{:S(2)}) collective-permute-start(bf16[2,128,1024]{2,1,0:T(8,128)(2,1)S(1)} %pad_maximum_fusion.3), channel_id=1, source_target_pairs={{0,1},{1,2},{2,3},{3,4},{4,5},{5,6},{6,7},{7,8},{8,9},{9,10},{10,1... | collective-permute-start | bytes 1572872 | tf_op jit(solution)/shard_map/ppermute | solution.py:61
  21.1 28.6 %copy-start.17 = (s32[3]{0:T(128)S(1)}, s32[3]{0:T(128)}, u32[]{:S(2)}) copy-start(s32[3]{0:T(128)} %constant.73.clone) | copy-start | bytes 40
  21.1 40.9 %copy-start.16 = (s32[1,3]{1,0:T(1,128)S(1)}, s32[1,3]{1,0:T(1,128)}, u32[]{:S(2)}) copy-start(s32[1,3]{1,0:T(1,128)} %param.14) | copy-start | bytes 40
  22.2 4.0 %collective-permute-start.2 = (bf16[8,32768]{1,0:T(8,128)(2,1)}, bf16[8,32768]{1,0:T(8,128)(2,1)S(1)}, u32[]{:S(2)}, u32[]{:S(2)}) collective-permute-start(bf16[8,32768]{1,0:T(8,128)(2,1)} %select_n.251), channel_id=1, source_target_pairs={{0,1},{1,0},{2,3},{3,2},{4,5},{5,4},{6,7},{7,6},{8,9},{9,8},{10,11... | collective-permute-start | bytes 1572872 | tf_op jit(solution)/shard_map/ppermute | solution.py:24
  24.4 162.7 %all-gather.3.cloned.1.call-start = ((), (), s32[]{:S(2)}) async-start(), calls=%async_computation.2 | async-start | bytes 4456448 | tf_op jit(solution)/shard_map/all_gather | solution.py:99
  24.8 73.7 %copy-start.10 = (bf16[128,1024]{1,0:T(8,128)(2,1)S(1)}, bf16[128,1024]{1,0:T(8,128)(2,1)}, u32[]{:S(2)}) copy-start(bf16[128,1024]{1,0:T(8,128)(2,1)} %param.10) | copy-start | bytes 786436
  24.8 73.7 %copy-start.11 = (bf16[128,1024]{1,0:T(8,128)(2,1)S(1)}, bf16[128,1024]{1,0:T(8,128)(2,1)}, u32[]{:S(2)}) copy-start(bf16[128,1024]{1,0:T(8,128)(2,1)} %param.9) | copy-start | bytes 786436
  26.5 7.6 %collective-permute-start.3 = (bf16[4,32768]{1,0:T(4,128)(2,1)S(1)}, bf16[4,32768]{1,0:T(4,128)(2,1)S(1)}, u32[]{:S(2)}, u32[]{:S(2)}) collective-permute-start(bf16[4,32768]{1,0:T(4,128)(2,1)S(1)} %broadcast_select_fusion.4), channel_id=1, source_target_pairs={{0,2},{2,0},{4,6},{6,4},{8,10},{10,8},{12,14},{14,12},{1,3},{3,1},... | collective-permute-start | bytes 786440 | tf_op jit(solution)/shard_map/ppermute | solution.py:27
  34.6 9.4 %collective-permute-start.4 = (bf16[2,32768]{1,0:T(2,128)(2,1)S(1)}, bf16[2,32768]{1,0:T(2,128)(2,1)S(1)}, u32[]{:S(2)}, u32[]{:S(2)}) collective-permute-start(bf16[2,32768]{1,0:T(2,128)(2,1)S(1)} %broadcast_select_fusion.5), channel_id=1, source_target_pairs={{0,4},{2,6},{4,0},{6,2},{8,12},{10,14},{12,8},{14,10},{1,5},{3,7},... | collective-permute-start | bytes 393224 | tf_op jit(solution)/shard_map/ppermute | solution.py:27
  34.7 51.3 %collective-permute-start.1 = (bf16[2,128,1024]{2,1,0:T(8,128)(2,1)S(1)}, bf16[2,128,1024]{2,1,0:T(8,128)(2,1)S(1)}, u32[]{:S(2)}, u32[]{:S(2)}) collective-permute-start(bf16[2,128,1024]{2,1,0:T(8,128)(2,1)S(1)} %pad_maximum_fusion.3), channel_id=1, source_target_pairs={{1,0},{2,1},{3,2},{4,3},{5,4},{6,5},{7,6},{8,7},{9,8},{10,9},{11,1... | collective-permute-start | bytes 1572872 | tf_op jit(solution)/shard_map/ppermute | solution.py:62
  44.5 14.1 %collective-permute-start.5 = (bf16[1,32768]{1,0:T(2,128)(2,1)S(1)}, bf16[1,32768]{1,0:T(2,128)(2,1)S(1)}, u32[]{:S(2)}, u32[]{:S(2)}) collective-permute-start(bf16[1,32768]{1,0:T(2,128)(2,1)S(1)} %broadcast_select_fusion.9), channel_id=1, source_target_pairs={{0,8},{2,10},{4,12},{6,14},{8,0},{10,2},{12,4},{14,6},{1,9},{3,11}... | collective-permute-start | bytes 196616 | tf_op jit(solution)/shard_map/ppermute | solution.py:27
  58.9 7.2 %collective-permute-start.6 = (bf16[1,32768]{1,0:T(2,128)(2,1)S(1)}, bf16[1,32768]{1,0:T(2,128)(2,1)S(1)}, u32[]{:S(2)}, u32[]{:S(2)}) collective-permute-start(bf16[1,32768]{1,0:T(2,128)(2,1)S(1)} %fusion.36), channel_id=1, source_target_pairs={{0,8},{2,10},{4,12},{6,14},{8,0},{10,2},{12,4},{14,6},{1,9},{3,11}... | collective-permute-start | bytes 196616 | tf_op jit(solution)/shard_map/ppermute | solution.py:27
  66.7 9.1 %collective-permute-start.7 = (bf16[2,32768]{1,0:T(2,128)(2,1)S(1)}, bf16[2,32768]{1,0:T(2,128)(2,1)S(1)}, u32[]{:S(2)}, u32[]{:S(2)}) collective-permute-start(bf16[2,32768]{1,0:T(2,128)(2,1)S(1)} %broadcast_select_fusion.12), channel_id=1, source_target_pairs={{0,4},{2,6},{4,0},{6,2},{8,12},{10,14},{12,8},{14,10},{1,5},{3,7},... | collective-permute-start | bytes 393224 | tf_op jit(solution)/shard_map/ppermute | solution.py:27
  76.2 20.4 %collective-permute-start.8 = (bf16[4,32768]{1,0:T(4,128)(2,1)S(1)}, bf16[4,32768]{1,0:T(4,128)(2,1)S(1)}, u32[]{:S(2)}, u32[]{:S(2)}) collective-permute-start(bf16[4,32768]{1,0:T(4,128)(2,1)S(1)} %maximum_select_fusion.4), channel_id=1, source_target_pairs={{0,2},{2,0},{4,6},{6,4},{8,10},{10,8},{12,14},{14,12},{1,3},{3,1},... | collective-permute-start | bytes 786440 | tf_op jit(solution)/shard_map/ppermute | solution.py:27
  97.1 4.0 %collective-permute-start.9 = (bf16[8,32768]{1,0:T(8,128)(2,1)S(1)}, bf16[8,32768]{1,0:T(8,128)(2,1)S(1)}, u32[]{:S(2)}, u32[]{:S(2)}) collective-permute-start(bf16[8,32768]{1,0:T(8,128)(2,1)S(1)} %maximum_select_fusion.2), channel_id=1, source_target_pairs={{0,1},{1,0},{2,3},{3,2},{4,5},{5,4},{6,7},{7,6},{8,9},{9,8},{10,11... | collective-permute-start | bytes 1572872 | tf_op jit(solution)/shard_map/ppermute | solution.py:24
  111.3 5.5 %copy-start.4 = (bf16[1,1024,1024]{1,2,0:T(8,128)(2,1)}, bf16[1,1024,1024]{1,2,0:T(8,128)(2,1)S(1)}, u32[]{:S(2)}) copy-start(bf16[1,1024,1024]{1,2,0:T(8,128)(2,1)S(1)} %copy.71) | copy-start | bytes 6291460
  116.7 1.6 copy-start.13
  118.2 2.1 copy-start.8
  118.3 6.9 %copy-start.15 = (bf16[64,2048]{1,0:T(8,128)(2,1)S(1)}, bf16[64,2048]{1,0:T(8,128)(2,1)}, u32[]{:S(2)}) copy-start(bf16[64,2048]{1,0:T(8,128)(2,1)} %param.11) | copy-start | bytes 786436
  120.3 18.3 %all-to-all-start.1 = ((bf16[1,128,16,64]{1,3,0,2:T(8,128)(2,1)}), bf16[1,128,16,64]{1,3,0,2:T(8,128)(2,1)S(1)}, u32[]{:S(2)}, u32[]{:S(2)}) async-start(bf16[1,128,16,64]{1,3,0,2:T(8,128)(2,1)} %bitcast.32), calls=%async_computation.1 | async-start | bytes 524288 | tf_op jit(solution)/shard_map/all_to_all | solution.py:169
  138.6 18.6 %all-to-all-start = ((bf16[16,128,64]{1,2,0:T(8,128)(2,1)}), bf16[16,128,64]{1,2,0:T(8,128)(2,1)S(1)}, u32[]{:S(2)}, u32[]{:S(2)}) async-start(bf16[16,128,64]{1,2,0:T(8,128)(2,1)} %bitcast.149), calls=%async_computation | async-start | bytes 524288 | tf_op jit(solution)/shard_map/all_to_all | solution.py:132
  163.2 5.6 %copy-start.14 = (bf16[1,1024,1024]{1,2,0:T(8,128)(2,1)S(1)}, bf16[1,1024,1024]{1,2,0:T(8,128)(2,1)}, u32[]{:S(2)}) copy-start(bf16[1,1024,1024]{1,2,0:T(8,128)(2,1)} %copy.70) | copy-start | bytes 6291460
  168.8 3.4 %copy-start.9 = (f32[8,128,1024]{1,2,0:T(8,128)S(1)}, f32[8,128,1024]{1,2,0:T(8,128)}, u32[]{:S(2)}) copy-start(f32[8,128,1024]{1,2,0:T(8,128)} %copy-done.8) | copy-start | bytes 12582916
  172.9 1.4 copy-start.6
  187.2 4.2 %collective-permute-start.12 = (bf16[8,32768]{1,0:T(8,128)(2,1)}, bf16[8,32768]{1,0:T(8,128)(2,1)}, u32[]{:S(2)}, u32[]{:S(2)}) collective-permute-start(bf16[8,32768]{1,0:T(8,128)(2,1)} %convert_element_type.91), channel_id=1, source_target_pairs={{0,1},{1,0},{2,3},{3,2},{4,5},{5,4},{6,7},{7,6},{8,9},{9,8},{10,11... | collective-permute-start | bytes 1572872 | tf_op jit(solution)/shard_map/ppermute | solution.py:24
  191.0 3.4 %copy-start.12 = (bf16[16,1,128,1,64]{2,0,4,3,1:T(8,128)(2,1)S(1)}, bf16[16,1,128,1,64]{2,0,4,3,1:T(8,128)(2,1)}, u32[]{:S(2)}) copy-start(bf16[16,1,128,1,64]{2,0,4,3,1:T(8,128)(2,1)} %copy.91) | copy-start | bytes 786436
  192.7 7.7 %collective-permute-start.13 = (bf16[4,32768]{1,0:T(4,128)(2,1)S(1)}, bf16[4,32768]{1,0:T(4,128)(2,1)S(1)}, u32[]{:S(2)}, u32[]{:S(2)}) collective-permute-start(bf16[4,32768]{1,0:T(4,128)(2,1)S(1)} %select_convert_fusion.1), channel_id=1, source_target_pairs={{0,2},{2,0},{4,6},{6,4},{8,10},{10,8},{12,14},{14,12},{1,3},{3,1},... | collective-permute-start | bytes 786440 | tf_op jit(solution)/shard_map/ppermute | solution.py:27
  194.4 7.2 %copy-start.2 = (f32[1,8,128,1024]{3,2,1,0:T(8,128)S(1)}, f32[1,8,128,1024]{3,2,1,0:T(8,128)}, u32[]{:S(2)}) copy-start(f32[1,8,128,1024]{3,2,1,0:T(8,128)} %copy.84) | copy-start | bytes 12582916
  194.4 7.2 %copy-start.3 = (f32[1,8,128,1024]{3,2,1,0:T(8,128)S(1)}, f32[1,8,128,1024]{3,2,1,0:T(8,128)}, u32[]{:S(2)}) copy-start(f32[1,8,128,1024]{3,2,1,0:T(8,128)} %stack.24) | copy-start | bytes 12582916
  200.8 3.9 %collective-permute-start.14 = (bf16[2,32768]{1,0:T(2,128)(2,1)S(1)}, bf16[2,32768]{1,0:T(2,128)(2,1)S(1)}, u32[]{:S(2)}, u32[]{:S(2)}) collective-permute-start(bf16[2,32768]{1,0:T(2,128)(2,1)S(1)} %select_convert_fusion.2), channel_id=1, source_target_pairs={{0,4},{2,6},{4,0},{6,2},{8,12},{10,14},{12,8},{14,10},{1,5},{3,7},... | collective-permute-start | bytes 393224 | tf_op jit(solution)/shard_map/ppermute | solution.py:27
  205.1 5.5 %collective-permute-start.15 = (bf16[1,32768]{1,0:T(2,128)(2,1)S(1)}, bf16[1,32768]{1,0:T(2,128)(2,1)S(1)}, u32[]{:S(2)}, u32[]{:S(2)}) collective-permute-start(bf16[1,32768]{1,0:T(2,128)(2,1)S(1)} %fusion.39), channel_id=1, source_target_pairs={{0,8},{2,10},{4,12},{6,14},{8,0},{10,2},{12,4},{14,6},{1,9},{3,11}... | collective-permute-start | bytes 196616 | tf_op jit(solution)/shard_map/ppermute | solution.py:27
  210.8 7.0 %collective-permute-start.16 = (bf16[1,32768]{1,0:T(2,128)(2,1)S(1)}, bf16[1,32768]{1,0:T(2,128)(2,1)S(1)}, u32[]{:S(2)}, u32[]{:S(2)}) collective-permute-start(bf16[1,32768]{1,0:T(2,128)(2,1)S(1)} %fusion.38), channel_id=1, source_target_pairs={{0,8},{2,10},{4,12},{6,14},{8,0},{10,2},{12,4},{14,6},{1,9},{3,11}... | collective-permute-start | bytes 196616 | tf_op jit(solution)/shard_map/ppermute | solution.py:27
  218.4 4.9 %collective-permute-start.17 = (bf16[2,32768]{1,0:T(2,128)(2,1)S(1)}, bf16[2,32768]{1,0:T(2,128)(2,1)S(1)}, u32[]{:S(2)}, u32[]{:S(2)}) collective-permute-start(bf16[2,32768]{1,0:T(2,128)(2,1)S(1)} %broadcast_select_fusion.11), channel_id=1, source_target_pairs={{0,4},{2,6},{4,0},{6,2},{8,12},{10,14},{12,8},{14,10},{1,5},{3,7},... | collective-permute-start | bytes 393224 | tf_op jit(solution)/shard_map/ppermute | solution.py:27
  223.8 7.2 %collective-permute-start.18 = (bf16[4,32768]{1,0:T(4,128)(2,1)S(1)}, bf16[4,32768]{1,0:T(4,128)(2,1)S(1)}, u32[]{:S(2)}, u32[]{:S(2)}) collective-permute-start(bf16[4,32768]{1,0:T(4,128)(2,1)S(1)} %maximum_select_fusion.5), channel_id=1, source_target_pairs={{0,2},{2,0},{4,6},{6,4},{8,10},{10,8},{12,14},{14,12},{1,3},{3,1},... | collective-permute-start | bytes 786440 | tf_op jit(solution)/shard_map/ppermute | solution.py:27
  227.7 14.9 %copy-start.5 = (bf16[1,1024,1024]{1,2,0:T(8,128)(2,1)S(1)}, bf16[1,1024,1024]{1,2,0:T(8,128)(2,1)}, u32[]{:S(2)}) copy-start(bf16[1,1024,1024]{1,2,0:T(8,128)(2,1)} %copy-done.4) | copy-start | bytes 6291460
  227.7 14.9 %copy-start.7 = (bf16[8,128,1024]{1,2,0:T(8,128)(2,1)S(1)}, bf16[8,128,1024]{1,2,0:T(8,128)(2,1)}, u32[]{:S(2)}) copy-start(bf16[8,128,1024]{1,2,0:T(8,128)(2,1)} %copy-done.6) | copy-start | bytes 6291460
  232.3 11.9 %collective-permute-start.19 = (bf16[8,32768]{1,0:T(8,128)(2,1)}, bf16[8,32768]{1,0:T(8,128)(2,1)}, u32[]{:S(2)}, u32[]{:S(2)}) collective-permute-start(bf16[8,32768]{1,0:T(8,128)(2,1)} %maximum_select_fusion.3), channel_id=1, source_target_pairs={{0,1},{1,0},{2,3},{3,2},{4,5},{5,4},{6,7},{7,6},{8,9},{9,8},{10,11... | collective-permute-start | bytes 1572872 | tf_op jit(solution)/shard_map/ppermute | solution.py:24
  237.0 27.7 %collective-permute-start.11 = (bf16[2,256,1024]{2,1,0:T(8,128)(2,1)}, bf16[2,256,1024]{2,1,0:T(8,128)(2,1)}, u32[]{:S(2)}, u32[]{:S(2)}) collective-permute-start(bf16[2,256,1024]{2,1,0:T(8,128)(2,1)} %pad_maximum_fusion.2), channel_id=1, source_target_pairs={{1,0},{2,1},{3,2},{4,3},{5,4},{6,5},{7,6},{8,7},{9,8},{10,9},{11,1... | collective-permute-start | bytes 3145736 | tf_op jit(solution)/shard_map/ppermute | solution.py:62
  239.0 26.1 %collective-permute-start.10 = (bf16[2,256,1024]{2,1,0:T(8,128)(2,1)}, bf16[2,256,1024]{2,1,0:T(8,128)(2,1)}, u32[]{:S(2)}, u32[]{:S(2)}) collective-permute-start(bf16[2,256,1024]{2,1,0:T(8,128)(2,1)} %pad_maximum_fusion.2), channel_id=1, source_target_pairs={{0,1},{1,2},{2,3},{3,4},{4,5},{5,6},{6,7},{7,8},{8,9},{9,10},{10,1... | collective-permute-start | bytes 3145736 | tf_op jit(solution)/shard_map/ppermute | solution.py:61
  247.5 20.6 %copy-start.1 = (bf16[128,1024]{1,0:T(8,128)(2,1)S(1)}, bf16[128,1024]{1,0:T(8,128)(2,1)}, u32[]{:S(2)}) copy-start(bf16[128,1024]{1,0:T(8,128)(2,1)} %param.8) | copy-start | bytes 786436
Sparse Core Ops, SparseCore 0:
  24.6 86.0 all-gather.4
  112.8 57.7 all-gather.2

commit v3 on v2

--- a/solution.py
+++ b/solution.py
@@ -95,8 +95,9 @@
     total_blocks = blocks_dev * count
     device = flat_index()
 
-    grad_out_all = lax.all_gather(grad_out, SEQ, axis=0, tiled=True)
     weight_all = lax.all_gather(out_weight, SEQ, axis=0, tiled=True)
+    weight_all, grad_out_after = lax.optimization_barrier((weight_all, grad_out))
+    grad_out_all = lax.all_gather(grad_out_after, SEQ, axis=0, tiled=True)
 
     paired = jnp.stack([keys, values])
     before, after = halo(paired)
@@ -126,13 +127,9 @@
     )
 
     w_rows = out_weight.shape[0]
-    upstream_cols = lax.dot_general(
-        grad_out_all, out_weight, (((1,), (1,)), ((), ())), preferred_element_type=jnp.float32
+    upstream = lax.dot_general(
+        grad_out, weight_all, (((1,), (1,)), ((), ())), preferred_element_type=jnp.float32
     ).astype(jnp.bfloat16)
-    upstream = lax.all_to_all(
-        upstream_cols.reshape(count, tok_rows, w_rows), SEQ, 0, 0, tiled=False
-    )
-    upstream = jnp.swapaxes(upstream, 0, 1).reshape(tok_rows, feature_count)
 
     attn_rows, dq_rows, dk_ext, dv_ext = [], [], [], []
     grad_ext = jnp.zeros((2, 3 * blocks_dev * BLK, feature_count), jnp.float32)

time: 278 us -> 289 us (1.040)
  other arithmetic: 23.4 us -> 30.5 us
  waiting for transfers between devices: 91.1 us -> 95.5 us
  starting transfers between devices: 64.9 us -> 68.2 us
    all_gather x1, waiting for transfers between devices: 0.02 us -> 45 us  [local(): grad_out_all = lax.all_gather(grad_out_after, SEQ, axis=0, tiled=True)]
    ppermute x12, waiting for transfers between devices: 53.6 us -> 36.2 us  [xor_swap(): return lax.ppermute(x, 'chip', [(i, i ^ m) for i in range(n)])]
    all_to_all x1 -> x0, waiting for transfers between devices: 13.4 us -> none  [local(): lax.all_to_all(upstream_cols.reshape(count, tok_rows, w_rows), SEQ, 0, 0,...]
    ppermute x12, starting transfers between devices: 36 us -> 26.8 us  [xor_swap(): return lax.ppermute(x, 'chip', [(i, i ^ m) for i in range(n)])]
    ppermute x4, starting transfers between devices: 7.24 us -> 16.3 us  [xor_swap(): return lax.ppermute(x, 'core', [(i, i ^ 1) for i in range(n)])]
    ppermute x2, starting transfers between devices: 5.02 us -> 12.7 us  [halo(): after = lax.ppermute(shard, SEQ, down)]
    ppermute x2, waiting for transfers between devices: 12.4 us -> 5.52 us  [halo(): after = lax.ppermute(shard, SEQ, down)]
    all_to_all x1, waiting for transfers between devices: 6.52 us -> 0.01 us  [local(): lax.all_to_all(attn_out.reshape(tok_rows, count, w_rows), SEQ, 1, 0, tile...]
  transfers between devices with their start and end apart: 24 -> 23, of which waited for: 18 -> 16; matrix products, arithmetic and copies ran while one was open for 32% -> 30% of each run, Pallas kernels for 0% -> 0%
where the time goes in v3:
time: 289 us; the launch traced here: 286 us
  waiting for transfers between devices  95.5 us (33%)
  starting transfers between devices  68.2 us (24%)
  local copies, waits for them, and re-layouts  50.6 us (18%)
  other arithmetic  30.5 us (11%)
  matrix products  23.4 us (8%)
  between operations  17.8 us (6%)
    all_gather x1, waiting for transfers between devices, local(): grad_out_all = lax.all_gather(grad_out_after, SEQ, axis=0, tiled=True)  45 us
    ppermute x12, waiting for transfers between devices, xor_swap(): return lax.ppermute(x, 'chip', [(i, i ^ m) for i in range(n)])  36.2 us
    ppermute x12, starting transfers between devices, xor_swap(): return lax.ppermute(x, 'chip', [(i, i ^ m) for i in range(n)])  26.8 us
    ppermute x4, starting transfers between devices, xor_swap(): return lax.ppermute(x, 'core', [(i, i ^ 1) for i in range(n)])  16.3 us
    ppermute x2, starting transfers between devices, halo(): after = lax.ppermute(shard, SEQ, down)  12.7 us
    unnamed x38, local copies, waits for them, and re-layouts  12.6 us
    another operation x2, local copies, waits for them, and re-layouts, local(): dkv = jnp.stack([dk, dv]).reshape(2, -1, BLK, feature_count)  10.4 us
    slice x3, local copies, waits for them, and re-layouts, local(): probs, probs_b, attn = attend(q, chosen[0], chosen[1], live_rows, up)  9.47 us
  transfers between devices with their start and end apart: 23, of which 16 were waited for; matrix products, arithmetic and copies ran while one was open for 30% of the time, Pallas kernels for 0%

profile of v3, /device:TPU:11, one launch (start us, length us, event | category | flops | bytes accessed | tf_op | source)
XLA Modules:
  0.0 286.0 jit_solution(7198897975941521833)
XLA Ops:
  8.3 3.7 %collective-permute-start = (bf16[2,128,1024]{2,1,0:T(8,128)(2,1)S(1)}, bf16[2,128,1024]{2,1,0:T(8,128)(2,1)S(1)}, u32[]{:S(2)}, u32[]{:S(2)}) collective-permute-start(bf16[2,128,1024]{2,1,0:T(8,128)(2,1)S(1)} %pad_maximum_fusion.3), channel_id=1, source_target_pairs={{0,1},{1,2},{2,3},{3,4},{4,5},{5,6},{6,7},{7,8},{8,9},{9,10},{10,1... | collective-permute-start | bytes 1572872 | tf_op jit(solution)/shard_map/ppermute | solution.py:61
  14.7 3.5 %collective-permute-done = bf16[2,128,1024]{2,1,0:T(8,128)(2,1)S(1)} collective-permute-done((bf16[2,128,1024]{2,1,0:T(8,128)(2,1)S(1)}, bf16[2,128,1024]{2,1,0:T(8,128)(2,1)S(1)}, u32[]{:S(2)}, u32[]{:S(2)}) %collective-permute-start) | collective-permute-done | bytes 524320 | tf_op jit(solution)/shard_map/ppermute | solution.py:61
  19.0 2.2 broadcast_select_fusion.2
  22.2 2.3 collective-permute-start.2
  27.0 7.2 %collective-permute-done.3 = bf16[4,32768]{1,0:T(4,128)(2,1)S(1)} collective-permute-done((bf16[4,32768]{1,0:T(4,128)(2,1)S(1)}, bf16[4,32768]{1,0:T(4,128)(2,1)S(1)}, u32[]{:S(2)}, u32[]{:S(2)}) %collective-permute-start.3) | collective-permute-done | bytes 262176 | tf_op jit(solution)/shard_map/ppermute | solution.py:27
  34.7 3.1 %collective-permute-start.1 = (bf16[2,128,1024]{2,1,0:T(8,128)(2,1)S(1)}, bf16[2,128,1024]{2,1,0:T(8,128)(2,1)S(1)}, u32[]{:S(2)}, u32[]{:S(2)}) collective-permute-start(bf16[2,128,1024]{2,1,0:T(8,128)(2,1)S(1)} %pad_maximum_fusion.3), channel_id=1, source_target_pairs={{1,0},{2,1},{3,2},{4,3},{5,4},{6,5},{7,6},{8,7},{9,8},{10,9},{11,1... | collective-permute-start | bytes 1572872 | tf_op jit(solution)/shard_map/ppermute | solution.py:62
  39.0 2.4 collective-permute-start.5
  41.4 3.7 %collective-permute-done.5 = bf16[1,32768]{1,0:T(2,128)(2,1)S(1)} collective-permute-done((bf16[1,32768]{1,0:T(2,128)(2,1)S(1)}, bf16[1,32768]{1,0:T(2,128)(2,1)S(1)}, u32[]{:S(2)}, u32[]{:S(2)}) %collective-permute-start.5) | collective-permute-done | bytes 65568 | tf_op jit(solution)/shard_map/ppermute | solution.py:27
  45.4 4.2 %collective-permute-start.6 = (bf16[1,32768]{1,0:T(2,128)(2,1)S(1)}, bf16[1,32768]{1,0:T(2,128)(2,1)S(1)}, u32[]{:S(2)}, u32[]{:S(2)}) collective-permute-start(bf16[1,32768]{1,0:T(2,128)(2,1)S(1)} %fusion.35), channel_id=1, source_target_pairs={{0,8},{2,10},{4,12},{6,14},{8,0},{10,2},{12,4},{14,6},{1,9},{3,11}... | collective-permute-start | bytes 196616 | tf_op jit(solution)/shard_map/ppermute | solution.py:27
  49.6 5.3 %collective-permute-done.6 = bf16[1,32768]{1,0:T(2,128)(2,1)S(1)} collective-permute-done((bf16[1,32768]{1,0:T(2,128)(2,1)S(1)}, bf16[1,32768]{1,0:T(2,128)(2,1)S(1)}, u32[]{:S(2)}, u32[]{:S(2)}) %collective-permute-start.6) | collective-permute-done | bytes 65568 | tf_op jit(solution)/shard_map/ppermute | solution.py:27
  55.6 9.8 %collective-permute-start.7 = (bf16[2,32768]{1,0:T(2,128)(2,1)S(1)}, bf16[2,32768]{1,0:T(2,128)(2,1)S(1)}, u32[]{:S(2)}, u32[]{:S(2)}) collective-permute-start(bf16[2,32768]{1,0:T(2,128)(2,1)S(1)} %broadcast_select_fusion.12), channel_id=1, source_target_pairs={{0,4},{2,6},{4,0},{6,2},{8,12},{10,14},{12,8},{14,10},{1,5},{3,7},... | collective-permute-start | bytes 393224 | tf_op jit(solution)/shard_map/ppermute | solution.py:27
  69.5 6.5 %collective-permute-done.8 = bf16[4,32768]{1,0:T(4,128)(2,1)S(1)} collective-permute-done((bf16[4,32768]{1,0:T(4,128)(2,1)S(1)}, bf16[4,32768]{1,0:T(4,128)(2,1)S(1)}, u32[]{:S(2)}, u32[]{:S(2)}) %collective-permute-start.8) | collective-permute-done | bytes 262176 | tf_op jit(solution)/shard_map/ppermute | solution.py:27
  76.5 13.4 %collective-permute-start.9 = (bf16[8,32768]{1,0:T(8,128)(2,1)S(1)}, bf16[8,32768]{1,0:T(8,128)(2,1)S(1)}, u32[]{:S(2)}, u32[]{:S(2)}) collective-permute-start(bf16[8,32768]{1,0:T(8,128)(2,1)S(1)} %maximum_select_fusion.2), channel_id=1, source_target_pairs={{0,1},{1,0},{2,3},{3,2},{4,5},{5,4},{6,7},{7,6},{8,9},{9,8},{10,11... | collective-permute-start | bytes 1572872 | tf_op jit(solution)/shard_map/ppermute | solution.py:24
  95.0 4.0 %fusion.43 = (bf16[1,1024,1024]{2,1,0:T(8,128)(2,1)}, bf16[1,1024,1024]{2,1,0:T(8,128)(2,1)S(1)}) fusion(bf16[2,1024,1024]{2,1,0:T(8,128)(2,1)} %constant_dynamic-update-slice_fusion), kind=kLoop, calls=%fused_computation.107 | loop fusion | bytes 8388608 | tf_op jit(solution)/shard_map/slice | solution.py:147
  99.0 2.6 copy.68
  101.6 2.9 copy.69
  106.9 2.0 convolution_convert_fusion.2
  108.8 6.1 %all-to-all-start = ((bf16[1,128,16,64]{1,3,0,2:T(8,128)(2,1)}), bf16[1,128,16,64]{1,3,0,2:T(8,128)(2,1)S(1)}, u32[]{:S(2)}, u32[]{:S(2)}) async-start(bf16[1,128,16,64]{1,3,0,2:T(8,128)(2,1)} %bitcast.32), calls=%async_computation | async-start | bytes 524288 | tf_op jit(solution)/shard_map/all_to_all | solution.py:166
  115.2 3.6 %convolution_convert_fusion.3 = bf16[1024,128]{1,0:T(8,128)(2,1)S(1)} fusion(bf16[1024,2048]{1,0:T(8,128)(2,1)} %all-gather.3.cloned.1.call-done, bf16[128,2048]{1,0:T(8,128)(2,1)S(1)} %copy-done.12), kind=kOutput, calls=%fused_computation.19 | convolution fusion | flops 537001984 | bytes 4980736 | tf_op jit(solution)/shard_map/dot_general | solution.py:130
  118.8 3.0 %multiply_reduce_fusion = (f32[8,128]{1,0:T(8,128)S(1)}, f32[8,128,1024]{1,2,0:T(8,128)}) fusion(f32[8,128,1024]{1,2,0:T(8,128)S(1)} %copy-done.7, f32[8,128]{1,0:T(8,128)S(1)} %get-tuple-element.47, bf16[128,8,128]{0,2,1:T(8,128)(2,1)S(1)} %bitcast.160, bf16[1024,8,128]{0,2,1:T(8,128)(2,1)S(1)} %bitcast.157), kind=kOutput, calls=%fused_computation.6 | convolution fusion | flops 271580160 | bytes 10756096 | tf_op jit(solution)/shard_map/ihd,jhd->hij/dot_general | solution.py:82
  122.5 3.0 %copy.103 = f32[128,8,8,128]{3,2,1,0:T(8,128)} copy(f32[128,8,8,128]{3,1,2,0:T(8,128)S(1)} %bitcast.148) | data formatting | bytes 8388608
  125.5 5.4 %copy.81 = f32[1,8,128,1024]{3,2,1,0:T(8,128)} copy(f32[1,8,128,1024]{2,1,3,0:T(8,128)} %bitcast.147) | data formatting | bytes 8388608 | tf_op jit(solution)/shard_map/stack | solution.py:151
  130.9 4.2 %multiply_convert_fusion = bf16[8,128,1024]{1,2,0:T(8,128)(2,1)S(1)} fusion(f32[8,128,1024]{1,2,0:T(8,128)} %get-tuple-element.50, f32[8,128]{1,0:T(8,128)S(1)} %get-tuple-element.49, f32[8,128,1024]{1,2,0:T(8,128)} %copy-done.6, f32[8,128]{1,0:T(8,128)S(1)} %get-tuple-element.47), kind=kLoop, calls=%fused_computation.5 | loop fusion | flops 5242880 | bytes 10493952 | tf_op jit(solution)/shard_map/convert_element_type | solution.py:84
  137.1 4.4 %copy.79 = f32[1024,8,128]{2,1,0:T(8,128)} copy(f32[1024,8,128]{2,0,1:T(8,128)S(1)} %convolution_bitcast_fusion) | data formatting | bytes 8388608 | tf_op jit(solution)/shard_map/hij,ihd->jhd/transpose | solution.py:86
  141.5 5.0 %stack.24 = f32[1,8,128,1024]{3,2,1,0:T(8,128)} reshape(f32[1024,8,128]{2,1,0:T(8,128)} %copy.79) | data formatting | bytes 8388608 | tf_op jit(solution)/shard_map/stack | solution.py:151
  146.5 1.7 fusion.5
  158.2 2.2 collective-permute-done.13
  161.6 3.1 %collective-permute-done.14 = bf16[2,32768]{1,0:T(2,128)(2,1)S(1)} collective-permute-done((bf16[2,32768]{1,0:T(2,128)(2,1)S(1)}, bf16[2,32768]{1,0:T(2,128)(2,1)S(1)}, u32[]{:S(2)}, u32[]{:S(2)}) %collective-permute-start.14) | collective-permute-done | bytes 131104 | tf_op jit(solution)/shard_map/ppermute | solution.py:27
  165.1 2.2 collective-permute-start.15
  167.5 3.0 %collective-permute-done.15 = bf16[1,32768]{1,0:T(2,128)(2,1)S(1)} collective-permute-done((bf16[1,32768]{1,0:T(2,128)(2,1)S(1)}, bf16[1,32768]{1,0:T(2,128)(2,1)S(1)}, u32[]{:S(2)}, u32[]{:S(2)}) %collective-permute-start.15) | collective-permute-done | bytes 65568 | tf_op jit(solution)/shard_map/ppermute | solution.py:27
  170.8 2.9 %collective-permute-start.16 = (bf16[1,32768]{1,0:T(2,128)(2,1)S(1)}, bf16[1,32768]{1,0:T(2,128)(2,1)S(1)}, u32[]{:S(2)}, u32[]{:S(2)}) collective-permute-start(bf16[1,32768]{1,0:T(2,128)(2,1)S(1)} %fusion.37), channel_id=1, source_target_pairs={{0,8},{2,10},{4,12},{6,14},{8,0},{10,2},{12,4},{14,6},{1,9},{3,11}... | collective-permute-start | bytes 196616 | tf_op jit(solution)/shard_map/ppermute | solution.py:27
  173.9 2.3 collective-permute-done.16
  176.8 2.4 collective-permute-start.17
  179.7 2.2 collective-permute-done.17
  184.1 2.3 pad_maximum_fusion.2
  186.3 9.6 %collective-permute-start.11 = (bf16[2,256,1024]{2,1,0:T(8,128)(2,1)}, bf16[2,256,1024]{2,1,0:T(8,128)(2,1)}, u32[]{:S(2)}, u32[]{:S(2)}) collective-permute-start(bf16[2,256,1024]{2,1,0:T(8,128)(2,1)} %pad_maximum_fusion.2), channel_id=1, source_target_pairs={{1,0},{2,1},{3,2},{4,3},{5,4},{6,5},{7,6},{8,7},{9,8},{10,9},{11,1... | collective-permute-start | bytes 3145736 | tf_op jit(solution)/shard_map/ppermute | solution.py:62
  195.9 2.3 collective-permute-start.10
  198.3 2.4 maximum_select_fusion.3
  200.9 2.9 %convolution_convert_fusion.1 = bf16[8,128,128]{2,1,0:T(8,128)(2,1)S(1)} fusion(bf16[1024,8,128]{0,2,1:T(8,128)(2,1)} %bitcast.146, bf16[8,128,1024]{1,2,0:T(8,128)(2,1)} %copy-done.5), kind=kOutput, calls=%fused_computation.17 | convolution fusion | flops 268566528 | bytes 4456448 | tf_op jit(solution)/shard_map/hij,jhd->ihd/dot_general | solution.py:85
  204.7 3.8 %convolution_convert_fusion = bf16[128,2048]{1,0:T(8,128)(2,1)} fusion(bf16[128,1024]{0,1:T(8,128)(2,1)} %bitcast.14, bf16[1024,2048]{1,0:T(8,128)(2,1)} %all-gather.3.cloned.1.call-done), kind=kOutput, calls=%fused_computation.8 | convolution fusion | flops 537133056 | bytes 4980736 | tf_op jit(solution)/shard_map/dot_general | solution.py:163
  208.5 1.8 maximum_select_fusion.1
  211.8 2.4 reshape.105
  214.2 2.4 reshape.104
  216.6 5.5 %collective-permute-done.11 = bf16[2,256,1024]{2,1,0:T(8,128)(2,1)} collective-permute-done((bf16[2,256,1024]{2,1,0:T(8,128)(2,1)}, bf16[2,256,1024]{2,1,0:T(8,128)(2,1)}, u32[]{:S(2)}, u32[]{:S(2)}) %collective-permute-start.11) | collective-permute-done | bytes 1048608 | tf_op jit(solution)/shard_map/ppermute | solution.py:62
  222.1 3.0 %collective-permute-done.10 = bf16[2,256,1024]{2,1,0:T(8,128)(2,1)} collective-permute-done((bf16[2,256,1024]{2,1,0:T(8,128)(2,1)}, bf16[2,256,1024]{2,1,0:T(8,128)(2,1)}, u32[]{:S(2)}, u32[]{:S(2)}) %collective-permute-start.10) | collective-permute-done | bytes 1048608 | tf_op jit(solution)/shard_map/ppermute | solution.py:61
  225.1 2.3 fusion.12
  228.2 45.0 %all-gather.5.cloned.1.call-done = bf16[2048,2048]{1,0:T(8,128)(2,1)} async-done(((bf16[128,2048]{1,0:T(8,128)(2,1)}), bf16[2048,2048]{1,0:T(8,128)(2,1)}) %all-gather.5.cloned.1.call-update) | async-done | bytes 8388624 | tf_op jit(solution)/shard_map/all_gather | solution.py:100
  273.3 5.9 %fusion.27 = f32[64,2048]{1,0:T(8,128)} fusion(bf16[2048,2048]{1,0:T(8,128)(2,1)} %all-gather.5.cloned.1.call-done, bf16[8,8,16,128]{3,2,1,0:T(8,128)(2,1)} %bitcast.155), kind=kOutput, calls=%fused_computation.65 | convolution fusion | flops 536870912 | bytes 9175040 | tf_op jit(solution)/shard_map/dot_general | solution.py:169
  (115 shorter events, 41.4 us)
Async XLA Ops:
  7.2 97.3 %copy-start = (bf16[128,1024]{1,0:T(8,128)(2,1)S(1)}, bf16[128,1024]{1,0:T(8,128)(2,1)}, u32[]{:S(2)}) copy-start(bf16[128,1024]{1,0:T(8,128)(2,1)} %param.8) | copy-start | bytes 786436
  7.2 108.0 %all-gather.3.cloned.1.call-start = ((), (), s32[]{:S(2)}) async-start(), calls=%async_computation.1 | async-start | bytes 4456448 | tf_op jit(solution)/shard_map/all_gather | solution.py:98
  8.3 9.8 %collective-permute-start = (bf16[2,128,1024]{2,1,0:T(8,128)(2,1)S(1)}, bf16[2,128,1024]{2,1,0:T(8,128)(2,1)S(1)}, u32[]{:S(2)}, u32[]{:S(2)}) collective-permute-start(bf16[2,128,1024]{2,1,0:T(8,128)(2,1)S(1)} %pad_maximum_fusion.3), channel_id=1, source_target_pairs={{0,1},{1,2},{2,3},{3,4},{4,5},{5,6},{6,7},{7,8},{8,9},{9,10},{10,1... | collective-permute-start | bytes 1572872 | tf_op jit(solution)/shard_map/ppermute | solution.py:61
  19.0 22.4 %copy-start.14 = (s32[3]{0:T(128)S(1)}, s32[3]{0:T(128)}, u32[]{:S(2)}) copy-start(s32[3]{0:T(128)} %constant.73.clone) | copy-start | bytes 40
  21.2 28.4 %copy-start.13 = (s32[1,3]{1,0:T(1,128)S(1)}, s32[1,3]{1,0:T(1,128)}, u32[]{:S(2)}) copy-start(s32[1,3]{1,0:T(1,128)} %param.14) | copy-start | bytes 40
  22.2 4.0 %collective-permute-start.2 = (bf16[8,32768]{1,0:T(8,128)(2,1)}, bf16[8,32768]{1,0:T(8,128)(2,1)S(1)}, u32[]{:S(2)}, u32[]{:S(2)}) collective-permute-start(bf16[8,32768]{1,0:T(8,128)(2,1)} %select_n.251), channel_id=1, source_target_pairs={{0,1},{1,0},{2,3},{3,2},{4,5},{5,4},{6,7},{7,6},{8,9},{9,8},{10,11... | collective-permute-start | bytes 1572872 | tf_op jit(solution)/shard_map/ppermute | solution.py:24
  24.7 65.1 %copy-start.8 = (bf16[128,1024]{1,0:T(8,128)(2,1)S(1)}, bf16[128,1024]{1,0:T(8,128)(2,1)}, u32[]{:S(2)}) copy-start(bf16[128,1024]{1,0:T(8,128)(2,1)} %param.10) | copy-start | bytes 786436
  24.7 65.1 %copy-start.9 = (bf16[128,1024]{1,0:T(8,128)(2,1)S(1)}, bf16[128,1024]{1,0:T(8,128)(2,1)}, u32[]{:S(2)}) copy-start(bf16[128,1024]{1,0:T(8,128)(2,1)} %param.9) | copy-start | bytes 786436
  26.6 7.6 %collective-permute-start.3 = (bf16[4,32768]{1,0:T(4,128)(2,1)S(1)}, bf16[4,32768]{1,0:T(4,128)(2,1)S(1)}, u32[]{:S(2)}, u32[]{:S(2)}) collective-permute-start(bf16[4,32768]{1,0:T(4,128)(2,1)S(1)} %broadcast_select_fusion.4), channel_id=1, source_target_pairs={{0,2},{2,0},{4,6},{6,4},{8,10},{10,8},{12,14},{14,12},{1,3},{3,1},... | collective-permute-start | bytes 786440 | tf_op jit(solution)/shard_map/ppermute | solution.py:27
  34.6 3.9 %collective-permute-start.4 = (bf16[2,32768]{1,0:T(2,128)(2,1)S(1)}, bf16[2,32768]{1,0:T(2,128)(2,1)S(1)}, u32[]{:S(2)}, u32[]{:S(2)}) collective-permute-start(bf16[2,32768]{1,0:T(2,128)(2,1)S(1)} %broadcast_select_fusion.5), channel_id=1, source_target_pairs={{0,4},{2,6},{4,0},{6,2},{8,12},{10,14},{12,8},{14,10},{1,5},{3,7},... | collective-permute-start | bytes 393224 | tf_op jit(solution)/shard_map/ppermute | solution.py:27
  34.7 34.0 %collective-permute-start.1 = (bf16[2,128,1024]{2,1,0:T(8,128)(2,1)S(1)}, bf16[2,128,1024]{2,1,0:T(8,128)(2,1)S(1)}, u32[]{:S(2)}, u32[]{:S(2)}) collective-permute-start(bf16[2,128,1024]{2,1,0:T(8,128)(2,1)S(1)} %pad_maximum_fusion.3), channel_id=1, source_target_pairs={{1,0},{2,1},{3,2},{4,3},{5,4},{6,5},{7,6},{8,7},{9,8},{10,9},{11,1... | collective-permute-start | bytes 1572872 | tf_op jit(solution)/shard_map/ppermute | solution.py:62
  39.0 6.1 %collective-permute-start.5 = (bf16[1,32768]{1,0:T(2,128)(2,1)S(1)}, bf16[1,32768]{1,0:T(2,128)(2,1)S(1)}, u32[]{:S(2)}, u32[]{:S(2)}) collective-permute-start(bf16[1,32768]{1,0:T(2,128)(2,1)S(1)} %broadcast_select_fusion.9), channel_id=1, source_target_pairs={{0,8},{2,10},{4,12},{6,14},{8,0},{10,2},{12,4},{14,6},{1,9},{3,11}... | collective-permute-start | bytes 196616 | tf_op jit(solution)/shard_map/ppermute | solution.py:27
  45.4 9.5 %collective-permute-start.6 = (bf16[1,32768]{1,0:T(2,128)(2,1)S(1)}, bf16[1,32768]{1,0:T(2,128)(2,1)S(1)}, u32[]{:S(2)}, u32[]{:S(2)}) collective-permute-start(bf16[1,32768]{1,0:T(2,128)(2,1)S(1)} %fusion.35), channel_id=1, source_target_pairs={{0,8},{2,10},{4,12},{6,14},{8,0},{10,2},{12,4},{14,6},{1,9},{3,11}... | collective-permute-start | bytes 196616 | tf_op jit(solution)/shard_map/ppermute | solution.py:27
  55.6 12.5 %collective-permute-start.7 = (bf16[2,32768]{1,0:T(2,128)(2,1)S(1)}, bf16[2,32768]{1,0:T(2,128)(2,1)S(1)}, u32[]{:S(2)}, u32[]{:S(2)}) collective-permute-start(bf16[2,32768]{1,0:T(2,128)(2,1)S(1)} %broadcast_select_fusion.12), channel_id=1, source_target_pairs={{0,4},{2,6},{4,0},{6,2},{8,12},{10,14},{12,8},{14,10},{1,5},{3,7},... | collective-permute-start | bytes 393224 | tf_op jit(solution)/shard_map/ppermute | solution.py:27
  68.6 7.5 %collective-permute-start.8 = (bf16[4,32768]{1,0:T(4,128)(2,1)S(1)}, bf16[4,32768]{1,0:T(4,128)(2,1)S(1)}, u32[]{:S(2)}, u32[]{:S(2)}) collective-permute-start(bf16[4,32768]{1,0:T(4,128)(2,1)S(1)} %maximum_select_fusion.4), channel_id=1, source_target_pairs={{0,2},{2,0},{4,6},{6,4},{8,10},{10,8},{12,14},{14,12},{1,3},{3,1},... | collective-permute-start | bytes 786440 | tf_op jit(solution)/shard_map/ppermute | solution.py:27
  76.5 16.1 %collective-permute-start.9 = (bf16[8,32768]{1,0:T(8,128)(2,1)S(1)}, bf16[8,32768]{1,0:T(8,128)(2,1)S(1)}, u32[]{:S(2)}, u32[]{:S(2)}) collective-permute-start(bf16[8,32768]{1,0:T(8,128)(2,1)S(1)} %maximum_select_fusion.2), channel_id=1, source_target_pairs={{0,1},{1,0},{2,3},{3,2},{4,5},{5,4},{6,7},{7,6},{8,9},{9,8},{10,11... | collective-permute-start | bytes 1572872 | tf_op jit(solution)/shard_map/ppermute | solution.py:24
  104.5 2.3 copy-start.4
  105.3 1.6 copy-start.10
  106.8 2.1 copy-start.6
  106.9 8.3 %copy-start.12 = (bf16[128,2048]{1,0:T(8,128)(2,1)S(1)}, bf16[128,2048]{1,0:T(8,128)(2,1)}, u32[]{:S(2)}) copy-start(bf16[128,2048]{1,0:T(8,128)(2,1)} %param.12) | copy-start | bytes 1572868
  108.8 10.0 %copy-start.11 = (bf16[1,1024,1024]{1,2,0:T(8,128)(2,1)S(1)}, bf16[1,1024,1024]{1,2,0:T(8,128)(2,1)}, u32[]{:S(2)}) copy-start(bf16[1,1024,1024]{1,2,0:T(8,128)(2,1)} %copy.68) | copy-start | bytes 6291460
  108.8 40.8 %all-to-all-start = ((bf16[1,128,16,64]{1,3,0,2:T(8,128)(2,1)}), bf16[1,128,16,64]{1,3,0,2:T(8,128)(2,1)S(1)}, u32[]{:S(2)}, u32[]{:S(2)}) async-start(bf16[1,128,16,64]{1,3,0,2:T(8,128)(2,1)} %bitcast.32), calls=%async_computation | async-start | bytes 524288 | tf_op jit(solution)/shard_map/all_to_all | solution.py:166
  114.9 158.3 %all-gather.5.cloned.1.call-start = ((), (), s32[]{:S(2)}) async-start(), calls=%async_computation.2 | async-start | bytes 8912896 | tf_op jit(solution)/shard_map/all_gather | solution.py:100
  115.2 3.6 %copy-start.7 = (f32[8,128,1024]{1,2,0:T(8,128)S(1)}, f32[8,128,1024]{1,2,0:T(8,128)}, u32[]{:S(2)}) copy-start(f32[8,128,1024]{1,2,0:T(8,128)} %copy-done.6) | copy-start | bytes 12582916
  135.1 1.4 copy-start.5
  149.3 2.3 collective-permute-start.12
  152.9 7.6 %collective-permute-start.13 = (bf16[4,32768]{1,0:T(4,128)(2,1)S(1)}, bf16[4,32768]{1,0:T(4,128)(2,1)S(1)}, u32[]{:S(2)}, u32[]{:S(2)}) collective-permute-start(bf16[4,32768]{1,0:T(4,128)(2,1)S(1)} %select_convert_fusion.1), channel_id=1, source_target_pairs={{0,2},{2,0},{4,6},{6,4},{8,10},{10,8},{12,14},{14,12},{1,3},{3,1},... | collective-permute-start | bytes 786440 | tf_op jit(solution)/shard_map/ppermute | solution.py:27
  154.1 2.5 copy-start.3
  155.5 2.6 copy-start.2
  160.8 3.9 %collective-permute-start.14 = (bf16[2,32768]{1,0:T(2,128)(2,1)S(1)}, bf16[2,32768]{1,0:T(2,128)(2,1)S(1)}, u32[]{:S(2)}, u32[]{:S(2)}) collective-permute-start(bf16[2,32768]{1,0:T(2,128)(2,1)S(1)} %select_convert_fusion.2), channel_id=1, source_target_pairs={{0,4},{2,6},{4,0},{6,2},{8,12},{10,14},{12,8},{14,10},{1,5},{3,7},... | collective-permute-start | bytes 393224 | tf_op jit(solution)/shard_map/ppermute | solution.py:27
  165.1 5.5 %collective-permute-start.15 = (bf16[1,32768]{1,0:T(2,128)(2,1)S(1)}, bf16[1,32768]{1,0:T(2,128)(2,1)S(1)}, u32[]{:S(2)}, u32[]{:S(2)}) collective-permute-start(bf16[1,32768]{1,0:T(2,128)(2,1)S(1)} %fusion.38), channel_id=1, source_target_pairs={{0,8},{2,10},{4,12},{6,14},{8,0},{10,2},{12,4},{14,6},{1,9},{3,11}... | collective-permute-start | bytes 196616 | tf_op jit(solution)/shard_map/ppermute | solution.py:27
  170.8 5.4 %collective-permute-start.16 = (bf16[1,32768]{1,0:T(2,128)(2,1)S(1)}, bf16[1,32768]{1,0:T(2,128)(2,1)S(1)}, u32[]{:S(2)}, u32[]{:S(2)}) collective-permute-start(bf16[1,32768]{1,0:T(2,128)(2,1)S(1)} %fusion.37), channel_id=1, source_target_pairs={{0,8},{2,10},{4,12},{6,14},{8,0},{10,2},{12,4},{14,6},{1,9},{3,11}... | collective-permute-start | bytes 196616 | tf_op jit(solution)/shard_map/ppermute | solution.py:27
  176.8 5.1 %collective-permute-start.17 = (bf16[2,32768]{1,0:T(2,128)(2,1)S(1)}, bf16[2,32768]{1,0:T(2,128)(2,1)S(1)}, u32[]{:S(2)}, u32[]{:S(2)}) collective-permute-start(bf16[2,32768]{1,0:T(2,128)(2,1)S(1)} %broadcast_select_fusion.11), channel_id=1, source_target_pairs={{0,4},{2,6},{4,0},{6,2},{8,12},{10,14},{12,8},{14,10},{1,5},{3,7},... | collective-permute-start | bytes 393224 | tf_op jit(solution)/shard_map/ppermute | solution.py:27
  182.3 15.9 %collective-permute-start.18 = (bf16[4,32768]{1,0:T(4,128)(2,1)S(1)}, bf16[4,32768]{1,0:T(4,128)(2,1)}, u32[]{:S(2)}, u32[]{:S(2)}) collective-permute-start(bf16[4,32768]{1,0:T(4,128)(2,1)S(1)} %maximum_select_fusion.5), channel_id=1, source_target_pairs={{0,2},{2,0},{4,6},{6,4},{8,10},{10,8},{12,14},{14,12},{1,3},{3,1},... | collective-permute-start | bytes 786440 | tf_op jit(solution)/shard_map/ppermute | solution.py:27
  186.3 35.8 %collective-permute-start.11 = (bf16[2,256,1024]{2,1,0:T(8,128)(2,1)}, bf16[2,256,1024]{2,1,0:T(8,128)(2,1)}, u32[]{:S(2)}, u32[]{:S(2)}) collective-permute-start(bf16[2,256,1024]{2,1,0:T(8,128)(2,1)} %pad_maximum_fusion.2), channel_id=1, source_target_pairs={{1,0},{2,1},{3,2},{4,3},{5,4},{6,5},{7,6},{8,7},{9,8},{10,9},{11,1... | collective-permute-start | bytes 3145736 | tf_op jit(solution)/shard_map/ppermute | solution.py:62
  195.9 29.2 %collective-permute-start.10 = (bf16[2,256,1024]{2,1,0:T(8,128)(2,1)}, bf16[2,256,1024]{2,1,0:T(8,128)(2,1)}, u32[]{:S(2)}, u32[]{:S(2)}) collective-permute-start(bf16[2,256,1024]{2,1,0:T(8,128)(2,1)} %pad_maximum_fusion.2), channel_id=1, source_target_pairs={{0,1},{1,2},{2,3},{3,4},{4,5},{5,6},{6,7},{7,8},{8,9},{9,10},{10,1... | collective-permute-start | bytes 3145736 | tf_op jit(solution)/shard_map/ppermute | solution.py:61
  200.6 7.9 %collective-permute-start.19 = (bf16[8,32768]{1,0:T(8,128)(2,1)}, bf16[8,32768]{1,0:T(8,128)(2,1)}, u32[]{:S(2)}, u32[]{:S(2)}) collective-permute-start(bf16[8,32768]{1,0:T(8,128)(2,1)} %maximum_select_fusion.3), channel_id=1, source_target_pairs={{0,1},{1,0},{2,3},{3,2},{4,5},{5,4},{6,7},{7,6},{8,9},{9,8},{10,11... | collective-permute-start | bytes 1572872 | tf_op jit(solution)/shard_map/ppermute | solution.py:24
  273.3 5.9 %copy-start.1 = (bf16[128,1024]{1,0:T(8,128)(2,1)S(1)}, bf16[128,1024]{1,0:T(8,128)(2,1)}, u32[]{:S(2)}) copy-start(bf16[128,1024]{1,0:T(8,128)(2,1)} %param.8) | copy-start | bytes 786436
Sparse Core Ops, SparseCore 0:
  38.0 57.6 all-gather.2
  184.2 89.0 all-gather.4

commit v4 on v2

--- a/solution.py
+++ b/solution.py
@@ -3,6 +3,7 @@
 import jax
 import jax.numpy as jnp
 from jax import lax
+from jax.experimental import pallas as pl
 from jax.sharding import Mesh
 from jax.sharding import PartitionSpec as P
 
@@ -63,28 +64,46 @@
     return before, after
 
 
-def attend(q, k, v, live, up):
-    scale = 1.0 / math.sqrt(q.shape[-1])
-    scores = jnp.einsum("ihd,jhd->hij", q, k, preferred_element_type=jnp.float32) * scale
-    scores = jnp.where(live[None, None, :], scores, NEG_FILL)
+def _attn_kernel(live_ref, q_ref, k_ref, v_ref, up_ref, attn_ref, dq_ref, dk_ref, dv_ref):
+    scale = 1.0 / math.sqrt(q_ref.shape[-1])
+    q = q_ref[...]
+    k = k_ref[...]
+    v = v_ref[...]
+    up = up_ref[...]
+    nt = (((1,), (1,)), ((), ()))
+    tn = (((0,), (0,)), ((), ()))
+    scores = lax.dot_general(q, k, nt, preferred_element_type=jnp.float32) * scale
+    scores = jnp.where(live_ref[...] > 0, scores, NEG_FILL)
     top = jnp.max(scores, axis=-1, keepdims=True)
     raised = jnp.exp(scores - top)
     probs = raised / jnp.sum(raised, axis=-1, keepdims=True)
     probs_b = probs.astype(jnp.bfloat16)
-    attn = jnp.einsum("hij,jhd->ihd", probs_b, v, preferred_element_type=jnp.float32)
-    attn = attn.astype(jnp.bfloat16)
-    return probs, probs_b, attn
-
-
-def attend_back(q, k, v, probs, probs_b, up):
-    scale = 1.0 / math.sqrt(q.shape[-1])
-    dv = jnp.einsum("hij,ihd->jhd", probs_b, up, preferred_element_type=jnp.float32)
-    dprobs = jnp.einsum("ihd,jhd->hij", up, v, preferred_element_type=jnp.float32)
+    attn_ref[...] = jnp.dot(probs_b, v, preferred_element_type=jnp.float32).astype(attn_ref.dtype)
+    dv_ref[...] = lax.dot_general(probs_b, up, tn, preferred_element_type=jnp.float32)
+    dprobs = lax.dot_general(up, v, nt, preferred_element_type=jnp.float32)
     rowdot = jnp.sum(probs * dprobs, axis=-1, keepdims=True)
     dscores = (scale * probs * (dprobs - rowdot)).astype(jnp.bfloat16)
-    dq = jnp.einsum("hij,jhd->ihd", dscores, k, preferred_element_type=jnp.float32)
-    dk = jnp.einsum("hij,ihd->jhd", dscores, q, preferred_element_type=jnp.float32)
-    return dq, dk, dv
+    dq_ref[...] = jnp.dot(dscores, k, preferred_element_type=jnp.float32).astype(dq_ref.dtype)
+    dk_ref[...] = lax.dot_general(dscores, q, tn, preferred_element_type=jnp.float32)
+
+def attention(live, q, k, v, up, heads):
+    rows, features = q.shape
+    keys_n = k.shape[0]
+    hd = features // heads
+    qspec = pl.BlockSpec((rows, hd), lambda h: (0, h))
+    kspec = pl.BlockSpec((keys_n, hd), lambda h: (0, h))
+    return pl.pallas_call(
+        _attn_kernel,
+        grid=(heads,),
+        in_specs=[pl.BlockSpec((1, keys_n), lambda h: (0, 0)), qspec, kspec, kspec, qspec],
+        out_specs=[qspec, qspec, kspec, kspec],
+        out_shape=[
+            jax.ShapeDtypeStruct((rows, features), jnp.bfloat16),
+            jax.ShapeDtypeStruct((rows, features), jnp.bfloat16),
+            jax.ShapeDtypeStruct((keys_n, features), jnp.float32),
+            jax.ShapeDtypeStruct((keys_n, features), jnp.float32),
+        ],
+    )(live, q, k, v, up)
 
 
 def local(query, keys, values, out_weight, grad_out, global_blocks, random_blocks):
@@ -134,33 +153,40 @@
     )
     upstream = jnp.swapaxes(upstream, 0, 1).reshape(tok_rows, feature_count)
 
-    attn_rows, dq_rows, dk_ext, dv_ext = [], [], [], []
-    grad_ext = jnp.zeros((2, 3 * blocks_dev * BLK, feature_count), jnp.float32)
-    global_terms = []
+    attn_rows, dq_rows = [], []
+    grad_ext = [jnp.zeros((3 * blocks_dev * BLK, feature_count), jnp.float32) for _ in range(2)]
+    global_local = None
     for b in range(blocks_dev):
-        chosen = [
-            lax.dynamic_slice_in_dim(extended, ext_index[b, j] * BLK, BLK, axis=1)
-            for j in range(n_local)
-        ]
-        chosen += [global_kv[g] for g in range(slots)]
-        chosen = jnp.concatenate(chosen, axis=1).reshape(2, -1, H, hd)
-        live_rows = jnp.repeat(live[b], BLK)
-        q = query[b * BLK : (b + 1) * BLK].reshape(BLK, H, hd)
-        up = upstream[b * BLK : (b + 1) * BLK].reshape(BLK, H, hd)
-        probs, probs_b, attn = attend(q, chosen[0], chosen[1], live_rows, up)
-        dq, dk, dv = attend_back(q, chosen[0], chosen[1], probs, probs_b, up)
-        attn_rows.append(attn.reshape(BLK, feature_count))
-        dq_rows.append(dq.reshape(BLK, feature_count).astype(jnp.bfloat16))
-        dkv = jnp.stack([dk, dv]).reshape(2, -1, BLK, feature_count)
-        for j in range(n_local):
-            start = ext_index[b, j] * BLK
-            cur = lax.dynamic_slice_in_dim(grad_ext, start, BLK, axis=1)
-            grad_ext = lax.dynamic_update_slice_in_dim(grad_ext, cur + dkv[:, j], start, axis=1)
-        global_terms.append(dkv[:, n_local:])
-    global_local = global_terms[0]
-    for t in global_terms[1:]:
-        global_local = global_local + t
-    global_total = butterfly_sum(jnp.swapaxes(global_local, 0, 1), jnp.bfloat16)
+        chosen = []
+        for side in range(2):
+            parts = [
+                lax.dynamic_slice_in_dim(extended[side], ext_index[b, j] * BLK, BLK, axis=0)
+                for j in range(n_local)
+            ]
+            parts += [global_kv[g, side] for g in range(slots)]
+            chosen.append(jnp.concatenate(parts, axis=0))
+        live_rows = jnp.repeat(live[b], BLK).astype(jnp.float32)[None]
+        q = query[b * BLK : (b + 1) * BLK]
+        up = upstream[b * BLK : (b + 1) * BLK]
+        attn, dq, dk, dv = attention(live_rows, q, chosen[0], chosen[1], up, H)
+        attn_rows.append(attn)
+        dq_rows.append(dq)
+        for side, grad in enumerate((dk, dv)):
+            for j in range(n_local):
+                start = ext_index[b, j] * BLK
+                cur = lax.dynamic_slice_in_dim(grad_ext[side], start, BLK, axis=0)
+                term = grad[j * BLK : (j + 1) * BLK]
+                grad_ext[side] = lax.dynamic_update_slice_in_dim(
+                    grad_ext[side], cur + term, start, axis=0
+                )
+        terms = jnp.stack(
+            [dk[n_local * BLK :].reshape(slots, BLK, feature_count),
+             dv[n_local * BLK :].reshape(slots, BLK, feature_count)],
+            axis=1,
+        )
+        global_local = terms if global_local is None else global_local + terms
+    grad_ext = jnp.stack(grad_ext)
+    global_total = butterfly_sum(global_local, jnp.bfloat16)
 
     attn_out = jnp.concatenate(attn_rows, axis=0)
     layer_out = jnp.dot(attn_out, weight_all, preferred_element_type=jnp.float32).astype(

time: 278 us -> 258 us (0.928)
  local copies, waits for them, and re-layouts: 51.5 us -> 25.4 us
  Pallas kernels: 0 us -> 12.3 us
  matrix products: 26.2 us -> 15.5 us
  starting transfers between devices: 64.9 us -> 72 us
  waiting for transfers between devices: 91.1 us -> 86.5 us
  other arithmetic: 23.4 us -> 26.7 us
    pallas_call x0 -> x1, Pallas kernels: none -> 12.3 us  [attention(): pl.pallas_call(_attn_kernel, grid=(heads,), in_specs=[pl.BlockSpec((1, ke...]
    all_to_all x1, waiting for transfers between devices: 6.52 us -> 17.8 us  [local(): lax.all_to_all(attn_out.reshape(tok_rows, count, w_rows), SEQ, 1, 0, tile...]
    another operation x4 -> x2, local copies, waits for them, and re-layouts: 10.5 us -> 0.01 us  [the longest x2 10.5 us: local(): dkv = jnp.stack([dk, dv]).reshape(2, -1, BLK, feature_count)]
    dot_general x6 -> x0, matrix products: 10.4 us -> none  [the longest x1 3.39 us: attend_back(): jnp.einsum('ihd,jhd->hij', up, v, preferred_element_type=jnp.float32)]
    slice x4 -> x3, local copies, waits for them, and re-layouts: 12.4 us -> 3.4 us  [the longest x1 1.83 us: local(): dv[n_local * BLK:].reshape(slots, BLK, feature_count)]
    dynamic_update_slice x5 -> x11, other arithmetic: 0.98 us -> 8.6 us  [local(): lax.dynamic_update_slice_in_dim(grad_ext[side], cur + term, start, axis=0)]
    unnamed x44 -> x48, local copies, waits for them, and re-layouts: 10.6 us -> 3.75 us
    ppermute x12, waiting for transfers between devices: 53.6 us -> 46.7 us  [xor_swap(): return lax.ppermute(x, 'chip', [(i, i ^ m) for i in range(n)])]
  transfers between devices with their start and end apart: 24 -> 24, of which waited for: 18 -> 14; matrix products, arithmetic and copies ran while one was open for 32% -> 24% of each run, Pallas kernels for 0% -> 5%
where the time goes in v4:
time: 258 us; the launch traced here: 256 us
  waiting for transfers between devices  86.5 us (34%)
  starting transfers between devices  72 us (28%)
  other arithmetic  26.7 us (10%)
  local copies, waits for them, and re-layouts  25.4 us (10%)
  between operations  17.9 us (7%)
  matrix products  15.5 us (6%)
  Pallas kernels  12.3 us (5%)
    ppermute x12, waiting for transfers between devices, xor_swap(): return lax.ppermute(x, 'chip', [(i, i ^ m) for i in range(n)])  46.7 us
    ppermute x12, starting transfers between devices, xor_swap(): return lax.ppermute(x, 'chip', [(i, i ^ m) for i in range(n)])  42.5 us
    all_to_all x1, waiting for transfers between devices, local(): lax.all_to_all(attn_out.reshape(tok_rows, count, w_rows), SEQ, 1, 0, tile...  17.8 us
    pallas_call x1, Pallas kernels, attention(): pl.pallas_call(_attn_kernel, grid=(heads,), in_specs=[pl.BlockSpec((1, ke...  12.3 us
    ppermute x2, waiting for transfers between devices, halo(): after = lax.ppermute(shard, SEQ, down)  9.58 us
    dynamic_update_slice x11, other arithmetic, local(): lax.dynamic_update_slice_in_dim(grad_ext[side], cur + term, start, axis=0)  8.6 us
    all_to_all x1, waiting for transfers between devices, local(): lax.all_to_all(upstream_cols.reshape(count, tok_rows, w_rows), SEQ, 0, 0,...  7.57 us
    all_to_all x1, starting transfers between devices, local(): lax.all_to_all(upstream_cols.reshape(count, tok_rows, w_rows), SEQ, 0, 0,...  6.82 us
  transfers between devices with their start and end apart: 24, of which 14 were waited for; matrix products, arithmetic and copies ran while one was open for 24% of the time, Pallas kernels for 5%

profile of v4, /device:TPU:11, one launch (start us, length us, event | category | flops | bytes accessed | tf_op | source)
XLA Modules:
  0.0 256.3 jit_solution(9879455543950482965)
XLA Ops:
  8.0 1.3 fusion.35
  10.6 1.9 broadcast_select_fusion.3
  12.5 3.7 %collective-permute-start = (bf16[2,128,1024]{2,1,0:T(8,128)(2,1)}, bf16[2,128,1024]{2,1,0:T(8,128)(2,1)S(1)}, u32[]{:S(2)}, u32[]{:S(2)}) collective-permute-start(bf16[2,128,1024]{2,1,0:T(8,128)(2,1)} %get-tuple-element.30), channel_id=1, source_target_pairs={{0,1},{1,2},{2,3},{3,4},{4,5},{5,6},{6,7},{7,8},{8,9},{9,10},{10,1... | collective-permute-start | bytes 1572872 | tf_op jit(solution)/shard_map/ppermute | solution.py:62
  16.2 1.9 collective-permute-start.1
  19.2 1.5 collective-permute-start.2
  24.5 4.1 %collective-permute-done = bf16[2,128,1024]{2,1,0:T(8,128)(2,1)S(1)} collective-permute-done((bf16[2,128,1024]{2,1,0:T(8,128)(2,1)}, bf16[2,128,1024]{2,1,0:T(8,128)(2,1)S(1)}, u32[]{:S(2)}, u32[]{:S(2)}) %collective-permute-start) | collective-permute-done | bytes 524320 | tf_op jit(solution)/shard_map/ppermute | solution.py:62
  28.6 9.6 %collective-permute-done.1 = bf16[2,128,1024]{2,1,0:T(8,128)(2,1)S(1)} collective-permute-done((bf16[2,128,1024]{2,1,0:T(8,128)(2,1)}, bf16[2,128,1024]{2,1,0:T(8,128)(2,1)S(1)}, u32[]{:S(2)}, u32[]{:S(2)}) %collective-permute-start.1) | collective-permute-done | bytes 524320 | tf_op jit(solution)/shard_map/ppermute | solution.py:63
  40.2 5.2 %collective-permute-done.4 = bf16[2,32768]{1,0:T(2,128)(2,1)S(1)} collective-permute-done((bf16[2,32768]{1,0:T(2,128)(2,1)S(1)}, bf16[2,32768]{1,0:T(2,128)(2,1)S(1)}, u32[]{:S(2)}, u32[]{:S(2)}) %collective-permute-start.4) | collective-permute-done | bytes 131104 | tf_op jit(solution)/shard_map/ppermute | solution.py:28
  45.9 1.9 collective-permute-start.5
  47.8 2.9 %collective-permute-done.5 = bf16[1,32768]{1,0:T(2,128)(2,1)S(1)} collective-permute-done((bf16[1,32768]{1,0:T(2,128)(2,1)S(1)}, bf16[1,32768]{1,0:T(2,128)(2,1)S(1)}, u32[]{:S(2)}, u32[]{:S(2)}) %collective-permute-start.5) | collective-permute-done | bytes 65568 | tf_op jit(solution)/shard_map/ppermute | solution.py:28
  51.0 1.8 collective-permute-start.6
  52.9 14.2 %collective-permute-done.6 = bf16[1,32768]{1,0:T(2,128)(2,1)S(1)} collective-permute-done((bf16[1,32768]{1,0:T(2,128)(2,1)S(1)}, bf16[1,32768]{1,0:T(2,128)(2,1)S(1)}, u32[]{:S(2)}, u32[]{:S(2)}) %collective-permute-start.6) | collective-permute-done | bytes 65568 | tf_op jit(solution)/shard_map/ppermute | solution.py:28
  67.7 1.9 collective-permute-start.7
  69.6 5.5 %collective-permute-done.7 = bf16[2,32768]{1,0:T(2,128)(2,1)S(1)} collective-permute-done((bf16[2,32768]{1,0:T(2,128)(2,1)S(1)}, bf16[2,32768]{1,0:T(2,128)(2,1)S(1)}, u32[]{:S(2)}, u32[]{:S(2)}) %collective-permute-start.7) | collective-permute-done | bytes 131104 | tf_op jit(solution)/shard_map/ppermute | solution.py:28
  75.6 22.8 %collective-permute-start.8 = (bf16[4,32768]{1,0:T(4,128)(2,1)S(1)}, bf16[4,32768]{1,0:T(4,128)(2,1)S(1)}, u32[]{:S(2)}, u32[]{:S(2)}) collective-permute-start(bf16[4,32768]{1,0:T(4,128)(2,1)S(1)} %maximum_select_fusion.4), channel_id=1, source_target_pairs={{0,2},{2,0},{4,6},{6,4},{8,10},{10,8},{12,14},{14,12},{1,3},{3,1},... | collective-permute-start | bytes 786440 | tf_op jit(solution)/shard_map/ppermute | solution.py:28
  98.5 1.4 copy-done.9
  99.9 4.2 %collective-permute-done.8 = bf16[4,32768]{1,0:T(4,128)(2,1)S(1)} collective-permute-done((bf16[4,32768]{1,0:T(4,128)(2,1)S(1)}, bf16[4,32768]{1,0:T(4,128)(2,1)S(1)}, u32[]{:S(2)}, u32[]{:S(2)}) %collective-permute-start.8) | collective-permute-done | bytes 262176 | tf_op jit(solution)/shard_map/ppermute | solution.py:28
  104.6 1.6 collective-permute-start.9
  106.2 6.0 %fusion.1 = bf16[8,16,8,128]{3,2,1,0:T(8,128)(2,1)S(1)} fusion(bf16[2048,2048]{1,0:T(8,128)(2,1)} %all-gather.3.cloned.1.call-done, bf16[64,2048]{1,0:T(8,128)(2,1)S(1)} %copy-done.13), kind=kOutput, calls=%fused_computation.11 | convolution fusion | flops 537001984 | bytes 8912896 | tf_op jit(solution)/shard_map/dot_general | solution.py:148
  113.0 6.8 %all-to-all-start = ((bf16[16,128,64]{1,2,0:T(8,128)(2,1)}), bf16[16,128,64]{1,2,0:T(8,128)(2,1)S(1)}, u32[]{:S(2)}, u32[]{:S(2)}) async-start(bf16[16,128,64]{1,2,0:T(8,128)(2,1)} %bitcast.113), calls=%async_computation | async-start | bytes 524288 | tf_op jit(solution)/shard_map/all_to_all | solution.py:151
  122.3 7.6 %all-to-all-done = bf16[16,128,64]{1,2,0:T(8,128)(2,1)S(1)} async-done(((bf16[16,128,64]{1,2,0:T(8,128)(2,1)}), bf16[16,128,64]{1,2,0:T(8,128)(2,1)S(1)}, u32[]{:S(2)}, u32[]{:S(2)}) %all-to-all-start) | async-done | bytes 262176 | tf_op jit(solution)/shard_map/all_to_all | solution.py:151
  131.4 12.3 %shard_map.119 = (bf16[128,1024]{1,0:T(8,128)(2,1)}, bf16[128,1024]{1,0:T(8,128)(2,1)}, f32[1024,1024]{1,0:T(8,128)}, f32[1024,1024]{1,0:T(8,128)}) custom-call(f32[1,1024]{1,0:T(1,128)} %bitcast.127, bf16[128,1024]{1,0:T(8,128)(2,1)} %q_ref.1, bf16[1024,1024]{1,0:T(8,128)(2,1)} %get-tuple-element.20.k_ref, bf16[1024,1024]{1,0:T(8,128)(2,1)} %get-tuple-element.19.v_ref, ...), custom_call_target="tpu_custom_call" | custom-call | tf_op jit(solution)/shard_map/pallas_call | solution.py:95
  143.7 1.4 slice.234
  145.2 1.8 slice.235
  147.0 2.2 slice_select_fusion
  151.8 2.1 convert_element_type.83
  154.1 2.7 %broadcast_select_fusion = f32[1,2,128,1024]{3,2,0,1:T(8,128)} fusion(pred[]{:T(512)S(6)} %eq.17, f32[2,1,128,1024]{3,2,0,1:T(8,128)} %bitcast.119, f32[2,1,128,1024]{3,2,0,1:T(8,128)} %bitcast.117), kind=kLoop, calls=%fused_computation.48 | loop fusion | flops 786432 | bytes 3145729 | tf_op jit(solution)/shard_map/jit(_where)/select_n | solution.py:43
  156.8 2.4 select_n.280
  159.2 1.3 fusion.13
  163.0 1.6 collective-permute-start.13
  167.0 3.6 %collective-permute-done.13 = bf16[4,32768]{1,0:T(4,128)(2,1)S(1)} collective-permute-done((bf16[4,32768]{1,0:T(4,128)(2,1)S(1)}, bf16[4,32768]{1,0:T(4,128)(2,1)S(1)}, u32[]{:S(2)}, u32[]{:S(2)}) %collective-permute-start.13) | collective-permute-done | bytes 262176 | tf_op jit(solution)/shard_map/ppermute | solution.py:28
  171.0 1.7 collective-permute-start.14
  175.5 2.2 collective-permute-start.15
  178.0 4.8 %collective-permute-done.15 = bf16[1,32768]{1,0:T(2,128)(2,1)S(1)} collective-permute-done((bf16[1,32768]{1,0:T(2,128)(2,1)S(1)}, bf16[1,32768]{1,0:T(2,128)(2,1)S(1)}, u32[]{:S(2)}, u32[]{:S(2)}) %collective-permute-start.15) | collective-permute-done | bytes 65568 | tf_op jit(solution)/shard_map/ppermute | solution.py:28
  183.0 3.3 %collective-permute-start.16 = (bf16[1,32768]{1,0:T(2,128)(2,1)S(1)}, bf16[1,32768]{1,0:T(2,128)(2,1)S(1)}, u32[]{:S(2)}, u32[]{:S(2)}) collective-permute-start(bf16[1,32768]{1,0:T(2,128)(2,1)S(1)} %fusion.28), channel_id=1, source_target_pairs={{0,8},{2,10},{4,12},{6,14},{8,0},{10,2},{12,4},{14,6},{1,9},{3,11}... | collective-permute-start | bytes 196616 | tf_op jit(solution)/shard_map/ppermute | solution.py:28
  186.4 4.0 %collective-permute-done.16 = bf16[1,32768]{1,0:T(2,128)(2,1)S(1)} collective-permute-done((bf16[1,32768]{1,0:T(2,128)(2,1)S(1)}, bf16[1,32768]{1,0:T(2,128)(2,1)S(1)}, u32[]{:S(2)}, u32[]{:S(2)}) %collective-permute-start.16) | collective-permute-done | bytes 65568 | tf_op jit(solution)/shard_map/ppermute | solution.py:28
  191.0 3.5 %collective-permute-start.17 = (bf16[2,32768]{1,0:T(2,128)(2,1)S(1)}, bf16[2,32768]{1,0:T(2,128)(2,1)S(1)}, u32[]{:S(2)}, u32[]{:S(2)}) collective-permute-start(bf16[2,32768]{1,0:T(2,128)(2,1)S(1)} %broadcast_select_fusion.12), channel_id=1, source_target_pairs={{0,4},{2,6},{4,0},{6,2},{8,12},{10,14},{12,8},{14,10},{1,5},{3,7},... | collective-permute-start | bytes 393224 | tf_op jit(solution)/shard_map/ppermute | solution.py:28
  195.5 2.3 collective-permute-start.10
  197.9 2.5 collective-permute-start.11
  201.2 5.6 %all-to-all-start.1 = ((bf16[1,128,16,64]{1,3,0,2:T(8,128)(2,1)}), bf16[1,128,16,64]{1,3,0,2:T(8,128)(2,1)S(1)}, u32[]{:S(2)}, u32[]{:S(2)}) async-start(bf16[1,128,16,64]{1,3,0,2:T(8,128)(2,1)} %bitcast.35), calls=%async_computation.1 | async-start | bytes 524288 | tf_op jit(solution)/shard_map/all_to_all | solution.py:195
  208.6 3.7 %convolution_convert_fusion = bf16[128,2048]{1,0:T(8,128)(2,1)} fusion(bf16[128,1024]{1,0:T(8,128)(2,1)S(1)} %copy-done.14, bf16[1024,2048]{1,0:T(8,128)(2,1)} %all-gather.5.cloned.1.call-done), kind=kOutput, calls=%fused_computation.4 | convolution fusion | flops 537133056 | bytes 4980736 | tf_op jit(solution)/shard_map/dot_general | solution.py:192
  212.3 17.8 %all-to-all-done.1 = bf16[1,128,16,64]{1,3,0,2:T(8,128)(2,1)S(1)} async-done(((bf16[1,128,16,64]{1,3,0,2:T(8,128)(2,1)}), bf16[1,128,16,64]{1,3,0,2:T(8,128)(2,1)S(1)}, u32[]{:S(2)}, u32[]{:S(2)}) %all-to-all-start.1) | async-done | bytes 262176 | tf_op jit(solution)/shard_map/all_to_all | solution.py:195
  230.7 3.3 %collective-permute-start.19 = (bf16[8,32768]{1,0:T(8,128)(2,1)S(1)}, bf16[8,32768]{1,0:T(8,128)(2,1)S(1)}, u32[]{:S(2)}, u32[]{:S(2)}) collective-permute-start(bf16[8,32768]{1,0:T(8,128)(2,1)S(1)} %maximum_select_fusion.3), channel_id=1, source_target_pairs={{0,1},{1,0},{2,3},{3,2},{4,5},{5,4},{6,7},{7,6},{8,9},{9,8},{10,11... | collective-permute-start | bytes 1572872 | tf_op jit(solution)/shard_map/ppermute | solution.py:25
  234.0 5.7 %fusion.15 = f32[64,2048]{1,0:T(8,128)} fusion(bf16[2048,2048]{1,0:T(8,128)(2,1)} %all-gather.3.cloned.1.call-done, bf16[8,8,16,128]{3,2,1,0:T(8,128)(2,1)S(1)} %bitcast.124), kind=kOutput, calls=%fused_computation.53 | convolution fusion | flops 536870912 | bytes 9175040 | tf_op jit(solution)/shard_map/dot_general | solution.py:198
  239.9 1.4 fusion.10
  241.3 2.6 %reshape.115 = f32[2,128,1024]{2,1,0:T(8,128)} reshape(f32[8,32768]{1,0:T(8,128)} %get-tuple-element.17) | data formatting | bytes 2097152 | tf_op jit(solution)/shard_map/convert_element_type | solution.py:213
  243.9 2.4 reshape.116
  246.3 2.3 fusion.8
  (120 shorter events, 29.8 us)
Async XLA Ops:
  7.2 13.6 %copy-start.16 = (s32[1,3]{1,0:T(1,128)S(1)}, s32[1,3]{1,0:T(1,128)}, u32[]{:S(2)}) copy-start(s32[1,3]{1,0:T(1,128)} %param.14) | copy-start | bytes 40
  7.2 99.0 %all-gather.3.cloned.1.call-start = ((), (), s32[]{:S(2)}) async-start(), calls=%async_computation.2 | async-start | bytes 8912896 | tf_op jit(solution)/shard_map/all_gather | solution.py:117
  7.9 200.7 %all-gather.5.cloned.1.call-start = ((), (), s32[]{:S(2)}) async-start(), calls=%async_computation.3 | async-start | bytes 4456448 | tf_op jit(solution)/shard_map/all_gather | solution.py:118
  10.6 13.0 %copy-start.17 = (s32[3]{0:T(128)S(1)}, s32[3]{0:T(128)}, u32[]{:S(2)}) copy-start(s32[3]{0:T(128)} %constant.80.clone) | copy-start | bytes 40
  12.5 16.0 %collective-permute-start = (bf16[2,128,1024]{2,1,0:T(8,128)(2,1)}, bf16[2,128,1024]{2,1,0:T(8,128)(2,1)S(1)}, u32[]{:S(2)}, u32[]{:S(2)}) collective-permute-start(bf16[2,128,1024]{2,1,0:T(8,128)(2,1)} %get-tuple-element.30), channel_id=1, source_target_pairs={{0,1},{1,2},{2,3},{3,4},{4,5},{5,6},{6,7},{7,8},{8,9},{9,10},{10,1... | collective-permute-start | bytes 1572872 | tf_op jit(solution)/shard_map/ppermute | solution.py:62
  16.2 21.9 %collective-permute-start.1 = (bf16[2,128,1024]{2,1,0:T(8,128)(2,1)}, bf16[2,128,1024]{2,1,0:T(8,128)(2,1)S(1)}, u32[]{:S(2)}, u32[]{:S(2)}) collective-permute-start(bf16[2,128,1024]{2,1,0:T(8,128)(2,1)} %get-tuple-element.30), channel_id=1, source_target_pairs={{1,0},{2,1},{3,2},{4,3},{5,4},{6,5},{7,6},{8,7},{9,8},{10,9},{11,1... | collective-permute-start | bytes 1572872 | tf_op jit(solution)/shard_map/ppermute | solution.py:63
  19.2 19.0 %copy-start.11 = (bf16[128,1024]{1,0:T(8,128)(2,1)S(1)}, bf16[128,1024]{1,0:T(8,128)(2,1)}, u32[]{:S(2)}) copy-start(bf16[128,1024]{1,0:T(8,128)(2,1)} %param.10) | copy-start | bytes 786436
  19.2 19.0 %copy-start.12 = (bf16[128,1024]{1,0:T(8,128)(2,1)S(1)}, bf16[128,1024]{1,0:T(8,128)(2,1)}, u32[]{:S(2)}) copy-start(bf16[128,1024]{1,0:T(8,128)(2,1)} %param.9) | copy-start | bytes 786436
  19.2 4.5 %collective-permute-start.2 = (bf16[8,32768]{1,0:T(8,128)(2,1)}, bf16[8,32768]{1,0:T(8,128)(2,1)S(1)}, u32[]{:S(2)}, u32[]{:S(2)}) collective-permute-start(bf16[8,32768]{1,0:T(8,128)(2,1)} %select_n.265), channel_id=1, source_target_pairs={{0,1},{1,0},{2,3},{3,2},{4,5},{5,4},{6,7},{7,6},{8,9},{9,8},{10,11... | collective-permute-start | bytes 1572872 | tf_op jit(solution)/shard_map/ppermute | solution.py:25
  24.1 15.3 %collective-permute-start.3 = (bf16[4,32768]{1,0:T(4,128)(2,1)S(1)}, bf16[4,32768]{1,0:T(4,128)(2,1)S(1)}, u32[]{:S(2)}, u32[]{:S(2)}) collective-permute-start(bf16[4,32768]{1,0:T(4,128)(2,1)S(1)} %broadcast_select_fusion.5), channel_id=1, source_target_pairs={{0,2},{2,0},{4,6},{6,4},{8,10},{10,8},{12,14},{14,12},{1,3},{3,1},... | collective-permute-start | bytes 786440 | tf_op jit(solution)/shard_map/ppermute | solution.py:28
  39.9 5.6 %collective-permute-start.4 = (bf16[2,32768]{1,0:T(2,128)(2,1)S(1)}, bf16[2,32768]{1,0:T(2,128)(2,1)S(1)}, u32[]{:S(2)}, u32[]{:S(2)}) collective-permute-start(bf16[2,32768]{1,0:T(2,128)(2,1)S(1)} %broadcast_select_fusion.6), channel_id=1, source_target_pairs={{0,4},{2,6},{4,0},{6,2},{8,12},{10,14},{12,8},{14,10},{1,5},{3,7},... | collective-permute-start | bytes 393224 | tf_op jit(solution)/shard_map/ppermute | solution.py:28
  45.9 4.8 %collective-permute-start.5 = (bf16[1,32768]{1,0:T(2,128)(2,1)S(1)}, bf16[1,32768]{1,0:T(2,128)(2,1)S(1)}, u32[]{:S(2)}, u32[]{:S(2)}) collective-permute-start(bf16[1,32768]{1,0:T(2,128)(2,1)S(1)} %broadcast_select_fusion.10), channel_id=1, source_target_pairs={{0,8},{2,10},{4,12},{6,14},{8,0},{10,2},{12,4},{14,6},{1,9},{3,11}... | collective-permute-start | bytes 196616 | tf_op jit(solution)/shard_map/ppermute | solution.py:28
  51.0 16.1 %collective-permute-start.6 = (bf16[1,32768]{1,0:T(2,128)(2,1)S(1)}, bf16[1,32768]{1,0:T(2,128)(2,1)S(1)}, u32[]{:S(2)}, u32[]{:S(2)}) collective-permute-start(bf16[1,32768]{1,0:T(2,128)(2,1)S(1)} %fusion.26), channel_id=1, source_target_pairs={{0,8},{2,10},{4,12},{6,14},{8,0},{10,2},{12,4},{14,6},{1,9},{3,11}... | collective-permute-start | bytes 196616 | tf_op jit(solution)/shard_map/ppermute | solution.py:28
  67.7 38.5 %copy-start.13 = (bf16[64,2048]{1,0:T(8,128)(2,1)S(1)}, bf16[64,2048]{1,0:T(8,128)(2,1)}, u32[]{:S(2)}) copy-start(bf16[64,2048]{1,0:T(8,128)(2,1)} %param.11) | copy-start | bytes 786436
  67.7 7.4 %collective-permute-start.7 = (bf16[2,32768]{1,0:T(2,128)(2,1)S(1)}, bf16[2,32768]{1,0:T(2,128)(2,1)S(1)}, u32[]{:S(2)}, u32[]{:S(2)}) collective-permute-start(bf16[2,32768]{1,0:T(2,128)(2,1)S(1)} %broadcast_select_fusion.13), channel_id=1, source_target_pairs={{0,4},{2,6},{4,0},{6,2},{8,12},{10,14},{12,8},{14,10},{1,5},{3,7},... | collective-permute-start | bytes 393224 | tf_op jit(solution)/shard_map/ppermute | solution.py:28
  75.6 28.5 %collective-permute-start.8 = (bf16[4,32768]{1,0:T(4,128)(2,1)S(1)}, bf16[4,32768]{1,0:T(4,128)(2,1)S(1)}, u32[]{:S(2)}, u32[]{:S(2)}) collective-permute-start(bf16[4,32768]{1,0:T(4,128)(2,1)S(1)} %maximum_select_fusion.4), channel_id=1, source_target_pairs={{0,2},{2,0},{4,6},{6,4},{8,10},{10,8},{12,14},{14,12},{1,3},{3,1},... | collective-permute-start | bytes 786440 | tf_op jit(solution)/shard_map/ppermute | solution.py:28
  98.5 5.6 %copy-start.10 = (bf16[1024,1024]{1,0:T(8,128)(2,1)}, bf16[1024,1024]{1,0:T(8,128)(2,1)S(1)}, u32[]{:S(2)}) copy-start(bf16[1024,1024]{1,0:T(8,128)(2,1)S(1)} %bitcast_dynamic-update-slice_fusion.5) | copy-start | bytes 6291460
  98.5 1.4 copy-start.9
  104.6 15.3 %collective-permute-start.9 = (bf16[8,32768]{1,0:T(8,128)(2,1)S(1)}, bf16[8,32768]{1,0:T(8,128)(2,1)S(1)}, u32[]{:S(2)}, u32[]{:S(2)}) collective-permute-start(bf16[8,32768]{1,0:T(8,128)(2,1)S(1)} %maximum_select_fusion.2), channel_id=1, source_target_pairs={{0,1},{1,0},{2,3},{3,2},{4,5},{5,4},{6,7},{7,6},{8,9},{9,8},{10,11... | collective-permute-start | bytes 1572872 | tf_op jit(solution)/shard_map/ppermute | solution.py:25
  113.0 16.8 %all-to-all-start = ((bf16[16,128,64]{1,2,0:T(8,128)(2,1)}), bf16[16,128,64]{1,2,0:T(8,128)(2,1)S(1)}, u32[]{:S(2)}, u32[]{:S(2)}) async-start(bf16[16,128,64]{1,2,0:T(8,128)(2,1)} %bitcast.113), calls=%async_computation | async-start | bytes 524288 | tf_op jit(solution)/shard_map/all_to_all | solution.py:151
  143.7 3.3 %copy-start.6 = (f32[1024,1024]{1,0:T(8,128)S(1)}, f32[1024,1024]{1,0:T(8,128)}, u32[]{:S(2)}) copy-start(f32[1024,1024]{1,0:T(8,128)} %get-tuple-element.11) | copy-start | bytes 12582916
  143.7 3.3 %copy-start.15 = (pred[384]{0:T(512)(128)(4,1)S(1)}, pred[384]{0:T(512)(128)(4,1)}, u32[]{:S(2)}) copy-start(pred[384]{0:T(512)(128)(4,1)} %constant.102) | copy-start | bytes 1156
  145.2 5.7 %copy-start.4 = (f32[256,1024]{1,0:T(8,128)}, f32[256,1024]{1,0:T(8,128)S(1)}, u32[]{:S(2)}) copy-start(f32[256,1024]{1,0:T(8,128)S(1)} %slice.234) | copy-start | bytes 3145732
  147.0 3.9 %copy-start.5 = (f32[256,1024]{1,0:T(8,128)}, f32[256,1024]{1,0:T(8,128)S(1)}, u32[]{:S(2)}) copy-start(f32[256,1024]{1,0:T(8,128)S(1)} %slice.235) | copy-start | bytes 3145732
  147.0 3.2 %copy-start.7 = (f32[1024,1024]{1,0:T(8,128)S(1)}, f32[1024,1024]{1,0:T(8,128)}, u32[]{:S(2)}) copy-start(f32[1024,1024]{1,0:T(8,128)} %get-tuple-element.12) | copy-start | bytes 12582916
  153.9 7.7 %collective-permute-start.12 = (bf16[8,32768]{1,0:T(8,128)(2,1)}, bf16[8,32768]{1,0:T(8,128)(2,1)}, u32[]{:S(2)}, u32[]{:S(2)}) collective-permute-start(bf16[8,32768]{1,0:T(8,128)(2,1)} %convert_element_type.83), channel_id=1, source_target_pairs={{0,1},{1,0},{2,3},{3,2},{4,5},{5,4},{6,7},{7,6},{8,9},{9,8},{10,11... | collective-permute-start | bytes 1572872 | tf_op jit(solution)/shard_map/ppermute | solution.py:25
  159.2 2.4 copy-start.8
  163.0 7.7 %collective-permute-start.13 = (bf16[4,32768]{1,0:T(4,128)(2,1)S(1)}, bf16[4,32768]{1,0:T(4,128)(2,1)S(1)}, u32[]{:S(2)}, u32[]{:S(2)}) collective-permute-start(bf16[4,32768]{1,0:T(4,128)(2,1)S(1)} %select_convert_fusion.1), channel_id=1, source_target_pairs={{0,2},{2,0},{4,6},{6,4},{8,10},{10,8},{12,14},{14,12},{1,3},{3,1},... | collective-permute-start | bytes 786440 | tf_op jit(solution)/shard_map/ppermute | solution.py:28
  167.0 10.7 %copy-start.2 = (f32[1,384,1024]{2,1,0:T(8,128)}, f32[1,384,1024]{2,1,0:T(8,128)S(1)}, u32[]{:S(2)}) copy-start(f32[1,384,1024]{2,1,0:T(8,128)S(1)} %bitcast_dynamic-update-slice_fusion) | copy-start | bytes 4718596
  171.0 4.1 %collective-permute-start.14 = (bf16[2,32768]{1,0:T(2,128)(2,1)S(1)}, bf16[2,32768]{1,0:T(2,128)(2,1)S(1)}, u32[]{:S(2)}, u32[]{:S(2)}) collective-permute-start(bf16[2,32768]{1,0:T(2,128)(2,1)S(1)} %select_convert_fusion.2), channel_id=1, source_target_pairs={{0,4},{2,6},{4,0},{6,2},{8,12},{10,14},{12,8},{14,10},{1,5},{3,7},... | collective-permute-start | bytes 393224 | tf_op jit(solution)/shard_map/ppermute | solution.py:28
  173.9 4.1 %copy-start = (f32[1,384,1024]{2,1,0:T(8,128)}, f32[1,384,1024]{2,1,0:T(8,128)S(1)}, u32[]{:S(2)}) copy-start(f32[1,384,1024]{2,1,0:T(8,128)S(1)} %bitcast_dynamic-update-slice_fusion.1) | copy-start | bytes 4718596
  175.5 7.3 %collective-permute-start.15 = (bf16[1,32768]{1,0:T(2,128)(2,1)S(1)}, bf16[1,32768]{1,0:T(2,128)(2,1)S(1)}, u32[]{:S(2)}, u32[]{:S(2)}) collective-permute-start(bf16[1,32768]{1,0:T(2,128)(2,1)S(1)} %fusion.29), channel_id=1, source_target_pairs={{0,8},{2,10},{4,12},{6,14},{8,0},{10,2},{12,4},{14,6},{1,9},{3,11}... | collective-permute-start | bytes 196616 | tf_op jit(solution)/shard_map/ppermute | solution.py:28
  183.0 17.4 %copy-start.14 = (bf16[128,1024]{1,0:T(8,128)(2,1)S(1)}, bf16[128,1024]{1,0:T(8,128)(2,1)}, u32[]{:S(2)}) copy-start(bf16[128,1024]{1,0:T(8,128)(2,1)} %get-tuple-element.9) | copy-start | bytes 786436
  183.0 7.4 %collective-permute-start.16 = (bf16[1,32768]{1,0:T(2,128)(2,1)S(1)}, bf16[1,32768]{1,0:T(2,128)(2,1)S(1)}, u32[]{:S(2)}, u32[]{:S(2)}) collective-permute-start(bf16[1,32768]{1,0:T(2,128)(2,1)S(1)} %fusion.28), channel_id=1, source_target_pairs={{0,8},{2,10},{4,12},{6,14},{8,0},{10,2},{12,4},{14,6},{1,9},{3,11}... | collective-permute-start | bytes 196616 | tf_op jit(solution)/shard_map/ppermute | solution.py:28
  191.0 15.8 %collective-permute-start.17 = (bf16[2,32768]{1,0:T(2,128)(2,1)S(1)}, bf16[2,32768]{1,0:T(2,128)(2,1)S(1)}, u32[]{:S(2)}, u32[]{:S(2)}) collective-permute-start(bf16[2,32768]{1,0:T(2,128)(2,1)S(1)} %broadcast_select_fusion.12), channel_id=1, source_target_pairs={{0,4},{2,6},{4,0},{6,2},{8,12},{10,14},{12,8},{14,10},{1,5},{3,7},... | collective-permute-start | bytes 393224 | tf_op jit(solution)/shard_map/ppermute | solution.py:28
  195.5 50.8 %collective-permute-start.10 = (bf16[2,256,1024]{2,1,0:T(8,128)(2,1)}, bf16[2,256,1024]{2,1,0:T(8,128)(2,1)}, u32[]{:S(2)}, u32[]{:S(2)}) collective-permute-start(bf16[2,256,1024]{2,1,0:T(8,128)(2,1)} %pad_maximum_fusion.3), channel_id=1, source_target_pairs={{0,1},{1,2},{2,3},{3,4},{4,5},{5,6},{6,7},{7,8},{8,9},{9,10},{10,1... | collective-permute-start | bytes 3145736 | tf_op jit(solution)/shard_map/ppermute | solution.py:62
  197.9 48.5 %collective-permute-start.11 = (bf16[2,256,1024]{2,1,0:T(8,128)(2,1)}, bf16[2,256,1024]{2,1,0:T(8,128)(2,1)}, u32[]{:S(2)}, u32[]{:S(2)}) collective-permute-start(bf16[2,256,1024]{2,1,0:T(8,128)(2,1)} %pad_maximum_fusion.3), channel_id=1, source_target_pairs={{1,0},{2,1},{3,2},{4,3},{5,4},{6,5},{7,6},{8,7},{9,8},{10,9},{11,1... | collective-permute-start | bytes 3145736 | tf_op jit(solution)/shard_map/ppermute | solution.py:63
  201.2 28.8 %all-to-all-start.1 = ((bf16[1,128,16,64]{1,3,0,2:T(8,128)(2,1)}), bf16[1,128,16,64]{1,3,0,2:T(8,128)(2,1)S(1)}, u32[]{:S(2)}, u32[]{:S(2)}) async-start(bf16[1,128,16,64]{1,3,0,2:T(8,128)(2,1)} %bitcast.35), calls=%async_computation.1 | async-start | bytes 524288 | tf_op jit(solution)/shard_map/all_to_all | solution.py:195
  207.3 22.9 %collective-permute-start.18 = (bf16[4,32768]{1,0:T(4,128)(2,1)S(1)}, bf16[4,32768]{1,0:T(4,128)(2,1)S(1)}, u32[]{:S(2)}, u32[]{:S(2)}) collective-permute-start(bf16[4,32768]{1,0:T(4,128)(2,1)S(1)} %maximum_select_fusion.5), channel_id=1, source_target_pairs={{0,2},{2,0},{4,6},{6,4},{8,10},{10,8},{12,14},{14,12},{1,3},{3,1},... | collective-permute-start | bytes 786440 | tf_op jit(solution)/shard_map/ppermute | solution.py:28
  230.7 9.0 %collective-permute-start.19 = (bf16[8,32768]{1,0:T(8,128)(2,1)S(1)}, bf16[8,32768]{1,0:T(8,128)(2,1)S(1)}, u32[]{:S(2)}, u32[]{:S(2)}) collective-permute-start(bf16[8,32768]{1,0:T(8,128)(2,1)S(1)} %maximum_select_fusion.3), channel_id=1, source_target_pairs={{0,1},{1,0},{2,3},{3,2},{4,5},{5,4},{6,7},{7,6},{8,9},{9,8},{10,11... | collective-permute-start | bytes 1572872 | tf_op jit(solution)/shard_map/ppermute | solution.py:25
  241.3 5.0 %copy-start.1 = (f32[1,384,1024]{2,1,0:T(8,128)S(1)}, f32[1,384,1024]{2,1,0:T(8,128)}, u32[]{:S(2)}) copy-start(f32[1,384,1024]{2,1,0:T(8,128)} %copy-done) | copy-start | bytes 4718596
  241.3 5.0 %copy-start.3 = (f32[1,384,1024]{2,1,0:T(8,128)S(1)}, f32[1,384,1024]{2,1,0:T(8,128)}, u32[]{:S(2)}) copy-start(f32[1,384,1024]{2,1,0:T(8,128)} %copy-done.2) | copy-start | bytes 4718596
Sparse Core Ops, SparseCore 0:
  10.2 85.8 all-gather.2
  98.2 59.8 all-gather.4

commit v5 on v4

--- a/solution.py
+++ b/solution.py
@@ -64,41 +64,69 @@
     return before, after
 
 
-def _attn_kernel(live_ref, q_ref, k_ref, v_ref, up_ref, attn_ref, dq_ref, dk_ref, dv_ref):
-    scale = 1.0 / math.sqrt(q_ref.shape[-1])
+def _probs(live_ref, q, k):
+    scale = 1.0 / math.sqrt(q.shape[-1])
+    nt = (((1,), (1,)), ((), ()))
+    scores = lax.dot_general(q, k, nt, preferred_element_type=jnp.float32) * scale
+    scores = jnp.where(live_ref[...] > 0, scores, NEG_FILL)
+    top = jnp.max(scores, axis=-1, keepdims=True)
+    raised = jnp.exp(scores - top)
+    return raised / jnp.sum(raised, axis=-1, keepdims=True)
+
+
+def _forward_kernel(live_ref, q_ref, k_ref, v_ref, attn_ref):
+    probs_b = _probs(live_ref, q_ref[...], k_ref[...]).astype(jnp.bfloat16)
+    attn = jnp.dot(probs_b, v_ref[...], preferred_element_type=jnp.float32)
+    attn_ref[...] = attn.astype(attn_ref.dtype)
+
+
+def _backward_kernel(live_ref, q_ref, k_ref, v_ref, up_ref, dq_ref, dk_ref, dv_ref):
     q = q_ref[...]
     k = k_ref[...]
     v = v_ref[...]
     up = up_ref[...]
+    scale = 1.0 / math.sqrt(q.shape[-1])
     nt = (((1,), (1,)), ((), ()))
     tn = (((0,), (0,)), ((), ()))
-    scores = lax.dot_general(q, k, nt, preferred_element_type=jnp.float32) * scale
-    scores = jnp.where(live_ref[...] > 0, scores, NEG_FILL)
-    top = jnp.max(scores, axis=-1, keepdims=True)
-    raised = jnp.exp(scores - top)
-    probs = raised / jnp.sum(raised, axis=-1, keepdims=True)
+    probs = _probs(live_ref, q, k)
     probs_b = probs.astype(jnp.bfloat16)
-    attn_ref[...] = jnp.dot(probs_b, v, preferred_element_type=jnp.float32).astype(attn_ref.dtype)
     dv_ref[...] = lax.dot_general(probs_b, up, tn, preferred_element_type=jnp.float32)
     dprobs = lax.dot_general(up, v, nt, preferred_element_type=jnp.float32)
     rowdot = jnp.sum(probs * dprobs, axis=-1, keepdims=True)
     dscores = (scale * probs * (dprobs - rowdot)).astype(jnp.bfloat16)
-    dq_ref[...] = jnp.dot(dscores, k, preferred_element_type=jnp.float32).astype(dq_ref.dtype)
+    dq = jnp.dot(dscores, k, preferred_element_type=jnp.float32)
+    dq_ref[...] = dq.astype(dq_ref.dtype)
     dk_ref[...] = lax.dot_general(dscores, q, tn, preferred_element_type=jnp.float32)
 
-def attention(live, q, k, v, up, heads):
+
+def _specs(rows, keys_n, hd):
+    qspec = pl.BlockSpec((rows, hd), lambda h: (0, h))
+    kspec = pl.BlockSpec((keys_n, hd), lambda h: (0, h))
+    return pl.BlockSpec((1, keys_n), lambda h: (0, 0)), qspec, kspec
+
+
+def attention_forward(live, q, k, v, heads):
+    rows, features = q.shape
+    lspec, qspec, kspec = _specs(rows, k.shape[0], features // heads)
+    return pl.pallas_call(
+        _forward_kernel,
+        grid=(heads,),
+        in_specs=[lspec, qspec, kspec, kspec],
+        out_specs=qspec,
+        out_shape=jax.ShapeDtypeStruct((rows, features), jnp.bfloat16),
+    )(live, q, k, v)
+
+
+def attention_backward(live, q, k, v, up, heads):
     rows, features = q.shape
     keys_n = k.shape[0]
-    hd = features // heads
-    qspec = pl.BlockSpec((rows, hd), lambda h: (0, h))
-    kspec = pl.BlockSpec((keys_n, hd), lambda h: (0, h))
+    lspec, qspec, kspec = _specs(rows, keys_n, features // heads)
     return pl.pallas_call(
-        _attn_kernel,
+        _backward_kernel,
         grid=(heads,),
-        in_specs=[pl.BlockSpec((1, keys_n), lambda h: (0, 0)), qspec, kspec, kspec, qspec],
-        out_specs=[qspec, qspec, kspec, kspec],
+        in_specs=[lspec, qspec, kspec, kspec, qspec],
+        out_specs=[qspec, kspec, kspec],
         out_shape=[
-            jax.ShapeDtypeStruct((rows, features), jnp.bfloat16),
             jax.ShapeDtypeStruct((rows, features), jnp.bfloat16),
             jax.ShapeDtypeStruct((keys_n, features), jnp.float32),
             jax.ShapeDtypeStruct((keys_n, features), jnp.float32),
@@ -168,7 +196,8 @@
         live_rows = jnp.repeat(live[b], BLK).astype(jnp.float32)[None]
         q = query[b * BLK : (b + 1) * BLK]
         up = upstream[b * BLK : (b + 1) * BLK]
-        attn, dq, dk, dv = attention(live_rows, q, chosen[0], chosen[1], up, H)
+        attn = attention_forward(live_rows, q, chosen[0], chosen[1], H)
+        dq, dk, dv = attention_backward(live_rows, q, chosen[0], chosen[1], up, H)
         attn_rows.append(attn)
         dq_rows.append(dq)
         for side, grad in enumerate((dk, dv)):

time: 258 us -> 283 us (1.097)
  waiting for transfers between devices: 86.5 us -> 120 us
  starting transfers between devices: 72 us -> 42.1 us
  blocking collectives: 0 us -> 18 us
  other arithmetic: 26.7 us -> 17.2 us
  Pallas kernels: 12.3 us -> 20.8 us
  local copies, waits for them, and re-layouts: 25.4 us -> 28.7 us
    ppermute x12, waiting for transfers between devices: 46.7 us -> 74.1 us  [xor_swap(): return lax.ppermute(x, 'chip', [(i, i ^ m) for i in range(n)])]
    all_gather x1, waiting for transfers between devices: 0.01 us -> 26.2 us  [local(): grad_out_all = lax.all_gather(grad_out, SEQ, axis=0, tiled=True)]
    ppermute x12, starting transfers between devices: 42.5 us -> 21 us  [xor_swap(): return lax.ppermute(x, 'chip', [(i, i ^ m) for i in range(n)])]
    all_to_all x0 -> x1, blocking collectives: none -> 18 us  [local(): lax.all_to_all(attn_out.reshape(tok_rows, count, w_rows), SEQ, 1, 0, tile...]
    all_to_all x1 -> x0, waiting for transfers between devices: 17.8 us -> none  [local(): lax.all_to_all(attn_out.reshape(tok_rows, count, w_rows), SEQ, 1, 0, tile...]
    pallas_call x1 -> x2, Pallas kernels: 12.3 us -> 20.8 us  [the longest x1 12.7 us: attention_backward(): pl.pallas_call(_backward_kernel, grid=(heads,), in_specs=[lspec, qspec, k...]
    unnamed x48 -> x32, local copies, waits for them, and re-layouts: 3.75 us -> 9.94 us
    ppermute x2, waiting for transfers between devices: 9.58 us -> 15.6 us  [halo(): after = lax.ppermute(shard, SEQ, down)]
  transfers between devices with their start and end apart: 24 -> 23, of which waited for: 14 -> 16; matrix products, arithmetic and copies ran while one was open for 24% -> 15% of each run, Pallas kernels for 5% -> 3%
where the time goes in v5:
time: 283 us; the launch traced here: 280 us
  waiting for transfers between devices  120 us (42%)
  starting transfers between devices  42.1 us (15%)
  local copies, waits for them, and re-layouts  28.7 us (10%)
  Pallas kernels  20.8 us (7%)
  blocking collectives  18 us (6%)
  between operations  17.8 us (6%)
  other arithmetic  17.2 us (6%)
  matrix products  15.6 us (6%)
    ppermute x12, waiting for transfers between devices, xor_swap(): return lax.ppermute(x, 'chip', [(i, i ^ m) for i in range(n)])  74.1 us
    all_gather x1, waiting for transfers between devices, local(): grad_out_all = lax.all_gather(grad_out, SEQ, axis=0, tiled=True)  26.2 us
    ppermute x12, starting transfers between devices, xor_swap(): return lax.ppermute(x, 'chip', [(i, i ^ m) for i in range(n)])  21 us
    all_to_all x1, blocking collectives, local(): lax.all_to_all(attn_out.reshape(tok_rows, count, w_rows), SEQ, 1, 0, tile...  18 us
    ppermute x2, waiting for transfers between devices, halo(): after = lax.ppermute(shard, SEQ, down)  15.6 us
    pallas_call x1, Pallas kernels, attention_backward(): pl.pallas_call(_backward_kernel, grid=(heads,), in_specs=[lspec, qspec, k...  12.7 us
    unnamed x32, local copies, waits for them, and re-layouts  9.94 us
    pallas_call x1, Pallas kernels, attention_forward(): pl.pallas_call(_forward_kernel, grid=(heads,), in_specs=[lspec, qspec, ks...  8.11 us
  transfers between devices with their start and end apart: 23, of which 16 were waited for; matrix products, arithmetic and copies ran while one was open for 15% of the time, Pallas kernels for 3%

profile of v5, /device:TPU:11, one launch (start us, length us, event | category | flops | bytes accessed | tf_op | source)
XLA Modules:
  0.0 280.2 jit_solution(8051011139464792032)
XLA Ops:
  8.0 1.3 fusion.35
  10.6 1.9 broadcast_select_fusion.3
  14.2 2.0 collective-permute-start.1
  16.2 3.5 %collective-permute-start = (bf16[2,128,1024]{2,1,0:T(8,128)(2,1)}, bf16[2,128,1024]{2,1,0:T(8,128)(2,1)S(1)}, u32[]{:S(2)}, u32[]{:S(2)}) collective-permute-start(bf16[2,128,1024]{2,1,0:T(8,128)(2,1)} %get-tuple-element.28), channel_id=1, source_target_pairs={{0,1},{1,2},{2,3},{3,4},{4,5},{5,6},{6,7},{7,8},{8,9},{9,10},{10,1... | collective-permute-start | bytes 1572872 | tf_op jit(solution)/shard_map/ppermute | solution.py:62
  20.5 2.2 collective-permute-start.3
  22.7 16.5 %collective-permute-done.3 = bf16[4,32768]{1,0:T(4,128)(2,1)S(1)} collective-permute-done((bf16[4,32768]{1,0:T(4,128)(2,1)S(1)}, bf16[4,32768]{1,0:T(4,128)(2,1)S(1)}, u32[]{:S(2)}, u32[]{:S(2)}) %collective-permute-start.3) | collective-permute-done | bytes 262176 | tf_op jit(solution)/shard_map/ppermute | solution.py:28
  42.6 1.8 collective-permute-done.4
  45.6 10.9 %collective-permute-done.5 = bf16[1,32768]{1,0:T(2,128)(2,1)S(1)} collective-permute-done((bf16[1,32768]{1,0:T(2,128)(2,1)S(1)}, bf16[1,32768]{1,0:T(2,128)(2,1)S(1)}, u32[]{:S(2)}, u32[]{:S(2)}) %collective-permute-start.5) | collective-permute-done | bytes 65568 | tf_op jit(solution)/shard_map/ppermute | solution.py:28
  56.8 4.2 %collective-permute-start.6 = (bf16[1,32768]{1,0:T(2,128)(2,1)S(1)}, bf16[1,32768]{1,0:T(2,128)(2,1)S(1)}, u32[]{:S(2)}, u32[]{:S(2)}) collective-permute-start(bf16[1,32768]{1,0:T(2,128)(2,1)S(1)} %fusion.26), channel_id=1, source_target_pairs={{0,8},{2,10},{4,12},{6,14},{8,0},{10,2},{12,4},{14,6},{1,9},{3,11}... | collective-permute-start | bytes 196616 | tf_op jit(solution)/shard_map/ppermute | solution.py:28
  61.1 11.9 %collective-permute-done.6 = bf16[1,32768]{1,0:T(2,128)(2,1)S(1)} collective-permute-done((bf16[1,32768]{1,0:T(2,128)(2,1)S(1)}, bf16[1,32768]{1,0:T(2,128)(2,1)S(1)}, u32[]{:S(2)}, u32[]{:S(2)}) %collective-permute-start.6) | collective-permute-done | bytes 65568 | tf_op jit(solution)/shard_map/ppermute | solution.py:28
  73.6 3.3 %collective-permute-start.7 = (bf16[2,32768]{1,0:T(2,128)(2,1)S(1)}, bf16[2,32768]{1,0:T(2,128)(2,1)S(1)}, u32[]{:S(2)}, u32[]{:S(2)}) collective-permute-start(bf16[2,32768]{1,0:T(2,128)(2,1)S(1)} %broadcast_select_fusion.13), channel_id=1, source_target_pairs={{0,4},{2,6},{4,0},{6,2},{8,12},{10,14},{12,8},{14,10},{1,5},{3,7},... | collective-permute-start | bytes 393224 | tf_op jit(solution)/shard_map/ppermute | solution.py:28
  76.9 1.8 fusion.21
  81.7 6.0 %collective-permute-done.8 = bf16[4,32768]{1,0:T(4,128)(2,1)S(1)} collective-permute-done((bf16[4,32768]{1,0:T(4,128)(2,1)S(1)}, bf16[4,32768]{1,0:T(4,128)(2,1)S(1)}, u32[]{:S(2)}, u32[]{:S(2)}) %collective-permute-start.8) | collective-permute-done | bytes 262176 | tf_op jit(solution)/shard_map/ppermute | solution.py:28
  88.2 2.0 collective-permute-start.9
  92.6 1.3 select_n.276
  93.9 1.8 fusion.19
  95.7 1.8 fusion.18
  98.7 8.1 %shard_map.119 = bf16[128,1024]{1,0:T(8,128)(2,1)} custom-call(f32[1,1024]{1,0:T(1,128)} %bitcast.128, bf16[128,1024]{1,0:T(8,128)(2,1)} %q_ref.3, bf16[1024,1024]{1,0:T(8,128)(2,1)} %get-tuple-element.18.k_ref, bf16[1024,1024]{1,0:T(8,128)(2,1)} %copy-done), custom_call_target="tpu_custom_call" | custom-call | tf_op jit(solution)/shard_map/pallas_call | solution.py:111
  106.8 1.1 copy.20
  107.9 18.0 %all_to_all.20 = bf16[1,128,16,64]{1,3,0,2:T(8,128)(2,1)S(1)} all-to-all(bf16[1,128,16,64]{1,3,0,2:T(8,128)(2,1)S(1)} %bitcast.127), channel_id=1, replica_groups=mesh['groups'=2,'chip'=8,'core'=2] {'chip','core'}, dimensions={2} | all-to-all | bytes 524288 | tf_op jit(solution)/shard_map/all_to_all | solution.py:224
  126.1 3.8 %convolution_convert_fusion = bf16[128,2048]{1,0:T(8,128)(2,1)} fusion(bf16[128,1024]{1,0:T(8,128)(2,1)} %shard_map.119, bf16[1024,2048]{1,0:T(8,128)(2,1)} %all-gather.3.cloned.1.call-done), kind=kOutput, calls=%fused_computation.4 | convolution fusion | flops 537133056 | bytes 4980736 | tf_op jit(solution)/shard_map/dot_general | solution.py:221
  130.0 26.2 %all-gather.5.cloned.1.call-done = bf16[2048,2048]{1,0:T(8,128)(2,1)} async-done(((bf16[128,2048]{1,0:T(8,128)(2,1)}), bf16[2048,2048]{1,0:T(8,128)(2,1)}) %all-gather.5.cloned.1.call-update) | async-done | bytes 8388624 | tf_op jit(solution)/shard_map/all_gather | solution.py:145
  156.2 6.0 %fusion.1 = bf16[8,16,8,128]{3,2,1,0:T(8,128)(2,1)S(1)} fusion(bf16[2048,2048]{1,0:T(8,128)(2,1)} %all-gather.5.cloned.1.call-done, bf16[64,2048]{1,0:T(8,128)(2,1)S(1)} %copy-done.6), kind=kOutput, calls=%fused_computation.11 | convolution fusion | flops 537001984 | bytes 8912896 | tf_op jit(solution)/shard_map/dot_general | solution.py:176
  163.0 5.1 %all-to-all-start = ((bf16[16,128,64]{1,2,0:T(8,128)(2,1)}), bf16[16,128,64]{1,2,0:T(8,128)(2,1)S(1)}, u32[]{:S(2)}, u32[]{:S(2)}) async-start(bf16[16,128,64]{1,2,0:T(8,128)(2,1)} %bitcast.113), calls=%async_computation | async-start | bytes 524288 | tf_op jit(solution)/shard_map/all_to_all | solution.py:179
  168.1 5.7 %fusion.15 = f32[64,2048]{1,0:T(8,128)} fusion(bf16[2048,2048]{1,0:T(8,128)(2,1)} %all-gather.5.cloned.1.call-done, bf16[8,8,16,128]{3,2,1,0:T(8,128)(2,1)S(1)} %bitcast.124), kind=kOutput, calls=%fused_computation.53 | convolution fusion | flops 536870912 | bytes 9175040 | tf_op jit(solution)/shard_map/dot_general | solution.py:227
  173.9 2.9 %all-to-all-done = bf16[16,128,64]{1,2,0:T(8,128)(2,1)S(1)} async-done(((bf16[16,128,64]{1,2,0:T(8,128)(2,1)}), bf16[16,128,64]{1,2,0:T(8,128)(2,1)S(1)}, u32[]{:S(2)}, u32[]{:S(2)}) %all-to-all-start) | async-done | bytes 262176 | tf_op jit(solution)/shard_map/all_to_all | solution.py:179
  177.6 12.7 %shard_map.120 = (bf16[128,1024]{1,0:T(8,128)(2,1)}, f32[1024,1024]{1,0:T(8,128)}, f32[1024,1024]{1,0:T(8,128)}) custom-call(f32[1,1024]{1,0:T(1,128)} %bitcast.129, bf16[128,1024]{1,0:T(8,128)(2,1)} %q_ref.3, bf16[1024,1024]{1,0:T(8,128)(2,1)} %get-tuple-element.18.k_ref, bf16[1024,1024]{1,0:T(8,128)(2,1)} %copy-done, bf16[128,1024]{1,0:T(8,128)(2,1)} %copy.19.up_ref), custom_call_target="tpu_custom_call" | custom-call | tf_op jit(solution)/shard_map/pallas_call | solution.py:124
  190.3 1.3 slice.234
  191.6 1.3 slice.235
  193.9 2.3 slice_select_fusion
  199.3 7.4 %collective-permute-done.13 = bf16[4,32768]{1,0:T(4,128)(2,1)S(1)} collective-permute-done((bf16[4,32768]{1,0:T(4,128)(2,1)S(1)}, bf16[4,32768]{1,0:T(4,128)(2,1)S(1)}, u32[]{:S(2)}, u32[]{:S(2)}) %collective-permute-start.13) | collective-permute-done | bytes 262176 | tf_op jit(solution)/shard_map/ppermute | solution.py:28
  207.6 3.8 %collective-permute-done.14 = bf16[2,32768]{1,0:T(2,128)(2,1)S(1)} collective-permute-done((bf16[2,32768]{1,0:T(2,128)(2,1)S(1)}, bf16[2,32768]{1,0:T(2,128)(2,1)S(1)}, u32[]{:S(2)}, u32[]{:S(2)}) %collective-permute-start.14) | collective-permute-done | bytes 131104 | tf_op jit(solution)/shard_map/ppermute | solution.py:28
  212.4 4.3 %collective-permute-done.15 = bf16[1,32768]{1,0:T(2,128)(2,1)S(1)} collective-permute-done((bf16[1,32768]{1,0:T(2,128)(2,1)S(1)}, bf16[1,32768]{1,0:T(2,128)(2,1)S(1)}, u32[]{:S(2)}, u32[]{:S(2)}) %collective-permute-start.15) | collective-permute-done | bytes 65568 | tf_op jit(solution)/shard_map/ppermute | solution.py:28
  216.9 1.3 collective-permute-start.16
  218.3 3.5 %collective-permute-done.16 = bf16[1,32768]{1,0:T(2,128)(2,1)S(1)} collective-permute-done((bf16[1,32768]{1,0:T(2,128)(2,1)S(1)}, bf16[1,32768]{1,0:T(2,128)(2,1)S(1)}, u32[]{:S(2)}, u32[]{:S(2)}) %collective-permute-start.16) | collective-permute-done | bytes 65568 | tf_op jit(solution)/shard_map/ppermute | solution.py:28
  222.4 2.6 collective-permute-start.17
  225.0 2.3 collective-permute-done.17
  227.8 5.2 %collective-permute-start.18 = (bf16[4,32768]{1,0:T(4,128)(2,1)S(1)}, bf16[4,32768]{1,0:T(4,128)(2,1)S(1)}, u32[]{:S(2)}, u32[]{:S(2)}) collective-permute-start(bf16[4,32768]{1,0:T(4,128)(2,1)S(1)} %maximum_select_fusion.5), channel_id=1, source_target_pairs={{0,2},{2,0},{4,6},{6,4},{8,10},{10,8},{12,14},{14,12},{1,3},{3,1},... | collective-permute-start | bytes 786440 | tf_op jit(solution)/shard_map/ppermute | solution.py:28
  233.4 4.9 %collective-permute-done.18 = bf16[4,32768]{1,0:T(4,128)(2,1)S(1)} collective-permute-done((bf16[4,32768]{1,0:T(4,128)(2,1)S(1)}, bf16[4,32768]{1,0:T(4,128)(2,1)S(1)}, u32[]{:S(2)}, u32[]{:S(2)}) %collective-permute-start.18) | collective-permute-done | bytes 262176 | tf_op jit(solution)/shard_map/ppermute | solution.py:28
  238.7 2.1 collective-permute-start.19
  241.1 1.1 pad_maximum_fusion.3
  242.2 1.9 collective-permute-start.11
  244.1 3.6 %collective-permute-start.10 = (bf16[2,256,1024]{2,1,0:T(8,128)(2,1)}, bf16[2,256,1024]{2,1,0:T(8,128)(2,1)}, u32[]{:S(2)}, u32[]{:S(2)}) collective-permute-start(bf16[2,256,1024]{2,1,0:T(8,128)(2,1)} %pad_maximum_fusion.3), channel_id=1, source_target_pairs={{0,1},{1,2},{2,3},{3,4},{4,5},{5,6},{6,7},{7,8},{8,9},{9,10},{10,1... | collective-permute-start | bytes 3145736 | tf_op jit(solution)/shard_map/ppermute | solution.py:62
  248.0 1.5 fusion.10
  249.5 2.4 reshape.115
  251.9 2.4 reshape.116
  254.3 15.6 %collective-permute-done.11 = bf16[2,256,1024]{2,1,0:T(8,128)(2,1)} collective-permute-done((bf16[2,256,1024]{2,1,0:T(8,128)(2,1)}, bf16[2,256,1024]{2,1,0:T(8,128)(2,1)}, u32[]{:S(2)}, u32[]{:S(2)}) %collective-permute-start.11) | collective-permute-done | bytes 1048608 | tf_op jit(solution)/shard_map/ppermute | solution.py:63
  270.3 2.3 fusion.8
  (104 shorter events, 25.5 us)
Async XLA Ops:
  7.2 119.0 %all-gather.3.cloned.1.call-start = ((), (), s32[]{:S(2)}) async-start(), calls=%async_computation.2 | async-start | bytes 4456448 | tf_op jit(solution)/shard_map/all_gather | solution.py:146
  7.9 148.3 %all-gather.5.cloned.1.call-start = ((), (), s32[]{:S(2)}) async-start(), calls=%async_computation.3 | async-start | bytes 8912896 | tf_op jit(solution)/shard_map/all_gather | solution.py:145
  13.5 9.1 %copy-start.9 = (s32[3]{0:T(128)S(1)}, s32[3]{0:T(128)}, u32[]{:S(2)}) copy-start(s32[3]{0:T(128)} %constant.80.clone) | copy-start | bytes 40
  13.5 9.1 %copy-start.8 = (s32[1,3]{1,0:T(1,128)S(1)}, s32[1,3]{1,0:T(1,128)}, u32[]{:S(2)}) copy-start(s32[1,3]{1,0:T(1,128)} %param.14) | copy-start | bytes 40
  13.5 6.5 %collective-permute-start.2 = (bf16[8,32768]{1,0:T(8,128)(2,1)}, bf16[8,32768]{1,0:T(8,128)(2,1)S(1)}, u32[]{:S(2)}, u32[]{:S(2)}) collective-permute-start(bf16[8,32768]{1,0:T(8,128)(2,1)} %select_n.265), channel_id=1, source_target_pairs={{0,1},{1,0},{2,3},{3,2},{4,5},{5,4},{6,7},{7,6},{8,9},{9,8},{10,11... | collective-permute-start | bytes 1572872 | tf_op jit(solution)/shard_map/ppermute | solution.py:25
  14.2 31.2 %collective-permute-start.1 = (bf16[2,128,1024]{2,1,0:T(8,128)(2,1)}, bf16[2,128,1024]{2,1,0:T(8,128)(2,1)S(1)}, u32[]{:S(2)}, u32[]{:S(2)}) collective-permute-start(bf16[2,128,1024]{2,1,0:T(8,128)(2,1)} %get-tuple-element.28), channel_id=1, source_target_pairs={{1,0},{2,1},{3,2},{4,3},{5,4},{6,5},{7,6},{8,7},{9,8},{10,9},{11,1... | collective-permute-start | bytes 1572872 | tf_op jit(solution)/shard_map/ppermute | solution.py:63
  16.2 29.2 %collective-permute-start = (bf16[2,128,1024]{2,1,0:T(8,128)(2,1)}, bf16[2,128,1024]{2,1,0:T(8,128)(2,1)S(1)}, u32[]{:S(2)}, u32[]{:S(2)}) collective-permute-start(bf16[2,128,1024]{2,1,0:T(8,128)(2,1)} %get-tuple-element.28), channel_id=1, source_target_pairs={{0,1},{1,2},{2,3},{3,4},{4,5},{5,6},{6,7},{7,8},{8,9},{9,10},{10,1... | collective-permute-start | bytes 1572872 | tf_op jit(solution)/shard_map/ppermute | solution.py:62
  20.1 25.4 %copy-start.3 = (bf16[128,1024]{1,0:T(8,128)(2,1)S(1)}, bf16[128,1024]{1,0:T(8,128)(2,1)}, u32[]{:S(2)}) copy-start(bf16[128,1024]{1,0:T(8,128)(2,1)} %param.10) | copy-start | bytes 786436
  20.1 25.4 %copy-start.4 = (bf16[128,1024]{1,0:T(8,128)(2,1)S(1)}, bf16[128,1024]{1,0:T(8,128)(2,1)}, u32[]{:S(2)}) copy-start(bf16[128,1024]{1,0:T(8,128)(2,1)} %param.9) | copy-start | bytes 786436
  20.5 18.7 %collective-permute-start.3 = (bf16[4,32768]{1,0:T(4,128)(2,1)S(1)}, bf16[4,32768]{1,0:T(4,128)(2,1)S(1)}, u32[]{:S(2)}, u32[]{:S(2)}) collective-permute-start(bf16[4,32768]{1,0:T(4,128)(2,1)S(1)} %broadcast_select_fusion.5), channel_id=1, source_target_pairs={{0,2},{2,0},{4,6},{6,4},{8,10},{10,8},{12,14},{14,12},{1,3},{3,1},... | collective-permute-start | bytes 786440 | tf_op jit(solution)/shard_map/ppermute | solution.py:28
  39.7 4.7 %collective-permute-start.4 = (bf16[2,32768]{1,0:T(2,128)(2,1)S(1)}, bf16[2,32768]{1,0:T(2,128)(2,1)S(1)}, u32[]{:S(2)}, u32[]{:S(2)}) collective-permute-start(bf16[2,32768]{1,0:T(2,128)(2,1)S(1)} %broadcast_select_fusion.6), channel_id=1, source_target_pairs={{0,4},{2,6},{4,0},{6,2},{8,12},{10,14},{12,8},{14,10},{1,5},{3,7},... | collective-permute-start | bytes 393224 | tf_op jit(solution)/shard_map/ppermute | solution.py:28
  44.8 11.6 %collective-permute-start.5 = (bf16[1,32768]{1,0:T(2,128)(2,1)S(1)}, bf16[1,32768]{1,0:T(2,128)(2,1)S(1)}, u32[]{:S(2)}, u32[]{:S(2)}) collective-permute-start(bf16[1,32768]{1,0:T(2,128)(2,1)S(1)} %broadcast_select_fusion.10), channel_id=1, source_target_pairs={{0,8},{2,10},{4,12},{6,14},{8,0},{10,2},{12,4},{14,6},{1,9},{3,11}... | collective-permute-start | bytes 196616 | tf_op jit(solution)/shard_map/ppermute | solution.py:28
  45.5 15.6 %copy-start.5 = (bf16[2,128,1024]{2,1,0:T(8,128)(2,1)}, bf16[2,128,1024]{2,1,0:T(8,128)(2,1)S(1)}, u32[]{:S(2)}) copy-start(bf16[2,128,1024]{2,1,0:T(8,128)(2,1)S(1)} %collective-permute-done) | copy-start | bytes 1572868
  56.8 16.2 %collective-permute-start.6 = (bf16[1,32768]{1,0:T(2,128)(2,1)S(1)}, bf16[1,32768]{1,0:T(2,128)(2,1)S(1)}, u32[]{:S(2)}, u32[]{:S(2)}) collective-permute-start(bf16[1,32768]{1,0:T(2,128)(2,1)S(1)} %fusion.26), channel_id=1, source_target_pairs={{0,8},{2,10},{4,12},{6,14},{8,0},{10,2},{12,4},{14,6},{1,9},{3,11}... | collective-permute-start | bytes 196616 | tf_op jit(solution)/shard_map/ppermute | solution.py:28
  73.6 6.8 %collective-permute-start.7 = (bf16[2,32768]{1,0:T(2,128)(2,1)S(1)}, bf16[2,32768]{1,0:T(2,128)(2,1)S(1)}, u32[]{:S(2)}, u32[]{:S(2)}) collective-permute-start(bf16[2,32768]{1,0:T(2,128)(2,1)S(1)} %broadcast_select_fusion.13), channel_id=1, source_target_pairs={{0,4},{2,6},{4,0},{6,2},{8,12},{10,14},{12,8},{14,10},{1,5},{3,7},... | collective-permute-start | bytes 393224 | tf_op jit(solution)/shard_map/ppermute | solution.py:28
  80.8 6.9 %collective-permute-start.8 = (bf16[4,32768]{1,0:T(4,128)(2,1)S(1)}, bf16[4,32768]{1,0:T(4,128)(2,1)S(1)}, u32[]{:S(2)}, u32[]{:S(2)}) collective-permute-start(bf16[4,32768]{1,0:T(4,128)(2,1)S(1)} %maximum_select_fusion.4), channel_id=1, source_target_pairs={{0,2},{2,0},{4,6},{6,4},{8,10},{10,8},{12,14},{14,12},{1,3},{3,1},... | collective-permute-start | bytes 786440 | tf_op jit(solution)/shard_map/ppermute | solution.py:28
  88.2 4.2 %collective-permute-start.9 = (bf16[8,32768]{1,0:T(8,128)(2,1)S(1)}, bf16[8,32768]{1,0:T(8,128)(2,1)S(1)}, u32[]{:S(2)}, u32[]{:S(2)}) collective-permute-start(bf16[8,32768]{1,0:T(8,128)(2,1)S(1)} %maximum_select_fusion.2), channel_id=1, source_target_pairs={{0,1},{1,0},{2,3},{3,2},{4,5},{5,4},{6,7},{7,6},{8,9},{9,8},{10,11... | collective-permute-start | bytes 1572872 | tf_op jit(solution)/shard_map/ppermute | solution.py:25
  97.4 1.3 copy-start
  126.1 30.1 %copy-start.6 = (bf16[64,2048]{1,0:T(8,128)(2,1)S(1)}, bf16[64,2048]{1,0:T(8,128)(2,1)}, u32[]{:S(2)}) copy-start(bf16[64,2048]{1,0:T(8,128)(2,1)} %param.11) | copy-start | bytes 786436
  163.0 13.8 %all-to-all-start = ((bf16[16,128,64]{1,2,0:T(8,128)(2,1)}), bf16[16,128,64]{1,2,0:T(8,128)(2,1)S(1)}, u32[]{:S(2)}, u32[]{:S(2)}) async-start(bf16[16,128,64]{1,2,0:T(8,128)(2,1)} %bitcast.113), calls=%async_computation | async-start | bytes 524288 | tf_op jit(solution)/shard_map/all_to_all | solution.py:179
  193.2 0.7 copy-start.7
  193.7 3.1 %copy-start.2 = (f32[1024,1024]{1,0:T(8,128)S(1)}, f32[1024,1024]{1,0:T(8,128)}, u32[]{:S(2)}) copy-start(f32[1024,1024]{1,0:T(8,128)} %get-tuple-element.10) | copy-start | bytes 12582916
  193.7 4.6 %collective-permute-start.12 = (bf16[8,32768]{1,0:T(8,128)(2,1)S(1)}, bf16[8,32768]{1,0:T(8,128)(2,1)S(1)}, u32[]{:S(2)}, u32[]{:S(2)}) collective-permute-start(bf16[8,32768]{1,0:T(8,128)(2,1)S(1)} %convert_element_type.83), channel_id=1, source_target_pairs={{0,1},{1,0},{2,3},{3,2},{4,5},{5,4},{6,7},{7,6},{8,9},{9,8},{10,11... | collective-permute-start | bytes 1572872 | tf_op jit(solution)/shard_map/ppermute | solution.py:25
  193.9 4.3 %copy-start.1 = (f32[1024,1024]{1,0:T(8,128)S(1)}, f32[1024,1024]{1,0:T(8,128)}, u32[]{:S(2)}) copy-start(f32[1024,1024]{1,0:T(8,128)} %get-tuple-element.9) | copy-start | bytes 12582916
  198.7 8.0 %collective-permute-start.13 = (bf16[4,32768]{1,0:T(4,128)(2,1)S(1)}, bf16[4,32768]{1,0:T(4,128)(2,1)S(1)}, u32[]{:S(2)}, u32[]{:S(2)}) collective-permute-start(bf16[4,32768]{1,0:T(4,128)(2,1)S(1)} %select_convert_fusion.1), channel_id=1, source_target_pairs={{0,2},{2,0},{4,6},{6,4},{8,10},{10,8},{12,14},{14,12},{1,3},{3,1},... | collective-permute-start | bytes 786440 | tf_op jit(solution)/shard_map/ppermute | solution.py:28
  207.1 4.3 %collective-permute-start.14 = (bf16[2,32768]{1,0:T(2,128)(2,1)S(1)}, bf16[2,32768]{1,0:T(2,128)(2,1)S(1)}, u32[]{:S(2)}, u32[]{:S(2)}) collective-permute-start(bf16[2,32768]{1,0:T(2,128)(2,1)S(1)} %select_convert_fusion.2), channel_id=1, source_target_pairs={{0,4},{2,6},{4,0},{6,2},{8,12},{10,14},{12,8},{14,10},{1,5},{3,7},... | collective-permute-start | bytes 393224 | tf_op jit(solution)/shard_map/ppermute | solution.py:28
  211.8 4.9 %collective-permute-start.15 = (bf16[1,32768]{1,0:T(2,128)(2,1)S(1)}, bf16[1,32768]{1,0:T(2,128)(2,1)S(1)}, u32[]{:S(2)}, u32[]{:S(2)}) collective-permute-start(bf16[1,32768]{1,0:T(2,128)(2,1)S(1)} %fusion.29), channel_id=1, source_target_pairs={{0,8},{2,10},{4,12},{6,14},{8,0},{10,2},{12,4},{14,6},{1,9},{3,11}... | collective-permute-start | bytes 196616 | tf_op jit(solution)/shard_map/ppermute | solution.py:28
  216.9 4.9 %collective-permute-start.16 = (bf16[1,32768]{1,0:T(2,128)(2,1)S(1)}, bf16[1,32768]{1,0:T(2,128)(2,1)S(1)}, u32[]{:S(2)}, u32[]{:S(2)}) collective-permute-start(bf16[1,32768]{1,0:T(2,128)(2,1)S(1)} %fusion.28), channel_id=1, source_target_pairs={{0,8},{2,10},{4,12},{6,14},{8,0},{10,2},{12,4},{14,6},{1,9},{3,11}... | collective-permute-start | bytes 196616 | tf_op jit(solution)/shard_map/ppermute | solution.py:28
  222.4 4.9 %collective-permute-start.17 = (bf16[2,32768]{1,0:T(2,128)(2,1)S(1)}, bf16[2,32768]{1,0:T(2,128)(2,1)S(1)}, u32[]{:S(2)}, u32[]{:S(2)}) collective-permute-start(bf16[2,32768]{1,0:T(2,128)(2,1)S(1)} %broadcast_select_fusion.12), channel_id=1, source_target_pairs={{0,4},{2,6},{4,0},{6,2},{8,12},{10,14},{12,8},{14,10},{1,5},{3,7},... | collective-permute-start | bytes 393224 | tf_op jit(solution)/shard_map/ppermute | solution.py:28
  227.8 10.5 %collective-permute-start.18 = (bf16[4,32768]{1,0:T(4,128)(2,1)S(1)}, bf16[4,32768]{1,0:T(4,128)(2,1)S(1)}, u32[]{:S(2)}, u32[]{:S(2)}) collective-permute-start(bf16[4,32768]{1,0:T(4,128)(2,1)S(1)} %maximum_select_fusion.5), channel_id=1, source_target_pairs={{0,2},{2,0},{4,6},{6,4},{8,10},{10,8},{12,14},{14,12},{1,3},{3,1},... | collective-permute-start | bytes 786440 | tf_op jit(solution)/shard_map/ppermute | solution.py:28
  238.7 9.1 %collective-permute-start.19 = (bf16[8,32768]{1,0:T(8,128)(2,1)S(1)}, bf16[8,32768]{1,0:T(8,128)(2,1)S(1)}, u32[]{:S(2)}, u32[]{:S(2)}) collective-permute-start(bf16[8,32768]{1,0:T(8,128)(2,1)S(1)} %maximum_select_fusion.3), channel_id=1, source_target_pairs={{0,1},{1,0},{2,3},{3,2},{4,5},{5,4},{6,7},{7,6},{8,9},{9,8},{10,11... | collective-permute-start | bytes 1572872 | tf_op jit(solution)/shard_map/ppermute | solution.py:25
  242.2 27.7 %collective-permute-start.11 = (bf16[2,256,1024]{2,1,0:T(8,128)(2,1)}, bf16[2,256,1024]{2,1,0:T(8,128)(2,1)}, u32[]{:S(2)}, u32[]{:S(2)}) collective-permute-start(bf16[2,256,1024]{2,1,0:T(8,128)(2,1)} %pad_maximum_fusion.3), channel_id=1, source_target_pairs={{1,0},{2,1},{3,2},{4,3},{5,4},{6,5},{7,6},{8,7},{9,8},{10,9},{11,1... | collective-permute-start | bytes 3145736 | tf_op jit(solution)/shard_map/ppermute | solution.py:63
  244.1 26.2 %collective-permute-start.10 = (bf16[2,256,1024]{2,1,0:T(8,128)(2,1)}, bf16[2,256,1024]{2,1,0:T(8,128)(2,1)}, u32[]{:S(2)}, u32[]{:S(2)}) collective-permute-start(bf16[2,256,1024]{2,1,0:T(8,128)(2,1)} %pad_maximum_fusion.3), channel_id=1, source_target_pairs={{0,1},{1,2},{2,3},{3,4},{4,5},{5,6},{6,7},{7,8},{8,9},{9,10},{10,1... | collective-permute-start | bytes 3145736 | tf_op jit(solution)/shard_map/ppermute | solution.py:62
Sparse Core Ops, SparseCore 0:
  10.2 66.0 all-gather.2
  78.5 77.6 all-gather.4

commit v6 on v5

--- a/solution.py
+++ b/solution.py
@@ -143,7 +143,8 @@
     device = flat_index()
 
     grad_out_all = lax.all_gather(grad_out, SEQ, axis=0, tiled=True)
-    weight_all = lax.all_gather(out_weight, SEQ, axis=0, tiled=True)
+    grad_out_all, weight_after = lax.optimization_barrier((grad_out_all, out_weight))
+    weight_all = lax.all_gather(weight_after, SEQ, axis=0, tiled=True)
 
     paired = jnp.stack([keys, values])
     before, after = halo(paired)

time: 283 us -> 275 us (0.972)
  waiting for transfers between devices: 120 us -> 108 us
  starting transfers between devices: 42.1 us -> 48 us
    all_gather x1, waiting for transfers between devices: 26.2 us -> 0.02 us  [local(): grad_out_all = lax.all_gather(grad_out, SEQ, axis=0, tiled=True)]
    ppermute x12, waiting for transfers between devices: 74.1 us -> 83.8 us  [xor_swap(): return lax.ppermute(x, 'chip', [(i, i ^ m) for i in range(n)])]
    ppermute x4, starting transfers between devices: 4.84 us -> 10.5 us  [xor_swap(): return lax.ppermute(x, 'core', [(i, i ^ 1) for i in range(n)])]
    all_to_all x1, waiting for transfers between devices: 2.93 us -> 7.96 us  [local(): lax.all_to_all(upstream_cols.reshape(count, tok_rows, w_rows), SEQ, 0, 0,...]
    unnamed x32 -> x34, local copies, waits for them, and re-layouts: 9.94 us -> 9.6 us
  transfers between devices with their start and end apart: 23 -> 23, of which waited for: 16 -> 15; matrix products, arithmetic and copies ran while one was open for 15% -> 19% of each run, Pallas kernels for 3% -> 8%
where the time goes in v6:
time: 275 us; the launch traced here: 271 us
  waiting for transfers between devices  108 us (39%)
  starting transfers between devices  48 us (17%)
  local copies, waits for them, and re-layouts  28.4 us (10%)
  Pallas kernels  20.8 us (8%)
  between operations  17.8 us (6%)
  other arithmetic  17.3 us (6%)
  blocking collectives  15.8 us (6%)
  matrix products  15.5 us (6%)
    ppermute x12, waiting for transfers between devices, xor_swap(): return lax.ppermute(x, 'chip', [(i, i ^ m) for i in range(n)])  83.8 us
    ppermute x12, starting transfers between devices, xor_swap(): return lax.ppermute(x, 'chip', [(i, i ^ m) for i in range(n)])  21.4 us
    all_to_all x1, blocking collectives, local(): lax.all_to_all(attn_out.reshape(tok_rows, count, w_rows), SEQ, 1, 0, tile...  15.8 us
    ppermute x2, waiting for transfers between devices, halo(): after = lax.ppermute(shard, SEQ, down)  15.6 us
    pallas_call x1, Pallas kernels, attention_backward(): pl.pallas_call(_backward_kernel, grid=(heads,), in_specs=[lspec, qspec, k...  12.7 us
    ppermute x4, starting transfers between devices, xor_swap(): return lax.ppermute(x, 'core', [(i, i ^ 1) for i in range(n)])  10.5 us
    unnamed x34, local copies, waits for them, and re-layouts  9.6 us
    pallas_call x1, Pallas kernels, attention_forward(): pl.pallas_call(_forward_kernel, grid=(heads,), in_specs=[lspec, qspec, ks...  8.12 us
  transfers between devices with their start and end apart: 23, of which 15 were waited for; matrix products, arithmetic and copies ran while one was open for 19% of the time, Pallas kernels for 8%

profile of v6, /device:TPU:11, one launch (start us, length us, event | category | flops | bytes accessed | tf_op | source)
XLA Modules:
  0.0 271.4 jit_solution(10302199345806107587)
XLA Ops:
  7.2 1.3 fusion.35
  9.8 1.9 broadcast_select_fusion.3
  13.5 2.0 collective-permute-start.1
  15.5 3.5 %collective-permute-start = (bf16[2,128,1024]{2,1,0:T(8,128)(2,1)}, bf16[2,128,1024]{2,1,0:T(8,128)(2,1)S(1)}, u32[]{:S(2)}, u32[]{:S(2)}) collective-permute-start(bf16[2,128,1024]{2,1,0:T(8,128)(2,1)} %get-tuple-element.32), channel_id=1, source_target_pairs={{0,1},{1,2},{2,3},{3,4},{4,5},{5,6},{6,7},{7,8},{8,9},{9,10},{10,1... | collective-permute-start | bytes 1572872 | tf_op jit(solution)/shard_map/ppermute | solution.py:62
  19.8 2.2 collective-permute-start.3
  22.0 19.3 %collective-permute-done.3 = bf16[4,32768]{1,0:T(4,128)(2,1)S(1)} collective-permute-done((bf16[4,32768]{1,0:T(4,128)(2,1)S(1)}, bf16[4,32768]{1,0:T(4,128)(2,1)S(1)}, u32[]{:S(2)}, u32[]{:S(2)}) %collective-permute-start.3) | collective-permute-done | bytes 262176 | tf_op jit(solution)/shard_map/ppermute | solution.py:28
  44.6 6.5 %collective-permute-done.4 = bf16[2,32768]{1,0:T(2,128)(2,1)S(1)} collective-permute-done((bf16[2,32768]{1,0:T(2,128)(2,1)S(1)}, bf16[2,32768]{1,0:T(2,128)(2,1)S(1)}, u32[]{:S(2)}, u32[]{:S(2)}) %collective-permute-start.4) | collective-permute-done | bytes 131104 | tf_op jit(solution)/shard_map/ppermute | solution.py:28
  51.6 3.0 %collective-permute-start.5 = (bf16[1,32768]{1,0:T(2,128)(2,1)S(1)}, bf16[1,32768]{1,0:T(2,128)(2,1)S(1)}, u32[]{:S(2)}, u32[]{:S(2)}) collective-permute-start(bf16[1,32768]{1,0:T(2,128)(2,1)S(1)} %broadcast_select_fusion.10), channel_id=1, source_target_pairs={{0,8},{2,10},{4,12},{6,14},{8,0},{10,2},{12,4},{14,6},{1,9},{3,11}... | collective-permute-start | bytes 196616 | tf_op jit(solution)/shard_map/ppermute | solution.py:28
  54.8 8.3 %collective-permute-done.5 = bf16[1,32768]{1,0:T(2,128)(2,1)S(1)} collective-permute-done((bf16[1,32768]{1,0:T(2,128)(2,1)S(1)}, bf16[1,32768]{1,0:T(2,128)(2,1)S(1)}, u32[]{:S(2)}, u32[]{:S(2)}) %collective-permute-start.5) | collective-permute-done | bytes 65568 | tf_op jit(solution)/shard_map/ppermute | solution.py:28
  63.4 3.8 %collective-permute-start.6 = (bf16[1,32768]{1,0:T(2,128)(2,1)S(1)}, bf16[1,32768]{1,0:T(2,128)(2,1)S(1)}, u32[]{:S(2)}, u32[]{:S(2)}) collective-permute-start(bf16[1,32768]{1,0:T(2,128)(2,1)S(1)} %fusion.26), channel_id=1, source_target_pairs={{0,8},{2,10},{4,12},{6,14},{8,0},{10,2},{12,4},{14,6},{1,9},{3,11}... | collective-permute-start | bytes 196616 | tf_op jit(solution)/shard_map/ppermute | solution.py:28
  67.3 12.8 %collective-permute-done.6 = bf16[1,32768]{1,0:T(2,128)(2,1)S(1)} collective-permute-done((bf16[1,32768]{1,0:T(2,128)(2,1)S(1)}, bf16[1,32768]{1,0:T(2,128)(2,1)S(1)}, u32[]{:S(2)}, u32[]{:S(2)}) %collective-permute-start.6) | collective-permute-done | bytes 65568 | tf_op jit(solution)/shard_map/ppermute | solution.py:28
  80.8 2.2 collective-permute-start.7
  83.0 1.8 fusion.21
  85.5 7.9 %collective-permute-done.7 = bf16[2,32768]{1,0:T(2,128)(2,1)S(1)} collective-permute-done((bf16[2,32768]{1,0:T(2,128)(2,1)S(1)}, bf16[2,32768]{1,0:T(2,128)(2,1)S(1)}, u32[]{:S(2)}, u32[]{:S(2)}) %collective-permute-start.7) | collective-permute-done | bytes 131104 | tf_op jit(solution)/shard_map/ppermute | solution.py:28
  94.7 4.9 %collective-permute-done.8 = bf16[4,32768]{1,0:T(4,128)(2,1)S(1)} collective-permute-done((bf16[4,32768]{1,0:T(4,128)(2,1)S(1)}, bf16[4,32768]{1,0:T(4,128)(2,1)S(1)}, u32[]{:S(2)}, u32[]{:S(2)}) %collective-permute-start.8) | collective-permute-done | bytes 262176 | tf_op jit(solution)/shard_map/ppermute | solution.py:28
  100.0 5.8 %collective-permute-start.9 = (bf16[8,32768]{1,0:T(8,128)(2,1)S(1)}, bf16[8,32768]{1,0:T(8,128)(2,1)S(1)}, u32[]{:S(2)}, u32[]{:S(2)}) collective-permute-start(bf16[8,32768]{1,0:T(8,128)(2,1)S(1)} %maximum_select_fusion.2), channel_id=1, source_target_pairs={{0,1},{1,0},{2,3},{3,2},{4,5},{5,4},{6,7},{7,6},{8,9},{9,8},{10,11... | collective-permute-start | bytes 1572872 | tf_op jit(solution)/shard_map/ppermute | solution.py:25
  108.1 1.3 select_n.276
  109.5 1.8 fusion.19
  111.2 1.8 fusion.18
  114.3 8.1 %shard_map.119 = bf16[128,1024]{1,0:T(8,128)(2,1)} custom-call(f32[1,1024]{1,0:T(1,128)} %bitcast.128, bf16[128,1024]{1,0:T(8,128)(2,1)} %q_ref.3, bf16[1024,1024]{1,0:T(8,128)(2,1)} %get-tuple-element.22.k_ref, bf16[1024,1024]{1,0:T(8,128)(2,1)} %copy-done), custom_call_target="tpu_custom_call" | custom-call | tf_op jit(solution)/shard_map/pallas_call | solution.py:111
  123.5 15.8 %all_to_all.20 = bf16[1,128,16,64]{1,3,0,2:T(8,128)(2,1)S(1)} all-to-all(bf16[1,128,16,64]{1,3,0,2:T(8,128)(2,1)S(1)} %bitcast.127), channel_id=1, replica_groups=mesh['groups'=2,'chip'=8,'core'=2] {'chip','core'}, dimensions={2} | all-to-all | bytes 524288 | tf_op jit(solution)/shard_map/all_to_all | solution.py:225
  139.6 6.0 %fusion.1 = bf16[8,16,8,128]{3,2,1,0:T(8,128)(2,1)S(1)} fusion(bf16[2048,2048]{1,0:T(8,128)(2,1)} %all-gather.3.cloned.1.call-done, bf16[64,2048]{1,0:T(8,128)(2,1)S(1)} %copy-done.7), kind=kOutput, calls=%fused_computation.11 | convolution fusion | flops 537001984 | bytes 8912896 | tf_op jit(solution)/shard_map/dot_general | solution.py:177
  146.4 4.8 %all-to-all-start = ((bf16[16,128,64]{1,2,0:T(8,128)(2,1)}), bf16[16,128,64]{1,2,0:T(8,128)(2,1)S(1)}, u32[]{:S(2)}, u32[]{:S(2)}) async-start(bf16[16,128,64]{1,2,0:T(8,128)(2,1)} %bitcast.113), calls=%async_computation | async-start | bytes 524288 | tf_op jit(solution)/shard_map/all_to_all | solution.py:180
  151.2 5.8 %fusion.15 = f32[64,2048]{1,0:T(8,128)} fusion(bf16[2048,2048]{1,0:T(8,128)(2,1)} %all-gather.3.cloned.1.call-done, bf16[8,8,16,128]{3,2,1,0:T(8,128)(2,1)S(1)} %bitcast.124), kind=kOutput, calls=%fused_computation.53 | convolution fusion | flops 536870912 | bytes 9175040 | tf_op jit(solution)/shard_map/dot_general | solution.py:228
  157.0 8.0 %all-to-all-done = bf16[16,128,64]{1,2,0:T(8,128)(2,1)S(1)} async-done(((bf16[16,128,64]{1,2,0:T(8,128)(2,1)}), bf16[16,128,64]{1,2,0:T(8,128)(2,1)S(1)}, u32[]{:S(2)}, u32[]{:S(2)}) %all-to-all-start) | async-done | bytes 262176 | tf_op jit(solution)/shard_map/all_to_all | solution.py:180
  165.8 12.7 %shard_map.120 = (bf16[128,1024]{1,0:T(8,128)(2,1)}, f32[1024,1024]{1,0:T(8,128)}, f32[1024,1024]{1,0:T(8,128)}) custom-call(f32[1,1024]{1,0:T(1,128)} %bitcast.129, bf16[128,1024]{1,0:T(8,128)(2,1)} %q_ref.3, bf16[1024,1024]{1,0:T(8,128)(2,1)} %get-tuple-element.22.k_ref, bf16[1024,1024]{1,0:T(8,128)(2,1)} %copy-done, bf16[128,1024]{1,0:T(8,128)(2,1)} %copy.19.up_ref), custom_call_target="tpu_custom_call" | custom-call | tf_op jit(solution)/shard_map/pallas_call | solution.py:124
  178.5 1.3 slice.234
  179.8 1.3 slice.235
  182.4 2.4 slice_select_fusion
  185.4 1.2 copy-done.1
  188.1 6.5 %collective-permute-done.13 = bf16[4,32768]{1,0:T(4,128)(2,1)S(1)} collective-permute-done((bf16[4,32768]{1,0:T(4,128)(2,1)S(1)}, bf16[4,32768]{1,0:T(4,128)(2,1)S(1)}, u32[]{:S(2)}, u32[]{:S(2)}) %collective-permute-start.13) | collective-permute-done | bytes 262176 | tf_op jit(solution)/shard_map/ppermute | solution.py:28
  195.2 3.7 %collective-permute-done.14 = bf16[2,32768]{1,0:T(2,128)(2,1)S(1)} collective-permute-done((bf16[2,32768]{1,0:T(2,128)(2,1)S(1)}, bf16[2,32768]{1,0:T(2,128)(2,1)S(1)}, u32[]{:S(2)}, u32[]{:S(2)}) %collective-permute-start.14) | collective-permute-done | bytes 131104 | tf_op jit(solution)/shard_map/ppermute | solution.py:28
  199.3 1.2 collective-permute-start.15
  200.8 3.5 %collective-permute-done.15 = bf16[1,32768]{1,0:T(2,128)(2,1)S(1)} collective-permute-done((bf16[1,32768]{1,0:T(2,128)(2,1)S(1)}, bf16[1,32768]{1,0:T(2,128)(2,1)S(1)}, u32[]{:S(2)}, u32[]{:S(2)}) %collective-permute-start.15) | collective-permute-done | bytes 65568 | tf_op jit(solution)/shard_map/ppermute | solution.py:28
  204.6 4.6 %collective-permute-start.16 = (bf16[1,32768]{1,0:T(2,128)(2,1)S(1)}, bf16[1,32768]{1,0:T(2,128)(2,1)S(1)}, u32[]{:S(2)}, u32[]{:S(2)}) collective-permute-start(bf16[1,32768]{1,0:T(2,128)(2,1)S(1)} %fusion.28), channel_id=1, source_target_pairs={{0,8},{2,10},{4,12},{6,14},{8,0},{10,2},{12,4},{14,6},{1,9},{3,11}... | collective-permute-start | bytes 196616 | tf_op jit(solution)/shard_map/ppermute | solution.py:28
  209.2 3.2 %collective-permute-done.16 = bf16[1,32768]{1,0:T(2,128)(2,1)S(1)} collective-permute-done((bf16[1,32768]{1,0:T(2,128)(2,1)S(1)}, bf16[1,32768]{1,0:T(2,128)(2,1)S(1)}, u32[]{:S(2)}, u32[]{:S(2)}) %collective-permute-start.16) | collective-permute-done | bytes 65568 | tf_op jit(solution)/shard_map/ppermute | solution.py:28
  213.3 3.7 %collective-permute-done.17 = bf16[2,32768]{1,0:T(2,128)(2,1)S(1)} collective-permute-done((bf16[2,32768]{1,0:T(2,128)(2,1)S(1)}, bf16[2,32768]{1,0:T(2,128)(2,1)S(1)}, u32[]{:S(2)}, u32[]{:S(2)}) %collective-permute-start.17) | collective-permute-done | bytes 131104 | tf_op jit(solution)/shard_map/ppermute | solution.py:28
  217.4 3.0 %collective-permute-start.18 = (bf16[4,32768]{1,0:T(4,128)(2,1)S(1)}, bf16[4,32768]{1,0:T(4,128)(2,1)S(1)}, u32[]{:S(2)}, u32[]{:S(2)}) collective-permute-start(bf16[4,32768]{1,0:T(4,128)(2,1)S(1)} %maximum_select_fusion.5), channel_id=1, source_target_pairs={{0,2},{2,0},{4,6},{6,4},{8,10},{10,8},{12,14},{14,12},{1,3},{3,1},... | collective-permute-start | bytes 786440 | tf_op jit(solution)/shard_map/ppermute | solution.py:28
  220.8 3.4 %collective-permute-done.18 = bf16[4,32768]{1,0:T(4,128)(2,1)S(1)} collective-permute-done((bf16[4,32768]{1,0:T(4,128)(2,1)S(1)}, bf16[4,32768]{1,0:T(4,128)(2,1)S(1)}, u32[]{:S(2)}, u32[]{:S(2)}) %collective-permute-start.18) | collective-permute-done | bytes 262176 | tf_op jit(solution)/shard_map/ppermute | solution.py:28
  224.7 3.6 %collective-permute-start.19 = (bf16[8,32768]{1,0:T(8,128)(2,1)S(1)}, bf16[8,32768]{1,0:T(8,128)(2,1)S(1)}, u32[]{:S(2)}, u32[]{:S(2)}) collective-permute-start(bf16[8,32768]{1,0:T(8,128)(2,1)S(1)} %maximum_select_fusion.3), channel_id=1, source_target_pairs={{0,1},{1,0},{2,3},{3,2},{4,5},{5,4},{6,7},{7,6},{8,9},{9,8},{10,11... | collective-permute-start | bytes 1572872 | tf_op jit(solution)/shard_map/ppermute | solution.py:25
  229.7 1.9 collective-permute-start.11
  231.6 3.6 %collective-permute-start.10 = (bf16[2,256,1024]{2,1,0:T(8,128)(2,1)}, bf16[2,256,1024]{2,1,0:T(8,128)(2,1)}, u32[]{:S(2)}, u32[]{:S(2)}) collective-permute-start(bf16[2,256,1024]{2,1,0:T(8,128)(2,1)} %pad_maximum_fusion.3), channel_id=1, source_target_pairs={{0,1},{1,2},{2,3},{3,4},{4,5},{5,6},{6,7},{7,8},{8,9},{9,10},{10,1... | collective-permute-start | bytes 3145736 | tf_op jit(solution)/shard_map/ppermute | solution.py:62
  235.4 1.5 fusion.10
  236.9 2.4 reshape.115
  239.3 2.4 reshape.116
  241.7 15.6 %collective-permute-done.11 = bf16[2,256,1024]{2,1,0:T(8,128)(2,1)} collective-permute-done((bf16[2,256,1024]{2,1,0:T(8,128)(2,1)}, bf16[2,256,1024]{2,1,0:T(8,128)(2,1)}, u32[]{:S(2)}, u32[]{:S(2)}) %collective-permute-start.11) | collective-permute-done | bytes 1048608 | tf_op jit(solution)/shard_map/ppermute | solution.py:63
  257.8 2.3 fusion.8
  260.9 3.7 %convolution_convert_fusion = bf16[128,2048]{1,0:T(8,128)(2,1)} fusion(bf16[128,1024]{1,0:T(8,128)(2,1)S(1)} %copy-done.5, bf16[1024,2048]{1,0:T(8,128)(2,1)} %all-gather.5.cloned.1.call-done), kind=kOutput, calls=%fused_computation.4 | convolution fusion | flops 537133056 | bytes 4980736 | tf_op jit(solution)/shard_map/dot_general | solution.py:222
  (106 shorter events, 24.2 us)
Async XLA Ops:
  7.2 132.4 %all-gather.3.cloned.1.call-start = ((), (), s32[]{:S(2)}) async-start(), calls=%async_computation.2 | async-start | bytes 8912896 | tf_op jit(solution)/shard_map/all_gather | solution.py:145
  12.8 9.2 %copy-start.10 = (s32[3]{0:T(128)S(1)}, s32[3]{0:T(128)}, u32[]{:S(2)}) copy-start(s32[3]{0:T(128)} %constant.80.clone) | copy-start | bytes 40
  12.8 9.2 %copy-start.9 = (s32[1,3]{1,0:T(1,128)S(1)}, s32[1,3]{1,0:T(1,128)}, u32[]{:S(2)}) copy-start(s32[1,3]{1,0:T(1,128)} %param.14) | copy-start | bytes 40
  12.8 6.6 %collective-permute-start.2 = (bf16[8,32768]{1,0:T(8,128)(2,1)}, bf16[8,32768]{1,0:T(8,128)(2,1)S(1)}, u32[]{:S(2)}, u32[]{:S(2)}) collective-permute-start(bf16[8,32768]{1,0:T(8,128)(2,1)} %select_n.265), channel_id=1, source_target_pairs={{0,1},{1,0},{2,3},{3,2},{4,5},{5,4},{6,7},{7,6},{8,9},{9,8},{10,11... | collective-permute-start | bytes 1572872 | tf_op jit(solution)/shard_map/ppermute | solution.py:25
  13.5 41.1 %collective-permute-start.1 = (bf16[2,128,1024]{2,1,0:T(8,128)(2,1)}, bf16[2,128,1024]{2,1,0:T(8,128)(2,1)S(1)}, u32[]{:S(2)}, u32[]{:S(2)}) collective-permute-start(bf16[2,128,1024]{2,1,0:T(8,128)(2,1)} %get-tuple-element.32), channel_id=1, source_target_pairs={{1,0},{2,1},{3,2},{4,3},{5,4},{6,5},{7,6},{8,7},{9,8},{10,9},{11,1... | collective-permute-start | bytes 1572872 | tf_op jit(solution)/shard_map/ppermute | solution.py:63
  15.5 39.1 %collective-permute-start = (bf16[2,128,1024]{2,1,0:T(8,128)(2,1)}, bf16[2,128,1024]{2,1,0:T(8,128)(2,1)S(1)}, u32[]{:S(2)}, u32[]{:S(2)}) collective-permute-start(bf16[2,128,1024]{2,1,0:T(8,128)(2,1)} %get-tuple-element.32), channel_id=1, source_target_pairs={{0,1},{1,2},{2,3},{3,4},{4,5},{5,6},{6,7},{7,8},{8,9},{9,10},{10,1... | collective-permute-start | bytes 1572872 | tf_op jit(solution)/shard_map/ppermute | solution.py:62
  19.1 241.8 %all-gather.5.cloned.1.call-start = ((), (), s32[]{:S(2)}) async-start(), calls=%async_computation.3 | async-start | bytes 4456448 | tf_op jit(solution)/shard_map/all_gather | solution.py:147
  19.4 35.3 %copy-start.3 = (bf16[128,1024]{1,0:T(8,128)(2,1)S(1)}, bf16[128,1024]{1,0:T(8,128)(2,1)}, u32[]{:S(2)}) copy-start(bf16[128,1024]{1,0:T(8,128)(2,1)} %param.10) | copy-start | bytes 786436
  19.4 35.2 %copy-start.4 = (bf16[128,1024]{1,0:T(8,128)(2,1)S(1)}, bf16[128,1024]{1,0:T(8,128)(2,1)}, u32[]{:S(2)}) copy-start(bf16[128,1024]{1,0:T(8,128)(2,1)} %param.9) | copy-start | bytes 786436
  19.8 21.5 %collective-permute-start.3 = (bf16[4,32768]{1,0:T(4,128)(2,1)S(1)}, bf16[4,32768]{1,0:T(4,128)(2,1)S(1)}, u32[]{:S(2)}, u32[]{:S(2)}) collective-permute-start(bf16[4,32768]{1,0:T(4,128)(2,1)S(1)} %broadcast_select_fusion.5), channel_id=1, source_target_pairs={{0,2},{2,0},{4,6},{6,4},{8,10},{10,8},{12,14},{14,12},{1,3},{3,1},... | collective-permute-start | bytes 786440 | tf_op jit(solution)/shard_map/ppermute | solution.py:28
  41.7 9.4 %collective-permute-start.4 = (bf16[2,32768]{1,0:T(2,128)(2,1)S(1)}, bf16[2,32768]{1,0:T(2,128)(2,1)S(1)}, u32[]{:S(2)}, u32[]{:S(2)}) collective-permute-start(bf16[2,32768]{1,0:T(2,128)(2,1)S(1)} %broadcast_select_fusion.6), channel_id=1, source_target_pairs={{0,4},{2,6},{4,0},{6,2},{8,12},{10,14},{12,8},{14,10},{1,5},{3,7},... | collective-permute-start | bytes 393224 | tf_op jit(solution)/shard_map/ppermute | solution.py:28
  51.6 11.5 %collective-permute-start.5 = (bf16[1,32768]{1,0:T(2,128)(2,1)S(1)}, bf16[1,32768]{1,0:T(2,128)(2,1)S(1)}, u32[]{:S(2)}, u32[]{:S(2)}) collective-permute-start(bf16[1,32768]{1,0:T(2,128)(2,1)S(1)} %broadcast_select_fusion.10), channel_id=1, source_target_pairs={{0,8},{2,10},{4,12},{6,14},{8,0},{10,2},{12,4},{14,6},{1,9},{3,11}... | collective-permute-start | bytes 196616 | tf_op jit(solution)/shard_map/ppermute | solution.py:28
  54.6 12.7 %copy-start.6 = (bf16[2,128,1024]{2,1,0:T(8,128)(2,1)}, bf16[2,128,1024]{2,1,0:T(8,128)(2,1)S(1)}, u32[]{:S(2)}) copy-start(bf16[2,128,1024]{2,1,0:T(8,128)(2,1)S(1)} %collective-permute-done) | copy-start | bytes 1572868
  63.4 16.8 %collective-permute-start.6 = (bf16[1,32768]{1,0:T(2,128)(2,1)S(1)}, bf16[1,32768]{1,0:T(2,128)(2,1)S(1)}, u32[]{:S(2)}, u32[]{:S(2)}) collective-permute-start(bf16[1,32768]{1,0:T(2,128)(2,1)S(1)} %fusion.26), channel_id=1, source_target_pairs={{0,8},{2,10},{4,12},{6,14},{8,0},{10,2},{12,4},{14,6},{1,9},{3,11}... | collective-permute-start | bytes 196616 | tf_op jit(solution)/shard_map/ppermute | solution.py:28
  80.8 12.6 %collective-permute-start.7 = (bf16[2,32768]{1,0:T(2,128)(2,1)S(1)}, bf16[2,32768]{1,0:T(2,128)(2,1)S(1)}, u32[]{:S(2)}, u32[]{:S(2)}) collective-permute-start(bf16[2,32768]{1,0:T(2,128)(2,1)S(1)} %broadcast_select_fusion.13), channel_id=1, source_target_pairs={{0,4},{2,6},{4,0},{6,2},{8,12},{10,14},{12,8},{14,10},{1,5},{3,7},... | collective-permute-start | bytes 393224 | tf_op jit(solution)/shard_map/ppermute | solution.py:28
  93.8 5.7 %collective-permute-start.8 = (bf16[4,32768]{1,0:T(4,128)(2,1)S(1)}, bf16[4,32768]{1,0:T(4,128)(2,1)S(1)}, u32[]{:S(2)}, u32[]{:S(2)}) collective-permute-start(bf16[4,32768]{1,0:T(4,128)(2,1)S(1)} %maximum_select_fusion.4), channel_id=1, source_target_pairs={{0,2},{2,0},{4,6},{6,4},{8,10},{10,8},{12,14},{14,12},{1,3},{3,1},... | collective-permute-start | bytes 786440 | tf_op jit(solution)/shard_map/ppermute | solution.py:28
  100.0 8.0 %collective-permute-start.9 = (bf16[8,32768]{1,0:T(8,128)(2,1)S(1)}, bf16[8,32768]{1,0:T(8,128)(2,1)S(1)}, u32[]{:S(2)}, u32[]{:S(2)}) collective-permute-start(bf16[8,32768]{1,0:T(8,128)(2,1)S(1)} %maximum_select_fusion.2), channel_id=1, source_target_pairs={{0,1},{1,0},{2,3},{3,2},{4,5},{5,4},{6,7},{7,6},{8,9},{9,8},{10,11... | collective-permute-start | bytes 1572872 | tf_op jit(solution)/shard_map/ppermute | solution.py:25
  113.0 1.3 copy-start
  114.3 25.3 %copy-start.7 = (bf16[64,2048]{1,0:T(8,128)(2,1)S(1)}, bf16[64,2048]{1,0:T(8,128)(2,1)}, u32[]{:S(2)}) copy-start(bf16[64,2048]{1,0:T(8,128)(2,1)} %param.11) | copy-start | bytes 786436
  146.4 18.5 %all-to-all-start = ((bf16[16,128,64]{1,2,0:T(8,128)(2,1)}), bf16[16,128,64]{1,2,0:T(8,128)(2,1)S(1)}, u32[]{:S(2)}, u32[]{:S(2)}) async-start(bf16[16,128,64]{1,2,0:T(8,128)(2,1)} %bitcast.113), calls=%async_computation | async-start | bytes 524288 | tf_op jit(solution)/shard_map/all_to_all | solution.py:180
  181.4 1.0 copy-start.8
  181.8 3.2 %copy-start.2 = (f32[1024,1024]{1,0:T(8,128)S(1)}, f32[1024,1024]{1,0:T(8,128)}, u32[]{:S(2)}) copy-start(f32[1024,1024]{1,0:T(8,128)} %get-tuple-element.14) | copy-start | bytes 12582916
  181.9 4.9 %collective-permute-start.12 = (bf16[8,32768]{1,0:T(8,128)(2,1)S(1)}, bf16[8,32768]{1,0:T(8,128)(2,1)S(1)}, u32[]{:S(2)}, u32[]{:S(2)}) collective-permute-start(bf16[8,32768]{1,0:T(8,128)(2,1)S(1)} %convert_element_type.83), channel_id=1, source_target_pairs={{0,1},{1,0},{2,3},{3,2},{4,5},{5,4},{6,7},{7,6},{8,9},{9,8},{10,11... | collective-permute-start | bytes 1572872 | tf_op jit(solution)/shard_map/ppermute | solution.py:25
  182.4 4.2 %copy-start.1 = (f32[1024,1024]{1,0:T(8,128)S(1)}, f32[1024,1024]{1,0:T(8,128)}, u32[]{:S(2)}) copy-start(f32[1024,1024]{1,0:T(8,128)} %get-tuple-element.13) | copy-start | bytes 12582916
  187.1 7.6 %collective-permute-start.13 = (bf16[4,32768]{1,0:T(4,128)(2,1)S(1)}, bf16[4,32768]{1,0:T(4,128)(2,1)S(1)}, u32[]{:S(2)}, u32[]{:S(2)}) collective-permute-start(bf16[4,32768]{1,0:T(4,128)(2,1)S(1)} %select_convert_fusion.1), channel_id=1, source_target_pairs={{0,2},{2,0},{4,6},{6,4},{8,10},{10,8},{12,14},{14,12},{1,3},{3,1},... | collective-permute-start | bytes 786440 | tf_op jit(solution)/shard_map/ppermute | solution.py:28
  195.0 3.9 %collective-permute-start.14 = (bf16[2,32768]{1,0:T(2,128)(2,1)S(1)}, bf16[2,32768]{1,0:T(2,128)(2,1)S(1)}, u32[]{:S(2)}, u32[]{:S(2)}) collective-permute-start(bf16[2,32768]{1,0:T(2,128)(2,1)S(1)} %select_convert_fusion.2), channel_id=1, source_target_pairs={{0,4},{2,6},{4,0},{6,2},{8,12},{10,14},{12,8},{14,10},{1,5},{3,7},... | collective-permute-start | bytes 393224 | tf_op jit(solution)/shard_map/ppermute | solution.py:28
  199.3 5.0 %collective-permute-start.15 = (bf16[1,32768]{1,0:T(2,128)(2,1)S(1)}, bf16[1,32768]{1,0:T(2,128)(2,1)S(1)}, u32[]{:S(2)}, u32[]{:S(2)}) collective-permute-start(bf16[1,32768]{1,0:T(2,128)(2,1)S(1)} %fusion.29), channel_id=1, source_target_pairs={{0,8},{2,10},{4,12},{6,14},{8,0},{10,2},{12,4},{14,6},{1,9},{3,11}... | collective-permute-start | bytes 196616 | tf_op jit(solution)/shard_map/ppermute | solution.py:28
  204.6 7.9 %collective-permute-start.16 = (bf16[1,32768]{1,0:T(2,128)(2,1)S(1)}, bf16[1,32768]{1,0:T(2,128)(2,1)S(1)}, u32[]{:S(2)}, u32[]{:S(2)}) collective-permute-start(bf16[1,32768]{1,0:T(2,128)(2,1)S(1)} %fusion.28), channel_id=1, source_target_pairs={{0,8},{2,10},{4,12},{6,14},{8,0},{10,2},{12,4},{14,6},{1,9},{3,11}... | collective-permute-start | bytes 196616 | tf_op jit(solution)/shard_map/ppermute | solution.py:28
  213.1 3.9 %collective-permute-start.17 = (bf16[2,32768]{1,0:T(2,128)(2,1)S(1)}, bf16[2,32768]{1,0:T(2,128)(2,1)S(1)}, u32[]{:S(2)}, u32[]{:S(2)}) collective-permute-start(bf16[2,32768]{1,0:T(2,128)(2,1)S(1)} %broadcast_select_fusion.12), channel_id=1, source_target_pairs={{0,4},{2,6},{4,0},{6,2},{8,12},{10,14},{12,8},{14,10},{1,5},{3,7},... | collective-permute-start | bytes 393224 | tf_op jit(solution)/shard_map/ppermute | solution.py:28
  217.4 6.8 %collective-permute-start.18 = (bf16[4,32768]{1,0:T(4,128)(2,1)S(1)}, bf16[4,32768]{1,0:T(4,128)(2,1)S(1)}, u32[]{:S(2)}, u32[]{:S(2)}) collective-permute-start(bf16[4,32768]{1,0:T(4,128)(2,1)S(1)} %maximum_select_fusion.5), channel_id=1, source_target_pairs={{0,2},{2,0},{4,6},{6,4},{8,10},{10,8},{12,14},{14,12},{1,3},{3,1},... | collective-permute-start | bytes 786440 | tf_op jit(solution)/shard_map/ppermute | solution.py:28
  224.7 10.5 %collective-permute-start.19 = (bf16[8,32768]{1,0:T(8,128)(2,1)S(1)}, bf16[8,32768]{1,0:T(8,128)(2,1)S(1)}, u32[]{:S(2)}, u32[]{:S(2)}) collective-permute-start(bf16[8,32768]{1,0:T(8,128)(2,1)S(1)} %maximum_select_fusion.3), channel_id=1, source_target_pairs={{0,1},{1,0},{2,3},{3,2},{4,5},{5,4},{6,7},{7,6},{8,9},{9,8},{10,11... | collective-permute-start | bytes 1572872 | tf_op jit(solution)/shard_map/ppermute | solution.py:25
  229.7 27.7 %collective-permute-start.11 = (bf16[2,256,1024]{2,1,0:T(8,128)(2,1)}, bf16[2,256,1024]{2,1,0:T(8,128)(2,1)}, u32[]{:S(2)}, u32[]{:S(2)}) collective-permute-start(bf16[2,256,1024]{2,1,0:T(8,128)(2,1)} %pad_maximum_fusion.3), channel_id=1, source_target_pairs={{1,0},{2,1},{3,2},{4,3},{5,4},{6,5},{7,6},{8,7},{9,8},{10,9},{11,1... | collective-permute-start | bytes 3145736 | tf_op jit(solution)/shard_map/ppermute | solution.py:63
  231.6 26.2 %collective-permute-start.10 = (bf16[2,256,1024]{2,1,0:T(8,128)(2,1)}, bf16[2,256,1024]{2,1,0:T(8,128)(2,1)}, u32[]{:S(2)}, u32[]{:S(2)}) collective-permute-start(bf16[2,256,1024]{2,1,0:T(8,128)(2,1)} %pad_maximum_fusion.3), channel_id=1, source_target_pairs={{0,1},{1,2},{2,3},{3,4},{4,5},{5,6},{6,7},{7,8},{8,9},{9,10},{10,1... | collective-permute-start | bytes 3145736 | tf_op jit(solution)/shard_map/ppermute | solution.py:62
  241.7 19.1 %copy-start.5 = (bf16[128,1024]{1,0:T(8,128)(2,1)S(1)}, bf16[128,1024]{1,0:T(8,128)(2,1)}, u32[]{:S(2)}) copy-start(bf16[128,1024]{1,0:T(8,128)(2,1)} %shard_map.119) | copy-start | bytes 786436
Sparse Core Ops, SparseCore 0:
  19.2 82.9 all-gather.2
  139.7 54.5 all-gather.4

commit v7 on v4

--- a/solution.py
+++ b/solution.py
@@ -55,6 +55,27 @@
     return parts.reshape(shape)
 
 
+def core_swap(x):
+    n = lax.axis_size("core")
+    return lax.ppermute(x, "core", [(i, i ^ 1) for i in range(n)])
+
+
+def gather_rows_deduped(x):
+    core = lax.axis_index("core")
+    rows, cols = x.shape
+    half = cols // 2
+    partner = core_swap(x)
+    pair = jnp.where(core == 0, jnp.concatenate([x, partner]), jnp.concatenate([partner, x]))
+    mine = lax.dynamic_slice_in_dim(pair, core * half, half, axis=1)
+    gathered = lax.all_gather(mine, "chip", axis=0, tiled=True)
+    other = core_swap(gathered)
+    return jnp.where(
+        core == 0,
+        jnp.concatenate([gathered, other], axis=1),
+        jnp.concatenate([other, gathered], axis=1),
+    )
+
+
 def halo(shard):
     count = lax.axis_size("chip") * lax.axis_size("core")
     up = [(i, i + 1) for i in range(count - 1)]
@@ -114,7 +135,7 @@
     total_blocks = blocks_dev * count
     device = flat_index()
 
-    grad_out_all = lax.all_gather(grad_out, SEQ, axis=0, tiled=True)
+    grad_out_all = gather_rows_deduped(grad_out)
     weight_all = lax.all_gather(out_weight, SEQ, axis=0, tiled=True)
 
     paired = jnp.stack([keys, values])

time: 258 us -> 262 us (1.016)
  starting transfers between devices: 72 us -> 58.4 us
  waiting for transfers between devices: 86.5 us -> 95.9 us
  local copies, waits for them, and re-layouts: 25.4 us -> 29.9 us
  matrix products: 15.5 us -> 19.5 us
    all_gather x1, waiting for transfers between devices: 0.01 us -> 18.6 us  [gather_rows_deduped(): gathered = lax.all_gather(mine, 'chip', axis=0, tiled=True)]
    ppermute x12, starting transfers between devices: 42.5 us -> 26.7 us  [xor_swap(): return lax.ppermute(x, 'chip', [(i, i ^ m) for i in range(n)])]
    ppermute x12, waiting for transfers between devices: 46.7 us -> 37.5 us  [xor_swap(): return lax.ppermute(x, 'chip', [(i, i ^ m) for i in range(n)])]
    unnamed x48, local copies, waits for them, and re-layouts: 3.75 us -> 8.99 us
    dot_general x1, matrix products: 5.74 us -> 9.17 us  [local(): lax.dot_general(attn_cols, grad_out_all, (((0,), (0,)), ((), ())), prefer...]
  transfers between devices with their start and end apart: 24 -> 26, of which waited for: 14 -> 15; matrix products, arithmetic and copies ran while one was open for 24% -> 27% of each run, Pallas kernels for 5% -> 5%
where the time goes in v7:
time: 262 us; the launch traced here: 261 us
  waiting for transfers between devices  95.9 us (37%)
  starting transfers between devices  58.4 us (22%)
  local copies, waits for them, and re-layouts  29.9 us (11%)
  other arithmetic  27.6 us (11%)
  matrix products  19.5 us (7%)
  between operations  17.9 us (7%)
  Pallas kernels  12.2 us (5%)
    ppermute x12, waiting for transfers between devices, xor_swap(): return lax.ppermute(x, 'chip', [(i, i ^ m) for i in range(n)])  37.5 us
    ppermute x12, starting transfers between devices, xor_swap(): return lax.ppermute(x, 'chip', [(i, i ^ m) for i in range(n)])  26.7 us
    all_gather x1, waiting for transfers between devices, gather_rows_deduped(): gathered = lax.all_gather(mine, 'chip', axis=0, tiled=True)  18.6 us
    all_to_all x1, waiting for transfers between devices, local(): lax.all_to_all(attn_out.reshape(tok_rows, count, w_rows), SEQ, 1, 0, tile...  17.8 us
    pallas_call x1, Pallas kernels, attention(): pl.pallas_call(_attn_kernel, grid=(heads,), in_specs=[pl.BlockSpec((1, ke...  12.2 us
    dot_general x1, matrix products, local(): lax.dot_general(attn_cols, grad_out_all, (((0,), (0,)), ((), ())), prefer...  9.17 us
    unnamed x48, local copies, waits for them, and re-layouts  8.99 us
    ppermute x2, waiting for transfers between devices, halo(): after = lax.ppermute(shard, SEQ, down)  8.66 us
  transfers between devices with their start and end apart: 26, of which 15 were waited for; matrix products, arithmetic and copies ran while one was open for 27% of the time, Pallas kernels for 5%

profile of v7, /device:TPU:11, one launch (start us, length us, event | category | flops | bytes accessed | tf_op | source)
XLA Modules:
  0.0 261.4 jit_solution(6168612788207541998)
XLA Ops:
  8.0 1.7 collective-permute-done.10
  9.7 2.0 fusion.11
  14.7 3.4 %collective-permute-start = (bf16[2,128,1024]{2,1,0:T(8,128)(2,1)}, bf16[2,128,1024]{2,1,0:T(8,128)(2,1)S(1)}, u32[]{:S(2)}, u32[]{:S(2)}) collective-permute-start(bf16[2,128,1024]{2,1,0:T(8,128)(2,1)} %get-tuple-element.30), channel_id=1, source_target_pairs={{0,1},{1,2},{2,3},{3,4},{4,5},{5,6},{6,7},{7,8},{8,9},{9,10},{10,1... | collective-permute-start | bytes 1572872 | tf_op jit(solution)/shard_map/ppermute | solution.py:83
  18.1 1.9 collective-permute-start.1
  21.0 1.5 collective-permute-start.2
  26.3 5.2 %collective-permute-done = bf16[2,128,1024]{2,1,0:T(8,128)(2,1)S(1)} collective-permute-done((bf16[2,128,1024]{2,1,0:T(8,128)(2,1)}, bf16[2,128,1024]{2,1,0:T(8,128)(2,1)S(1)}, u32[]{:S(2)}, u32[]{:S(2)}) %collective-permute-start) | collective-permute-done | bytes 524320 | tf_op jit(solution)/shard_map/ppermute | solution.py:83
  31.5 8.7 %collective-permute-done.1 = bf16[2,128,1024]{2,1,0:T(8,128)(2,1)S(1)} collective-permute-done((bf16[2,128,1024]{2,1,0:T(8,128)(2,1)}, bf16[2,128,1024]{2,1,0:T(8,128)(2,1)S(1)}, u32[]{:S(2)}, u32[]{:S(2)}) %collective-permute-start.1) | collective-permute-done | bytes 524320 | tf_op jit(solution)/shard_map/ppermute | solution.py:84
  43.6 3.3 %collective-permute-done.4 = bf16[2,32768]{1,0:T(2,128)(2,1)S(1)} collective-permute-done((bf16[2,32768]{1,0:T(2,128)(2,1)S(1)}, bf16[2,32768]{1,0:T(2,128)(2,1)S(1)}, u32[]{:S(2)}, u32[]{:S(2)}) %collective-permute-start.4) | collective-permute-done | bytes 131104 | tf_op jit(solution)/shard_map/ppermute | solution.py:28
  47.4 1.8 collective-permute-start.5
  50.1 2.2 collective-permute-done.5
  52.6 1.8 collective-permute-start.6
  55.0 12.1 %collective-permute-done.6 = bf16[1,32768]{1,0:T(2,128)(2,1)S(1)} collective-permute-done((bf16[1,32768]{1,0:T(2,128)(2,1)S(1)}, bf16[1,32768]{1,0:T(2,128)(2,1)S(1)}, u32[]{:S(2)}, u32[]{:S(2)}) %collective-permute-start.6) | collective-permute-done | bytes 65568 | tf_op jit(solution)/shard_map/ppermute | solution.py:28
  67.8 7.9 %collective-permute-start.7 = (bf16[2,32768]{1,0:T(2,128)(2,1)S(1)}, bf16[2,32768]{1,0:T(2,128)(2,1)S(1)}, u32[]{:S(2)}, u32[]{:S(2)}) collective-permute-start(bf16[2,32768]{1,0:T(2,128)(2,1)S(1)} %broadcast_select_fusion.13), channel_id=1, source_target_pairs={{0,4},{2,6},{4,0},{6,2},{8,12},{10,14},{12,8},{14,10},{1,5},{3,7},... | collective-permute-start | bytes 393224 | tf_op jit(solution)/shard_map/ppermute | solution.py:28
  77.2 18.6 %all-gather.3.cloned.1.call-done = bf16[2048,1024]{1,0:T(8,128)(2,1)} async-done(((bf16[256,1024]{1,0:T(8,128)(2,1)}), bf16[2048,1024]{1,0:T(8,128)(2,1)}) %all-gather.3.cloned.1.call-update) | async-done | bytes 4194320 | tf_op jit(solution)/shard_map/all_gather | solution.py:70
  96.7 3.6 %collective-permute-start.8 = (bf16[4,32768]{1,0:T(4,128)(2,1)S(1)}, bf16[4,32768]{1,0:T(4,128)(2,1)S(1)}, u32[]{:S(2)}, u32[]{:S(2)}) collective-permute-start(bf16[4,32768]{1,0:T(4,128)(2,1)S(1)} %maximum_select_fusion.9), channel_id=1, source_target_pairs={{0,2},{2,0},{4,6},{6,4},{8,10},{10,8},{12,14},{14,12},{1,3},{3,1},... | collective-permute-start | bytes 786440 | tf_op jit(solution)/shard_map/ppermute | solution.py:28
  102.5 4.5 %collective-permute-done.8 = bf16[4,32768]{1,0:T(4,128)(2,1)S(1)} collective-permute-done((bf16[4,32768]{1,0:T(4,128)(2,1)S(1)}, bf16[4,32768]{1,0:T(4,128)(2,1)S(1)}, u32[]{:S(2)}, u32[]{:S(2)}) %collective-permute-start.8) | collective-permute-done | bytes 262176 | tf_op jit(solution)/shard_map/ppermute | solution.py:28
  108.1 6.6 %fusion.2 = bf16[8,16,8,128]{3,2,1,0:T(8,128)(2,1)S(1)} fusion(bf16[64,2048]{1,0:T(8,128)(2,1)S(1)} %copy-done.12, bf16[2048,1024]{1,0:T(8,128)(2,1)S(1)} %collective-permute-done.11, bf16[2048,1024]{1,0:T(8,128)(2,1)} %all-gather.3.cloned.1.call-done, pred[]{:T(512)S(6)} %eq.47), kind=kOutput, calls=%fused_computation.13 | convolution fusion | flops 574750720 | bytes 8912897 | tf_op jit(solution)/shard_map/dot_general | solution.py:169
  115.6 7.6 %all-to-all-start = ((bf16[16,128,64]{1,2,0:T(8,128)(2,1)}), bf16[16,128,64]{1,2,0:T(8,128)(2,1)S(1)}, u32[]{:S(2)}, u32[]{:S(2)}) async-start(bf16[16,128,64]{1,2,0:T(8,128)(2,1)} %bitcast.111), calls=%async_computation | async-start | bytes 524288 | tf_op jit(solution)/shard_map/all_to_all | solution.py:172
  125.6 6.3 %all-to-all-done = bf16[16,128,64]{1,2,0:T(8,128)(2,1)S(1)} async-done(((bf16[16,128,64]{1,2,0:T(8,128)(2,1)}), bf16[16,128,64]{1,2,0:T(8,128)(2,1)S(1)}, u32[]{:S(2)}, u32[]{:S(2)}) %all-to-all-start) | async-done | bytes 262176 | tf_op jit(solution)/shard_map/all_to_all | solution.py:172
  133.5 12.2 %shard_map.119 = (bf16[128,1024]{1,0:T(8,128)(2,1)}, bf16[128,1024]{1,0:T(8,128)(2,1)}, f32[1024,1024]{1,0:T(8,128)}, f32[1024,1024]{1,0:T(8,128)}) custom-call(f32[1,1024]{1,0:T(1,128)} %bitcast.125, bf16[128,1024]{1,0:T(8,128)(2,1)} %q_ref.1, bf16[1024,1024]{1,0:T(8,128)(2,1)} %get-tuple-element.20.k_ref, bf16[1024,1024]{1,0:T(8,128)(2,1)} %get-tuple-element.19.v_ref, ...), custom_call_target="tpu_custom_call" | custom-call | tf_op jit(solution)/shard_map/pallas_call | solution.py:116
  145.6 1.4 slice.234
  147.1 1.8 slice.235
  149.0 2.2 slice_select_fusion
  153.7 2.1 convert_element_type.83
  155.7 2.7 %broadcast_select_fusion = f32[1,2,128,1024]{3,2,0,1:T(8,128)} fusion(pred[]{:T(512)S(6)} %eq.19, f32[2,1,128,1024]{3,2,0,1:T(8,128)} %bitcast.117, f32[2,1,128,1024]{3,2,0,1:T(8,128)} %bitcast.115), kind=kLoop, calls=%fused_computation.57 | loop fusion | flops 786432 | bytes 3145729 | tf_op jit(solution)/shard_map/jit(_where)/select_n | solution.py:43
  158.4 2.4 select_n.304
  160.8 1.3 fusion.17
  162.1 1.1 add_dynamic-update-slice_fusion.3
  163.3 1.1 convert_add_fusion
  165.6 1.1 add_dynamic-update-slice_fusion.2
  168.0 4.0 %collective-permute-done.15 = bf16[4,32768]{1,0:T(4,128)(2,1)S(1)} collective-permute-done((bf16[4,32768]{1,0:T(4,128)(2,1)S(1)}, bf16[4,32768]{1,0:T(4,128)(2,1)S(1)}, u32[]{:S(2)}, u32[]{:S(2)}) %collective-permute-start.15) | collective-permute-done | bytes 262176 | tf_op jit(solution)/shard_map/ppermute | solution.py:28
  172.4 2.1 collective-permute-start.16
  175.7 1.7 collective-permute-done.16
  178.3 4.3 %collective-permute-done.17 = bf16[1,32768]{1,0:T(2,128)(2,1)S(1)} collective-permute-done((bf16[1,32768]{1,0:T(2,128)(2,1)S(1)}, bf16[1,32768]{1,0:T(2,128)(2,1)S(1)}, u32[]{:S(2)}, u32[]{:S(2)}) %collective-permute-start.17) | collective-permute-done | bytes 65568 | tf_op jit(solution)/shard_map/ppermute | solution.py:28
  183.2 4.6 %collective-permute-done.18 = bf16[1,32768]{1,0:T(2,128)(2,1)S(1)} collective-permute-done((bf16[1,32768]{1,0:T(2,128)(2,1)S(1)}, bf16[1,32768]{1,0:T(2,128)(2,1)S(1)}, u32[]{:S(2)}, u32[]{:S(2)}) %collective-permute-start.18) | collective-permute-done | bytes 65568 | tf_op jit(solution)/shard_map/ppermute | solution.py:28
  188.3 6.1 %collective-permute-start.19 = (bf16[2,32768]{1,0:T(2,128)(2,1)S(1)}, bf16[2,32768]{1,0:T(2,128)(2,1)S(1)}, u32[]{:S(2)}, u32[]{:S(2)}) collective-permute-start(bf16[2,32768]{1,0:T(2,128)(2,1)S(1)} %broadcast_select_fusion.12), channel_id=1, source_target_pairs={{0,4},{2,6},{4,0},{6,2},{8,12},{10,14},{12,8},{14,10},{1,5},{3,7},... | collective-permute-start | bytes 393224 | tf_op jit(solution)/shard_map/ppermute | solution.py:28
  195.5 3.2 %collective-permute-start.12 = (bf16[2,256,1024]{2,1,0:T(8,128)(2,1)}, bf16[2,256,1024]{2,1,0:T(8,128)(2,1)}, u32[]{:S(2)}, u32[]{:S(2)}) collective-permute-start(bf16[2,256,1024]{2,1,0:T(8,128)(2,1)} %pad_maximum_fusion.3), channel_id=1, source_target_pairs={{0,1},{1,2},{2,3},{3,4},{4,5},{5,6},{6,7},{7,8},{8,9},{9,10},{10,1... | collective-permute-start | bytes 3145736 | tf_op jit(solution)/shard_map/ppermute | solution.py:83
  198.7 3.3 %collective-permute-start.13 = (bf16[2,256,1024]{2,1,0:T(8,128)(2,1)}, bf16[2,256,1024]{2,1,0:T(8,128)(2,1)}, u32[]{:S(2)}, u32[]{:S(2)}) collective-permute-start(bf16[2,256,1024]{2,1,0:T(8,128)(2,1)} %pad_maximum_fusion.3), channel_id=1, source_target_pairs={{1,0},{2,1},{3,2},{4,3},{5,4},{6,5},{7,6},{8,7},{9,8},{10,9},{11,1... | collective-permute-start | bytes 3145736 | tf_op jit(solution)/shard_map/ppermute | solution.py:84
  202.9 5.6 %all-to-all-start.1 = ((bf16[1,128,16,64]{1,3,0,2:T(8,128)(2,1)}), bf16[1,128,16,64]{1,3,0,2:T(8,128)(2,1)S(1)}, u32[]{:S(2)}, u32[]{:S(2)}) async-start(bf16[1,128,16,64]{1,3,0,2:T(8,128)(2,1)} %bitcast.35), calls=%async_computation.1 | async-start | bytes 524288 | tf_op jit(solution)/shard_map/all_to_all | solution.py:216
  209.0 1.2 collective-permute-start.20
  210.2 3.7 %convolution_convert_fusion = bf16[128,2048]{1,0:T(8,128)(2,1)} fusion(bf16[128,1024]{1,0:T(8,128)(2,1)S(1)} %copy-done.11, bf16[1024,2048]{1,0:T(8,128)(2,1)} %all-gather.5.cloned.1.call-done), kind=kOutput, calls=%fused_computation.5 | convolution fusion | flops 537133056 | bytes 4980736 | tf_op jit(solution)/shard_map/dot_general | solution.py:213
  213.9 17.8 %all-to-all-done.1 = bf16[1,128,16,64]{1,3,0,2:T(8,128)(2,1)S(1)} async-done(((bf16[1,128,16,64]{1,3,0,2:T(8,128)(2,1)}), bf16[1,128,16,64]{1,3,0,2:T(8,128)(2,1)S(1)}, u32[]{:S(2)}, u32[]{:S(2)}) %all-to-all-start.1) | async-done | bytes 262176 | tf_op jit(solution)/shard_map/all_to_all | solution.py:216
  232.4 3.3 %collective-permute-start.21 = (bf16[8,32768]{1,0:T(8,128)(2,1)S(1)}, bf16[8,32768]{1,0:T(8,128)(2,1)S(1)}, u32[]{:S(2)}, u32[]{:S(2)}) collective-permute-start(bf16[8,32768]{1,0:T(8,128)(2,1)S(1)} %maximum_select_fusion.8), channel_id=1, source_target_pairs={{0,1},{1,0},{2,3},{3,2},{4,5},{5,4},{6,7},{7,6},{8,9},{9,8},{10,11... | collective-permute-start | bytes 1572872 | tf_op jit(solution)/shard_map/ppermute | solution.py:25
  235.6 9.2 %fusion.1 = f32[64,2048]{1,0:T(8,128)} fusion(bf16[2048,1024]{1,0:T(8,128)(2,1)} %copy-done.15, bf16[2048,1024]{1,0:T(8,128)(2,1)} %all-gather.3.cloned.1.call-done, pred[]{:T(512)S(6)} %eq.47, bf16[8,8,16,128]{3,2,1,0:T(8,128)(2,1)S(1)} %bitcast.124), kind=kOutput, calls=%fused_computation.12 | convolution fusion | flops 574619648 | bytes 9175041 | tf_op jit(solution)/shard_map/dot_general | solution.py:219
  245.0 1.4 fusion.14
  246.4 2.6 reshape.115
  249.0 2.4 reshape.116
  251.4 2.3 fusion.9
  (125 shorter events, 34.3 us)
Async XLA Ops:
  7.2 4.7 %copy-start.13 = (s32[2]{0:T(128)S(1)}, s32[2]{0:T(128)}, u32[]{:S(2)}) copy-start(s32[2]{0:T(128)} %param.13) | copy-start | bytes 28
  7.2 6.6 %copy-start.10 = (bf16[128,1024]{1,0:T(8,128)(2,1)S(1)}, bf16[128,1024]{1,0:T(8,128)(2,1)}, u32[]{:S(2)}) copy-start(bf16[128,1024]{1,0:T(8,128)(2,1)} %param.9) | copy-start | bytes 786436
  7.2 6.6 %copy-start.9 = (bf16[128,1024]{1,0:T(8,128)(2,1)S(1)}, bf16[128,1024]{1,0:T(8,128)(2,1)}, u32[]{:S(2)}) copy-start(bf16[128,1024]{1,0:T(8,128)(2,1)} %param.10) | copy-start | bytes 786436
  7.2 88.6 %all-gather.3.cloned.1.call-start = ((), (), s32[]{:S(2)}) async-start(), calls=%async_computation.2 | async-start | bytes 4718592 | tf_op jit(solution)/shard_map/all_gather | solution.py:70
  7.2 2.5 collective-permute-start.10
  11.8 10.8 %copy-start.16 = (s32[1,3]{1,0:T(1,128)S(1)}, s32[1,3]{1,0:T(1,128)}, u32[]{:S(2)}) copy-start(s32[1,3]{1,0:T(1,128)} %param.14) | copy-start | bytes 40
  11.8 198.4 %all-gather.5.cloned.1.call-start = ((), (), s32[]{:S(2)}) async-start(), calls=%async_computation.3 | async-start | bytes 4456448 | tf_op jit(solution)/shard_map/all_gather | solution.py:139
  13.8 11.6 %copy-start.17 = (s32[3]{0:T(128)S(1)}, s32[3]{0:T(128)}, u32[]{:S(2)}) copy-start(s32[3]{0:T(128)} %constant.84.clone) | copy-start | bytes 40
  14.7 16.8 %collective-permute-start = (bf16[2,128,1024]{2,1,0:T(8,128)(2,1)}, bf16[2,128,1024]{2,1,0:T(8,128)(2,1)S(1)}, u32[]{:S(2)}, u32[]{:S(2)}) collective-permute-start(bf16[2,128,1024]{2,1,0:T(8,128)(2,1)} %get-tuple-element.30), channel_id=1, source_target_pairs={{0,1},{1,2},{2,3},{3,4},{4,5},{5,6},{6,7},{7,8},{8,9},{9,10},{10,1... | collective-permute-start | bytes 1572872 | tf_op jit(solution)/shard_map/ppermute | solution.py:83
  18.1 22.1 %collective-permute-start.1 = (bf16[2,128,1024]{2,1,0:T(8,128)(2,1)}, bf16[2,128,1024]{2,1,0:T(8,128)(2,1)S(1)}, u32[]{:S(2)}, u32[]{:S(2)}) collective-permute-start(bf16[2,128,1024]{2,1,0:T(8,128)(2,1)} %get-tuple-element.30), channel_id=1, source_target_pairs={{1,0},{2,1},{3,2},{4,3},{5,4},{6,5},{7,6},{8,7},{9,8},{10,9},{11,1... | collective-permute-start | bytes 1572872 | tf_op jit(solution)/shard_map/ppermute | solution.py:84
  21.0 4.5 %collective-permute-start.2 = (bf16[8,32768]{1,0:T(8,128)(2,1)}, bf16[8,32768]{1,0:T(8,128)(2,1)S(1)}, u32[]{:S(2)}, u32[]{:S(2)}) collective-permute-start(bf16[8,32768]{1,0:T(8,128)(2,1)} %select_n.284), channel_id=1, source_target_pairs={{0,1},{1,0},{2,3},{3,2},{4,5},{5,4},{6,7},{7,6},{8,9},{9,8},{10,11... | collective-permute-start | bytes 1572872 | tf_op jit(solution)/shard_map/ppermute | solution.py:25
  25.9 15.3 %collective-permute-start.3 = (bf16[4,32768]{1,0:T(4,128)(2,1)S(1)}, bf16[4,32768]{1,0:T(4,128)(2,1)S(1)}, u32[]{:S(2)}, u32[]{:S(2)}) collective-permute-start(bf16[4,32768]{1,0:T(4,128)(2,1)S(1)} %broadcast_select_fusion.5), channel_id=1, source_target_pairs={{0,2},{2,0},{4,6},{6,4},{8,10},{10,8},{12,14},{14,12},{1,3},{3,1},... | collective-permute-start | bytes 786440 | tf_op jit(solution)/shard_map/ppermute | solution.py:28
  41.7 5.2 %collective-permute-start.4 = (bf16[2,32768]{1,0:T(2,128)(2,1)S(1)}, bf16[2,32768]{1,0:T(2,128)(2,1)S(1)}, u32[]{:S(2)}, u32[]{:S(2)}) collective-permute-start(bf16[2,32768]{1,0:T(2,128)(2,1)S(1)} %broadcast_select_fusion.6), channel_id=1, source_target_pairs={{0,4},{2,6},{4,0},{6,2},{8,12},{10,14},{12,8},{14,10},{1,5},{3,7},... | collective-permute-start | bytes 393224 | tf_op jit(solution)/shard_map/ppermute | solution.py:28
  47.4 4.8 %collective-permute-start.5 = (bf16[1,32768]{1,0:T(2,128)(2,1)S(1)}, bf16[1,32768]{1,0:T(2,128)(2,1)S(1)}, u32[]{:S(2)}, u32[]{:S(2)}) collective-permute-start(bf16[1,32768]{1,0:T(2,128)(2,1)S(1)} %broadcast_select_fusion.10), channel_id=1, source_target_pairs={{0,8},{2,10},{4,12},{6,14},{8,0},{10,2},{12,4},{14,6},{1,9},{3,11}... | collective-permute-start | bytes 196616 | tf_op jit(solution)/shard_map/ppermute | solution.py:28
  52.6 14.6 %collective-permute-start.6 = (bf16[1,32768]{1,0:T(2,128)(2,1)S(1)}, bf16[1,32768]{1,0:T(2,128)(2,1)S(1)}, u32[]{:S(2)}, u32[]{:S(2)}) collective-permute-start(bf16[1,32768]{1,0:T(2,128)(2,1)S(1)} %fusion.29), channel_id=1, source_target_pairs={{0,8},{2,10},{4,12},{6,14},{8,0},{10,2},{12,4},{14,6},{1,9},{3,11}... | collective-permute-start | bytes 196616 | tf_op jit(solution)/shard_map/ppermute | solution.py:28
  67.8 40.4 %copy-start.12 = (bf16[64,2048]{1,0:T(8,128)(2,1)S(1)}, bf16[64,2048]{1,0:T(8,128)(2,1)}, u32[]{:S(2)}) copy-start(bf16[64,2048]{1,0:T(8,128)(2,1)} %param.11) | copy-start | bytes 786436
  67.8 28.4 %collective-permute-start.7 = (bf16[2,32768]{1,0:T(2,128)(2,1)S(1)}, bf16[2,32768]{1,0:T(2,128)(2,1)S(1)}, u32[]{:S(2)}, u32[]{:S(2)}) collective-permute-start(bf16[2,32768]{1,0:T(2,128)(2,1)S(1)} %broadcast_select_fusion.13), channel_id=1, source_target_pairs={{0,4},{2,6},{4,0},{6,2},{8,12},{10,14},{12,8},{14,10},{1,5},{3,7},... | collective-permute-start | bytes 393224 | tf_op jit(solution)/shard_map/ppermute | solution.py:28
  95.8 12.3 %collective-permute-start.11 = (bf16[2048,1024]{1,0:T(8,128)(2,1)}, bf16[2048,1024]{1,0:T(8,128)(2,1)S(1)}, u32[]{:S(2)}, u32[]{:S(2)}) collective-permute-start(bf16[2048,1024]{1,0:T(8,128)(2,1)} %all-gather.3.cloned.1.call-done), channel_id=1, source_target_pairs={{0,1},{1,0},{2,3},{3,2},{4,5},{5,4},{6,7},{7,6},{8,9},{9,8},{10,11... | collective-permute-start | bytes 12582920 | tf_op jit(solution)/shard_map/ppermute | solution.py:60
  96.7 10.3 %collective-permute-start.8 = (bf16[4,32768]{1,0:T(4,128)(2,1)S(1)}, bf16[4,32768]{1,0:T(4,128)(2,1)S(1)}, u32[]{:S(2)}, u32[]{:S(2)}) collective-permute-start(bf16[4,32768]{1,0:T(4,128)(2,1)S(1)} %maximum_select_fusion.9), channel_id=1, source_target_pairs={{0,2},{2,0},{4,6},{6,4},{8,10},{10,8},{12,14},{14,12},{1,3},{3,1},... | collective-permute-start | bytes 786440 | tf_op jit(solution)/shard_map/ppermute | solution.py:28
  107.5 15.7 %collective-permute-start.9 = (bf16[8,32768]{1,0:T(8,128)(2,1)S(1)}, bf16[8,32768]{1,0:T(8,128)(2,1)S(1)}, u32[]{:S(2)}, u32[]{:S(2)}) collective-permute-start(bf16[8,32768]{1,0:T(8,128)(2,1)S(1)} %maximum_select_fusion.7), channel_id=1, source_target_pairs={{0,1},{1,0},{2,3},{3,2},{4,5},{5,4},{6,7},{7,6},{8,9},{9,8},{10,11... | collective-permute-start | bytes 1572872 | tf_op jit(solution)/shard_map/ppermute | solution.py:25
  108.1 6.6 %copy-start.15 = (bf16[2048,1024]{1,0:T(8,128)(2,1)}, bf16[2048,1024]{1,0:T(8,128)(2,1)S(1)}, u32[]{:S(2)}) copy-start(bf16[2048,1024]{1,0:T(8,128)(2,1)S(1)} %collective-permute-done.11) | copy-start | bytes 12582916
  115.6 16.4 %all-to-all-start = ((bf16[16,128,64]{1,2,0:T(8,128)(2,1)}), bf16[16,128,64]{1,2,0:T(8,128)(2,1)S(1)}, u32[]{:S(2)}, u32[]{:S(2)}) async-start(bf16[16,128,64]{1,2,0:T(8,128)(2,1)} %bitcast.111), calls=%async_computation | async-start | bytes 524288 | tf_op jit(solution)/shard_map/all_to_all | solution.py:172
  145.6 3.3 %copy-start.6 = (f32[1024,1024]{1,0:T(8,128)S(1)}, f32[1024,1024]{1,0:T(8,128)}, u32[]{:S(2)}) copy-start(f32[1024,1024]{1,0:T(8,128)} %get-tuple-element.11) | copy-start | bytes 12582916
  145.6 3.3 %copy-start.14 = (pred[384]{0:T(512)(128)(4,1)S(1)}, pred[384]{0:T(512)(128)(4,1)}, u32[]{:S(2)}) copy-start(pred[384]{0:T(512)(128)(4,1)} %constant.106) | copy-start | bytes 1156
  147.1 5.6 %copy-start.4 = (f32[256,1024]{1,0:T(8,128)}, f32[256,1024]{1,0:T(8,128)S(1)}, u32[]{:S(2)}) copy-start(f32[256,1024]{1,0:T(8,128)S(1)} %slice.234) | copy-start | bytes 3145732
  148.9 3.8 %copy-start.5 = (f32[256,1024]{1,0:T(8,128)}, f32[256,1024]{1,0:T(8,128)S(1)}, u32[]{:S(2)}) copy-start(f32[256,1024]{1,0:T(8,128)S(1)} %slice.235) | copy-start | bytes 3145732
  148.9 3.1 %copy-start.7 = (f32[1024,1024]{1,0:T(8,128)S(1)}, f32[1024,1024]{1,0:T(8,128)}, u32[]{:S(2)}) copy-start(f32[1024,1024]{1,0:T(8,128)} %get-tuple-element.12) | copy-start | bytes 12582916
  155.7 7.5 %collective-permute-start.14 = (bf16[8,32768]{1,0:T(8,128)(2,1)}, bf16[8,32768]{1,0:T(8,128)(2,1)}, u32[]{:S(2)}, u32[]{:S(2)}) collective-permute-start(bf16[8,32768]{1,0:T(8,128)(2,1)} %convert_element_type.83), channel_id=1, source_target_pairs={{0,1},{1,0},{2,3},{3,2},{4,5},{5,4},{6,7},{7,6},{8,9},{9,8},{10,11... | collective-permute-start | bytes 1572872 | tf_op jit(solution)/shard_map/ppermute | solution.py:25
  160.8 2.4 copy-start.8
  164.6 7.4 %collective-permute-start.15 = (bf16[4,32768]{1,0:T(4,128)(2,1)S(1)}, bf16[4,32768]{1,0:T(4,128)(2,1)S(1)}, u32[]{:S(2)}, u32[]{:S(2)}) collective-permute-start(bf16[4,32768]{1,0:T(4,128)(2,1)S(1)} %select_convert_fusion.1), channel_id=1, source_target_pairs={{0,2},{2,0},{4,6},{6,4},{8,10},{10,8},{12,14},{14,12},{1,3},{3,1},... | collective-permute-start | bytes 786440 | tf_op jit(solution)/shard_map/ppermute | solution.py:28
  168.0 10.0 %copy-start.2 = (f32[1,384,1024]{2,1,0:T(8,128)}, f32[1,384,1024]{2,1,0:T(8,128)S(1)}, u32[]{:S(2)}) copy-start(f32[1,384,1024]{2,1,0:T(8,128)S(1)} %bitcast_dynamic-update-slice_fusion) | copy-start | bytes 4718596
  172.4 5.0 %collective-permute-start.16 = (bf16[2,32768]{1,0:T(2,128)(2,1)S(1)}, bf16[2,32768]{1,0:T(2,128)(2,1)S(1)}, u32[]{:S(2)}, u32[]{:S(2)}) collective-permute-start(bf16[2,32768]{1,0:T(2,128)(2,1)S(1)} %select_convert_fusion.2), channel_id=1, source_target_pairs={{0,4},{2,6},{4,0},{6,2},{8,12},{10,14},{12,8},{14,10},{1,5},{3,7},... | collective-permute-start | bytes 393224 | tf_op jit(solution)/shard_map/ppermute | solution.py:28
  175.7 2.7 %copy-start = (f32[1,384,1024]{2,1,0:T(8,128)}, f32[1,384,1024]{2,1,0:T(8,128)S(1)}, u32[]{:S(2)}) copy-start(f32[1,384,1024]{2,1,0:T(8,128)S(1)} %bitcast_dynamic-update-slice_fusion.1) | copy-start | bytes 4718596
  177.8 4.9 %collective-permute-start.17 = (bf16[1,32768]{1,0:T(2,128)(2,1)S(1)}, bf16[1,32768]{1,0:T(2,128)(2,1)S(1)}, u32[]{:S(2)}, u32[]{:S(2)}) collective-permute-start(bf16[1,32768]{1,0:T(2,128)(2,1)S(1)} %fusion.32), channel_id=1, source_target_pairs={{0,8},{2,10},{4,12},{6,14},{8,0},{10,2},{12,4},{14,6},{1,9},{3,11}... | collective-permute-start | bytes 196616 | tf_op jit(solution)/shard_map/ppermute | solution.py:28
  182.9 19.2 %copy-start.11 = (bf16[128,1024]{1,0:T(8,128)(2,1)S(1)}, bf16[128,1024]{1,0:T(8,128)(2,1)}, u32[]{:S(2)}) copy-start(bf16[128,1024]{1,0:T(8,128)(2,1)} %get-tuple-element.9) | copy-start | bytes 786436
  182.9 4.9 %collective-permute-start.18 = (bf16[1,32768]{1,0:T(2,128)(2,1)S(1)}, bf16[1,32768]{1,0:T(2,128)(2,1)S(1)}, u32[]{:S(2)}, u32[]{:S(2)}) collective-permute-start(bf16[1,32768]{1,0:T(2,128)(2,1)S(1)} %fusion.31), channel_id=1, source_target_pairs={{0,8},{2,10},{4,12},{6,14},{8,0},{10,2},{12,4},{14,6},{1,9},{3,11}... | collective-permute-start | bytes 196616 | tf_op jit(solution)/shard_map/ppermute | solution.py:28
  188.3 20.1 %collective-permute-start.19 = (bf16[2,32768]{1,0:T(2,128)(2,1)S(1)}, bf16[2,32768]{1,0:T(2,128)(2,1)S(1)}, u32[]{:S(2)}, u32[]{:S(2)}) collective-permute-start(bf16[2,32768]{1,0:T(2,128)(2,1)S(1)} %broadcast_select_fusion.12), channel_id=1, source_target_pairs={{0,4},{2,6},{4,0},{6,2},{8,12},{10,14},{12,8},{14,10},{1,5},{3,7},... | collective-permute-start | bytes 393224 | tf_op jit(solution)/shard_map/ppermute | solution.py:28
  195.5 55.9 %collective-permute-start.12 = (bf16[2,256,1024]{2,1,0:T(8,128)(2,1)}, bf16[2,256,1024]{2,1,0:T(8,128)(2,1)}, u32[]{:S(2)}, u32[]{:S(2)}) collective-permute-start(bf16[2,256,1024]{2,1,0:T(8,128)(2,1)} %pad_maximum_fusion.3), channel_id=1, source_target_pairs={{0,1},{1,2},{2,3},{3,4},{4,5},{5,6},{6,7},{7,8},{8,9},{9,10},{10,1... | collective-permute-start | bytes 3145736 | tf_op jit(solution)/shard_map/ppermute | solution.py:83
  198.7 52.7 %collective-permute-start.13 = (bf16[2,256,1024]{2,1,0:T(8,128)(2,1)}, bf16[2,256,1024]{2,1,0:T(8,128)(2,1)}, u32[]{:S(2)}, u32[]{:S(2)}) collective-permute-start(bf16[2,256,1024]{2,1,0:T(8,128)(2,1)} %pad_maximum_fusion.3), channel_id=1, source_target_pairs={{1,0},{2,1},{3,2},{4,3},{5,4},{6,5},{7,6},{8,7},{9,8},{10,9},{11,1... | collective-permute-start | bytes 3145736 | tf_op jit(solution)/shard_map/ppermute | solution.py:84
  202.9 28.8 %all-to-all-start.1 = ((bf16[1,128,16,64]{1,3,0,2:T(8,128)(2,1)}), bf16[1,128,16,64]{1,3,0,2:T(8,128)(2,1)S(1)}, u32[]{:S(2)}, u32[]{:S(2)}) async-start(bf16[1,128,16,64]{1,3,0,2:T(8,128)(2,1)} %bitcast.35), calls=%async_computation.1 | async-start | bytes 524288 | tf_op jit(solution)/shard_map/all_to_all | solution.py:216
  209.0 22.9 %collective-permute-start.20 = (bf16[4,32768]{1,0:T(4,128)(2,1)S(1)}, bf16[4,32768]{1,0:T(4,128)(2,1)S(1)}, u32[]{:S(2)}, u32[]{:S(2)}) collective-permute-start(bf16[4,32768]{1,0:T(4,128)(2,1)S(1)} %maximum_select_fusion.10), channel_id=1, source_target_pairs={{0,2},{2,0},{4,6},{6,4},{8,10},{10,8},{12,14},{14,12},{1,3},{3,1},... | collective-permute-start | bytes 786440 | tf_op jit(solution)/shard_map/ppermute | solution.py:28
  232.4 12.4 %collective-permute-start.21 = (bf16[8,32768]{1,0:T(8,128)(2,1)S(1)}, bf16[8,32768]{1,0:T(8,128)(2,1)S(1)}, u32[]{:S(2)}, u32[]{:S(2)}) collective-permute-start(bf16[8,32768]{1,0:T(8,128)(2,1)S(1)} %maximum_select_fusion.8), channel_id=1, source_target_pairs={{0,1},{1,0},{2,3},{3,2},{4,5},{5,4},{6,7},{7,6},{8,9},{9,8},{10,11... | collective-permute-start | bytes 1572872 | tf_op jit(solution)/shard_map/ppermute | solution.py:25
  246.4 5.0 %copy-start.1 = (f32[1,384,1024]{2,1,0:T(8,128)S(1)}, f32[1,384,1024]{2,1,0:T(8,128)}, u32[]{:S(2)}) copy-start(f32[1,384,1024]{2,1,0:T(8,128)} %copy-done) | copy-start | bytes 4718596
  246.4 5.0 %copy-start.3 = (f32[1,384,1024]{2,1,0:T(8,128)S(1)}, f32[1,384,1024]{2,1,0:T(8,128)}, u32[]{:S(2)}) copy-start(f32[1,384,1024]{2,1,0:T(8,128)} %copy-done.2) | copy-start | bytes 4718596
Sparse Core Ops, SparseCore 0:
  11.9 83.8 all-gather.2
  97.9 55.7 all-gather.4

commit v8 on v4

--- a/solution.py
+++ b/solution.py
@@ -32,27 +32,32 @@
     count = lax.axis_size("chip") * lax.axis_size("core")
     levels = count.bit_length() - 1
     shape = x.shape
-    flat = x.reshape(count, -1)
+    buf = x.reshape(count, -1)
     d = flat_index()
-    parts = flat
+    start, size = 0, count
     for k in range(levels):
-        half = parts.shape[0] // 2
-        lo, hi = parts[:half], parts[half:]
-        upper = ((d >> k) & 1) == 1
-        send = jnp.where(upper, lo, hi)
-        keep = jnp.where(upper, hi, lo)
+        size //= 2
+        upper = (d >> k) & 1
+        mine = start + upper * size
+        theirs = start + (1 - upper) * size
+        send = lax.dynamic_slice_in_dim(buf, theirs, size, axis=0)
         if wire is not None:
             send = send.astype(wire)
-        parts = keep + xor_swap(send, k).astype(keep.dtype)
+        got = xor_swap(send, k).astype(buf.dtype)
+        keep = lax.dynamic_slice_in_dim(buf, mine, size, axis=0)
+        buf = lax.dynamic_update_slice_in_dim(buf, keep + got, mine, axis=0)
+        start = mine
+    if wire is not None:
+        buf = buf.astype(wire)
     for k in reversed(range(levels)):
-        upper = ((d >> k) & 1) == 1
-        if wire is not None and k == levels - 1:
-            parts = parts.astype(wire)
-        other = xor_swap(parts, k)
-        parts = jnp.where(
-            upper, jnp.concatenate([other, parts]), jnp.concatenate([parts, other])
-        )
-    return parts.reshape(shape)
+        upper = (d >> k) & 1
+        seg = lax.dynamic_slice_in_dim(buf, start, size, axis=0)
+        got = xor_swap(seg, k)
+        other = start + (1 - 2 * upper) * size
+        buf = lax.dynamic_update_slice_in_dim(buf, got, other, axis=0)
+        start = jnp.minimum(start, other)
+        size *= 2
+    return buf.reshape(shape)
 
 
 def halo(shard):
@@ -203,17 +208,20 @@
         [grad_ext[:, : blocks_dev * BLK], grad_ext[:, 2 * blocks_dev * BLK :]], axis=1
     ).astype(jnp.bfloat16)
     from_prev, from_next = halo(rims)
-    own = grad_ext[:, blocks_dev * BLK : 2 * blocks_dev * BLK]
-    own = own + from_prev[:, blocks_dev * BLK :].astype(jnp.float32)
-    own = own + from_next[:, : blocks_dev * BLK].astype(jnp.float32)
-    for g in range(slots):
-        start = (global_blocks[g] % blocks_dev) * BLK
-        add = jnp.where(owners[g] == device, global_total[g], jnp.zeros_like(global_total[g]))
-        cur = lax.dynamic_slice_in_dim(own, start, BLK, axis=1)
-        own = lax.dynamic_update_slice_in_dim(own, cur + add, start, axis=1)
-    own = own.astype(jnp.bfloat16)
+    finished = []
+    for side in range(2):
+        own = grad_ext[side, blocks_dev * BLK : 2 * blocks_dev * BLK]
+        own = own + from_prev[side, blocks_dev * BLK :].astype(jnp.float32)
+        own = own + from_next[side, : blocks_dev * BLK].astype(jnp.float32)
+        for g in range(slots):
+            start = (global_blocks[g] % blocks_dev) * BLK
+            total = global_total[g, side].astype(jnp.float32)
+            add = jnp.where(owners[g] == device, total, jnp.zeros_like(total))
+            cur = lax.dynamic_slice_in_dim(own, start, BLK, axis=0)
+            own = lax.dynamic_update_slice_in_dim(own, cur + add, start, axis=0)
+        finished.append(own.astype(jnp.bfloat16))
     grad_query = jnp.concatenate(dq_rows, axis=0)
-    return (layer_out, grad_query, own[0], own[1], grad_weight)
+    return (layer_out, grad_query, finished[0], finished[1], grad_weight)
 
 
 def solution(mesh):

time: 258 us -> 268 us (1.039)
  local copies, waits for them, and re-layouts: 25.4 us -> 55.3 us
  waiting for transfers between devices: 86.5 us -> 72.9 us
  other arithmetic: 26.7 us -> 21.8 us
    dynamic_update_slice x0 -> x10, local copies, waits for them, and re-layouts: none -> 27.6 us  [the longest x8 24.4 us: butterfly_sum(): buf = lax.dynamic_update_slice_in_dim(buf, got, other, axis=0)]
    unnamed x48, local copies, waits for them, and re-layouts: 3.75 us -> 11.6 us
    select_n x13 -> x1, other arithmetic: 8.74 us -> 1.15 us  [local(): masked.append(jnp.where(owners[g] == device, block, jnp.zeros_like(block)))]
    ppermute x12, starting transfers between devices: 42.5 us -> 36.9 us  [xor_swap(): return lax.ppermute(x, 'chip', [(i, i ^ m) for i in range(n)])]
    convert_element_type x2 -> x0, local copies, waits for them, and re-layouts: 5 us -> none  [local(): own = lax.dynamic_update_slice_in_dim(own, cur + add, start, axis=1)]
    select_n x4 -> x0, local copies, waits for them, and re-layouts: 4.23 us -> none  [the longest x2 2.66 us: butterfly_sum(): keep = jnp.where(upper, hi, lo)]
    ppermute x12, waiting for transfers between devices: 46.7 us -> 42.6 us  [xor_swap(): return lax.ppermute(x, 'chip', [(i, i ^ m) for i in range(n)])]
    ppermute x2, waiting for transfers between devices: 4.1 us -> 0.01 us  [halo(): before = lax.ppermute(shard, SEQ, up)]
  transfers between devices with their start and end apart: 24 -> 24, of which waited for: 14 -> 12; matrix products, arithmetic and copies ran while one was open for 24% -> 33% of each run, Pallas kernels for 5% -> 5%
where the time goes in v8:
time: 268 us; the launch traced here: 267 us
  waiting for transfers between devices  72.9 us (27%)
  starting transfers between devices  71.3 us (27%)
  local copies, waits for them, and re-layouts  55.3 us (21%)
  other arithmetic  21.8 us (8%)
  between operations  18.1 us (7%)
  matrix products  15.5 us (6%)
  Pallas kernels  12.2 us (5%)
    ppermute x12, waiting for transfers between devices, xor_swap(): return lax.ppermute(x, 'chip', [(i, i ^ m) for i in range(n)])  42.6 us
    ppermute x12, starting transfers between devices, xor_swap(): return lax.ppermute(x, 'chip', [(i, i ^ m) for i in range(n)])  36.9 us
    dynamic_update_slice x8, local copies, waits for them, and re-layouts, butterfly_sum(): buf = lax.dynamic_update_slice_in_dim(buf, got, other, axis=0)  24.4 us
    all_to_all x1, waiting for transfers between devices, local(): lax.all_to_all(attn_out.reshape(tok_rows, count, w_rows), SEQ, 1, 0, tile...  14.3 us
    pallas_call x1, Pallas kernels, attention(): pl.pallas_call(_attn_kernel, grid=(heads,), in_specs=[pl.BlockSpec((1, ke...  12.2 us
    dynamic_update_slice x11, other arithmetic, local(): lax.dynamic_update_slice_in_dim(grad_ext[side], cur + term, start, axis=0)  12 us
    unnamed x48, local copies, waits for them, and re-layouts  11.6 us
    ppermute x4, starting transfers between devices, xor_swap(): return lax.ppermute(x, 'core', [(i, i ^ 1) for i in range(n)])  10.5 us
  transfers between devices with their start and end apart: 24, of which 12 were waited for; matrix products, arithmetic and copies ran while one was open for 33% of the time, Pallas kernels for 5%

profile of v8, /device:TPU:11, one launch (start us, length us, event | category | flops | bytes accessed | tf_op | source)
XLA Modules:
  0.0 267.0 jit_solution(2485732161214221115)
XLA Ops:
  7.9 1.9 pad_maximum_fusion.5
  9.8 3.7 %collective-permute-start = (bf16[2,128,1024]{2,1,0:T(8,128)(2,1)}, bf16[2,128,1024]{2,1,0:T(8,128)(2,1)S(1)}, u32[]{:S(2)}, u32[]{:S(2)}) collective-permute-start(bf16[2,128,1024]{2,1,0:T(8,128)(2,1)} %pad_maximum_fusion.5), channel_id=1, source_target_pairs={{0,1},{1,2},{2,3},{3,4},{4,5},{5,6},{6,7},{7,8},{8,9},{9,10},{10,1... | collective-permute-start | bytes 1572872 | tf_op jit(solution)/shard_map/ppermute | solution.py:67
  13.5 1.9 collective-permute-start.1
  25.9 10.0 %collective-permute-done.1 = bf16[2,128,1024]{2,1,0:T(8,128)(2,1)S(1)} collective-permute-done((bf16[2,128,1024]{2,1,0:T(8,128)(2,1)}, bf16[2,128,1024]{2,1,0:T(8,128)(2,1)S(1)}, u32[]{:S(2)}, u32[]{:S(2)}) %collective-permute-start.1) | collective-permute-done | bytes 524320 | tf_op jit(solution)/shard_map/ppermute | solution.py:68
  38.7 4.1 %collective-permute-done.4 = bf16[2,32768]{1,0:T(2,128)(2,1)S(1)} collective-permute-done((bf16[2,32768]{1,0:T(2,128)(2,1)S(1)}, bf16[2,32768]{1,0:T(2,128)(2,1)S(1)}, u32[]{:S(2)}, u32[]{:S(2)}) %collective-permute-start.4) | collective-permute-done | bytes 131104 | tf_op jit(solution)/shard_map/ppermute | solution.py:28
  43.2 1.9 collective-permute-start.5
  45.9 2.1 collective-permute-done.5
  48.2 2.2 dynamic_update_slice.93
  50.6 1.8 collective-permute-start.6
  52.5 1.9 fusion.21
  54.3 9.1 %collective-permute-done.6 = bf16[1,32768]{1,0:T(2,128)(2,1)S(1)} collective-permute-done((bf16[1,32768]{1,0:T(2,128)(2,1)S(1)}, bf16[1,32768]{1,0:T(2,128)(2,1)S(1)}, u32[]{:S(2)}, u32[]{:S(2)}) %collective-permute-start.6) | collective-permute-done | bytes 65568 | tf_op jit(solution)/shard_map/ppermute | solution.py:28
  63.4 2.2 dynamic_update_slice.94
  65.8 6.9 %collective-permute-start.7 = (bf16[2,32768]{1,0:T(2,128)(2,1)S(1)}, bf16[2,32768]{1,0:T(2,128)(2,1)S(1)}, u32[]{:S(2)}, u32[]{:S(2)}) collective-permute-start(bf16[2,32768]{1,0:T(2,128)(2,1)S(1)} %constant_dynamic-slice_fusion.3), channel_id=1, source_target_pairs={{0,4},{2,6},{4,0},{6,2},{8,12},{10,14},{12,8},{14,10},{1,5},{3,7},... | collective-permute-start | bytes 393224 | tf_op jit(solution)/shard_map/ppermute | solution.py:28
  74.2 11.2 %collective-permute-done.7 = bf16[2,32768]{1,0:T(2,128)(2,1)S(1)} collective-permute-done((bf16[2,32768]{1,0:T(2,128)(2,1)S(1)}, bf16[2,32768]{1,0:T(2,128)(2,1)S(1)}, u32[]{:S(2)}, u32[]{:S(2)}) %collective-permute-start.7) | collective-permute-done | bytes 131104 | tf_op jit(solution)/shard_map/ppermute | solution.py:28
  85.4 2.9 %dynamic_update_slice.95 = bf16[16,32768]{1,0:T(8,128)(2,1)S(1)} dynamic-update-slice(bf16[16,32768]{1,0:T(8,128)(2,1)S(1)} %dynamic_update_slice.94, bf16[2,32768]{1,0:T(2,128)(2,1)S(1)} %collective-permute-done.7, s32[]{:T(128)S(6)} %select_n.226, s32[]{:T(128)} %constant.78.clone.1) | dynamic-update-slice | bytes 262148 | tf_op jit(solution)/shard_map/dynamic_update_slice | solution.py:57
  88.5 11.9 %collective-permute-start.8 = (bf16[4,32768]{1,0:T(4,128)(2,1)S(1)}, bf16[4,32768]{1,0:T(4,128)(2,1)S(1)}, u32[]{:S(2)}, u32[]{:S(2)}) collective-permute-start(bf16[4,32768]{1,0:T(4,128)(2,1)S(1)} %constant_dynamic-slice_fusion.2), channel_id=1, source_target_pairs={{0,2},{2,0},{4,6},{6,4},{8,10},{10,8},{12,14},{14,12},{1,3},{3,1},... | collective-permute-start | bytes 786440 | tf_op jit(solution)/shard_map/ppermute | solution.py:28
  102.6 2.4 collective-permute-done.8
  105.1 2.7 %dynamic_update_slice.96 = bf16[16,32768]{1,0:T(8,128)(2,1)S(1)} dynamic-update-slice(bf16[16,32768]{1,0:T(8,128)(2,1)S(1)} %dynamic_update_slice.95, bf16[4,32768]{1,0:T(4,128)(2,1)S(1)} %collective-permute-done.8, s32[]{:T(128)S(6)} %select_n.228, s32[]{:T(128)} %constant.78.clone.1) | dynamic-update-slice | bytes 524292 | tf_op jit(solution)/shard_map/dynamic_update_slice | solution.py:57
  108.0 4.2 %collective-permute-start.9 = (bf16[8,32768]{1,0:T(8,128)(2,1)S(1)}, bf16[8,32768]{1,0:T(8,128)(2,1)S(1)}, u32[]{:S(2)}, u32[]{:S(2)}) collective-permute-start(bf16[8,32768]{1,0:T(8,128)(2,1)S(1)} %constant_dynamic-slice_fusion.1), channel_id=1, source_target_pairs={{0,1},{1,0},{2,3},{3,2},{4,5},{5,4},{6,7},{7,6},{8,9},{9,8},{10,11... | collective-permute-start | bytes 1572872 | tf_op jit(solution)/shard_map/ppermute | solution.py:25
  112.1 6.0 %fusion = bf16[8,16,8,128]{3,2,1,0:T(8,128)(2,1)S(1)} fusion(bf16[2048,2048]{1,0:T(8,128)(2,1)} %all-gather.3.cloned.1.call-done, bf16[64,2048]{1,0:T(8,128)(2,1)S(1)} %copy-done.13), kind=kOutput, calls=%fused_computation.6 | convolution fusion | flops 537001984 | bytes 8912896 | tf_op jit(solution)/shard_map/dot_general | solution.py:153
  119.0 7.4 %all-to-all-start = ((bf16[16,128,64]{1,2,0:T(8,128)(2,1)}), bf16[16,128,64]{1,2,0:T(8,128)(2,1)S(1)}, u32[]{:S(2)}, u32[]{:S(2)}) async-start(bf16[16,128,64]{1,2,0:T(8,128)(2,1)} %bitcast.135), calls=%async_computation | async-start | bytes 524288 | tf_op jit(solution)/shard_map/all_to_all | solution.py:156
  127.1 4.3 %dynamic_update_slice.97 = bf16[16,32768]{1,0:T(8,128)(2,1)S(1)} dynamic-update-slice(bf16[16,32768]{1,0:T(8,128)(2,1)S(1)} %dynamic_update_slice.96, bf16[8,32768]{1,0:T(8,128)(2,1)S(1)} %collective-permute-done.9, s32[]{:T(128)S(6)} %select_n.230, s32[]{:T(128)} %constant.78.clone.1) | dynamic-update-slice | bytes 1048580 | tf_op jit(solution)/shard_map/dynamic_update_slice | solution.py:57
  133.7 5.2 %all-to-all-done = bf16[16,128,64]{1,2,0:T(8,128)(2,1)S(1)} async-done(((bf16[16,128,64]{1,2,0:T(8,128)(2,1)}), bf16[16,128,64]{1,2,0:T(8,128)(2,1)S(1)}, u32[]{:S(2)}, u32[]{:S(2)}) %all-to-all-start) | async-done | bytes 262176 | tf_op jit(solution)/shard_map/all_to_all | solution.py:156
  140.4 12.2 %shard_map.119 = (bf16[128,1024]{1,0:T(8,128)(2,1)}, bf16[128,1024]{1,0:T(8,128)(2,1)}, f32[1024,1024]{1,0:T(8,128)}, f32[1024,1024]{1,0:T(8,128)}) custom-call(f32[1,1024]{1,0:T(1,128)} %bitcast.149, bf16[128,1024]{1,0:T(8,128)(2,1)} %q_ref.1, bf16[1024,1024]{1,0:T(8,128)(2,1)} %get-tuple-element.20.k_ref, bf16[1024,1024]{1,0:T(8,128)(2,1)} %get-tuple-element.19.v_ref, ...), custom_call_target="tpu_custom_call" | custom-call | tf_op jit(solution)/shard_map/pallas_call | solution.py:100
  155.6 3.0 %slice_select_fusion = (f32[384,1024]{1,0:T(8,128)}, f32[384,1024]{1,0:T(8,128)S(1)}) fusion(f32[1024,1024]{1,0:T(8,128)} %get-tuple-element.12, pred[384]{0:T(512)(128)(4,1)S(1)} %copy-done.15, f32[1024,1024]{1,0:T(8,128)S(1)} %copy-done.7), kind=kLoop, calls=%fused_computation.4 | loop fusion | flops 786432 | bytes 6291840 | tf_op jit(solution)/shard_map/dynamic_update_slice | solution.py:184
  160.2 1.6 pad_maximum_fusion
  161.8 1.7 reshape.169
  163.7 2.1 fusion.8
  165.8 2.1 fusion.7
  172.3 3.3 %collective-permute-done.13 = bf16[4,32768]{1,0:T(4,128)(2,1)S(1)} collective-permute-done((bf16[4,32768]{1,0:T(4,128)(2,1)S(1)}, bf16[4,32768]{1,0:T(4,128)(2,1)S(1)}, u32[]{:S(2)}, u32[]{:S(2)}) %collective-permute-start.13) | collective-permute-done | bytes 262176 | tf_op jit(solution)/shard_map/ppermute | solution.py:28
  177.3 2.6 collective-permute-done.14
  180.3 3.8 %collective-permute-start.15 = (bf16[1,32768]{1,0:T(2,128)(2,1)S(1)}, bf16[1,32768]{1,0:T(2,128)(2,1)S(1)}, u32[]{:S(2)}, u32[]{:S(2)}) collective-permute-start(bf16[1,32768]{1,0:T(2,128)(2,1)S(1)} %dynamic-slice_convert_fusion.3), channel_id=1, source_target_pairs={{0,8},{2,10},{4,12},{6,14},{8,0},{10,2},{12,4},{14,6},{1,9},{3,11}... | collective-permute-start | bytes 196616 | tf_op jit(solution)/shard_map/ppermute | solution.py:28
  185.2 2.6 collective-permute-done.15
  189.2 4.6 %collective-permute-start.16 = (bf16[1,32768]{1,0:T(2,128)(2,1)S(1)}, bf16[1,32768]{1,0:T(2,128)(2,1)S(1)}, u32[]{:S(2)}, u32[]{:S(2)}) collective-permute-start(bf16[1,32768]{1,0:T(2,128)(2,1)S(1)} %constant_dynamic-slice_fusion), channel_id=1, source_target_pairs={{0,8},{2,10},{4,12},{6,14},{8,0},{10,2},{12,4},{14,6},{1,9},{3,11}... | collective-permute-start | bytes 196616 | tf_op jit(solution)/shard_map/ppermute | solution.py:28
  194.0 5.2 %collective-permute-done.16 = bf16[1,32768]{1,0:T(2,128)(2,1)S(1)} collective-permute-done((bf16[1,32768]{1,0:T(2,128)(2,1)S(1)}, bf16[1,32768]{1,0:T(2,128)(2,1)S(1)}, u32[]{:S(2)}, u32[]{:S(2)}) %collective-permute-start.16) | collective-permute-done | bytes 65568 | tf_op jit(solution)/shard_map/ppermute | solution.py:28
  199.2 2.2 dynamic_update_slice.114
  202.2 2.5 collective-permute-start.17
  204.7 1.9 collective-permute-start.10
  206.7 2.8 %collective-permute-start.11 = (bf16[2,256,1024]{2,1,0:T(8,128)(2,1)S(1)}, bf16[2,256,1024]{2,1,0:T(8,128)(2,1)}, u32[]{:S(2)}, u32[]{:S(2)}) collective-permute-start(bf16[2,256,1024]{2,1,0:T(8,128)(2,1)S(1)} %pad_maximum_fusion.4), channel_id=1, source_target_pairs={{1,0},{2,1},{3,2},{4,3},{5,4},{6,5},{7,6},{8,7},{9,8},{10,9},{11,1... | collective-permute-start | bytes 3145736 | tf_op jit(solution)/shard_map/ppermute | solution.py:68
  210.3 6.1 %all-to-all-start.1 = ((bf16[1,128,16,64]{1,3,0,2:T(8,128)(2,1)}), bf16[1,128,16,64]{1,3,0,2:T(8,128)(2,1)S(1)}, u32[]{:S(2)}, u32[]{:S(2)}) async-start(bf16[1,128,16,64]{1,3,0,2:T(8,128)(2,1)} %bitcast.43), calls=%async_computation.1 | async-start | bytes 524288 | tf_op jit(solution)/shard_map/all_to_all | solution.py:200
  216.4 3.0 %dynamic_update_slice.115 = bf16[16,32768]{1,0:T(8,128)(2,1)S(1)} dynamic-update-slice(bf16[16,32768]{1,0:T(8,128)(2,1)S(1)} %dynamic_update_slice.114, bf16[2,32768]{1,0:T(2,128)(2,1)S(1)} %collective-permute-done.17, s32[]{:T(128)S(6)} %select_n.226, s32[]{:T(128)} %constant.78.clone.1) | dynamic-update-slice | bytes 262148 | tf_op jit(solution)/shard_map/dynamic_update_slice | solution.py:57
  220.9 3.7 %convolution_convert_fusion = bf16[128,2048]{1,0:T(8,128)(2,1)} fusion(bf16[128,1024]{1,0:T(8,128)(2,1)S(1)} %copy-done.14, bf16[1024,2048]{1,0:T(8,128)(2,1)} %all-gather.5.cloned.1.call-done), kind=kOutput, calls=%fused_computation | convolution fusion | flops 537133056 | bytes 4980736 | tf_op jit(solution)/shard_map/dot_general | solution.py:197
  224.6 14.3 %all-to-all-done.1 = bf16[1,128,16,64]{1,3,0,2:T(8,128)(2,1)S(1)} async-done(((bf16[1,128,16,64]{1,3,0,2:T(8,128)(2,1)}), bf16[1,128,16,64]{1,3,0,2:T(8,128)(2,1)S(1)}, u32[]{:S(2)}, u32[]{:S(2)}) %all-to-all-start.1) | async-done | bytes 262176 | tf_op jit(solution)/shard_map/all_to_all | solution.py:200
  239.1 2.8 %dynamic_update_slice.116 = bf16[16,32768]{1,0:T(8,128)(2,1)S(1)} dynamic-update-slice(bf16[16,32768]{1,0:T(8,128)(2,1)S(1)} %dynamic_update_slice.115, bf16[4,32768]{1,0:T(4,128)(2,1)S(1)} %collective-permute-done.18, s32[]{:T(128)S(6)} %select_n.228, s32[]{:T(128)} %constant.78.clone.1) | dynamic-update-slice | bytes 524292 | tf_op jit(solution)/shard_map/dynamic_update_slice | solution.py:57
  242.1 4.7 %collective-permute-start.19 = (bf16[8,32768]{1,0:T(8,128)(2,1)S(1)}, bf16[8,32768]{1,0:T(8,128)(2,1)S(1)}, u32[]{:S(2)}, u32[]{:S(2)}) collective-permute-start(bf16[8,32768]{1,0:T(8,128)(2,1)S(1)} %constant_dynamic-slice_fusion.10), channel_id=1, source_target_pairs={{0,1},{1,0},{2,3},{3,2},{4,5},{5,4},{6,7},{7,6},{8,9},{9,8},{10,11... | collective-permute-start | bytes 1572872 | tf_op jit(solution)/shard_map/ppermute | solution.py:25
  246.7 5.7 %fusion.16 = f32[64,2048]{1,0:T(8,128)} fusion(bf16[2048,2048]{1,0:T(8,128)(2,1)} %all-gather.3.cloned.1.call-done, bf16[8,8,16,128]{3,2,1,0:T(8,128)(2,1)S(1)} %bitcast.146), kind=kOutput, calls=%fused_computation.47 | convolution fusion | flops 536870912 | bytes 9175040 | tf_op jit(solution)/shard_map/dot_general | solution.py:203
  252.5 4.4 %dynamic_update_slice.117 = bf16[16,32768]{1,0:T(8,128)(2,1)S(1)} dynamic-update-slice(bf16[16,32768]{1,0:T(8,128)(2,1)S(1)} %dynamic_update_slice.116, bf16[8,32768]{1,0:T(8,128)(2,1)S(1)} %collective-permute-done.19, s32[]{:T(128)S(6)} %select_n.230, s32[]{:T(128)} %constant.78.clone.1) | dynamic-update-slice | bytes 1048580 | tf_op jit(solution)/shard_map/dynamic_update_slice | solution.py:57
  257.4 2.8 %fusion.6 = (bf16[128,1024]{1,0:T(8,128)(2,1)}, bf16[128,1024]{1,0:T(8,128)(2,1)}) fusion(f32[1,384,1024]{2,1,0:T(8,128)} %copy-done.3, bf16[2,2,128,1024]{3,2,1,0:T(8,128)(2,1)S(1)} %reshape.170, bf16[2,256,1024]{2,1,0:T(8,128)(2,1)} %collective-permute-done.11, bf16[2,256,1024]{2,1,0:T(8,128)(2,1)} %collective-permute-done.10, pred[]{:T(512)S(6)} %eq.18, ...), kind=kLoop, calls=%fused_computation.19 | loop fusion | flops 2883584 | bytes 3670018 | tf_op jit(solution)/shard_map/convert_element_type | solution.py:222
  (128 shorter events, 39.4 us)
Async XLA Ops:
  7.2 105.0 %all-gather.3.cloned.1.call-start = ((), (), s32[]{:S(2)}) async-start(), calls=%async_computation.2 | async-start | bytes 8912896 | tf_op jit(solution)/shard_map/all_gather | solution.py:122
  7.9 213.0 %all-gather.5.cloned.1.call-start = ((), (), s32[]{:S(2)}) async-start(), calls=%async_computation.3 | async-start | bytes 4456448 | tf_op jit(solution)/shard_map/all_gather | solution.py:123
  9.8 16.0 %collective-permute-start = (bf16[2,128,1024]{2,1,0:T(8,128)(2,1)}, bf16[2,128,1024]{2,1,0:T(8,128)(2,1)S(1)}, u32[]{:S(2)}, u32[]{:S(2)}) collective-permute-start(bf16[2,128,1024]{2,1,0:T(8,128)(2,1)} %pad_maximum_fusion.5), channel_id=1, source_target_pairs={{0,1},{1,2},{2,3},{3,4},{4,5},{5,6},{6,7},{7,8},{8,9},{9,10},{10,1... | collective-permute-start | bytes 1572872 | tf_op jit(solution)/shard_map/ppermute | solution.py:67
  13.5 22.3 %collective-permute-start.1 = (bf16[2,128,1024]{2,1,0:T(8,128)(2,1)}, bf16[2,128,1024]{2,1,0:T(8,128)(2,1)S(1)}, u32[]{:S(2)}, u32[]{:S(2)}) collective-permute-start(bf16[2,128,1024]{2,1,0:T(8,128)(2,1)} %pad_maximum_fusion.5), channel_id=1, source_target_pairs={{1,0},{2,1},{3,2},{4,3},{5,4},{6,5},{7,6},{8,7},{9,8},{10,9},{11,1... | collective-permute-start | bytes 1572872 | tf_op jit(solution)/shard_map/ppermute | solution.py:68
  19.3 3.0 %copy-start.16 = (s32[1,3]{1,0:T(1,128)S(1)}, s32[1,3]{1,0:T(1,128)}, u32[]{:S(2)}) copy-start(s32[1,3]{1,0:T(1,128)} %param.14) | copy-start | bytes 40
  19.3 5.7 %copy-start.17 = (s32[3]{0:T(128)S(1)}, s32[3]{0:T(128)}, u32[]{:S(2)}) copy-start(s32[3]{0:T(128)} %constant.90.clone) | copy-start | bytes 40
  19.9 16.7 %copy-start.8 = (bf16[128,1024]{1,0:T(8,128)(2,1)S(1)}, bf16[128,1024]{1,0:T(8,128)(2,1)}, u32[]{:S(2)}) copy-start(bf16[128,1024]{1,0:T(8,128)(2,1)} %param.10) | copy-start | bytes 786436
  19.9 16.7 %copy-start.9 = (bf16[128,1024]{1,0:T(8,128)(2,1)S(1)}, bf16[128,1024]{1,0:T(8,128)(2,1)}, u32[]{:S(2)}) copy-start(bf16[128,1024]{1,0:T(8,128)(2,1)} %param.9) | copy-start | bytes 786436
  20.8 4.4 %collective-permute-start.2 = (bf16[8,32768]{1,0:T(8,128)(2,1)}, bf16[8,32768]{1,0:T(8,128)(2,1)S(1)}, u32[]{:S(2)}, u32[]{:S(2)}) collective-permute-start(bf16[8,32768]{1,0:T(8,128)(2,1)} %constant_dynamic-slice_fusion.8), channel_id=1, source_target_pairs={{0,1},{1,0},{2,3},{3,2},{4,5},{5,4},{6,7},{7,6},{8,9},{9,8},{10,11... | collective-permute-start | bytes 1572872 | tf_op jit(solution)/shard_map/ppermute | solution.py:25
  25.5 11.4 %collective-permute-start.3 = (bf16[4,32768]{1,0:T(4,128)(2,1)S(1)}, bf16[4,32768]{1,0:T(4,128)(2,1)S(1)}, u32[]{:S(2)}, u32[]{:S(2)}) collective-permute-start(bf16[4,32768]{1,0:T(4,128)(2,1)S(1)} %constant_dynamic-slice_fusion.7), channel_id=1, source_target_pairs={{0,2},{2,0},{4,6},{6,4},{8,10},{10,8},{12,14},{14,12},{1,3},{3,1},... | collective-permute-start | bytes 786440 | tf_op jit(solution)/shard_map/ppermute | solution.py:28
  25.9 10.0 %copy-start.11 = (bf16[2,128,1024]{2,1,0:T(8,128)(2,1)}, bf16[2,128,1024]{2,1,0:T(8,128)(2,1)S(1)}, u32[]{:S(2)}) copy-start(bf16[2,128,1024]{2,1,0:T(8,128)(2,1)S(1)} %collective-permute-done) | copy-start | bytes 1572868
  35.8 0.8 copy-start.10
  36.8 1.0 copy-start.12
  37.4 5.4 %collective-permute-start.4 = (bf16[2,32768]{1,0:T(2,128)(2,1)S(1)}, bf16[2,32768]{1,0:T(2,128)(2,1)S(1)}, u32[]{:S(2)}, u32[]{:S(2)}) collective-permute-start(bf16[2,32768]{1,0:T(2,128)(2,1)S(1)} %constant_dynamic-slice_fusion.6), channel_id=1, source_target_pairs={{0,4},{2,6},{4,0},{6,2},{8,12},{10,14},{12,8},{14,10},{1,5},{3,7},... | collective-permute-start | bytes 393224 | tf_op jit(solution)/shard_map/ppermute | solution.py:28
  43.2 4.8 %collective-permute-start.5 = (bf16[1,32768]{1,0:T(2,128)(2,1)S(1)}, bf16[1,32768]{1,0:T(2,128)(2,1)S(1)}, u32[]{:S(2)}, u32[]{:S(2)}) collective-permute-start(bf16[1,32768]{1,0:T(2,128)(2,1)S(1)} %constant_dynamic-slice_fusion.5), channel_id=1, source_target_pairs={{0,8},{2,10},{4,12},{6,14},{8,0},{10,2},{12,4},{14,6},{1,9},{3,11}... | collective-permute-start | bytes 196616 | tf_op jit(solution)/shard_map/ppermute | solution.py:28
  50.6 12.7 %collective-permute-start.6 = (bf16[1,32768]{1,0:T(2,128)(2,1)S(1)}, bf16[1,32768]{1,0:T(2,128)(2,1)S(1)}, u32[]{:S(2)}, u32[]{:S(2)}) collective-permute-start(bf16[1,32768]{1,0:T(2,128)(2,1)S(1)} %constant_dynamic-slice_fusion.4), channel_id=1, source_target_pairs={{0,8},{2,10},{4,12},{6,14},{8,0},{10,2},{12,4},{14,6},{1,9},{3,11}... | collective-permute-start | bytes 196616 | tf_op jit(solution)/shard_map/ppermute | solution.py:28
  65.8 19.6 %collective-permute-start.7 = (bf16[2,32768]{1,0:T(2,128)(2,1)S(1)}, bf16[2,32768]{1,0:T(2,128)(2,1)S(1)}, u32[]{:S(2)}, u32[]{:S(2)}) collective-permute-start(bf16[2,32768]{1,0:T(2,128)(2,1)S(1)} %constant_dynamic-slice_fusion.3), channel_id=1, source_target_pairs={{0,4},{2,6},{4,0},{6,2},{8,12},{10,14},{12,8},{14,10},{1,5},{3,7},... | collective-permute-start | bytes 393224 | tf_op jit(solution)/shard_map/ppermute | solution.py:28
  74.2 38.0 %copy-start.13 = (bf16[64,2048]{1,0:T(8,128)(2,1)S(1)}, bf16[64,2048]{1,0:T(8,128)(2,1)}, u32[]{:S(2)}) copy-start(bf16[64,2048]{1,0:T(8,128)(2,1)} %param.11) | copy-start | bytes 786436
  88.5 16.6 %collective-permute-start.8 = (bf16[4,32768]{1,0:T(4,128)(2,1)S(1)}, bf16[4,32768]{1,0:T(4,128)(2,1)S(1)}, u32[]{:S(2)}, u32[]{:S(2)}) collective-permute-start(bf16[4,32768]{1,0:T(4,128)(2,1)S(1)} %constant_dynamic-slice_fusion.2), channel_id=1, source_target_pairs={{0,2},{2,0},{4,6},{6,4},{8,10},{10,8},{12,14},{14,12},{1,3},{3,1},... | collective-permute-start | bytes 786440 | tf_op jit(solution)/shard_map/ppermute | solution.py:28
  108.0 19.1 %collective-permute-start.9 = (bf16[8,32768]{1,0:T(8,128)(2,1)S(1)}, bf16[8,32768]{1,0:T(8,128)(2,1)S(1)}, u32[]{:S(2)}, u32[]{:S(2)}) collective-permute-start(bf16[8,32768]{1,0:T(8,128)(2,1)S(1)} %constant_dynamic-slice_fusion.1), channel_id=1, source_target_pairs={{0,1},{1,0},{2,3},{3,2},{4,5},{5,4},{6,7},{7,6},{8,9},{9,8},{10,11... | collective-permute-start | bytes 1572872 | tf_op jit(solution)/shard_map/ppermute | solution.py:25
  119.0 20.0 %all-to-all-start = ((bf16[16,128,64]{1,2,0:T(8,128)(2,1)}), bf16[16,128,64]{1,2,0:T(8,128)(2,1)S(1)}, u32[]{:S(2)}, u32[]{:S(2)}) async-start(bf16[16,128,64]{1,2,0:T(8,128)(2,1)} %bitcast.135), calls=%async_computation | async-start | bytes 524288 | tf_op jit(solution)/shard_map/all_to_all | solution.py:156
  152.6 2.9 %copy-start.7 = (f32[1024,1024]{1,0:T(8,128)S(1)}, f32[1024,1024]{1,0:T(8,128)}, u32[]{:S(2)}) copy-start(f32[1024,1024]{1,0:T(8,128)} %get-tuple-element.11) | copy-start | bytes 12582916
  152.6 2.9 %copy-start.15 = (pred[384]{0:T(512)(128)(4,1)S(1)}, pred[384]{0:T(512)(128)(4,1)}, u32[]{:S(2)}) copy-start(pred[384]{0:T(512)(128)(4,1)} %constant.112) | copy-start | bytes 1156
  159.0 1.2 copy-start.1
  163.6 4.2 %collective-permute-start.12 = (bf16[8,32768]{1,0:T(8,128)(2,1)S(1)}, bf16[8,32768]{1,0:T(8,128)(2,1)S(1)}, u32[]{:S(2)}, u32[]{:S(2)}) collective-permute-start(bf16[8,32768]{1,0:T(8,128)(2,1)S(1)} %dynamic-slice_convert_fusion), channel_id=1, source_target_pairs={{0,1},{1,0},{2,3},{3,2},{4,5},{5,4},{6,7},{7,6},{8,9},{9,8},{10,11... | collective-permute-start | bytes 1572872 | tf_op jit(solution)/shard_map/ppermute | solution.py:25
  167.8 1.9 copy-start
  167.8 3.0 %copy-start.2 = (f32[384,1024]{1,0:T(8,128)S(1)}, f32[384,1024]{1,0:T(8,128)}, u32[]{:S(2)}) copy-start(f32[384,1024]{1,0:T(8,128)} %copy-done.1) | copy-start | bytes 4718596
  168.2 7.5 %collective-permute-start.13 = (bf16[4,32768]{1,0:T(4,128)(2,1)S(1)}, bf16[4,32768]{1,0:T(4,128)(2,1)S(1)}, u32[]{:S(2)}, u32[]{:S(2)}) collective-permute-start(bf16[4,32768]{1,0:T(4,128)(2,1)S(1)} %dynamic-slice_convert_fusion.1), channel_id=1, source_target_pairs={{0,2},{2,0},{4,6},{6,4},{8,10},{10,8},{12,14},{14,12},{1,3},{3,1},... | collective-permute-start | bytes 786440 | tf_op jit(solution)/shard_map/ppermute | solution.py:28
  176.0 3.9 %collective-permute-start.14 = (bf16[2,32768]{1,0:T(2,128)(2,1)S(1)}, bf16[2,32768]{1,0:T(2,128)(2,1)S(1)}, u32[]{:S(2)}, u32[]{:S(2)}) collective-permute-start(bf16[2,32768]{1,0:T(2,128)(2,1)S(1)} %dynamic-slice_convert_fusion.2), channel_id=1, source_target_pairs={{0,4},{2,6},{4,0},{6,2},{8,12},{10,14},{12,8},{14,10},{1,5},{3,7},... | collective-permute-start | bytes 393224 | tf_op jit(solution)/shard_map/ppermute | solution.py:28
  177.3 10.5 %copy-start.5 = (f32[1,384,1024]{2,1,0:T(8,128)}, f32[1,384,1024]{2,1,0:T(8,128)S(1)}, u32[]{:S(2)}) copy-start(f32[1,384,1024]{2,1,0:T(8,128)S(1)} %bitcast_dynamic-update-slice_fusion.1) | copy-start | bytes 4718596
  180.3 7.5 %collective-permute-start.15 = (bf16[1,32768]{1,0:T(2,128)(2,1)S(1)}, bf16[1,32768]{1,0:T(2,128)(2,1)S(1)}, u32[]{:S(2)}, u32[]{:S(2)}) collective-permute-start(bf16[1,32768]{1,0:T(2,128)(2,1)S(1)} %dynamic-slice_convert_fusion.3), channel_id=1, source_target_pairs={{0,8},{2,10},{4,12},{6,14},{8,0},{10,2},{12,4},{14,6},{1,9},{3,11}... | collective-permute-start | bytes 196616 | tf_op jit(solution)/shard_map/ppermute | solution.py:28
  185.2 2.6 copy-start.3
  188.9 4.9 %copy-start.4 = (f32[1,384,1024]{2,1,0:T(8,128)S(1)}, f32[1,384,1024]{2,1,0:T(8,128)}, u32[]{:S(2)}) copy-start(f32[1,384,1024]{2,1,0:T(8,128)} %copy-done.3) | copy-start | bytes 4718596
  189.0 4.9 %copy-start.6 = (f32[1,384,1024]{2,1,0:T(8,128)S(1)}, f32[1,384,1024]{2,1,0:T(8,128)}, u32[]{:S(2)}) copy-start(f32[1,384,1024]{2,1,0:T(8,128)} %copy-done.5) | copy-start | bytes 4718596
  189.2 9.9 %collective-permute-start.16 = (bf16[1,32768]{1,0:T(2,128)(2,1)S(1)}, bf16[1,32768]{1,0:T(2,128)(2,1)S(1)}, u32[]{:S(2)}, u32[]{:S(2)}) collective-permute-start(bf16[1,32768]{1,0:T(2,128)(2,1)S(1)} %constant_dynamic-slice_fusion), channel_id=1, source_target_pairs={{0,8},{2,10},{4,12},{6,14},{8,0},{10,2},{12,4},{14,6},{1,9},{3,11}... | collective-permute-start | bytes 196616 | tf_op jit(solution)/shard_map/ppermute | solution.py:28
  194.0 15.5 %copy-start.14 = (bf16[128,1024]{1,0:T(8,128)(2,1)S(1)}, bf16[128,1024]{1,0:T(8,128)(2,1)}, u32[]{:S(2)}) copy-start(bf16[128,1024]{1,0:T(8,128)(2,1)} %get-tuple-element.9) | copy-start | bytes 786436
  202.2 14.2 %collective-permute-start.17 = (bf16[2,32768]{1,0:T(2,128)(2,1)}, bf16[2,32768]{1,0:T(2,128)(2,1)S(1)}, u32[]{:S(2)}, u32[]{:S(2)}) collective-permute-start(bf16[2,32768]{1,0:T(2,128)(2,1)} %constant_dynamic-slice_fusion.9), channel_id=1, source_target_pairs={{0,4},{2,6},{4,0},{6,2},{8,12},{10,14},{12,8},{14,10},{1,5},{3,7},... | collective-permute-start | bytes 393224 | tf_op jit(solution)/shard_map/ppermute | solution.py:28
  204.7 52.6 %collective-permute-start.10 = (bf16[2,256,1024]{2,1,0:T(8,128)(2,1)S(1)}, bf16[2,256,1024]{2,1,0:T(8,128)(2,1)}, u32[]{:S(2)}, u32[]{:S(2)}) collective-permute-start(bf16[2,256,1024]{2,1,0:T(8,128)(2,1)S(1)} %pad_maximum_fusion.4), channel_id=1, source_target_pairs={{0,1},{1,2},{2,3},{3,4},{4,5},{5,6},{6,7},{7,8},{8,9},{9,10},{10,1... | collective-permute-start | bytes 3145736 | tf_op jit(solution)/shard_map/ppermute | solution.py:67
  206.7 50.7 %collective-permute-start.11 = (bf16[2,256,1024]{2,1,0:T(8,128)(2,1)S(1)}, bf16[2,256,1024]{2,1,0:T(8,128)(2,1)}, u32[]{:S(2)}, u32[]{:S(2)}) collective-permute-start(bf16[2,256,1024]{2,1,0:T(8,128)(2,1)S(1)} %pad_maximum_fusion.4), channel_id=1, source_target_pairs={{1,0},{2,1},{3,2},{4,3},{5,4},{6,5},{7,6},{8,7},{9,8},{10,9},{11,1... | collective-permute-start | bytes 3145736 | tf_op jit(solution)/shard_map/ppermute | solution.py:68
  210.3 28.6 %all-to-all-start.1 = ((bf16[1,128,16,64]{1,3,0,2:T(8,128)(2,1)}), bf16[1,128,16,64]{1,3,0,2:T(8,128)(2,1)S(1)}, u32[]{:S(2)}, u32[]{:S(2)}) async-start(bf16[1,128,16,64]{1,3,0,2:T(8,128)(2,1)} %bitcast.43), calls=%async_computation.1 | async-start | bytes 524288 | tf_op jit(solution)/shard_map/all_to_all | solution.py:200
  219.6 19.5 %collective-permute-start.18 = (bf16[4,32768]{1,0:T(4,128)(2,1)S(1)}, bf16[4,32768]{1,0:T(4,128)(2,1)S(1)}, u32[]{:S(2)}, u32[]{:S(2)}) collective-permute-start(bf16[4,32768]{1,0:T(4,128)(2,1)S(1)} %constant_dynamic-slice_fusion.11), channel_id=1, source_target_pairs={{0,2},{2,0},{4,6},{6,4},{8,10},{10,8},{12,14},{14,12},{1,3},{3,1},... | collective-permute-start | bytes 786440 | tf_op jit(solution)/shard_map/ppermute | solution.py:28
  242.1 10.4 %collective-permute-start.19 = (bf16[8,32768]{1,0:T(8,128)(2,1)S(1)}, bf16[8,32768]{1,0:T(8,128)(2,1)S(1)}, u32[]{:S(2)}, u32[]{:S(2)}) collective-permute-start(bf16[8,32768]{1,0:T(8,128)(2,1)S(1)} %constant_dynamic-slice_fusion.10), channel_id=1, source_target_pairs={{0,1},{1,0},{2,3},{3,2},{4,5},{5,4},{6,7},{7,6},{8,9},{9,8},{10,11... | collective-permute-start | bytes 1572872 | tf_op jit(solution)/shard_map/ppermute | solution.py:25
Sparse Core Ops, SparseCore 0:
  10.2 85.7 all-gather.2
  98.2 56.2 all-gather.4

commit v9 on v4

--- a/solution.py
+++ b/solution.py
@@ -114,7 +114,6 @@
     total_blocks = blocks_dev * count
     device = flat_index()
 
-    grad_out_all = lax.all_gather(grad_out, SEQ, axis=0, tiled=True)
     weight_all = lax.all_gather(out_weight, SEQ, axis=0, tiled=True)
 
     paired = jnp.stack([keys, values])
@@ -144,14 +143,9 @@
         axis=1,
     )
 
-    w_rows = out_weight.shape[0]
-    upstream_cols = lax.dot_general(
-        grad_out_all, out_weight, (((1,), (1,)), ((), ())), preferred_element_type=jnp.float32
+    upstream = lax.dot_general(
+        grad_out, weight_all, (((1,), (1,)), ((), ())), preferred_element_type=jnp.float32
     ).astype(jnp.bfloat16)
-    upstream = lax.all_to_all(
-        upstream_cols.reshape(count, tok_rows, w_rows), SEQ, 0, 0, tiled=False
-    )
-    upstream = jnp.swapaxes(upstream, 0, 1).reshape(tok_rows, feature_count)
 
     attn_rows, dq_rows = [], []
     grad_ext = [jnp.zeros((3 * blocks_dev * BLK, feature_count), jnp.float32) for _ in range(2)]
@@ -192,12 +186,12 @@
     layer_out = jnp.dot(attn_out, weight_all, preferred_element_type=jnp.float32).astype(
         jnp.bfloat16
     )
-    attn_cols = lax.all_to_all(
-        attn_out.reshape(tok_rows, count, w_rows), SEQ, 1, 0, tiled=False
-    ).reshape(count * tok_rows, w_rows)
-    grad_weight = lax.dot_general(
-        attn_cols, grad_out_all, (((0,), (0,)), ((), ())), preferred_element_type=jnp.float32
-    )
+    partial = lax.dot_general(
+        attn_out, grad_out, (((0,), (0,)), ((), ())), preferred_element_type=jnp.float32
+    )
+    grad_weight = lax.psum_scatter(
+        partial.astype(jnp.bfloat16), SEQ, scatter_dimension=0, tiled=True
+    ).astype(jnp.float32)
 
     rims = jnp.concatenate(
         [grad_ext[:, : blocks_dev * BLK], grad_ext[:, 2 * blocks_dev * BLK :]], axis=1

time: 258 us -> 276 us (1.070); the launches traced: 256 us -> 272 us
  waiting for transfers between devices: 86.5 us -> 130 us
  starting transfers between devices: 72 us -> 46.5 us
  other arithmetic: 26.7 us -> 32.2 us
  matrix products: 15.5 us -> 11.4 us
  local copies, waits for them, and re-layouts: 25.4 us -> 21.5 us
    reduce_scatter x0 -> x1, waiting for transfers between devices: none -> 58.2 us  [local(): lax.psum_scatter(partial.astype(jnp.bfloat16), SEQ, scatter_dimension=0,...]
    all_to_all x2 -> x0, waiting for transfers between devices: 25.3 us -> none  [the longest x1 17.8 us: local(): lax.all_to_all(attn_out.reshape(tok_rows, count, w_rows), SEQ, 1, 0, tile...]
    ppermute x12, starting transfers between devices: 42.5 us -> 26.4 us  [xor_swap(): return lax.ppermute(x, 'chip', [(i, i ^ m) for i in range(n)])]
    ppermute x12, waiting for transfers between devices: 46.7 us -> 62.2 us  [xor_swap(): return lax.ppermute(x, 'chip', [(i, i ^ m) for i in range(n)])]
    all_to_all x2 -> x0, starting transfers between devices: 12.4 us -> none  [the longest x1 6.82 us: local(): lax.all_to_all(upstream_cols.reshape(count, tok_rows, w_rows), SEQ, 0, 0,...]
    ppermute x2, starting transfers between devices: 4.45 us -> 10.1 us  [halo(): after = lax.ppermute(shard, SEQ, down)]
    dynamic_update_slice x11, other arithmetic: 8.6 us -> 13.3 us  [local(): lax.dynamic_update_slice_in_dim(grad_ext[side], cur + term, start, axis=0)]
    ppermute x2, waiting for transfers between devices: 4.1 us -> 0.01 us  [halo(): before = lax.ppermute(shard, SEQ, up)]
  transfers between devices with their start and end apart: 24 -> 22, of which waited for: 14 -> 13; matrix products, arithmetic and copies ran while one was open for 24% -> 16% of each run, Pallas kernels for 5% -> 0%
where the time goes in v9:
time: 276 us; the launch traced here: 272 us
  waiting for transfers between devices  130 us (47%)
  starting transfers between devices  46.5 us (17%)
  other arithmetic  32.2 us (12%)
  local copies, waits for them, and re-layouts  21.5 us (8%)
  between operations  17.8 us (6%)
  Pallas kernels  12.2 us (4%)
  matrix products  11.4 us (4%)
    ppermute x12, waiting for transfers between devices, xor_swap(): return lax.ppermute(x, 'chip', [(i, i ^ m) for i in range(n)])  62.2 us
    reduce_scatter x1, waiting for transfers between devices, local(): lax.psum_scatter(partial.astype(jnp.bfloat16), SEQ, scatter_dimension=0,...  58.2 us
    ppermute x12, starting transfers between devices, xor_swap(): return lax.ppermute(x, 'chip', [(i, i ^ m) for i in range(n)])  26.4 us
    dynamic_update_slice x11, other arithmetic, local(): lax.dynamic_update_slice_in_dim(grad_ext[side], cur + term, start, axis=0)  13.3 us
    pallas_call x1, Pallas kernels, attention(): pl.pallas_call(_attn_kernel, grid=(heads,), in_specs=[pl.BlockSpec((1, ke...  12.2 us
    ppermute x2, starting transfers between devices, halo(): after = lax.ppermute(shard, SEQ, down)  10.1 us
    ppermute x2, waiting for transfers between devices, halo(): after = lax.ppermute(shard, SEQ, down)  9.49 us
    ppermute x2, starting transfers between devices, halo(): before = lax.ppermute(shard, SEQ, up)  6.79 us
  transfers between devices with their start and end apart: 22, of which 13 were waited for; matrix products, arithmetic and copies ran while one was open for 16% of the time, Pallas kernels for 0%

profile of v9, /device:TPU:11, one launch (start us, length us, event | category | flops | bytes accessed | tf_op | source)
XLA Modules:
  0.0 271.5 jit_solution(330775784201179317)
XLA Ops:
  7.2 1.3 fusion.31
  9.8 1.9 broadcast_select_fusion.3
  13.5 2.0 collective-permute-start.1
  15.5 3.5 %collective-permute-start = (bf16[2,128,1024]{2,1,0:T(8,128)(2,1)}, bf16[2,128,1024]{2,1,0:T(8,128)(2,1)S(1)}, u32[]{:S(2)}, u32[]{:S(2)}) collective-permute-start(bf16[2,128,1024]{2,1,0:T(8,128)(2,1)} %get-tuple-element.30), channel_id=1, source_target_pairs={{0,1},{1,2},{2,3},{3,4},{4,5},{5,6},{6,7},{7,8},{8,9},{9,10},{10,1... | collective-permute-start | bytes 1572872 | tf_op jit(solution)/shard_map/ppermute | solution.py:62
  19.4 1.2 add.158
  20.9 2.2 collective-permute-start.3
  23.1 15.4 %collective-permute-done.3 = bf16[4,32768]{1,0:T(4,128)(2,1)S(1)} collective-permute-done((bf16[4,32768]{1,0:T(4,128)(2,1)S(1)}, bf16[4,32768]{1,0:T(4,128)(2,1)S(1)}, u32[]{:S(2)}, u32[]{:S(2)}) %collective-permute-start.3) | collective-permute-done | bytes 262176 | tf_op jit(solution)/shard_map/ppermute | solution.py:28
  41.8 3.0 %collective-permute-done.4 = bf16[2,32768]{1,0:T(2,128)(2,1)S(1)} collective-permute-done((bf16[2,32768]{1,0:T(2,128)(2,1)S(1)}, bf16[2,32768]{1,0:T(2,128)(2,1)S(1)}, u32[]{:S(2)}, u32[]{:S(2)}) %collective-permute-start.4) | collective-permute-done | bytes 131104 | tf_op jit(solution)/shard_map/ppermute | solution.py:28
  46.1 4.5 %collective-permute-done.5 = bf16[1,32768]{1,0:T(2,128)(2,1)S(1)} collective-permute-done((bf16[1,32768]{1,0:T(2,128)(2,1)S(1)}, bf16[1,32768]{1,0:T(2,128)(2,1)S(1)}, u32[]{:S(2)}, u32[]{:S(2)}) %collective-permute-start.5) | collective-permute-done | bytes 65568 | tf_op jit(solution)/shard_map/ppermute | solution.py:28
  51.2 10.1 %collective-permute-done.6 = bf16[1,32768]{1,0:T(2,128)(2,1)S(1)} collective-permute-done((bf16[1,32768]{1,0:T(2,128)(2,1)S(1)}, bf16[1,32768]{1,0:T(2,128)(2,1)S(1)}, u32[]{:S(2)}, u32[]{:S(2)}) %collective-permute-start.6) | collective-permute-done | bytes 65568 | tf_op jit(solution)/shard_map/ppermute | solution.py:28
  61.9 16.1 %collective-permute-start.7 = (bf16[2,32768]{1,0:T(2,128)(2,1)S(1)}, bf16[2,32768]{1,0:T(2,128)(2,1)S(1)}, u32[]{:S(2)}, u32[]{:S(2)}) collective-permute-start(bf16[2,32768]{1,0:T(2,128)(2,1)S(1)} %broadcast_select_fusion.13), channel_id=1, source_target_pairs={{0,4},{2,6},{4,0},{6,2},{8,12},{10,14},{12,8},{14,10},{1,5},{3,7},... | collective-permute-start | bytes 393224 | tf_op jit(solution)/shard_map/ppermute | solution.py:28
  78.1 3.0 %collective-permute-done.7 = bf16[2,32768]{1,0:T(2,128)(2,1)S(1)} collective-permute-done((bf16[2,32768]{1,0:T(2,128)(2,1)S(1)}, bf16[2,32768]{1,0:T(2,128)(2,1)S(1)}, u32[]{:S(2)}, u32[]{:S(2)}) %collective-permute-start.7) | collective-permute-done | bytes 131104 | tf_op jit(solution)/shard_map/ppermute | solution.py:28
  81.7 6.3 %collective-permute-done.8 = bf16[4,32768]{1,0:T(4,128)(2,1)S(1)} collective-permute-done((bf16[4,32768]{1,0:T(4,128)(2,1)S(1)}, bf16[4,32768]{1,0:T(4,128)(2,1)S(1)}, u32[]{:S(2)}, u32[]{:S(2)}) %collective-permute-start.8) | collective-permute-done | bytes 262176 | tf_op jit(solution)/shard_map/ppermute | solution.py:28
  88.5 2.4 collective-permute-start.9
  91.0 1.3 copy-done.8
  92.3 1.3 copy-done.9
  96.2 4.4 %convolution_convert_fusion.2.up_ref = bf16[128,1024]{1,0:T(8,128)(2,1)} fusion(bf16[128,2048]{1,0:T(8,128)(2,1)S(1)} %copy-done, bf16[1024,2048]{1,0:T(8,128)(2,1)} %all-gather.2.cloned.1.call-done), kind=kOutput, calls=%fused_computation.11 | convolution fusion | flops 537001984 | bytes 4980736 | tf_op jit(solution)/shard_map/dot_general | solution.py:146
  101.2 12.2 %shard_map.119 = (bf16[128,1024]{1,0:T(8,128)(2,1)}, bf16[128,1024]{1,0:T(8,128)(2,1)}, f32[1024,1024]{1,0:T(8,128)}, f32[1024,1024]{1,0:T(8,128)}) custom-call(f32[1,1024]{1,0:T(1,128)} %bitcast.103, bf16[128,1024]{1,0:T(8,128)(2,1)} %q_ref.1, bf16[1024,1024]{1,0:T(8,128)(2,1)} %get-tuple-element.20.k_ref, bf16[1024,1024]{1,0:T(8,128)(2,1)} %get-tuple-element.19.v_ref, ...), custom_call_target="tpu_custom_call" | custom-call | tf_op jit(solution)/shard_map/pallas_call | solution.py:95
  113.4 1.3 slice.234
  114.7 1.3 slice.235
  118.2 3.4 %slice_select_fusion = (f32[384,1024]{1,0:T(8,128)}, f32[384,1024]{1,0:T(8,128)S(1)}) fusion(f32[1024,1024]{1,0:T(8,128)} %get-tuple-element.12, pred[384]{0:T(512)(128)(4,1)S(1)} %copy-done.13, f32[1024,1024]{1,0:T(8,128)} %get-tuple-element.11), kind=kLoop, calls=%fused_computation.9 | loop fusion | flops 786432 | bytes 6291840 | tf_op jit(solution)/shard_map/dynamic_update_slice | solution.py:173
  121.7 1.9 fusion.11
  123.6 2.0 fusion.10
  125.6 1.9 add_dynamic-update-slice_fusion.1
  127.5 1.9 add_dynamic-update-slice_fusion
  129.5 1.1 broadcast_select_fusion
  130.6 1.4 select_n.280
  132.0 1.6 copy.36
  133.6 1.4 bitcast_dynamic-update-slice_fusion
  135.2 1.5 convert_add_fusion
  137.1 7.1 %collective-permute-done.13 = bf16[4,32768]{1,0:T(4,128)(2,1)S(1)} collective-permute-done((bf16[4,32768]{1,0:T(4,128)(2,1)S(1)}, bf16[4,32768]{1,0:T(4,128)(2,1)S(1)}, u32[]{:S(2)}, u32[]{:S(2)}) %collective-permute-start.13) | collective-permute-done | bytes 262176 | tf_op jit(solution)/shard_map/ppermute | solution.py:28
  144.7 1.2 collective-permute-start.14
  145.9 2.6 collective-permute-done.14
  150.0 3.8 %collective-permute-done.15 = bf16[1,32768]{1,0:T(2,128)(2,1)S(1)} collective-permute-done((bf16[1,32768]{1,0:T(2,128)(2,1)S(1)}, bf16[1,32768]{1,0:T(2,128)(2,1)S(1)}, u32[]{:S(2)}, u32[]{:S(2)}) %collective-permute-start.15) | collective-permute-done | bytes 65568 | tf_op jit(solution)/shard_map/ppermute | solution.py:28
  154.0 2.2 collective-permute-start.16
  156.3 3.2 %collective-permute-done.16 = bf16[1,32768]{1,0:T(2,128)(2,1)S(1)} collective-permute-done((bf16[1,32768]{1,0:T(2,128)(2,1)S(1)}, bf16[1,32768]{1,0:T(2,128)(2,1)S(1)}, u32[]{:S(2)}, u32[]{:S(2)}) %collective-permute-start.16) | collective-permute-done | bytes 65568 | tf_op jit(solution)/shard_map/ppermute | solution.py:28
  160.1 2.7 collective-permute-start.17
  163.0 3.1 %collective-permute-done.17 = bf16[2,32768]{1,0:T(2,128)(2,1)S(1)} collective-permute-done((bf16[2,32768]{1,0:T(2,128)(2,1)S(1)}, bf16[2,32768]{1,0:T(2,128)(2,1)S(1)}, u32[]{:S(2)}, u32[]{:S(2)}) %collective-permute-start.17) | collective-permute-done | bytes 131104 | tf_op jit(solution)/shard_map/ppermute | solution.py:28
  167.8 8.1 %collective-permute-start.11 = (bf16[2,256,1024]{2,1,0:T(8,128)(2,1)}, bf16[2,256,1024]{2,1,0:T(8,128)(2,1)}, u32[]{:S(2)}, u32[]{:S(2)}) collective-permute-start(bf16[2,256,1024]{2,1,0:T(8,128)(2,1)} %pad_maximum_fusion.3), channel_id=1, source_target_pairs={{1,0},{2,1},{3,2},{4,3},{5,4},{6,5},{7,6},{8,7},{9,8},{10,9},{11,1... | collective-permute-start | bytes 3145736 | tf_op jit(solution)/shard_map/ppermute | solution.py:63
  175.9 3.3 %collective-permute-start.10 = (bf16[2,256,1024]{2,1,0:T(8,128)(2,1)}, bf16[2,256,1024]{2,1,0:T(8,128)(2,1)}, u32[]{:S(2)}, u32[]{:S(2)}) collective-permute-start(bf16[2,256,1024]{2,1,0:T(8,128)(2,1)} %pad_maximum_fusion.3), channel_id=1, source_target_pairs={{0,1},{1,2},{2,3},{3,4},{4,5},{5,6},{6,7},{7,8},{8,9},{9,10},{10,1... | collective-permute-start | bytes 3145736 | tf_op jit(solution)/shard_map/ppermute | solution.py:62
  179.7 3.3 %convolution_convert_fusion = bf16[1024,2048]{1,0:T(8,128)(2,1)} fusion(bf16[128,1024]{1,0:T(8,128)(2,1)S(1)} %copy-done.12, bf16[128,2048]{1,0:T(8,128)(2,1)S(1)} %copy-done), kind=kOutput, calls=%fused_computation | convolution fusion | flops 538968064 | bytes 4980736 | tf_op jit(solution)/shard_map/dot_general | solution.py:189
  183.1 3.7 %convolution_convert_fusion.1 = bf16[128,2048]{1,0:T(8,128)(2,1)} fusion(bf16[128,1024]{1,0:T(8,128)(2,1)S(1)} %copy-done.12, bf16[1024,2048]{1,0:T(8,128)(2,1)} %all-gather.2.cloned.1.call-done), kind=kOutput, calls=%fused_computation.5 | convolution fusion | flops 537133056 | bytes 4980736 | tf_op jit(solution)/shard_map/dot_general | solution.py:186
  188.1 2.5 reshape.106
  190.6 1.2 reshape.107
  191.8 9.5 %collective-permute-done.11 = bf16[2,256,1024]{2,1,0:T(8,128)(2,1)} collective-permute-done((bf16[2,256,1024]{2,1,0:T(8,128)(2,1)}, bf16[2,256,1024]{2,1,0:T(8,128)(2,1)}, u32[]{:S(2)}, u32[]{:S(2)}) %collective-permute-start.11) | collective-permute-done | bytes 1048608 | tf_op jit(solution)/shard_map/ppermute | solution.py:63
  201.3 2.6 fusion.7
  204.7 58.2 %reduce-scatter.2.cloned.1.call-done = bf16[64,2048]{1,0:T(8,128)(2,1)} async-done(((bf16[1024,2048]{1,0:T(8,128)(2,1)}), bf16[64,2048]{1,0:T(8,128)(2,1)}) %reduce-scatter.2.cloned.1.call-update) | async-done | bytes 262160 | tf_op jit(solution)/shard_map/reduce_scatter | solution.py:192
  262.9 1.8 convert_element_type.104
  (109 shorter events, 20.7 us)
Async XLA Ops:
  7.2 89.0 %copy-start = (bf16[128,2048]{1,0:T(8,128)(2,1)S(1)}, bf16[128,2048]{1,0:T(8,128)(2,1)}, u32[]{:S(2)}) copy-start(bf16[128,2048]{1,0:T(8,128)(2,1)} %param.12) | copy-start | bytes 1572868
  7.2 89.0 %all-gather.2.cloned.1.call-start = ((), (), s32[]{:S(2)}) async-start(), calls=%async_computation.1 | async-start | bytes 4456448 | tf_op jit(solution)/shard_map/all_gather | solution.py:117
  12.8 10.3 %copy-start.15 = (s32[3]{0:T(128)S(1)}, s32[3]{0:T(128)}, u32[]{:S(2)}) copy-start(s32[3]{0:T(128)} %constant.80.clone) | copy-start | bytes 40
  12.8 10.3 %copy-start.14 = (s32[1,3]{1,0:T(1,128)S(1)}, s32[1,3]{1,0:T(1,128)}, u32[]{:S(2)}) copy-start(s32[1,3]{1,0:T(1,128)} %param.14) | copy-start | bytes 40
  12.8 6.6 %collective-permute-start.2 = (bf16[8,32768]{1,0:T(8,128)(2,1)}, bf16[8,32768]{1,0:T(8,128)(2,1)}, u32[]{:S(2)}, u32[]{:S(2)}) collective-permute-start(bf16[8,32768]{1,0:T(8,128)(2,1)} %select_n.265), channel_id=1, source_target_pairs={{0,1},{1,0},{2,3},{3,2},{4,5},{5,4},{6,7},{7,6},{8,9},{9,8},{10,11... | collective-permute-start | bytes 1572872 | tf_op jit(solution)/shard_map/ppermute | solution.py:25
  13.5 32.5 %collective-permute-start.1 = (bf16[2,128,1024]{2,1,0:T(8,128)(2,1)}, bf16[2,128,1024]{2,1,0:T(8,128)(2,1)S(1)}, u32[]{:S(2)}, u32[]{:S(2)}) collective-permute-start(bf16[2,128,1024]{2,1,0:T(8,128)(2,1)} %get-tuple-element.30), channel_id=1, source_target_pairs={{1,0},{2,1},{3,2},{4,3},{5,4},{6,5},{7,6},{8,7},{9,8},{10,9},{11,1... | collective-permute-start | bytes 1572872 | tf_op jit(solution)/shard_map/ppermute | solution.py:63
  15.5 30.4 %collective-permute-start = (bf16[2,128,1024]{2,1,0:T(8,128)(2,1)}, bf16[2,128,1024]{2,1,0:T(8,128)(2,1)S(1)}, u32[]{:S(2)}, u32[]{:S(2)}) collective-permute-start(bf16[2,128,1024]{2,1,0:T(8,128)(2,1)} %get-tuple-element.30), channel_id=1, source_target_pairs={{0,1},{1,2},{2,3},{3,4},{4,5},{5,6},{6,7},{7,8},{8,9},{9,10},{10,1... | collective-permute-start | bytes 1572872 | tf_op jit(solution)/shard_map/ppermute | solution.py:62
  19.1 243.8 %reduce-scatter.2.cloned.1.call-start = ((), (), s32[]{:S(2)}) async-start(), calls=%async_computation.2 | async-start | bytes 4456448 | tf_op jit(solution)/shard_map/reduce_scatter | solution.py:192
  19.4 26.6 %copy-start.10 = (bf16[128,1024]{1,0:T(8,128)(2,1)S(1)}, bf16[128,1024]{1,0:T(8,128)(2,1)}, u32[]{:S(2)}) copy-start(bf16[128,1024]{1,0:T(8,128)(2,1)} %param.10) | copy-start | bytes 786436
  19.4 26.6 %copy-start.11 = (bf16[128,1024]{1,0:T(8,128)(2,1)S(1)}, bf16[128,1024]{1,0:T(8,128)(2,1)}, u32[]{:S(2)}) copy-start(bf16[128,1024]{1,0:T(8,128)(2,1)} %param.9) | copy-start | bytes 786436
  20.9 17.6 %collective-permute-start.3 = (bf16[4,32768]{1,0:T(4,128)(2,1)S(1)}, bf16[4,32768]{1,0:T(4,128)(2,1)S(1)}, u32[]{:S(2)}, u32[]{:S(2)}) collective-permute-start(bf16[4,32768]{1,0:T(4,128)(2,1)S(1)} %broadcast_select_fusion.5), channel_id=1, source_target_pairs={{0,2},{2,0},{4,6},{6,4},{8,10},{10,8},{12,14},{14,12},{1,3},{3,1},... | collective-permute-start | bytes 786440 | tf_op jit(solution)/shard_map/ppermute | solution.py:28
  38.9 5.9 %collective-permute-start.4 = (bf16[2,32768]{1,0:T(2,128)(2,1)S(1)}, bf16[2,32768]{1,0:T(2,128)(2,1)S(1)}, u32[]{:S(2)}, u32[]{:S(2)}) collective-permute-start(bf16[2,32768]{1,0:T(2,128)(2,1)S(1)} %broadcast_select_fusion.6), channel_id=1, source_target_pairs={{0,4},{2,6},{4,0},{6,2},{8,12},{10,14},{12,8},{14,10},{1,5},{3,7},... | collective-permute-start | bytes 393224 | tf_op jit(solution)/shard_map/ppermute | solution.py:28
  45.4 5.2 %collective-permute-start.5 = (bf16[1,32768]{1,0:T(2,128)(2,1)S(1)}, bf16[1,32768]{1,0:T(2,128)(2,1)S(1)}, u32[]{:S(2)}, u32[]{:S(2)}) collective-permute-start(bf16[1,32768]{1,0:T(2,128)(2,1)S(1)} %broadcast_select_fusion.10), channel_id=1, source_target_pairs={{0,8},{2,10},{4,12},{6,14},{8,0},{10,2},{12,4},{14,6},{1,9},{3,11}... | collective-permute-start | bytes 196616 | tf_op jit(solution)/shard_map/ppermute | solution.py:28
  50.9 10.4 %collective-permute-start.6 = (bf16[1,32768]{1,0:T(2,128)(2,1)S(1)}, bf16[1,32768]{1,0:T(2,128)(2,1)S(1)}, u32[]{:S(2)}, u32[]{:S(2)}) collective-permute-start(bf16[1,32768]{1,0:T(2,128)(2,1)S(1)} %fusion.22), channel_id=1, source_target_pairs={{0,8},{2,10},{4,12},{6,14},{8,0},{10,2},{12,4},{14,6},{1,9},{3,11}... | collective-permute-start | bytes 196616 | tf_op jit(solution)/shard_map/ppermute | solution.py:28
  61.9 19.2 %collective-permute-start.7 = (bf16[2,32768]{1,0:T(2,128)(2,1)S(1)}, bf16[2,32768]{1,0:T(2,128)(2,1)S(1)}, u32[]{:S(2)}, u32[]{:S(2)}) collective-permute-start(bf16[2,32768]{1,0:T(2,128)(2,1)S(1)} %broadcast_select_fusion.13), channel_id=1, source_target_pairs={{0,4},{2,6},{4,0},{6,2},{8,12},{10,14},{12,8},{14,10},{1,5},{3,7},... | collective-permute-start | bytes 393224 | tf_op jit(solution)/shard_map/ppermute | solution.py:28
  81.5 6.5 %collective-permute-start.8 = (bf16[4,32768]{1,0:T(4,128)(2,1)S(1)}, bf16[4,32768]{1,0:T(4,128)(2,1)S(1)}, u32[]{:S(2)}, u32[]{:S(2)}) collective-permute-start(bf16[4,32768]{1,0:T(4,128)(2,1)S(1)} %maximum_select_fusion.4), channel_id=1, source_target_pairs={{0,2},{2,0},{4,6},{6,4},{8,10},{10,8},{12,14},{14,12},{1,3},{3,1},... | collective-permute-start | bytes 786440 | tf_op jit(solution)/shard_map/ppermute | solution.py:28
  88.5 5.1 %collective-permute-start.9 = (bf16[8,32768]{1,0:T(8,128)(2,1)S(1)}, bf16[8,32768]{1,0:T(8,128)(2,1)S(1)}, u32[]{:S(2)}, u32[]{:S(2)}) collective-permute-start(bf16[8,32768]{1,0:T(8,128)(2,1)S(1)} %maximum_select_fusion.2), channel_id=1, source_target_pairs={{0,1},{1,0},{2,3},{3,2},{4,5},{5,4},{6,7},{7,6},{8,9},{9,8},{10,11... | collective-permute-start | bytes 1572872 | tf_op jit(solution)/shard_map/ppermute | solution.py:25
  91.0 1.3 copy-start.8
  92.3 1.3 copy-start.9
  116.0 1.0 copy-start.4
  116.0 2.2 copy-start.13
  118.2 3.5 %copy-start.7 = (f32[1024,1024]{1,0:T(8,128)S(1)}, f32[1024,1024]{1,0:T(8,128)}, u32[]{:S(2)}) copy-start(f32[1024,1024]{1,0:T(8,128)} %get-tuple-element.12) | copy-start | bytes 12582916
  118.2 17.0 %collective-permute-start.12 = (bf16[8,32768]{1,0:T(8,128)(2,1)}, bf16[8,32768]{1,0:T(8,128)(2,1)}, u32[]{:S(2)}, u32[]{:S(2)}) collective-permute-start(bf16[8,32768]{1,0:T(8,128)(2,1)} %convert_element_type.89), channel_id=1, source_target_pairs={{0,1},{1,0},{2,3},{3,2},{4,5},{5,4},{6,7},{7,6},{8,9},{9,8},{10,11... | collective-permute-start | bytes 1572872 | tf_op jit(solution)/shard_map/ppermute | solution.py:25
  123.6 5.9 %copy-start.5 = (f32[256,1024]{1,0:T(8,128)S(1)}, f32[256,1024]{1,0:T(8,128)}, u32[]{:S(2)}) copy-start(f32[256,1024]{1,0:T(8,128)} %copy-done.4) | copy-start | bytes 3145732
  132.0 3.0 %copy-start.6 = (f32[1024,1024]{1,0:T(8,128)S(1)}, f32[1024,1024]{1,0:T(8,128)}, u32[]{:S(2)}) copy-start(f32[1024,1024]{1,0:T(8,128)} %get-tuple-element.11) | copy-start | bytes 12582916
  135.0 27.7 %copy-start.3 = (f32[1,384,1024]{2,1,0:T(8,128)}, f32[1,384,1024]{2,1,0:T(8,128)S(1)}, u32[]{:S(2)}) copy-start(f32[1,384,1024]{2,1,0:T(8,128)S(1)} %bitcast_dynamic-update-slice_fusion) | copy-start | bytes 4718596
  136.9 7.4 %collective-permute-start.13 = (bf16[4,32768]{1,0:T(4,128)(2,1)S(1)}, bf16[4,32768]{1,0:T(4,128)(2,1)S(1)}, u32[]{:S(2)}, u32[]{:S(2)}) collective-permute-start(bf16[4,32768]{1,0:T(4,128)(2,1)S(1)} %select_convert_fusion.1), channel_id=1, source_target_pairs={{0,2},{2,0},{4,6},{6,4},{8,10},{10,8},{12,14},{14,12},{1,3},{3,1},... | collective-permute-start | bytes 786440 | tf_op jit(solution)/shard_map/ppermute | solution.py:28
  144.7 3.9 %collective-permute-start.14 = (bf16[2,32768]{1,0:T(2,128)(2,1)S(1)}, bf16[2,32768]{1,0:T(2,128)(2,1)S(1)}, u32[]{:S(2)}, u32[]{:S(2)}) collective-permute-start(bf16[2,32768]{1,0:T(2,128)(2,1)S(1)} %select_convert_fusion.2), channel_id=1, source_target_pairs={{0,4},{2,6},{4,0},{6,2},{8,12},{10,14},{12,8},{14,10},{1,5},{3,7},... | collective-permute-start | bytes 393224 | tf_op jit(solution)/shard_map/ppermute | solution.py:28
  148.9 4.9 %collective-permute-start.15 = (bf16[1,32768]{1,0:T(2,128)(2,1)S(1)}, bf16[1,32768]{1,0:T(2,128)(2,1)S(1)}, u32[]{:S(2)}, u32[]{:S(2)}) collective-permute-start(bf16[1,32768]{1,0:T(2,128)(2,1)S(1)} %fusion.25), channel_id=1, source_target_pairs={{0,8},{2,10},{4,12},{6,14},{8,0},{10,2},{12,4},{14,6},{1,9},{3,11}... | collective-permute-start | bytes 196616 | tf_op jit(solution)/shard_map/ppermute | solution.py:28
  154.0 5.5 %collective-permute-start.16 = (bf16[1,32768]{1,0:T(2,128)(2,1)S(1)}, bf16[1,32768]{1,0:T(2,128)(2,1)S(1)}, u32[]{:S(2)}, u32[]{:S(2)}) collective-permute-start(bf16[1,32768]{1,0:T(2,128)(2,1)S(1)} %fusion.24), channel_id=1, source_target_pairs={{0,8},{2,10},{4,12},{6,14},{8,0},{10,2},{12,4},{14,6},{1,9},{3,11}... | collective-permute-start | bytes 196616 | tf_op jit(solution)/shard_map/ppermute | solution.py:28
  156.3 6.7 %copy-start.1 = (f32[1,384,1024]{2,1,0:T(8,128)}, f32[1,384,1024]{2,1,0:T(8,128)S(1)}, u32[]{:S(2)}) copy-start(f32[1,384,1024]{2,1,0:T(8,128)S(1)} %bitcast_dynamic-update-slice_fusion.1) | copy-start | bytes 4718596
  160.1 6.0 %collective-permute-start.17 = (bf16[2,32768]{1,0:T(2,128)(2,1)S(1)}, bf16[2,32768]{1,0:T(2,128)(2,1)S(1)}, u32[]{:S(2)}, u32[]{:S(2)}) collective-permute-start(bf16[2,32768]{1,0:T(2,128)(2,1)S(1)} %broadcast_select_fusion.12), channel_id=1, source_target_pairs={{0,4},{2,6},{4,0},{6,2},{8,12},{10,14},{12,8},{14,10},{1,5},{3,7},... | collective-permute-start | bytes 393224 | tf_op jit(solution)/shard_map/ppermute | solution.py:28
  166.6 12.6 %collective-permute-start.18 = (bf16[4,32768]{1,0:T(4,128)(2,1)S(1)}, bf16[4,32768]{1,0:T(4,128)(2,1)S(1)}, u32[]{:S(2)}, u32[]{:S(2)}) collective-permute-start(bf16[4,32768]{1,0:T(4,128)(2,1)S(1)} %maximum_select_fusion.5), channel_id=1, source_target_pairs={{0,2},{2,0},{4,6},{6,4},{8,10},{10,8},{12,14},{14,12},{1,3},{3,1},... | collective-permute-start | bytes 786440 | tf_op jit(solution)/shard_map/ppermute | solution.py:28
  166.8 13.0 %copy-start.12 = (bf16[128,1024]{1,0:T(8,128)(2,1)S(1)}, bf16[128,1024]{1,0:T(8,128)(2,1)}, u32[]{:S(2)}) copy-start(bf16[128,1024]{1,0:T(8,128)(2,1)} %get-tuple-element.9) | copy-start | bytes 786436
  167.8 33.5 %collective-permute-start.11 = (bf16[2,256,1024]{2,1,0:T(8,128)(2,1)}, bf16[2,256,1024]{2,1,0:T(8,128)(2,1)}, u32[]{:S(2)}, u32[]{:S(2)}) collective-permute-start(bf16[2,256,1024]{2,1,0:T(8,128)(2,1)} %pad_maximum_fusion.3), channel_id=1, source_target_pairs={{1,0},{2,1},{3,2},{4,3},{5,4},{6,5},{7,6},{8,7},{9,8},{10,9},{11,1... | collective-permute-start | bytes 3145736 | tf_op jit(solution)/shard_map/ppermute | solution.py:63
  175.9 25.4 %collective-permute-start.10 = (bf16[2,256,1024]{2,1,0:T(8,128)(2,1)}, bf16[2,256,1024]{2,1,0:T(8,128)(2,1)}, u32[]{:S(2)}, u32[]{:S(2)}) collective-permute-start(bf16[2,256,1024]{2,1,0:T(8,128)(2,1)} %pad_maximum_fusion.3), channel_id=1, source_target_pairs={{0,1},{1,2},{2,3},{3,4},{4,5},{5,6},{6,7},{7,8},{8,9},{9,10},{10,1... | collective-permute-start | bytes 3145736 | tf_op jit(solution)/shard_map/ppermute | solution.py:62
  179.7 7.1 %collective-permute-start.19 = (bf16[8,32768]{1,0:T(8,128)(2,1)S(1)}, bf16[8,32768]{1,0:T(8,128)(2,1)S(1)}, u32[]{:S(2)}, u32[]{:S(2)}) collective-permute-start(bf16[8,32768]{1,0:T(8,128)(2,1)S(1)} %maximum_select_fusion.3), channel_id=1, source_target_pairs={{0,1},{1,0},{2,3},{3,2},{4,5},{5,4},{6,7},{7,6},{8,9},{9,8},{10,11... | collective-permute-start | bytes 1572872 | tf_op jit(solution)/shard_map/ppermute | solution.py:25
  188.1 13.2 %copy-start.2 = (f32[1,384,1024]{2,1,0:T(8,128)S(1)}, f32[1,384,1024]{2,1,0:T(8,128)}, u32[]{:S(2)}) copy-start(f32[1,384,1024]{2,1,0:T(8,128)} %copy-done.1) | copy-start | bytes 4718596
Sparse Core Ops, SparseCore 0:
  19.2 58.1 all-gather.1
  183.2 79.6 reduce-scatter.1

commit v10 on v4

--- a/solution.py
+++ b/solution.py
@@ -203,17 +203,20 @@
         [grad_ext[:, : blocks_dev * BLK], grad_ext[:, 2 * blocks_dev * BLK :]], axis=1
     ).astype(jnp.bfloat16)
     from_prev, from_next = halo(rims)
-    own = grad_ext[:, blocks_dev * BLK : 2 * blocks_dev * BLK]
-    own = own + from_prev[:, blocks_dev * BLK :].astype(jnp.float32)
-    own = own + from_next[:, : blocks_dev * BLK].astype(jnp.float32)
-    for g in range(slots):
-        start = (global_blocks[g] % blocks_dev) * BLK
-        add = jnp.where(owners[g] == device, global_total[g], jnp.zeros_like(global_total[g]))
-        cur = lax.dynamic_slice_in_dim(own, start, BLK, axis=1)
-        own = lax.dynamic_update_slice_in_dim(own, cur + add, start, axis=1)
-    own = own.astype(jnp.bfloat16)
+    finished = []
+    for side in range(2):
+        own = grad_ext[side, blocks_dev * BLK : 2 * blocks_dev * BLK]
+        own = own + from_prev[side, blocks_dev * BLK :].astype(jnp.float32)
+        own = own + from_next[side, : blocks_dev * BLK].astype(jnp.float32)
+        for g in range(slots):
+            start = (global_blocks[g] % blocks_dev) * BLK
+            total = global_total[g, side]
+            add = jnp.where(owners[g] == device, total, jnp.zeros_like(total))
+            cur = lax.dynamic_slice_in_dim(own, start, BLK, axis=0)
+            own = lax.dynamic_update_slice_in_dim(own, cur + add, start, axis=0)
+        finished.append(own.astype(jnp.bfloat16))
     grad_query = jnp.concatenate(dq_rows, axis=0)
-    return (layer_out, grad_query, own[0], own[1], grad_weight)
+    return (layer_out, grad_query, finished[0], finished[1], grad_weight)
 
 
 def solution(mesh):

time: 258 us -> 247 us (0.957)
  local copies, waits for them, and re-layouts: 25.4 us -> 19.1 us
  other arithmetic: 26.7 us -> 23.6 us
  waiting for transfers between devices: 86.5 us -> 83.5 us
    convert_element_type x2 -> x0, local copies, waits for them, and re-layouts: 5 us -> none  [local(): own = lax.dynamic_update_slice_in_dim(own, cur + add, start, axis=1)]
    ppermute x2, starting transfers between devices: 6 us -> 9.62 us  [halo(): before = lax.ppermute(shard, SEQ, up)]
  transfers between devices with their start and end apart: 24 -> 24, of which waited for: 14 -> 15; matrix products, arithmetic and copies ran while one was open for 24% -> 22% of each run, Pallas kernels for 5% -> 5%
where the time goes in v10:
time: 247 us; the launch traced here: 244 us
  waiting for transfers between devices  83.5 us (34%)
  starting transfers between devices  72.7 us (29%)
  other arithmetic  23.6 us (10%)
  local copies, waits for them, and re-layouts  19.1 us (8%)
  between operations  17.8 us (7%)
  matrix products  15.5 us (6%)
  Pallas kernels  12.3 us (5%)
    ppermute x12, waiting for transfers between devices, xor_swap(): return lax.ppermute(x, 'chip', [(i, i ^ m) for i in range(n)])  45.6 us
    ppermute x12, starting transfers between devices, xor_swap(): return lax.ppermute(x, 'chip', [(i, i ^ m) for i in range(n)])  42.7 us
    all_to_all x1, waiting for transfers between devices, local(): lax.all_to_all(attn_out.reshape(tok_rows, count, w_rows), SEQ, 1, 0, tile...  15.9 us
    pallas_call x1, Pallas kernels, attention(): pl.pallas_call(_attn_kernel, grid=(heads,), in_specs=[pl.BlockSpec((1, ke...  12.3 us
    ppermute x2, starting transfers between devices, halo(): before = lax.ppermute(shard, SEQ, up)  9.62 us
    ppermute x2, waiting for transfers between devices, halo(): after = lax.ppermute(shard, SEQ, down)  9.58 us
    dynamic_update_slice x11, other arithmetic, local(): lax.dynamic_update_slice_in_dim(grad_ext[side], cur + term, start, axis=0)  9.1 us
    all_to_all x1, waiting for transfers between devices, local(): lax.all_to_all(upstream_cols.reshape(count, tok_rows, w_rows), SEQ, 0, 0,...  7.6 us
  transfers between devices with their start and end apart: 24, of which 15 were waited for; matrix products, arithmetic and copies ran while one was open for 22% of the time, Pallas kernels for 5%

profile of v10, /device:TPU:11, one launch (start us, length us, event | category | flops | bytes accessed | tf_op | source)
XLA Modules:
  0.0 244.4 jit_solution(13322740352995558698)
XLA Ops:
  8.0 1.3 fusion.40
  10.6 1.9 broadcast_select_fusion.3
  12.5 3.7 %collective-permute-start = (bf16[2,128,1024]{2,1,0:T(8,128)(2,1)}, bf16[2,128,1024]{2,1,0:T(8,128)(2,1)S(1)}, u32[]{:S(2)}, u32[]{:S(2)}) collective-permute-start(bf16[2,128,1024]{2,1,0:T(8,128)(2,1)} %get-tuple-element.28), channel_id=1, source_target_pairs={{0,1},{1,2},{2,3},{3,4},{4,5},{5,6},{6,7},{7,8},{8,9},{9,10},{10,1... | collective-permute-start | bytes 1572872 | tf_op jit(solution)/shard_map/ppermute | solution.py:62
  16.2 1.9 collective-permute-start.1
  19.2 1.5 collective-permute-start.2
  24.5 4.1 %collective-permute-done = bf16[2,128,1024]{2,1,0:T(8,128)(2,1)S(1)} collective-permute-done((bf16[2,128,1024]{2,1,0:T(8,128)(2,1)}, bf16[2,128,1024]{2,1,0:T(8,128)(2,1)S(1)}, u32[]{:S(2)}, u32[]{:S(2)}) %collective-permute-start) | collective-permute-done | bytes 524320 | tf_op jit(solution)/shard_map/ppermute | solution.py:62
  28.6 9.6 %collective-permute-done.1 = bf16[2,128,1024]{2,1,0:T(8,128)(2,1)S(1)} collective-permute-done((bf16[2,128,1024]{2,1,0:T(8,128)(2,1)}, bf16[2,128,1024]{2,1,0:T(8,128)(2,1)S(1)}, u32[]{:S(2)}, u32[]{:S(2)}) %collective-permute-start.1) | collective-permute-done | bytes 524320 | tf_op jit(solution)/shard_map/ppermute | solution.py:63
  40.2 5.2 %collective-permute-done.4 = bf16[2,32768]{1,0:T(2,128)(2,1)S(1)} collective-permute-done((bf16[2,32768]{1,0:T(2,128)(2,1)S(1)}, bf16[2,32768]{1,0:T(2,128)(2,1)S(1)}, u32[]{:S(2)}, u32[]{:S(2)}) %collective-permute-start.4) | collective-permute-done | bytes 131104 | tf_op jit(solution)/shard_map/ppermute | solution.py:28
  45.9 1.9 collective-permute-start.5
  47.8 2.9 %collective-permute-done.5 = bf16[1,32768]{1,0:T(2,128)(2,1)S(1)} collective-permute-done((bf16[1,32768]{1,0:T(2,128)(2,1)S(1)}, bf16[1,32768]{1,0:T(2,128)(2,1)S(1)}, u32[]{:S(2)}, u32[]{:S(2)}) %collective-permute-start.5) | collective-permute-done | bytes 65568 | tf_op jit(solution)/shard_map/ppermute | solution.py:28
  51.0 1.8 collective-permute-start.6
  52.9 14.2 %collective-permute-done.6 = bf16[1,32768]{1,0:T(2,128)(2,1)S(1)} collective-permute-done((bf16[1,32768]{1,0:T(2,128)(2,1)S(1)}, bf16[1,32768]{1,0:T(2,128)(2,1)S(1)}, u32[]{:S(2)}, u32[]{:S(2)}) %collective-permute-start.6) | collective-permute-done | bytes 65568 | tf_op jit(solution)/shard_map/ppermute | solution.py:28
  67.7 1.9 collective-permute-start.7
  69.6 5.5 %collective-permute-done.7 = bf16[2,32768]{1,0:T(2,128)(2,1)S(1)} collective-permute-done((bf16[2,32768]{1,0:T(2,128)(2,1)S(1)}, bf16[2,32768]{1,0:T(2,128)(2,1)S(1)}, u32[]{:S(2)}, u32[]{:S(2)}) %collective-permute-start.7) | collective-permute-done | bytes 131104 | tf_op jit(solution)/shard_map/ppermute | solution.py:28
  75.6 22.8 %collective-permute-start.8 = (bf16[4,32768]{1,0:T(4,128)(2,1)S(1)}, bf16[4,32768]{1,0:T(4,128)(2,1)S(1)}, u32[]{:S(2)}, u32[]{:S(2)}) collective-permute-start(bf16[4,32768]{1,0:T(4,128)(2,1)S(1)} %maximum_select_fusion.4), channel_id=1, source_target_pairs={{0,2},{2,0},{4,6},{6,4},{8,10},{10,8},{12,14},{14,12},{1,3},{3,1},... | collective-permute-start | bytes 786440 | tf_op jit(solution)/shard_map/ppermute | solution.py:28
  98.5 1.4 copy-done.4
  99.9 4.2 %collective-permute-done.8 = bf16[4,32768]{1,0:T(4,128)(2,1)S(1)} collective-permute-done((bf16[4,32768]{1,0:T(4,128)(2,1)S(1)}, bf16[4,32768]{1,0:T(4,128)(2,1)S(1)}, u32[]{:S(2)}, u32[]{:S(2)}) %collective-permute-start.8) | collective-permute-done | bytes 262176 | tf_op jit(solution)/shard_map/ppermute | solution.py:28
  104.6 1.6 collective-permute-start.9
  106.2 6.0 %fusion = bf16[8,16,8,128]{3,2,1,0:T(8,128)(2,1)S(1)} fusion(bf16[2048,2048]{1,0:T(8,128)(2,1)} %all-gather.3.cloned.1.call-done, bf16[64,2048]{1,0:T(8,128)(2,1)S(1)} %copy-done.8), kind=kOutput, calls=%fused_computation.7 | convolution fusion | flops 537001984 | bytes 8912896 | tf_op jit(solution)/shard_map/dot_general | solution.py:148
  113.0 6.8 %all-to-all-start = ((bf16[16,128,64]{1,2,0:T(8,128)(2,1)}), bf16[16,128,64]{1,2,0:T(8,128)(2,1)S(1)}, u32[]{:S(2)}, u32[]{:S(2)}) async-start(bf16[16,128,64]{1,2,0:T(8,128)(2,1)} %bitcast.145), calls=%async_computation | async-start | bytes 524288 | tf_op jit(solution)/shard_map/all_to_all | solution.py:151
  122.3 7.6 %all-to-all-done = bf16[16,128,64]{1,2,0:T(8,128)(2,1)S(1)} async-done(((bf16[16,128,64]{1,2,0:T(8,128)(2,1)}), bf16[16,128,64]{1,2,0:T(8,128)(2,1)S(1)}, u32[]{:S(2)}, u32[]{:S(2)}) %all-to-all-start) | async-done | bytes 262176 | tf_op jit(solution)/shard_map/all_to_all | solution.py:151
  131.4 12.3 %shard_map.119 = (bf16[128,1024]{1,0:T(8,128)(2,1)}, bf16[128,1024]{1,0:T(8,128)(2,1)}, f32[1024,1024]{1,0:T(8,128)}, f32[1024,1024]{1,0:T(8,128)}) custom-call(f32[1,1024]{1,0:T(1,128)} %bitcast.159, bf16[128,1024]{1,0:T(8,128)(2,1)} %q_ref.1, bf16[1024,1024]{1,0:T(8,128)(2,1)} %get-tuple-element.20.k_ref, bf16[1024,1024]{1,0:T(8,128)(2,1)} %get-tuple-element.19.v_ref, ...), custom_call_target="tpu_custom_call" | custom-call | tf_op jit(solution)/shard_map/pallas_call | solution.py:95
  143.7 1.3 slice.245
  145.0 1.3 slice.246
  149.1 1.7 slice_select_fusion
  151.3 2.1 convert_element_type.108
  153.6 2.4 select_n.304
  156.0 1.3 fusion.9
  157.3 1.2 fusion.8
  159.8 1.7 collective-permute-start.13
  164.0 3.8 %collective-permute-done.13 = bf16[4,32768]{1,0:T(4,128)(2,1)S(1)} collective-permute-done((bf16[4,32768]{1,0:T(4,128)(2,1)S(1)}, bf16[4,32768]{1,0:T(4,128)(2,1)S(1)}, u32[]{:S(2)}, u32[]{:S(2)}) %collective-permute-start.13) | collective-permute-done | bytes 262176 | tf_op jit(solution)/shard_map/ppermute | solution.py:28
  168.2 1.4 collective-permute-start.14
  170.8 1.3 collective-permute-done.14
  172.5 1.5 collective-permute-start.15
  175.1 2.3 collective-permute-done.15
  177.6 3.3 %collective-permute-start.16 = (bf16[1,32768]{1,0:T(2,128)(2,1)S(1)}, bf16[1,32768]{1,0:T(2,128)(2,1)S(1)}, u32[]{:S(2)}, u32[]{:S(2)}) collective-permute-start(bf16[1,32768]{1,0:T(2,128)(2,1)S(1)} %fusion.34), channel_id=1, source_target_pairs={{0,8},{2,10},{4,12},{6,14},{8,0},{10,2},{12,4},{14,6},{1,9},{3,11}... | collective-permute-start | bytes 196616 | tf_op jit(solution)/shard_map/ppermute | solution.py:28
  181.1 3.1 %collective-permute-done.16 = bf16[1,32768]{1,0:T(2,128)(2,1)S(1)} collective-permute-done((bf16[1,32768]{1,0:T(2,128)(2,1)S(1)}, bf16[1,32768]{1,0:T(2,128)(2,1)S(1)}, u32[]{:S(2)}, u32[]{:S(2)}) %collective-permute-start.16) | collective-permute-done | bytes 65568 | tf_op jit(solution)/shard_map/ppermute | solution.py:28
  184.8 4.5 %collective-permute-start.17 = (bf16[2,32768]{1,0:T(2,128)(2,1)S(1)}, bf16[2,32768]{1,0:T(2,128)(2,1)S(1)}, u32[]{:S(2)}, u32[]{:S(2)}) collective-permute-start(bf16[2,32768]{1,0:T(2,128)(2,1)S(1)} %broadcast_select_fusion.12), channel_id=1, source_target_pairs={{0,4},{2,6},{4,0},{6,2},{8,12},{10,14},{12,8},{14,10},{1,5},{3,7},... | collective-permute-start | bytes 393224 | tf_op jit(solution)/shard_map/ppermute | solution.py:28
  189.3 5.9 %collective-permute-start.10 = (bf16[2,256,1024]{2,1,0:T(8,128)(2,1)S(1)}, bf16[2,256,1024]{2,1,0:T(8,128)(2,1)}, u32[]{:S(2)}, u32[]{:S(2)}) collective-permute-start(bf16[2,256,1024]{2,1,0:T(8,128)(2,1)S(1)} %pad_maximum_fusion.3), channel_id=1, source_target_pairs={{0,1},{1,2},{2,3},{3,4},{4,5},{5,6},{6,7},{7,8},{8,9},{9,10},{10,1... | collective-permute-start | bytes 3145736 | tf_op jit(solution)/shard_map/ppermute | solution.py:62
  195.3 1.9 collective-permute-start.11
  198.0 5.0 %all-to-all-start.1 = ((bf16[1,128,16,64]{1,3,0,2:T(8,128)(2,1)}), bf16[1,128,16,64]{1,3,0,2:T(8,128)(2,1)S(1)}, u32[]{:S(2)}, u32[]{:S(2)}) async-start(bf16[1,128,16,64]{1,3,0,2:T(8,128)(2,1)} %bitcast.39), calls=%async_computation.1 | async-start | bytes 524288 | tf_op jit(solution)/shard_map/all_to_all | solution.py:195
  203.6 1.2 collective-permute-start.18
  204.8 3.7 %convolution_convert_fusion = bf16[128,2048]{1,0:T(8,128)(2,1)} fusion(bf16[128,1024]{1,0:T(8,128)(2,1)S(1)} %copy-done.9, bf16[1024,2048]{1,0:T(8,128)(2,1)} %all-gather.5.cloned.1.call-done), kind=kOutput, calls=%fused_computation | convolution fusion | flops 537133056 | bytes 4980736 | tf_op jit(solution)/shard_map/dot_general | solution.py:192
  208.5 15.9 %all-to-all-done.1 = bf16[1,128,16,64]{1,3,0,2:T(8,128)(2,1)S(1)} async-done(((bf16[1,128,16,64]{1,3,0,2:T(8,128)(2,1)}), bf16[1,128,16,64]{1,3,0,2:T(8,128)(2,1)S(1)}, u32[]{:S(2)}, u32[]{:S(2)}) %all-to-all-start.1) | async-done | bytes 262176 | tf_op jit(solution)/shard_map/all_to_all | solution.py:195
  224.6 2.0 collective-permute-done.18
  227.1 1.3 collective-permute-start.19
  228.4 5.7 %fusion.17 = f32[64,2048]{1,0:T(8,128)} fusion(bf16[2048,2048]{1,0:T(8,128)(2,1)} %all-gather.3.cloned.1.call-done, bf16[8,8,16,128]{3,2,1,0:T(8,128)(2,1)S(1)} %bitcast.156), kind=kOutput, calls=%fused_computation.54 | convolution fusion | flops 536870912 | bytes 9175040 | tf_op jit(solution)/shard_map/dot_general | solution.py:198
  234.8 2.8 %fusion.7 = (bf16[128,1024]{1,0:T(8,128)(2,1)}, bf16[128,1024]{1,0:T(8,128)(2,1)}) fusion(f32[1,384,1024]{2,1,0:T(8,128)} %copy-done, bf16[2,2,128,1024]{3,2,1,0:T(8,128)(2,1)S(1)} %select_n.316, bf16[2,256,1024]{2,1,0:T(8,128)(2,1)} %collective-permute-done.11, bf16[2,256,1024]{2,1,0:T(8,128)(2,1)} %collective-permute-done.10, pred[]{:T(512)S(6)} %eq.23, ...), kind=kLoop, calls=%fused_computation.23 | loop fusion | flops 2883584 | bytes 3670018 | tf_op jit(solution)/shard_map/convert_element_type | solution.py:217
  (106 shorter events, 26.6 us)
Async XLA Ops:
  7.2 13.6 %copy-start.11 = (s32[1,3]{1,0:T(1,128)S(1)}, s32[1,3]{1,0:T(1,128)}, u32[]{:S(2)}) copy-start(s32[1,3]{1,0:T(1,128)} %param.14) | copy-start | bytes 40
  7.2 99.0 %all-gather.3.cloned.1.call-start = ((), (), s32[]{:S(2)}) async-start(), calls=%async_computation.2 | async-start | bytes 8912896 | tf_op jit(solution)/shard_map/all_gather | solution.py:117
  7.9 196.9 %all-gather.5.cloned.1.call-start = ((), (), s32[]{:S(2)}) async-start(), calls=%async_computation.3 | async-start | bytes 4456448 | tf_op jit(solution)/shard_map/all_gather | solution.py:118
  10.6 13.0 %copy-start.12 = (s32[3]{0:T(128)S(1)}, s32[3]{0:T(128)}, u32[]{:S(2)}) copy-start(s32[3]{0:T(128)} %constant.85.clone) | copy-start | bytes 40
  12.5 16.0 %collective-permute-start = (bf16[2,128,1024]{2,1,0:T(8,128)(2,1)}, bf16[2,128,1024]{2,1,0:T(8,128)(2,1)S(1)}, u32[]{:S(2)}, u32[]{:S(2)}) collective-permute-start(bf16[2,128,1024]{2,1,0:T(8,128)(2,1)} %get-tuple-element.28), channel_id=1, source_target_pairs={{0,1},{1,2},{2,3},{3,4},{4,5},{5,6},{6,7},{7,8},{8,9},{9,10},{10,1... | collective-permute-start | bytes 1572872 | tf_op jit(solution)/shard_map/ppermute | solution.py:62
  16.2 21.9 %collective-permute-start.1 = (bf16[2,128,1024]{2,1,0:T(8,128)(2,1)}, bf16[2,128,1024]{2,1,0:T(8,128)(2,1)S(1)}, u32[]{:S(2)}, u32[]{:S(2)}) collective-permute-start(bf16[2,128,1024]{2,1,0:T(8,128)(2,1)} %get-tuple-element.28), channel_id=1, source_target_pairs={{1,0},{2,1},{3,2},{4,3},{5,4},{6,5},{7,6},{8,7},{9,8},{10,9},{11,1... | collective-permute-start | bytes 1572872 | tf_op jit(solution)/shard_map/ppermute | solution.py:63
  19.2 19.0 %copy-start.6 = (bf16[128,1024]{1,0:T(8,128)(2,1)S(1)}, bf16[128,1024]{1,0:T(8,128)(2,1)}, u32[]{:S(2)}) copy-start(bf16[128,1024]{1,0:T(8,128)(2,1)} %param.10) | copy-start | bytes 786436
  19.2 19.0 %copy-start.7 = (bf16[128,1024]{1,0:T(8,128)(2,1)S(1)}, bf16[128,1024]{1,0:T(8,128)(2,1)}, u32[]{:S(2)}) copy-start(bf16[128,1024]{1,0:T(8,128)(2,1)} %param.9) | copy-start | bytes 786436
  19.2 4.5 %collective-permute-start.2 = (bf16[8,32768]{1,0:T(8,128)(2,1)}, bf16[8,32768]{1,0:T(8,128)(2,1)S(1)}, u32[]{:S(2)}, u32[]{:S(2)}) collective-permute-start(bf16[8,32768]{1,0:T(8,128)(2,1)} %select_n.289), channel_id=1, source_target_pairs={{0,1},{1,0},{2,3},{3,2},{4,5},{5,4},{6,7},{7,6},{8,9},{9,8},{10,11... | collective-permute-start | bytes 1572872 | tf_op jit(solution)/shard_map/ppermute | solution.py:25
  24.1 15.3 %collective-permute-start.3 = (bf16[4,32768]{1,0:T(4,128)(2,1)S(1)}, bf16[4,32768]{1,0:T(4,128)(2,1)S(1)}, u32[]{:S(2)}, u32[]{:S(2)}) collective-permute-start(bf16[4,32768]{1,0:T(4,128)(2,1)S(1)} %broadcast_select_fusion.5), channel_id=1, source_target_pairs={{0,2},{2,0},{4,6},{6,4},{8,10},{10,8},{12,14},{14,12},{1,3},{3,1},... | collective-permute-start | bytes 786440 | tf_op jit(solution)/shard_map/ppermute | solution.py:28
  39.9 5.6 %collective-permute-start.4 = (bf16[2,32768]{1,0:T(2,128)(2,1)S(1)}, bf16[2,32768]{1,0:T(2,128)(2,1)S(1)}, u32[]{:S(2)}, u32[]{:S(2)}) collective-permute-start(bf16[2,32768]{1,0:T(2,128)(2,1)S(1)} %broadcast_select_fusion.6), channel_id=1, source_target_pairs={{0,4},{2,6},{4,0},{6,2},{8,12},{10,14},{12,8},{14,10},{1,5},{3,7},... | collective-permute-start | bytes 393224 | tf_op jit(solution)/shard_map/ppermute | solution.py:28
  45.9 4.8 %collective-permute-start.5 = (bf16[1,32768]{1,0:T(2,128)(2,1)S(1)}, bf16[1,32768]{1,0:T(2,128)(2,1)S(1)}, u32[]{:S(2)}, u32[]{:S(2)}) collective-permute-start(bf16[1,32768]{1,0:T(2,128)(2,1)S(1)} %broadcast_select_fusion.10), channel_id=1, source_target_pairs={{0,8},{2,10},{4,12},{6,14},{8,0},{10,2},{12,4},{14,6},{1,9},{3,11}... | collective-permute-start | bytes 196616 | tf_op jit(solution)/shard_map/ppermute | solution.py:28
  51.0 16.1 %collective-permute-start.6 = (bf16[1,32768]{1,0:T(2,128)(2,1)S(1)}, bf16[1,32768]{1,0:T(2,128)(2,1)S(1)}, u32[]{:S(2)}, u32[]{:S(2)}) collective-permute-start(bf16[1,32768]{1,0:T(2,128)(2,1)S(1)} %fusion.32), channel_id=1, source_target_pairs={{0,8},{2,10},{4,12},{6,14},{8,0},{10,2},{12,4},{14,6},{1,9},{3,11}... | collective-permute-start | bytes 196616 | tf_op jit(solution)/shard_map/ppermute | solution.py:28
  67.7 38.5 %copy-start.8 = (bf16[64,2048]{1,0:T(8,128)(2,1)S(1)}, bf16[64,2048]{1,0:T(8,128)(2,1)}, u32[]{:S(2)}) copy-start(bf16[64,2048]{1,0:T(8,128)(2,1)} %param.11) | copy-start | bytes 786436
  67.7 7.4 %collective-permute-start.7 = (bf16[2,32768]{1,0:T(2,128)(2,1)S(1)}, bf16[2,32768]{1,0:T(2,128)(2,1)S(1)}, u32[]{:S(2)}, u32[]{:S(2)}) collective-permute-start(bf16[2,32768]{1,0:T(2,128)(2,1)S(1)} %broadcast_select_fusion.13), channel_id=1, source_target_pairs={{0,4},{2,6},{4,0},{6,2},{8,12},{10,14},{12,8},{14,10},{1,5},{3,7},... | collective-permute-start | bytes 393224 | tf_op jit(solution)/shard_map/ppermute | solution.py:28
  75.6 28.5 %collective-permute-start.8 = (bf16[4,32768]{1,0:T(4,128)(2,1)S(1)}, bf16[4,32768]{1,0:T(4,128)(2,1)S(1)}, u32[]{:S(2)}, u32[]{:S(2)}) collective-permute-start(bf16[4,32768]{1,0:T(4,128)(2,1)S(1)} %maximum_select_fusion.4), channel_id=1, source_target_pairs={{0,2},{2,0},{4,6},{6,4},{8,10},{10,8},{12,14},{14,12},{1,3},{3,1},... | collective-permute-start | bytes 786440 | tf_op jit(solution)/shard_map/ppermute | solution.py:28
  98.5 5.6 %copy-start.5 = (bf16[1024,1024]{1,0:T(8,128)(2,1)}, bf16[1024,1024]{1,0:T(8,128)(2,1)S(1)}, u32[]{:S(2)}) copy-start(bf16[1024,1024]{1,0:T(8,128)(2,1)S(1)} %bitcast_dynamic-update-slice_fusion.5) | copy-start | bytes 6291460
  98.5 1.4 copy-start.4
  104.6 15.3 %collective-permute-start.9 = (bf16[8,32768]{1,0:T(8,128)(2,1)S(1)}, bf16[8,32768]{1,0:T(8,128)(2,1)S(1)}, u32[]{:S(2)}, u32[]{:S(2)}) collective-permute-start(bf16[8,32768]{1,0:T(8,128)(2,1)S(1)} %maximum_select_fusion.2), channel_id=1, source_target_pairs={{0,1},{1,0},{2,3},{3,2},{4,5},{5,4},{6,7},{7,6},{8,9},{9,8},{10,11... | collective-permute-start | bytes 1572872 | tf_op jit(solution)/shard_map/ppermute | solution.py:25
  113.0 16.8 %all-to-all-start = ((bf16[16,128,64]{1,2,0:T(8,128)(2,1)}), bf16[16,128,64]{1,2,0:T(8,128)(2,1)S(1)}, u32[]{:S(2)}, u32[]{:S(2)}) async-start(bf16[16,128,64]{1,2,0:T(8,128)(2,1)} %bitcast.145), calls=%async_computation | async-start | bytes 524288 | tf_op jit(solution)/shard_map/all_to_all | solution.py:151
  146.3 2.8 %copy-start.2 = (f32[1024,1024]{1,0:T(8,128)S(1)}, f32[1024,1024]{1,0:T(8,128)}, u32[]{:S(2)}) copy-start(f32[1024,1024]{1,0:T(8,128)} %get-tuple-element.11) | copy-start | bytes 12582916
  147.3 1.8 copy-start.10
  153.4 5.0 %collective-permute-start.12 = (bf16[8,32768]{1,0:T(8,128)(2,1)}, bf16[8,32768]{1,0:T(8,128)(2,1)}, u32[]{:S(2)}, u32[]{:S(2)}) collective-permute-start(bf16[8,32768]{1,0:T(8,128)(2,1)} %convert_element_type.108), channel_id=1, source_target_pairs={{0,1},{1,0},{2,3},{3,2},{4,5},{5,4},{6,7},{7,6},{8,9},{9,8},{10,11... | collective-permute-start | bytes 1572872 | tf_op jit(solution)/shard_map/ppermute | solution.py:25
  156.0 2.5 %copy-start.3 = (f32[8,32768]{1,0:T(8,128)S(1)}, f32[8,32768]{1,0:T(8,128)}, u32[]{:S(2)}) copy-start(f32[8,32768]{1,0:T(8,128)} %select_n.304) | copy-start | bytes 3145732
  159.8 8.0 %collective-permute-start.13 = (bf16[4,32768]{1,0:T(4,128)(2,1)S(1)}, bf16[4,32768]{1,0:T(4,128)(2,1)S(1)}, u32[]{:S(2)}, u32[]{:S(2)}) collective-permute-start(bf16[4,32768]{1,0:T(4,128)(2,1)S(1)} %select_convert_fusion.1), channel_id=1, source_target_pairs={{0,2},{2,0},{4,6},{6,4},{8,10},{10,8},{12,14},{14,12},{1,3},{3,1},... | collective-permute-start | bytes 786440 | tf_op jit(solution)/shard_map/ppermute | solution.py:28
  168.2 3.9 %collective-permute-start.14 = (bf16[2,32768]{1,0:T(2,128)(2,1)S(1)}, bf16[2,32768]{1,0:T(2,128)(2,1)S(1)}, u32[]{:S(2)}, u32[]{:S(2)}) collective-permute-start(bf16[2,32768]{1,0:T(2,128)(2,1)S(1)} %select_convert_fusion.2), channel_id=1, source_target_pairs={{0,4},{2,6},{4,0},{6,2},{8,12},{10,14},{12,8},{14,10},{1,5},{3,7},... | collective-permute-start | bytes 393224 | tf_op jit(solution)/shard_map/ppermute | solution.py:28
  170.8 10.3 %copy-start.1 = (f32[1,384,1024]{2,1,0:T(8,128)}, f32[1,384,1024]{2,1,0:T(8,128)S(1)}, u32[]{:S(2)}) copy-start(f32[1,384,1024]{2,1,0:T(8,128)S(1)} %bitcast_dynamic-update-slice_fusion.1) | copy-start | bytes 4718596
  172.5 4.9 %collective-permute-start.15 = (bf16[1,32768]{1,0:T(2,128)(2,1)S(1)}, bf16[1,32768]{1,0:T(2,128)(2,1)S(1)}, u32[]{:S(2)}, u32[]{:S(2)}) collective-permute-start(bf16[1,32768]{1,0:T(2,128)(2,1)S(1)} %fusion.35), channel_id=1, source_target_pairs={{0,8},{2,10},{4,12},{6,14},{8,0},{10,2},{12,4},{14,6},{1,9},{3,11}... | collective-permute-start | bytes 196616 | tf_op jit(solution)/shard_map/ppermute | solution.py:28
  175.1 5.9 %copy-start = (f32[1,384,1024]{2,1,0:T(8,128)}, f32[1,384,1024]{2,1,0:T(8,128)S(1)}, u32[]{:S(2)}) copy-start(f32[1,384,1024]{2,1,0:T(8,128)S(1)} %bitcast_dynamic-update-slice_fusion) | copy-start | bytes 4718596
  177.6 6.6 %collective-permute-start.16 = (bf16[1,32768]{1,0:T(2,128)(2,1)S(1)}, bf16[1,32768]{1,0:T(2,128)(2,1)S(1)}, u32[]{:S(2)}, u32[]{:S(2)}) collective-permute-start(bf16[1,32768]{1,0:T(2,128)(2,1)S(1)} %fusion.34), channel_id=1, source_target_pairs={{0,8},{2,10},{4,12},{6,14},{8,0},{10,2},{12,4},{14,6},{1,9},{3,11}... | collective-permute-start | bytes 196616 | tf_op jit(solution)/shard_map/ppermute | solution.py:28
  181.1 16.1 %copy-start.9 = (bf16[128,1024]{1,0:T(8,128)(2,1)S(1)}, bf16[128,1024]{1,0:T(8,128)(2,1)}, u32[]{:S(2)}) copy-start(bf16[128,1024]{1,0:T(8,128)(2,1)} %get-tuple-element.9) | copy-start | bytes 786436
  184.8 18.3 %collective-permute-start.17 = (bf16[2,32768]{1,0:T(2,128)(2,1)S(1)}, bf16[2,32768]{1,0:T(2,128)(2,1)S(1)}, u32[]{:S(2)}, u32[]{:S(2)}) collective-permute-start(bf16[2,32768]{1,0:T(2,128)(2,1)S(1)} %broadcast_select_fusion.12), channel_id=1, source_target_pairs={{0,4},{2,6},{4,0},{6,2},{8,12},{10,14},{12,8},{14,10},{1,5},{3,7},... | collective-permute-start | bytes 393224 | tf_op jit(solution)/shard_map/ppermute | solution.py:28
  189.3 45.5 %collective-permute-start.10 = (bf16[2,256,1024]{2,1,0:T(8,128)(2,1)S(1)}, bf16[2,256,1024]{2,1,0:T(8,128)(2,1)}, u32[]{:S(2)}, u32[]{:S(2)}) collective-permute-start(bf16[2,256,1024]{2,1,0:T(8,128)(2,1)S(1)} %pad_maximum_fusion.3), channel_id=1, source_target_pairs={{0,1},{1,2},{2,3},{3,4},{4,5},{5,6},{6,7},{7,8},{8,9},{9,10},{10,1... | collective-permute-start | bytes 3145736 | tf_op jit(solution)/shard_map/ppermute | solution.py:62
  195.3 39.6 %collective-permute-start.11 = (bf16[2,256,1024]{2,1,0:T(8,128)(2,1)S(1)}, bf16[2,256,1024]{2,1,0:T(8,128)(2,1)}, u32[]{:S(2)}, u32[]{:S(2)}) collective-permute-start(bf16[2,256,1024]{2,1,0:T(8,128)(2,1)S(1)} %pad_maximum_fusion.3), channel_id=1, source_target_pairs={{1,0},{2,1},{3,2},{4,3},{5,4},{6,5},{7,6},{8,7},{9,8},{10,9},{11,1... | collective-permute-start | bytes 3145736 | tf_op jit(solution)/shard_map/ppermute | solution.py:63
  198.0 26.4 %all-to-all-start.1 = ((bf16[1,128,16,64]{1,3,0,2:T(8,128)(2,1)}), bf16[1,128,16,64]{1,3,0,2:T(8,128)(2,1)S(1)}, u32[]{:S(2)}, u32[]{:S(2)}) async-start(bf16[1,128,16,64]{1,3,0,2:T(8,128)(2,1)} %bitcast.39), calls=%async_computation.1 | async-start | bytes 524288 | tf_op jit(solution)/shard_map/all_to_all | solution.py:195
  203.6 23.1 %collective-permute-start.18 = (bf16[4,32768]{1,0:T(4,128)(2,1)S(1)}, bf16[4,32768]{1,0:T(4,128)(2,1)S(1)}, u32[]{:S(2)}, u32[]{:S(2)}) collective-permute-start(bf16[4,32768]{1,0:T(4,128)(2,1)S(1)} %maximum_select_fusion.5), channel_id=1, source_target_pairs={{0,2},{2,0},{4,6},{6,4},{8,10},{10,8},{12,14},{14,12},{1,3},{3,1},... | collective-permute-start | bytes 786440 | tf_op jit(solution)/shard_map/ppermute | solution.py:28
  227.1 7.0 %collective-permute-start.19 = (bf16[8,32768]{1,0:T(8,128)(2,1)S(1)}, bf16[8,32768]{1,0:T(8,128)(2,1)S(1)}, u32[]{:S(2)}, u32[]{:S(2)}) collective-permute-start(bf16[8,32768]{1,0:T(8,128)(2,1)S(1)} %maximum_select_fusion.3), channel_id=1, source_target_pairs={{0,1},{1,0},{2,3},{3,2},{4,5},{5,4},{6,7},{7,6},{8,9},{9,8},{10,11... | collective-permute-start | bytes 1572872 | tf_op jit(solution)/shard_map/ppermute | solution.py:25
Sparse Core Ops, SparseCore 0:
  10.2 85.8 all-gather.2
  98.2 59.8 all-gather.4

commit v11 on v10

--- a/solution.py
+++ b/solution.py
@@ -28,13 +28,11 @@
     return lax.ppermute(x, "chip", [(i, i ^ m) for i in range(n)])
 
 
-def butterfly_sum(x, wire=None):
+def butterfly_halves(x, wire=None):
     count = lax.axis_size("chip") * lax.axis_size("core")
     levels = count.bit_length() - 1
-    shape = x.shape
-    flat = x.reshape(count, -1)
     d = flat_index()
-    parts = flat
+    parts = x.reshape(count, -1)
     for k in range(levels):
         half = parts.shape[0] // 2
         lo, hi = parts[:half], parts[half:]
@@ -44,15 +42,26 @@
         if wire is not None:
             send = send.astype(wire)
         parts = keep + xor_swap(send, k).astype(keep.dtype)
+    if wire is not None:
+        parts = parts.astype(wire)
+    return parts
+
+
+def butterfly_doubling(parts, shape):
+    count = lax.axis_size("chip") * lax.axis_size("core")
+    levels = count.bit_length() - 1
+    d = flat_index()
     for k in reversed(range(levels)):
         upper = ((d >> k) & 1) == 1
-        if wire is not None and k == levels - 1:
-            parts = parts.astype(wire)
         other = xor_swap(parts, k)
         parts = jnp.where(
             upper, jnp.concatenate([other, parts]), jnp.concatenate([parts, other])
         )
     return parts.reshape(shape)
+
+
+def butterfly_sum(x, wire=None):
+    return butterfly_doubling(butterfly_halves(x, wire), x.shape)
 
 
 def halo(shard):
@@ -186,15 +195,17 @@
         )
         global_local = terms if global_local is None else global_local + terms
     grad_ext = jnp.stack(grad_ext)
-    global_total = butterfly_sum(global_local, jnp.bfloat16)
-
     attn_out = jnp.concatenate(attn_rows, axis=0)
-    layer_out = jnp.dot(attn_out, weight_all, preferred_element_type=jnp.float32).astype(
-        jnp.bfloat16
-    )
     attn_cols = lax.all_to_all(
         attn_out.reshape(tok_rows, count, w_rows), SEQ, 1, 0, tiled=False
     ).reshape(count * tok_rows, w_rows)
+    halves = butterfly_halves(global_local, jnp.bfloat16)
+    attn_cols, halves = lax.optimization_barrier((attn_cols, halves))
+    global_total = butterfly_doubling(halves, global_local.shape)
+
+    layer_out = jnp.dot(attn_out, weight_all, preferred_element_type=jnp.float32).astype(
+        jnp.bfloat16
+    )
     grad_weight = lax.dot_general(
         attn_cols, grad_out_all, (((0,), (0,)), ((), ())), preferred_element_type=jnp.float32
     )

time: 247 us -> 257 us (1.040)
  other arithmetic: 23.6 us -> 30.9 us
  local copies, waits for them, and re-layouts: 19.1 us -> 23 us
  waiting for transfers between devices: 83.5 us -> 87.1 us
  starting transfers between devices: 72.7 us -> 69.5 us
    ppermute x12, waiting for transfers between devices: 45.6 us -> 65.1 us  [xor_swap(): return lax.ppermute(x, 'chip', [(i, i ^ m) for i in range(n)])]
    all_to_all x1, waiting for transfers between devices: 15.9 us -> 0.01 us  [local(): lax.all_to_all(attn_out.reshape(tok_rows, count, w_rows), SEQ, 1, 0, tile...]
    ppermute x2, starting transfers between devices: 9.62 us -> 6.88 us  [halo(): before = lax.ppermute(shard, SEQ, up)]
    unnamed x38 -> x41, local copies, waits for them, and re-layouts: 3.46 us -> 5.63 us
  transfers between devices with their start and end apart: 24 -> 24, of which waited for: 15 -> 13; matrix products, arithmetic and copies ran while one was open for 22% -> 25% of each run, Pallas kernels for 5% -> 5%
where the time goes in v11:
time: 257 us; the launch traced here: 256 us
  waiting for transfers between devices  87.1 us (34%)
  starting transfers between devices  69.5 us (27%)
  other arithmetic  30.9 us (12%)
  local copies, waits for them, and re-layouts  23 us (9%)
  between operations  17.8 us (7%)
  matrix products  15.5 us (6%)
  Pallas kernels  12.3 us (5%)
    ppermute x12, waiting for transfers between devices, xor_swap(): return lax.ppermute(x, 'chip', [(i, i ^ m) for i in range(n)])  65.1 us
    ppermute x12, starting transfers between devices, xor_swap(): return lax.ppermute(x, 'chip', [(i, i ^ m) for i in range(n)])  40.8 us
    pallas_call x1, Pallas kernels, attention(): pl.pallas_call(_attn_kernel, grid=(heads,), in_specs=[pl.BlockSpec((1, ke...  12.3 us
    dynamic_update_slice x11, other arithmetic, local(): lax.dynamic_update_slice_in_dim(grad_ext[side], cur + term, start, axis=0)  10.8 us
    ppermute x2, waiting for transfers between devices, halo(): after = lax.ppermute(shard, SEQ, down)  9.58 us
    all_to_all x1, waiting for transfers between devices, local(): lax.all_to_all(upstream_cols.reshape(count, tok_rows, w_rows), SEQ, 0, 0,...  7.6 us
    ppermute x2, starting transfers between devices, halo(): before = lax.ppermute(shard, SEQ, up)  6.88 us
    all_to_all x1, starting transfers between devices, local(): lax.all_to_all(upstream_cols.reshape(count, tok_rows, w_rows), SEQ, 0, 0,...  6.82 us
  transfers between devices with their start and end apart: 24, of which 13 were waited for; matrix products, arithmetic and copies ran while one was open for 25% of the time, Pallas kernels for 5%

profile of v11, /device:TPU:11, one launch (start us, length us, event | category | flops | bytes accessed | tf_op | source)
XLA Modules:
  0.0 256.0 jit_solution(4373084761539746279)
XLA Ops:
  8.0 1.3 fusion.37
  10.6 1.9 broadcast_select_fusion.3
  12.5 3.7 %collective-permute-start = (bf16[2,128,1024]{2,1,0:T(8,128)(2,1)}, bf16[2,128,1024]{2,1,0:T(8,128)(2,1)S(1)}, u32[]{:S(2)}, u32[]{:S(2)}) collective-permute-start(bf16[2,128,1024]{2,1,0:T(8,128)(2,1)} %get-tuple-element.32), channel_id=1, source_target_pairs={{0,1},{1,2},{2,3},{3,4},{4,5},{5,6},{6,7},{7,8},{8,9},{9,10},{10,1... | collective-permute-start | bytes 1572872 | tf_op jit(solution)/shard_map/ppermute | solution.py:71
  16.2 1.9 collective-permute-start.1
  19.2 1.5 collective-permute-start.2
  24.5 4.1 %collective-permute-done = bf16[2,128,1024]{2,1,0:T(8,128)(2,1)S(1)} collective-permute-done((bf16[2,128,1024]{2,1,0:T(8,128)(2,1)}, bf16[2,128,1024]{2,1,0:T(8,128)(2,1)S(1)}, u32[]{:S(2)}, u32[]{:S(2)}) %collective-permute-start) | collective-permute-done | bytes 524320 | tf_op jit(solution)/shard_map/ppermute | solution.py:71
  28.6 9.6 %collective-permute-done.1 = bf16[2,128,1024]{2,1,0:T(8,128)(2,1)S(1)} collective-permute-done((bf16[2,128,1024]{2,1,0:T(8,128)(2,1)}, bf16[2,128,1024]{2,1,0:T(8,128)(2,1)S(1)}, u32[]{:S(2)}, u32[]{:S(2)}) %collective-permute-start.1) | collective-permute-done | bytes 524320 | tf_op jit(solution)/shard_map/ppermute | solution.py:72
  40.2 5.2 %collective-permute-done.4 = bf16[2,32768]{1,0:T(2,128)(2,1)S(1)} collective-permute-done((bf16[2,32768]{1,0:T(2,128)(2,1)S(1)}, bf16[2,32768]{1,0:T(2,128)(2,1)S(1)}, u32[]{:S(2)}, u32[]{:S(2)}) %collective-permute-start.4) | collective-permute-done | bytes 131104 | tf_op jit(solution)/shard_map/ppermute | solution.py:28
  45.9 1.9 collective-permute-start.5
  47.8 2.9 %collective-permute-done.5 = bf16[1,32768]{1,0:T(2,128)(2,1)S(1)} collective-permute-done((bf16[1,32768]{1,0:T(2,128)(2,1)S(1)}, bf16[1,32768]{1,0:T(2,128)(2,1)S(1)}, u32[]{:S(2)}, u32[]{:S(2)}) %collective-permute-start.5) | collective-permute-done | bytes 65568 | tf_op jit(solution)/shard_map/ppermute | solution.py:28
  51.0 1.8 collective-permute-start.6
  52.9 14.2 %collective-permute-done.6 = bf16[1,32768]{1,0:T(2,128)(2,1)S(1)} collective-permute-done((bf16[1,32768]{1,0:T(2,128)(2,1)S(1)}, bf16[1,32768]{1,0:T(2,128)(2,1)S(1)}, u32[]{:S(2)}, u32[]{:S(2)}) %collective-permute-start.6) | collective-permute-done | bytes 65568 | tf_op jit(solution)/shard_map/ppermute | solution.py:28
  67.7 1.9 collective-permute-start.7
  69.6 5.5 %collective-permute-done.7 = bf16[2,32768]{1,0:T(2,128)(2,1)S(1)} collective-permute-done((bf16[2,32768]{1,0:T(2,128)(2,1)S(1)}, bf16[2,32768]{1,0:T(2,128)(2,1)S(1)}, u32[]{:S(2)}, u32[]{:S(2)}) %collective-permute-start.7) | collective-permute-done | bytes 131104 | tf_op jit(solution)/shard_map/ppermute | solution.py:28
  75.6 22.8 %collective-permute-start.8 = (bf16[4,32768]{1,0:T(4,128)(2,1)S(1)}, bf16[4,32768]{1,0:T(4,128)(2,1)S(1)}, u32[]{:S(2)}, u32[]{:S(2)}) collective-permute-start(bf16[4,32768]{1,0:T(4,128)(2,1)S(1)} %maximum_select_fusion.4), channel_id=1, source_target_pairs={{0,2},{2,0},{4,6},{6,4},{8,10},{10,8},{12,14},{14,12},{1,3},{3,1},... | collective-permute-start | bytes 786440 | tf_op jit(solution)/shard_map/ppermute | solution.py:28
  98.5 1.4 copy-done.4
  99.9 4.2 %collective-permute-done.8 = bf16[4,32768]{1,0:T(4,128)(2,1)S(1)} collective-permute-done((bf16[4,32768]{1,0:T(4,128)(2,1)S(1)}, bf16[4,32768]{1,0:T(4,128)(2,1)S(1)}, u32[]{:S(2)}, u32[]{:S(2)}) %collective-permute-start.8) | collective-permute-done | bytes 262176 | tf_op jit(solution)/shard_map/ppermute | solution.py:28
  104.6 1.6 collective-permute-start.9
  106.2 6.0 %fusion = bf16[8,16,8,128]{3,2,1,0:T(8,128)(2,1)S(1)} fusion(bf16[2048,2048]{1,0:T(8,128)(2,1)} %all-gather.3.cloned.1.call-done, bf16[64,2048]{1,0:T(8,128)(2,1)S(1)} %copy-done.8), kind=kOutput, calls=%fused_computation.7 | convolution fusion | flops 537001984 | bytes 8912896 | tf_op jit(solution)/shard_map/dot_general | solution.py:157
  113.0 6.8 %all-to-all-start = ((bf16[16,128,64]{1,2,0:T(8,128)(2,1)}), bf16[16,128,64]{1,2,0:T(8,128)(2,1)S(1)}, u32[]{:S(2)}, u32[]{:S(2)}) async-start(bf16[16,128,64]{1,2,0:T(8,128)(2,1)} %bitcast.146), calls=%async_computation | async-start | bytes 524288 | tf_op jit(solution)/shard_map/all_to_all | solution.py:160
  122.3 7.6 %all-to-all-done = bf16[16,128,64]{1,2,0:T(8,128)(2,1)S(1)} async-done(((bf16[16,128,64]{1,2,0:T(8,128)(2,1)}), bf16[16,128,64]{1,2,0:T(8,128)(2,1)S(1)}, u32[]{:S(2)}, u32[]{:S(2)}) %all-to-all-start) | async-done | bytes 262176 | tf_op jit(solution)/shard_map/all_to_all | solution.py:160
  131.4 12.3 %shard_map.119 = (bf16[128,1024]{1,0:T(8,128)(2,1)}, bf16[128,1024]{1,0:T(8,128)(2,1)}, f32[1024,1024]{1,0:T(8,128)}, f32[1024,1024]{1,0:T(8,128)}) custom-call(f32[1,1024]{1,0:T(1,128)} %bitcast.161, bf16[128,1024]{1,0:T(8,128)(2,1)} %q_ref.1, bf16[1024,1024]{1,0:T(8,128)(2,1)} %get-tuple-element.24.k_ref, bf16[1024,1024]{1,0:T(8,128)(2,1)} %get-tuple-element.23.v_ref, ...), custom_call_target="tpu_custom_call" | custom-call | tf_op jit(solution)/shard_map/pallas_call | solution.py:104
  143.7 1.3 slice.245
  145.0 1.3 slice.246
  149.1 1.7 slice_select_fusion
  151.3 2.1 convert_element_type.108
  153.6 2.4 select_n.304
  156.0 1.3 fusion.9
  160.6 1.6 collective-permute-start.13
  167.7 4.7 %all-to-all-start.1 = ((bf16[1,128,16,64]{1,3,0,2:T(8,128)(2,1)}), bf16[1,128,16,64]{1,3,0,2:T(8,128)(2,1)}, u32[]{:S(2)}, u32[]{:S(2)}) async-start(bf16[1,128,16,64]{1,3,0,2:T(8,128)(2,1)} %bitcast.158), calls=%async_computation.1 | async-start | bytes 524288 | tf_op jit(solution)/shard_map/all_to_all | solution.py:199
  172.4 2.0 convert_add_fusion.1
  174.7 1.9 bitcast_dynamic-update-slice_fusion.1
  176.6 4.0 %collective-permute-done.14 = bf16[2,32768]{1,0:T(2,128)(2,1)S(1)} collective-permute-done((bf16[2,32768]{1,0:T(2,128)(2,1)S(1)}, bf16[2,32768]{1,0:T(2,128)(2,1)S(1)}, u32[]{:S(2)}, u32[]{:S(2)}) %collective-permute-start.14) | collective-permute-done | bytes 131104 | tf_op jit(solution)/shard_map/ppermute | solution.py:28
  181.7 2.9 %collective-permute-start.15 = (bf16[1,32768]{1,0:T(2,128)(2,1)}, bf16[1,32768]{1,0:T(2,128)(2,1)S(1)}, u32[]{:S(2)}, u32[]{:S(2)}) collective-permute-start(bf16[1,32768]{1,0:T(2,128)(2,1)} %fusion.32), channel_id=1, source_target_pairs={{0,8},{2,10},{4,12},{6,14},{8,0},{10,2},{12,4},{14,6},{1,9},{3,11}... | collective-permute-start | bytes 196616 | tf_op jit(solution)/shard_map/ppermute | solution.py:28
  184.6 1.9 bitcast_dynamic-update-slice_fusion
  187.7 3.1 %collective-permute-done.15 = bf16[1,32768]{1,0:T(2,128)(2,1)S(1)} collective-permute-done((bf16[1,32768]{1,0:T(2,128)(2,1)}, bf16[1,32768]{1,0:T(2,128)(2,1)S(1)}, u32[]{:S(2)}, u32[]{:S(2)}) %collective-permute-start.15) | collective-permute-done | bytes 65568 | tf_op jit(solution)/shard_map/ppermute | solution.py:28
  191.0 3.1 %collective-permute-start.16 = (bf16[1,32768]{1,0:T(2,128)(2,1)S(1)}, bf16[1,32768]{1,0:T(2,128)(2,1)S(1)}, u32[]{:S(2)}, u32[]{:S(2)}) collective-permute-start(bf16[1,32768]{1,0:T(2,128)(2,1)S(1)} %fusion.31), channel_id=1, source_target_pairs={{0,8},{2,10},{4,12},{6,14},{8,0},{10,2},{12,4},{14,6},{1,9},{3,11}... | collective-permute-start | bytes 196616 | tf_op jit(solution)/shard_map/ppermute | solution.py:28
  194.1 1.3 maximum_convert_fusion
  195.4 3.1 %collective-permute-done.16 = bf16[1,32768]{1,0:T(2,128)(2,1)S(1)} collective-permute-done((bf16[1,32768]{1,0:T(2,128)(2,1)S(1)}, bf16[1,32768]{1,0:T(2,128)(2,1)S(1)}, u32[]{:S(2)}, u32[]{:S(2)}) %collective-permute-start.16) | collective-permute-done | bytes 65568 | tf_op jit(solution)/shard_map/ppermute | solution.py:28
  199.1 3.3 %collective-permute-start.17 = (bf16[2,32768]{1,0:T(2,128)(2,1)S(1)}, bf16[2,32768]{1,0:T(2,128)(2,1)S(1)}, u32[]{:S(2)}, u32[]{:S(2)}) collective-permute-start(bf16[2,32768]{1,0:T(2,128)(2,1)S(1)} %broadcast_select_fusion.12), channel_id=1, source_target_pairs={{0,4},{2,6},{4,0},{6,2},{8,12},{10,14},{12,8},{14,10},{1,5},{3,7},... | collective-permute-start | bytes 393224 | tf_op jit(solution)/shard_map/ppermute | solution.py:28
  203.5 3.2 %collective-permute-start.10 = (bf16[2,256,1024]{2,1,0:T(8,128)(2,1)}, bf16[2,256,1024]{2,1,0:T(8,128)(2,1)}, u32[]{:S(2)}, u32[]{:S(2)}) collective-permute-start(bf16[2,256,1024]{2,1,0:T(8,128)(2,1)} %pad_maximum_fusion.3), channel_id=1, source_target_pairs={{0,1},{1,2},{2,3},{3,4},{4,5},{5,6},{6,7},{7,8},{8,9},{9,10},{10,1... | collective-permute-start | bytes 3145736 | tf_op jit(solution)/shard_map/ppermute | solution.py:71
  206.7 1.9 collective-permute-start.11
  209.9 3.7 %convolution_convert_fusion = bf16[128,2048]{1,0:T(8,128)(2,1)} fusion(bf16[128,1024]{1,0:T(8,128)(2,1)S(1)} %copy-done.10, bf16[1024,2048]{1,0:T(8,128)(2,1)} %all-gather.5.cloned.1.call-done), kind=kOutput, calls=%fused_computation | convolution fusion | flops 537133056 | bytes 4980736 | tf_op jit(solution)/shard_map/dot_general | solution.py:206
  213.6 21.9 %collective-permute-done.18 = bf16[4,32768]{1,0:T(4,128)(2,1)S(1)} collective-permute-done((bf16[4,32768]{1,0:T(4,128)(2,1)S(1)}, bf16[4,32768]{1,0:T(4,128)(2,1)S(1)}, u32[]{:S(2)}, u32[]{:S(2)}) %collective-permute-start.18) | collective-permute-done | bytes 262176 | tf_op jit(solution)/shard_map/ppermute | solution.py:28
  235.9 3.1 %collective-permute-start.19 = (bf16[8,32768]{1,0:T(8,128)(2,1)S(1)}, bf16[8,32768]{1,0:T(8,128)(2,1)S(1)}, u32[]{:S(2)}, u32[]{:S(2)}) collective-permute-start(bf16[8,32768]{1,0:T(8,128)(2,1)S(1)} %maximum_select_fusion.3), channel_id=1, source_target_pairs={{0,1},{1,0},{2,3},{3,2},{4,5},{5,4},{6,7},{7,6},{8,9},{9,8},{10,11... | collective-permute-start | bytes 1572872 | tf_op jit(solution)/shard_map/ppermute | solution.py:25
  239.0 5.7 %fusion.39 = f32[64,2048]{1,0:T(8,128)} fusion(bf16[2048,64]{0,1:T(8,128)(2,1)S(1)} %bitcast.157, bf16[2048,2048]{1,0:T(8,128)(2,1)} %all-gather.3.cloned.1.call-done), kind=kOutput, calls=%fused_computation.116 | convolution fusion | flops 536870912 | bytes 9175040 | tf_op jit(solution)/shard_map/dot_general | solution.py:209
  244.9 1.3 select_n.316
  246.2 2.9 %fusion.7 = (bf16[128,1024]{1,0:T(8,128)(2,1)}, bf16[128,1024]{1,0:T(8,128)(2,1)}) fusion(f32[1,384,1024]{2,1,0:T(8,128)} %bitcast_dynamic-update-slice_fusion, bf16[2,2,128,1024]{3,2,1,0:T(8,128)(2,1)} %select_n.316, bf16[2,256,1024]{2,1,0:T(8,128)(2,1)} %collective-permute-done.11, bf16[2,256,1024]{2,1,0:T(8,128)(2,1)} %collective-permute-done.10, ...), kind=kLoop, calls=%fused_computation.23 | loop fusion | flops 2883584 | bytes 3670018 | tf_op jit(solution)/shard_map/convert_element_type | solution.py:228
  (109 shorter events, 31.3 us)
Async XLA Ops:
  7.2 13.6 %copy-start.12 = (s32[1,3]{1,0:T(1,128)S(1)}, s32[1,3]{1,0:T(1,128)}, u32[]{:S(2)}) copy-start(s32[1,3]{1,0:T(1,128)} %param.14) | copy-start | bytes 40
  7.2 99.0 %all-gather.3.cloned.1.call-start = ((), (), s32[]{:S(2)}) async-start(), calls=%async_computation.2 | async-start | bytes 8912896 | tf_op jit(solution)/shard_map/all_gather | solution.py:126
  7.9 201.9 %all-gather.5.cloned.1.call-start = ((), (), s32[]{:S(2)}) async-start(), calls=%async_computation.3 | async-start | bytes 4456448 | tf_op jit(solution)/shard_map/all_gather | solution.py:127
  10.6 13.0 %copy-start.13 = (s32[3]{0:T(128)S(1)}, s32[3]{0:T(128)}, u32[]{:S(2)}) copy-start(s32[3]{0:T(128)} %constant.85.clone) | copy-start | bytes 40
  12.5 16.0 %collective-permute-start = (bf16[2,128,1024]{2,1,0:T(8,128)(2,1)}, bf16[2,128,1024]{2,1,0:T(8,128)(2,1)S(1)}, u32[]{:S(2)}, u32[]{:S(2)}) collective-permute-start(bf16[2,128,1024]{2,1,0:T(8,128)(2,1)} %get-tuple-element.32), channel_id=1, source_target_pairs={{0,1},{1,2},{2,3},{3,4},{4,5},{5,6},{6,7},{7,8},{8,9},{9,10},{10,1... | collective-permute-start | bytes 1572872 | tf_op jit(solution)/shard_map/ppermute | solution.py:71
  16.2 21.9 %collective-permute-start.1 = (bf16[2,128,1024]{2,1,0:T(8,128)(2,1)}, bf16[2,128,1024]{2,1,0:T(8,128)(2,1)S(1)}, u32[]{:S(2)}, u32[]{:S(2)}) collective-permute-start(bf16[2,128,1024]{2,1,0:T(8,128)(2,1)} %get-tuple-element.32), channel_id=1, source_target_pairs={{1,0},{2,1},{3,2},{4,3},{5,4},{6,5},{7,6},{8,7},{9,8},{10,9},{11,1... | collective-permute-start | bytes 1572872 | tf_op jit(solution)/shard_map/ppermute | solution.py:72
  19.2 19.0 %copy-start.6 = (bf16[128,1024]{1,0:T(8,128)(2,1)S(1)}, bf16[128,1024]{1,0:T(8,128)(2,1)}, u32[]{:S(2)}) copy-start(bf16[128,1024]{1,0:T(8,128)(2,1)} %param.10) | copy-start | bytes 786436
  19.2 19.0 %copy-start.7 = (bf16[128,1024]{1,0:T(8,128)(2,1)S(1)}, bf16[128,1024]{1,0:T(8,128)(2,1)}, u32[]{:S(2)}) copy-start(bf16[128,1024]{1,0:T(8,128)(2,1)} %param.9) | copy-start | bytes 786436
  19.2 4.5 %collective-permute-start.2 = (bf16[8,32768]{1,0:T(8,128)(2,1)}, bf16[8,32768]{1,0:T(8,128)(2,1)S(1)}, u32[]{:S(2)}, u32[]{:S(2)}) collective-permute-start(bf16[8,32768]{1,0:T(8,128)(2,1)} %select_n.289), channel_id=1, source_target_pairs={{0,1},{1,0},{2,3},{3,2},{4,5},{5,4},{6,7},{7,6},{8,9},{9,8},{10,11... | collective-permute-start | bytes 1572872 | tf_op jit(solution)/shard_map/ppermute | solution.py:25
  24.1 15.3 %collective-permute-start.3 = (bf16[4,32768]{1,0:T(4,128)(2,1)S(1)}, bf16[4,32768]{1,0:T(4,128)(2,1)S(1)}, u32[]{:S(2)}, u32[]{:S(2)}) collective-permute-start(bf16[4,32768]{1,0:T(4,128)(2,1)S(1)} %broadcast_select_fusion.5), channel_id=1, source_target_pairs={{0,2},{2,0},{4,6},{6,4},{8,10},{10,8},{12,14},{14,12},{1,3},{3,1},... | collective-permute-start | bytes 786440 | tf_op jit(solution)/shard_map/ppermute | solution.py:28
  39.9 5.6 %collective-permute-start.4 = (bf16[2,32768]{1,0:T(2,128)(2,1)S(1)}, bf16[2,32768]{1,0:T(2,128)(2,1)S(1)}, u32[]{:S(2)}, u32[]{:S(2)}) collective-permute-start(bf16[2,32768]{1,0:T(2,128)(2,1)S(1)} %broadcast_select_fusion.6), channel_id=1, source_target_pairs={{0,4},{2,6},{4,0},{6,2},{8,12},{10,14},{12,8},{14,10},{1,5},{3,7},... | collective-permute-start | bytes 393224 | tf_op jit(solution)/shard_map/ppermute | solution.py:28
  45.9 4.8 %collective-permute-start.5 = (bf16[1,32768]{1,0:T(2,128)(2,1)S(1)}, bf16[1,32768]{1,0:T(2,128)(2,1)S(1)}, u32[]{:S(2)}, u32[]{:S(2)}) collective-permute-start(bf16[1,32768]{1,0:T(2,128)(2,1)S(1)} %broadcast_select_fusion.10), channel_id=1, source_target_pairs={{0,8},{2,10},{4,12},{6,14},{8,0},{10,2},{12,4},{14,6},{1,9},{3,11}... | collective-permute-start | bytes 196616 | tf_op jit(solution)/shard_map/ppermute | solution.py:28
  51.0 16.1 %collective-permute-start.6 = (bf16[1,32768]{1,0:T(2,128)(2,1)S(1)}, bf16[1,32768]{1,0:T(2,128)(2,1)S(1)}, u32[]{:S(2)}, u32[]{:S(2)}) collective-permute-start(bf16[1,32768]{1,0:T(2,128)(2,1)S(1)} %fusion.29), channel_id=1, source_target_pairs={{0,8},{2,10},{4,12},{6,14},{8,0},{10,2},{12,4},{14,6},{1,9},{3,11}... | collective-permute-start | bytes 196616 | tf_op jit(solution)/shard_map/ppermute | solution.py:28
  67.7 38.5 %copy-start.8 = (bf16[64,2048]{1,0:T(8,128)(2,1)S(1)}, bf16[64,2048]{1,0:T(8,128)(2,1)}, u32[]{:S(2)}) copy-start(bf16[64,2048]{1,0:T(8,128)(2,1)} %param.11) | copy-start | bytes 786436
  67.7 7.4 %collective-permute-start.7 = (bf16[2,32768]{1,0:T(2,128)(2,1)S(1)}, bf16[2,32768]{1,0:T(2,128)(2,1)S(1)}, u32[]{:S(2)}, u32[]{:S(2)}) collective-permute-start(bf16[2,32768]{1,0:T(2,128)(2,1)S(1)} %broadcast_select_fusion.13), channel_id=1, source_target_pairs={{0,4},{2,6},{4,0},{6,2},{8,12},{10,14},{12,8},{14,10},{1,5},{3,7},... | collective-permute-start | bytes 393224 | tf_op jit(solution)/shard_map/ppermute | solution.py:28
  75.6 28.5 %collective-permute-start.8 = (bf16[4,32768]{1,0:T(4,128)(2,1)S(1)}, bf16[4,32768]{1,0:T(4,128)(2,1)S(1)}, u32[]{:S(2)}, u32[]{:S(2)}) collective-permute-start(bf16[4,32768]{1,0:T(4,128)(2,1)S(1)} %maximum_select_fusion.4), channel_id=1, source_target_pairs={{0,2},{2,0},{4,6},{6,4},{8,10},{10,8},{12,14},{14,12},{1,3},{3,1},... | collective-permute-start | bytes 786440 | tf_op jit(solution)/shard_map/ppermute | solution.py:28
  98.5 5.6 %copy-start.5 = (bf16[1024,1024]{1,0:T(8,128)(2,1)}, bf16[1024,1024]{1,0:T(8,128)(2,1)S(1)}, u32[]{:S(2)}) copy-start(bf16[1024,1024]{1,0:T(8,128)(2,1)S(1)} %bitcast_dynamic-update-slice_fusion.5) | copy-start | bytes 6291460
  98.5 1.4 copy-start.4
  104.6 15.3 %collective-permute-start.9 = (bf16[8,32768]{1,0:T(8,128)(2,1)S(1)}, bf16[8,32768]{1,0:T(8,128)(2,1)S(1)}, u32[]{:S(2)}, u32[]{:S(2)}) collective-permute-start(bf16[8,32768]{1,0:T(8,128)(2,1)S(1)} %maximum_select_fusion.2), channel_id=1, source_target_pairs={{0,1},{1,0},{2,3},{3,2},{4,5},{5,4},{6,7},{7,6},{8,9},{9,8},{10,11... | collective-permute-start | bytes 1572872 | tf_op jit(solution)/shard_map/ppermute | solution.py:25
  113.0 16.8 %all-to-all-start = ((bf16[16,128,64]{1,2,0:T(8,128)(2,1)}), bf16[16,128,64]{1,2,0:T(8,128)(2,1)S(1)}, u32[]{:S(2)}, u32[]{:S(2)}) async-start(bf16[16,128,64]{1,2,0:T(8,128)(2,1)} %bitcast.146), calls=%async_computation | async-start | bytes 524288 | tf_op jit(solution)/shard_map/all_to_all | solution.py:160
  146.3 2.8 %copy-start.1 = (f32[1024,1024]{1,0:T(8,128)S(1)}, f32[1024,1024]{1,0:T(8,128)}, u32[]{:S(2)}) copy-start(f32[1024,1024]{1,0:T(8,128)} %get-tuple-element.13) | copy-start | bytes 12582916
  147.2 1.8 copy-start.11
  153.4 5.0 %collective-permute-start.12 = (bf16[8,32768]{1,0:T(8,128)(2,1)}, bf16[8,32768]{1,0:T(8,128)(2,1)}, u32[]{:S(2)}, u32[]{:S(2)}) collective-permute-start(bf16[8,32768]{1,0:T(8,128)(2,1)} %convert_element_type.108), channel_id=1, source_target_pairs={{0,1},{1,0},{2,3},{3,2},{4,5},{5,4},{6,7},{7,6},{8,9},{9,8},{10,11... | collective-permute-start | bytes 1572872 | tf_op jit(solution)/shard_map/ppermute | solution.py:25
  156.0 2.5 copy-start.3
  159.6 5.0 %copy-start.2 = (f32[8,32768]{1,0:T(8,128)}, f32[8,32768]{1,0:T(8,128)S(1)}, u32[]{:S(2)}) copy-start(f32[8,32768]{1,0:T(8,128)S(1)} %convert_add_fusion) | copy-start | bytes 3145732
  160.6 11.8 %collective-permute-start.13 = (bf16[4,32768]{1,0:T(4,128)(2,1)}, bf16[4,32768]{1,0:T(4,128)(2,1)}, u32[]{:S(2)}, u32[]{:S(2)}) collective-permute-start(bf16[4,32768]{1,0:T(4,128)(2,1)} %select_convert_fusion.1), channel_id=1, source_target_pairs={{0,2},{2,0},{4,6},{6,4},{8,10},{10,8},{12,14},{14,12},{1,3},{3,1},... | collective-permute-start | bytes 786440 | tf_op jit(solution)/shard_map/ppermute | solution.py:28
  164.5 2.4 copy-start.9
  167.7 18.8 %all-to-all-start.1 = ((bf16[1,128,16,64]{1,3,0,2:T(8,128)(2,1)}), bf16[1,128,16,64]{1,3,0,2:T(8,128)(2,1)}, u32[]{:S(2)}, u32[]{:S(2)}) async-start(bf16[1,128,16,64]{1,3,0,2:T(8,128)(2,1)} %bitcast.158), calls=%async_computation.1 | async-start | bytes 524288 | tf_op jit(solution)/shard_map/all_to_all | solution.py:199
  174.6 6.1 %collective-permute-start.14 = (bf16[2,32768]{1,0:T(2,128)(2,1)S(1)}, bf16[2,32768]{1,0:T(2,128)(2,1)S(1)}, u32[]{:S(2)}, u32[]{:S(2)}) collective-permute-start(bf16[2,32768]{1,0:T(2,128)(2,1)S(1)} %select_convert_fusion.2), channel_id=1, source_target_pairs={{0,4},{2,6},{4,0},{6,2},{8,12},{10,14},{12,8},{14,10},{1,5},{3,7},... | collective-permute-start | bytes 393224 | tf_op jit(solution)/shard_map/ppermute | solution.py:28
  176.6 17.5 %copy-start = (f32[1,384,1024]{2,1,0:T(8,128)S(1)}, f32[1,384,1024]{2,1,0:T(8,128)}, u32[]{:S(2)}) copy-start(f32[1,384,1024]{2,1,0:T(8,128)} %bitcast_dynamic-update-slice_fusion.1) | copy-start | bytes 4718596
  181.7 9.1 %collective-permute-start.15 = (bf16[1,32768]{1,0:T(2,128)(2,1)}, bf16[1,32768]{1,0:T(2,128)(2,1)S(1)}, u32[]{:S(2)}, u32[]{:S(2)}) collective-permute-start(bf16[1,32768]{1,0:T(2,128)(2,1)} %fusion.32), channel_id=1, source_target_pairs={{0,8},{2,10},{4,12},{6,14},{8,0},{10,2},{12,4},{14,6},{1,9},{3,11}... | collective-permute-start | bytes 196616 | tf_op jit(solution)/shard_map/ppermute | solution.py:28
  191.0 7.5 %collective-permute-start.16 = (bf16[1,32768]{1,0:T(2,128)(2,1)S(1)}, bf16[1,32768]{1,0:T(2,128)(2,1)S(1)}, u32[]{:S(2)}, u32[]{:S(2)}) collective-permute-start(bf16[1,32768]{1,0:T(2,128)(2,1)S(1)} %fusion.31), channel_id=1, source_target_pairs={{0,8},{2,10},{4,12},{6,14},{8,0},{10,2},{12,4},{14,6},{1,9},{3,11}... | collective-permute-start | bytes 196616 | tf_op jit(solution)/shard_map/ppermute | solution.py:28
  195.4 14.4 %copy-start.10 = (bf16[128,1024]{1,0:T(8,128)(2,1)S(1)}, bf16[128,1024]{1,0:T(8,128)(2,1)}, u32[]{:S(2)}) copy-start(bf16[128,1024]{1,0:T(8,128)(2,1)} %get-tuple-element.11) | copy-start | bytes 786436
  199.1 9.5 %collective-permute-start.17 = (bf16[2,32768]{1,0:T(2,128)(2,1)S(1)}, bf16[2,32768]{1,0:T(2,128)(2,1)S(1)}, u32[]{:S(2)}, u32[]{:S(2)}) collective-permute-start(bf16[2,32768]{1,0:T(2,128)(2,1)S(1)} %broadcast_select_fusion.12), channel_id=1, source_target_pairs={{0,4},{2,6},{4,0},{6,2},{8,12},{10,14},{12,8},{14,10},{1,5},{3,7},... | collective-permute-start | bytes 393224 | tf_op jit(solution)/shard_map/ppermute | solution.py:28
  203.5 42.8 %collective-permute-start.10 = (bf16[2,256,1024]{2,1,0:T(8,128)(2,1)}, bf16[2,256,1024]{2,1,0:T(8,128)(2,1)}, u32[]{:S(2)}, u32[]{:S(2)}) collective-permute-start(bf16[2,256,1024]{2,1,0:T(8,128)(2,1)} %pad_maximum_fusion.3), channel_id=1, source_target_pairs={{0,1},{1,2},{2,3},{3,4},{4,5},{5,6},{6,7},{7,8},{8,9},{9,10},{10,1... | collective-permute-start | bytes 3145736 | tf_op jit(solution)/shard_map/ppermute | solution.py:71
  206.7 39.6 %collective-permute-start.11 = (bf16[2,256,1024]{2,1,0:T(8,128)(2,1)}, bf16[2,256,1024]{2,1,0:T(8,128)(2,1)}, u32[]{:S(2)}, u32[]{:S(2)}) collective-permute-start(bf16[2,256,1024]{2,1,0:T(8,128)(2,1)} %pad_maximum_fusion.3), channel_id=1, source_target_pairs={{1,0},{2,1},{3,2},{4,3},{5,4},{6,5},{7,6},{8,7},{9,8},{10,9},{11,1... | collective-permute-start | bytes 3145736 | tf_op jit(solution)/shard_map/ppermute | solution.py:72
  209.1 26.4 %collective-permute-start.18 = (bf16[4,32768]{1,0:T(4,128)(2,1)S(1)}, bf16[4,32768]{1,0:T(4,128)(2,1)S(1)}, u32[]{:S(2)}, u32[]{:S(2)}) collective-permute-start(bf16[4,32768]{1,0:T(4,128)(2,1)S(1)} %maximum_select_fusion.5), channel_id=1, source_target_pairs={{0,2},{2,0},{4,6},{6,4},{8,10},{10,8},{12,14},{14,12},{1,3},{3,1},... | collective-permute-start | bytes 786440 | tf_op jit(solution)/shard_map/ppermute | solution.py:28
  235.9 8.8 %collective-permute-start.19 = (bf16[8,32768]{1,0:T(8,128)(2,1)S(1)}, bf16[8,32768]{1,0:T(8,128)(2,1)S(1)}, u32[]{:S(2)}, u32[]{:S(2)}) collective-permute-start(bf16[8,32768]{1,0:T(8,128)(2,1)S(1)} %maximum_select_fusion.3), channel_id=1, source_target_pairs={{0,1},{1,0},{2,3},{3,2},{4,5},{5,4},{6,7},{7,6},{8,9},{9,8},{10,11... | collective-permute-start | bytes 1572872 | tf_op jit(solution)/shard_map/ppermute | solution.py:25
Sparse Core Ops, SparseCore 0:
  10.2 85.8 all-gather.2
  98.2 59.8 all-gather.4

commit v12 on v11

--- a/solution.py
+++ b/solution.py
@@ -127,8 +127,6 @@
     weight_all = lax.all_gather(out_weight, SEQ, axis=0, tiled=True)
 
     paired = jnp.stack([keys, values])
-    before, after = halo(paired)
-    extended = jnp.concatenate([before, paired, after], axis=1)
 
     slots = global_blocks.shape[0]
     owners = global_blocks // blocks_dev
@@ -137,7 +135,12 @@
         start = (global_blocks[g] % blocks_dev) * BLK
         block = lax.dynamic_slice_in_dim(paired, start, BLK, axis=1)
         masked.append(jnp.where(owners[g] == device, block, jnp.zeros_like(block)))
-    global_kv = butterfly_sum(jnp.stack(masked))
+    masked = jnp.stack(masked)
+    halves = butterfly_halves(masked)
+    halves, paired_late = lax.optimization_barrier((halves, paired))
+    global_kv = butterfly_doubling(halves, masked.shape)
+    before, after = halo(paired_late)
+    extended = jnp.concatenate([before, paired, after], axis=1)
 
     local_ids = jnp.arange(blocks_dev, dtype=jnp.int32)
     global_ids = device * blocks_dev + local_ids
@@ -195,17 +198,15 @@
         )
         global_local = terms if global_local is None else global_local + terms
     grad_ext = jnp.stack(grad_ext)
+    global_total = butterfly_sum(global_local, jnp.bfloat16)
+
     attn_out = jnp.concatenate(attn_rows, axis=0)
+    layer_out = jnp.dot(attn_out, weight_all, preferred_element_type=jnp.float32).astype(
+        jnp.bfloat16
+    )
     attn_cols = lax.all_to_all(
         attn_out.reshape(tok_rows, count, w_rows), SEQ, 1, 0, tiled=False
     ).reshape(count * tok_rows, w_rows)
-    halves = butterfly_halves(global_local, jnp.bfloat16)
-    attn_cols, halves = lax.optimization_barrier((attn_cols, halves))
-    global_total = butterfly_doubling(halves, global_local.shape)
-
-    layer_out = jnp.dot(attn_out, weight_all, preferred_element_type=jnp.float32).astype(
-        jnp.bfloat16
-    )
     grad_weight = lax.dot_general(
         attn_cols, grad_out_all, (((0,), (0,)), ((), ())), preferred_element_type=jnp.float32
     )

time: 257 us -> 261 us (1.016)
  waiting for transfers between devices: 87.1 us -> 115 us
  starting transfers between devices: 69.5 us -> 54.5 us
  other arithmetic: 30.9 us -> 22.9 us
    ppermute x12, waiting for transfers between devices: 65.1 us -> 41.9 us  [xor_swap(): return lax.ppermute(x, 'chip', [(i, i ^ m) for i in range(n)])]
    all_gather x1, waiting for transfers between devices: 0.01 us -> 20.4 us  [local(): grad_out_all = lax.all_gather(grad_out, SEQ, axis=0, tiled=True)]
    ppermute x12, starting transfers between devices: 40.8 us -> 21.2 us  [xor_swap(): return lax.ppermute(x, 'chip', [(i, i ^ m) for i in range(n)])]
    all_to_all x1, waiting for transfers between devices: 0.01 us -> 17.4 us  [local(): lax.all_to_all(attn_out.reshape(tok_rows, count, w_rows), SEQ, 1, 0, tile...]
    ppermute x2, waiting for transfers between devices: 4.1 us -> 17.9 us  [halo(): before = lax.ppermute(shard, SEQ, up)]
    ppermute x2, waiting for transfers between devices: 9.58 us -> 3.27 us  [halo(): after = lax.ppermute(shard, SEQ, down)]
    all_to_all x1, waiting for transfers between devices: 7.6 us -> 12.4 us  [local(): lax.all_to_all(upstream_cols.reshape(count, tok_rows, w_rows), SEQ, 0, 0,...]
    ppermute x2, starting transfers between devices: 6.88 us -> 11.1 us  [halo(): before = lax.ppermute(shard, SEQ, up)]
  transfers between devices with their start and end apart: 24 -> 24, of which waited for: 13 -> 15; matrix products, arithmetic and copies ran while one was open for 25% -> 20% of each run, Pallas kernels for 5% -> 5%
where the time goes in v12:
time: 261 us; the launch traced here: 260 us
  waiting for transfers between devices  115 us (44%)
  starting transfers between devices  54.5 us (21%)
  other arithmetic  22.9 us (9%)
  local copies, waits for them, and re-layouts  22.5 us (9%)
  between operations  17.8 us (7%)
  matrix products  15.5 us (6%)
  Pallas kernels  12.2 us (5%)
    ppermute x12, waiting for transfers between devices, xor_swap(): return lax.ppermute(x, 'chip', [(i, i ^ m) for i in range(n)])  41.9 us
    ppermute x12, starting transfers between devices, xor_swap(): return lax.ppermute(x, 'chip', [(i, i ^ m) for i in range(n)])  21.2 us
    all_gather x1, waiting for transfers between devices, local(): grad_out_all = lax.all_gather(grad_out, SEQ, axis=0, tiled=True)  20.4 us
    ppermute x2, waiting for transfers between devices, halo(): before = lax.ppermute(shard, SEQ, up)  17.9 us
    all_to_all x1, waiting for transfers between devices, local(): lax.all_to_all(attn_out.reshape(tok_rows, count, w_rows), SEQ, 1, 0, tile...  17.4 us
    all_to_all x1, waiting for transfers between devices, local(): lax.all_to_all(upstream_cols.reshape(count, tok_rows, w_rows), SEQ, 0, 0,...  12.4 us
    pallas_call x1, Pallas kernels, attention(): pl.pallas_call(_attn_kernel, grid=(heads,), in_specs=[pl.BlockSpec((1, ke...  12.2 us
    ppermute x2, starting transfers between devices, halo(): before = lax.ppermute(shard, SEQ, up)  11.1 us
  transfers between devices with their start and end apart: 24, of which 15 were waited for; matrix products, arithmetic and copies ran while one was open for 20% of the time, Pallas kernels for 5%

profile of v12, /device:TPU:11, one launch (start us, length us, event | category | flops | bytes accessed | tf_op | source)
XLA Modules:
  0.0 260.0 jit_solution(11075452760562189497)
XLA Ops:
  7.2 1.3 fusion.41
  9.8 1.1 pad_maximum_fusion.4
  12.2 1.3 collective-permute-done
  13.9 1.3 collective-permute-start.1
  15.2 6.3 %collective-permute-done.1 = bf16[4,32768]{1,0:T(4,128)(2,1)S(1)} collective-permute-done((bf16[4,32768]{1,0:T(4,128)(2,1)S(1)}, bf16[4,32768]{1,0:T(4,128)(2,1)S(1)}, u32[]{:S(2)}, u32[]{:S(2)}) %collective-permute-start.1) | collective-permute-done | bytes 262176 | tf_op jit(solution)/shard_map/ppermute | solution.py:28
  22.3 3.6 %collective-permute-done.2 = bf16[2,32768]{1,0:T(2,128)(2,1)S(1)} collective-permute-done((bf16[2,32768]{1,0:T(2,128)(2,1)S(1)}, bf16[2,32768]{1,0:T(2,128)(2,1)S(1)}, u32[]{:S(2)}, u32[]{:S(2)}) %collective-permute-start.2) | collective-permute-done | bytes 131104 | tf_op jit(solution)/shard_map/ppermute | solution.py:28
  26.3 2.4 collective-permute-start.3
  28.7 3.2 %collective-permute-done.3 = bf16[1,32768]{1,0:T(2,128)(2,1)S(1)} collective-permute-done((bf16[1,32768]{1,0:T(2,128)(2,1)S(1)}, bf16[1,32768]{1,0:T(2,128)(2,1)S(1)}, u32[]{:S(2)}, u32[]{:S(2)}) %collective-permute-start.3) | collective-permute-done | bytes 65568 | tf_op jit(solution)/shard_map/ppermute | solution.py:28
  32.2 2.9 %collective-permute-start.6 = (bf16[1,32768]{1,0:T(2,128)(2,1)S(1)}, bf16[1,32768]{1,0:T(2,128)(2,1)S(1)}, u32[]{:S(2)}, u32[]{:S(2)}) collective-permute-start(bf16[1,32768]{1,0:T(2,128)(2,1)S(1)} %fusion.32), channel_id=1, source_target_pairs={{0,8},{2,10},{4,12},{6,14},{8,0},{10,2},{12,4},{14,6},{1,9},{3,11}... | collective-permute-start | bytes 196616 | tf_op jit(solution)/shard_map/ppermute | solution.py:28
  35.1 11.7 %collective-permute-done.6 = bf16[1,32768]{1,0:T(2,128)(2,1)S(1)} collective-permute-done((bf16[1,32768]{1,0:T(2,128)(2,1)S(1)}, bf16[1,32768]{1,0:T(2,128)(2,1)S(1)}, u32[]{:S(2)}, u32[]{:S(2)}) %collective-permute-start.6) | collective-permute-done | bytes 65568 | tf_op jit(solution)/shard_map/ppermute | solution.py:28
  50.1 4.1 %collective-permute-done.7 = bf16[2,32768]{1,0:T(2,128)(2,1)S(1)} collective-permute-done((bf16[2,32768]{1,0:T(2,128)(2,1)S(1)}, bf16[2,32768]{1,0:T(2,128)(2,1)S(1)}, u32[]{:S(2)}, u32[]{:S(2)}) %collective-permute-start.7) | collective-permute-done | bytes 131104 | tf_op jit(solution)/shard_map/ppermute | solution.py:28
  54.7 1.2 collective-permute-start.8
  56.0 8.9 %collective-permute-start.4 = (bf16[2,128,1024]{2,1,0:T(8,128)(2,1)S(1)}, bf16[2,128,1024]{2,1,0:T(8,128)(2,1)S(1)}, u32[]{:S(2)}, u32[]{:S(2)}) collective-permute-start(bf16[2,128,1024]{2,1,0:T(8,128)(2,1)S(1)} %get-tuple-element.11), channel_id=1, source_target_pairs={{0,1},{1,2},{2,3},{3,4},{4,5},{5,6},{6,7},{7,8},{8,9},{9,10},{10,1... | collective-permute-start | bytes 1572872 | tf_op jit(solution)/shard_map/ppermute | solution.py:71
  65.0 1.9 collective-permute-start.5
  67.4 3.5 %collective-permute-start.9 = (bf16[8,32768]{1,0:T(8,128)(2,1)S(1)}, bf16[8,32768]{1,0:T(8,128)(2,1)S(1)}, u32[]{:S(2)}, u32[]{:S(2)}) collective-permute-start(bf16[8,32768]{1,0:T(8,128)(2,1)S(1)} %maximum_select_fusion.2), channel_id=1, source_target_pairs={{0,1},{1,0},{2,3},{3,2},{4,5},{5,4},{6,7},{7,6},{8,9},{9,8},{10,11... | collective-permute-start | bytes 1572872 | tf_op jit(solution)/shard_map/ppermute | solution.py:25
  70.9 17.9 %collective-permute-done.4 = bf16[2,128,1024]{2,1,0:T(8,128)(2,1)S(1)} collective-permute-done((bf16[2,128,1024]{2,1,0:T(8,128)(2,1)S(1)}, bf16[2,128,1024]{2,1,0:T(8,128)(2,1)S(1)}, u32[]{:S(2)}, u32[]{:S(2)}) %collective-permute-start.4) | collective-permute-done | bytes 524320 | tf_op jit(solution)/shard_map/ppermute | solution.py:71
  88.8 3.3 %collective-permute-done.5 = bf16[2,128,1024]{2,1,0:T(8,128)(2,1)S(1)} collective-permute-done((bf16[2,128,1024]{2,1,0:T(8,128)(2,1)S(1)}, bf16[2,128,1024]{2,1,0:T(8,128)(2,1)S(1)}, u32[]{:S(2)}, u32[]{:S(2)}) %collective-permute-start.5) | collective-permute-done | bytes 524320 | tf_op jit(solution)/shard_map/ppermute | solution.py:72
  96.1 1.3 copy-done.4
  98.2 20.4 %all-gather.3.cloned.1.call-done = bf16[2048,2048]{1,0:T(8,128)(2,1)} async-done(((bf16[128,2048]{1,0:T(8,128)(2,1)}), bf16[2048,2048]{1,0:T(8,128)(2,1)}) %all-gather.3.cloned.1.call-update) | async-done | bytes 8388624 | tf_op jit(solution)/shard_map/all_gather | solution.py:126
  118.5 6.0 %fusion = bf16[8,16,8,128]{3,2,1,0:T(8,128)(2,1)S(1)} fusion(bf16[2048,2048]{1,0:T(8,128)(2,1)} %all-gather.3.cloned.1.call-done, bf16[64,2048]{1,0:T(8,128)(2,1)S(1)} %copy-done.7), kind=kOutput, calls=%fused_computation.7 | convolution fusion | flops 537001984 | bytes 8912896 | tf_op jit(solution)/shard_map/dot_general | solution.py:160
  125.3 4.5 %all-to-all-start = ((bf16[16,128,64]{1,2,0:T(8,128)(2,1)}), bf16[16,128,64]{1,2,0:T(8,128)(2,1)S(1)}, u32[]{:S(2)}, u32[]{:S(2)}) async-start(bf16[16,128,64]{1,2,0:T(8,128)(2,1)} %bitcast.145), calls=%async_computation | async-start | bytes 524288 | tf_op jit(solution)/shard_map/all_to_all | solution.py:163
  132.3 12.4 %all-to-all-done = bf16[16,128,64]{1,2,0:T(8,128)(2,1)S(1)} async-done(((bf16[16,128,64]{1,2,0:T(8,128)(2,1)}), bf16[16,128,64]{1,2,0:T(8,128)(2,1)S(1)}, u32[]{:S(2)}, u32[]{:S(2)}) %all-to-all-start) | async-done | bytes 262176 | tf_op jit(solution)/shard_map/all_to_all | solution.py:163
  146.2 12.2 %shard_map.119 = (bf16[128,1024]{1,0:T(8,128)(2,1)}, bf16[128,1024]{1,0:T(8,128)(2,1)}, f32[1024,1024]{1,0:T(8,128)}, f32[1024,1024]{1,0:T(8,128)}) custom-call(f32[1,1024]{1,0:T(1,128)} %bitcast.159, bf16[128,1024]{1,0:T(8,128)(2,1)} %q_ref.1, bf16[1024,1024]{1,0:T(8,128)(2,1)} %get-tuple-element.24.k_ref, bf16[1024,1024]{1,0:T(8,128)(2,1)} %get-tuple-element.23.v_ref, ...), custom_call_target="tpu_custom_call" | custom-call | tf_op jit(solution)/shard_map/pallas_call | solution.py:104
  158.4 1.3 slice.245
  159.7 1.3 slice.246
  163.8 1.8 slice_select_fusion
  166.1 2.1 convert_element_type.108
  168.2 2.4 select_n.304
  170.6 1.3 fusion.9
  171.9 1.2 fusion.8
  175.5 1.1 add_dynamic-update-slice_fusion.1
  176.8 1.1 add_dynamic-update-slice_fusion
  178.0 3.8 %collective-permute-done.13 = bf16[4,32768]{1,0:T(4,128)(2,1)S(1)} collective-permute-done((bf16[4,32768]{1,0:T(4,128)(2,1)S(1)}, bf16[4,32768]{1,0:T(4,128)(2,1)S(1)}, u32[]{:S(2)}, u32[]{:S(2)}) %collective-permute-start.13) | collective-permute-done | bytes 262176 | tf_op jit(solution)/shard_map/ppermute | solution.py:28
  184.0 2.1 collective-permute-done.14
  186.5 2.2 collective-permute-start.15
  189.8 2.6 collective-permute-done.15
  192.6 4.6 %collective-permute-start.16 = (bf16[1,32768]{1,0:T(2,128)(2,1)S(1)}, bf16[1,32768]{1,0:T(2,128)(2,1)S(1)}, u32[]{:S(2)}, u32[]{:S(2)}) collective-permute-start(bf16[1,32768]{1,0:T(2,128)(2,1)S(1)} %fusion.34), channel_id=1, source_target_pairs={{0,8},{2,10},{4,12},{6,14},{8,0},{10,2},{12,4},{14,6},{1,9},{3,11}... | collective-permute-start | bytes 196616 | tf_op jit(solution)/shard_map/ppermute | solution.py:28
  197.4 4.5 %collective-permute-done.16 = bf16[1,32768]{1,0:T(2,128)(2,1)S(1)} collective-permute-done((bf16[1,32768]{1,0:T(2,128)(2,1)S(1)}, bf16[1,32768]{1,0:T(2,128)(2,1)S(1)}, u32[]{:S(2)}, u32[]{:S(2)}) %collective-permute-start.16) | collective-permute-done | bytes 65568 | tf_op jit(solution)/shard_map/ppermute | solution.py:28
  202.5 3.3 %collective-permute-start.17 = (bf16[2,32768]{1,0:T(2,128)(2,1)S(1)}, bf16[2,32768]{1,0:T(2,128)(2,1)S(1)}, u32[]{:S(2)}, u32[]{:S(2)}) collective-permute-start(bf16[2,32768]{1,0:T(2,128)(2,1)S(1)} %broadcast_select_fusion.5), channel_id=1, source_target_pairs={{0,4},{2,6},{4,0},{6,2},{8,12},{10,14},{12,8},{14,10},{1,5},{3,7},... | collective-permute-start | bytes 393224 | tf_op jit(solution)/shard_map/ppermute | solution.py:28
  205.8 2.1 collective-permute-start.10
  207.9 2.6 collective-permute-start.11
  211.4 5.7 %all-to-all-start.1 = ((bf16[1,128,16,64]{1,3,0,2:T(8,128)(2,1)}), bf16[1,128,16,64]{1,3,0,2:T(8,128)(2,1)S(1)}, u32[]{:S(2)}, u32[]{:S(2)}) async-start(bf16[1,128,16,64]{1,3,0,2:T(8,128)(2,1)} %bitcast.39), calls=%async_computation.1 | async-start | bytes 524288 | tf_op jit(solution)/shard_map/all_to_all | solution.py:207
  217.6 1.2 collective-permute-start.18
  218.8 3.7 %convolution_convert_fusion = bf16[128,2048]{1,0:T(8,128)(2,1)} fusion(bf16[128,1024]{1,0:T(8,128)(2,1)S(1)} %copy-done.8, bf16[1024,2048]{1,0:T(8,128)(2,1)} %all-gather.5.cloned.1.call-done), kind=kOutput, calls=%fused_computation | convolution fusion | flops 537133056 | bytes 4980736 | tf_op jit(solution)/shard_map/dot_general | solution.py:204
  222.5 17.4 %all-to-all-done.1 = bf16[1,128,16,64]{1,3,0,2:T(8,128)(2,1)S(1)} async-done(((bf16[1,128,16,64]{1,3,0,2:T(8,128)(2,1)}), bf16[1,128,16,64]{1,3,0,2:T(8,128)(2,1)S(1)}, u32[]{:S(2)}, u32[]{:S(2)}) %all-to-all-start.1) | async-done | bytes 262176 | tf_op jit(solution)/shard_map/all_to_all | solution.py:207
  240.6 3.3 %collective-permute-start.19 = (bf16[8,32768]{1,0:T(8,128)(2,1)S(1)}, bf16[8,32768]{1,0:T(8,128)(2,1)S(1)}, u32[]{:S(2)}, u32[]{:S(2)}) collective-permute-start(bf16[8,32768]{1,0:T(8,128)(2,1)S(1)} %maximum_select_fusion.3), channel_id=1, source_target_pairs={{0,1},{1,0},{2,3},{3,2},{4,5},{5,4},{6,7},{7,6},{8,9},{9,8},{10,11... | collective-permute-start | bytes 1572872 | tf_op jit(solution)/shard_map/ppermute | solution.py:25
  243.9 5.7 %fusion.17 = f32[64,2048]{1,0:T(8,128)} fusion(bf16[2048,2048]{1,0:T(8,128)(2,1)} %all-gather.3.cloned.1.call-done, bf16[8,8,16,128]{3,2,1,0:T(8,128)(2,1)S(1)} %bitcast.156), kind=kOutput, calls=%fused_computation.54 | convolution fusion | flops 536870912 | bytes 9175040 | tf_op jit(solution)/shard_map/dot_general | solution.py:210
  250.3 2.8 %fusion.7 = (bf16[128,1024]{1,0:T(8,128)(2,1)}, bf16[128,1024]{1,0:T(8,128)(2,1)}) fusion(f32[1,384,1024]{2,1,0:T(8,128)} %copy-done, bf16[2,2,128,1024]{3,2,1,0:T(8,128)(2,1)S(1)} %select_n.316, bf16[2,256,1024]{2,1,0:T(8,128)(2,1)} %collective-permute-done.11, bf16[2,256,1024]{2,1,0:T(8,128)(2,1)} %collective-permute-done.10, pred[]{:T(512)S(6)} %eq.23, ...), kind=kLoop, calls=%fused_computation.23 | loop fusion | flops 2883584 | bytes 3670018 | tf_op jit(solution)/shard_map/convert_element_type | solution.py:229
  (104 shorter events, 28.1 us)
Async XLA Ops:
  7.2 111.3 %all-gather.3.cloned.1.call-start = ((), (), s32[]{:S(2)}) async-start(), calls=%async_computation.2 | async-start | bytes 8912896 | tf_op jit(solution)/shard_map/all_gather | solution.py:126
  11.2 2.3 collective-permute-start
  13.9 33.6 %copy-start.10 = (s32[1,3]{1,0:T(1,128)S(1)}, s32[1,3]{1,0:T(1,128)}, u32[]{:S(2)}) copy-start(s32[1,3]{1,0:T(1,128)} %param.14) | copy-start | bytes 40
  13.9 7.6 %collective-permute-start.1 = (bf16[4,32768]{1,0:T(4,128)(2,1)S(1)}, bf16[4,32768]{1,0:T(4,128)(2,1)S(1)}, u32[]{:S(2)}, u32[]{:S(2)}) collective-permute-start(bf16[4,32768]{1,0:T(4,128)(2,1)S(1)} %broadcast_select_fusion.7), channel_id=1, source_target_pairs={{0,2},{2,0},{4,6},{6,4},{8,10},{10,8},{12,14},{14,12},{1,3},{3,1},... | collective-permute-start | bytes 786440 | tf_op jit(solution)/shard_map/ppermute | solution.py:28
  15.2 40.7 %copy-start.11 = (s32[3]{0:T(128)S(1)}, s32[3]{0:T(128)}, u32[]{:S(2)}) copy-start(s32[3]{0:T(128)} %constant.85.clone) | copy-start | bytes 40
  21.9 70.1 %copy-start.5 = (bf16[128,1024]{1,0:T(8,128)(2,1)S(1)}, bf16[128,1024]{1,0:T(8,128)(2,1)}, u32[]{:S(2)}) copy-start(bf16[128,1024]{1,0:T(8,128)(2,1)} %param.10) | copy-start | bytes 786436
  21.9 70.1 %copy-start.6 = (bf16[128,1024]{1,0:T(8,128)(2,1)S(1)}, bf16[128,1024]{1,0:T(8,128)(2,1)}, u32[]{:S(2)}) copy-start(bf16[128,1024]{1,0:T(8,128)(2,1)} %param.9) | copy-start | bytes 786436
  22.0 3.9 %collective-permute-start.2 = (bf16[2,32768]{1,0:T(2,128)(2,1)S(1)}, bf16[2,32768]{1,0:T(2,128)(2,1)S(1)}, u32[]{:S(2)}, u32[]{:S(2)}) collective-permute-start(bf16[2,32768]{1,0:T(2,128)(2,1)S(1)} %broadcast_select_fusion.8), channel_id=1, source_target_pairs={{0,4},{2,6},{4,0},{6,2},{8,12},{10,14},{12,8},{14,10},{1,5},{3,7},... | collective-permute-start | bytes 393224 | tf_op jit(solution)/shard_map/ppermute | solution.py:28
  22.2 196.6 %all-gather.5.cloned.1.call-start = ((), (), s32[]{:S(2)}) async-start(), calls=%async_computation.3 | async-start | bytes 4456448 | tf_op jit(solution)/shard_map/all_gather | solution.py:127
  26.3 5.6 %collective-permute-start.3 = (bf16[1,32768]{1,0:T(2,128)(2,1)S(1)}, bf16[1,32768]{1,0:T(2,128)(2,1)S(1)}, u32[]{:S(2)}, u32[]{:S(2)}) collective-permute-start(bf16[1,32768]{1,0:T(2,128)(2,1)S(1)} %broadcast_select_fusion.12), channel_id=1, source_target_pairs={{0,8},{2,10},{4,12},{6,14},{8,0},{10,2},{12,4},{14,6},{1,9},{3,11}... | collective-permute-start | bytes 196616 | tf_op jit(solution)/shard_map/ppermute | solution.py:28
  32.2 14.6 %collective-permute-start.6 = (bf16[1,32768]{1,0:T(2,128)(2,1)S(1)}, bf16[1,32768]{1,0:T(2,128)(2,1)S(1)}, u32[]{:S(2)}, u32[]{:S(2)}) collective-permute-start(bf16[1,32768]{1,0:T(2,128)(2,1)S(1)} %fusion.32), channel_id=1, source_target_pairs={{0,8},{2,10},{4,12},{6,14},{8,0},{10,2},{12,4},{14,6},{1,9},{3,11}... | collective-permute-start | bytes 196616 | tf_op jit(solution)/shard_map/ppermute | solution.py:28
  47.4 6.8 %collective-permute-start.7 = (bf16[2,32768]{1,0:T(2,128)(2,1)S(1)}, bf16[2,32768]{1,0:T(2,128)(2,1)S(1)}, u32[]{:S(2)}, u32[]{:S(2)}) collective-permute-start(bf16[2,32768]{1,0:T(2,128)(2,1)S(1)} %broadcast_select_fusion.6), channel_id=1, source_target_pairs={{0,4},{2,6},{4,0},{6,2},{8,12},{10,14},{12,8},{14,10},{1,5},{3,7},... | collective-permute-start | bytes 393224 | tf_op jit(solution)/shard_map/ppermute | solution.py:28
  54.7 12.2 %collective-permute-start.8 = (bf16[4,32768]{1,0:T(4,128)(2,1)S(1)}, bf16[4,32768]{1,0:T(4,128)(2,1)S(1)}, u32[]{:S(2)}, u32[]{:S(2)}) collective-permute-start(bf16[4,32768]{1,0:T(4,128)(2,1)S(1)} %maximum_select_fusion.4), channel_id=1, source_target_pairs={{0,2},{2,0},{4,6},{6,4},{8,10},{10,8},{12,14},{14,12},{1,3},{3,1},... | collective-permute-start | bytes 786440 | tf_op jit(solution)/shard_map/ppermute | solution.py:28
  56.0 32.7 %collective-permute-start.4 = (bf16[2,128,1024]{2,1,0:T(8,128)(2,1)S(1)}, bf16[2,128,1024]{2,1,0:T(8,128)(2,1)S(1)}, u32[]{:S(2)}, u32[]{:S(2)}) collective-permute-start(bf16[2,128,1024]{2,1,0:T(8,128)(2,1)S(1)} %get-tuple-element.11), channel_id=1, source_target_pairs={{0,1},{1,2},{2,3},{3,4},{4,5},{5,6},{6,7},{7,8},{8,9},{9,10},{10,1... | collective-permute-start | bytes 1572872 | tf_op jit(solution)/shard_map/ppermute | solution.py:71
  65.0 27.0 %collective-permute-start.5 = (bf16[2,128,1024]{2,1,0:T(8,128)(2,1)S(1)}, bf16[2,128,1024]{2,1,0:T(8,128)(2,1)S(1)}, u32[]{:S(2)}, u32[]{:S(2)}) collective-permute-start(bf16[2,128,1024]{2,1,0:T(8,128)(2,1)S(1)} %get-tuple-element.11), channel_id=1, source_target_pairs={{1,0},{2,1},{3,2},{4,3},{5,4},{6,5},{7,6},{8,7},{9,8},{10,9},{11,1... | collective-permute-start | bytes 1572872 | tf_op jit(solution)/shard_map/ppermute | solution.py:72
  67.4 62.4 %collective-permute-start.9 = (bf16[8,32768]{1,0:T(8,128)(2,1)S(1)}, bf16[8,32768]{1,0:T(8,128)(2,1)S(1)}, u32[]{:S(2)}, u32[]{:S(2)}) collective-permute-start(bf16[8,32768]{1,0:T(8,128)(2,1)S(1)} %maximum_select_fusion.2), channel_id=1, source_target_pairs={{0,1},{1,0},{2,3},{3,2},{4,5},{5,4},{6,7},{7,6},{8,9},{9,8},{10,11... | collective-permute-start | bytes 1572872 | tf_op jit(solution)/shard_map/ppermute | solution.py:25
  93.8 24.7 %copy-start.7 = (bf16[64,2048]{1,0:T(8,128)(2,1)S(1)}, bf16[64,2048]{1,0:T(8,128)(2,1)}, u32[]{:S(2)}) copy-start(bf16[64,2048]{1,0:T(8,128)(2,1)} %param.11) | copy-start | bytes 786436
  96.1 1.4 copy-start.4
  125.3 19.4 %all-to-all-start = ((bf16[16,128,64]{1,2,0:T(8,128)(2,1)}), bf16[16,128,64]{1,2,0:T(8,128)(2,1)S(1)}, u32[]{:S(2)}, u32[]{:S(2)}) async-start(bf16[16,128,64]{1,2,0:T(8,128)(2,1)} %bitcast.145), calls=%async_computation | async-start | bytes 524288 | tf_op jit(solution)/shard_map/all_to_all | solution.py:163
  161.0 2.8 %copy-start.2 = (f32[1024,1024]{1,0:T(8,128)S(1)}, f32[1024,1024]{1,0:T(8,128)}, u32[]{:S(2)}) copy-start(f32[1024,1024]{1,0:T(8,128)} %get-tuple-element.15) | copy-start | bytes 12582916
  162.0 1.8 copy-start.9
  168.2 4.9 %collective-permute-start.12 = (bf16[8,32768]{1,0:T(8,128)(2,1)}, bf16[8,32768]{1,0:T(8,128)(2,1)}, u32[]{:S(2)}, u32[]{:S(2)}) collective-permute-start(bf16[8,32768]{1,0:T(8,128)(2,1)} %convert_element_type.108), channel_id=1, source_target_pairs={{0,1},{1,0},{2,3},{3,2},{4,5},{5,4},{6,7},{7,6},{8,9},{9,8},{10,11... | collective-permute-start | bytes 1572872 | tf_op jit(solution)/shard_map/ppermute | solution.py:25
  170.6 2.5 copy-start.3
  174.4 7.4 %collective-permute-start.13 = (bf16[4,32768]{1,0:T(4,128)(2,1)S(1)}, bf16[4,32768]{1,0:T(4,128)(2,1)S(1)}, u32[]{:S(2)}, u32[]{:S(2)}) collective-permute-start(bf16[4,32768]{1,0:T(4,128)(2,1)S(1)} %select_convert_fusion.1), channel_id=1, source_target_pairs={{0,2},{2,0},{4,6},{6,4},{8,10},{10,8},{12,14},{14,12},{1,3},{3,1},... | collective-permute-start | bytes 786440 | tf_op jit(solution)/shard_map/ppermute | solution.py:28
  182.2 3.9 %collective-permute-start.14 = (bf16[2,32768]{1,0:T(2,128)(2,1)S(1)}, bf16[2,32768]{1,0:T(2,128)(2,1)S(1)}, u32[]{:S(2)}, u32[]{:S(2)}) collective-permute-start(bf16[2,32768]{1,0:T(2,128)(2,1)S(1)} %select_convert_fusion.2), channel_id=1, source_target_pairs={{0,4},{2,6},{4,0},{6,2},{8,12},{10,14},{12,8},{14,10},{1,5},{3,7},... | collective-permute-start | bytes 393224 | tf_op jit(solution)/shard_map/ppermute | solution.py:28
  184.0 13.4 %copy-start.1 = (f32[1,384,1024]{2,1,0:T(8,128)}, f32[1,384,1024]{2,1,0:T(8,128)S(1)}, u32[]{:S(2)}) copy-start(f32[1,384,1024]{2,1,0:T(8,128)S(1)} %bitcast_dynamic-update-slice_fusion.1) | copy-start | bytes 4718596
  186.5 5.9 %collective-permute-start.15 = (bf16[1,32768]{1,0:T(2,128)(2,1)S(1)}, bf16[1,32768]{1,0:T(2,128)(2,1)S(1)}, u32[]{:S(2)}, u32[]{:S(2)}) collective-permute-start(bf16[1,32768]{1,0:T(2,128)(2,1)S(1)} %fusion.35), channel_id=1, source_target_pairs={{0,8},{2,10},{4,12},{6,14},{8,0},{10,2},{12,4},{14,6},{1,9},{3,11}... | collective-permute-start | bytes 196616 | tf_op jit(solution)/shard_map/ppermute | solution.py:28
  189.8 7.6 %copy-start = (f32[1,384,1024]{2,1,0:T(8,128)}, f32[1,384,1024]{2,1,0:T(8,128)S(1)}, u32[]{:S(2)}) copy-start(f32[1,384,1024]{2,1,0:T(8,128)S(1)} %bitcast_dynamic-update-slice_fusion) | copy-start | bytes 4718596
  192.6 9.2 %collective-permute-start.16 = (bf16[1,32768]{1,0:T(2,128)(2,1)S(1)}, bf16[1,32768]{1,0:T(2,128)(2,1)S(1)}, u32[]{:S(2)}, u32[]{:S(2)}) collective-permute-start(bf16[1,32768]{1,0:T(2,128)(2,1)S(1)} %fusion.34), channel_id=1, source_target_pairs={{0,8},{2,10},{4,12},{6,14},{8,0},{10,2},{12,4},{14,6},{1,9},{3,11}... | collective-permute-start | bytes 196616 | tf_op jit(solution)/shard_map/ppermute | solution.py:28
  197.4 13.1 %copy-start.8 = (bf16[128,1024]{1,0:T(8,128)(2,1)S(1)}, bf16[128,1024]{1,0:T(8,128)(2,1)}, u32[]{:S(2)}) copy-start(bf16[128,1024]{1,0:T(8,128)(2,1)} %get-tuple-element.13) | copy-start | bytes 786436
  202.5 14.6 %collective-permute-start.17 = (bf16[2,32768]{1,0:T(2,128)(2,1)S(1)}, bf16[2,32768]{1,0:T(2,128)(2,1)S(1)}, u32[]{:S(2)}, u32[]{:S(2)}) collective-permute-start(bf16[2,32768]{1,0:T(2,128)(2,1)S(1)} %broadcast_select_fusion.5), channel_id=1, source_target_pairs={{0,4},{2,6},{4,0},{6,2},{8,12},{10,14},{12,8},{14,10},{1,5},{3,7},... | collective-permute-start | bytes 393224 | tf_op jit(solution)/shard_map/ppermute | solution.py:28
  205.8 44.5 %collective-permute-start.10 = (bf16[2,256,1024]{2,1,0:T(8,128)(2,1)S(1)}, bf16[2,256,1024]{2,1,0:T(8,128)(2,1)}, u32[]{:S(2)}, u32[]{:S(2)}) collective-permute-start(bf16[2,256,1024]{2,1,0:T(8,128)(2,1)S(1)} %pad_maximum_fusion.3), channel_id=1, source_target_pairs={{0,1},{1,2},{2,3},{3,4},{4,5},{5,6},{6,7},{7,8},{8,9},{9,10},{10,1... | collective-permute-start | bytes 3145736 | tf_op jit(solution)/shard_map/ppermute | solution.py:71
  207.9 42.4 %collective-permute-start.11 = (bf16[2,256,1024]{2,1,0:T(8,128)(2,1)S(1)}, bf16[2,256,1024]{2,1,0:T(8,128)(2,1)}, u32[]{:S(2)}, u32[]{:S(2)}) collective-permute-start(bf16[2,256,1024]{2,1,0:T(8,128)(2,1)S(1)} %pad_maximum_fusion.3), channel_id=1, source_target_pairs={{1,0},{2,1},{3,2},{4,3},{5,4},{6,5},{7,6},{8,7},{9,8},{10,9},{11,1... | collective-permute-start | bytes 3145736 | tf_op jit(solution)/shard_map/ppermute | solution.py:72
  211.4 28.6 %all-to-all-start.1 = ((bf16[1,128,16,64]{1,3,0,2:T(8,128)(2,1)}), bf16[1,128,16,64]{1,3,0,2:T(8,128)(2,1)S(1)}, u32[]{:S(2)}, u32[]{:S(2)}) async-start(bf16[1,128,16,64]{1,3,0,2:T(8,128)(2,1)} %bitcast.39), calls=%async_computation.1 | async-start | bytes 524288 | tf_op jit(solution)/shard_map/all_to_all | solution.py:207
  217.6 22.5 %collective-permute-start.18 = (bf16[4,32768]{1,0:T(4,128)(2,1)S(1)}, bf16[4,32768]{1,0:T(4,128)(2,1)S(1)}, u32[]{:S(2)}, u32[]{:S(2)}) collective-permute-start(bf16[4,32768]{1,0:T(4,128)(2,1)S(1)} %maximum_select_fusion.5), channel_id=1, source_target_pairs={{0,2},{2,0},{4,6},{6,4},{8,10},{10,8},{12,14},{14,12},{1,3},{3,1},... | collective-permute-start | bytes 786440 | tf_op jit(solution)/shard_map/ppermute | solution.py:28
  240.6 9.0 %collective-permute-start.19 = (bf16[8,32768]{1,0:T(8,128)(2,1)S(1)}, bf16[8,32768]{1,0:T(8,128)(2,1)S(1)}, u32[]{:S(2)}, u32[]{:S(2)}) collective-permute-start(bf16[8,32768]{1,0:T(8,128)(2,1)S(1)} %maximum_select_fusion.3), channel_id=1, source_target_pairs={{0,1},{1,0},{2,3},{3,2},{4,5},{5,4},{6,7},{7,6},{8,9},{9,8},{10,11... | collective-permute-start | bytes 1572872 | tf_op jit(solution)/shard_map/ppermute | solution.py:25
Sparse Core Ops, SparseCore 0:
  22.3 96.1 all-gather.2
  120.7 53.8 all-gather.4

commit v13 on v10

--- a/solution.py
+++ b/solution.py
@@ -64,7 +64,7 @@
     return before, after
 
 
-def _attn_kernel(live_ref, q_ref, k_ref, v_ref, up_ref, attn_ref, dq_ref, dk_ref, dv_ref):
+def _attn_kernel(live_ref, q_ref, k_ref, v_ref, up_ref, attn_ref, dq_ref, dk_ref, dv_ref, dg_ref):
     scale = 1.0 / math.sqrt(q_ref.shape[-1])
     q = q_ref[...]
     k = k_ref[...]
@@ -79,29 +79,37 @@
     probs = raised / jnp.sum(raised, axis=-1, keepdims=True)
     probs_b = probs.astype(jnp.bfloat16)
     attn_ref[...] = jnp.dot(probs_b, v, preferred_element_type=jnp.float32).astype(attn_ref.dtype)
-    dv_ref[...] = lax.dot_general(probs_b, up, tn, preferred_element_type=jnp.float32)
+    n_local = dk_ref.shape[0]
+    dv = lax.dot_general(probs_b, up, tn, preferred_element_type=jnp.float32)
+    dv_ref[...] = dv[:n_local]
+    dg_ref[1] = dv[n_local:]
     dprobs = lax.dot_general(up, v, nt, preferred_element_type=jnp.float32)
     rowdot = jnp.sum(probs * dprobs, axis=-1, keepdims=True)
     dscores = (scale * probs * (dprobs - rowdot)).astype(jnp.bfloat16)
     dq_ref[...] = jnp.dot(dscores, k, preferred_element_type=jnp.float32).astype(dq_ref.dtype)
-    dk_ref[...] = lax.dot_general(dscores, q, tn, preferred_element_type=jnp.float32)
-
-def attention(live, q, k, v, up, heads):
+    dk = lax.dot_general(dscores, q, tn, preferred_element_type=jnp.float32)
+    dk_ref[...] = dk[:n_local]
+    dg_ref[0] = dk[n_local:]
+
+def attention(live, q, k, v, up, heads, local_n):
     rows, features = q.shape
     keys_n = k.shape[0]
     hd = features // heads
     qspec = pl.BlockSpec((rows, hd), lambda h: (0, h))
     kspec = pl.BlockSpec((keys_n, hd), lambda h: (0, h))
+    lspec = pl.BlockSpec((local_n, hd), lambda h: (0, h))
+    gspec = pl.BlockSpec((2, keys_n - local_n, hd), lambda h: (0, 0, h))
     return pl.pallas_call(
         _attn_kernel,
         grid=(heads,),
         in_specs=[pl.BlockSpec((1, keys_n), lambda h: (0, 0)), qspec, kspec, kspec, qspec],
-        out_specs=[qspec, qspec, kspec, kspec],
+        out_specs=[qspec, qspec, lspec, lspec, gspec],
         out_shape=[
             jax.ShapeDtypeStruct((rows, features), jnp.bfloat16),
             jax.ShapeDtypeStruct((rows, features), jnp.bfloat16),
-            jax.ShapeDtypeStruct((keys_n, features), jnp.float32),
-            jax.ShapeDtypeStruct((keys_n, features), jnp.float32),
+            jax.ShapeDtypeStruct((local_n, features), jnp.float32),
+            jax.ShapeDtypeStruct((local_n, features), jnp.float32),
+            jax.ShapeDtypeStruct((2, keys_n - local_n, features), jnp.float32),
         ],
     )(live, q, k, v, up)
 
@@ -168,7 +176,7 @@
         live_rows = jnp.repeat(live[b], BLK).astype(jnp.float32)[None]
         q = query[b * BLK : (b + 1) * BLK]
         up = upstream[b * BLK : (b + 1) * BLK]
-        attn, dq, dk, dv = attention(live_rows, q, chosen[0], chosen[1], up, H)
+        attn, dq, dk, dv, dg = attention(live_rows, q, chosen[0], chosen[1], up, H, n_local * BLK)
         attn_rows.append(attn)
         dq_rows.append(dq)
         for side, grad in enumerate((dk, dv)):
@@ -179,11 +187,7 @@
                 grad_ext[side] = lax.dynamic_update_slice_in_dim(
                     grad_ext[side], cur + term, start, axis=0
                 )
-        terms = jnp.stack(
-            [dk[n_local * BLK :].reshape(slots, BLK, feature_count),
-             dv[n_local * BLK :].reshape(slots, BLK, feature_count)],
-            axis=1,
-        )
+        terms = dg
         global_local = terms if global_local is None else global_local + terms
     grad_ext = jnp.stack(grad_ext)
     global_total = butterfly_sum(global_local, jnp.bfloat16)
@@ -210,7 +214,7 @@
         own = own + from_next[side, : blocks_dev * BLK].astype(jnp.float32)
         for g in range(slots):
             start = (global_blocks[g] % blocks_dev) * BLK
-            total = global_total[g, side]
+            total = global_total[side, g * BLK : (g + 1) * BLK]
             add = jnp.where(owners[g] == device, total, jnp.zeros_like(total))
             cur = lax.dynamic_slice_in_dim(own, start, BLK, axis=0)
             own = lax.dynamic_update_slice_in_dim(own, cur + add, start, axis=0)

time: 247 us -> 245 us (level)
  waiting for transfers between devices: 83.5 us -> 86.4 us
  local copies, waits for them, and re-layouts: 19.1 us -> 16.3 us
    dynamic_update_slice x11, other arithmetic: 9.1 us -> 6.08 us  [local(): lax.dynamic_update_slice_in_dim(grad_ext[side], cur + term, start, axis=0)]
    slice x2 -> x0, local copies, waits for them, and re-layouts: 2.59 us -> none  [the longest x1 1.3 us: local(): dv[n_local * BLK:].reshape(slots, BLK, feature_count)]
  transfers between devices with their start and end apart: 24 -> 24, of which waited for: 15 -> 15; matrix products, arithmetic and copies ran while one was open for 22% -> 20% of each run, Pallas kernels for 5% -> 5%
where the time goes in v13:
time: 245 us; the launch traced here: 244 us
  waiting for transfers between devices  86.4 us (35%)
  starting transfers between devices  72.9 us (30%)
  other arithmetic  22.7 us (9%)
  between operations  17.9 us (7%)
  local copies, waits for them, and re-layouts  16.3 us (7%)
  matrix products  15.5 us (6%)
  Pallas kernels  12.4 us (5%)
    ppermute x12, waiting for transfers between devices, xor_swap(): return lax.ppermute(x, 'chip', [(i, i ^ m) for i in range(n)])  47.2 us
    ppermute x12, starting transfers between devices, xor_swap(): return lax.ppermute(x, 'chip', [(i, i ^ m) for i in range(n)])  42.6 us
    all_to_all x1, waiting for transfers between devices, local(): lax.all_to_all(attn_out.reshape(tok_rows, count, w_rows), SEQ, 1, 0, tile...  17.3 us
    pallas_call x1, Pallas kernels, attention(): pl.pallas_call(_attn_kernel, grid=(heads,), in_specs=[pl.BlockSpec((1, ke...  12.4 us
    ppermute x2, waiting for transfers between devices, halo(): after = lax.ppermute(shard, SEQ, down)  9.58 us
    ppermute x2, starting transfers between devices, halo(): before = lax.ppermute(shard, SEQ, up)  8.05 us
    all_to_all x1, waiting for transfers between devices, local(): lax.all_to_all(upstream_cols.reshape(count, tok_rows, w_rows), SEQ, 0, 0,...  7.61 us
    all_to_all x1, starting transfers between devices, local(): lax.all_to_all(upstream_cols.reshape(count, tok_rows, w_rows), SEQ, 0, 0,...  6.82 us
  transfers between devices with their start and end apart: 24, of which 15 were waited for; matrix products, arithmetic and copies ran while one was open for 20% of the time, Pallas kernels for 5%

profile of v13, /device:TPU:11, one launch (start us, length us, event | category | flops | bytes accessed | tf_op | source)
XLA Modules:
  0.0 244.0 jit_solution(11691680960905655603)
XLA Ops:
  8.0 1.3 fusion.35
  10.6 1.9 broadcast_select_fusion.2
  12.5 3.7 %collective-permute-start = (bf16[2,128,1024]{2,1,0:T(8,128)(2,1)}, bf16[2,128,1024]{2,1,0:T(8,128)(2,1)S(1)}, u32[]{:S(2)}, u32[]{:S(2)}) collective-permute-start(bf16[2,128,1024]{2,1,0:T(8,128)(2,1)} %get-tuple-element.30), channel_id=1, source_target_pairs={{0,1},{1,2},{2,3},{3,4},{4,5},{5,6},{6,7},{7,8},{8,9},{9,10},{10,1... | collective-permute-start | bytes 1572872 | tf_op jit(solution)/shard_map/ppermute | solution.py:62
  16.2 1.9 collective-permute-start.1
  19.2 1.5 collective-permute-start.2
  24.5 4.1 %collective-permute-done = bf16[2,128,1024]{2,1,0:T(8,128)(2,1)S(1)} collective-permute-done((bf16[2,128,1024]{2,1,0:T(8,128)(2,1)}, bf16[2,128,1024]{2,1,0:T(8,128)(2,1)S(1)}, u32[]{:S(2)}, u32[]{:S(2)}) %collective-permute-start) | collective-permute-done | bytes 524320 | tf_op jit(solution)/shard_map/ppermute | solution.py:62
  28.6 9.6 %collective-permute-done.1 = bf16[2,128,1024]{2,1,0:T(8,128)(2,1)S(1)} collective-permute-done((bf16[2,128,1024]{2,1,0:T(8,128)(2,1)}, bf16[2,128,1024]{2,1,0:T(8,128)(2,1)S(1)}, u32[]{:S(2)}, u32[]{:S(2)}) %collective-permute-start.1) | collective-permute-done | bytes 524320 | tf_op jit(solution)/shard_map/ppermute | solution.py:63
  40.2 5.2 %collective-permute-done.4 = bf16[2,32768]{1,0:T(2,128)(2,1)S(1)} collective-permute-done((bf16[2,32768]{1,0:T(2,128)(2,1)S(1)}, bf16[2,32768]{1,0:T(2,128)(2,1)S(1)}, u32[]{:S(2)}, u32[]{:S(2)}) %collective-permute-start.4) | collective-permute-done | bytes 131104 | tf_op jit(solution)/shard_map/ppermute | solution.py:28
  45.9 1.9 collective-permute-start.5
  47.8 2.9 %collective-permute-done.5 = bf16[1,32768]{1,0:T(2,128)(2,1)S(1)} collective-permute-done((bf16[1,32768]{1,0:T(2,128)(2,1)S(1)}, bf16[1,32768]{1,0:T(2,128)(2,1)S(1)}, u32[]{:S(2)}, u32[]{:S(2)}) %collective-permute-start.5) | collective-permute-done | bytes 65568 | tf_op jit(solution)/shard_map/ppermute | solution.py:28
  51.0 1.8 collective-permute-start.6
  52.9 14.2 %collective-permute-done.6 = bf16[1,32768]{1,0:T(2,128)(2,1)S(1)} collective-permute-done((bf16[1,32768]{1,0:T(2,128)(2,1)S(1)}, bf16[1,32768]{1,0:T(2,128)(2,1)S(1)}, u32[]{:S(2)}, u32[]{:S(2)}) %collective-permute-start.6) | collective-permute-done | bytes 65568 | tf_op jit(solution)/shard_map/ppermute | solution.py:28
  67.7 1.9 collective-permute-start.7
  69.6 5.5 %collective-permute-done.7 = bf16[2,32768]{1,0:T(2,128)(2,1)S(1)} collective-permute-done((bf16[2,32768]{1,0:T(2,128)(2,1)S(1)}, bf16[2,32768]{1,0:T(2,128)(2,1)S(1)}, u32[]{:S(2)}, u32[]{:S(2)}) %collective-permute-start.7) | collective-permute-done | bytes 131104 | tf_op jit(solution)/shard_map/ppermute | solution.py:28
  75.6 22.8 %collective-permute-start.8 = (bf16[4,32768]{1,0:T(4,128)(2,1)S(1)}, bf16[4,32768]{1,0:T(4,128)(2,1)S(1)}, u32[]{:S(2)}, u32[]{:S(2)}) collective-permute-start(bf16[4,32768]{1,0:T(4,128)(2,1)S(1)} %maximum_select_fusion.4), channel_id=1, source_target_pairs={{0,2},{2,0},{4,6},{6,4},{8,10},{10,8},{12,14},{14,12},{1,3},{3,1},... | collective-permute-start | bytes 786440 | tf_op jit(solution)/shard_map/ppermute | solution.py:28
  98.5 1.4 copy-done.6
  99.9 4.2 %collective-permute-done.8 = bf16[4,32768]{1,0:T(4,128)(2,1)S(1)} collective-permute-done((bf16[4,32768]{1,0:T(4,128)(2,1)S(1)}, bf16[4,32768]{1,0:T(4,128)(2,1)S(1)}, u32[]{:S(2)}, u32[]{:S(2)}) %collective-permute-start.8) | collective-permute-done | bytes 262176 | tf_op jit(solution)/shard_map/ppermute | solution.py:28
  104.6 1.6 collective-permute-start.9
  106.2 6.0 %fusion = bf16[8,16,8,128]{3,2,1,0:T(8,128)(2,1)S(1)} fusion(bf16[2048,2048]{1,0:T(8,128)(2,1)} %all-gather.3.cloned.1.call-done, bf16[64,2048]{1,0:T(8,128)(2,1)S(1)} %copy-done.10), kind=kOutput, calls=%fused_computation.5 | convolution fusion | flops 537001984 | bytes 8912896 | tf_op jit(solution)/shard_map/dot_general | solution.py:156
  113.0 6.8 %all-to-all-start = ((bf16[16,128,64]{1,2,0:T(8,128)(2,1)}), bf16[16,128,64]{1,2,0:T(8,128)(2,1)S(1)}, u32[]{:S(2)}, u32[]{:S(2)}) async-start(bf16[16,128,64]{1,2,0:T(8,128)(2,1)} %bitcast.103), calls=%async_computation | async-start | bytes 524288 | tf_op jit(solution)/shard_map/all_to_all | solution.py:159
  122.3 7.6 %all-to-all-done = bf16[16,128,64]{1,2,0:T(8,128)(2,1)S(1)} async-done(((bf16[16,128,64]{1,2,0:T(8,128)(2,1)}), bf16[16,128,64]{1,2,0:T(8,128)(2,1)S(1)}, u32[]{:S(2)}, u32[]{:S(2)}) %all-to-all-start) | async-done | bytes 262176 | tf_op jit(solution)/shard_map/all_to_all | solution.py:159
  131.4 12.4 %shard_map.119 = (bf16[128,1024]{1,0:T(8,128)(2,1)}, bf16[128,1024]{1,0:T(8,128)(2,1)}, f32[768,1024]{1,0:T(8,128)}, f32[768,1024]{1,0:T(8,128)}, f32[2,256,1024]{2,1,0:T(8,128)}) custom-call(f32[1,1024]{1,0:T(1,128)} %bitcast.113, bf16[128,1024]{1,0:T(8,128)(2,1)} %q_ref.1, bf16[1024,1024]{1,0:T(8,128)(2,1)} %get-tuple-element.22.k_ref, ...), custom_call_target="tpu_custom_call" | custom-call | tf_op jit(solution)/shard_map/pallas_call | solution.py:102
  143.8 2.9 %slice_select_fusion.2 = f32[1,256,1024]{2,1,0:T(8,128)} fusion(f32[2,256,1024]{2,1,0:T(8,128)} %get-tuple-element.14, pred[]{:T(512)S(6)} %eq.19), kind=kLoop, calls=%fused_computation.14 | loop fusion | flops 262144 | bytes 3145729 | tf_op jit(solution)/shard_map/jit(_where)/select_n | solution.py:43
  146.6 2.4 select_convert_fusion
  149.1 1.8 slice_select_fusion
  151.9 2.4 select_n.304
  154.3 2.1 convert_element_type.104
  156.7 1.2 fusion.7
  157.9 1.2 fusion.6
  159.4 1.7 collective-permute-start.13
  161.6 5.9 %collective-permute-done.13 = bf16[4,32768]{1,0:T(4,128)(2,1)S(1)} collective-permute-done((bf16[4,32768]{1,0:T(4,128)(2,1)S(1)}, bf16[4,32768]{1,0:T(4,128)(2,1)S(1)}, u32[]{:S(2)}, u32[]{:S(2)}) %collective-permute-start.13) | collective-permute-done | bytes 262176 | tf_op jit(solution)/shard_map/ppermute | solution.py:28
  167.8 1.4 collective-permute-start.14
  169.2 1.1 bitcast_dynamic-update-slice_fusion.1
  170.3 1.3 collective-permute-done.14
  172.1 1.5 collective-permute-start.15
  173.6 3.3 %collective-permute-done.15 = bf16[1,32768]{1,0:T(2,128)(2,1)S(1)} collective-permute-done((bf16[1,32768]{1,0:T(2,128)(2,1)S(1)}, bf16[1,32768]{1,0:T(2,128)(2,1)S(1)}, u32[]{:S(2)}, u32[]{:S(2)}) %collective-permute-start.15) | collective-permute-done | bytes 65568 | tf_op jit(solution)/shard_map/ppermute | solution.py:28
  177.2 3.2 %collective-permute-start.16 = (bf16[1,32768]{1,0:T(2,128)(2,1)S(1)}, bf16[1,32768]{1,0:T(2,128)(2,1)S(1)}, u32[]{:S(2)}, u32[]{:S(2)}) collective-permute-start(bf16[1,32768]{1,0:T(2,128)(2,1)S(1)} %fusion.29), channel_id=1, source_target_pairs={{0,8},{2,10},{4,12},{6,14},{8,0},{10,2},{12,4},{14,6},{1,9},{3,11}... | collective-permute-start | bytes 196616 | tf_op jit(solution)/shard_map/ppermute | solution.py:28
  180.6 3.1 %collective-permute-done.16 = bf16[1,32768]{1,0:T(2,128)(2,1)S(1)} collective-permute-done((bf16[1,32768]{1,0:T(2,128)(2,1)S(1)}, bf16[1,32768]{1,0:T(2,128)(2,1)S(1)}, u32[]{:S(2)}, u32[]{:S(2)}) %collective-permute-start.16) | collective-permute-done | bytes 65568 | tf_op jit(solution)/shard_map/ppermute | solution.py:28
  184.3 4.5 %collective-permute-start.17 = (bf16[2,32768]{1,0:T(2,128)(2,1)S(1)}, bf16[2,32768]{1,0:T(2,128)(2,1)S(1)}, u32[]{:S(2)}, u32[]{:S(2)}) collective-permute-start(bf16[2,32768]{1,0:T(2,128)(2,1)S(1)} %broadcast_select_fusion.11), channel_id=1, source_target_pairs={{0,4},{2,6},{4,0},{6,2},{8,12},{10,14},{12,8},{14,10},{1,5},{3,7},... | collective-permute-start | bytes 393224 | tf_op jit(solution)/shard_map/ppermute | solution.py:28
  188.9 4.4 %collective-permute-start.10 = (bf16[2,256,1024]{2,1,0:T(8,128)(2,1)S(1)}, bf16[2,256,1024]{2,1,0:T(8,128)(2,1)}, u32[]{:S(2)}, u32[]{:S(2)}) collective-permute-start(bf16[2,256,1024]{2,1,0:T(8,128)(2,1)S(1)} %pad_maximum_fusion.2), channel_id=1, source_target_pairs={{0,1},{1,2},{2,3},{3,4},{4,5},{5,6},{6,7},{7,8},{8,9},{9,10},{10,1... | collective-permute-start | bytes 3145736 | tf_op jit(solution)/shard_map/ppermute | solution.py:62
  193.3 1.9 collective-permute-start.11
  196.1 5.2 %all-to-all-start.1 = ((bf16[1,128,16,64]{1,3,0,2:T(8,128)(2,1)}), bf16[1,128,16,64]{1,3,0,2:T(8,128)(2,1)S(1)}, u32[]{:S(2)}, u32[]{:S(2)}) async-start(bf16[1,128,16,64]{1,3,0,2:T(8,128)(2,1)} %bitcast.33), calls=%async_computation.1 | async-start | bytes 524288 | tf_op jit(solution)/shard_map/all_to_all | solution.py:199
  201.8 1.2 collective-permute-start.18
  203.1 3.7 %convolution_convert_fusion = bf16[128,2048]{1,0:T(8,128)(2,1)} fusion(bf16[128,1024]{1,0:T(8,128)(2,1)S(1)} %copy-done.11, bf16[1024,2048]{1,0:T(8,128)(2,1)} %all-gather.5.cloned.1.call-done), kind=kOutput, calls=%fused_computation | convolution fusion | flops 537133056 | bytes 4980736 | tf_op jit(solution)/shard_map/dot_general | solution.py:196
  206.8 17.3 %all-to-all-done.1 = bf16[1,128,16,64]{1,3,0,2:T(8,128)(2,1)S(1)} async-done(((bf16[1,128,16,64]{1,3,0,2:T(8,128)(2,1)}), bf16[1,128,16,64]{1,3,0,2:T(8,128)(2,1)S(1)}, u32[]{:S(2)}, u32[]{:S(2)}) %all-to-all-start.1) | async-done | bytes 262176 | tf_op jit(solution)/shard_map/all_to_all | solution.py:199
  225.1 2.8 %collective-permute-start.19 = (bf16[8,32768]{1,0:T(8,128)(2,1)S(1)}, bf16[8,32768]{1,0:T(8,128)(2,1)S(1)}, u32[]{:S(2)}, u32[]{:S(2)}) collective-permute-start(bf16[8,32768]{1,0:T(8,128)(2,1)S(1)} %maximum_select_fusion.3), channel_id=1, source_target_pairs={{0,1},{1,0},{2,3},{3,2},{4,5},{5,4},{6,7},{7,6},{8,9},{9,8},{10,11... | collective-permute-start | bytes 1572872 | tf_op jit(solution)/shard_map/ppermute | solution.py:25
  227.9 5.7 %fusion.16 = f32[64,2048]{1,0:T(8,128)} fusion(bf16[2048,2048]{1,0:T(8,128)(2,1)} %all-gather.3.cloned.1.call-done, bf16[8,8,16,128]{3,2,1,0:T(8,128)(2,1)S(1)} %bitcast.110), kind=kOutput, calls=%fused_computation.50 | convolution fusion | flops 536870912 | bytes 9175040 | tf_op jit(solution)/shard_map/dot_general | solution.py:202
  234.4 2.8 %fusion.15 = (bf16[128,1024]{1,0:T(8,128)(2,1)}, bf16[128,1024]{1,0:T(8,128)(2,1)}) fusion(f32[1,384,1024]{2,1,0:T(8,128)} %copy-done, bf16[2,256,1024]{2,1,0:T(8,128)(2,1)S(1)} %select_n.316, bf16[2,256,1024]{2,1,0:T(8,128)(2,1)} %collective-permute-done.11, bf16[2,256,1024]{2,1,0:T(8,128)(2,1)} %collective-permute-done.10, pred[]{:T(512)S(6)} %eq.23, ...), kind=kLoop, calls=%fused_computation.49 | loop fusion | flops 2883584 | bytes 3670018 | tf_op jit(solution)/shard_map/convert_element_type | solution.py:221
  (108 shorter events, 19.7 us)
Async XLA Ops:
  7.2 13.6 %copy-start.13 = (s32[1,3]{1,0:T(1,128)S(1)}, s32[1,3]{1,0:T(1,128)}, u32[]{:S(2)}) copy-start(s32[1,3]{1,0:T(1,128)} %param.14) | copy-start | bytes 40
  7.2 99.0 %all-gather.3.cloned.1.call-start = ((), (), s32[]{:S(2)}) async-start(), calls=%async_computation.2 | async-start | bytes 8912896 | tf_op jit(solution)/shard_map/all_gather | solution.py:125
  7.9 195.1 %all-gather.5.cloned.1.call-start = ((), (), s32[]{:S(2)}) async-start(), calls=%async_computation.3 | async-start | bytes 4456448 | tf_op jit(solution)/shard_map/all_gather | solution.py:126
  10.6 13.0 %copy-start.14 = (s32[3]{0:T(128)S(1)}, s32[3]{0:T(128)}, u32[]{:S(2)}) copy-start(s32[3]{0:T(128)} %constant.85.clone) | copy-start | bytes 40
  12.5 16.0 %collective-permute-start = (bf16[2,128,1024]{2,1,0:T(8,128)(2,1)}, bf16[2,128,1024]{2,1,0:T(8,128)(2,1)S(1)}, u32[]{:S(2)}, u32[]{:S(2)}) collective-permute-start(bf16[2,128,1024]{2,1,0:T(8,128)(2,1)} %get-tuple-element.30), channel_id=1, source_target_pairs={{0,1},{1,2},{2,3},{3,4},{4,5},{5,6},{6,7},{7,8},{8,9},{9,10},{10,1... | collective-permute-start | bytes 1572872 | tf_op jit(solution)/shard_map/ppermute | solution.py:62
  16.2 21.9 %collective-permute-start.1 = (bf16[2,128,1024]{2,1,0:T(8,128)(2,1)}, bf16[2,128,1024]{2,1,0:T(8,128)(2,1)S(1)}, u32[]{:S(2)}, u32[]{:S(2)}) collective-permute-start(bf16[2,128,1024]{2,1,0:T(8,128)(2,1)} %get-tuple-element.30), channel_id=1, source_target_pairs={{1,0},{2,1},{3,2},{4,3},{5,4},{6,5},{7,6},{8,7},{9,8},{10,9},{11,1... | collective-permute-start | bytes 1572872 | tf_op jit(solution)/shard_map/ppermute | solution.py:63
  19.2 19.0 %copy-start.8 = (bf16[128,1024]{1,0:T(8,128)(2,1)S(1)}, bf16[128,1024]{1,0:T(8,128)(2,1)}, u32[]{:S(2)}) copy-start(bf16[128,1024]{1,0:T(8,128)(2,1)} %param.10) | copy-start | bytes 786436
  19.2 19.0 %copy-start.9 = (bf16[128,1024]{1,0:T(8,128)(2,1)S(1)}, bf16[128,1024]{1,0:T(8,128)(2,1)}, u32[]{:S(2)}) copy-start(bf16[128,1024]{1,0:T(8,128)(2,1)} %param.9) | copy-start | bytes 786436
  19.2 4.5 %collective-permute-start.2 = (bf16[8,32768]{1,0:T(8,128)(2,1)}, bf16[8,32768]{1,0:T(8,128)(2,1)S(1)}, u32[]{:S(2)}, u32[]{:S(2)}) collective-permute-start(bf16[8,32768]{1,0:T(8,128)(2,1)} %select_n.289), channel_id=1, source_target_pairs={{0,1},{1,0},{2,3},{3,2},{4,5},{5,4},{6,7},{7,6},{8,9},{9,8},{10,11... | collective-permute-start | bytes 1572872 | tf_op jit(solution)/shard_map/ppermute | solution.py:25
  24.1 15.3 %collective-permute-start.3 = (bf16[4,32768]{1,0:T(4,128)(2,1)S(1)}, bf16[4,32768]{1,0:T(4,128)(2,1)S(1)}, u32[]{:S(2)}, u32[]{:S(2)}) collective-permute-start(bf16[4,32768]{1,0:T(4,128)(2,1)S(1)} %broadcast_select_fusion.4), channel_id=1, source_target_pairs={{0,2},{2,0},{4,6},{6,4},{8,10},{10,8},{12,14},{14,12},{1,3},{3,1},... | collective-permute-start | bytes 786440 | tf_op jit(solution)/shard_map/ppermute | solution.py:28
  39.9 5.6 %collective-permute-start.4 = (bf16[2,32768]{1,0:T(2,128)(2,1)S(1)}, bf16[2,32768]{1,0:T(2,128)(2,1)S(1)}, u32[]{:S(2)}, u32[]{:S(2)}) collective-permute-start(bf16[2,32768]{1,0:T(2,128)(2,1)S(1)} %broadcast_select_fusion.5), channel_id=1, source_target_pairs={{0,4},{2,6},{4,0},{6,2},{8,12},{10,14},{12,8},{14,10},{1,5},{3,7},... | collective-permute-start | bytes 393224 | tf_op jit(solution)/shard_map/ppermute | solution.py:28
  45.9 4.8 %collective-permute-start.5 = (bf16[1,32768]{1,0:T(2,128)(2,1)S(1)}, bf16[1,32768]{1,0:T(2,128)(2,1)S(1)}, u32[]{:S(2)}, u32[]{:S(2)}) collective-permute-start(bf16[1,32768]{1,0:T(2,128)(2,1)S(1)} %broadcast_select_fusion.9), channel_id=1, source_target_pairs={{0,8},{2,10},{4,12},{6,14},{8,0},{10,2},{12,4},{14,6},{1,9},{3,11}... | collective-permute-start | bytes 196616 | tf_op jit(solution)/shard_map/ppermute | solution.py:28
  51.0 16.1 %collective-permute-start.6 = (bf16[1,32768]{1,0:T(2,128)(2,1)S(1)}, bf16[1,32768]{1,0:T(2,128)(2,1)S(1)}, u32[]{:S(2)}, u32[]{:S(2)}) collective-permute-start(bf16[1,32768]{1,0:T(2,128)(2,1)S(1)} %fusion.27), channel_id=1, source_target_pairs={{0,8},{2,10},{4,12},{6,14},{8,0},{10,2},{12,4},{14,6},{1,9},{3,11}... | collective-permute-start | bytes 196616 | tf_op jit(solution)/shard_map/ppermute | solution.py:28
  67.7 38.5 %copy-start.10 = (bf16[64,2048]{1,0:T(8,128)(2,1)S(1)}, bf16[64,2048]{1,0:T(8,128)(2,1)}, u32[]{:S(2)}) copy-start(bf16[64,2048]{1,0:T(8,128)(2,1)} %param.11) | copy-start | bytes 786436
  67.7 7.4 %collective-permute-start.7 = (bf16[2,32768]{1,0:T(2,128)(2,1)S(1)}, bf16[2,32768]{1,0:T(2,128)(2,1)S(1)}, u32[]{:S(2)}, u32[]{:S(2)}) collective-permute-start(bf16[2,32768]{1,0:T(2,128)(2,1)S(1)} %broadcast_select_fusion.12), channel_id=1, source_target_pairs={{0,4},{2,6},{4,0},{6,2},{8,12},{10,14},{12,8},{14,10},{1,5},{3,7},... | collective-permute-start | bytes 393224 | tf_op jit(solution)/shard_map/ppermute | solution.py:28
  75.6 28.5 %collective-permute-start.8 = (bf16[4,32768]{1,0:T(4,128)(2,1)S(1)}, bf16[4,32768]{1,0:T(4,128)(2,1)S(1)}, u32[]{:S(2)}, u32[]{:S(2)}) collective-permute-start(bf16[4,32768]{1,0:T(4,128)(2,1)S(1)} %maximum_select_fusion.4), channel_id=1, source_target_pairs={{0,2},{2,0},{4,6},{6,4},{8,10},{10,8},{12,14},{14,12},{1,3},{3,1},... | collective-permute-start | bytes 786440 | tf_op jit(solution)/shard_map/ppermute | solution.py:28
  98.5 5.6 %copy-start.7 = (bf16[1024,1024]{1,0:T(8,128)(2,1)}, bf16[1024,1024]{1,0:T(8,128)(2,1)S(1)}, u32[]{:S(2)}) copy-start(bf16[1024,1024]{1,0:T(8,128)(2,1)S(1)} %bitcast_dynamic-update-slice_fusion.5) | copy-start | bytes 6291460
  98.5 1.4 copy-start.6
  104.6 15.3 %collective-permute-start.9 = (bf16[8,32768]{1,0:T(8,128)(2,1)S(1)}, bf16[8,32768]{1,0:T(8,128)(2,1)S(1)}, u32[]{:S(2)}, u32[]{:S(2)}) collective-permute-start(bf16[8,32768]{1,0:T(8,128)(2,1)S(1)} %maximum_select_fusion.2), channel_id=1, source_target_pairs={{0,1},{1,0},{2,3},{3,2},{4,5},{5,4},{6,7},{7,6},{8,9},{9,8},{10,11... | collective-permute-start | bytes 1572872 | tf_op jit(solution)/shard_map/ppermute | solution.py:25
  113.0 16.8 %all-to-all-start = ((bf16[16,128,64]{1,2,0:T(8,128)(2,1)}), bf16[16,128,64]{1,2,0:T(8,128)(2,1)S(1)}, u32[]{:S(2)}, u32[]{:S(2)}) async-start(bf16[16,128,64]{1,2,0:T(8,128)(2,1)} %bitcast.103), calls=%async_computation | async-start | bytes 524288 | tf_op jit(solution)/shard_map/all_to_all | solution.py:159
  143.7 5.3 %copy-start.2 = (f32[768,1024]{1,0:T(8,128)S(1)}, f32[768,1024]{1,0:T(8,128)}, u32[]{:S(2)}) copy-start(f32[768,1024]{1,0:T(8,128)} %get-tuple-element.13) | copy-start | bytes 9437188
  143.8 5.3 %copy-start.12 = (pred[384]{0:T(512)(128)(4,1)S(1)}, pred[384]{0:T(512)(128)(4,1)}, u32[]{:S(2)}) copy-start(pred[384]{0:T(512)(128)(4,1)} %constant.107) | copy-start | bytes 1156
  149.1 2.4 copy-start.4
  156.4 2.7 %copy-start.5 = (f32[8,32768]{1,0:T(8,128)S(1)}, f32[8,32768]{1,0:T(8,128)}, u32[]{:S(2)}) copy-start(f32[8,32768]{1,0:T(8,128)} %select_n.304) | copy-start | bytes 3145732
  156.4 2.7 %collective-permute-start.12 = (bf16[8,32768]{1,0:T(8,128)(2,1)}, bf16[8,32768]{1,0:T(8,128)(2,1)S(1)}, u32[]{:S(2)}, u32[]{:S(2)}) collective-permute-start(bf16[8,32768]{1,0:T(8,128)(2,1)} %convert_element_type.104), channel_id=1, source_target_pairs={{0,1},{1,0},{2,3},{3,2},{4,5},{5,4},{6,7},{7,6},{8,9},{9,8},{10,11... | collective-permute-start | bytes 1572872 | tf_op jit(solution)/shard_map/ppermute | solution.py:25
  159.1 2.0 copy-start.3
  159.4 8.0 %collective-permute-start.13 = (bf16[4,32768]{1,0:T(4,128)(2,1)S(1)}, bf16[4,32768]{1,0:T(4,128)(2,1)S(1)}, u32[]{:S(2)}, u32[]{:S(2)}) collective-permute-start(bf16[4,32768]{1,0:T(4,128)(2,1)S(1)} %select_convert_fusion.1), channel_id=1, source_target_pairs={{0,2},{2,0},{4,6},{6,4},{8,10},{10,8},{12,14},{14,12},{1,3},{3,1},... | collective-permute-start | bytes 786440 | tf_op jit(solution)/shard_map/ppermute | solution.py:28
  167.8 3.9 %collective-permute-start.14 = (bf16[2,32768]{1,0:T(2,128)(2,1)S(1)}, bf16[2,32768]{1,0:T(2,128)(2,1)S(1)}, u32[]{:S(2)}, u32[]{:S(2)}) collective-permute-start(bf16[2,32768]{1,0:T(2,128)(2,1)S(1)} %select_convert_fusion.2), channel_id=1, source_target_pairs={{0,4},{2,6},{4,0},{6,2},{8,12},{10,14},{12,8},{14,10},{1,5},{3,7},... | collective-permute-start | bytes 393224 | tf_op jit(solution)/shard_map/ppermute | solution.py:28
  170.3 10.2 %copy-start.1 = (f32[1,384,1024]{2,1,0:T(8,128)}, f32[1,384,1024]{2,1,0:T(8,128)S(1)}, u32[]{:S(2)}) copy-start(f32[1,384,1024]{2,1,0:T(8,128)S(1)} %bitcast_dynamic-update-slice_fusion.1) | copy-start | bytes 4718596
  172.1 4.9 %collective-permute-start.15 = (bf16[1,32768]{1,0:T(2,128)(2,1)S(1)}, bf16[1,32768]{1,0:T(2,128)(2,1)S(1)}, u32[]{:S(2)}, u32[]{:S(2)}) collective-permute-start(bf16[1,32768]{1,0:T(2,128)(2,1)S(1)} %fusion.30), channel_id=1, source_target_pairs={{0,8},{2,10},{4,12},{6,14},{8,0},{10,2},{12,4},{14,6},{1,9},{3,11}... | collective-permute-start | bytes 196616 | tf_op jit(solution)/shard_map/ppermute | solution.py:28
  173.6 6.9 %copy-start = (f32[1,384,1024]{2,1,0:T(8,128)}, f32[1,384,1024]{2,1,0:T(8,128)S(1)}, u32[]{:S(2)}) copy-start(f32[1,384,1024]{2,1,0:T(8,128)S(1)} %bitcast_dynamic-update-slice_fusion) | copy-start | bytes 4718596
  177.2 6.5 %collective-permute-start.16 = (bf16[1,32768]{1,0:T(2,128)(2,1)S(1)}, bf16[1,32768]{1,0:T(2,128)(2,1)S(1)}, u32[]{:S(2)}, u32[]{:S(2)}) collective-permute-start(bf16[1,32768]{1,0:T(2,128)(2,1)S(1)} %fusion.29), channel_id=1, source_target_pairs={{0,8},{2,10},{4,12},{6,14},{8,0},{10,2},{12,4},{14,6},{1,9},{3,11}... | collective-permute-start | bytes 196616 | tf_op jit(solution)/shard_map/ppermute | solution.py:28
  180.6 14.6 %copy-start.11 = (bf16[128,1024]{1,0:T(8,128)(2,1)S(1)}, bf16[128,1024]{1,0:T(8,128)(2,1)}, u32[]{:S(2)}) copy-start(bf16[128,1024]{1,0:T(8,128)(2,1)} %get-tuple-element.10) | copy-start | bytes 786436
  184.3 17.0 %collective-permute-start.17 = (bf16[2,32768]{1,0:T(2,128)(2,1)S(1)}, bf16[2,32768]{1,0:T(2,128)(2,1)S(1)}, u32[]{:S(2)}, u32[]{:S(2)}) collective-permute-start(bf16[2,32768]{1,0:T(2,128)(2,1)S(1)} %broadcast_select_fusion.11), channel_id=1, source_target_pairs={{0,4},{2,6},{4,0},{6,2},{8,12},{10,14},{12,8},{14,10},{1,5},{3,7},... | collective-permute-start | bytes 393224 | tf_op jit(solution)/shard_map/ppermute | solution.py:28
  188.9 45.5 %collective-permute-start.10 = (bf16[2,256,1024]{2,1,0:T(8,128)(2,1)S(1)}, bf16[2,256,1024]{2,1,0:T(8,128)(2,1)}, u32[]{:S(2)}, u32[]{:S(2)}) collective-permute-start(bf16[2,256,1024]{2,1,0:T(8,128)(2,1)S(1)} %pad_maximum_fusion.2), channel_id=1, source_target_pairs={{0,1},{1,2},{2,3},{3,4},{4,5},{5,6},{6,7},{7,8},{8,9},{9,10},{10,1... | collective-permute-start | bytes 3145736 | tf_op jit(solution)/shard_map/ppermute | solution.py:62
  193.3 41.1 %collective-permute-start.11 = (bf16[2,256,1024]{2,1,0:T(8,128)(2,1)S(1)}, bf16[2,256,1024]{2,1,0:T(8,128)(2,1)}, u32[]{:S(2)}, u32[]{:S(2)}) collective-permute-start(bf16[2,256,1024]{2,1,0:T(8,128)(2,1)S(1)} %pad_maximum_fusion.2), channel_id=1, source_target_pairs={{1,0},{2,1},{3,2},{4,3},{5,4},{6,5},{7,6},{8,7},{9,8},{10,9},{11,1... | collective-permute-start | bytes 3145736 | tf_op jit(solution)/shard_map/ppermute | solution.py:63
  196.1 27.9 %all-to-all-start.1 = ((bf16[1,128,16,64]{1,3,0,2:T(8,128)(2,1)}), bf16[1,128,16,64]{1,3,0,2:T(8,128)(2,1)S(1)}, u32[]{:S(2)}, u32[]{:S(2)}) async-start(bf16[1,128,16,64]{1,3,0,2:T(8,128)(2,1)} %bitcast.33), calls=%async_computation.1 | async-start | bytes 524288 | tf_op jit(solution)/shard_map/all_to_all | solution.py:199
  201.8 22.9 %collective-permute-start.18 = (bf16[4,32768]{1,0:T(4,128)(2,1)S(1)}, bf16[4,32768]{1,0:T(4,128)(2,1)S(1)}, u32[]{:S(2)}, u32[]{:S(2)}) collective-permute-start(bf16[4,32768]{1,0:T(4,128)(2,1)S(1)} %maximum_select_fusion.5), channel_id=1, source_target_pairs={{0,2},{2,0},{4,6},{6,4},{8,10},{10,8},{12,14},{14,12},{1,3},{3,1},... | collective-permute-start | bytes 786440 | tf_op jit(solution)/shard_map/ppermute | solution.py:28
  225.1 8.5 %collective-permute-start.19 = (bf16[8,32768]{1,0:T(8,128)(2,1)S(1)}, bf16[8,32768]{1,0:T(8,128)(2,1)S(1)}, u32[]{:S(2)}, u32[]{:S(2)}) collective-permute-start(bf16[8,32768]{1,0:T(8,128)(2,1)S(1)} %maximum_select_fusion.3), channel_id=1, source_target_pairs={{0,1},{1,0},{2,3},{3,2},{4,5},{5,4},{6,7},{7,6},{8,9},{9,8},{10,11... | collective-permute-start | bytes 1572872 | tf_op jit(solution)/shard_map/ppermute | solution.py:25
Sparse Core Ops, SparseCore 0:
  10.2 85.8 all-gather.2
  98.2 60.5 all-gather.4

commit v14 on v13

--- a/solution.py
+++ b/solution.py
@@ -37,10 +37,9 @@
     parts = flat
     for k in range(levels):
         half = parts.shape[0] // 2
-        lo, hi = parts[:half], parts[half:]
-        upper = ((d >> k) & 1) == 1
-        send = jnp.where(upper, lo, hi)
-        keep = jnp.where(upper, hi, lo)
+        bit = (d >> k) & 1
+        send = lax.dynamic_slice_in_dim(parts, (1 - bit) * half, half, axis=0)
+        keep = lax.dynamic_slice_in_dim(parts, bit * half, half, axis=0)
         if wire is not None:
             send = send.astype(wire)
         parts = keep + xor_swap(send, k).astype(keep.dtype)

time: 245 us -> 239 us (0.976)
  waiting for transfers between devices: 86.4 us -> 81 us
  other arithmetic: 22.7 us -> 17.7 us
  starting transfers between devices: 72.9 us -> 76.6 us
    ppermute x12, waiting for transfers between devices: 47.2 us -> 42.2 us  [xor_swap(): return lax.ppermute(x, 'chip', [(i, i ^ m) for i in range(n)])]
    select_n x5 -> x1, other arithmetic: 5.48 us -> 1.15 us  [local(): masked.append(jnp.where(owners[g] == device, block, jnp.zeros_like(block)))]
    ppermute x2, waiting for transfers between devices: 4.1 us -> 0.01 us  [halo(): before = lax.ppermute(shard, SEQ, up)]
    select_n x3 -> x0, local copies, waits for them, and re-layouts: 3.68 us -> none  [the longest x2 2.64 us: butterfly_sum(): keep = jnp.where(upper, hi, lo)]
    reshape x0 -> x2, local copies, waits for them, and re-layouts: none -> 3.31 us  [butterfly_sum(): flat = x.reshape(count, -1)]
    all_to_all x1, waiting for transfers between devices: 7.61 us -> 10.7 us  [local(): lax.all_to_all(upstream_cols.reshape(count, tok_rows, w_rows), SEQ, 0, 0,...]
    convert_element_type x4 -> x0, other arithmetic: 3 us -> none  [butterfly_sum(): send = send.astype(wire)]
  transfers between devices with their start and end apart: 24 -> 24, of which waited for: 15 -> 14; matrix products, arithmetic and copies ran while one was open for 20% -> 19% of each run, Pallas kernels for 5% -> 5%
where the time goes in v14:
time: 239 us; the launch traced here: 238 us
  waiting for transfers between devices  81 us (34%)
  starting transfers between devices  76.6 us (32%)
  between operations  17.9 us (7%)
  other arithmetic  17.7 us (7%)
  local copies, waits for them, and re-layouts  17 us (7%)
  matrix products  15.5 us (6%)
  Pallas kernels  12.3 us (5%)
    ppermute x12, starting transfers between devices, xor_swap(): return lax.ppermute(x, 'chip', [(i, i ^ m) for i in range(n)])  43.2 us
    ppermute x12, waiting for transfers between devices, xor_swap(): return lax.ppermute(x, 'chip', [(i, i ^ m) for i in range(n)])  42.2 us
    all_to_all x1, waiting for transfers between devices, local(): lax.all_to_all(attn_out.reshape(tok_rows, count, w_rows), SEQ, 1, 0, tile...  17.3 us
    pallas_call x1, Pallas kernels, attention(): pl.pallas_call(_attn_kernel, grid=(heads,), in_specs=[pl.BlockSpec((1, ke...  12.3 us
    all_to_all x1, waiting for transfers between devices, local(): lax.all_to_all(upstream_cols.reshape(count, tok_rows, w_rows), SEQ, 0, 0,...  10.7 us
    ppermute x2, waiting for transfers between devices, halo(): after = lax.ppermute(shard, SEQ, down)  10.1 us
    all_to_all x1, starting transfers between devices, local(): lax.all_to_all(upstream_cols.reshape(count, tok_rows, w_rows), SEQ, 0, 0,...  8.7 us
    ppermute x4, starting transfers between devices, xor_swap(): return lax.ppermute(x, 'core', [(i, i ^ 1) for i in range(n)])  7.86 us
  transfers between devices with their start and end apart: 24, of which 14 were waited for; matrix products, arithmetic and copies ran while one was open for 19% of the time, Pallas kernels for 5%

profile of v14, /device:TPU:11, one launch (start us, length us, event | category | flops | bytes accessed | tf_op | source)
XLA Modules:
  0.0 238.0 jit_solution(11879700832011134754)
XLA Ops:
  7.9 1.9 pad_maximum_fusion.4
  9.8 3.7 %collective-permute-start = (bf16[2,128,1024]{2,1,0:T(8,128)(2,1)}, bf16[2,128,1024]{2,1,0:T(8,128)(2,1)S(1)}, u32[]{:S(2)}, u32[]{:S(2)}) collective-permute-start(bf16[2,128,1024]{2,1,0:T(8,128)(2,1)} %pad_maximum_fusion.4), channel_id=1, source_target_pairs={{0,1},{1,2},{2,3},{3,4},{4,5},{5,6},{6,7},{7,8},{8,9},{9,10},{10,1... | collective-permute-start | bytes 1572872 | tf_op jit(solution)/shard_map/ppermute | solution.py:61
  13.5 1.9 collective-permute-start.1
  15.5 1.3 fusion.30
  18.1 1.1 broadcast_select_fusion.1
  20.8 1.5 collective-permute-start.2
  25.7 10.1 %collective-permute-done.1 = bf16[2,128,1024]{2,1,0:T(8,128)(2,1)S(1)} collective-permute-done((bf16[2,128,1024]{2,1,0:T(8,128)(2,1)}, bf16[2,128,1024]{2,1,0:T(8,128)(2,1)S(1)}, u32[]{:S(2)}, u32[]{:S(2)}) %collective-permute-start.1) | collective-permute-done | bytes 524320 | tf_op jit(solution)/shard_map/ppermute | solution.py:62
  37.3 5.6 %collective-permute-done.4 = bf16[2,32768]{1,0:T(2,128)(2,1)S(1)} collective-permute-done((bf16[2,32768]{1,0:T(2,128)(2,1)S(1)}, bf16[2,32768]{1,0:T(2,128)(2,1)S(1)}, u32[]{:S(2)}, u32[]{:S(2)}) %collective-permute-start.4) | collective-permute-done | bytes 131104 | tf_op jit(solution)/shard_map/ppermute | solution.py:28
  43.2 1.8 collective-permute-start.5
  45.1 2.9 %collective-permute-done.5 = bf16[1,32768]{1,0:T(2,128)(2,1)S(1)} collective-permute-done((bf16[1,32768]{1,0:T(2,128)(2,1)S(1)}, bf16[1,32768]{1,0:T(2,128)(2,1)S(1)}, u32[]{:S(2)}, u32[]{:S(2)}) %collective-permute-start.5) | collective-permute-done | bytes 65568 | tf_op jit(solution)/shard_map/ppermute | solution.py:28
  48.2 1.8 collective-permute-start.6
  50.0 3.1 %collective-permute-done.6 = bf16[1,32768]{1,0:T(2,128)(2,1)S(1)} collective-permute-done((bf16[1,32768]{1,0:T(2,128)(2,1)S(1)}, bf16[1,32768]{1,0:T(2,128)(2,1)S(1)}, u32[]{:S(2)}, u32[]{:S(2)}) %collective-permute-start.6) | collective-permute-done | bytes 65568 | tf_op jit(solution)/shard_map/ppermute | solution.py:28
  53.7 15.8 %collective-permute-start.7 = (bf16[2,32768]{1,0:T(2,128)(2,1)S(1)}, bf16[2,32768]{1,0:T(2,128)(2,1)S(1)}, u32[]{:S(2)}, u32[]{:S(2)}) collective-permute-start(bf16[2,32768]{1,0:T(2,128)(2,1)S(1)} %broadcast_select_fusion.3), channel_id=1, source_target_pairs={{0,4},{2,6},{4,0},{6,2},{8,12},{10,14},{12,8},{14,10},{1,5},{3,7},... | collective-permute-start | bytes 393224 | tf_op jit(solution)/shard_map/ppermute | solution.py:28
  69.6 13.0 %collective-permute-done.7 = bf16[2,32768]{1,0:T(2,128)(2,1)S(1)} collective-permute-done((bf16[2,32768]{1,0:T(2,128)(2,1)S(1)}, bf16[2,32768]{1,0:T(2,128)(2,1)S(1)}, u32[]{:S(2)}, u32[]{:S(2)}) %collective-permute-start.7) | collective-permute-done | bytes 131104 | tf_op jit(solution)/shard_map/ppermute | solution.py:28
  83.1 9.5 %collective-permute-start.8 = (bf16[4,32768]{1,0:T(4,128)(2,1)S(1)}, bf16[4,32768]{1,0:T(4,128)(2,1)S(1)}, u32[]{:S(2)}, u32[]{:S(2)}) collective-permute-start(bf16[4,32768]{1,0:T(4,128)(2,1)S(1)} %maximum_select_fusion.4), channel_id=1, source_target_pairs={{0,2},{2,0},{4,6},{6,4},{8,10},{10,8},{12,14},{14,12},{1,3},{3,1},... | collective-permute-start | bytes 786440 | tf_op jit(solution)/shard_map/ppermute | solution.py:28
  92.7 1.4 copy-done.7
  94.1 2.8 %collective-permute-done.8 = bf16[4,32768]{1,0:T(4,128)(2,1)S(1)} collective-permute-done((bf16[4,32768]{1,0:T(4,128)(2,1)S(1)}, bf16[4,32768]{1,0:T(4,128)(2,1)S(1)}, u32[]{:S(2)}, u32[]{:S(2)}) %collective-permute-start.8) | collective-permute-done | bytes 262176 | tf_op jit(solution)/shard_map/ppermute | solution.py:28
  97.3 3.1 %collective-permute-start.9 = (bf16[8,32768]{1,0:T(8,128)(2,1)S(1)}, bf16[8,32768]{1,0:T(8,128)(2,1)S(1)}, u32[]{:S(2)}, u32[]{:S(2)}) collective-permute-start(bf16[8,32768]{1,0:T(8,128)(2,1)S(1)} %maximum_select_fusion.2), channel_id=1, source_target_pairs={{0,1},{1,0},{2,3},{3,2},{4,5},{5,4},{6,7},{7,6},{8,9},{9,8},{10,11... | collective-permute-start | bytes 1572872 | tf_op jit(solution)/shard_map/ppermute | solution.py:25
  100.3 6.0 %fusion = bf16[8,16,8,128]{3,2,1,0:T(8,128)(2,1)S(1)} fusion(bf16[2048,2048]{1,0:T(8,128)(2,1)} %all-gather.3.cloned.1.call-done, bf16[64,2048]{1,0:T(8,128)(2,1)S(1)} %copy-done.9), kind=kOutput, calls=%fused_computation.5 | convolution fusion | flops 537001984 | bytes 8912896 | tf_op jit(solution)/shard_map/dot_general | solution.py:155
  107.2 8.7 %all-to-all-start = ((bf16[16,128,64]{1,2,0:T(8,128)(2,1)}), bf16[16,128,64]{1,2,0:T(8,128)(2,1)S(1)}, u32[]{:S(2)}, u32[]{:S(2)}) async-start(bf16[16,128,64]{1,2,0:T(8,128)(2,1)} %bitcast.107), calls=%async_computation | async-start | bytes 524288 | tf_op jit(solution)/shard_map/all_to_all | solution.py:158
  116.6 0.9 fusion.20
  117.4 0.8 fusion.19
  118.3 10.7 %all-to-all-done = bf16[16,128,64]{1,2,0:T(8,128)(2,1)S(1)} async-done(((bf16[16,128,64]{1,2,0:T(8,128)(2,1)}), bf16[16,128,64]{1,2,0:T(8,128)(2,1)S(1)}, u32[]{:S(2)}, u32[]{:S(2)}) %all-to-all-start) | async-done | bytes 262176 | tf_op jit(solution)/shard_map/all_to_all | solution.py:158
  129.0 0.8 copy.19.up_ref
  130.5 12.3 %shard_map.119 = (bf16[128,1024]{1,0:T(8,128)(2,1)}, bf16[128,1024]{1,0:T(8,128)(2,1)}, f32[768,1024]{1,0:T(8,128)}, f32[768,1024]{1,0:T(8,128)}, f32[2,256,1024]{2,1,0:T(8,128)}) custom-call(f32[1,1024]{1,0:T(1,128)} %bitcast.119, bf16[128,1024]{1,0:T(8,128)(2,1)} %q_ref.1, bf16[1024,1024]{1,0:T(8,128)(2,1)} %get-tuple-element.22.k_ref, ...), custom_call_target="tpu_custom_call" | custom-call | tf_op jit(solution)/shard_map/pallas_call | solution.py:101
  142.9 2.3 slice_select_fusion
  146.2 2.8 %reshape.176 = f32[16,32768]{1,0:T(8,128)} reshape(f32[2,256,1024]{2,1,0:T(8,128)} %get-tuple-element.14) | data formatting | bytes 4194304 | tf_op jit(solution)/shard_map/reshape | solution.py:35
  149.0 1.4 dynamic-slice_convert_fusion
  150.9 1.2 fusion.7
  152.1 1.3 fusion.6
  153.6 1.3 collective-permute-start.13
  155.5 6.0 %collective-permute-done.13 = bf16[4,32768]{1,0:T(4,128)(2,1)S(1)} collective-permute-done((bf16[4,32768]{1,0:T(4,128)(2,1)S(1)}, bf16[4,32768]{1,0:T(4,128)(2,1)S(1)}, u32[]{:S(2)}, u32[]{:S(2)}) %collective-permute-start.13) | collective-permute-done | bytes 262176 | tf_op jit(solution)/shard_map/ppermute | solution.py:28
  162.3 1.1 bitcast_dynamic-update-slice_fusion.1
  163.4 2.2 collective-permute-done.14
  165.9 1.3 collective-permute-start.15
  167.3 3.5 %collective-permute-done.15 = bf16[1,32768]{1,0:T(2,128)(2,1)S(1)} collective-permute-done((bf16[1,32768]{1,0:T(2,128)(2,1)S(1)}, bf16[1,32768]{1,0:T(2,128)(2,1)S(1)}, u32[]{:S(2)}, u32[]{:S(2)}) %collective-permute-start.15) | collective-permute-done | bytes 65568 | tf_op jit(solution)/shard_map/ppermute | solution.py:28
  171.0 3.1 %collective-permute-start.16 = (bf16[1,32768]{1,0:T(2,128)(2,1)S(1)}, bf16[1,32768]{1,0:T(2,128)(2,1)S(1)}, u32[]{:S(2)}, u32[]{:S(2)}) collective-permute-start(bf16[1,32768]{1,0:T(2,128)(2,1)S(1)} %add_convert_fusion), channel_id=1, source_target_pairs={{0,8},{2,10},{4,12},{6,14},{8,0},{10,2},{12,4},{14,6},{1,9},{3,11}... | collective-permute-start | bytes 196616 | tf_op jit(solution)/shard_map/ppermute | solution.py:28
  174.3 2.2 collective-permute-done.16
  177.0 6.2 %collective-permute-start.17 = (bf16[2,32768]{1,0:T(2,128)(2,1)S(1)}, bf16[2,32768]{1,0:T(2,128)(2,1)S(1)}, u32[]{:S(2)}, u32[]{:S(2)}) collective-permute-start(bf16[2,32768]{1,0:T(2,128)(2,1)S(1)} %broadcast_select_fusion.2), channel_id=1, source_target_pairs={{0,4},{2,6},{4,0},{6,2},{8,12},{10,14},{12,8},{14,10},{1,5},{3,7},... | collective-permute-start | bytes 393224 | tf_op jit(solution)/shard_map/ppermute | solution.py:28
  183.3 3.9 %collective-permute-start.10 = (bf16[2,256,1024]{2,1,0:T(8,128)(2,1)S(1)}, bf16[2,256,1024]{2,1,0:T(8,128)(2,1)}, u32[]{:S(2)}, u32[]{:S(2)}) collective-permute-start(bf16[2,256,1024]{2,1,0:T(8,128)(2,1)S(1)} %pad_maximum_fusion.3), channel_id=1, source_target_pairs={{0,1},{1,2},{2,3},{3,4},{4,5},{5,6},{6,7},{7,8},{8,9},{9,10},{10,1... | collective-permute-start | bytes 3145736 | tf_op jit(solution)/shard_map/ppermute | solution.py:61
  187.3 1.9 collective-permute-start.11
  190.1 5.3 %all-to-all-start.1 = ((bf16[1,128,16,64]{1,3,0,2:T(8,128)(2,1)}), bf16[1,128,16,64]{1,3,0,2:T(8,128)(2,1)S(1)}, u32[]{:S(2)}, u32[]{:S(2)}) async-start(bf16[1,128,16,64]{1,3,0,2:T(8,128)(2,1)} %bitcast.35), calls=%async_computation.1 | async-start | bytes 524288 | tf_op jit(solution)/shard_map/all_to_all | solution.py:198
  195.8 1.2 collective-permute-start.18
  197.1 3.7 %convolution_convert_fusion = bf16[128,2048]{1,0:T(8,128)(2,1)} fusion(bf16[128,1024]{1,0:T(8,128)(2,1)S(1)} %copy-done.10, bf16[1024,2048]{1,0:T(8,128)(2,1)} %all-gather.5.cloned.1.call-done), kind=kOutput, calls=%fused_computation | convolution fusion | flops 537133056 | bytes 4980736 | tf_op jit(solution)/shard_map/dot_general | solution.py:195
  200.8 17.3 %all-to-all-done.1 = bf16[1,128,16,64]{1,3,0,2:T(8,128)(2,1)S(1)} async-done(((bf16[1,128,16,64]{1,3,0,2:T(8,128)(2,1)}), bf16[1,128,16,64]{1,3,0,2:T(8,128)(2,1)S(1)}, u32[]{:S(2)}, u32[]{:S(2)}) %all-to-all-start.1) | async-done | bytes 262176 | tf_op jit(solution)/shard_map/all_to_all | solution.py:198
  219.1 2.8 %collective-permute-start.19 = (bf16[8,32768]{1,0:T(8,128)(2,1)S(1)}, bf16[8,32768]{1,0:T(8,128)(2,1)S(1)}, u32[]{:S(2)}, u32[]{:S(2)}) collective-permute-start(bf16[8,32768]{1,0:T(8,128)(2,1)S(1)} %maximum_select_fusion.3), channel_id=1, source_target_pairs={{0,1},{1,0},{2,3},{3,2},{4,5},{5,4},{6,7},{7,6},{8,9},{9,8},{10,11... | collective-permute-start | bytes 1572872 | tf_op jit(solution)/shard_map/ppermute | solution.py:25
  222.0 5.7 %fusion.16 = f32[64,2048]{1,0:T(8,128)} fusion(bf16[2048,2048]{1,0:T(8,128)(2,1)} %all-gather.3.cloned.1.call-done, bf16[8,8,16,128]{3,2,1,0:T(8,128)(2,1)S(1)} %bitcast.116), kind=kOutput, calls=%fused_computation.50 | convolution fusion | flops 536870912 | bytes 9175040 | tf_op jit(solution)/shard_map/dot_general | solution.py:201
  228.4 2.8 %fusion.15 = (bf16[128,1024]{1,0:T(8,128)(2,1)}, bf16[128,1024]{1,0:T(8,128)(2,1)}) fusion(f32[1,384,1024]{2,1,0:T(8,128)} %copy-done, bf16[2,256,1024]{2,1,0:T(8,128)(2,1)S(1)} %select_n.248, bf16[2,256,1024]{2,1,0:T(8,128)(2,1)} %collective-permute-done.11, bf16[2,256,1024]{2,1,0:T(8,128)(2,1)} %collective-permute-done.10, pred[]{:T(512)S(6)} %eq.38, ...), kind=kLoop, calls=%fused_computation.49 | loop fusion | flops 2883584 | bytes 3670018 | tf_op jit(solution)/shard_map/convert_element_type | solution.py:220
  (106 shorter events, 16.8 us)
Async XLA Ops:
  7.2 93.2 %all-gather.3.cloned.1.call-start = ((), (), s32[]{:S(2)}) async-start(), calls=%async_computation.2 | async-start | bytes 8912896 | tf_op jit(solution)/shard_map/all_gather | solution.py:124
  7.9 189.2 %all-gather.5.cloned.1.call-start = ((), (), s32[]{:S(2)}) async-start(), calls=%async_computation.3 | async-start | bytes 4456448 | tf_op jit(solution)/shard_map/all_gather | solution.py:125
  9.8 15.9 %collective-permute-start = (bf16[2,128,1024]{2,1,0:T(8,128)(2,1)}, bf16[2,128,1024]{2,1,0:T(8,128)(2,1)S(1)}, u32[]{:S(2)}, u32[]{:S(2)}) collective-permute-start(bf16[2,128,1024]{2,1,0:T(8,128)(2,1)} %pad_maximum_fusion.4), channel_id=1, source_target_pairs={{0,1},{1,2},{2,3},{3,4},{4,5},{5,6},{6,7},{7,8},{8,9},{9,10},{10,1... | collective-permute-start | bytes 1572872 | tf_op jit(solution)/shard_map/ppermute | solution.py:61
  13.5 22.3 %collective-permute-start.1 = (bf16[2,128,1024]{2,1,0:T(8,128)(2,1)}, bf16[2,128,1024]{2,1,0:T(8,128)(2,1)S(1)}, u32[]{:S(2)}, u32[]{:S(2)}) collective-permute-start(bf16[2,128,1024]{2,1,0:T(8,128)(2,1)} %pad_maximum_fusion.4), channel_id=1, source_target_pairs={{1,0},{2,1},{3,2},{4,3},{5,4},{6,5},{7,6},{8,7},{9,8},{10,9},{11,1... | collective-permute-start | bytes 1572872 | tf_op jit(solution)/shard_map/ppermute | solution.py:62
  19.3 3.0 %copy-start.12 = (s32[1,3]{1,0:T(1,128)S(1)}, s32[1,3]{1,0:T(1,128)}, u32[]{:S(2)}) copy-start(s32[1,3]{1,0:T(1,128)} %param.14) | copy-start | bytes 40
  19.3 5.6 %copy-start.13 = (s32[3]{0:T(128)S(1)}, s32[3]{0:T(128)}, u32[]{:S(2)}) copy-start(s32[3]{0:T(128)} %constant.91.clone) | copy-start | bytes 40
  19.9 16.0 %copy-start.5 = (bf16[128,1024]{1,0:T(8,128)(2,1)S(1)}, bf16[128,1024]{1,0:T(8,128)(2,1)}, u32[]{:S(2)}) copy-start(bf16[128,1024]{1,0:T(8,128)(2,1)} %param.10) | copy-start | bytes 786436
  19.9 15.9 %copy-start.6 = (bf16[128,1024]{1,0:T(8,128)(2,1)S(1)}, bf16[128,1024]{1,0:T(8,128)(2,1)}, u32[]{:S(2)}) copy-start(bf16[128,1024]{1,0:T(8,128)(2,1)} %param.9) | copy-start | bytes 786436
  20.8 4.3 %collective-permute-start.2 = (bf16[8,32768]{1,0:T(8,128)(2,1)}, bf16[8,32768]{1,0:T(8,128)(2,1)S(1)}, u32[]{:S(2)}, u32[]{:S(2)}) collective-permute-start(bf16[8,32768]{1,0:T(8,128)(2,1)} %constant_dynamic-slice_fusion.3), channel_id=1, source_target_pairs={{0,1},{1,0},{2,3},{3,2},{4,5},{5,4},{6,7},{7,6},{8,9},{9,8},{10,11... | collective-permute-start | bytes 1572872 | tf_op jit(solution)/shard_map/ppermute | solution.py:25
  25.3 11.3 %collective-permute-start.3 = (bf16[4,32768]{1,0:T(4,128)(2,1)S(1)}, bf16[4,32768]{1,0:T(4,128)(2,1)S(1)}, u32[]{:S(2)}, u32[]{:S(2)}) collective-permute-start(bf16[4,32768]{1,0:T(4,128)(2,1)S(1)} %constant_dynamic-slice_fusion.2), channel_id=1, source_target_pairs={{0,2},{2,0},{4,6},{6,4},{8,10},{10,8},{12,14},{14,12},{1,3},{3,1},... | collective-permute-start | bytes 786440 | tf_op jit(solution)/shard_map/ppermute | solution.py:28
  37.0 5.9 %collective-permute-start.4 = (bf16[2,32768]{1,0:T(2,128)(2,1)S(1)}, bf16[2,32768]{1,0:T(2,128)(2,1)S(1)}, u32[]{:S(2)}, u32[]{:S(2)}) collective-permute-start(bf16[2,32768]{1,0:T(2,128)(2,1)S(1)} %constant_dynamic-slice_fusion.1), channel_id=1, source_target_pairs={{0,4},{2,6},{4,0},{6,2},{8,12},{10,14},{12,8},{14,10},{1,5},{3,7},... | collective-permute-start | bytes 393224 | tf_op jit(solution)/shard_map/ppermute | solution.py:28
  43.2 4.8 %collective-permute-start.5 = (bf16[1,32768]{1,0:T(2,128)(2,1)S(1)}, bf16[1,32768]{1,0:T(2,128)(2,1)S(1)}, u32[]{:S(2)}, u32[]{:S(2)}) collective-permute-start(bf16[1,32768]{1,0:T(2,128)(2,1)S(1)} %constant_dynamic-slice_fusion), channel_id=1, source_target_pairs={{0,8},{2,10},{4,12},{6,14},{8,0},{10,2},{12,4},{14,6},{1,9},{3,11}... | collective-permute-start | bytes 196616 | tf_op jit(solution)/shard_map/ppermute | solution.py:28
  48.2 4.9 %collective-permute-start.6 = (bf16[1,32768]{1,0:T(2,128)(2,1)S(1)}, bf16[1,32768]{1,0:T(2,128)(2,1)S(1)}, u32[]{:S(2)}, u32[]{:S(2)}) collective-permute-start(bf16[1,32768]{1,0:T(2,128)(2,1)S(1)} %dynamic-slice_add_fusion.2), channel_id=1, source_target_pairs={{0,8},{2,10},{4,12},{6,14},{8,0},{10,2},{12,4},{14,6},{1,9},{3,11}... | collective-permute-start | bytes 196616 | tf_op jit(solution)/shard_map/ppermute | solution.py:28
  53.7 46.7 %copy-start.9 = (bf16[64,2048]{1,0:T(8,128)(2,1)S(1)}, bf16[64,2048]{1,0:T(8,128)(2,1)}, u32[]{:S(2)}) copy-start(bf16[64,2048]{1,0:T(8,128)(2,1)} %param.11) | copy-start | bytes 786436
  53.7 28.9 %collective-permute-start.7 = (bf16[2,32768]{1,0:T(2,128)(2,1)S(1)}, bf16[2,32768]{1,0:T(2,128)(2,1)S(1)}, u32[]{:S(2)}, u32[]{:S(2)}) collective-permute-start(bf16[2,32768]{1,0:T(2,128)(2,1)S(1)} %broadcast_select_fusion.3), channel_id=1, source_target_pairs={{0,4},{2,6},{4,0},{6,2},{8,12},{10,14},{12,8},{14,10},{1,5},{3,7},... | collective-permute-start | bytes 393224 | tf_op jit(solution)/shard_map/ppermute | solution.py:28
  83.1 13.8 %collective-permute-start.8 = (bf16[4,32768]{1,0:T(4,128)(2,1)S(1)}, bf16[4,32768]{1,0:T(4,128)(2,1)S(1)}, u32[]{:S(2)}, u32[]{:S(2)}) collective-permute-start(bf16[4,32768]{1,0:T(4,128)(2,1)S(1)} %maximum_select_fusion.4), channel_id=1, source_target_pairs={{0,2},{2,0},{4,6},{6,4},{8,10},{10,8},{12,14},{14,12},{1,3},{3,1},... | collective-permute-start | bytes 786440 | tf_op jit(solution)/shard_map/ppermute | solution.py:28
  92.6 4.2 %copy-start.8 = (bf16[1024,1024]{1,0:T(8,128)(2,1)}, bf16[1024,1024]{1,0:T(8,128)(2,1)S(1)}, u32[]{:S(2)}) copy-start(bf16[1024,1024]{1,0:T(8,128)(2,1)S(1)} %bitcast_dynamic-update-slice_fusion.5) | copy-start | bytes 6291460
  92.7 1.4 copy-start.7
  97.3 18.6 %collective-permute-start.9 = (bf16[8,32768]{1,0:T(8,128)(2,1)S(1)}, bf16[8,32768]{1,0:T(8,128)(2,1)S(1)}, u32[]{:S(2)}, u32[]{:S(2)}) collective-permute-start(bf16[8,32768]{1,0:T(8,128)(2,1)S(1)} %maximum_select_fusion.2), channel_id=1, source_target_pairs={{0,1},{1,0},{2,3},{3,2},{4,5},{5,4},{6,7},{7,6},{8,9},{9,8},{10,11... | collective-permute-start | bytes 1572872 | tf_op jit(solution)/shard_map/ppermute | solution.py:25
  107.2 21.9 %all-to-all-start = ((bf16[16,128,64]{1,2,0:T(8,128)(2,1)}), bf16[16,128,64]{1,2,0:T(8,128)(2,1)S(1)}, u32[]{:S(2)}, u32[]{:S(2)}) async-start(bf16[16,128,64]{1,2,0:T(8,128)(2,1)} %bitcast.107), calls=%async_computation | async-start | bytes 524288 | tf_op jit(solution)/shard_map/all_to_all | solution.py:158
  130.5 12.3 %copy-start.11 = (pred[384]{0:T(512)(128)(4,1)S(1)}, pred[384]{0:T(512)(128)(4,1)}, u32[]{:S(2)}) copy-start(pred[384]{0:T(512)(128)(4,1)} %constant.113) | copy-start | bytes 1156
  142.9 2.8 %copy-start.4 = (f32[768,1024]{1,0:T(8,128)S(1)}, f32[768,1024]{1,0:T(8,128)}, u32[]{:S(2)}) copy-start(f32[768,1024]{1,0:T(8,128)} %get-tuple-element.12) | copy-start | bytes 9437188
  149.0 4.4 %copy-start.2 = (f32[16,32768]{1,0:T(8,128)S(1)}, f32[16,32768]{1,0:T(8,128)}, u32[]{:S(2)}) copy-start(f32[16,32768]{1,0:T(8,128)} %reshape.176) | copy-start | bytes 6291460
  150.4 3.0 %collective-permute-start.12 = (bf16[8,32768]{1,0:T(8,128)(2,1)S(1)}, bf16[8,32768]{1,0:T(8,128)(2,1)S(1)}, u32[]{:S(2)}, u32[]{:S(2)}) collective-permute-start(bf16[8,32768]{1,0:T(8,128)(2,1)S(1)} %dynamic-slice_convert_fusion), channel_id=1, source_target_pairs={{0,1},{1,0},{2,3},{3,2},{4,5},{5,4},{6,7},{7,6},{8,9},{9,8},{10,11... | collective-permute-start | bytes 1572872 | tf_op jit(solution)/shard_map/ppermute | solution.py:25
  152.1 2.9 %copy-start.3 = (f32[768,1024]{1,0:T(8,128)S(1)}, f32[768,1024]{1,0:T(8,128)}, u32[]{:S(2)}) copy-start(f32[768,1024]{1,0:T(8,128)} %get-tuple-element.13) | copy-start | bytes 9437188
  153.6 7.8 %collective-permute-start.13 = (bf16[4,32768]{1,0:T(4,128)(2,1)S(1)}, bf16[4,32768]{1,0:T(4,128)(2,1)S(1)}, u32[]{:S(2)}, u32[]{:S(2)}) collective-permute-start(bf16[4,32768]{1,0:T(4,128)(2,1)S(1)} %dynamic-slice_convert_fusion.1), channel_id=1, source_target_pairs={{0,2},{2,0},{4,6},{6,4},{8,10},{10,8},{12,14},{14,12},{1,3},{3,1},... | collective-permute-start | bytes 786440 | tf_op jit(solution)/shard_map/ppermute | solution.py:28
  161.7 3.9 %collective-permute-start.14 = (bf16[2,32768]{1,0:T(2,128)(2,1)S(1)}, bf16[2,32768]{1,0:T(2,128)(2,1)S(1)}, u32[]{:S(2)}, u32[]{:S(2)}) collective-permute-start(bf16[2,32768]{1,0:T(2,128)(2,1)S(1)} %dynamic-slice_convert_fusion.2), channel_id=1, source_target_pairs={{0,4},{2,6},{4,0},{6,2},{8,12},{10,14},{12,8},{14,10},{1,5},{3,7},... | collective-permute-start | bytes 393224 | tf_op jit(solution)/shard_map/ppermute | solution.py:28
  163.4 10.8 %copy-start.1 = (f32[1,384,1024]{2,1,0:T(8,128)}, f32[1,384,1024]{2,1,0:T(8,128)S(1)}, u32[]{:S(2)}) copy-start(f32[1,384,1024]{2,1,0:T(8,128)S(1)} %bitcast_dynamic-update-slice_fusion.1) | copy-start | bytes 4718596
  165.9 4.9 %collective-permute-start.15 = (bf16[1,32768]{1,0:T(2,128)(2,1)S(1)}, bf16[1,32768]{1,0:T(2,128)(2,1)S(1)}, u32[]{:S(2)}, u32[]{:S(2)}) collective-permute-start(bf16[1,32768]{1,0:T(2,128)(2,1)S(1)} %dynamic-slice_convert_fusion.3), channel_id=1, source_target_pairs={{0,8},{2,10},{4,12},{6,14},{8,0},{10,2},{12,4},{14,6},{1,9},{3,11}... | collective-permute-start | bytes 196616 | tf_op jit(solution)/shard_map/ppermute | solution.py:28
  167.3 6.9 %copy-start = (f32[1,384,1024]{2,1,0:T(8,128)}, f32[1,384,1024]{2,1,0:T(8,128)S(1)}, u32[]{:S(2)}) copy-start(f32[1,384,1024]{2,1,0:T(8,128)S(1)} %bitcast_dynamic-update-slice_fusion) | copy-start | bytes 4718596
  171.0 5.4 %collective-permute-start.16 = (bf16[1,32768]{1,0:T(2,128)(2,1)S(1)}, bf16[1,32768]{1,0:T(2,128)(2,1)S(1)}, u32[]{:S(2)}, u32[]{:S(2)}) collective-permute-start(bf16[1,32768]{1,0:T(2,128)(2,1)S(1)} %add_convert_fusion), channel_id=1, source_target_pairs={{0,8},{2,10},{4,12},{6,14},{8,0},{10,2},{12,4},{14,6},{1,9},{3,11}... | collective-permute-start | bytes 196616 | tf_op jit(solution)/shard_map/ppermute | solution.py:28
  174.2 15.0 %copy-start.10 = (bf16[128,1024]{1,0:T(8,128)(2,1)S(1)}, bf16[128,1024]{1,0:T(8,128)(2,1)}, u32[]{:S(2)}) copy-start(bf16[128,1024]{1,0:T(8,128)(2,1)} %get-tuple-element.10) | copy-start | bytes 786436
  177.0 18.3 %collective-permute-start.17 = (bf16[2,32768]{1,0:T(2,128)(2,1)S(1)}, bf16[2,32768]{1,0:T(2,128)(2,1)S(1)}, u32[]{:S(2)}, u32[]{:S(2)}) collective-permute-start(bf16[2,32768]{1,0:T(2,128)(2,1)S(1)} %broadcast_select_fusion.2), channel_id=1, source_target_pairs={{0,4},{2,6},{4,0},{6,2},{8,12},{10,14},{12,8},{14,10},{1,5},{3,7},... | collective-permute-start | bytes 393224 | tf_op jit(solution)/shard_map/ppermute | solution.py:28
  183.3 45.1 %collective-permute-start.10 = (bf16[2,256,1024]{2,1,0:T(8,128)(2,1)S(1)}, bf16[2,256,1024]{2,1,0:T(8,128)(2,1)}, u32[]{:S(2)}, u32[]{:S(2)}) collective-permute-start(bf16[2,256,1024]{2,1,0:T(8,128)(2,1)S(1)} %pad_maximum_fusion.3), channel_id=1, source_target_pairs={{0,1},{1,2},{2,3},{3,4},{4,5},{5,6},{6,7},{7,8},{8,9},{9,10},{10,1... | collective-permute-start | bytes 3145736 | tf_op jit(solution)/shard_map/ppermute | solution.py:61
  187.3 41.1 %collective-permute-start.11 = (bf16[2,256,1024]{2,1,0:T(8,128)(2,1)S(1)}, bf16[2,256,1024]{2,1,0:T(8,128)(2,1)}, u32[]{:S(2)}, u32[]{:S(2)}) collective-permute-start(bf16[2,256,1024]{2,1,0:T(8,128)(2,1)S(1)} %pad_maximum_fusion.3), channel_id=1, source_target_pairs={{1,0},{2,1},{3,2},{4,3},{5,4},{6,5},{7,6},{8,7},{9,8},{10,9},{11,1... | collective-permute-start | bytes 3145736 | tf_op jit(solution)/shard_map/ppermute | solution.py:62
  190.1 28.0 %all-to-all-start.1 = ((bf16[1,128,16,64]{1,3,0,2:T(8,128)(2,1)}), bf16[1,128,16,64]{1,3,0,2:T(8,128)(2,1)S(1)}, u32[]{:S(2)}, u32[]{:S(2)}) async-start(bf16[1,128,16,64]{1,3,0,2:T(8,128)(2,1)} %bitcast.35), calls=%async_computation.1 | async-start | bytes 524288 | tf_op jit(solution)/shard_map/all_to_all | solution.py:198
  195.8 22.8 %collective-permute-start.18 = (bf16[4,32768]{1,0:T(4,128)(2,1)S(1)}, bf16[4,32768]{1,0:T(4,128)(2,1)S(1)}, u32[]{:S(2)}, u32[]{:S(2)}) collective-permute-start(bf16[4,32768]{1,0:T(4,128)(2,1)S(1)} %maximum_select_fusion.5), channel_id=1, source_target_pairs={{0,2},{2,0},{4,6},{6,4},{8,10},{10,8},{12,14},{14,12},{1,3},{3,1},... | collective-permute-start | bytes 786440 | tf_op jit(solution)/shard_map/ppermute | solution.py:28
  219.1 8.6 %collective-permute-start.19 = (bf16[8,32768]{1,0:T(8,128)(2,1)S(1)}, bf16[8,32768]{1,0:T(8,128)(2,1)S(1)}, u32[]{:S(2)}, u32[]{:S(2)}) collective-permute-start(bf16[8,32768]{1,0:T(8,128)(2,1)S(1)} %maximum_select_fusion.3), channel_id=1, source_target_pairs={{0,1},{1,0},{2,3},{3,2},{4,5},{5,4},{6,7},{7,6},{8,9},{9,8},{10,11... | collective-permute-start | bytes 1572872 | tf_op jit(solution)/shard_map/ppermute | solution.py:25
Sparse Core Ops, SparseCore 0:
  10.2 86.0 all-gather.2
  98.4 59.9 all-gather.4

commit v15 on v14

--- a/solution.py
+++ b/solution.py
@@ -4,6 +4,7 @@
 import jax.numpy as jnp
 from jax import lax
 from jax.experimental import pallas as pl
+from jax.experimental.pallas import tpu as pltpu
 from jax.sharding import Mesh
 from jax.sharding import PartitionSpec as P
 
@@ -63,7 +64,7 @@
     return before, after
 
 
-def _attn_kernel(live_ref, q_ref, k_ref, v_ref, up_ref, attn_ref, dq_ref, dk_ref, dv_ref, dg_ref):
+def _attn_kernel(ext_ref, live_ref, q_ref, k_ref, v_ref, up_ref, attn_ref, dq_ref, gk_ref, gv_ref, dg_ref):
     scale = 1.0 / math.sqrt(q_ref.shape[-1])
     q = q_ref[...]
     k = k_ref[...]
@@ -78,39 +79,48 @@
     probs = raised / jnp.sum(raised, axis=-1, keepdims=True)
     probs_b = probs.astype(jnp.bfloat16)
     attn_ref[...] = jnp.dot(probs_b, v, preferred_element_type=jnp.float32).astype(attn_ref.dtype)
-    n_local = dk_ref.shape[0]
+    n_local = k.shape[0] - dg_ref.shape[1]
+    blk = dg_ref.shape[1] // 2
     dv = lax.dot_general(probs_b, up, tn, preferred_element_type=jnp.float32)
-    dv_ref[...] = dv[:n_local]
     dg_ref[1] = dv[n_local:]
     dprobs = lax.dot_general(up, v, nt, preferred_element_type=jnp.float32)
     rowdot = jnp.sum(probs * dprobs, axis=-1, keepdims=True)
     dscores = (scale * probs * (dprobs - rowdot)).astype(jnp.bfloat16)
     dq_ref[...] = jnp.dot(dscores, k, preferred_element_type=jnp.float32).astype(dq_ref.dtype)
     dk = lax.dot_general(dscores, q, tn, preferred_element_type=jnp.float32)
-    dk_ref[...] = dk[:n_local]
     dg_ref[0] = dk[n_local:]
-
-def attention(live, q, k, v, up, heads, local_n):
+    gk_ref[...] = jnp.zeros_like(gk_ref)
+    gv_ref[...] = jnp.zeros_like(gv_ref)
+    for j in range(n_local // blk):
+        at = pl.ds(pl.multiple_of(ext_ref[j] * blk, blk), blk)
+        gk_ref[at, :] += dk[j * blk : (j + 1) * blk]
+        gv_ref[at, :] += dv[j * blk : (j + 1) * blk]
+
+def attention(ext, live, q, k, v, up, heads, local_n, ext_n):
     rows, features = q.shape
     keys_n = k.shape[0]
     hd = features // heads
-    qspec = pl.BlockSpec((rows, hd), lambda h: (0, h))
-    kspec = pl.BlockSpec((keys_n, hd), lambda h: (0, h))
-    lspec = pl.BlockSpec((local_n, hd), lambda h: (0, h))
-    gspec = pl.BlockSpec((2, keys_n - local_n, hd), lambda h: (0, 0, h))
+    qspec = pl.BlockSpec((rows, hd), lambda h, e: (0, h))
+    kspec = pl.BlockSpec((keys_n, hd), lambda h, e: (0, h))
+    espec = pl.BlockSpec((ext_n, hd), lambda h, e: (0, h))
+    gspec = pl.BlockSpec((2, keys_n - local_n, hd), lambda h, e: (0, 0, h))
+    grid_spec = pltpu.PrefetchScalarGridSpec(
+        num_scalar_prefetch=1,
+        grid=(heads,),
+        in_specs=[pl.BlockSpec((1, keys_n), lambda h, e: (0, 0)), qspec, kspec, kspec, qspec],
+        out_specs=[qspec, qspec, espec, espec, gspec],
+    )
     return pl.pallas_call(
         _attn_kernel,
-        grid=(heads,),
-        in_specs=[pl.BlockSpec((1, keys_n), lambda h: (0, 0)), qspec, kspec, kspec, qspec],
-        out_specs=[qspec, qspec, lspec, lspec, gspec],
+        grid_spec=grid_spec,
         out_shape=[
             jax.ShapeDtypeStruct((rows, features), jnp.bfloat16),
             jax.ShapeDtypeStruct((rows, features), jnp.bfloat16),
-            jax.ShapeDtypeStruct((local_n, features), jnp.float32),
-            jax.ShapeDtypeStruct((local_n, features), jnp.float32),
+            jax.ShapeDtypeStruct((ext_n, features), jnp.float32),
+            jax.ShapeDtypeStruct((ext_n, features), jnp.float32),
             jax.ShapeDtypeStruct((2, keys_n - local_n, features), jnp.float32),
         ],
-    )(live, q, k, v, up)
+    )(ext, live, q, k, v, up)
 
 
 def local(query, keys, values, out_weight, grad_out, global_blocks, random_blocks):
@@ -175,17 +185,12 @@
         live_rows = jnp.repeat(live[b], BLK).astype(jnp.float32)[None]
         q = query[b * BLK : (b + 1) * BLK]
         up = upstream[b * BLK : (b + 1) * BLK]
-        attn, dq, dk, dv, dg = attention(live_rows, q, chosen[0], chosen[1], up, H, n_local * BLK)
+        attn, dq, gk, gv, dg = attention(
+            ext_index[b], live_rows, q, chosen[0], chosen[1], up, H, n_local * BLK, 3 * blocks_dev * BLK
+        )
         attn_rows.append(attn)
         dq_rows.append(dq)
-        for side, grad in enumerate((dk, dv)):
-            for j in range(n_local):
-                start = ext_index[b, j] * BLK
-                cur = lax.dynamic_slice_in_dim(grad_ext[side], start, BLK, axis=0)
-                term = grad[j * BLK : (j + 1) * BLK]
-                grad_ext[side] = lax.dynamic_update_slice_in_dim(
-                    grad_ext[side], cur + term, start, axis=0
-                )
+        grad_ext = [grad_ext[0] + gk, grad_ext[1] + gv]
         terms = dg
         global_local = terms if global_local is None else global_local + terms
     grad_ext = jnp.stack(grad_ext)

time: 239 us -> 253 us (1.059); the launches traced: 238 us -> 248 us
  waiting for transfers between devices: 81 us -> 116 us
  starting transfers between devices: 76.6 us -> 58.5 us
  other arithmetic: 17.7 us -> 12.6 us
    all_gather x1, waiting for transfers between devices: 0.01 us -> 35.2 us  [local(): weight_all = lax.all_gather(out_weight, SEQ, axis=0, tiled=True)]
    ppermute x12, waiting for transfers between devices: 42.2 us -> 65.8 us  [xor_swap(): return lax.ppermute(x, 'chip', [(i, i ^ m) for i in range(n)])]
    ppermute x12, starting transfers between devices: 43.2 us -> 21.3 us  [xor_swap(): return lax.ppermute(x, 'chip', [(i, i ^ m) for i in range(n)])]
    all_to_all x1, waiting for transfers between devices: 17.3 us -> 0.01 us  [local(): lax.all_to_all(attn_out.reshape(tok_rows, count, w_rows), SEQ, 1, 0, tile...]
    ppermute x2, waiting for transfers between devices: 10.1 us -> 1.46 us  [halo(): after = lax.ppermute(shard, SEQ, down)]
    dynamic_update_slice x11 -> x0, other arithmetic: 6.64 us -> none  [local(): lax.dynamic_update_slice_in_dim(grad_ext[side], cur + term, start, axis=0)]
    all_gather x1, waiting for transfers between devices: 0.01 us -> 5.78 us  [local(): grad_out_all = lax.all_gather(grad_out, SEQ, axis=0, tiled=True)]
    ppermute x2, starting transfers between devices: 7.64 us -> 13.3 us  [halo(): before = lax.ppermute(shard, SEQ, up)]
  transfers between devices with their start and end apart: 24 -> 24, of which waited for: 14 -> 15; matrix products, arithmetic and copies ran while one was open for 19% -> 13% of each run, Pallas kernels for 5% -> 0%
where the time goes in v15:
time: 253 us; the launch traced here: 248 us
  waiting for transfers between devices  116 us (46%)
  starting transfers between devices  58.5 us (23%)
  between operations  17.8 us (7%)
  matrix products  15.5 us (6%)
  local copies, waits for them, and re-layouts  14.7 us (6%)
  Pallas kernels  12.7 us (5%)
  other arithmetic  12.6 us (5%)
    ppermute x12, waiting for transfers between devices, xor_swap(): return lax.ppermute(x, 'chip', [(i, i ^ m) for i in range(n)])  65.8 us
    all_gather x1, waiting for transfers between devices, local(): weight_all = lax.all_gather(out_weight, SEQ, axis=0, tiled=True)  35.2 us
    ppermute x12, starting transfers between devices, xor_swap(): return lax.ppermute(x, 'chip', [(i, i ^ m) for i in range(n)])  21.3 us
    ppermute x2, starting transfers between devices, halo(): before = lax.ppermute(shard, SEQ, up)  13.3 us
    pallas_call x1, Pallas kernels, attention(): pl.pallas_call(_attn_kernel, grid_spec=grid_spec, out_shape=[jax.ShapeDty...  12.7 us
    all_to_all x1, starting transfers between devices, local(): lax.all_to_all(upstream_cols.reshape(count, tok_rows, w_rows), SEQ, 0, 0,...  7.66 us
    all_to_all x1, starting transfers between devices, local(): lax.all_to_all(attn_out.reshape(tok_rows, count, w_rows), SEQ, 1, 0, tile...  7.24 us
    all_to_all x1, waiting for transfers between devices, local(): lax.all_to_all(upstream_cols.reshape(count, tok_rows, w_rows), SEQ, 0, 0,...  6.2 us
  transfers between devices with their start and end apart: 24, of which 15 were waited for; matrix products, arithmetic and copies ran while one was open for 13% of the time, Pallas kernels for 0%

profile of v15, /device:TPU:11, one launch (start us, length us, event | category | flops | bytes accessed | tf_op | source)
XLA Modules:
  0.0 248.3 jit_solution(392348787855180019)
XLA Ops:
  7.2 1.9 pad_maximum_fusion.4
  9.1 3.7 %collective-permute-start = (bf16[2,128,1024]{2,1,0:T(8,128)(2,1)}, bf16[2,128,1024]{2,1,0:T(8,128)(2,1)}, u32[]{:S(2)}, u32[]{:S(2)}) collective-permute-start(bf16[2,128,1024]{2,1,0:T(8,128)(2,1)} %pad_maximum_fusion.4), channel_id=1, source_target_pairs={{0,1},{1,2},{2,3},{3,4},{4,5},{5,6},{6,7},{7,8},{8,9},{9,10},{10,1... | collective-permute-start | bytes 1572872 | tf_op jit(solution)/shard_map/ppermute | solution.py:62
  12.8 1.9 collective-permute-start.1
  14.7 1.3 fusion.26
  17.3 1.1 broadcast_select_fusion.1
  19.2 1.6 collective-permute-start.2
  24.8 1.5 collective-permute-done.1
  26.3 1.2 pad_maximum_fusion
  27.6 5.4 %collective-permute-done.3 = bf16[4,32768]{1,0:T(4,128)(2,1)S(1)} collective-permute-done((bf16[4,32768]{1,0:T(4,128)(2,1)S(1)}, bf16[4,32768]{1,0:T(4,128)(2,1)S(1)}, u32[]{:S(2)}, u32[]{:S(2)}) %collective-permute-start.3) | collective-permute-done | bytes 262176 | tf_op jit(solution)/shard_map/ppermute | solution.py:29
  33.4 1.1 fusion.18
  34.6 8.7 %collective-permute-done.4 = bf16[2,32768]{1,0:T(2,128)(2,1)S(1)} collective-permute-done((bf16[2,32768]{1,0:T(2,128)(2,1)S(1)}, bf16[2,32768]{1,0:T(2,128)(2,1)S(1)}, u32[]{:S(2)}, u32[]{:S(2)}) %collective-permute-start.4) | collective-permute-done | bytes 131104 | tf_op jit(solution)/shard_map/ppermute | solution.py:29
  43.7 4.9 %collective-permute-start.5 = (bf16[1,32768]{1,0:T(2,128)(2,1)S(1)}, bf16[1,32768]{1,0:T(2,128)(2,1)S(1)}, u32[]{:S(2)}, u32[]{:S(2)}) collective-permute-start(bf16[1,32768]{1,0:T(2,128)(2,1)S(1)} %constant_dynamic-slice_fusion), channel_id=1, source_target_pairs={{0,8},{2,10},{4,12},{6,14},{8,0},{10,2},{12,4},{14,6},{1,9},{3,11}... | collective-permute-start | bytes 196616 | tf_op jit(solution)/shard_map/ppermute | solution.py:29
  48.6 6.2 %collective-permute-done.5 = bf16[1,32768]{1,0:T(2,128)(2,1)S(1)} collective-permute-done((bf16[1,32768]{1,0:T(2,128)(2,1)S(1)}, bf16[1,32768]{1,0:T(2,128)(2,1)S(1)}, u32[]{:S(2)}, u32[]{:S(2)}) %collective-permute-start.5) | collective-permute-done | bytes 65568 | tf_op jit(solution)/shard_map/ppermute | solution.py:29
  54.9 2.7 %collective-permute-start.6 = (bf16[1,32768]{1,0:T(2,128)(2,1)S(1)}, bf16[1,32768]{1,0:T(2,128)(2,1)S(1)}, u32[]{:S(2)}, u32[]{:S(2)}) collective-permute-start(bf16[1,32768]{1,0:T(2,128)(2,1)S(1)} %dynamic-slice_add_fusion.2), channel_id=1, source_target_pairs={{0,8},{2,10},{4,12},{6,14},{8,0},{10,2},{12,4},{14,6},{1,9},{3,11}... | collective-permute-start | bytes 196616 | tf_op jit(solution)/shard_map/ppermute | solution.py:29
  57.7 12.3 %collective-permute-done.6 = bf16[1,32768]{1,0:T(2,128)(2,1)S(1)} collective-permute-done((bf16[1,32768]{1,0:T(2,128)(2,1)S(1)}, bf16[1,32768]{1,0:T(2,128)(2,1)S(1)}, u32[]{:S(2)}, u32[]{:S(2)}) %collective-permute-start.6) | collective-permute-done | bytes 65568 | tf_op jit(solution)/shard_map/ppermute | solution.py:29
  70.5 0.8 collective-permute-start.7
  71.4 12.4 %collective-permute-done.7 = bf16[2,32768]{1,0:T(2,128)(2,1)S(1)} collective-permute-done((bf16[2,32768]{1,0:T(2,128)(2,1)S(1)}, bf16[2,32768]{1,0:T(2,128)(2,1)S(1)}, u32[]{:S(2)}, u32[]{:S(2)}) %collective-permute-start.7) | collective-permute-done | bytes 131104 | tf_op jit(solution)/shard_map/ppermute | solution.py:29
  84.2 3.6 %collective-permute-start.8 = (bf16[4,32768]{1,0:T(4,128)(2,1)S(1)}, bf16[4,32768]{1,0:T(4,128)(2,1)S(1)}, u32[]{:S(2)}, u32[]{:S(2)}) collective-permute-start(bf16[4,32768]{1,0:T(4,128)(2,1)S(1)} %maximum_select_fusion.4), channel_id=1, source_target_pairs={{0,2},{2,0},{4,6},{6,4},{8,10},{10,8},{12,14},{14,12},{1,3},{3,1},... | collective-permute-start | bytes 786440 | tf_op jit(solution)/shard_map/ppermute | solution.py:29
  87.9 1.5 copy-done.4
  89.4 4.2 %collective-permute-done.8 = bf16[4,32768]{1,0:T(4,128)(2,1)S(1)} collective-permute-done((bf16[4,32768]{1,0:T(4,128)(2,1)S(1)}, bf16[4,32768]{1,0:T(4,128)(2,1)S(1)}, u32[]{:S(2)}, u32[]{:S(2)}) %collective-permute-start.8) | collective-permute-done | bytes 262176 | tf_op jit(solution)/shard_map/ppermute | solution.py:29
  94.0 1.6 collective-permute-start.9
  95.6 5.8 %all-gather.3.cloned.1.call-done = bf16[2048,2048]{1,0:T(8,128)(2,1)} async-done(((bf16[128,2048]{1,0:T(8,128)(2,1)}), bf16[2048,2048]{1,0:T(8,128)(2,1)}) %all-gather.3.cloned.1.call-update) | async-done | bytes 8388624 | tf_op jit(solution)/shard_map/all_gather | solution.py:134
  101.4 6.0 %fusion = bf16[8,16,8,128]{3,2,1,0:T(8,128)(2,1)S(1)} fusion(bf16[2048,2048]{1,0:T(8,128)(2,1)} %all-gather.3.cloned.1.call-done, bf16[64,2048]{1,0:T(8,128)(2,1)S(1)} %copy-done.6), kind=kOutput, calls=%fused_computation.3 | convolution fusion | flops 537001984 | bytes 8912896 | tf_op jit(solution)/shard_map/dot_general | solution.py:165
  108.2 7.7 %all-to-all-start = ((bf16[16,128,64]{1,2,0:T(8,128)(2,1)}), bf16[16,128,64]{1,2,0:T(8,128)(2,1)S(1)}, u32[]{:S(2)}, u32[]{:S(2)}) async-start(bf16[16,128,64]{1,2,0:T(8,128)(2,1)} %bitcast.105), calls=%async_computation | async-start | bytes 524288 | tf_op jit(solution)/shard_map/all_to_all | solution.py:168
  116.6 0.8 fusion.16
  117.5 0.9 fusion.15
  118.3 6.2 %all-to-all-done = bf16[16,128,64]{1,2,0:T(8,128)(2,1)S(1)} async-done(((bf16[16,128,64]{1,2,0:T(8,128)(2,1)}), bf16[16,128,64]{1,2,0:T(8,128)(2,1)S(1)}, u32[]{:S(2)}, u32[]{:S(2)}) %all-to-all-start) | async-done | bytes 262176 | tf_op jit(solution)/shard_map/all_to_all | solution.py:168
  124.5 0.8 copy.19.up_ref
  126.0 12.7 %shard_map.119 = (bf16[128,1024]{1,0:T(8,128)(2,1)}, bf16[128,1024]{1,0:T(8,128)(2,1)}, f32[384,1024]{1,0:T(8,128)}, f32[384,1024]{1,0:T(8,128)}, f32[2,256,1024]{2,1,0:T(8,128)}) custom-call(s32[6]{0:T(128)} %add_bitcast_fusion.ext_ref, f32[1,1024]{1,0:T(1,128)} %bitcast.119, bf16[128,1024]{1,0:T(8,128)(2,1)} %q_ref.1, ...), custom_call_target="tpu_custom_call" | custom-call | tf_op jit(solution)/shard_map/pallas_call | solution.py:113
  138.8 1.7 reshape.172
  140.7 1.9 collective-permute-done.12
  143.3 7.3 %collective-permute-done.13 = bf16[4,32768]{1,0:T(4,128)(2,1)S(1)} collective-permute-done((bf16[4,32768]{1,0:T(4,128)(2,1)S(1)}, bf16[4,32768]{1,0:T(4,128)(2,1)S(1)}, u32[]{:S(2)}, u32[]{:S(2)}) %collective-permute-start.13) | collective-permute-done | bytes 262176 | tf_op jit(solution)/shard_map/ppermute | solution.py:29
  150.9 1.0 collective-permute-start.14
  151.9 2.9 %collective-permute-done.14 = bf16[2,32768]{1,0:T(2,128)(2,1)S(1)} collective-permute-done((bf16[2,32768]{1,0:T(2,128)(2,1)S(1)}, bf16[2,32768]{1,0:T(2,128)(2,1)S(1)}, u32[]{:S(2)}, u32[]{:S(2)}) %collective-permute-start.14) | collective-permute-done | bytes 131104 | tf_op jit(solution)/shard_map/ppermute | solution.py:29
  155.8 0.9 collective-permute-start.15
  156.7 4.1 %collective-permute-done.15 = bf16[1,32768]{1,0:T(2,128)(2,1)S(1)} collective-permute-done((bf16[1,32768]{1,0:T(2,128)(2,1)}, bf16[1,32768]{1,0:T(2,128)(2,1)S(1)}, u32[]{:S(2)}, u32[]{:S(2)}) %collective-permute-start.15) | collective-permute-done | bytes 65568 | tf_op jit(solution)/shard_map/ppermute | solution.py:29
  161.0 2.7 %collective-permute-start.16 = (bf16[1,32768]{1,0:T(2,128)(2,1)S(1)}, bf16[1,32768]{1,0:T(2,128)(2,1)S(1)}, u32[]{:S(2)}, u32[]{:S(2)}) collective-permute-start(bf16[1,32768]{1,0:T(2,128)(2,1)S(1)} %add_convert_fusion), channel_id=1, source_target_pairs={{0,8},{2,10},{4,12},{6,14},{8,0},{10,2},{12,4},{14,6},{1,9},{3,11}... | collective-permute-start | bytes 196616 | tf_op jit(solution)/shard_map/ppermute | solution.py:29
  163.9 2.4 collective-permute-done.16
  166.9 2.4 collective-permute-start.17
  169.4 9.6 %collective-permute-start.10 = (bf16[2,256,1024]{2,1,0:T(8,128)(2,1)S(1)}, bf16[2,256,1024]{2,1,0:T(8,128)(2,1)}, u32[]{:S(2)}, u32[]{:S(2)}) collective-permute-start(bf16[2,256,1024]{2,1,0:T(8,128)(2,1)S(1)} %pad_maximum_fusion.3), channel_id=1, source_target_pairs={{0,1},{1,2},{2,3},{3,4},{4,5},{5,6},{6,7},{7,8},{8,9},{9,10},{10,1... | collective-permute-start | bytes 3145736 | tf_op jit(solution)/shard_map/ppermute | solution.py:62
  179.0 3.4 %collective-permute-start.11 = (bf16[2,256,1024]{2,1,0:T(8,128)(2,1)S(1)}, bf16[2,256,1024]{2,1,0:T(8,128)(2,1)}, u32[]{:S(2)}, u32[]{:S(2)}) collective-permute-start(bf16[2,256,1024]{2,1,0:T(8,128)(2,1)S(1)} %pad_maximum_fusion.3), channel_id=1, source_target_pairs={{1,0},{2,1},{3,2},{4,3},{5,4},{6,5},{7,6},{8,7},{9,8},{10,9},{11,1... | collective-permute-start | bytes 3145736 | tf_op jit(solution)/shard_map/ppermute | solution.py:63
  182.5 0.8 copy.20
  183.3 7.2 %all-to-all-start.1 = ((bf16[1,128,16,64]{1,3,0,2:T(8,128)(2,1)}), bf16[1,128,16,64]{1,3,0,2:T(8,128)(2,1)S(1)}, u32[]{:S(2)}, u32[]{:S(2)}) async-start(bf16[1,128,16,64]{1,3,0,2:T(8,128)(2,1)} %bitcast.34), calls=%async_computation.1 | async-start | bytes 524288 | tf_op jit(solution)/shard_map/all_to_all | solution.py:203
  191.1 1.2 collective-permute-start.18
  192.3 35.2 %all-gather.5.cloned.1.call-done = bf16[1024,2048]{1,0:T(8,128)(2,1)} async-done(((bf16[64,2048]{1,0:T(8,128)(2,1)}), bf16[1024,2048]{1,0:T(8,128)(2,1)}) %all-gather.5.cloned.1.call-update) | async-done | bytes 4194320 | tf_op jit(solution)/shard_map/all_gather | solution.py:135
  227.5 3.7 %convolution_convert_fusion = bf16[128,2048]{1,0:T(8,128)(2,1)} fusion(bf16[128,1024]{1,0:T(8,128)(2,1)S(1)} %copy-done.7, bf16[1024,2048]{1,0:T(8,128)(2,1)} %all-gather.5.cloned.1.call-done), kind=kOutput, calls=%fused_computation | convolution fusion | flops 537133056 | bytes 4980736 | tf_op jit(solution)/shard_map/dot_general | solution.py:200
  232.2 5.7 %fusion.12 = f32[64,2048]{1,0:T(8,128)} fusion(bf16[2048,2048]{1,0:T(8,128)(2,1)} %all-gather.3.cloned.1.call-done, bf16[8,8,16,128]{3,2,1,0:T(8,128)(2,1)S(1)} %bitcast.116), kind=kOutput, calls=%fused_computation.34 | convolution fusion | flops 536870912 | bytes 9175040 | tf_op jit(solution)/shard_map/dot_general | solution.py:206
  238.7 2.8 %fusion.11 = (bf16[128,1024]{1,0:T(8,128)(2,1)}, bf16[128,1024]{1,0:T(8,128)(2,1)}) fusion(f32[1,384,1024]{2,1,0:T(8,128)} %bitcast.114, bf16[2,256,1024]{2,1,0:T(8,128)(2,1)S(1)} %select_n.226, bf16[2,256,1024]{2,1,0:T(8,128)(2,1)} %collective-permute-done.11, bf16[2,256,1024]{2,1,0:T(8,128)(2,1)} %collective-permute-done.10, pred[]{:T(512)S(6)} %eq.38, ...), kind=kLoop, calls=%fused_computation.33 | loop fusion | flops 2883584 | bytes 3670018 | tf_op jit(solution)/shard_map/convert_element_type | solution.py:225
  (88 shorter events, 13.0 us)
Async XLA Ops:
  7.2 94.2 %all-gather.3.cloned.1.call-start = ((), (), s32[]{:S(2)}) async-start(), calls=%async_computation.2 | async-start | bytes 8912896 | tf_op jit(solution)/shard_map/all_gather | solution.py:134
  9.1 15.7 %collective-permute-start = (bf16[2,128,1024]{2,1,0:T(8,128)(2,1)}, bf16[2,128,1024]{2,1,0:T(8,128)(2,1)}, u32[]{:S(2)}, u32[]{:S(2)}) collective-permute-start(bf16[2,128,1024]{2,1,0:T(8,128)(2,1)} %pad_maximum_fusion.4), channel_id=1, source_target_pairs={{0,1},{1,2},{2,3},{3,4},{4,5},{5,6},{6,7},{7,8},{8,9},{9,10},{10,1... | collective-permute-start | bytes 1572872 | tf_op jit(solution)/shard_map/ppermute | solution.py:62
  12.8 13.5 %collective-permute-start.1 = (bf16[2,128,1024]{2,1,0:T(8,128)(2,1)}, bf16[2,128,1024]{2,1,0:T(8,128)(2,1)S(1)}, u32[]{:S(2)}, u32[]{:S(2)}) collective-permute-start(bf16[2,128,1024]{2,1,0:T(8,128)(2,1)} %pad_maximum_fusion.4), channel_id=1, source_target_pairs={{1,0},{2,1},{3,2},{4,3},{5,4},{6,5},{7,6},{8,7},{9,8},{10,9},{11,1... | collective-permute-start | bytes 1572872 | tf_op jit(solution)/shard_map/ppermute | solution.py:63
  18.6 2.3 copy-start.8
  18.6 4.8 %copy-start.10 = (s32[1,3]{1,0:T(1,128)S(1)}, s32[1,3]{1,0:T(1,128)}, u32[]{:S(2)}) copy-start(s32[1,3]{1,0:T(1,128)} %constant.90) | copy-start | bytes 40
  18.6 5.4 %copy-start.9 = (s32[3]{0:T(128)S(1)}, s32[3]{0:T(128)}, u32[]{:S(2)}) copy-start(s32[3]{0:T(128)} %constant.87.clone) | copy-start | bytes 40
  19.1 7.2 %copy-start = (bf16[128,1024]{1,0:T(8,128)(2,1)S(1)}, bf16[128,1024]{1,0:T(8,128)(2,1)}, u32[]{:S(2)}) copy-start(bf16[128,1024]{1,0:T(8,128)(2,1)} %param.10) | copy-start | bytes 786436
  19.2 7.1 %copy-start.1 = (bf16[128,1024]{1,0:T(8,128)(2,1)S(1)}, bf16[128,1024]{1,0:T(8,128)(2,1)}, u32[]{:S(2)}) copy-start(bf16[128,1024]{1,0:T(8,128)(2,1)} %param.9) | copy-start | bytes 786436
  19.2 4.9 %collective-permute-start.2 = (bf16[8,32768]{1,0:T(8,128)(2,1)S(1)}, bf16[8,32768]{1,0:T(8,128)(2,1)S(1)}, u32[]{:S(2)}, u32[]{:S(2)}) collective-permute-start(bf16[8,32768]{1,0:T(8,128)(2,1)S(1)} %constant_dynamic-slice_fusion.3), channel_id=1, source_target_pairs={{0,1},{1,0},{2,3},{3,2},{4,5},{5,4},{6,7},{7,6},{8,9},{9,8},{10,11... | collective-permute-start | bytes 1572872 | tf_op jit(solution)/shard_map/ppermute | solution.py:26
  24.4 8.6 %collective-permute-start.3 = (bf16[4,32768]{1,0:T(4,128)(2,1)S(1)}, bf16[4,32768]{1,0:T(4,128)(2,1)S(1)}, u32[]{:S(2)}, u32[]{:S(2)}) collective-permute-start(bf16[4,32768]{1,0:T(4,128)(2,1)S(1)} %constant_dynamic-slice_fusion.2), channel_id=1, source_target_pairs={{0,2},{2,0},{4,6},{6,4},{8,10},{10,8},{12,14},{14,12},{1,3},{3,1},... | collective-permute-start | bytes 786440 | tf_op jit(solution)/shard_map/ppermute | solution.py:29
  33.4 9.9 %collective-permute-start.4 = (bf16[2,32768]{1,0:T(2,128)(2,1)S(1)}, bf16[2,32768]{1,0:T(2,128)(2,1)S(1)}, u32[]{:S(2)}, u32[]{:S(2)}) collective-permute-start(bf16[2,32768]{1,0:T(2,128)(2,1)S(1)} %constant_dynamic-slice_fusion.1), channel_id=1, source_target_pairs={{0,4},{2,6},{4,0},{6,2},{8,12},{10,14},{12,8},{14,10},{1,5},{3,7},... | collective-permute-start | bytes 393224 | tf_op jit(solution)/shard_map/ppermute | solution.py:29
  43.7 11.1 %collective-permute-start.5 = (bf16[1,32768]{1,0:T(2,128)(2,1)S(1)}, bf16[1,32768]{1,0:T(2,128)(2,1)S(1)}, u32[]{:S(2)}, u32[]{:S(2)}) collective-permute-start(bf16[1,32768]{1,0:T(2,128)(2,1)S(1)} %constant_dynamic-slice_fusion), channel_id=1, source_target_pairs={{0,8},{2,10},{4,12},{6,14},{8,0},{10,2},{12,4},{14,6},{1,9},{3,11}... | collective-permute-start | bytes 196616 | tf_op jit(solution)/shard_map/ppermute | solution.py:29
  54.9 15.0 %collective-permute-start.6 = (bf16[1,32768]{1,0:T(2,128)(2,1)S(1)}, bf16[1,32768]{1,0:T(2,128)(2,1)S(1)}, u32[]{:S(2)}, u32[]{:S(2)}) collective-permute-start(bf16[1,32768]{1,0:T(2,128)(2,1)S(1)} %dynamic-slice_add_fusion.2), channel_id=1, source_target_pairs={{0,8},{2,10},{4,12},{6,14},{8,0},{10,2},{12,4},{14,6},{1,9},{3,11}... | collective-permute-start | bytes 196616 | tf_op jit(solution)/shard_map/ppermute | solution.py:29
  70.5 30.9 %copy-start.6 = (bf16[64,2048]{1,0:T(8,128)(2,1)S(1)}, bf16[64,2048]{1,0:T(8,128)(2,1)}, u32[]{:S(2)}) copy-start(bf16[64,2048]{1,0:T(8,128)(2,1)} %param.11) | copy-start | bytes 786436
  70.5 13.2 %collective-permute-start.7 = (bf16[2,32768]{1,0:T(2,128)(2,1)S(1)}, bf16[2,32768]{1,0:T(2,128)(2,1)S(1)}, u32[]{:S(2)}, u32[]{:S(2)}) collective-permute-start(bf16[2,32768]{1,0:T(2,128)(2,1)S(1)} %broadcast_select_fusion.3), channel_id=1, source_target_pairs={{0,4},{2,6},{4,0},{6,2},{8,12},{10,14},{12,8},{14,10},{1,5},{3,7},... | collective-permute-start | bytes 393224 | tf_op jit(solution)/shard_map/ppermute | solution.py:29
  84.2 9.3 %collective-permute-start.8 = (bf16[4,32768]{1,0:T(4,128)(2,1)S(1)}, bf16[4,32768]{1,0:T(4,128)(2,1)S(1)}, u32[]{:S(2)}, u32[]{:S(2)}) collective-permute-start(bf16[4,32768]{1,0:T(4,128)(2,1)S(1)} %maximum_select_fusion.4), channel_id=1, source_target_pairs={{0,2},{2,0},{4,6},{6,4},{8,10},{10,8},{12,14},{14,12},{1,3},{3,1},... | collective-permute-start | bytes 786440 | tf_op jit(solution)/shard_map/ppermute | solution.py:29
  87.9 5.7 %copy-start.5 = (bf16[1024,1024]{1,0:T(8,128)(2,1)}, bf16[1024,1024]{1,0:T(8,128)(2,1)S(1)}, u32[]{:S(2)}) copy-start(bf16[1024,1024]{1,0:T(8,128)(2,1)S(1)} %bitcast_dynamic-update-slice_fusion.3) | copy-start | bytes 6291460
  87.9 1.5 copy-start.4
  94.0 21.9 %collective-permute-start.9 = (bf16[8,32768]{1,0:T(8,128)(2,1)S(1)}, bf16[8,32768]{1,0:T(8,128)(2,1)S(1)}, u32[]{:S(2)}, u32[]{:S(2)}) collective-permute-start(bf16[8,32768]{1,0:T(8,128)(2,1)S(1)} %maximum_select_fusion.2), channel_id=1, source_target_pairs={{0,1},{1,0},{2,3},{3,2},{4,5},{5,4},{6,7},{7,6},{8,9},{9,8},{10,11... | collective-permute-start | bytes 1572872 | tf_op jit(solution)/shard_map/ppermute | solution.py:26
  108.2 16.3 %all-to-all-start = ((bf16[16,128,64]{1,2,0:T(8,128)(2,1)}), bf16[16,128,64]{1,2,0:T(8,128)(2,1)S(1)}, u32[]{:S(2)}, u32[]{:S(2)}) async-start(bf16[16,128,64]{1,2,0:T(8,128)(2,1)} %bitcast.105), calls=%async_computation | async-start | bytes 524288 | tf_op jit(solution)/shard_map/all_to_all | solution.py:168
  115.9 111.7 %all-gather.5.cloned.1.call-start = ((), (), s32[]{:S(2)}) async-start(), calls=%async_computation.3 | async-start | bytes 4456448 | tf_op jit(solution)/shard_map/all_gather | solution.py:135
  140.6 2.0 collective-permute-start.12
  142.7 21.1 %copy-start.2 = (f32[384,1024]{1,0:T(8,128)S(1)}, f32[384,1024]{1,0:T(8,128)}, u32[]{:S(2)}) copy-start(f32[384,1024]{1,0:T(8,128)} %get-tuple-element.12) | copy-start | bytes 4718596
  142.7 21.1 %copy-start.3 = (f32[384,1024]{1,0:T(8,128)S(1)}, f32[384,1024]{1,0:T(8,128)}, u32[]{:S(2)}) copy-start(f32[384,1024]{1,0:T(8,128)} %get-tuple-element.13) | copy-start | bytes 4718596
  142.8 7.8 %collective-permute-start.13 = (bf16[4,32768]{1,0:T(4,128)(2,1)S(1)}, bf16[4,32768]{1,0:T(4,128)(2,1)S(1)}, u32[]{:S(2)}, u32[]{:S(2)}) collective-permute-start(bf16[4,32768]{1,0:T(4,128)(2,1)S(1)} %dynamic-slice_convert_fusion.1), channel_id=1, source_target_pairs={{0,2},{2,0},{4,6},{6,4},{8,10},{10,8},{12,14},{14,12},{1,3},{3,1},... | collective-permute-start | bytes 786440 | tf_op jit(solution)/shard_map/ppermute | solution.py:29
  150.9 3.9 %collective-permute-start.14 = (bf16[2,32768]{1,0:T(2,128)(2,1)S(1)}, bf16[2,32768]{1,0:T(2,128)(2,1)S(1)}, u32[]{:S(2)}, u32[]{:S(2)}) collective-permute-start(bf16[2,32768]{1,0:T(2,128)(2,1)S(1)} %dynamic-slice_convert_fusion.2), channel_id=1, source_target_pairs={{0,4},{2,6},{4,0},{6,2},{8,12},{10,14},{12,8},{14,10},{1,5},{3,7},... | collective-permute-start | bytes 393224 | tf_op jit(solution)/shard_map/ppermute | solution.py:29
  155.8 5.0 %collective-permute-start.15 = (bf16[1,32768]{1,0:T(2,128)(2,1)}, bf16[1,32768]{1,0:T(2,128)(2,1)S(1)}, u32[]{:S(2)}, u32[]{:S(2)}) collective-permute-start(bf16[1,32768]{1,0:T(2,128)(2,1)} %dynamic-slice_convert_fusion.3), channel_id=1, source_target_pairs={{0,8},{2,10},{4,12},{6,14},{8,0},{10,2},{12,4},{14,6},{1,9},{3,11}... | collective-permute-start | bytes 196616 | tf_op jit(solution)/shard_map/ppermute | solution.py:29
  161.0 5.3 %collective-permute-start.16 = (bf16[1,32768]{1,0:T(2,128)(2,1)S(1)}, bf16[1,32768]{1,0:T(2,128)(2,1)S(1)}, u32[]{:S(2)}, u32[]{:S(2)}) collective-permute-start(bf16[1,32768]{1,0:T(2,128)(2,1)S(1)} %add_convert_fusion), channel_id=1, source_target_pairs={{0,8},{2,10},{4,12},{6,14},{8,0},{10,2},{12,4},{14,6},{1,9},{3,11}... | collective-permute-start | bytes 196616 | tf_op jit(solution)/shard_map/ppermute | solution.py:29
  163.9 18.6 %copy-start.7 = (bf16[128,1024]{1,0:T(8,128)(2,1)S(1)}, bf16[128,1024]{1,0:T(8,128)(2,1)}, u32[]{:S(2)}) copy-start(bf16[128,1024]{1,0:T(8,128)(2,1)} %get-tuple-element.10) | copy-start | bytes 786436
  166.9 23.7 %collective-permute-start.17 = (bf16[2,32768]{1,0:T(2,128)(2,1)S(1)}, bf16[2,32768]{1,0:T(2,128)(2,1)S(1)}, u32[]{:S(2)}, u32[]{:S(2)}) collective-permute-start(bf16[2,32768]{1,0:T(2,128)(2,1)S(1)} %broadcast_select_fusion.2), channel_id=1, source_target_pairs={{0,4},{2,6},{4,0},{6,2},{8,12},{10,14},{12,8},{14,10},{1,5},{3,7},... | collective-permute-start | bytes 393224 | tf_op jit(solution)/shard_map/ppermute | solution.py:29
  169.4 69.3 %collective-permute-start.10 = (bf16[2,256,1024]{2,1,0:T(8,128)(2,1)S(1)}, bf16[2,256,1024]{2,1,0:T(8,128)(2,1)}, u32[]{:S(2)}, u32[]{:S(2)}) collective-permute-start(bf16[2,256,1024]{2,1,0:T(8,128)(2,1)S(1)} %pad_maximum_fusion.3), channel_id=1, source_target_pairs={{0,1},{1,2},{2,3},{3,4},{4,5},{5,6},{6,7},{7,8},{8,9},{9,10},{10,1... | collective-permute-start | bytes 3145736 | tf_op jit(solution)/shard_map/ppermute | solution.py:62
  179.0 59.6 %collective-permute-start.11 = (bf16[2,256,1024]{2,1,0:T(8,128)(2,1)S(1)}, bf16[2,256,1024]{2,1,0:T(8,128)(2,1)}, u32[]{:S(2)}, u32[]{:S(2)}) collective-permute-start(bf16[2,256,1024]{2,1,0:T(8,128)(2,1)S(1)} %pad_maximum_fusion.3), channel_id=1, source_target_pairs={{1,0},{2,1},{3,2},{4,3},{5,4},{6,5},{7,6},{8,7},{9,8},{10,9},{11,1... | collective-permute-start | bytes 3145736 | tf_op jit(solution)/shard_map/ppermute | solution.py:63
  183.3 47.9 %all-to-all-start.1 = ((bf16[1,128,16,64]{1,3,0,2:T(8,128)(2,1)}), bf16[1,128,16,64]{1,3,0,2:T(8,128)(2,1)S(1)}, u32[]{:S(2)}, u32[]{:S(2)}) async-start(bf16[1,128,16,64]{1,3,0,2:T(8,128)(2,1)} %bitcast.34), calls=%async_computation.1 | async-start | bytes 524288 | tf_op jit(solution)/shard_map/all_to_all | solution.py:203
  191.1 40.3 %collective-permute-start.18 = (bf16[4,32768]{1,0:T(4,128)(2,1)S(1)}, bf16[4,32768]{1,0:T(4,128)(2,1)S(1)}, u32[]{:S(2)}, u32[]{:S(2)}) collective-permute-start(bf16[4,32768]{1,0:T(4,128)(2,1)S(1)} %maximum_select_fusion.5), channel_id=1, source_target_pairs={{0,2},{2,0},{4,6},{6,4},{8,10},{10,8},{12,14},{14,12},{1,3},{3,1},... | collective-permute-start | bytes 786440 | tf_op jit(solution)/shard_map/ppermute | solution.py:29
  231.9 6.1 %collective-permute-start.19 = (bf16[8,32768]{1,0:T(8,128)(2,1)S(1)}, bf16[8,32768]{1,0:T(8,128)(2,1)S(1)}, u32[]{:S(2)}, u32[]{:S(2)}) collective-permute-start(bf16[8,32768]{1,0:T(8,128)(2,1)S(1)} %maximum_select_fusion.3), channel_id=1, source_target_pairs={{0,1},{1,0},{2,3},{3,2},{4,5},{5,4},{6,7},{7,6},{8,9},{9,8},{10,11... | collective-permute-start | bytes 1572872 | tf_op jit(solution)/shard_map/ppermute | solution.py:26
Sparse Core Ops, SparseCore 0:
  20.9 80.3 all-gather.2
  156.8 70.6 all-gather.4

commit v16 on v15

--- a/solution.py
+++ b/solution.py
@@ -131,8 +131,9 @@
     total_blocks = blocks_dev * count
     device = flat_index()
 
-    grad_out_all = lax.all_gather(grad_out, SEQ, axis=0, tiled=True)
-    weight_all = lax.all_gather(out_weight, SEQ, axis=0, tiled=True)
+    both = lax.all_gather(jnp.concatenate([grad_out, out_weight]), SEQ, axis=0, tiled=False)
+    grad_out_all = both[:, : grad_out.shape[0]]
+    weight_all = both[:, grad_out.shape[0] :]
 
     paired = jnp.stack([keys, values])
     before, after = halo(paired)
@@ -163,11 +164,9 @@
 
     w_rows = out_weight.shape[0]
     upstream_cols = lax.dot_general(
-        grad_out_all, out_weight, (((1,), (1,)), ((), ())), preferred_element_type=jnp.float32
+        grad_out_all, out_weight, (((2,), (1,)), ((), ())), preferred_element_type=jnp.float32
     ).astype(jnp.bfloat16)
-    upstream = lax.all_to_all(
-        upstream_cols.reshape(count, tok_rows, w_rows), SEQ, 0, 0, tiled=False
-    )
+    upstream = lax.all_to_all(upstream_cols, SEQ, 0, 0, tiled=False)
     upstream = jnp.swapaxes(upstream, 0, 1).reshape(tok_rows, feature_count)
 
     attn_rows, dq_rows = [], []
@@ -197,14 +196,15 @@
     global_total = butterfly_sum(global_local, jnp.bfloat16)
 
     attn_out = jnp.concatenate(attn_rows, axis=0)
-    layer_out = jnp.dot(attn_out, weight_all, preferred_element_type=jnp.float32).astype(
-        jnp.bfloat16
-    )
+    layer_out = lax.dot_general(
+        attn_out.reshape(tok_rows, count, w_rows), weight_all, (((1, 2), (0, 1)), ((), ())),
+        preferred_element_type=jnp.float32,
+    ).astype(jnp.bfloat16)
     attn_cols = lax.all_to_all(
         attn_out.reshape(tok_rows, count, w_rows), SEQ, 1, 0, tiled=False
-    ).reshape(count * tok_rows, w_rows)
+    )
     grad_weight = lax.dot_general(
-        attn_cols, grad_out_all, (((0,), (0,)), ((), ())), preferred_element_type=jnp.float32
+        attn_cols, grad_out_all, (((0, 1), (0, 1)), ((), ())), preferred_element_type=jnp.float32
     )
 
     rims = jnp.concatenate(

time: 253 us -> 259 us (1.024); the launches traced: 248 us -> 258 us
  waiting for transfers between devices: 116 us -> 130 us
  starting transfers between devices: 58.5 us -> 53.7 us
    ppermute x12, waiting for transfers between devices: 65.8 us -> 92.8 us  [xor_swap(): return lax.ppermute(x, 'chip', [(i, i ^ m) for i in range(n)])]
    all_gather x2 -> x1, waiting for transfers between devices: 41 us -> 28.8 us  [local(): lax.all_gather(jnp.concatenate([grad_out, out_weight]), SEQ, axis=0, tile...]
    ppermute x4, starting transfers between devices: 3.55 us -> 6.78 us  [xor_swap(): return lax.ppermute(x, 'core', [(i, i ^ 1) for i in range(n)])]
  transfers between devices with their start and end apart: 24 -> 23, of which waited for: 15 -> 14; matrix products, arithmetic and copies ran while one was open for 13% -> 13% of each run, Pallas kernels for 0% -> 0%
where the time goes in v16:
time: 259 us; the launch traced here: 258 us
  waiting for transfers between devices  130 us (50%)
  starting transfers between devices  53.7 us (21%)
  between operations  17.8 us (7%)
  matrix products  16.3 us (6%)
  other arithmetic  14.6 us (6%)
  local copies, waits for them, and re-layouts  13 us (5%)
  Pallas kernels  12.7 us (5%)
    ppermute x12, waiting for transfers between devices, xor_swap(): return lax.ppermute(x, 'chip', [(i, i ^ m) for i in range(n)])  92.8 us
    all_gather x1, waiting for transfers between devices, local(): lax.all_gather(jnp.concatenate([grad_out, out_weight]), SEQ, axis=0, tile...  28.8 us
    ppermute x12, starting transfers between devices, xor_swap(): return lax.ppermute(x, 'chip', [(i, i ^ m) for i in range(n)])  20.8 us
    pallas_call x1, Pallas kernels, attention(): pl.pallas_call(_attn_kernel, grid_spec=grid_spec, out_shape=[jax.ShapeDty...  12.7 us
    ppermute x2, starting transfers between devices, halo(): before = lax.ppermute(shard, SEQ, up)  11.7 us
    ppermute x4, starting transfers between devices, xor_swap(): return lax.ppermute(x, 'core', [(i, i ^ 1) for i in range(n)])  6.78 us
    dot_general x1, matrix products, local(): lax.dot_general(grad_out_all, out_weight, (((2,), (1,)), ((), ())), prefe...  6.74 us
    all_to_all x1, waiting for transfers between devices, local(): upstream = lax.all_to_all(upstream_cols, SEQ, 0, 0, tiled=False)  6.26 us
  transfers between devices with their start and end apart: 23, of which 14 were waited for; matrix products, arithmetic and copies ran while one was open for 13% of the time, Pallas kernels for 0%

profile of v16, /device:TPU:11, one launch (start us, length us, event | category | flops | bytes accessed | tf_op | source)
XLA Modules:
  0.0 258.0 jit_solution(499297536586716679)
XLA Ops:
  7.2 1.9 pad_maximum_fusion.5
  9.1 3.7 %collective-permute-start = (bf16[2,128,1024]{2,1,0:T(8,128)(2,1)}, bf16[2,128,1024]{2,1,0:T(8,128)(2,1)}, u32[]{:S(2)}, u32[]{:S(2)}) collective-permute-start(bf16[2,128,1024]{2,1,0:T(8,128)(2,1)} %pad_maximum_fusion.5), channel_id=1, source_target_pairs={{0,1},{1,2},{2,3},{3,4},{4,5},{5,6},{6,7},{7,8},{8,9},{9,10},{10,1... | collective-permute-start | bytes 1572872 | tf_op jit(solution)/shard_map/ppermute | solution.py:62
  12.8 1.9 collective-permute-start.1
  14.7 1.3 fusion.42
  17.3 1.1 broadcast_select_fusion.1
  19.2 1.6 collective-permute-start.2
  20.8 2.0 pad_maximum_fusion.4
  26.8 1.2 pad_maximum_fusion
  28.1 6.1 %collective-permute-done.3 = bf16[4,32768]{1,0:T(4,128)(2,1)S(1)} collective-permute-done((bf16[4,32768]{1,0:T(4,128)(2,1)S(1)}, bf16[4,32768]{1,0:T(4,128)(2,1)S(1)}, u32[]{:S(2)}, u32[]{:S(2)}) %collective-permute-start.3) | collective-permute-done | bytes 262176 | tf_op jit(solution)/shard_map/ppermute | solution.py:29
  34.7 1.1 fusion.32
  35.8 10.4 %collective-permute-done.4 = bf16[2,32768]{1,0:T(2,128)(2,1)S(1)} collective-permute-done((bf16[2,32768]{1,0:T(2,128)(2,1)S(1)}, bf16[2,32768]{1,0:T(2,128)(2,1)S(1)}, u32[]{:S(2)}, u32[]{:S(2)}) %collective-permute-start.4) | collective-permute-done | bytes 131104 | tf_op jit(solution)/shard_map/ppermute | solution.py:29
  46.6 5.5 %collective-permute-start.5 = (bf16[1,32768]{1,0:T(2,128)(2,1)S(1)}, bf16[1,32768]{1,0:T(2,128)(2,1)S(1)}, u32[]{:S(2)}, u32[]{:S(2)}) collective-permute-start(bf16[1,32768]{1,0:T(2,128)(2,1)S(1)} %constant_dynamic-slice_fusion), channel_id=1, source_target_pairs={{0,8},{2,10},{4,12},{6,14},{8,0},{10,2},{12,4},{14,6},{1,9},{3,11}... | collective-permute-start | bytes 196616 | tf_op jit(solution)/shard_map/ppermute | solution.py:29
  52.1 11.8 %collective-permute-done.5 = bf16[1,32768]{1,0:T(2,128)(2,1)S(1)} collective-permute-done((bf16[1,32768]{1,0:T(2,128)(2,1)S(1)}, bf16[1,32768]{1,0:T(2,128)(2,1)S(1)}, u32[]{:S(2)}, u32[]{:S(2)}) %collective-permute-start.5) | collective-permute-done | bytes 65568 | tf_op jit(solution)/shard_map/ppermute | solution.py:29
  64.0 3.1 %collective-permute-start.6 = (bf16[1,32768]{1,0:T(2,128)(2,1)S(1)}, bf16[1,32768]{1,0:T(2,128)(2,1)S(1)}, u32[]{:S(2)}, u32[]{:S(2)}) collective-permute-start(bf16[1,32768]{1,0:T(2,128)(2,1)S(1)} %dynamic-slice_add_fusion.2), channel_id=1, source_target_pairs={{0,8},{2,10},{4,12},{6,14},{8,0},{10,2},{12,4},{14,6},{1,9},{3,11}... | collective-permute-start | bytes 196616 | tf_op jit(solution)/shard_map/ppermute | solution.py:29
  67.2 3.7 %collective-permute-done.6 = bf16[1,32768]{1,0:T(2,128)(2,1)S(1)} collective-permute-done((bf16[1,32768]{1,0:T(2,128)(2,1)S(1)}, bf16[1,32768]{1,0:T(2,128)(2,1)S(1)}, u32[]{:S(2)}, u32[]{:S(2)}) %collective-permute-start.6) | collective-permute-done | bytes 65568 | tf_op jit(solution)/shard_map/ppermute | solution.py:29
  71.5 3.0 %collective-permute-start.7 = (bf16[2,32768]{1,0:T(2,128)(2,1)S(1)}, bf16[2,32768]{1,0:T(2,128)(2,1)S(1)}, u32[]{:S(2)}, u32[]{:S(2)}) collective-permute-start(bf16[2,32768]{1,0:T(2,128)(2,1)S(1)} %broadcast_select_fusion.3), channel_id=1, source_target_pairs={{0,4},{2,6},{4,0},{6,2},{8,12},{10,14},{12,8},{14,10},{1,5},{3,7},... | collective-permute-start | bytes 393224 | tf_op jit(solution)/shard_map/ppermute | solution.py:29
  74.6 14.5 %collective-permute-done.7 = bf16[2,32768]{1,0:T(2,128)(2,1)S(1)} collective-permute-done((bf16[2,32768]{1,0:T(2,128)(2,1)S(1)}, bf16[2,32768]{1,0:T(2,128)(2,1)S(1)}, u32[]{:S(2)}, u32[]{:S(2)}) %collective-permute-start.7) | collective-permute-done | bytes 131104 | tf_op jit(solution)/shard_map/ppermute | solution.py:29
  89.7 1.3 copy-done.4
  91.1 12.0 %collective-permute-done.8 = bf16[4,32768]{1,0:T(4,128)(2,1)S(1)} collective-permute-done((bf16[4,32768]{1,0:T(4,128)(2,1)S(1)}, bf16[4,32768]{1,0:T(4,128)(2,1)S(1)}, u32[]{:S(2)}, u32[]{:S(2)}) %collective-permute-start.8) | collective-permute-done | bytes 262176 | tf_op jit(solution)/shard_map/ppermute | solution.py:29
  103.5 2.0 collective-permute-start.9
  105.5 28.8 %all-gather.3.cloned.1.call-done = bf16[3072,2048]{1,0:T(8,128)(2,1)} async-done(((bf16[192,2048]{1,0:T(8,128)(2,1)}), bf16[3072,2048]{1,0:T(8,128)(2,1)}) %all-gather.3.cloned.1.call-update) | async-done | bytes 12582928 | tf_op jit(solution)/shard_map/all_gather | solution.py:134
  134.3 6.7 %fusion.15 = bf16[16,128,64]{1,2,0:T(8,128)(2,1)} fusion(bf16[16,192,2048]{2,1,0:T(8,128)(2,1)} %bitcast.117, bf16[64,2048]{1,0:T(8,128)(2,1)S(1)} %copy-done.7), kind=kOutput, calls=%fused_computation.10 | convolution fusion | flops 537001984 | bytes 8912896 | tf_op jit(solution)/shard_map/dot_general | solution.py:166
  141.0 5.1 %all-to-all-start = ((bf16[16,128,64]{1,2,0:T(8,128)(2,1)}), bf16[16,128,64]{1,2,0:T(8,128)(2,1)S(1)}, u32[]{:S(2)}, u32[]{:S(2)}) async-start(bf16[16,128,64]{1,2,0:T(8,128)(2,1)} %fusion.15), calls=%async_computation | async-start | bytes 524288 | tf_op jit(solution)/shard_map/all_to_all | solution.py:169
  146.8 0.9 fusion.30
  147.7 0.9 fusion.29
  148.6 6.3 %all-to-all-done = bf16[16,128,64]{1,2,0:T(8,128)(2,1)S(1)} async-done(((bf16[16,128,64]{1,2,0:T(8,128)(2,1)}), bf16[16,128,64]{1,2,0:T(8,128)(2,1)S(1)}, u32[]{:S(2)}, u32[]{:S(2)}) %all-to-all-start) | async-done | bytes 262176 | tf_op jit(solution)/shard_map/all_to_all | solution.py:169
  154.8 0.8 copy.19.up_ref
  156.3 12.7 %shard_map.119 = (bf16[128,1024]{1,0:T(8,128)(2,1)}, bf16[128,1024]{1,0:T(8,128)(2,1)}, f32[384,1024]{1,0:T(8,128)}, f32[384,1024]{1,0:T(8,128)}, f32[2,256,1024]{2,1,0:T(8,128)}) custom-call(s32[6]{0:T(128)} %add_bitcast_fusion.ext_ref, f32[1,1024]{1,0:T(1,128)} %bitcast.116, bf16[128,1024]{1,0:T(8,128)(2,1)} %q_ref.1, ...), custom_call_target="tpu_custom_call" | custom-call | tf_op jit(solution)/shard_map/pallas_call | solution.py:113
  169.1 1.7 reshape.172
  171.0 1.9 collective-permute-done.12
  173.6 7.3 %collective-permute-done.13 = bf16[4,32768]{1,0:T(4,128)(2,1)S(1)} collective-permute-done((bf16[4,32768]{1,0:T(4,128)(2,1)S(1)}, bf16[4,32768]{1,0:T(4,128)(2,1)S(1)}, u32[]{:S(2)}, u32[]{:S(2)}) %collective-permute-start.13) | collective-permute-done | bytes 262176 | tf_op jit(solution)/shard_map/ppermute | solution.py:29
  181.2 1.0 collective-permute-start.14
  182.2 2.9 %collective-permute-done.14 = bf16[2,32768]{1,0:T(2,128)(2,1)S(1)} collective-permute-done((bf16[2,32768]{1,0:T(2,128)(2,1)S(1)}, bf16[2,32768]{1,0:T(2,128)(2,1)S(1)}, u32[]{:S(2)}, u32[]{:S(2)}) %collective-permute-start.14) | collective-permute-done | bytes 131104 | tf_op jit(solution)/shard_map/ppermute | solution.py:29
  185.4 0.9 collective-permute-start.15
  186.3 4.0 %collective-permute-done.15 = bf16[1,32768]{1,0:T(2,128)(2,1)S(1)} collective-permute-done((bf16[1,32768]{1,0:T(2,128)(2,1)S(1)}, bf16[1,32768]{1,0:T(2,128)(2,1)S(1)}, u32[]{:S(2)}, u32[]{:S(2)}) %collective-permute-start.15) | collective-permute-done | bytes 65568 | tf_op jit(solution)/shard_map/ppermute | solution.py:29
  190.5 2.6 %collective-permute-start.16 = (bf16[1,32768]{1,0:T(2,128)(2,1)S(1)}, bf16[1,32768]{1,0:T(2,128)(2,1)S(1)}, u32[]{:S(2)}, u32[]{:S(2)}) collective-permute-start(bf16[1,32768]{1,0:T(2,128)(2,1)S(1)} %add_convert_fusion), channel_id=1, source_target_pairs={{0,8},{2,10},{4,12},{6,14},{8,0},{10,2},{12,4},{14,6},{1,9},{3,11}... | collective-permute-start | bytes 196616 | tf_op jit(solution)/shard_map/ppermute | solution.py:29
  193.3 2.6 collective-permute-done.16
  196.4 2.4 collective-permute-start.17
  198.9 8.0 %collective-permute-start.10 = (bf16[2,256,1024]{2,1,0:T(8,128)(2,1)S(1)}, bf16[2,256,1024]{2,1,0:T(8,128)(2,1)}, u32[]{:S(2)}, u32[]{:S(2)}) collective-permute-start(bf16[2,256,1024]{2,1,0:T(8,128)(2,1)S(1)} %pad_maximum_fusion.3), channel_id=1, source_target_pairs={{0,1},{1,2},{2,3},{3,4},{4,5},{5,6},{6,7},{7,8},{8,9},{9,10},{10,1... | collective-permute-start | bytes 3145736 | tf_op jit(solution)/shard_map/ppermute | solution.py:62
  206.9 2.1 collective-permute-start.11
  209.0 0.8 copy.20
  209.9 5.3 %all-to-all-start.1 = ((bf16[1,128,16,64]{1,3,0,2:T(8,128)(2,1)}), bf16[1,128,16,64]{1,3,0,2:T(8,128)(2,1)S(1)}, u32[]{:S(2)}, u32[]{:S(2)}) async-start(bf16[1,128,16,64]{1,3,0,2:T(8,128)(2,1)} %bitcast.38), calls=%async_computation.1 | async-start | bytes 524288 | tf_op jit(solution)/shard_map/all_to_all | solution.py:203
  215.6 1.2 collective-permute-start.18
  216.9 3.8 %fusion.9 = bf16[128,2048]{1,0:T(8,128)(2,1)} fusion(bf16[128,16,64]{0,2,1:T(8,128)(2,1)} %bitcast.31, bf16[16,192,2048]{2,1,0:T(8,128)(2,1)} %bitcast.118), kind=kOutput, calls=%fused_computation.7 | convolution fusion | flops 537133056 | bytes 4980736 | tf_op jit(solution)/shard_map/dot_general | solution.py:199
  220.7 17.6 %collective-permute-done.18 = bf16[4,32768]{1,0:T(4,128)(2,1)S(1)} collective-permute-done((bf16[4,32768]{1,0:T(4,128)(2,1)S(1)}, bf16[4,32768]{1,0:T(4,128)(2,1)S(1)}, u32[]{:S(2)}, u32[]{:S(2)}) %collective-permute-start.18) | collective-permute-done | bytes 262176 | tf_op jit(solution)/shard_map/ppermute | solution.py:29
  238.7 3.1 %collective-permute-start.19 = (bf16[8,32768]{1,0:T(8,128)(2,1)S(1)}, bf16[8,32768]{1,0:T(8,128)(2,1)S(1)}, u32[]{:S(2)}, u32[]{:S(2)}) collective-permute-start(bf16[8,32768]{1,0:T(8,128)(2,1)S(1)} %maximum_select_fusion.3), channel_id=1, source_target_pairs={{0,1},{1,0},{2,3},{3,2},{4,5},{5,4},{6,7},{7,6},{8,9},{9,8},{10,11... | collective-permute-start | bytes 1572872 | tf_op jit(solution)/shard_map/ppermute | solution.py:26
  241.9 5.7 %fusion.12 = f32[64,2048]{1,0:T(8,128)} fusion(bf16[16,192,2048]{2,1,0:T(8,128)(2,1)} %bitcast.119, bf16[1,128,16,64]{1,3,0,2:T(8,128)(2,1)S(1)} %all-to-all-done.1), kind=kOutput, calls=%fused_computation.8 | convolution fusion | flops 536870912 | bytes 9175040 | tf_op jit(solution)/shard_map/dot_general | solution.py:206
  248.4 2.8 %fusion.28 = (bf16[128,1024]{1,0:T(8,128)(2,1)}, bf16[128,1024]{1,0:T(8,128)(2,1)}) fusion(f32[1,384,1024]{2,1,0:T(8,128)} %bitcast.113, bf16[2,256,1024]{2,1,0:T(8,128)(2,1)S(1)} %select_n.226, bf16[2,256,1024]{2,1,0:T(8,128)(2,1)} %collective-permute-done.11, bf16[2,256,1024]{2,1,0:T(8,128)(2,1)} %collective-permute-done.10, pred[]{:T(512)S(6)} %eq.38, ...), kind=kLoop, calls=%fused_computation.41 | loop fusion | flops 2883584 | bytes 3670018 | tf_op jit(solution)/shard_map/convert_element_type | solution.py:225
  (84 shorter events, 11.1 us)
Async XLA Ops:
  7.2 127.1 %all-gather.3.cloned.1.call-start = ((), (), s32[]{:S(2)}) async-start(), calls=%async_computation.2 | async-start | bytes 13369344 | tf_op jit(solution)/shard_map/all_gather | solution.py:134
  9.1 17.7 %collective-permute-start = (bf16[2,128,1024]{2,1,0:T(8,128)(2,1)}, bf16[2,128,1024]{2,1,0:T(8,128)(2,1)}, u32[]{:S(2)}, u32[]{:S(2)}) collective-permute-start(bf16[2,128,1024]{2,1,0:T(8,128)(2,1)} %pad_maximum_fusion.5), channel_id=1, source_target_pairs={{0,1},{1,2},{2,3},{3,4},{4,5},{5,6},{6,7},{7,8},{8,9},{9,10},{10,1... | collective-permute-start | bytes 1572872 | tf_op jit(solution)/shard_map/ppermute | solution.py:62
  12.8 14.0 %collective-permute-start.1 = (bf16[2,128,1024]{2,1,0:T(8,128)(2,1)}, bf16[2,128,1024]{2,1,0:T(8,128)(2,1)S(1)}, u32[]{:S(2)}, u32[]{:S(2)}) collective-permute-start(bf16[2,128,1024]{2,1,0:T(8,128)(2,1)} %pad_maximum_fusion.5), channel_id=1, source_target_pairs={{1,0},{2,1},{3,2},{4,3},{5,4},{6,5},{7,6},{8,7},{9,8},{10,9},{11,1... | collective-permute-start | bytes 1572872 | tf_op jit(solution)/shard_map/ppermute | solution.py:63
  18.6 2.2 copy-start.7
  19.1 3.7 %copy-start.8 = (s32[1,3]{1,0:T(1,128)S(1)}, s32[1,3]{1,0:T(1,128)}, u32[]{:S(2)}) copy-start(s32[1,3]{1,0:T(1,128)} %param.14) | copy-start | bytes 40
  19.1 6.3 %copy-start.10 = (s32[1,3]{1,0:T(1,128)S(1)}, s32[1,3]{1,0:T(1,128)}, u32[]{:S(2)}) copy-start(s32[1,3]{1,0:T(1,128)} %constant.90) | copy-start | bytes 40
  19.1 6.9 %copy-start.9 = (s32[3]{0:T(128)S(1)}, s32[3]{0:T(128)}, u32[]{:S(2)}) copy-start(s32[3]{0:T(128)} %constant.87.clone) | copy-start | bytes 40
  19.2 7.6 %copy-start = (bf16[128,1024]{1,0:T(8,128)(2,1)S(1)}, bf16[128,1024]{1,0:T(8,128)(2,1)}, u32[]{:S(2)}) copy-start(bf16[128,1024]{1,0:T(8,128)(2,1)} %param.10) | copy-start | bytes 786436
  19.2 7.6 %copy-start.1 = (bf16[128,1024]{1,0:T(8,128)(2,1)S(1)}, bf16[128,1024]{1,0:T(8,128)(2,1)}, u32[]{:S(2)}) copy-start(bf16[128,1024]{1,0:T(8,128)(2,1)} %param.9) | copy-start | bytes 786436
  19.2 6.9 %collective-permute-start.2 = (bf16[8,32768]{1,0:T(8,128)(2,1)S(1)}, bf16[8,32768]{1,0:T(8,128)(2,1)S(1)}, u32[]{:S(2)}, u32[]{:S(2)}) collective-permute-start(bf16[8,32768]{1,0:T(8,128)(2,1)S(1)} %constant_dynamic-slice_fusion.3), channel_id=1, source_target_pairs={{0,1},{1,0},{2,3},{3,2},{4,5},{5,4},{6,7},{7,6},{8,9},{9,8},{10,11... | collective-permute-start | bytes 1572872 | tf_op jit(solution)/shard_map/ppermute | solution.py:26
  26.4 7.8 %collective-permute-start.3 = (bf16[4,32768]{1,0:T(4,128)(2,1)S(1)}, bf16[4,32768]{1,0:T(4,128)(2,1)S(1)}, u32[]{:S(2)}, u32[]{:S(2)}) collective-permute-start(bf16[4,32768]{1,0:T(4,128)(2,1)S(1)} %constant_dynamic-slice_fusion.2), channel_id=1, source_target_pairs={{0,2},{2,0},{4,6},{6,4},{8,10},{10,8},{12,14},{14,12},{1,3},{3,1},... | collective-permute-start | bytes 786440 | tf_op jit(solution)/shard_map/ppermute | solution.py:29
  34.6 11.6 %collective-permute-start.4 = (bf16[2,32768]{1,0:T(2,128)(2,1)S(1)}, bf16[2,32768]{1,0:T(2,128)(2,1)S(1)}, u32[]{:S(2)}, u32[]{:S(2)}) collective-permute-start(bf16[2,32768]{1,0:T(2,128)(2,1)S(1)} %constant_dynamic-slice_fusion.1), channel_id=1, source_target_pairs={{0,4},{2,6},{4,0},{6,2},{8,12},{10,14},{12,8},{14,10},{1,5},{3,7},... | collective-permute-start | bytes 393224 | tf_op jit(solution)/shard_map/ppermute | solution.py:29
  46.6 17.2 %collective-permute-start.5 = (bf16[1,32768]{1,0:T(2,128)(2,1)S(1)}, bf16[1,32768]{1,0:T(2,128)(2,1)S(1)}, u32[]{:S(2)}, u32[]{:S(2)}) collective-permute-start(bf16[1,32768]{1,0:T(2,128)(2,1)S(1)} %constant_dynamic-slice_fusion), channel_id=1, source_target_pairs={{0,8},{2,10},{4,12},{6,14},{8,0},{10,2},{12,4},{14,6},{1,9},{3,11}... | collective-permute-start | bytes 196616 | tf_op jit(solution)/shard_map/ppermute | solution.py:29
  64.0 6.9 %collective-permute-start.6 = (bf16[1,32768]{1,0:T(2,128)(2,1)S(1)}, bf16[1,32768]{1,0:T(2,128)(2,1)S(1)}, u32[]{:S(2)}, u32[]{:S(2)}) collective-permute-start(bf16[1,32768]{1,0:T(2,128)(2,1)S(1)} %dynamic-slice_add_fusion.2), channel_id=1, source_target_pairs={{0,8},{2,10},{4,12},{6,14},{8,0},{10,2},{12,4},{14,6},{1,9},{3,11}... | collective-permute-start | bytes 196616 | tf_op jit(solution)/shard_map/ppermute | solution.py:29
  71.5 17.6 %collective-permute-start.7 = (bf16[2,32768]{1,0:T(2,128)(2,1)S(1)}, bf16[2,32768]{1,0:T(2,128)(2,1)S(1)}, u32[]{:S(2)}, u32[]{:S(2)}) collective-permute-start(bf16[2,32768]{1,0:T(2,128)(2,1)S(1)} %broadcast_select_fusion.3), channel_id=1, source_target_pairs={{0,4},{2,6},{4,0},{6,2},{8,12},{10,14},{12,8},{14,10},{1,5},{3,7},... | collective-permute-start | bytes 393224 | tf_op jit(solution)/shard_map/ppermute | solution.py:29
  89.5 13.5 %collective-permute-start.8 = (bf16[4,32768]{1,0:T(4,128)(2,1)S(1)}, bf16[4,32768]{1,0:T(4,128)(2,1)S(1)}, u32[]{:S(2)}, u32[]{:S(2)}) collective-permute-start(bf16[4,32768]{1,0:T(4,128)(2,1)S(1)} %maximum_select_fusion.4), channel_id=1, source_target_pairs={{0,2},{2,0},{4,6},{6,4},{8,10},{10,8},{12,14},{14,12},{1,3},{3,1},... | collective-permute-start | bytes 786440 | tf_op jit(solution)/shard_map/ppermute | solution.py:29
  89.7 13.4 %copy-start.5 = (bf16[1024,1024]{1,0:T(8,128)(2,1)}, bf16[1024,1024]{1,0:T(8,128)(2,1)S(1)}, u32[]{:S(2)}) copy-start(bf16[1024,1024]{1,0:T(8,128)(2,1)S(1)} %bitcast_dynamic-update-slice_fusion.3) | copy-start | bytes 6291460
  89.7 1.4 copy-start.4
  103.5 42.6 %collective-permute-start.9 = (bf16[8,32768]{1,0:T(8,128)(2,1)S(1)}, bf16[8,32768]{1,0:T(8,128)(2,1)S(1)}, u32[]{:S(2)}, u32[]{:S(2)}) collective-permute-start(bf16[8,32768]{1,0:T(8,128)(2,1)S(1)} %maximum_select_fusion.2), channel_id=1, source_target_pairs={{0,1},{1,0},{2,3},{3,2},{4,5},{5,4},{6,7},{7,6},{8,9},{9,8},{10,11... | collective-permute-start | bytes 1572872 | tf_op jit(solution)/shard_map/ppermute | solution.py:26
  141.0 13.8 %all-to-all-start = ((bf16[16,128,64]{1,2,0:T(8,128)(2,1)}), bf16[16,128,64]{1,2,0:T(8,128)(2,1)S(1)}, u32[]{:S(2)}, u32[]{:S(2)}) async-start(bf16[16,128,64]{1,2,0:T(8,128)(2,1)} %fusion.15), calls=%async_computation | async-start | bytes 524288 | tf_op jit(solution)/shard_map/all_to_all | solution.py:169
  170.9 2.0 collective-permute-start.12
  172.9 20.1 %copy-start.2 = (f32[384,1024]{1,0:T(8,128)S(1)}, f32[384,1024]{1,0:T(8,128)}, u32[]{:S(2)}) copy-start(f32[384,1024]{1,0:T(8,128)} %get-tuple-element.12) | copy-start | bytes 4718596
  173.0 20.1 %copy-start.3 = (f32[384,1024]{1,0:T(8,128)S(1)}, f32[384,1024]{1,0:T(8,128)}, u32[]{:S(2)}) copy-start(f32[384,1024]{1,0:T(8,128)} %get-tuple-element.13) | copy-start | bytes 4718596
  173.1 7.8 %collective-permute-start.13 = (bf16[4,32768]{1,0:T(4,128)(2,1)S(1)}, bf16[4,32768]{1,0:T(4,128)(2,1)S(1)}, u32[]{:S(2)}, u32[]{:S(2)}) collective-permute-start(bf16[4,32768]{1,0:T(4,128)(2,1)S(1)} %dynamic-slice_convert_fusion.1), channel_id=1, source_target_pairs={{0,2},{2,0},{4,6},{6,4},{8,10},{10,8},{12,14},{14,12},{1,3},{3,1},... | collective-permute-start | bytes 786440 | tf_op jit(solution)/shard_map/ppermute | solution.py:29
  181.2 3.9 %collective-permute-start.14 = (bf16[2,32768]{1,0:T(2,128)(2,1)S(1)}, bf16[2,32768]{1,0:T(2,128)(2,1)S(1)}, u32[]{:S(2)}, u32[]{:S(2)}) collective-permute-start(bf16[2,32768]{1,0:T(2,128)(2,1)S(1)} %dynamic-slice_convert_fusion.2), channel_id=1, source_target_pairs={{0,4},{2,6},{4,0},{6,2},{8,12},{10,14},{12,8},{14,10},{1,5},{3,7},... | collective-permute-start | bytes 393224 | tf_op jit(solution)/shard_map/ppermute | solution.py:29
  185.4 4.9 %collective-permute-start.15 = (bf16[1,32768]{1,0:T(2,128)(2,1)S(1)}, bf16[1,32768]{1,0:T(2,128)(2,1)S(1)}, u32[]{:S(2)}, u32[]{:S(2)}) collective-permute-start(bf16[1,32768]{1,0:T(2,128)(2,1)S(1)} %dynamic-slice_convert_fusion.3), channel_id=1, source_target_pairs={{0,8},{2,10},{4,12},{6,14},{8,0},{10,2},{12,4},{14,6},{1,9},{3,11}... | collective-permute-start | bytes 196616 | tf_op jit(solution)/shard_map/ppermute | solution.py:29
  190.5 5.4 %collective-permute-start.16 = (bf16[1,32768]{1,0:T(2,128)(2,1)S(1)}, bf16[1,32768]{1,0:T(2,128)(2,1)S(1)}, u32[]{:S(2)}, u32[]{:S(2)}) collective-permute-start(bf16[1,32768]{1,0:T(2,128)(2,1)S(1)} %add_convert_fusion), channel_id=1, source_target_pairs={{0,8},{2,10},{4,12},{6,14},{8,0},{10,2},{12,4},{14,6},{1,9},{3,11}... | collective-permute-start | bytes 196616 | tf_op jit(solution)/shard_map/ppermute | solution.py:29
  193.2 15.8 %copy-start.6 = (bf16[128,1024]{1,0:T(8,128)(2,1)S(1)}, bf16[128,1024]{1,0:T(8,128)(2,1)}, u32[]{:S(2)}) copy-start(bf16[128,1024]{1,0:T(8,128)(2,1)} %get-tuple-element.10) | copy-start | bytes 786436
  196.4 18.7 %collective-permute-start.17 = (bf16[2,32768]{1,0:T(2,128)(2,1)S(1)}, bf16[2,32768]{1,0:T(2,128)(2,1)S(1)}, u32[]{:S(2)}, u32[]{:S(2)}) collective-permute-start(bf16[2,32768]{1,0:T(2,128)(2,1)S(1)} %broadcast_select_fusion.2), channel_id=1, source_target_pairs={{0,4},{2,6},{4,0},{6,2},{8,12},{10,14},{12,8},{14,10},{1,5},{3,7},... | collective-permute-start | bytes 393224 | tf_op jit(solution)/shard_map/ppermute | solution.py:29
  198.9 49.5 %collective-permute-start.10 = (bf16[2,256,1024]{2,1,0:T(8,128)(2,1)S(1)}, bf16[2,256,1024]{2,1,0:T(8,128)(2,1)}, u32[]{:S(2)}, u32[]{:S(2)}) collective-permute-start(bf16[2,256,1024]{2,1,0:T(8,128)(2,1)S(1)} %pad_maximum_fusion.3), channel_id=1, source_target_pairs={{0,1},{1,2},{2,3},{3,4},{4,5},{5,6},{6,7},{7,8},{8,9},{9,10},{10,1... | collective-permute-start | bytes 3145736 | tf_op jit(solution)/shard_map/ppermute | solution.py:62
  206.9 41.5 %collective-permute-start.11 = (bf16[2,256,1024]{2,1,0:T(8,128)(2,1)S(1)}, bf16[2,256,1024]{2,1,0:T(8,128)(2,1)}, u32[]{:S(2)}, u32[]{:S(2)}) collective-permute-start(bf16[2,256,1024]{2,1,0:T(8,128)(2,1)S(1)} %pad_maximum_fusion.3), channel_id=1, source_target_pairs={{1,0},{2,1},{3,2},{4,3},{5,4},{6,5},{7,6},{8,7},{9,8},{10,9},{11,1... | collective-permute-start | bytes 3145736 | tf_op jit(solution)/shard_map/ppermute | solution.py:63
  209.9 32.0 %all-to-all-start.1 = ((bf16[1,128,16,64]{1,3,0,2:T(8,128)(2,1)}), bf16[1,128,16,64]{1,3,0,2:T(8,128)(2,1)S(1)}, u32[]{:S(2)}, u32[]{:S(2)}) async-start(bf16[1,128,16,64]{1,3,0,2:T(8,128)(2,1)} %bitcast.38), calls=%async_computation.1 | async-start | bytes 524288 | tf_op jit(solution)/shard_map/all_to_all | solution.py:203
  215.6 22.7 %collective-permute-start.18 = (bf16[4,32768]{1,0:T(4,128)(2,1)S(1)}, bf16[4,32768]{1,0:T(4,128)(2,1)S(1)}, u32[]{:S(2)}, u32[]{:S(2)}) collective-permute-start(bf16[4,32768]{1,0:T(4,128)(2,1)S(1)} %maximum_select_fusion.5), channel_id=1, source_target_pairs={{0,2},{2,0},{4,6},{6,4},{8,10},{10,8},{12,14},{14,12},{1,3},{3,1},... | collective-permute-start | bytes 786440 | tf_op jit(solution)/shard_map/ppermute | solution.py:29
  238.7 8.9 %collective-permute-start.19 = (bf16[8,32768]{1,0:T(8,128)(2,1)S(1)}, bf16[8,32768]{1,0:T(8,128)(2,1)S(1)}, u32[]{:S(2)}, u32[]{:S(2)}) collective-permute-start(bf16[8,32768]{1,0:T(8,128)(2,1)S(1)} %maximum_select_fusion.3), channel_id=1, source_target_pairs={{0,1},{1,0},{2,3},{3,2},{4,5},{5,4},{6,7},{7,6},{8,9},{9,8},{10,11... | collective-permute-start | bytes 1572872 | tf_op jit(solution)/shard_map/ppermute | solution.py:26
Sparse Core Ops, SparseCore 0:
  22.9 111.2 all-gather.2

commit v17 on v15

--- a/solution.py
+++ b/solution.py
@@ -194,12 +194,13 @@
         terms = dg
         global_local = terms if global_local is None else global_local + terms
     grad_ext = jnp.stack(grad_ext)
-    global_total = butterfly_sum(global_local, jnp.bfloat16)
-
     attn_out = jnp.concatenate(attn_rows, axis=0)
     layer_out = jnp.dot(attn_out, weight_all, preferred_element_type=jnp.float32).astype(
         jnp.bfloat16
     )
+    layer_out, global_local = lax.optimization_barrier((layer_out, global_local))
+    global_total = butterfly_sum(global_local, jnp.bfloat16)
+
     attn_cols = lax.all_to_all(
         attn_out.reshape(tok_rows, count, w_rows), SEQ, 1, 0, tiled=False
     ).reshape(count * tok_rows, w_rows)

time: 253 us -> 245 us (0.968); the launches traced: 248 us -> 245 us
  waiting for transfers between devices: 116 us -> 95.4 us
  starting transfers between devices: 58.5 us -> 73.6 us
  other arithmetic: 12.6 us -> 15.7 us
    all_gather x1, waiting for transfers between devices: 35.2 us -> 15.2 us  [local(): weight_all = lax.all_gather(out_weight, SEQ, axis=0, tiled=True)]
    ppermute x12, starting transfers between devices: 21.3 us -> 38.2 us  [xor_swap(): return lax.ppermute(x, 'chip', [(i, i ^ m) for i in range(n)])]
    ppermute x12, waiting for transfers between devices: 65.8 us -> 54.6 us  [xor_swap(): return lax.ppermute(x, 'chip', [(i, i ^ m) for i in range(n)])]
    ppermute x2, waiting for transfers between devices: 1.46 us -> 12.5 us  [halo(): after = lax.ppermute(shard, SEQ, down)]
    ppermute x2, starting transfers between devices: 13.3 us -> 6.71 us  [halo(): before = lax.ppermute(shard, SEQ, up)]
    all_gather x1, waiting for transfers between devices: 5.78 us -> 0.01 us  [local(): grad_out_all = lax.all_gather(grad_out, SEQ, axis=0, tiled=True)]
    all_to_all x1, waiting for transfers between devices: 6.2 us -> 10.8 us  [local(): lax.all_to_all(upstream_cols.reshape(count, tok_rows, w_rows), SEQ, 0, 0,...]
    ppermute x4, starting transfers between devices: 3.55 us -> 7.4 us  [xor_swap(): return lax.ppermute(x, 'core', [(i, i ^ 1) for i in range(n)])]
  transfers between devices with their start and end apart: 24 -> 24, of which waited for: 15 -> 15; matrix products, arithmetic and copies ran while one was open for 13% -> 14% of each run, Pallas kernels for 0% -> 5%
where the time goes in v17:
time: 245 us
  waiting for transfers between devices  95.4 us (39%)
  starting transfers between devices  73.6 us (30%)
  between operations  17.8 us (7%)
  other arithmetic  15.7 us (6%)
  matrix products  15.6 us (6%)
  local copies, waits for them, and re-layouts  13.8 us (6%)
  Pallas kernels  12.7 us (5%)
    ppermute x12, waiting for transfers between devices, xor_swap(): return lax.ppermute(x, 'chip', [(i, i ^ m) for i in range(n)])  54.6 us
    ppermute x12, starting transfers between devices, xor_swap(): return lax.ppermute(x, 'chip', [(i, i ^ m) for i in range(n)])  38.2 us
    all_gather x1, waiting for transfers between devices, local(): weight_all = lax.all_gather(out_weight, SEQ, axis=0, tiled=True)  15.2 us
    pallas_call x1, Pallas kernels, attention(): pl.pallas_call(_attn_kernel, grid_spec=grid_spec, out_shape=[jax.ShapeDty...  12.7 us
    ppermute x2, waiting for transfers between devices, halo(): after = lax.ppermute(shard, SEQ, down)  12.5 us
    all_to_all x1, waiting for transfers between devices, local(): lax.all_to_all(upstream_cols.reshape(count, tok_rows, w_rows), SEQ, 0, 0,...  10.8 us
    all_to_all x1, starting transfers between devices, local(): lax.all_to_all(upstream_cols.reshape(count, tok_rows, w_rows), SEQ, 0, 0,...  8.59 us
    all_to_all x1, starting transfers between devices, local(): lax.all_to_all(attn_out.reshape(tok_rows, count, w_rows), SEQ, 1, 0, tile...  8.13 us
  transfers between devices with their start and end apart: 24, of which 15 were waited for; matrix products, arithmetic and copies ran while one was open for 14% of the time, Pallas kernels for 5%

profile of v17, /device:TPU:11, one launch (start us, length us, event | category | flops | bytes accessed | tf_op | source)
XLA Modules:
  0.0 244.7 jit_solution(11698509197555888845)
XLA Ops:
  7.9 1.9 pad_maximum_fusion.4
  9.8 3.7 %collective-permute-start = (bf16[2,128,1024]{2,1,0:T(8,128)(2,1)}, bf16[2,128,1024]{2,1,0:T(8,128)(2,1)}, u32[]{:S(2)}, u32[]{:S(2)}) collective-permute-start(bf16[2,128,1024]{2,1,0:T(8,128)(2,1)} %pad_maximum_fusion.4), channel_id=1, source_target_pairs={{0,1},{1,2},{2,3},{3,4},{4,5},{5,6},{6,7},{7,8},{8,9},{9,10},{10,1... | collective-permute-start | bytes 1572872 | tf_op jit(solution)/shard_map/ppermute | solution.py:62
  13.5 1.9 collective-permute-start.1
  15.5 1.3 fusion.26
  18.1 1.1 broadcast_select_fusion.1
  20.0 1.6 collective-permute-start.2
  25.6 10.3 %collective-permute-done.1 = bf16[2,128,1024]{2,1,0:T(8,128)(2,1)S(1)} collective-permute-done((bf16[2,128,1024]{2,1,0:T(8,128)(2,1)}, bf16[2,128,1024]{2,1,0:T(8,128)(2,1)S(1)}, u32[]{:S(2)}, u32[]{:S(2)}) %collective-permute-start.1) | collective-permute-done | bytes 524320 | tf_op jit(solution)/shard_map/ppermute | solution.py:63
  35.9 1.2 pad_maximum_fusion
  37.6 1.1 fusion.18
  38.7 4.1 %collective-permute-done.4 = bf16[2,32768]{1,0:T(2,128)(2,1)S(1)} collective-permute-done((bf16[2,32768]{1,0:T(2,128)(2,1)S(1)}, bf16[2,32768]{1,0:T(2,128)(2,1)S(1)}, u32[]{:S(2)}, u32[]{:S(2)}) %collective-permute-start.4) | collective-permute-done | bytes 131104 | tf_op jit(solution)/shard_map/ppermute | solution.py:29
  43.2 1.9 collective-permute-start.5
  45.1 2.9 %collective-permute-done.5 = bf16[1,32768]{1,0:T(2,128)(2,1)S(1)} collective-permute-done((bf16[1,32768]{1,0:T(2,128)(2,1)S(1)}, bf16[1,32768]{1,0:T(2,128)(2,1)S(1)}, u32[]{:S(2)}, u32[]{:S(2)}) %collective-permute-start.5) | collective-permute-done | bytes 65568 | tf_op jit(solution)/shard_map/ppermute | solution.py:29
  48.2 1.9 collective-permute-start.6
  50.1 3.0 %collective-permute-done.6 = bf16[1,32768]{1,0:T(2,128)(2,1)S(1)} collective-permute-done((bf16[1,32768]{1,0:T(2,128)(2,1)S(1)}, bf16[1,32768]{1,0:T(2,128)(2,1)S(1)}, u32[]{:S(2)}, u32[]{:S(2)}) %collective-permute-start.6) | collective-permute-done | bytes 65568 | tf_op jit(solution)/shard_map/ppermute | solution.py:29
  53.7 14.5 %collective-permute-start.7 = (bf16[2,32768]{1,0:T(2,128)(2,1)S(1)}, bf16[2,32768]{1,0:T(2,128)(2,1)S(1)}, u32[]{:S(2)}, u32[]{:S(2)}) collective-permute-start(bf16[2,32768]{1,0:T(2,128)(2,1)S(1)} %broadcast_select_fusion.3), channel_id=1, source_target_pairs={{0,4},{2,6},{4,0},{6,2},{8,12},{10,14},{12,8},{14,10},{1,5},{3,7},... | collective-permute-start | bytes 393224 | tf_op jit(solution)/shard_map/ppermute | solution.py:29
  68.3 11.7 %collective-permute-done.7 = bf16[2,32768]{1,0:T(2,128)(2,1)S(1)} collective-permute-done((bf16[2,32768]{1,0:T(2,128)(2,1)S(1)}, bf16[2,32768]{1,0:T(2,128)(2,1)S(1)}, u32[]{:S(2)}, u32[]{:S(2)}) %collective-permute-start.7) | collective-permute-done | bytes 131104 | tf_op jit(solution)/shard_map/ppermute | solution.py:29
  80.5 12.2 %collective-permute-start.8 = (bf16[4,32768]{1,0:T(4,128)(2,1)S(1)}, bf16[4,32768]{1,0:T(4,128)(2,1)S(1)}, u32[]{:S(2)}, u32[]{:S(2)}) collective-permute-start(bf16[4,32768]{1,0:T(4,128)(2,1)S(1)} %maximum_select_fusion.4), channel_id=1, source_target_pairs={{0,2},{2,0},{4,6},{6,4},{8,10},{10,8},{12,14},{14,12},{1,3},{3,1},... | collective-permute-start | bytes 786440 | tf_op jit(solution)/shard_map/ppermute | solution.py:29
  92.8 1.3 copy-done.4
  94.0 3.0 %collective-permute-done.8 = bf16[4,32768]{1,0:T(4,128)(2,1)S(1)} collective-permute-done((bf16[4,32768]{1,0:T(4,128)(2,1)S(1)}, bf16[4,32768]{1,0:T(4,128)(2,1)S(1)}, u32[]{:S(2)}, u32[]{:S(2)}) %collective-permute-start.8) | collective-permute-done | bytes 262176 | tf_op jit(solution)/shard_map/ppermute | solution.py:29
  97.5 3.0 %collective-permute-start.9 = (bf16[8,32768]{1,0:T(8,128)(2,1)S(1)}, bf16[8,32768]{1,0:T(8,128)(2,1)S(1)}, u32[]{:S(2)}, u32[]{:S(2)}) collective-permute-start(bf16[8,32768]{1,0:T(8,128)(2,1)S(1)} %maximum_select_fusion.2), channel_id=1, source_target_pairs={{0,1},{1,0},{2,3},{3,2},{4,5},{5,4},{6,7},{7,6},{8,9},{9,8},{10,11... | collective-permute-start | bytes 1572872 | tf_op jit(solution)/shard_map/ppermute | solution.py:26
  100.5 6.0 %fusion = bf16[8,16,8,128]{3,2,1,0:T(8,128)(2,1)S(1)} fusion(bf16[2048,2048]{1,0:T(8,128)(2,1)} %all-gather.3.cloned.1.call-done, bf16[64,2048]{1,0:T(8,128)(2,1)S(1)} %copy-done.6), kind=kOutput, calls=%fused_computation.3 | convolution fusion | flops 537001984 | bytes 8912896 | tf_op jit(solution)/shard_map/dot_general | solution.py:165
  107.3 8.6 %all-to-all-start = ((bf16[16,128,64]{1,2,0:T(8,128)(2,1)}), bf16[16,128,64]{1,2,0:T(8,128)(2,1)S(1)}, u32[]{:S(2)}, u32[]{:S(2)}) async-start(bf16[16,128,64]{1,2,0:T(8,128)(2,1)} %bitcast.105), calls=%async_computation | async-start | bytes 524288 | tf_op jit(solution)/shard_map/all_to_all | solution.py:168
  117.4 0.8 fusion.15
  118.3 10.8 %all-to-all-done = bf16[16,128,64]{1,2,0:T(8,128)(2,1)S(1)} async-done(((bf16[16,128,64]{1,2,0:T(8,128)(2,1)}), bf16[16,128,64]{1,2,0:T(8,128)(2,1)S(1)}, u32[]{:S(2)}, u32[]{:S(2)}) %all-to-all-start) | async-done | bytes 262176 | tf_op jit(solution)/shard_map/all_to_all | solution.py:168
  129.1 0.8 copy.19.up_ref
  130.6 12.7 %shard_map.119 = (bf16[128,1024]{1,0:T(8,128)(2,1)}, bf16[128,1024]{1,0:T(8,128)(2,1)}, f32[384,1024]{1,0:T(8,128)}, f32[384,1024]{1,0:T(8,128)}, f32[2,256,1024]{2,1,0:T(8,128)}) custom-call(s32[6]{0:T(128)} %add_bitcast_fusion.ext_ref, f32[1,1024]{1,0:T(1,128)} %bitcast.120, bf16[128,1024]{1,0:T(8,128)(2,1)} %q_ref.1, ...), custom_call_target="tpu_custom_call" | custom-call | tf_op jit(solution)/shard_map/pallas_call | solution.py:113
  143.3 15.2 %all-gather.5.cloned.1.call-done = bf16[1024,2048]{1,0:T(8,128)(2,1)} async-done(((bf16[64,2048]{1,0:T(8,128)(2,1)}), bf16[1024,2048]{1,0:T(8,128)(2,1)}) %all-gather.5.cloned.1.call-update) | async-done | bytes 4194320 | tf_op jit(solution)/shard_map/all_gather | solution.py:135
  158.5 3.8 %convolution_convert_fusion = bf16[128,2048]{1,0:T(8,128)(2,1)} fusion(bf16[128,1024]{1,0:T(8,128)(2,1)} %get-tuple-element.12, bf16[1024,2048]{1,0:T(8,128)(2,1)} %all-gather.5.cloned.1.call-done), kind=kOutput, calls=%fused_computation | convolution fusion | flops 537133056 | bytes 4980736 | tf_op jit(solution)/shard_map/dot_general | solution.py:198
  162.3 1.7 reshape.172
  164.4 1.7 collective-permute-done.12
  166.7 7.4 %collective-permute-done.13 = bf16[4,32768]{1,0:T(4,128)(2,1)S(1)} collective-permute-done((bf16[4,32768]{1,0:T(4,128)(2,1)S(1)}, bf16[4,32768]{1,0:T(4,128)(2,1)S(1)}, u32[]{:S(2)}, u32[]{:S(2)}) %collective-permute-start.13) | collective-permute-done | bytes 262176 | tf_op jit(solution)/shard_map/ppermute | solution.py:29
  174.6 3.6 %collective-permute-done.14 = bf16[2,32768]{1,0:T(2,128)(2,1)S(1)} collective-permute-done((bf16[2,32768]{1,0:T(2,128)(2,1)S(1)}, bf16[2,32768]{1,0:T(2,128)(2,1)S(1)}, u32[]{:S(2)}, u32[]{:S(2)}) %collective-permute-start.14) | collective-permute-done | bytes 131104 | tf_op jit(solution)/shard_map/ppermute | solution.py:29
  179.2 4.2 %collective-permute-done.15 = bf16[1,32768]{1,0:T(2,128)(2,1)S(1)} collective-permute-done((bf16[1,32768]{1,0:T(2,128)(2,1)S(1)}, bf16[1,32768]{1,0:T(2,128)(2,1)S(1)}, u32[]{:S(2)}, u32[]{:S(2)}) %collective-permute-start.15) | collective-permute-done | bytes 65568 | tf_op jit(solution)/shard_map/ppermute | solution.py:29
  183.6 2.3 collective-permute-start.16
  185.9 2.7 %collective-permute-done.16 = bf16[1,32768]{1,0:T(2,128)(2,1)S(1)} collective-permute-done((bf16[1,32768]{1,0:T(2,128)(2,1)S(1)}, bf16[1,32768]{1,0:T(2,128)(2,1)S(1)}, u32[]{:S(2)}, u32[]{:S(2)}) %collective-permute-start.16) | collective-permute-done | bytes 65568 | tf_op jit(solution)/shard_map/ppermute | solution.py:29
  189.2 2.4 collective-permute-start.17
  191.6 0.8 copy.20
  192.4 8.1 %all-to-all-start.1 = ((bf16[1,128,16,64]{1,3,0,2:T(8,128)(2,1)}), bf16[1,128,16,64]{1,3,0,2:T(8,128)(2,1)S(1)}, u32[]{:S(2)}, u32[]{:S(2)}) async-start(bf16[1,128,16,64]{1,3,0,2:T(8,128)(2,1)} %bitcast.118), calls=%async_computation.1 | async-start | bytes 524288 | tf_op jit(solution)/shard_map/all_to_all | solution.py:204
  200.6 2.2 maximum_select_fusion.5
  202.8 1.2 collective-permute-start.18
  204.2 2.6 %collective-permute-start.11 = (bf16[2,256,1024]{2,1,0:T(8,128)(2,1)S(1)}, bf16[2,256,1024]{2,1,0:T(8,128)(2,1)}, u32[]{:S(2)}, u32[]{:S(2)}) collective-permute-start(bf16[2,256,1024]{2,1,0:T(8,128)(2,1)S(1)} %pad_maximum_fusion.3), channel_id=1, source_target_pairs={{1,0},{2,1},{3,2},{4,3},{5,4},{6,5},{7,6},{8,7},{9,8},{10,9},{11,1... | collective-permute-start | bytes 3145736 | tf_op jit(solution)/shard_map/ppermute | solution.py:63
  206.8 3.0 %collective-permute-start.10 = (bf16[2,256,1024]{2,1,0:T(8,128)(2,1)S(1)}, bf16[2,256,1024]{2,1,0:T(8,128)(2,1)}, u32[]{:S(2)}, u32[]{:S(2)}) collective-permute-start(bf16[2,256,1024]{2,1,0:T(8,128)(2,1)S(1)} %pad_maximum_fusion.3), channel_id=1, source_target_pairs={{0,1},{1,2},{2,3},{3,4},{4,5},{5,6},{6,7},{7,8},{8,9},{9,10},{10,1... | collective-permute-start | bytes 3145736 | tf_op jit(solution)/shard_map/ppermute | solution.py:62
  210.0 12.0 %collective-permute-done.18 = bf16[4,32768]{1,0:T(4,128)(2,1)} collective-permute-done((bf16[4,32768]{1,0:T(4,128)(2,1)}, bf16[4,32768]{1,0:T(4,128)(2,1)}, u32[]{:S(2)}, u32[]{:S(2)}) %collective-permute-start.18) | collective-permute-done | bytes 262176 | tf_op jit(solution)/shard_map/ppermute | solution.py:29
  222.0 1.8 maximum_select_fusion.3
  223.8 2.5 %collective-permute-start.19 = (bf16[8,32768]{1,0:T(8,128)(2,1)S(1)}, bf16[8,32768]{1,0:T(8,128)(2,1)S(1)}, u32[]{:S(2)}, u32[]{:S(2)}) collective-permute-start(bf16[8,32768]{1,0:T(8,128)(2,1)S(1)} %maximum_select_fusion.3), channel_id=1, source_target_pairs={{0,1},{1,0},{2,3},{3,2},{4,5},{5,4},{6,7},{7,6},{8,9},{9,8},{10,11... | collective-permute-start | bytes 1572872 | tf_op jit(solution)/shard_map/ppermute | solution.py:26
  226.4 5.7 %fusion.12 = f32[64,2048]{1,0:T(8,128)} fusion(bf16[2048,2048]{1,0:T(8,128)(2,1)} %all-gather.3.cloned.1.call-done, bf16[8,8,16,128]{3,2,1,0:T(8,128)(2,1)S(1)} %bitcast.116), kind=kOutput, calls=%fused_computation.34 | convolution fusion | flops 536870912 | bytes 9175040 | tf_op jit(solution)/shard_map/dot_general | solution.py:207
  232.8 2.2 collective-permute-done.11
  235.0 2.8 %fusion.11 = (bf16[128,1024]{1,0:T(8,128)(2,1)}, bf16[128,1024]{1,0:T(8,128)(2,1)}) fusion(f32[1,384,1024]{2,1,0:T(8,128)} %bitcast.114, bf16[2,256,1024]{2,1,0:T(8,128)(2,1)S(1)} %select_n.226, bf16[2,256,1024]{2,1,0:T(8,128)(2,1)} %collective-permute-done.11, bf16[2,256,1024]{2,1,0:T(8,128)(2,1)} %collective-permute-done.10, pred[]{:T(512)S(6)} %eq.38, ...), kind=kLoop, calls=%fused_computation.33 | loop fusion | flops 2883584 | bytes 3670018 | tf_op jit(solution)/shard_map/convert_element_type | solution.py:226
  (88 shorter events, 13.6 us)
Async XLA Ops:
  7.2 93.3 %all-gather.3.cloned.1.call-start = ((), (), s32[]{:S(2)}) async-start(), calls=%async_computation.2 | async-start | bytes 8912896 | tf_op jit(solution)/shard_map/all_gather | solution.py:134
  7.9 150.6 %all-gather.5.cloned.1.call-start = ((), (), s32[]{:S(2)}) async-start(), calls=%async_computation.3 | async-start | bytes 4456448 | tf_op jit(solution)/shard_map/all_gather | solution.py:135
  9.8 15.8 %collective-permute-start = (bf16[2,128,1024]{2,1,0:T(8,128)(2,1)}, bf16[2,128,1024]{2,1,0:T(8,128)(2,1)}, u32[]{:S(2)}, u32[]{:S(2)}) collective-permute-start(bf16[2,128,1024]{2,1,0:T(8,128)(2,1)} %pad_maximum_fusion.4), channel_id=1, source_target_pairs={{0,1},{1,2},{2,3},{3,4},{4,5},{5,6},{6,7},{7,8},{8,9},{9,10},{10,1... | collective-permute-start | bytes 1572872 | tf_op jit(solution)/shard_map/ppermute | solution.py:62
  13.5 22.3 %collective-permute-start.1 = (bf16[2,128,1024]{2,1,0:T(8,128)(2,1)}, bf16[2,128,1024]{2,1,0:T(8,128)(2,1)S(1)}, u32[]{:S(2)}, u32[]{:S(2)}) collective-permute-start(bf16[2,128,1024]{2,1,0:T(8,128)(2,1)} %pad_maximum_fusion.4), channel_id=1, source_target_pairs={{1,0},{2,1},{3,2},{4,3},{5,4},{6,5},{7,6},{8,7},{9,8},{10,9},{11,1... | collective-permute-start | bytes 1572872 | tf_op jit(solution)/shard_map/ppermute | solution.py:63
  19.3 2.3 copy-start.8
  19.3 4.8 %copy-start.10 = (s32[1,3]{1,0:T(1,128)S(1)}, s32[1,3]{1,0:T(1,128)}, u32[]{:S(2)}) copy-start(s32[1,3]{1,0:T(1,128)} %constant.90) | copy-start | bytes 40
  19.4 5.4 %copy-start.9 = (s32[3]{0:T(128)S(1)}, s32[3]{0:T(128)}, u32[]{:S(2)}) copy-start(s32[3]{0:T(128)} %constant.87.clone) | copy-start | bytes 40
  19.9 15.9 %copy-start = (bf16[128,1024]{1,0:T(8,128)(2,1)S(1)}, bf16[128,1024]{1,0:T(8,128)(2,1)}, u32[]{:S(2)}) copy-start(bf16[128,1024]{1,0:T(8,128)(2,1)} %param.10) | copy-start | bytes 786436
  19.9 15.9 %copy-start.1 = (bf16[128,1024]{1,0:T(8,128)(2,1)S(1)}, bf16[128,1024]{1,0:T(8,128)(2,1)}, u32[]{:S(2)}) copy-start(bf16[128,1024]{1,0:T(8,128)(2,1)} %param.9) | copy-start | bytes 786436
  20.0 4.9 %collective-permute-start.2 = (bf16[8,32768]{1,0:T(8,128)(2,1)S(1)}, bf16[8,32768]{1,0:T(8,128)(2,1)S(1)}, u32[]{:S(2)}, u32[]{:S(2)}) collective-permute-start(bf16[8,32768]{1,0:T(8,128)(2,1)S(1)} %constant_dynamic-slice_fusion.3), channel_id=1, source_target_pairs={{0,1},{1,0},{2,3},{3,2},{4,5},{5,4},{6,7},{7,6},{8,9},{9,8},{10,11... | collective-permute-start | bytes 1572872 | tf_op jit(solution)/shard_map/ppermute | solution.py:26
  25.2 12.0 %collective-permute-start.3 = (bf16[4,32768]{1,0:T(4,128)(2,1)S(1)}, bf16[4,32768]{1,0:T(4,128)(2,1)S(1)}, u32[]{:S(2)}, u32[]{:S(2)}) collective-permute-start(bf16[4,32768]{1,0:T(4,128)(2,1)S(1)} %constant_dynamic-slice_fusion.2), channel_id=1, source_target_pairs={{0,2},{2,0},{4,6},{6,4},{8,10},{10,8},{12,14},{14,12},{1,3},{3,1},... | collective-permute-start | bytes 786440 | tf_op jit(solution)/shard_map/ppermute | solution.py:29
  37.5 5.3 %collective-permute-start.4 = (bf16[2,32768]{1,0:T(2,128)(2,1)S(1)}, bf16[2,32768]{1,0:T(2,128)(2,1)S(1)}, u32[]{:S(2)}, u32[]{:S(2)}) collective-permute-start(bf16[2,32768]{1,0:T(2,128)(2,1)S(1)} %constant_dynamic-slice_fusion.1), channel_id=1, source_target_pairs={{0,4},{2,6},{4,0},{6,2},{8,12},{10,14},{12,8},{14,10},{1,5},{3,7},... | collective-permute-start | bytes 393224 | tf_op jit(solution)/shard_map/ppermute | solution.py:29
  43.2 4.8 %collective-permute-start.5 = (bf16[1,32768]{1,0:T(2,128)(2,1)S(1)}, bf16[1,32768]{1,0:T(2,128)(2,1)S(1)}, u32[]{:S(2)}, u32[]{:S(2)}) collective-permute-start(bf16[1,32768]{1,0:T(2,128)(2,1)S(1)} %constant_dynamic-slice_fusion), channel_id=1, source_target_pairs={{0,8},{2,10},{4,12},{6,14},{8,0},{10,2},{12,4},{14,6},{1,9},{3,11}... | collective-permute-start | bytes 196616 | tf_op jit(solution)/shard_map/ppermute | solution.py:29
  48.2 4.9 %collective-permute-start.6 = (bf16[1,32768]{1,0:T(2,128)(2,1)S(1)}, bf16[1,32768]{1,0:T(2,128)(2,1)S(1)}, u32[]{:S(2)}, u32[]{:S(2)}) collective-permute-start(bf16[1,32768]{1,0:T(2,128)(2,1)S(1)} %dynamic-slice_add_fusion.2), channel_id=1, source_target_pairs={{0,8},{2,10},{4,12},{6,14},{8,0},{10,2},{12,4},{14,6},{1,9},{3,11}... | collective-permute-start | bytes 196616 | tf_op jit(solution)/shard_map/ppermute | solution.py:29
  53.7 46.7 %copy-start.6 = (bf16[64,2048]{1,0:T(8,128)(2,1)S(1)}, bf16[64,2048]{1,0:T(8,128)(2,1)}, u32[]{:S(2)}) copy-start(bf16[64,2048]{1,0:T(8,128)(2,1)} %param.11) | copy-start | bytes 786436
  53.7 26.2 %collective-permute-start.7 = (bf16[2,32768]{1,0:T(2,128)(2,1)S(1)}, bf16[2,32768]{1,0:T(2,128)(2,1)S(1)}, u32[]{:S(2)}, u32[]{:S(2)}) collective-permute-start(bf16[2,32768]{1,0:T(2,128)(2,1)S(1)} %broadcast_select_fusion.3), channel_id=1, source_target_pairs={{0,4},{2,6},{4,0},{6,2},{8,12},{10,14},{12,8},{14,10},{1,5},{3,7},... | collective-permute-start | bytes 393224 | tf_op jit(solution)/shard_map/ppermute | solution.py:29
  80.5 16.6 %collective-permute-start.8 = (bf16[4,32768]{1,0:T(4,128)(2,1)S(1)}, bf16[4,32768]{1,0:T(4,128)(2,1)S(1)}, u32[]{:S(2)}, u32[]{:S(2)}) collective-permute-start(bf16[4,32768]{1,0:T(4,128)(2,1)S(1)} %maximum_select_fusion.4), channel_id=1, source_target_pairs={{0,2},{2,0},{4,6},{6,4},{8,10},{10,8},{12,14},{14,12},{1,3},{3,1},... | collective-permute-start | bytes 786440 | tf_op jit(solution)/shard_map/ppermute | solution.py:29
  92.7 1.3 copy-start.4
  94.0 3.0 %copy-start.5 = (bf16[1024,1024]{1,0:T(8,128)(2,1)}, bf16[1024,1024]{1,0:T(8,128)(2,1)S(1)}, u32[]{:S(2)}) copy-start(bf16[1024,1024]{1,0:T(8,128)(2,1)S(1)} %bitcast_dynamic-update-slice_fusion.3) | copy-start | bytes 6291460
  97.5 18.4 %collective-permute-start.9 = (bf16[8,32768]{1,0:T(8,128)(2,1)S(1)}, bf16[8,32768]{1,0:T(8,128)(2,1)S(1)}, u32[]{:S(2)}, u32[]{:S(2)}) collective-permute-start(bf16[8,32768]{1,0:T(8,128)(2,1)S(1)} %maximum_select_fusion.2), channel_id=1, source_target_pairs={{0,1},{1,0},{2,3},{3,2},{4,5},{5,4},{6,7},{7,6},{8,9},{9,8},{10,11... | collective-permute-start | bytes 1572872 | tf_op jit(solution)/shard_map/ppermute | solution.py:26
  107.3 21.8 %all-to-all-start = ((bf16[16,128,64]{1,2,0:T(8,128)(2,1)}), bf16[16,128,64]{1,2,0:T(8,128)(2,1)S(1)}, u32[]{:S(2)}, u32[]{:S(2)}) async-start(bf16[16,128,64]{1,2,0:T(8,128)(2,1)} %bitcast.105), calls=%async_computation | async-start | bytes 524288 | tf_op jit(solution)/shard_map/all_to_all | solution.py:168
  164.1 2.0 collective-permute-start.12
  166.2 25.5 %copy-start.7 = (bf16[128,1024]{1,0:T(8,128)(2,1)S(1)}, bf16[128,1024]{1,0:T(8,128)(2,1)}, u32[]{:S(2)}) copy-start(bf16[128,1024]{1,0:T(8,128)(2,1)} %get-tuple-element.12) | copy-start | bytes 786436
  166.3 7.7 %collective-permute-start.13 = (bf16[4,32768]{1,0:T(4,128)(2,1)S(1)}, bf16[4,32768]{1,0:T(4,128)(2,1)S(1)}, u32[]{:S(2)}, u32[]{:S(2)}) collective-permute-start(bf16[4,32768]{1,0:T(4,128)(2,1)S(1)} %dynamic-slice_convert_fusion.1), channel_id=1, source_target_pairs={{0,2},{2,0},{4,6},{6,4},{8,10},{10,8},{12,14},{14,12},{1,3},{3,1},... | collective-permute-start | bytes 786440 | tf_op jit(solution)/shard_map/ppermute | solution.py:29
  174.2 29.8 %copy-start.2 = (f32[384,1024]{1,0:T(8,128)S(1)}, f32[384,1024]{1,0:T(8,128)}, u32[]{:S(2)}) copy-start(f32[384,1024]{1,0:T(8,128)} %get-tuple-element.16) | copy-start | bytes 4718596
  174.2 29.8 %copy-start.3 = (f32[384,1024]{1,0:T(8,128)S(1)}, f32[384,1024]{1,0:T(8,128)}, u32[]{:S(2)}) copy-start(f32[384,1024]{1,0:T(8,128)} %get-tuple-element.17) | copy-start | bytes 4718596
  174.3 3.9 %collective-permute-start.14 = (bf16[2,32768]{1,0:T(2,128)(2,1)S(1)}, bf16[2,32768]{1,0:T(2,128)(2,1)S(1)}, u32[]{:S(2)}, u32[]{:S(2)}) collective-permute-start(bf16[2,32768]{1,0:T(2,128)(2,1)S(1)} %dynamic-slice_convert_fusion.2), channel_id=1, source_target_pairs={{0,4},{2,6},{4,0},{6,2},{8,12},{10,14},{12,8},{14,10},{1,5},{3,7},... | collective-permute-start | bytes 393224 | tf_op jit(solution)/shard_map/ppermute | solution.py:29
  178.5 4.9 %collective-permute-start.15 = (bf16[1,32768]{1,0:T(2,128)(2,1)S(1)}, bf16[1,32768]{1,0:T(2,128)(2,1)S(1)}, u32[]{:S(2)}, u32[]{:S(2)}) collective-permute-start(bf16[1,32768]{1,0:T(2,128)(2,1)S(1)} %dynamic-slice_convert_fusion.3), channel_id=1, source_target_pairs={{0,8},{2,10},{4,12},{6,14},{8,0},{10,2},{12,4},{14,6},{1,9},{3,11}... | collective-permute-start | bytes 196616 | tf_op jit(solution)/shard_map/ppermute | solution.py:29
  183.6 5.0 %collective-permute-start.16 = (bf16[1,32768]{1,0:T(2,128)(2,1)S(1)}, bf16[1,32768]{1,0:T(2,128)(2,1)S(1)}, u32[]{:S(2)}, u32[]{:S(2)}) collective-permute-start(bf16[1,32768]{1,0:T(2,128)(2,1)S(1)} %add_convert_fusion), channel_id=1, source_target_pairs={{0,8},{2,10},{4,12},{6,14},{8,0},{10,2},{12,4},{14,6},{1,9},{3,11}... | collective-permute-start | bytes 196616 | tf_op jit(solution)/shard_map/ppermute | solution.py:29
  189.2 11.4 %collective-permute-start.17 = (bf16[2,32768]{1,0:T(2,128)(2,1)S(1)}, bf16[2,32768]{1,0:T(2,128)(2,1)}, u32[]{:S(2)}, u32[]{:S(2)}) collective-permute-start(bf16[2,32768]{1,0:T(2,128)(2,1)S(1)} %broadcast_select_fusion.2), channel_id=1, source_target_pairs={{0,4},{2,6},{4,0},{6,2},{8,12},{10,14},{12,8},{14,10},{1,5},{3,7},... | collective-permute-start | bytes 393224 | tf_op jit(solution)/shard_map/ppermute | solution.py:29
  192.4 17.3 %all-to-all-start.1 = ((bf16[1,128,16,64]{1,3,0,2:T(8,128)(2,1)}), bf16[1,128,16,64]{1,3,0,2:T(8,128)(2,1)S(1)}, u32[]{:S(2)}, u32[]{:S(2)}) async-start(bf16[1,128,16,64]{1,3,0,2:T(8,128)(2,1)} %bitcast.118), calls=%async_computation.1 | async-start | bytes 524288 | tf_op jit(solution)/shard_map/all_to_all | solution.py:204
  202.8 19.2 %collective-permute-start.18 = (bf16[4,32768]{1,0:T(4,128)(2,1)}, bf16[4,32768]{1,0:T(4,128)(2,1)}, u32[]{:S(2)}, u32[]{:S(2)}) collective-permute-start(bf16[4,32768]{1,0:T(4,128)(2,1)} %maximum_select_fusion.5), channel_id=1, source_target_pairs={{0,2},{2,0},{4,6},{6,4},{8,10},{10,8},{12,14},{14,12},{1,3},{3,1},... | collective-permute-start | bytes 786440 | tf_op jit(solution)/shard_map/ppermute | solution.py:29
  204.2 30.8 %collective-permute-start.11 = (bf16[2,256,1024]{2,1,0:T(8,128)(2,1)S(1)}, bf16[2,256,1024]{2,1,0:T(8,128)(2,1)}, u32[]{:S(2)}, u32[]{:S(2)}) collective-permute-start(bf16[2,256,1024]{2,1,0:T(8,128)(2,1)S(1)} %pad_maximum_fusion.3), channel_id=1, source_target_pairs={{1,0},{2,1},{3,2},{4,3},{5,4},{6,5},{7,6},{8,7},{9,8},{10,9},{11,1... | collective-permute-start | bytes 3145736 | tf_op jit(solution)/shard_map/ppermute | solution.py:63
  206.8 28.3 %collective-permute-start.10 = (bf16[2,256,1024]{2,1,0:T(8,128)(2,1)S(1)}, bf16[2,256,1024]{2,1,0:T(8,128)(2,1)}, u32[]{:S(2)}, u32[]{:S(2)}) collective-permute-start(bf16[2,256,1024]{2,1,0:T(8,128)(2,1)S(1)} %pad_maximum_fusion.3), channel_id=1, source_target_pairs={{0,1},{1,2},{2,3},{3,4},{4,5},{5,6},{6,7},{7,8},{8,9},{9,10},{10,1... | collective-permute-start | bytes 3145736 | tf_op jit(solution)/shard_map/ppermute | solution.py:62
  223.8 8.3 %collective-permute-start.19 = (bf16[8,32768]{1,0:T(8,128)(2,1)S(1)}, bf16[8,32768]{1,0:T(8,128)(2,1)S(1)}, u32[]{:S(2)}, u32[]{:S(2)}) collective-permute-start(bf16[8,32768]{1,0:T(8,128)(2,1)S(1)} %maximum_select_fusion.3), channel_id=1, source_target_pairs={{0,1},{1,0},{2,3},{3,2},{4,5},{5,4},{6,7},{7,6},{8,9},{9,8},{10,11... | collective-permute-start | bytes 1572872 | tf_op jit(solution)/shard_map/ppermute | solution.py:26
Sparse Core Ops, SparseCore 0:
  10.2 85.9 all-gather.2
  98.3 60.1 all-gather.4

commit v18 on v14

--- a/solution.py
+++ b/solution.py
@@ -189,15 +189,16 @@
         terms = dg
         global_local = terms if global_local is None else global_local + terms
     grad_ext = jnp.stack(grad_ext)
-    global_total = butterfly_sum(global_local, jnp.bfloat16)
-
     attn_out = jnp.concatenate(attn_rows, axis=0)
-    layer_out = jnp.dot(attn_out, weight_all, preferred_element_type=jnp.float32).astype(
-        jnp.bfloat16
-    )
     attn_cols = lax.all_to_all(
         attn_out.reshape(tok_rows, count, w_rows), SEQ, 1, 0, tiled=False
     ).reshape(count * tok_rows, w_rows)
+    attn_cols, global_local = lax.optimization_barrier((attn_cols, global_local))
+    global_total = butterfly_sum(global_local, jnp.bfloat16)
+
+    layer_out = jnp.dot(attn_out, weight_all, preferred_element_type=jnp.float32).astype(
+        jnp.bfloat16
+    )
     grad_weight = lax.dot_general(
         attn_cols, grad_out_all, (((0,), (0,)), ((), ())), preferred_element_type=jnp.float32
     )

time: 239 us -> 253 us (1.059)
  waiting for transfers between devices: 81 us -> 92.8 us
  other arithmetic: 17.7 us -> 21.8 us
    ppermute x12, waiting for transfers between devices: 42.2 us -> 64.8 us  [xor_swap(): return lax.ppermute(x, 'chip', [(i, i ^ m) for i in range(n)])]
    all_to_all x1, waiting for transfers between devices: 17.3 us -> 6.35 us  [local(): lax.all_to_all(attn_out.reshape(tok_rows, count, w_rows), SEQ, 1, 0, tile...]
    dynamic_update_slice x11, other arithmetic: 6.64 us -> 10.7 us  [local(): lax.dynamic_update_slice_in_dim(grad_ext[side], cur + term, start, axis=0)]
  transfers between devices with their start and end apart: 24 -> 24, of which waited for: 14 -> 14; matrix products, arithmetic and copies ran while one was open for 19% -> 20% of each run, Pallas kernels for 5% -> 5%
where the time goes in v18:
time: 253 us; the launch traced here: 252 us
  waiting for transfers between devices  92.8 us (37%)
  starting transfers between devices  75 us (30%)
  other arithmetic  21.8 us (9%)
  between operations  17.9 us (7%)
  local copies, waits for them, and re-layouts  16.6 us (7%)
  matrix products  15.5 us (6%)
  Pallas kernels  12.3 us (5%)
    ppermute x12, waiting for transfers between devices, xor_swap(): return lax.ppermute(x, 'chip', [(i, i ^ m) for i in range(n)])  64.8 us
    ppermute x12, starting transfers between devices, xor_swap(): return lax.ppermute(x, 'chip', [(i, i ^ m) for i in range(n)])  40.9 us
    pallas_call x1, Pallas kernels, attention(): pl.pallas_call(_attn_kernel, grid=(heads,), in_specs=[pl.BlockSpec((1, ke...  12.3 us
    dynamic_update_slice x11, other arithmetic, local(): lax.dynamic_update_slice_in_dim(grad_ext[side], cur + term, start, axis=0)  10.7 us
    all_to_all x1, waiting for transfers between devices, local(): lax.all_to_all(upstream_cols.reshape(count, tok_rows, w_rows), SEQ, 0, 0,...  10.7 us
    ppermute x2, waiting for transfers between devices, halo(): after = lax.ppermute(shard, SEQ, down)  10.1 us
    all_to_all x1, starting transfers between devices, local(): lax.all_to_all(upstream_cols.reshape(count, tok_rows, w_rows), SEQ, 0, 0,...  8.7 us
    ppermute x4, starting transfers between devices, xor_swap(): return lax.ppermute(x, 'core', [(i, i ^ 1) for i in range(n)])  8.56 us
  transfers between devices with their start and end apart: 24, of which 14 were waited for; matrix products, arithmetic and copies ran while one was open for 20% of the time, Pallas kernels for 5%

profile of v18, /device:TPU:11, one launch (start us, length us, event | category | flops | bytes accessed | tf_op | source)
XLA Modules:
  0.0 251.8 jit_solution(6505692244384631574)
XLA Ops:
  7.9 1.9 pad_maximum_fusion.4
  9.8 3.7 %collective-permute-start = (bf16[2,128,1024]{2,1,0:T(8,128)(2,1)}, bf16[2,128,1024]{2,1,0:T(8,128)(2,1)S(1)}, u32[]{:S(2)}, u32[]{:S(2)}) collective-permute-start(bf16[2,128,1024]{2,1,0:T(8,128)(2,1)} %pad_maximum_fusion.4), channel_id=1, source_target_pairs={{0,1},{1,2},{2,3},{3,4},{4,5},{5,6},{6,7},{7,8},{8,9},{9,10},{10,1... | collective-permute-start | bytes 1572872 | tf_op jit(solution)/shard_map/ppermute | solution.py:61
  13.5 1.9 collective-permute-start.1
  15.5 1.3 fusion.27
  18.1 1.1 broadcast_select_fusion.1
  20.8 1.5 collective-permute-start.2
  25.7 10.1 %collective-permute-done.1 = bf16[2,128,1024]{2,1,0:T(8,128)(2,1)S(1)} collective-permute-done((bf16[2,128,1024]{2,1,0:T(8,128)(2,1)}, bf16[2,128,1024]{2,1,0:T(8,128)(2,1)S(1)}, u32[]{:S(2)}, u32[]{:S(2)}) %collective-permute-start.1) | collective-permute-done | bytes 524320 | tf_op jit(solution)/shard_map/ppermute | solution.py:62
  37.3 5.6 %collective-permute-done.4 = bf16[2,32768]{1,0:T(2,128)(2,1)S(1)} collective-permute-done((bf16[2,32768]{1,0:T(2,128)(2,1)S(1)}, bf16[2,32768]{1,0:T(2,128)(2,1)S(1)}, u32[]{:S(2)}, u32[]{:S(2)}) %collective-permute-start.4) | collective-permute-done | bytes 131104 | tf_op jit(solution)/shard_map/ppermute | solution.py:28
  43.2 1.8 collective-permute-start.5
  45.1 2.9 %collective-permute-done.5 = bf16[1,32768]{1,0:T(2,128)(2,1)S(1)} collective-permute-done((bf16[1,32768]{1,0:T(2,128)(2,1)S(1)}, bf16[1,32768]{1,0:T(2,128)(2,1)S(1)}, u32[]{:S(2)}, u32[]{:S(2)}) %collective-permute-start.5) | collective-permute-done | bytes 65568 | tf_op jit(solution)/shard_map/ppermute | solution.py:28
  48.2 1.8 collective-permute-start.6
  50.0 3.1 %collective-permute-done.6 = bf16[1,32768]{1,0:T(2,128)(2,1)S(1)} collective-permute-done((bf16[1,32768]{1,0:T(2,128)(2,1)S(1)}, bf16[1,32768]{1,0:T(2,128)(2,1)S(1)}, u32[]{:S(2)}, u32[]{:S(2)}) %collective-permute-start.6) | collective-permute-done | bytes 65568 | tf_op jit(solution)/shard_map/ppermute | solution.py:28
  53.7 15.8 %collective-permute-start.7 = (bf16[2,32768]{1,0:T(2,128)(2,1)S(1)}, bf16[2,32768]{1,0:T(2,128)(2,1)S(1)}, u32[]{:S(2)}, u32[]{:S(2)}) collective-permute-start(bf16[2,32768]{1,0:T(2,128)(2,1)S(1)} %broadcast_select_fusion.3), channel_id=1, source_target_pairs={{0,4},{2,6},{4,0},{6,2},{8,12},{10,14},{12,8},{14,10},{1,5},{3,7},... | collective-permute-start | bytes 393224 | tf_op jit(solution)/shard_map/ppermute | solution.py:28
  69.6 13.0 %collective-permute-done.7 = bf16[2,32768]{1,0:T(2,128)(2,1)S(1)} collective-permute-done((bf16[2,32768]{1,0:T(2,128)(2,1)S(1)}, bf16[2,32768]{1,0:T(2,128)(2,1)S(1)}, u32[]{:S(2)}, u32[]{:S(2)}) %collective-permute-start.7) | collective-permute-done | bytes 131104 | tf_op jit(solution)/shard_map/ppermute | solution.py:28
  83.1 9.5 %collective-permute-start.8 = (bf16[4,32768]{1,0:T(4,128)(2,1)S(1)}, bf16[4,32768]{1,0:T(4,128)(2,1)S(1)}, u32[]{:S(2)}, u32[]{:S(2)}) collective-permute-start(bf16[4,32768]{1,0:T(4,128)(2,1)S(1)} %maximum_select_fusion.4), channel_id=1, source_target_pairs={{0,2},{2,0},{4,6},{6,4},{8,10},{10,8},{12,14},{14,12},{1,3},{3,1},... | collective-permute-start | bytes 786440 | tf_op jit(solution)/shard_map/ppermute | solution.py:28
  92.7 1.4 copy-done.6
  94.1 2.8 %collective-permute-done.8 = bf16[4,32768]{1,0:T(4,128)(2,1)S(1)} collective-permute-done((bf16[4,32768]{1,0:T(4,128)(2,1)S(1)}, bf16[4,32768]{1,0:T(4,128)(2,1)S(1)}, u32[]{:S(2)}, u32[]{:S(2)}) %collective-permute-start.8) | collective-permute-done | bytes 262176 | tf_op jit(solution)/shard_map/ppermute | solution.py:28
  97.3 3.1 %collective-permute-start.9 = (bf16[8,32768]{1,0:T(8,128)(2,1)S(1)}, bf16[8,32768]{1,0:T(8,128)(2,1)S(1)}, u32[]{:S(2)}, u32[]{:S(2)}) collective-permute-start(bf16[8,32768]{1,0:T(8,128)(2,1)S(1)} %maximum_select_fusion.2), channel_id=1, source_target_pairs={{0,1},{1,0},{2,3},{3,2},{4,5},{5,4},{6,7},{7,6},{8,9},{9,8},{10,11... | collective-permute-start | bytes 1572872 | tf_op jit(solution)/shard_map/ppermute | solution.py:25
  100.3 6.0 %fusion = bf16[8,16,8,128]{3,2,1,0:T(8,128)(2,1)S(1)} fusion(bf16[2048,2048]{1,0:T(8,128)(2,1)} %all-gather.3.cloned.1.call-done, bf16[64,2048]{1,0:T(8,128)(2,1)S(1)} %copy-done.8), kind=kOutput, calls=%fused_computation.5 | convolution fusion | flops 537001984 | bytes 8912896 | tf_op jit(solution)/shard_map/dot_general | solution.py:155
  107.2 8.7 %all-to-all-start = ((bf16[16,128,64]{1,2,0:T(8,128)(2,1)}), bf16[16,128,64]{1,2,0:T(8,128)(2,1)S(1)}, u32[]{:S(2)}, u32[]{:S(2)}) async-start(bf16[16,128,64]{1,2,0:T(8,128)(2,1)} %bitcast.108), calls=%async_computation | async-start | bytes 524288 | tf_op jit(solution)/shard_map/all_to_all | solution.py:158
  118.3 10.7 %all-to-all-done = bf16[16,128,64]{1,2,0:T(8,128)(2,1)S(1)} async-done(((bf16[16,128,64]{1,2,0:T(8,128)(2,1)}), bf16[16,128,64]{1,2,0:T(8,128)(2,1)S(1)}, u32[]{:S(2)}, u32[]{:S(2)}) %all-to-all-start) | async-done | bytes 262176 | tf_op jit(solution)/shard_map/all_to_all | solution.py:158
  130.5 12.3 %shard_map.119 = (bf16[128,1024]{1,0:T(8,128)(2,1)}, bf16[128,1024]{1,0:T(8,128)(2,1)}, f32[768,1024]{1,0:T(8,128)}, f32[768,1024]{1,0:T(8,128)}, f32[2,256,1024]{2,1,0:T(8,128)}) custom-call(f32[1,1024]{1,0:T(1,128)} %bitcast.122, bf16[128,1024]{1,0:T(8,128)(2,1)} %q_ref.1, bf16[1024,1024]{1,0:T(8,128)(2,1)} %get-tuple-element.26.k_ref, ...), custom_call_target="tpu_custom_call" | custom-call | tf_op jit(solution)/shard_map/pallas_call | solution.py:101
  142.9 2.2 slice_select_fusion
  145.0 1.2 fusion.13
  146.3 1.2 fusion.12
  148.3 4.6 %all-to-all-start.1 = ((bf16[1,128,16,64]{1,3,0,2:T(8,128)(2,1)}), bf16[1,128,16,64]{1,3,0,2:T(8,128)(2,1)S(1)}, u32[]{:S(2)}, u32[]{:S(2)}) async-start(bf16[1,128,16,64]{1,3,0,2:T(8,128)(2,1)} %bitcast.120), calls=%async_computation.1 | async-start | bytes 524288 | tf_op jit(solution)/shard_map/all_to_all | solution.py:193
  152.9 1.2 add_dynamic-update-slice_fusion.3
  154.1 1.1 add_dynamic-update-slice_fusion.2
  155.2 6.4 %all-to-all-done.1 = bf16[1,128,16,64]{1,3,0,2:T(8,128)(2,1)S(1)} async-done(((bf16[1,128,16,64]{1,3,0,2:T(8,128)(2,1)}), bf16[1,128,16,64]{1,3,0,2:T(8,128)(2,1)S(1)}, u32[]{:S(2)}, u32[]{:S(2)}) %all-to-all-start.1) | async-done | bytes 262176 | tf_op jit(solution)/shard_map/all_to_all | solution.py:193
  161.9 2.8 %reshape.176 = f32[16,32768]{1,0:T(8,128)} reshape(f32[2,256,1024]{2,1,0:T(8,128)} %get-tuple-element.17) | data formatting | bytes 4194304 | tf_op jit(solution)/shard_map/reshape | solution.py:35
  164.6 1.4 dynamic-slice_convert_fusion
  166.1 1.2 fusion.7
  167.3 1.3 fusion.6
  168.9 1.2 collective-permute-start.13
  170.6 5.7 %collective-permute-done.13 = bf16[4,32768]{1,0:T(4,128)(2,1)S(1)} collective-permute-done((bf16[4,32768]{1,0:T(4,128)(2,1)S(1)}, bf16[4,32768]{1,0:T(4,128)(2,1)S(1)}, u32[]{:S(2)}, u32[]{:S(2)}) %collective-permute-start.13) | collective-permute-done | bytes 262176 | tf_op jit(solution)/shard_map/ppermute | solution.py:28
  176.6 2.1 collective-permute-start.14
  179.9 1.7 collective-permute-done.14
  182.3 4.4 %collective-permute-done.15 = bf16[1,32768]{1,0:T(2,128)(2,1)S(1)} collective-permute-done((bf16[1,32768]{1,0:T(2,128)(2,1)S(1)}, bf16[1,32768]{1,0:T(2,128)(2,1)S(1)}, u32[]{:S(2)}, u32[]{:S(2)}) %collective-permute-start.15) | collective-permute-done | bytes 65568 | tf_op jit(solution)/shard_map/ppermute | solution.py:28
  187.4 4.4 %collective-permute-done.16 = bf16[1,32768]{1,0:T(2,128)(2,1)S(1)} collective-permute-done((bf16[1,32768]{1,0:T(2,128)(2,1)S(1)}, bf16[1,32768]{1,0:T(2,128)(2,1)S(1)}, u32[]{:S(2)}, u32[]{:S(2)}) %collective-permute-start.16) | collective-permute-done | bytes 65568 | tf_op jit(solution)/shard_map/ppermute | solution.py:28
  192.4 6.1 %collective-permute-start.17 = (bf16[2,32768]{1,0:T(2,128)(2,1)S(1)}, bf16[2,32768]{1,0:T(2,128)(2,1)S(1)}, u32[]{:S(2)}, u32[]{:S(2)}) collective-permute-start(bf16[2,32768]{1,0:T(2,128)(2,1)S(1)} %broadcast_select_fusion.2), channel_id=1, source_target_pairs={{0,4},{2,6},{4,0},{6,2},{8,12},{10,14},{12,8},{14,10},{1,5},{3,7},... | collective-permute-start | bytes 393224 | tf_op jit(solution)/shard_map/ppermute | solution.py:28
  198.6 4.1 %collective-permute-start.10 = (bf16[2,256,1024]{2,1,0:T(8,128)(2,1)S(1)}, bf16[2,256,1024]{2,1,0:T(8,128)(2,1)}, u32[]{:S(2)}, u32[]{:S(2)}) collective-permute-start(bf16[2,256,1024]{2,1,0:T(8,128)(2,1)S(1)} %pad_maximum_fusion.3), channel_id=1, source_target_pairs={{0,1},{1,2},{2,3},{3,4},{4,5},{5,6},{6,7},{7,8},{8,9},{9,10},{10,1... | collective-permute-start | bytes 3145736 | tf_op jit(solution)/shard_map/ppermute | solution.py:61
  202.7 2.4 collective-permute-start.11
  205.6 1.3 collective-permute-start.18
  207.0 3.7 %convolution_convert_fusion = bf16[128,2048]{1,0:T(8,128)(2,1)} fusion(bf16[128,1024]{1,0:T(8,128)(2,1)S(1)} %copy-done.10, bf16[1024,2048]{1,0:T(8,128)(2,1)} %all-gather.5.cloned.1.call-done), kind=kOutput, calls=%fused_computation | convolution fusion | flops 537133056 | bytes 4980736 | tf_op jit(solution)/shard_map/dot_general | solution.py:199
  210.7 20.6 %collective-permute-done.18 = bf16[4,32768]{1,0:T(4,128)(2,1)S(1)} collective-permute-done((bf16[4,32768]{1,0:T(4,128)(2,1)S(1)}, bf16[4,32768]{1,0:T(4,128)(2,1)S(1)}, u32[]{:S(2)}, u32[]{:S(2)}) %collective-permute-start.18) | collective-permute-done | bytes 262176 | tf_op jit(solution)/shard_map/ppermute | solution.py:28
  231.8 3.9 %collective-permute-start.19 = (bf16[8,32768]{1,0:T(8,128)(2,1)S(1)}, bf16[8,32768]{1,0:T(8,128)(2,1)S(1)}, u32[]{:S(2)}, u32[]{:S(2)}) collective-permute-start(bf16[8,32768]{1,0:T(8,128)(2,1)S(1)} %maximum_select_fusion.3), channel_id=1, source_target_pairs={{0,1},{1,0},{2,3},{3,2},{4,5},{5,4},{6,7},{7,6},{8,9},{9,8},{10,11... | collective-permute-start | bytes 1572872 | tf_op jit(solution)/shard_map/ppermute | solution.py:25
  235.7 5.7 %fusion.29 = f32[64,2048]{1,0:T(8,128)} fusion(bf16[2048,64]{0,1:T(8,128)(2,1)S(1)} %bitcast.117, bf16[2048,2048]{1,0:T(8,128)(2,1)} %all-gather.3.cloned.1.call-done), kind=kOutput, calls=%fused_computation.104 | convolution fusion | flops 536870912 | bytes 9175040 | tf_op jit(solution)/shard_map/dot_general | solution.py:202
  242.2 2.8 %fusion.15 = (bf16[128,1024]{1,0:T(8,128)(2,1)}, bf16[128,1024]{1,0:T(8,128)(2,1)}) fusion(f32[1,384,1024]{2,1,0:T(8,128)} %copy-done, bf16[2,256,1024]{2,1,0:T(8,128)(2,1)S(1)} %select_n.248, bf16[2,256,1024]{2,1,0:T(8,128)(2,1)} %collective-permute-done.11, bf16[2,256,1024]{2,1,0:T(8,128)(2,1)} %collective-permute-done.10, pred[]{:T(512)S(6)} %eq.38, ...), kind=kLoop, calls=%fused_computation.49 | loop fusion | flops 2883584 | bytes 3670018 | tf_op jit(solution)/shard_map/convert_element_type | solution.py:221
  (107 shorter events, 18.9 us)
Async XLA Ops:
  7.2 93.2 %all-gather.3.cloned.1.call-start = ((), (), s32[]{:S(2)}) async-start(), calls=%async_computation.2 | async-start | bytes 8912896 | tf_op jit(solution)/shard_map/all_gather | solution.py:124
  7.9 199.1 %all-gather.5.cloned.1.call-start = ((), (), s32[]{:S(2)}) async-start(), calls=%async_computation.3 | async-start | bytes 4456448 | tf_op jit(solution)/shard_map/all_gather | solution.py:125
  9.8 15.9 %collective-permute-start = (bf16[2,128,1024]{2,1,0:T(8,128)(2,1)}, bf16[2,128,1024]{2,1,0:T(8,128)(2,1)S(1)}, u32[]{:S(2)}, u32[]{:S(2)}) collective-permute-start(bf16[2,128,1024]{2,1,0:T(8,128)(2,1)} %pad_maximum_fusion.4), channel_id=1, source_target_pairs={{0,1},{1,2},{2,3},{3,4},{4,5},{5,6},{6,7},{7,8},{8,9},{9,10},{10,1... | collective-permute-start | bytes 1572872 | tf_op jit(solution)/shard_map/ppermute | solution.py:61
  13.5 22.3 %collective-permute-start.1 = (bf16[2,128,1024]{2,1,0:T(8,128)(2,1)}, bf16[2,128,1024]{2,1,0:T(8,128)(2,1)S(1)}, u32[]{:S(2)}, u32[]{:S(2)}) collective-permute-start(bf16[2,128,1024]{2,1,0:T(8,128)(2,1)} %pad_maximum_fusion.4), channel_id=1, source_target_pairs={{1,0},{2,1},{3,2},{4,3},{5,4},{6,5},{7,6},{8,7},{9,8},{10,9},{11,1... | collective-permute-start | bytes 1572872 | tf_op jit(solution)/shard_map/ppermute | solution.py:62
  19.3 3.0 %copy-start.12 = (s32[1,3]{1,0:T(1,128)S(1)}, s32[1,3]{1,0:T(1,128)}, u32[]{:S(2)}) copy-start(s32[1,3]{1,0:T(1,128)} %param.14) | copy-start | bytes 40
  19.3 5.6 %copy-start.13 = (s32[3]{0:T(128)S(1)}, s32[3]{0:T(128)}, u32[]{:S(2)}) copy-start(s32[3]{0:T(128)} %constant.91.clone) | copy-start | bytes 40
  19.9 16.0 %copy-start.4 = (bf16[128,1024]{1,0:T(8,128)(2,1)S(1)}, bf16[128,1024]{1,0:T(8,128)(2,1)}, u32[]{:S(2)}) copy-start(bf16[128,1024]{1,0:T(8,128)(2,1)} %param.10) | copy-start | bytes 786436
  19.9 15.9 %copy-start.5 = (bf16[128,1024]{1,0:T(8,128)(2,1)S(1)}, bf16[128,1024]{1,0:T(8,128)(2,1)}, u32[]{:S(2)}) copy-start(bf16[128,1024]{1,0:T(8,128)(2,1)} %param.9) | copy-start | bytes 786436
  20.8 4.3 %collective-permute-start.2 = (bf16[8,32768]{1,0:T(8,128)(2,1)}, bf16[8,32768]{1,0:T(8,128)(2,1)S(1)}, u32[]{:S(2)}, u32[]{:S(2)}) collective-permute-start(bf16[8,32768]{1,0:T(8,128)(2,1)} %constant_dynamic-slice_fusion.3), channel_id=1, source_target_pairs={{0,1},{1,0},{2,3},{3,2},{4,5},{5,4},{6,7},{7,6},{8,9},{9,8},{10,11... | collective-permute-start | bytes 1572872 | tf_op jit(solution)/shard_map/ppermute | solution.py:25
  25.3 11.3 %collective-permute-start.3 = (bf16[4,32768]{1,0:T(4,128)(2,1)S(1)}, bf16[4,32768]{1,0:T(4,128)(2,1)S(1)}, u32[]{:S(2)}, u32[]{:S(2)}) collective-permute-start(bf16[4,32768]{1,0:T(4,128)(2,1)S(1)} %constant_dynamic-slice_fusion.2), channel_id=1, source_target_pairs={{0,2},{2,0},{4,6},{6,4},{8,10},{10,8},{12,14},{14,12},{1,3},{3,1},... | collective-permute-start | bytes 786440 | tf_op jit(solution)/shard_map/ppermute | solution.py:28
  37.0 5.9 %collective-permute-start.4 = (bf16[2,32768]{1,0:T(2,128)(2,1)S(1)}, bf16[2,32768]{1,0:T(2,128)(2,1)S(1)}, u32[]{:S(2)}, u32[]{:S(2)}) collective-permute-start(bf16[2,32768]{1,0:T(2,128)(2,1)S(1)} %constant_dynamic-slice_fusion.1), channel_id=1, source_target_pairs={{0,4},{2,6},{4,0},{6,2},{8,12},{10,14},{12,8},{14,10},{1,5},{3,7},... | collective-permute-start | bytes 393224 | tf_op jit(solution)/shard_map/ppermute | solution.py:28
  43.2 4.8 %collective-permute-start.5 = (bf16[1,32768]{1,0:T(2,128)(2,1)S(1)}, bf16[1,32768]{1,0:T(2,128)(2,1)S(1)}, u32[]{:S(2)}, u32[]{:S(2)}) collective-permute-start(bf16[1,32768]{1,0:T(2,128)(2,1)S(1)} %constant_dynamic-slice_fusion), channel_id=1, source_target_pairs={{0,8},{2,10},{4,12},{6,14},{8,0},{10,2},{12,4},{14,6},{1,9},{3,11}... | collective-permute-start | bytes 196616 | tf_op jit(solution)/shard_map/ppermute | solution.py:28
  48.2 4.9 %collective-permute-start.6 = (bf16[1,32768]{1,0:T(2,128)(2,1)S(1)}, bf16[1,32768]{1,0:T(2,128)(2,1)S(1)}, u32[]{:S(2)}, u32[]{:S(2)}) collective-permute-start(bf16[1,32768]{1,0:T(2,128)(2,1)S(1)} %dynamic-slice_add_fusion.2), channel_id=1, source_target_pairs={{0,8},{2,10},{4,12},{6,14},{8,0},{10,2},{12,4},{14,6},{1,9},{3,11}... | collective-permute-start | bytes 196616 | tf_op jit(solution)/shard_map/ppermute | solution.py:28
  53.7 46.7 %copy-start.8 = (bf16[64,2048]{1,0:T(8,128)(2,1)S(1)}, bf16[64,2048]{1,0:T(8,128)(2,1)}, u32[]{:S(2)}) copy-start(bf16[64,2048]{1,0:T(8,128)(2,1)} %param.11) | copy-start | bytes 786436
  53.7 28.9 %collective-permute-start.7 = (bf16[2,32768]{1,0:T(2,128)(2,1)S(1)}, bf16[2,32768]{1,0:T(2,128)(2,1)S(1)}, u32[]{:S(2)}, u32[]{:S(2)}) collective-permute-start(bf16[2,32768]{1,0:T(2,128)(2,1)S(1)} %broadcast_select_fusion.3), channel_id=1, source_target_pairs={{0,4},{2,6},{4,0},{6,2},{8,12},{10,14},{12,8},{14,10},{1,5},{3,7},... | collective-permute-start | bytes 393224 | tf_op jit(solution)/shard_map/ppermute | solution.py:28
  83.1 13.8 %collective-permute-start.8 = (bf16[4,32768]{1,0:T(4,128)(2,1)S(1)}, bf16[4,32768]{1,0:T(4,128)(2,1)S(1)}, u32[]{:S(2)}, u32[]{:S(2)}) collective-permute-start(bf16[4,32768]{1,0:T(4,128)(2,1)S(1)} %maximum_select_fusion.4), channel_id=1, source_target_pairs={{0,2},{2,0},{4,6},{6,4},{8,10},{10,8},{12,14},{14,12},{1,3},{3,1},... | collective-permute-start | bytes 786440 | tf_op jit(solution)/shard_map/ppermute | solution.py:28
  92.6 4.2 %copy-start.7 = (bf16[1024,1024]{1,0:T(8,128)(2,1)}, bf16[1024,1024]{1,0:T(8,128)(2,1)S(1)}, u32[]{:S(2)}) copy-start(bf16[1024,1024]{1,0:T(8,128)(2,1)S(1)} %bitcast_dynamic-update-slice_fusion.5) | copy-start | bytes 6291460
  92.7 1.4 copy-start.6
  97.3 18.6 %collective-permute-start.9 = (bf16[8,32768]{1,0:T(8,128)(2,1)S(1)}, bf16[8,32768]{1,0:T(8,128)(2,1)S(1)}, u32[]{:S(2)}, u32[]{:S(2)}) collective-permute-start(bf16[8,32768]{1,0:T(8,128)(2,1)S(1)} %maximum_select_fusion.2), channel_id=1, source_target_pairs={{0,1},{1,0},{2,3},{3,2},{4,5},{5,4},{6,7},{7,6},{8,9},{9,8},{10,11... | collective-permute-start | bytes 1572872 | tf_op jit(solution)/shard_map/ppermute | solution.py:25
  107.2 21.9 %all-to-all-start = ((bf16[16,128,64]{1,2,0:T(8,128)(2,1)}), bf16[16,128,64]{1,2,0:T(8,128)(2,1)S(1)}, u32[]{:S(2)}, u32[]{:S(2)}) async-start(bf16[16,128,64]{1,2,0:T(8,128)(2,1)} %bitcast.108), calls=%async_computation | async-start | bytes 524288 | tf_op jit(solution)/shard_map/all_to_all | solution.py:158
  130.5 12.3 %copy-start.11 = (pred[384]{0:T(512)(128)(4,1)S(1)}, pred[384]{0:T(512)(128)(4,1)}, u32[]{:S(2)}) copy-start(pred[384]{0:T(512)(128)(4,1)} %constant.113) | copy-start | bytes 1156
  145.0 2.4 copy-start.9
  148.3 13.3 %all-to-all-start.1 = ((bf16[1,128,16,64]{1,3,0,2:T(8,128)(2,1)}), bf16[1,128,16,64]{1,3,0,2:T(8,128)(2,1)S(1)}, u32[]{:S(2)}, u32[]{:S(2)}) async-start(bf16[1,128,16,64]{1,3,0,2:T(8,128)(2,1)} %bitcast.120), calls=%async_computation.1 | async-start | bytes 524288 | tf_op jit(solution)/shard_map/all_to_all | solution.py:193
  164.6 4.0 %copy-start.2 = (f32[16,32768]{1,0:T(8,128)S(1)}, f32[16,32768]{1,0:T(8,128)}, u32[]{:S(2)}) copy-start(f32[16,32768]{1,0:T(8,128)} %reshape.176) | copy-start | bytes 6291460
  166.1 2.6 %collective-permute-start.12 = (bf16[8,32768]{1,0:T(8,128)(2,1)S(1)}, bf16[8,32768]{1,0:T(8,128)(2,1)S(1)}, u32[]{:S(2)}, u32[]{:S(2)}) collective-permute-start(bf16[8,32768]{1,0:T(8,128)(2,1)S(1)} %dynamic-slice_convert_fusion), channel_id=1, source_target_pairs={{0,1},{1,0},{2,3},{3,2},{4,5},{5,4},{6,7},{7,6},{8,9},{9,8},{10,11... | collective-permute-start | bytes 1572872 | tf_op jit(solution)/shard_map/ppermute | solution.py:25
  167.3 2.7 %copy-start.3 = (f32[768,1024]{1,0:T(8,128)S(1)}, f32[768,1024]{1,0:T(8,128)}, u32[]{:S(2)}) copy-start(f32[768,1024]{1,0:T(8,128)} %get-tuple-element.15) | copy-start | bytes 9437188
  168.9 7.4 %collective-permute-start.13 = (bf16[4,32768]{1,0:T(4,128)(2,1)S(1)}, bf16[4,32768]{1,0:T(4,128)(2,1)S(1)}, u32[]{:S(2)}, u32[]{:S(2)}) collective-permute-start(bf16[4,32768]{1,0:T(4,128)(2,1)S(1)} %dynamic-slice_convert_fusion.1), channel_id=1, source_target_pairs={{0,2},{2,0},{4,6},{6,4},{8,10},{10,8},{12,14},{14,12},{1,3},{3,1},... | collective-permute-start | bytes 786440 | tf_op jit(solution)/shard_map/ppermute | solution.py:28
  176.6 5.0 %collective-permute-start.14 = (bf16[2,32768]{1,0:T(2,128)(2,1)S(1)}, bf16[2,32768]{1,0:T(2,128)(2,1)S(1)}, u32[]{:S(2)}, u32[]{:S(2)}) collective-permute-start(bf16[2,32768]{1,0:T(2,128)(2,1)S(1)} %dynamic-slice_convert_fusion.2), channel_id=1, source_target_pairs={{0,4},{2,6},{4,0},{6,2},{8,12},{10,14},{12,8},{14,10},{1,5},{3,7},... | collective-permute-start | bytes 393224 | tf_op jit(solution)/shard_map/ppermute | solution.py:28
  179.9 7.5 %copy-start.1 = (f32[1,384,1024]{2,1,0:T(8,128)}, f32[1,384,1024]{2,1,0:T(8,128)S(1)}, u32[]{:S(2)}) copy-start(f32[1,384,1024]{2,1,0:T(8,128)S(1)} %bitcast_dynamic-update-slice_fusion.1) | copy-start | bytes 4718596
  181.9 4.9 %collective-permute-start.15 = (bf16[1,32768]{1,0:T(2,128)(2,1)S(1)}, bf16[1,32768]{1,0:T(2,128)(2,1)S(1)}, u32[]{:S(2)}, u32[]{:S(2)}) collective-permute-start(bf16[1,32768]{1,0:T(2,128)(2,1)S(1)} %dynamic-slice_convert_fusion.3), channel_id=1, source_target_pairs={{0,8},{2,10},{4,12},{6,14},{8,0},{10,2},{12,4},{14,6},{1,9},{3,11}... | collective-permute-start | bytes 196616 | tf_op jit(solution)/shard_map/ppermute | solution.py:28
  182.3 5.1 %copy-start = (f32[1,384,1024]{2,1,0:T(8,128)}, f32[1,384,1024]{2,1,0:T(8,128)S(1)}, u32[]{:S(2)}) copy-start(f32[1,384,1024]{2,1,0:T(8,128)S(1)} %bitcast_dynamic-update-slice_fusion) | copy-start | bytes 4718596
  187.0 4.9 %collective-permute-start.16 = (bf16[1,32768]{1,0:T(2,128)(2,1)S(1)}, bf16[1,32768]{1,0:T(2,128)(2,1)S(1)}, u32[]{:S(2)}, u32[]{:S(2)}) collective-permute-start(bf16[1,32768]{1,0:T(2,128)(2,1)S(1)} %add_convert_fusion), channel_id=1, source_target_pairs={{0,8},{2,10},{4,12},{6,14},{8,0},{10,2},{12,4},{14,6},{1,9},{3,11}... | collective-permute-start | bytes 196616 | tf_op jit(solution)/shard_map/ppermute | solution.py:28
  187.4 19.6 %copy-start.10 = (bf16[128,1024]{1,0:T(8,128)(2,1)S(1)}, bf16[128,1024]{1,0:T(8,128)(2,1)}, u32[]{:S(2)}) copy-start(bf16[128,1024]{1,0:T(8,128)(2,1)} %get-tuple-element.12) | copy-start | bytes 786436
  192.4 12.7 %collective-permute-start.17 = (bf16[2,32768]{1,0:T(2,128)(2,1)S(1)}, bf16[2,32768]{1,0:T(2,128)(2,1)S(1)}, u32[]{:S(2)}, u32[]{:S(2)}) collective-permute-start(bf16[2,32768]{1,0:T(2,128)(2,1)S(1)} %broadcast_select_fusion.2), channel_id=1, source_target_pairs={{0,4},{2,6},{4,0},{6,2},{8,12},{10,14},{12,8},{14,10},{1,5},{3,7},... | collective-permute-start | bytes 393224 | tf_op jit(solution)/shard_map/ppermute | solution.py:28
  198.6 43.5 %collective-permute-start.10 = (bf16[2,256,1024]{2,1,0:T(8,128)(2,1)S(1)}, bf16[2,256,1024]{2,1,0:T(8,128)(2,1)}, u32[]{:S(2)}, u32[]{:S(2)}) collective-permute-start(bf16[2,256,1024]{2,1,0:T(8,128)(2,1)S(1)} %pad_maximum_fusion.3), channel_id=1, source_target_pairs={{0,1},{1,2},{2,3},{3,4},{4,5},{5,6},{6,7},{7,8},{8,9},{9,10},{10,1... | collective-permute-start | bytes 3145736 | tf_op jit(solution)/shard_map/ppermute | solution.py:61
  202.7 39.4 %collective-permute-start.11 = (bf16[2,256,1024]{2,1,0:T(8,128)(2,1)S(1)}, bf16[2,256,1024]{2,1,0:T(8,128)(2,1)}, u32[]{:S(2)}, u32[]{:S(2)}) collective-permute-start(bf16[2,256,1024]{2,1,0:T(8,128)(2,1)S(1)} %pad_maximum_fusion.3), channel_id=1, source_target_pairs={{1,0},{2,1},{3,2},{4,3},{5,4},{6,5},{7,6},{8,7},{9,8},{10,9},{11,1... | collective-permute-start | bytes 3145736 | tf_op jit(solution)/shard_map/ppermute | solution.py:62
  205.6 25.7 %collective-permute-start.18 = (bf16[4,32768]{1,0:T(4,128)(2,1)S(1)}, bf16[4,32768]{1,0:T(4,128)(2,1)S(1)}, u32[]{:S(2)}, u32[]{:S(2)}) collective-permute-start(bf16[4,32768]{1,0:T(4,128)(2,1)S(1)} %maximum_select_fusion.5), channel_id=1, source_target_pairs={{0,2},{2,0},{4,6},{6,4},{8,10},{10,8},{12,14},{14,12},{1,3},{3,1},... | collective-permute-start | bytes 786440 | tf_op jit(solution)/shard_map/ppermute | solution.py:28
  231.8 9.7 %collective-permute-start.19 = (bf16[8,32768]{1,0:T(8,128)(2,1)S(1)}, bf16[8,32768]{1,0:T(8,128)(2,1)S(1)}, u32[]{:S(2)}, u32[]{:S(2)}) collective-permute-start(bf16[8,32768]{1,0:T(8,128)(2,1)S(1)} %maximum_select_fusion.3), channel_id=1, source_target_pairs={{0,1},{1,0},{2,3},{3,2},{4,5},{5,4},{6,7},{7,6},{8,9},{9,8},{10,11... | collective-permute-start | bytes 1572872 | tf_op jit(solution)/shard_map/ppermute | solution.py:25
Sparse Core Ops, SparseCore 0:
  10.2 86.0 all-gather.2
  98.4 60.0 all-gather.4

commit v19 on v14

--- a/solution.py
+++ b/solution.py
@@ -64,11 +64,18 @@
 
 
 def _attn_kernel(live_ref, q_ref, k_ref, v_ref, up_ref, attn_ref, dq_ref, dk_ref, dv_ref, dg_ref):
-    scale = 1.0 / math.sqrt(q_ref.shape[-1])
-    q = q_ref[...]
-    k = k_ref[...]
-    v = v_ref[...]
-    up = up_ref[...]
+    width = q_ref.shape[-1] // 2
+    for i in range(2):
+        cols = slice(i * width, (i + 1) * width)
+        _one_head(live_ref, q_ref, k_ref, v_ref, up_ref, attn_ref, dq_ref, dk_ref, dv_ref, dg_ref, cols)
+
+
+def _one_head(live_ref, q_ref, k_ref, v_ref, up_ref, attn_ref, dq_ref, dk_ref, dv_ref, dg_ref, cols):
+    q = q_ref[:, cols]
+    k = k_ref[:, cols]
+    v = v_ref[:, cols]
+    up = up_ref[:, cols]
+    scale = 1.0 / math.sqrt(q.shape[-1])
     nt = (((1,), (1,)), ((), ()))
     tn = (((0,), (0,)), ((), ()))
     scores = lax.dot_general(q, k, nt, preferred_element_type=jnp.float32) * scale
@@ -77,30 +84,30 @@
     raised = jnp.exp(scores - top)
     probs = raised / jnp.sum(raised, axis=-1, keepdims=True)
     probs_b = probs.astype(jnp.bfloat16)
-    attn_ref[...] = jnp.dot(probs_b, v, preferred_element_type=jnp.float32).astype(attn_ref.dtype)
+    attn_ref[:, cols] = jnp.dot(probs_b, v, preferred_element_type=jnp.float32).astype(attn_ref.dtype)
     n_local = dk_ref.shape[0]
     dv = lax.dot_general(probs_b, up, tn, preferred_element_type=jnp.float32)
-    dv_ref[...] = dv[:n_local]
-    dg_ref[1] = dv[n_local:]
+    dv_ref[:, cols] = dv[:n_local]
+    dg_ref[1, :, cols] = dv[n_local:]
     dprobs = lax.dot_general(up, v, nt, preferred_element_type=jnp.float32)
     rowdot = jnp.sum(probs * dprobs, axis=-1, keepdims=True)
     dscores = (scale * probs * (dprobs - rowdot)).astype(jnp.bfloat16)
-    dq_ref[...] = jnp.dot(dscores, k, preferred_element_type=jnp.float32).astype(dq_ref.dtype)
+    dq_ref[:, cols] = jnp.dot(dscores, k, preferred_element_type=jnp.float32).astype(dq_ref.dtype)
     dk = lax.dot_general(dscores, q, tn, preferred_element_type=jnp.float32)
-    dk_ref[...] = dk[:n_local]
-    dg_ref[0] = dk[n_local:]
+    dk_ref[:, cols] = dk[:n_local]
+    dg_ref[0, :, cols] = dk[n_local:]
 
 def attention(live, q, k, v, up, heads, local_n):
     rows, features = q.shape
     keys_n = k.shape[0]
-    hd = features // heads
+    hd = 2 * features // heads
     qspec = pl.BlockSpec((rows, hd), lambda h: (0, h))
     kspec = pl.BlockSpec((keys_n, hd), lambda h: (0, h))
     lspec = pl.BlockSpec((local_n, hd), lambda h: (0, h))
     gspec = pl.BlockSpec((2, keys_n - local_n, hd), lambda h: (0, 0, h))
     return pl.pallas_call(
         _attn_kernel,
-        grid=(heads,),
+        grid=(heads // 2,),
         in_specs=[pl.BlockSpec((1, keys_n), lambda h: (0, 0)), qspec, kspec, kspec, qspec],
         out_specs=[qspec, qspec, lspec, lspec, gspec],
         out_shape=[

time: 239 us -> 238 us (level)
  starting transfers between devices: 76.6 us -> 72.6 us
  waiting for transfers between devices: 81 us -> 85 us
    ppermute x12, starting transfers between devices: 43.2 us -> 38.5 us  [xor_swap(): return lax.ppermute(x, 'chip', [(i, i ^ m) for i in range(n)])]
    ppermute x12, waiting for transfers between devices: 42.2 us -> 46.1 us  [xor_swap(): return lax.ppermute(x, 'chip', [(i, i ^ m) for i in range(n)])]
  transfers between devices with their start and end apart: 24 -> 24, of which waited for: 14 -> 13; matrix products, arithmetic and copies ran while one was open for 19% -> 19% of each run, Pallas kernels for 5% -> 5%
where the time goes in v19:
time: 238 us; the launch traced here: 237 us
  waiting for transfers between devices  85 us (36%)
  starting transfers between devices  72.6 us (31%)
  between operations  17.9 us (8%)
  other arithmetic  17.7 us (7%)
  local copies, waits for them, and re-layouts  17 us (7%)
  matrix products  15.5 us (7%)
  Pallas kernels  11.4 us (5%)
    ppermute x12, waiting for transfers between devices, xor_swap(): return lax.ppermute(x, 'chip', [(i, i ^ m) for i in range(n)])  46.1 us
    ppermute x12, starting transfers between devices, xor_swap(): return lax.ppermute(x, 'chip', [(i, i ^ m) for i in range(n)])  38.5 us
    all_to_all x1, waiting for transfers between devices, local(): lax.all_to_all(attn_out.reshape(tok_rows, count, w_rows), SEQ, 1, 0, tile...  17.2 us
    pallas_call x1, Pallas kernels, attention(): pl.pallas_call(_attn_kernel, grid=(heads // 2,), in_specs=[pl.BlockSpec((...  11.4 us
    all_to_all x1, waiting for transfers between devices, local(): lax.all_to_all(upstream_cols.reshape(count, tok_rows, w_rows), SEQ, 0, 0,...  10.7 us
    ppermute x2, waiting for transfers between devices, halo(): after = lax.ppermute(shard, SEQ, down)  10.1 us
    all_to_all x1, starting transfers between devices, local(): lax.all_to_all(upstream_cols.reshape(count, tok_rows, w_rows), SEQ, 0, 0,...  8.7 us
    ppermute x4, starting transfers between devices, xor_swap(): return lax.ppermute(x, 'core', [(i, i ^ 1) for i in range(n)])  8.38 us
  transfers between devices with their start and end apart: 24, of which 13 were waited for; matrix products, arithmetic and copies ran while one was open for 19% of the time, Pallas kernels for 5%

profile of v19, /device:TPU:11, one launch (start us, length us, event | category | flops | bytes accessed | tf_op | source)
XLA Modules:
  0.0 237.1 jit_solution(6742453488689236073)
XLA Ops:
  7.9 1.9 pad_maximum_fusion.4
  9.8 3.7 %collective-permute-start = (bf16[2,128,1024]{2,1,0:T(8,128)(2,1)}, bf16[2,128,1024]{2,1,0:T(8,128)(2,1)S(1)}, u32[]{:S(2)}, u32[]{:S(2)}) collective-permute-start(bf16[2,128,1024]{2,1,0:T(8,128)(2,1)} %pad_maximum_fusion.4), channel_id=1, source_target_pairs={{0,1},{1,2},{2,3},{3,4},{4,5},{5,6},{6,7},{7,8},{8,9},{9,10},{10,1... | collective-permute-start | bytes 1572872 | tf_op jit(solution)/shard_map/ppermute | solution.py:61
  13.5 1.9 collective-permute-start.1
  15.5 1.3 fusion.30
  18.1 1.1 broadcast_select_fusion.1
  20.8 1.5 collective-permute-start.2
  25.7 10.1 %collective-permute-done.1 = bf16[2,128,1024]{2,1,0:T(8,128)(2,1)S(1)} collective-permute-done((bf16[2,128,1024]{2,1,0:T(8,128)(2,1)}, bf16[2,128,1024]{2,1,0:T(8,128)(2,1)S(1)}, u32[]{:S(2)}, u32[]{:S(2)}) %collective-permute-start.1) | collective-permute-done | bytes 524320 | tf_op jit(solution)/shard_map/ppermute | solution.py:62
  37.3 5.6 %collective-permute-done.4 = bf16[2,32768]{1,0:T(2,128)(2,1)S(1)} collective-permute-done((bf16[2,32768]{1,0:T(2,128)(2,1)S(1)}, bf16[2,32768]{1,0:T(2,128)(2,1)S(1)}, u32[]{:S(2)}, u32[]{:S(2)}) %collective-permute-start.4) | collective-permute-done | bytes 131104 | tf_op jit(solution)/shard_map/ppermute | solution.py:28
  43.2 1.8 collective-permute-start.5
  45.1 2.9 %collective-permute-done.5 = bf16[1,32768]{1,0:T(2,128)(2,1)S(1)} collective-permute-done((bf16[1,32768]{1,0:T(2,128)(2,1)S(1)}, bf16[1,32768]{1,0:T(2,128)(2,1)S(1)}, u32[]{:S(2)}, u32[]{:S(2)}) %collective-permute-start.5) | collective-permute-done | bytes 65568 | tf_op jit(solution)/shard_map/ppermute | solution.py:28
  48.2 1.8 collective-permute-start.6
  50.0 3.1 %collective-permute-done.6 = bf16[1,32768]{1,0:T(2,128)(2,1)S(1)} collective-permute-done((bf16[1,32768]{1,0:T(2,128)(2,1)S(1)}, bf16[1,32768]{1,0:T(2,128)(2,1)S(1)}, u32[]{:S(2)}, u32[]{:S(2)}) %collective-permute-start.6) | collective-permute-done | bytes 65568 | tf_op jit(solution)/shard_map/ppermute | solution.py:28
  53.7 15.8 %collective-permute-start.7 = (bf16[2,32768]{1,0:T(2,128)(2,1)S(1)}, bf16[2,32768]{1,0:T(2,128)(2,1)S(1)}, u32[]{:S(2)}, u32[]{:S(2)}) collective-permute-start(bf16[2,32768]{1,0:T(2,128)(2,1)S(1)} %broadcast_select_fusion.3), channel_id=1, source_target_pairs={{0,4},{2,6},{4,0},{6,2},{8,12},{10,14},{12,8},{14,10},{1,5},{3,7},... | collective-permute-start | bytes 393224 | tf_op jit(solution)/shard_map/ppermute | solution.py:28
  69.6 13.0 %collective-permute-done.7 = bf16[2,32768]{1,0:T(2,128)(2,1)S(1)} collective-permute-done((bf16[2,32768]{1,0:T(2,128)(2,1)S(1)}, bf16[2,32768]{1,0:T(2,128)(2,1)S(1)}, u32[]{:S(2)}, u32[]{:S(2)}) %collective-permute-start.7) | collective-permute-done | bytes 131104 | tf_op jit(solution)/shard_map/ppermute | solution.py:28
  83.1 9.5 %collective-permute-start.8 = (bf16[4,32768]{1,0:T(4,128)(2,1)S(1)}, bf16[4,32768]{1,0:T(4,128)(2,1)S(1)}, u32[]{:S(2)}, u32[]{:S(2)}) collective-permute-start(bf16[4,32768]{1,0:T(4,128)(2,1)S(1)} %maximum_select_fusion.4), channel_id=1, source_target_pairs={{0,2},{2,0},{4,6},{6,4},{8,10},{10,8},{12,14},{14,12},{1,3},{3,1},... | collective-permute-start | bytes 786440 | tf_op jit(solution)/shard_map/ppermute | solution.py:28
  92.7 1.4 copy-done.7
  94.1 2.8 %collective-permute-done.8 = bf16[4,32768]{1,0:T(4,128)(2,1)S(1)} collective-permute-done((bf16[4,32768]{1,0:T(4,128)(2,1)S(1)}, bf16[4,32768]{1,0:T(4,128)(2,1)S(1)}, u32[]{:S(2)}, u32[]{:S(2)}) %collective-permute-start.8) | collective-permute-done | bytes 262176 | tf_op jit(solution)/shard_map/ppermute | solution.py:28
  97.3 3.1 %collective-permute-start.9 = (bf16[8,32768]{1,0:T(8,128)(2,1)S(1)}, bf16[8,32768]{1,0:T(8,128)(2,1)S(1)}, u32[]{:S(2)}, u32[]{:S(2)}) collective-permute-start(bf16[8,32768]{1,0:T(8,128)(2,1)S(1)} %maximum_select_fusion.2), channel_id=1, source_target_pairs={{0,1},{1,0},{2,3},{3,2},{4,5},{5,4},{6,7},{7,6},{8,9},{9,8},{10,11... | collective-permute-start | bytes 1572872 | tf_op jit(solution)/shard_map/ppermute | solution.py:25
  100.3 6.0 %fusion = bf16[8,16,8,128]{3,2,1,0:T(8,128)(2,1)S(1)} fusion(bf16[2048,2048]{1,0:T(8,128)(2,1)} %all-gather.3.cloned.1.call-done, bf16[64,2048]{1,0:T(8,128)(2,1)S(1)} %copy-done.9), kind=kOutput, calls=%fused_computation.5 | convolution fusion | flops 537001984 | bytes 8912896 | tf_op jit(solution)/shard_map/dot_general | solution.py:162
  107.2 8.7 %all-to-all-start = ((bf16[16,128,64]{1,2,0:T(8,128)(2,1)}), bf16[16,128,64]{1,2,0:T(8,128)(2,1)S(1)}, u32[]{:S(2)}, u32[]{:S(2)}) async-start(bf16[16,128,64]{1,2,0:T(8,128)(2,1)} %bitcast.107), calls=%async_computation | async-start | bytes 524288 | tf_op jit(solution)/shard_map/all_to_all | solution.py:165
  116.6 0.9 fusion.20
  117.4 0.8 fusion.19
  118.3 10.7 %all-to-all-done = bf16[16,128,64]{1,2,0:T(8,128)(2,1)S(1)} async-done(((bf16[16,128,64]{1,2,0:T(8,128)(2,1)}), bf16[16,128,64]{1,2,0:T(8,128)(2,1)S(1)}, u32[]{:S(2)}, u32[]{:S(2)}) %all-to-all-start) | async-done | bytes 262176 | tf_op jit(solution)/shard_map/all_to_all | solution.py:165
  129.0 0.8 copy.19.up_ref
  130.5 11.4 %shard_map.119 = (bf16[128,1024]{1,0:T(8,128)(2,1)}, bf16[128,1024]{1,0:T(8,128)(2,1)}, f32[768,1024]{1,0:T(8,128)}, f32[768,1024]{1,0:T(8,128)}, f32[2,256,1024]{2,1,0:T(8,128)}) custom-call(f32[1,1024]{1,0:T(1,128)} %bitcast.119, bf16[128,1024]{1,0:T(8,128)(2,1)} %q_ref.1, bf16[1024,1024]{1,0:T(8,128)(2,1)} %get-tuple-element.22.k_ref, ...), custom_call_target="tpu_custom_call" | custom-call | tf_op jit(solution)/shard_map/pallas_call | solution.py:108
  141.9 2.3 slice_select_fusion
  145.3 2.8 %reshape.176 = f32[16,32768]{1,0:T(8,128)} reshape(f32[2,256,1024]{2,1,0:T(8,128)} %get-tuple-element.14) | data formatting | bytes 4194304 | tf_op jit(solution)/shard_map/reshape | solution.py:35
  148.1 1.4 dynamic-slice_convert_fusion
  150.1 1.2 fusion.7
  151.3 1.3 fusion.6
  152.8 1.1 collective-permute-start.13
  154.5 6.4 %collective-permute-done.13 = bf16[4,32768]{1,0:T(4,128)(2,1)S(1)} collective-permute-done((bf16[4,32768]{1,0:T(4,128)(2,1)S(1)}, bf16[4,32768]{1,0:T(4,128)(2,1)S(1)}, u32[]{:S(2)}, u32[]{:S(2)}) %collective-permute-start.13) | collective-permute-done | bytes 262176 | tf_op jit(solution)/shard_map/ppermute | solution.py:28
  161.5 1.1 bitcast_dynamic-update-slice_fusion.1
  162.6 2.8 %collective-permute-done.14 = bf16[2,32768]{1,0:T(2,128)(2,1)S(1)} collective-permute-done((bf16[2,32768]{1,0:T(2,128)(2,1)S(1)}, bf16[2,32768]{1,0:T(2,128)(2,1)S(1)}, u32[]{:S(2)}, u32[]{:S(2)}) %collective-permute-start.14) | collective-permute-done | bytes 131104 | tf_op jit(solution)/shard_map/ppermute | solution.py:28
  166.4 4.2 %collective-permute-done.15 = bf16[1,32768]{1,0:T(2,128)(2,1)S(1)} collective-permute-done((bf16[1,32768]{1,0:T(2,128)(2,1)S(1)}, bf16[1,32768]{1,0:T(2,128)(2,1)S(1)}, u32[]{:S(2)}, u32[]{:S(2)}) %collective-permute-start.15) | collective-permute-done | bytes 65568 | tf_op jit(solution)/shard_map/ppermute | solution.py:28
  170.8 2.7 %collective-permute-start.16 = (bf16[1,32768]{1,0:T(2,128)(2,1)S(1)}, bf16[1,32768]{1,0:T(2,128)(2,1)S(1)}, u32[]{:S(2)}, u32[]{:S(2)}) collective-permute-start(bf16[1,32768]{1,0:T(2,128)(2,1)S(1)} %add_convert_fusion), channel_id=1, source_target_pairs={{0,8},{2,10},{4,12},{6,14},{8,0},{10,2},{12,4},{14,6},{1,9},{3,11}... | collective-permute-start | bytes 196616 | tf_op jit(solution)/shard_map/ppermute | solution.py:28
  173.7 4.9 %collective-permute-done.16 = bf16[1,32768]{1,0:T(2,128)(2,1)S(1)} collective-permute-done((bf16[1,32768]{1,0:T(2,128)(2,1)S(1)}, bf16[1,32768]{1,0:T(2,128)(2,1)S(1)}, u32[]{:S(2)}, u32[]{:S(2)}) %collective-permute-start.16) | collective-permute-done | bytes 65568 | tf_op jit(solution)/shard_map/ppermute | solution.py:28
  179.2 2.9 %collective-permute-start.17 = (bf16[2,32768]{1,0:T(2,128)(2,1)S(1)}, bf16[2,32768]{1,0:T(2,128)(2,1)S(1)}, u32[]{:S(2)}, u32[]{:S(2)}) collective-permute-start(bf16[2,32768]{1,0:T(2,128)(2,1)S(1)} %broadcast_select_fusion.2), channel_id=1, source_target_pairs={{0,4},{2,6},{4,0},{6,2},{8,12},{10,14},{12,8},{14,10},{1,5},{3,7},... | collective-permute-start | bytes 393224 | tf_op jit(solution)/shard_map/ppermute | solution.py:28
  182.2 3.7 %collective-permute-start.10 = (bf16[2,256,1024]{2,1,0:T(8,128)(2,1)S(1)}, bf16[2,256,1024]{2,1,0:T(8,128)(2,1)}, u32[]{:S(2)}, u32[]{:S(2)}) collective-permute-start(bf16[2,256,1024]{2,1,0:T(8,128)(2,1)S(1)} %pad_maximum_fusion.3), channel_id=1, source_target_pairs={{0,1},{1,2},{2,3},{3,4},{4,5},{5,6},{6,7},{7,8},{8,9},{9,10},{10,1... | collective-permute-start | bytes 3145736 | tf_op jit(solution)/shard_map/ppermute | solution.py:61
  185.9 1.9 collective-permute-start.11
  187.8 0.8 copy.20
  188.7 5.7 %all-to-all-start.1 = ((bf16[1,128,16,64]{1,3,0,2:T(8,128)(2,1)}), bf16[1,128,16,64]{1,3,0,2:T(8,128)(2,1)S(1)}, u32[]{:S(2)}, u32[]{:S(2)}) async-start(bf16[1,128,16,64]{1,3,0,2:T(8,128)(2,1)} %bitcast.35), calls=%async_computation.1 | async-start | bytes 524288 | tf_op jit(solution)/shard_map/all_to_all | solution.py:205
  194.9 1.2 collective-permute-start.18
  196.2 3.7 %convolution_convert_fusion = bf16[128,2048]{1,0:T(8,128)(2,1)} fusion(bf16[128,1024]{1,0:T(8,128)(2,1)S(1)} %copy-done.10, bf16[1024,2048]{1,0:T(8,128)(2,1)} %all-gather.5.cloned.1.call-done), kind=kOutput, calls=%fused_computation | convolution fusion | flops 537133056 | bytes 4980736 | tf_op jit(solution)/shard_map/dot_general | solution.py:202
  199.9 17.2 %all-to-all-done.1 = bf16[1,128,16,64]{1,3,0,2:T(8,128)(2,1)S(1)} async-done(((bf16[1,128,16,64]{1,3,0,2:T(8,128)(2,1)}), bf16[1,128,16,64]{1,3,0,2:T(8,128)(2,1)S(1)}, u32[]{:S(2)}, u32[]{:S(2)}) %all-to-all-start.1) | async-done | bytes 262176 | tf_op jit(solution)/shard_map/all_to_all | solution.py:205
  217.8 3.2 %collective-permute-start.19 = (bf16[8,32768]{1,0:T(8,128)(2,1)S(1)}, bf16[8,32768]{1,0:T(8,128)(2,1)S(1)}, u32[]{:S(2)}, u32[]{:S(2)}) collective-permute-start(bf16[8,32768]{1,0:T(8,128)(2,1)S(1)} %maximum_select_fusion.3), channel_id=1, source_target_pairs={{0,1},{1,0},{2,3},{3,2},{4,5},{5,4},{6,7},{7,6},{8,9},{9,8},{10,11... | collective-permute-start | bytes 1572872 | tf_op jit(solution)/shard_map/ppermute | solution.py:25
  221.0 5.7 %fusion.16 = f32[64,2048]{1,0:T(8,128)} fusion(bf16[2048,2048]{1,0:T(8,128)(2,1)} %all-gather.3.cloned.1.call-done, bf16[8,8,16,128]{3,2,1,0:T(8,128)(2,1)S(1)} %bitcast.116), kind=kOutput, calls=%fused_computation.50 | convolution fusion | flops 536870912 | bytes 9175040 | tf_op jit(solution)/shard_map/dot_general | solution.py:208
  227.5 2.8 %fusion.15 = (bf16[128,1024]{1,0:T(8,128)(2,1)}, bf16[128,1024]{1,0:T(8,128)(2,1)}) fusion(f32[1,384,1024]{2,1,0:T(8,128)} %copy-done, bf16[2,256,1024]{2,1,0:T(8,128)(2,1)S(1)} %select_n.248, bf16[2,256,1024]{2,1,0:T(8,128)(2,1)} %collective-permute-done.11, bf16[2,256,1024]{2,1,0:T(8,128)(2,1)} %collective-permute-done.10, pred[]{:T(512)S(6)} %eq.38, ...), kind=kLoop, calls=%fused_computation.49 | loop fusion | flops 2883584 | bytes 3670018 | tf_op jit(solution)/shard_map/convert_element_type | solution.py:227
  (106 shorter events, 16.1 us)
Async XLA Ops:
  7.2 93.2 %all-gather.3.cloned.1.call-start = ((), (), s32[]{:S(2)}) async-start(), calls=%async_computation.2 | async-start | bytes 8912896 | tf_op jit(solution)/shard_map/all_gather | solution.py:131
  7.9 188.3 %all-gather.5.cloned.1.call-start = ((), (), s32[]{:S(2)}) async-start(), calls=%async_computation.3 | async-start | bytes 4456448 | tf_op jit(solution)/shard_map/all_gather | solution.py:132
  9.8 15.9 %collective-permute-start = (bf16[2,128,1024]{2,1,0:T(8,128)(2,1)}, bf16[2,128,1024]{2,1,0:T(8,128)(2,1)S(1)}, u32[]{:S(2)}, u32[]{:S(2)}) collective-permute-start(bf16[2,128,1024]{2,1,0:T(8,128)(2,1)} %pad_maximum_fusion.4), channel_id=1, source_target_pairs={{0,1},{1,2},{2,3},{3,4},{4,5},{5,6},{6,7},{7,8},{8,9},{9,10},{10,1... | collective-permute-start | bytes 1572872 | tf_op jit(solution)/shard_map/ppermute | solution.py:61
  13.5 22.3 %collective-permute-start.1 = (bf16[2,128,1024]{2,1,0:T(8,128)(2,1)}, bf16[2,128,1024]{2,1,0:T(8,128)(2,1)S(1)}, u32[]{:S(2)}, u32[]{:S(2)}) collective-permute-start(bf16[2,128,1024]{2,1,0:T(8,128)(2,1)} %pad_maximum_fusion.4), channel_id=1, source_target_pairs={{1,0},{2,1},{3,2},{4,3},{5,4},{6,5},{7,6},{8,7},{9,8},{10,9},{11,1... | collective-permute-start | bytes 1572872 | tf_op jit(solution)/shard_map/ppermute | solution.py:62
  19.3 3.0 %copy-start.12 = (s32[1,3]{1,0:T(1,128)S(1)}, s32[1,3]{1,0:T(1,128)}, u32[]{:S(2)}) copy-start(s32[1,3]{1,0:T(1,128)} %param.14) | copy-start | bytes 40
  19.3 5.6 %copy-start.13 = (s32[3]{0:T(128)S(1)}, s32[3]{0:T(128)}, u32[]{:S(2)}) copy-start(s32[3]{0:T(128)} %constant.91.clone) | copy-start | bytes 40
  19.9 16.0 %copy-start.5 = (bf16[128,1024]{1,0:T(8,128)(2,1)S(1)}, bf16[128,1024]{1,0:T(8,128)(2,1)}, u32[]{:S(2)}) copy-start(bf16[128,1024]{1,0:T(8,128)(2,1)} %param.10) | copy-start | bytes 786436
  19.9 15.9 %copy-start.6 = (bf16[128,1024]{1,0:T(8,128)(2,1)S(1)}, bf16[128,1024]{1,0:T(8,128)(2,1)}, u32[]{:S(2)}) copy-start(bf16[128,1024]{1,0:T(8,128)(2,1)} %param.9) | copy-start | bytes 786436
  20.8 4.3 %collective-permute-start.2 = (bf16[8,32768]{1,0:T(8,128)(2,1)}, bf16[8,32768]{1,0:T(8,128)(2,1)S(1)}, u32[]{:S(2)}, u32[]{:S(2)}) collective-permute-start(bf16[8,32768]{1,0:T(8,128)(2,1)} %constant_dynamic-slice_fusion.3), channel_id=1, source_target_pairs={{0,1},{1,0},{2,3},{3,2},{4,5},{5,4},{6,7},{7,6},{8,9},{9,8},{10,11... | collective-permute-start | bytes 1572872 | tf_op jit(solution)/shard_map/ppermute | solution.py:25
  25.3 11.3 %collective-permute-start.3 = (bf16[4,32768]{1,0:T(4,128)(2,1)S(1)}, bf16[4,32768]{1,0:T(4,128)(2,1)S(1)}, u32[]{:S(2)}, u32[]{:S(2)}) collective-permute-start(bf16[4,32768]{1,0:T(4,128)(2,1)S(1)} %constant_dynamic-slice_fusion.2), channel_id=1, source_target_pairs={{0,2},{2,0},{4,6},{6,4},{8,10},{10,8},{12,14},{14,12},{1,3},{3,1},... | collective-permute-start | bytes 786440 | tf_op jit(solution)/shard_map/ppermute | solution.py:28
  37.0 5.9 %collective-permute-start.4 = (bf16[2,32768]{1,0:T(2,128)(2,1)S(1)}, bf16[2,32768]{1,0:T(2,128)(2,1)S(1)}, u32[]{:S(2)}, u32[]{:S(2)}) collective-permute-start(bf16[2,32768]{1,0:T(2,128)(2,1)S(1)} %constant_dynamic-slice_fusion.1), channel_id=1, source_target_pairs={{0,4},{2,6},{4,0},{6,2},{8,12},{10,14},{12,8},{14,10},{1,5},{3,7},... | collective-permute-start | bytes 393224 | tf_op jit(solution)/shard_map/ppermute | solution.py:28
  43.2 4.8 %collective-permute-start.5 = (bf16[1,32768]{1,0:T(2,128)(2,1)S(1)}, bf16[1,32768]{1,0:T(2,128)(2,1)S(1)}, u32[]{:S(2)}, u32[]{:S(2)}) collective-permute-start(bf16[1,32768]{1,0:T(2,128)(2,1)S(1)} %constant_dynamic-slice_fusion), channel_id=1, source_target_pairs={{0,8},{2,10},{4,12},{6,14},{8,0},{10,2},{12,4},{14,6},{1,9},{3,11}... | collective-permute-start | bytes 196616 | tf_op jit(solution)/shard_map/ppermute | solution.py:28
  48.2 4.9 %collective-permute-start.6 = (bf16[1,32768]{1,0:T(2,128)(2,1)S(1)}, bf16[1,32768]{1,0:T(2,128)(2,1)S(1)}, u32[]{:S(2)}, u32[]{:S(2)}) collective-permute-start(bf16[1,32768]{1,0:T(2,128)(2,1)S(1)} %dynamic-slice_add_fusion.2), channel_id=1, source_target_pairs={{0,8},{2,10},{4,12},{6,14},{8,0},{10,2},{12,4},{14,6},{1,9},{3,11}... | collective-permute-start | bytes 196616 | tf_op jit(solution)/shard_map/ppermute | solution.py:28
  53.7 46.7 %copy-start.9 = (bf16[64,2048]{1,0:T(8,128)(2,1)S(1)}, bf16[64,2048]{1,0:T(8,128)(2,1)}, u32[]{:S(2)}) copy-start(bf16[64,2048]{1,0:T(8,128)(2,1)} %param.11) | copy-start | bytes 786436
  53.7 28.9 %collective-permute-start.7 = (bf16[2,32768]{1,0:T(2,128)(2,1)S(1)}, bf16[2,32768]{1,0:T(2,128)(2,1)S(1)}, u32[]{:S(2)}, u32[]{:S(2)}) collective-permute-start(bf16[2,32768]{1,0:T(2,128)(2,1)S(1)} %broadcast_select_fusion.3), channel_id=1, source_target_pairs={{0,4},{2,6},{4,0},{6,2},{8,12},{10,14},{12,8},{14,10},{1,5},{3,7},... | collective-permute-start | bytes 393224 | tf_op jit(solution)/shard_map/ppermute | solution.py:28
  83.1 13.8 %collective-permute-start.8 = (bf16[4,32768]{1,0:T(4,128)(2,1)S(1)}, bf16[4,32768]{1,0:T(4,128)(2,1)S(1)}, u32[]{:S(2)}, u32[]{:S(2)}) collective-permute-start(bf16[4,32768]{1,0:T(4,128)(2,1)S(1)} %maximum_select_fusion.4), channel_id=1, source_target_pairs={{0,2},{2,0},{4,6},{6,4},{8,10},{10,8},{12,14},{14,12},{1,3},{3,1},... | collective-permute-start | bytes 786440 | tf_op jit(solution)/shard_map/ppermute | solution.py:28
  92.6 4.2 %copy-start.8 = (bf16[1024,1024]{1,0:T(8,128)(2,1)}, bf16[1024,1024]{1,0:T(8,128)(2,1)S(1)}, u32[]{:S(2)}) copy-start(bf16[1024,1024]{1,0:T(8,128)(2,1)S(1)} %bitcast_dynamic-update-slice_fusion.5) | copy-start | bytes 6291460
  92.7 1.4 copy-start.7
  97.3 18.6 %collective-permute-start.9 = (bf16[8,32768]{1,0:T(8,128)(2,1)S(1)}, bf16[8,32768]{1,0:T(8,128)(2,1)S(1)}, u32[]{:S(2)}, u32[]{:S(2)}) collective-permute-start(bf16[8,32768]{1,0:T(8,128)(2,1)S(1)} %maximum_select_fusion.2), channel_id=1, source_target_pairs={{0,1},{1,0},{2,3},{3,2},{4,5},{5,4},{6,7},{7,6},{8,9},{9,8},{10,11... | collective-permute-start | bytes 1572872 | tf_op jit(solution)/shard_map/ppermute | solution.py:25
  107.2 21.9 %all-to-all-start = ((bf16[16,128,64]{1,2,0:T(8,128)(2,1)}), bf16[16,128,64]{1,2,0:T(8,128)(2,1)S(1)}, u32[]{:S(2)}, u32[]{:S(2)}) async-start(bf16[16,128,64]{1,2,0:T(8,128)(2,1)} %bitcast.107), calls=%async_computation | async-start | bytes 524288 | tf_op jit(solution)/shard_map/all_to_all | solution.py:165
  130.5 11.4 %copy-start.11 = (pred[384]{0:T(512)(128)(4,1)S(1)}, pred[384]{0:T(512)(128)(4,1)}, u32[]{:S(2)}) copy-start(pred[384]{0:T(512)(128)(4,1)} %constant.113) | copy-start | bytes 1156
  141.9 2.9 %copy-start.4 = (f32[768,1024]{1,0:T(8,128)S(1)}, f32[768,1024]{1,0:T(8,128)}, u32[]{:S(2)}) copy-start(f32[768,1024]{1,0:T(8,128)} %get-tuple-element.12) | copy-start | bytes 9437188
  148.1 4.5 %copy-start.2 = (f32[16,32768]{1,0:T(8,128)S(1)}, f32[16,32768]{1,0:T(8,128)}, u32[]{:S(2)}) copy-start(f32[16,32768]{1,0:T(8,128)} %reshape.176) | copy-start | bytes 6291460
  149.5 3.1 %collective-permute-start.12 = (bf16[8,32768]{1,0:T(8,128)(2,1)S(1)}, bf16[8,32768]{1,0:T(8,128)(2,1)S(1)}, u32[]{:S(2)}, u32[]{:S(2)}) collective-permute-start(bf16[8,32768]{1,0:T(8,128)(2,1)S(1)} %dynamic-slice_convert_fusion), channel_id=1, source_target_pairs={{0,1},{1,0},{2,3},{3,2},{4,5},{5,4},{6,7},{7,6},{8,9},{9,8},{10,11... | collective-permute-start | bytes 1572872 | tf_op jit(solution)/shard_map/ppermute | solution.py:25
  151.3 2.7 %copy-start.3 = (f32[768,1024]{1,0:T(8,128)S(1)}, f32[768,1024]{1,0:T(8,128)}, u32[]{:S(2)}) copy-start(f32[768,1024]{1,0:T(8,128)} %get-tuple-element.13) | copy-start | bytes 9437188
  152.8 8.0 %collective-permute-start.13 = (bf16[4,32768]{1,0:T(4,128)(2,1)S(1)}, bf16[4,32768]{1,0:T(4,128)(2,1)S(1)}, u32[]{:S(2)}, u32[]{:S(2)}) collective-permute-start(bf16[4,32768]{1,0:T(4,128)(2,1)S(1)} %dynamic-slice_convert_fusion.1), channel_id=1, source_target_pairs={{0,2},{2,0},{4,6},{6,4},{8,10},{10,8},{12,14},{14,12},{1,3},{3,1},... | collective-permute-start | bytes 786440 | tf_op jit(solution)/shard_map/ppermute | solution.py:28
  161.1 4.3 %collective-permute-start.14 = (bf16[2,32768]{1,0:T(2,128)(2,1)S(1)}, bf16[2,32768]{1,0:T(2,128)(2,1)S(1)}, u32[]{:S(2)}, u32[]{:S(2)}) collective-permute-start(bf16[2,32768]{1,0:T(2,128)(2,1)S(1)} %dynamic-slice_convert_fusion.2), channel_id=1, source_target_pairs={{0,4},{2,6},{4,0},{6,2},{8,12},{10,14},{12,8},{14,10},{1,5},{3,7},... | collective-permute-start | bytes 393224 | tf_op jit(solution)/shard_map/ppermute | solution.py:28
  162.6 11.0 %copy-start.1 = (f32[1,384,1024]{2,1,0:T(8,128)}, f32[1,384,1024]{2,1,0:T(8,128)S(1)}, u32[]{:S(2)}) copy-start(f32[1,384,1024]{2,1,0:T(8,128)S(1)} %bitcast_dynamic-update-slice_fusion.1) | copy-start | bytes 4718596
  165.7 4.9 %collective-permute-start.15 = (bf16[1,32768]{1,0:T(2,128)(2,1)S(1)}, bf16[1,32768]{1,0:T(2,128)(2,1)S(1)}, u32[]{:S(2)}, u32[]{:S(2)}) collective-permute-start(bf16[1,32768]{1,0:T(2,128)(2,1)S(1)} %dynamic-slice_convert_fusion.3), channel_id=1, source_target_pairs={{0,8},{2,10},{4,12},{6,14},{8,0},{10,2},{12,4},{14,6},{1,9},{3,11}... | collective-permute-start | bytes 196616 | tf_op jit(solution)/shard_map/ppermute | solution.py:28
  166.4 7.3 %copy-start = (f32[1,384,1024]{2,1,0:T(8,128)}, f32[1,384,1024]{2,1,0:T(8,128)S(1)}, u32[]{:S(2)}) copy-start(f32[1,384,1024]{2,1,0:T(8,128)S(1)} %bitcast_dynamic-update-slice_fusion) | copy-start | bytes 4718596
  170.8 7.8 %collective-permute-start.16 = (bf16[1,32768]{1,0:T(2,128)(2,1)S(1)}, bf16[1,32768]{1,0:T(2,128)(2,1)S(1)}, u32[]{:S(2)}, u32[]{:S(2)}) collective-permute-start(bf16[1,32768]{1,0:T(2,128)(2,1)S(1)} %add_convert_fusion), channel_id=1, source_target_pairs={{0,8},{2,10},{4,12},{6,14},{8,0},{10,2},{12,4},{14,6},{1,9},{3,11}... | collective-permute-start | bytes 196616 | tf_op jit(solution)/shard_map/ppermute | solution.py:28
  173.7 14.2 %copy-start.10 = (bf16[128,1024]{1,0:T(8,128)(2,1)S(1)}, bf16[128,1024]{1,0:T(8,128)(2,1)}, u32[]{:S(2)}) copy-start(bf16[128,1024]{1,0:T(8,128)(2,1)} %get-tuple-element.10) | copy-start | bytes 786436
  179.2 15.2 %collective-permute-start.17 = (bf16[2,32768]{1,0:T(2,128)(2,1)S(1)}, bf16[2,32768]{1,0:T(2,128)(2,1)S(1)}, u32[]{:S(2)}, u32[]{:S(2)}) collective-permute-start(bf16[2,32768]{1,0:T(2,128)(2,1)S(1)} %broadcast_select_fusion.2), channel_id=1, source_target_pairs={{0,4},{2,6},{4,0},{6,2},{8,12},{10,14},{12,8},{14,10},{1,5},{3,7},... | collective-permute-start | bytes 393224 | tf_op jit(solution)/shard_map/ppermute | solution.py:28
  182.2 45.3 %collective-permute-start.10 = (bf16[2,256,1024]{2,1,0:T(8,128)(2,1)S(1)}, bf16[2,256,1024]{2,1,0:T(8,128)(2,1)}, u32[]{:S(2)}, u32[]{:S(2)}) collective-permute-start(bf16[2,256,1024]{2,1,0:T(8,128)(2,1)S(1)} %pad_maximum_fusion.3), channel_id=1, source_target_pairs={{0,1},{1,2},{2,3},{3,4},{4,5},{5,6},{6,7},{7,8},{8,9},{9,10},{10,1... | collective-permute-start | bytes 3145736 | tf_op jit(solution)/shard_map/ppermute | solution.py:61
  185.9 41.6 %collective-permute-start.11 = (bf16[2,256,1024]{2,1,0:T(8,128)(2,1)S(1)}, bf16[2,256,1024]{2,1,0:T(8,128)(2,1)}, u32[]{:S(2)}, u32[]{:S(2)}) collective-permute-start(bf16[2,256,1024]{2,1,0:T(8,128)(2,1)S(1)} %pad_maximum_fusion.3), channel_id=1, source_target_pairs={{1,0},{2,1},{3,2},{4,3},{5,4},{6,5},{7,6},{8,7},{9,8},{10,9},{11,1... | collective-permute-start | bytes 3145736 | tf_op jit(solution)/shard_map/ppermute | solution.py:62
  188.7 28.4 %all-to-all-start.1 = ((bf16[1,128,16,64]{1,3,0,2:T(8,128)(2,1)}), bf16[1,128,16,64]{1,3,0,2:T(8,128)(2,1)S(1)}, u32[]{:S(2)}, u32[]{:S(2)}) async-start(bf16[1,128,16,64]{1,3,0,2:T(8,128)(2,1)} %bitcast.35), calls=%async_computation.1 | async-start | bytes 524288 | tf_op jit(solution)/shard_map/all_to_all | solution.py:205
  194.9 22.4 %collective-permute-start.18 = (bf16[4,32768]{1,0:T(4,128)(2,1)S(1)}, bf16[4,32768]{1,0:T(4,128)(2,1)S(1)}, u32[]{:S(2)}, u32[]{:S(2)}) collective-permute-start(bf16[4,32768]{1,0:T(4,128)(2,1)S(1)} %maximum_select_fusion.5), channel_id=1, source_target_pairs={{0,2},{2,0},{4,6},{6,4},{8,10},{10,8},{12,14},{14,12},{1,3},{3,1},... | collective-permute-start | bytes 786440 | tf_op jit(solution)/shard_map/ppermute | solution.py:28
  217.8 9.0 %collective-permute-start.19 = (bf16[8,32768]{1,0:T(8,128)(2,1)S(1)}, bf16[8,32768]{1,0:T(8,128)(2,1)S(1)}, u32[]{:S(2)}, u32[]{:S(2)}) collective-permute-start(bf16[8,32768]{1,0:T(8,128)(2,1)S(1)} %maximum_select_fusion.3), channel_id=1, source_target_pairs={{0,1},{1,0},{2,3},{3,2},{4,5},{5,4},{6,7},{7,6},{8,9},{9,8},{10,11... | collective-permute-start | bytes 1572872 | tf_op jit(solution)/shard_map/ppermute | solution.py:25
Sparse Core Ops, SparseCore 0:
  10.2 86.0 all-gather.2
  98.4 59.9 all-gather.4

commit v20 on v19

--- a/solution.py
+++ b/solution.py
@@ -64,8 +64,8 @@
 
 
 def _attn_kernel(live_ref, q_ref, k_ref, v_ref, up_ref, attn_ref, dq_ref, dk_ref, dv_ref, dg_ref):
-    width = q_ref.shape[-1] // 2
-    for i in range(2):
+    width = q_ref.shape[-1] // 4
+    for i in range(4):
         cols = slice(i * width, (i + 1) * width)
         _one_head(live_ref, q_ref, k_ref, v_ref, up_ref, attn_ref, dq_ref, dk_ref, dv_ref, dg_ref, cols)
 
@@ -100,14 +100,14 @@
 def attention(live, q, k, v, up, heads, local_n):
     rows, features = q.shape
     keys_n = k.shape[0]
-    hd = 2 * features // heads
+    hd = 4 * features // heads
     qspec = pl.BlockSpec((rows, hd), lambda h: (0, h))
     kspec = pl.BlockSpec((keys_n, hd), lambda h: (0, h))
     lspec = pl.BlockSpec((local_n, hd), lambda h: (0, h))
     gspec = pl.BlockSpec((2, keys_n - local_n, hd), lambda h: (0, 0, h))
     return pl.pallas_call(
         _attn_kernel,
-        grid=(heads // 2,),
+        grid=(heads // 4,),
         in_specs=[pl.BlockSpec((1, keys_n), lambda h: (0, 0)), qspec, kspec, kspec, qspec],
         out_specs=[qspec, qspec, lspec, lspec, gspec],
         out_shape=[

time: 238 us -> 239 us (level)
  no operation moved by 1% of the time
where the time goes in v20:
time: 239 us; the launch traced here: 238 us
  waiting for transfers between devices  84.2 us (35%)
  starting transfers between devices  74.1 us (31%)
  between operations  17.9 us (7%)
  other arithmetic  17.7 us (7%)
  local copies, waits for them, and re-layouts  17.1 us (7%)
  matrix products  15.5 us (6%)
  Pallas kernels  11.7 us (5%)
    ppermute x12, waiting for transfers between devices, xor_swap(): return lax.ppermute(x, 'chip', [(i, i ^ m) for i in range(n)])  45.8 us
    ppermute x12, starting transfers between devices, xor_swap(): return lax.ppermute(x, 'chip', [(i, i ^ m) for i in range(n)])  40.4 us
    all_to_all x1, waiting for transfers between devices, local(): lax.all_to_all(attn_out.reshape(tok_rows, count, w_rows), SEQ, 1, 0, tile...  16.8 us
    pallas_call x1, Pallas kernels, attention(): pl.pallas_call(_attn_kernel, grid=(heads // 4,), in_specs=[pl.BlockSpec((...  11.7 us
    all_to_all x1, waiting for transfers between devices, local(): lax.all_to_all(upstream_cols.reshape(count, tok_rows, w_rows), SEQ, 0, 0,...  10.7 us
    ppermute x2, waiting for transfers between devices, halo(): after = lax.ppermute(shard, SEQ, down)  10.1 us
    all_to_all x1, starting transfers between devices, local(): lax.all_to_all(upstream_cols.reshape(count, tok_rows, w_rows), SEQ, 0, 0,...  8.7 us
    ppermute x4, starting transfers between devices, xor_swap(): return lax.ppermute(x, 'core', [(i, i ^ 1) for i in range(n)])  8.29 us
  transfers between devices with their start and end apart: 24, of which 13 were waited for; matrix products, arithmetic and copies ran while one was open for 19% of the time, Pallas kernels for 5%

profile of v20, /device:TPU:11, one launch (start us, length us, event | category | flops | bytes accessed | tf_op | source)
XLA Modules:
  0.0 238.2 jit_solution(9197355173428980277)
XLA Ops:
  7.9 1.9 pad_maximum_fusion.4
  9.8 3.7 %collective-permute-start = (bf16[2,128,1024]{2,1,0:T(8,128)(2,1)}, bf16[2,128,1024]{2,1,0:T(8,128)(2,1)S(1)}, u32[]{:S(2)}, u32[]{:S(2)}) collective-permute-start(bf16[2,128,1024]{2,1,0:T(8,128)(2,1)} %pad_maximum_fusion.4), channel_id=1, source_target_pairs={{0,1},{1,2},{2,3},{3,4},{4,5},{5,6},{6,7},{7,8},{8,9},{9,10},{10,1... | collective-permute-start | bytes 1572872 | tf_op jit(solution)/shard_map/ppermute | solution.py:61
  13.5 1.9 collective-permute-start.1
  15.5 1.3 fusion.30
  18.1 1.1 broadcast_select_fusion.1
  20.8 1.5 collective-permute-start.2
  25.7 10.1 %collective-permute-done.1 = bf16[2,128,1024]{2,1,0:T(8,128)(2,1)S(1)} collective-permute-done((bf16[2,128,1024]{2,1,0:T(8,128)(2,1)}, bf16[2,128,1024]{2,1,0:T(8,128)(2,1)S(1)}, u32[]{:S(2)}, u32[]{:S(2)}) %collective-permute-start.1) | collective-permute-done | bytes 524320 | tf_op jit(solution)/shard_map/ppermute | solution.py:62
  37.3 5.6 %collective-permute-done.4 = bf16[2,32768]{1,0:T(2,128)(2,1)S(1)} collective-permute-done((bf16[2,32768]{1,0:T(2,128)(2,1)S(1)}, bf16[2,32768]{1,0:T(2,128)(2,1)S(1)}, u32[]{:S(2)}, u32[]{:S(2)}) %collective-permute-start.4) | collective-permute-done | bytes 131104 | tf_op jit(solution)/shard_map/ppermute | solution.py:28
  43.2 1.8 collective-permute-start.5
  45.1 2.9 %collective-permute-done.5 = bf16[1,32768]{1,0:T(2,128)(2,1)S(1)} collective-permute-done((bf16[1,32768]{1,0:T(2,128)(2,1)S(1)}, bf16[1,32768]{1,0:T(2,128)(2,1)S(1)}, u32[]{:S(2)}, u32[]{:S(2)}) %collective-permute-start.5) | collective-permute-done | bytes 65568 | tf_op jit(solution)/shard_map/ppermute | solution.py:28
  48.2 1.8 collective-permute-start.6
  50.0 3.1 %collective-permute-done.6 = bf16[1,32768]{1,0:T(2,128)(2,1)S(1)} collective-permute-done((bf16[1,32768]{1,0:T(2,128)(2,1)S(1)}, bf16[1,32768]{1,0:T(2,128)(2,1)S(1)}, u32[]{:S(2)}, u32[]{:S(2)}) %collective-permute-start.6) | collective-permute-done | bytes 65568 | tf_op jit(solution)/shard_map/ppermute | solution.py:28
  53.7 15.8 %collective-permute-start.7 = (bf16[2,32768]{1,0:T(2,128)(2,1)S(1)}, bf16[2,32768]{1,0:T(2,128)(2,1)S(1)}, u32[]{:S(2)}, u32[]{:S(2)}) collective-permute-start(bf16[2,32768]{1,0:T(2,128)(2,1)S(1)} %broadcast_select_fusion.3), channel_id=1, source_target_pairs={{0,4},{2,6},{4,0},{6,2},{8,12},{10,14},{12,8},{14,10},{1,5},{3,7},... | collective-permute-start | bytes 393224 | tf_op jit(solution)/shard_map/ppermute | solution.py:28
  69.6 13.0 %collective-permute-done.7 = bf16[2,32768]{1,0:T(2,128)(2,1)S(1)} collective-permute-done((bf16[2,32768]{1,0:T(2,128)(2,1)S(1)}, bf16[2,32768]{1,0:T(2,128)(2,1)S(1)}, u32[]{:S(2)}, u32[]{:S(2)}) %collective-permute-start.7) | collective-permute-done | bytes 131104 | tf_op jit(solution)/shard_map/ppermute | solution.py:28
  83.1 9.5 %collective-permute-start.8 = (bf16[4,32768]{1,0:T(4,128)(2,1)S(1)}, bf16[4,32768]{1,0:T(4,128)(2,1)S(1)}, u32[]{:S(2)}, u32[]{:S(2)}) collective-permute-start(bf16[4,32768]{1,0:T(4,128)(2,1)S(1)} %maximum_select_fusion.4), channel_id=1, source_target_pairs={{0,2},{2,0},{4,6},{6,4},{8,10},{10,8},{12,14},{14,12},{1,3},{3,1},... | collective-permute-start | bytes 786440 | tf_op jit(solution)/shard_map/ppermute | solution.py:28
  92.7 1.4 copy-done.7
  94.1 2.8 %collective-permute-done.8 = bf16[4,32768]{1,0:T(4,128)(2,1)S(1)} collective-permute-done((bf16[4,32768]{1,0:T(4,128)(2,1)S(1)}, bf16[4,32768]{1,0:T(4,128)(2,1)S(1)}, u32[]{:S(2)}, u32[]{:S(2)}) %collective-permute-start.8) | collective-permute-done | bytes 262176 | tf_op jit(solution)/shard_map/ppermute | solution.py:28
  97.3 3.1 %collective-permute-start.9 = (bf16[8,32768]{1,0:T(8,128)(2,1)S(1)}, bf16[8,32768]{1,0:T(8,128)(2,1)S(1)}, u32[]{:S(2)}, u32[]{:S(2)}) collective-permute-start(bf16[8,32768]{1,0:T(8,128)(2,1)S(1)} %maximum_select_fusion.2), channel_id=1, source_target_pairs={{0,1},{1,0},{2,3},{3,2},{4,5},{5,4},{6,7},{7,6},{8,9},{9,8},{10,11... | collective-permute-start | bytes 1572872 | tf_op jit(solution)/shard_map/ppermute | solution.py:25
  100.3 6.0 %fusion = bf16[8,16,8,128]{3,2,1,0:T(8,128)(2,1)S(1)} fusion(bf16[2048,2048]{1,0:T(8,128)(2,1)} %all-gather.3.cloned.1.call-done, bf16[64,2048]{1,0:T(8,128)(2,1)S(1)} %copy-done.9), kind=kOutput, calls=%fused_computation.5 | convolution fusion | flops 537001984 | bytes 8912896 | tf_op jit(solution)/shard_map/dot_general | solution.py:162
  107.2 8.7 %all-to-all-start = ((bf16[16,128,64]{1,2,0:T(8,128)(2,1)}), bf16[16,128,64]{1,2,0:T(8,128)(2,1)S(1)}, u32[]{:S(2)}, u32[]{:S(2)}) async-start(bf16[16,128,64]{1,2,0:T(8,128)(2,1)} %bitcast.107), calls=%async_computation | async-start | bytes 524288 | tf_op jit(solution)/shard_map/all_to_all | solution.py:165
  116.6 0.9 fusion.20
  117.4 0.8 fusion.19
  118.3 10.7 %all-to-all-done = bf16[16,128,64]{1,2,0:T(8,128)(2,1)S(1)} async-done(((bf16[16,128,64]{1,2,0:T(8,128)(2,1)}), bf16[16,128,64]{1,2,0:T(8,128)(2,1)S(1)}, u32[]{:S(2)}, u32[]{:S(2)}) %all-to-all-start) | async-done | bytes 262176 | tf_op jit(solution)/shard_map/all_to_all | solution.py:165
  129.0 0.8 copy.19.up_ref
  130.5 11.7 %shard_map.119 = (bf16[128,1024]{1,0:T(8,128)(2,1)}, bf16[128,1024]{1,0:T(8,128)(2,1)}, f32[768,1024]{1,0:T(8,128)}, f32[768,1024]{1,0:T(8,128)}, f32[2,256,1024]{2,1,0:T(8,128)}) custom-call(f32[1,1024]{1,0:T(1,128)} %bitcast.119, bf16[128,1024]{1,0:T(8,128)(2,1)} %q_ref.1, bf16[1024,1024]{1,0:T(8,128)(2,1)} %get-tuple-element.22.k_ref, ...), custom_call_target="tpu_custom_call" | custom-call | tf_op jit(solution)/shard_map/pallas_call | solution.py:108
  142.3 2.3 slice_select_fusion
  145.6 2.8 %reshape.176 = f32[16,32768]{1,0:T(8,128)} reshape(f32[2,256,1024]{2,1,0:T(8,128)} %get-tuple-element.14) | data formatting | bytes 4194304 | tf_op jit(solution)/shard_map/reshape | solution.py:35
  148.4 1.5 dynamic-slice_convert_fusion
  150.3 1.2 fusion.7
  151.5 1.4 fusion.6
  153.1 1.1 collective-permute-start.13
  154.8 6.3 %collective-permute-done.13 = bf16[4,32768]{1,0:T(4,128)(2,1)S(1)} collective-permute-done((bf16[4,32768]{1,0:T(4,128)(2,1)S(1)}, bf16[4,32768]{1,0:T(4,128)(2,1)S(1)}, u32[]{:S(2)}, u32[]{:S(2)}) %collective-permute-start.13) | collective-permute-done | bytes 262176 | tf_op jit(solution)/shard_map/ppermute | solution.py:28
  161.9 1.1 bitcast_dynamic-update-slice_fusion.1
  163.0 2.6 %collective-permute-done.14 = bf16[2,32768]{1,0:T(2,128)(2,1)S(1)} collective-permute-done((bf16[2,32768]{1,0:T(2,128)(2,1)S(1)}, bf16[2,32768]{1,0:T(2,128)(2,1)S(1)}, u32[]{:S(2)}, u32[]{:S(2)}) %collective-permute-start.14) | collective-permute-done | bytes 131104 | tf_op jit(solution)/shard_map/ppermute | solution.py:28
  165.9 1.1 collective-permute-start.15
  167.1 3.7 %collective-permute-done.15 = bf16[1,32768]{1,0:T(2,128)(2,1)S(1)} collective-permute-done((bf16[1,32768]{1,0:T(2,128)(2,1)S(1)}, bf16[1,32768]{1,0:T(2,128)(2,1)S(1)}, u32[]{:S(2)}, u32[]{:S(2)}) %collective-permute-start.15) | collective-permute-done | bytes 65568 | tf_op jit(solution)/shard_map/ppermute | solution.py:28
  171.0 4.5 %collective-permute-start.16 = (bf16[1,32768]{1,0:T(2,128)(2,1)S(1)}, bf16[1,32768]{1,0:T(2,128)(2,1)S(1)}, u32[]{:S(2)}, u32[]{:S(2)}) collective-permute-start(bf16[1,32768]{1,0:T(2,128)(2,1)S(1)} %add_convert_fusion), channel_id=1, source_target_pairs={{0,8},{2,10},{4,12},{6,14},{8,0},{10,2},{12,4},{14,6},{1,9},{3,11}... | collective-permute-start | bytes 196616 | tf_op jit(solution)/shard_map/ppermute | solution.py:28
  175.7 5.4 %collective-permute-done.16 = bf16[1,32768]{1,0:T(2,128)(2,1)S(1)} collective-permute-done((bf16[1,32768]{1,0:T(2,128)(2,1)S(1)}, bf16[1,32768]{1,0:T(2,128)(2,1)S(1)}, u32[]{:S(2)}, u32[]{:S(2)}) %collective-permute-start.16) | collective-permute-done | bytes 65568 | tf_op jit(solution)/shard_map/ppermute | solution.py:28
  181.7 2.3 collective-permute-start.17
  184.0 2.2 collective-permute-start.10
  186.2 2.5 %collective-permute-start.11 = (bf16[2,256,1024]{2,1,0:T(8,128)(2,1)S(1)}, bf16[2,256,1024]{2,1,0:T(8,128)(2,1)}, u32[]{:S(2)}, u32[]{:S(2)}) collective-permute-start(bf16[2,256,1024]{2,1,0:T(8,128)(2,1)S(1)} %pad_maximum_fusion.3), channel_id=1, source_target_pairs={{1,0},{2,1},{3,2},{4,3},{5,4},{6,5},{7,6},{8,7},{9,8},{10,9},{11,1... | collective-permute-start | bytes 3145736 | tf_op jit(solution)/shard_map/ppermute | solution.py:62
  189.6 6.3 %all-to-all-start.1 = ((bf16[1,128,16,64]{1,3,0,2:T(8,128)(2,1)}), bf16[1,128,16,64]{1,3,0,2:T(8,128)(2,1)S(1)}, u32[]{:S(2)}, u32[]{:S(2)}) async-start(bf16[1,128,16,64]{1,3,0,2:T(8,128)(2,1)} %bitcast.35), calls=%async_computation.1 | async-start | bytes 524288 | tf_op jit(solution)/shard_map/all_to_all | solution.py:205
  196.4 1.2 collective-permute-start.18
  197.7 3.7 %convolution_convert_fusion = bf16[128,2048]{1,0:T(8,128)(2,1)} fusion(bf16[128,1024]{1,0:T(8,128)(2,1)S(1)} %copy-done.10, bf16[1024,2048]{1,0:T(8,128)(2,1)} %all-gather.5.cloned.1.call-done), kind=kOutput, calls=%fused_computation | convolution fusion | flops 537133056 | bytes 4980736 | tf_op jit(solution)/shard_map/dot_general | solution.py:202
  201.4 16.8 %all-to-all-done.1 = bf16[1,128,16,64]{1,3,0,2:T(8,128)(2,1)S(1)} async-done(((bf16[1,128,16,64]{1,3,0,2:T(8,128)(2,1)}), bf16[1,128,16,64]{1,3,0,2:T(8,128)(2,1)S(1)}, u32[]{:S(2)}, u32[]{:S(2)}) %all-to-all-start.1) | async-done | bytes 262176 | tf_op jit(solution)/shard_map/all_to_all | solution.py:205
  218.9 3.3 %collective-permute-start.19 = (bf16[8,32768]{1,0:T(8,128)(2,1)S(1)}, bf16[8,32768]{1,0:T(8,128)(2,1)S(1)}, u32[]{:S(2)}, u32[]{:S(2)}) collective-permute-start(bf16[8,32768]{1,0:T(8,128)(2,1)S(1)} %maximum_select_fusion.3), channel_id=1, source_target_pairs={{0,1},{1,0},{2,3},{3,2},{4,5},{5,4},{6,7},{7,6},{8,9},{9,8},{10,11... | collective-permute-start | bytes 1572872 | tf_op jit(solution)/shard_map/ppermute | solution.py:25
  222.1 5.7 %fusion.16 = f32[64,2048]{1,0:T(8,128)} fusion(bf16[2048,2048]{1,0:T(8,128)(2,1)} %all-gather.3.cloned.1.call-done, bf16[8,8,16,128]{3,2,1,0:T(8,128)(2,1)S(1)} %bitcast.116), kind=kOutput, calls=%fused_computation.50 | convolution fusion | flops 536870912 | bytes 9175040 | tf_op jit(solution)/shard_map/dot_general | solution.py:208
  228.6 2.8 %fusion.15 = (bf16[128,1024]{1,0:T(8,128)(2,1)}, bf16[128,1024]{1,0:T(8,128)(2,1)}) fusion(f32[1,384,1024]{2,1,0:T(8,128)} %copy-done, bf16[2,256,1024]{2,1,0:T(8,128)(2,1)S(1)} %select_n.248, bf16[2,256,1024]{2,1,0:T(8,128)(2,1)} %collective-permute-done.11, bf16[2,256,1024]{2,1,0:T(8,128)(2,1)} %collective-permute-done.10, pred[]{:T(512)S(6)} %eq.38, ...), kind=kLoop, calls=%fused_computation.49 | loop fusion | flops 2883584 | bytes 3670018 | tf_op jit(solution)/shard_map/convert_element_type | solution.py:227
  (106 shorter events, 16.4 us)
Async XLA Ops:
  7.2 93.2 %all-gather.3.cloned.1.call-start = ((), (), s32[]{:S(2)}) async-start(), calls=%async_computation.2 | async-start | bytes 8912896 | tf_op jit(solution)/shard_map/all_gather | solution.py:131
  7.9 189.8 %all-gather.5.cloned.1.call-start = ((), (), s32[]{:S(2)}) async-start(), calls=%async_computation.3 | async-start | bytes 4456448 | tf_op jit(solution)/shard_map/all_gather | solution.py:132
  9.8 15.9 %collective-permute-start = (bf16[2,128,1024]{2,1,0:T(8,128)(2,1)}, bf16[2,128,1024]{2,1,0:T(8,128)(2,1)S(1)}, u32[]{:S(2)}, u32[]{:S(2)}) collective-permute-start(bf16[2,128,1024]{2,1,0:T(8,128)(2,1)} %pad_maximum_fusion.4), channel_id=1, source_target_pairs={{0,1},{1,2},{2,3},{3,4},{4,5},{5,6},{6,7},{7,8},{8,9},{9,10},{10,1... | collective-permute-start | bytes 1572872 | tf_op jit(solution)/shard_map/ppermute | solution.py:61
  13.5 22.3 %collective-permute-start.1 = (bf16[2,128,1024]{2,1,0:T(8,128)(2,1)}, bf16[2,128,1024]{2,1,0:T(8,128)(2,1)S(1)}, u32[]{:S(2)}, u32[]{:S(2)}) collective-permute-start(bf16[2,128,1024]{2,1,0:T(8,128)(2,1)} %pad_maximum_fusion.4), channel_id=1, source_target_pairs={{1,0},{2,1},{3,2},{4,3},{5,4},{6,5},{7,6},{8,7},{9,8},{10,9},{11,1... | collective-permute-start | bytes 1572872 | tf_op jit(solution)/shard_map/ppermute | solution.py:62
  19.3 3.0 %copy-start.12 = (s32[1,3]{1,0:T(1,128)S(1)}, s32[1,3]{1,0:T(1,128)}, u32[]{:S(2)}) copy-start(s32[1,3]{1,0:T(1,128)} %param.14) | copy-start | bytes 40
  19.3 5.6 %copy-start.13 = (s32[3]{0:T(128)S(1)}, s32[3]{0:T(128)}, u32[]{:S(2)}) copy-start(s32[3]{0:T(128)} %constant.91.clone) | copy-start | bytes 40
  19.9 16.0 %copy-start.5 = (bf16[128,1024]{1,0:T(8,128)(2,1)S(1)}, bf16[128,1024]{1,0:T(8,128)(2,1)}, u32[]{:S(2)}) copy-start(bf16[128,1024]{1,0:T(8,128)(2,1)} %param.10) | copy-start | bytes 786436
  19.9 15.9 %copy-start.6 = (bf16[128,1024]{1,0:T(8,128)(2,1)S(1)}, bf16[128,1024]{1,0:T(8,128)(2,1)}, u32[]{:S(2)}) copy-start(bf16[128,1024]{1,0:T(8,128)(2,1)} %param.9) | copy-start | bytes 786436
  20.8 4.3 %collective-permute-start.2 = (bf16[8,32768]{1,0:T(8,128)(2,1)}, bf16[8,32768]{1,0:T(8,128)(2,1)S(1)}, u32[]{:S(2)}, u32[]{:S(2)}) collective-permute-start(bf16[8,32768]{1,0:T(8,128)(2,1)} %constant_dynamic-slice_fusion.3), channel_id=1, source_target_pairs={{0,1},{1,0},{2,3},{3,2},{4,5},{5,4},{6,7},{7,6},{8,9},{9,8},{10,11... | collective-permute-start | bytes 1572872 | tf_op jit(solution)/shard_map/ppermute | solution.py:25
  25.3 11.3 %collective-permute-start.3 = (bf16[4,32768]{1,0:T(4,128)(2,1)S(1)}, bf16[4,32768]{1,0:T(4,128)(2,1)S(1)}, u32[]{:S(2)}, u32[]{:S(2)}) collective-permute-start(bf16[4,32768]{1,0:T(4,128)(2,1)S(1)} %constant_dynamic-slice_fusion.2), channel_id=1, source_target_pairs={{0,2},{2,0},{4,6},{6,4},{8,10},{10,8},{12,14},{14,12},{1,3},{3,1},... | collective-permute-start | bytes 786440 | tf_op jit(solution)/shard_map/ppermute | solution.py:28
  37.0 5.9 %collective-permute-start.4 = (bf16[2,32768]{1,0:T(2,128)(2,1)S(1)}, bf16[2,32768]{1,0:T(2,128)(2,1)S(1)}, u32[]{:S(2)}, u32[]{:S(2)}) collective-permute-start(bf16[2,32768]{1,0:T(2,128)(2,1)S(1)} %constant_dynamic-slice_fusion.1), channel_id=1, source_target_pairs={{0,4},{2,6},{4,0},{6,2},{8,12},{10,14},{12,8},{14,10},{1,5},{3,7},... | collective-permute-start | bytes 393224 | tf_op jit(solution)/shard_map/ppermute | solution.py:28
  43.2 4.8 %collective-permute-start.5 = (bf16[1,32768]{1,0:T(2,128)(2,1)S(1)}, bf16[1,32768]{1,0:T(2,128)(2,1)S(1)}, u32[]{:S(2)}, u32[]{:S(2)}) collective-permute-start(bf16[1,32768]{1,0:T(2,128)(2,1)S(1)} %constant_dynamic-slice_fusion), channel_id=1, source_target_pairs={{0,8},{2,10},{4,12},{6,14},{8,0},{10,2},{12,4},{14,6},{1,9},{3,11}... | collective-permute-start | bytes 196616 | tf_op jit(solution)/shard_map/ppermute | solution.py:28
  48.2 4.9 %collective-permute-start.6 = (bf16[1,32768]{1,0:T(2,128)(2,1)S(1)}, bf16[1,32768]{1,0:T(2,128)(2,1)S(1)}, u32[]{:S(2)}, u32[]{:S(2)}) collective-permute-start(bf16[1,32768]{1,0:T(2,128)(2,1)S(1)} %dynamic-slice_add_fusion.2), channel_id=1, source_target_pairs={{0,8},{2,10},{4,12},{6,14},{8,0},{10,2},{12,4},{14,6},{1,9},{3,11}... | collective-permute-start | bytes 196616 | tf_op jit(solution)/shard_map/ppermute | solution.py:28
  53.7 46.7 %copy-start.9 = (bf16[64,2048]{1,0:T(8,128)(2,1)S(1)}, bf16[64,2048]{1,0:T(8,128)(2,1)}, u32[]{:S(2)}) copy-start(bf16[64,2048]{1,0:T(8,128)(2,1)} %param.11) | copy-start | bytes 786436
  53.7 28.9 %collective-permute-start.7 = (bf16[2,32768]{1,0:T(2,128)(2,1)S(1)}, bf16[2,32768]{1,0:T(2,128)(2,1)S(1)}, u32[]{:S(2)}, u32[]{:S(2)}) collective-permute-start(bf16[2,32768]{1,0:T(2,128)(2,1)S(1)} %broadcast_select_fusion.3), channel_id=1, source_target_pairs={{0,4},{2,6},{4,0},{6,2},{8,12},{10,14},{12,8},{14,10},{1,5},{3,7},... | collective-permute-start | bytes 393224 | tf_op jit(solution)/shard_map/ppermute | solution.py:28
  83.1 13.8 %collective-permute-start.8 = (bf16[4,32768]{1,0:T(4,128)(2,1)S(1)}, bf16[4,32768]{1,0:T(4,128)(2,1)S(1)}, u32[]{:S(2)}, u32[]{:S(2)}) collective-permute-start(bf16[4,32768]{1,0:T(4,128)(2,1)S(1)} %maximum_select_fusion.4), channel_id=1, source_target_pairs={{0,2},{2,0},{4,6},{6,4},{8,10},{10,8},{12,14},{14,12},{1,3},{3,1},... | collective-permute-start | bytes 786440 | tf_op jit(solution)/shard_map/ppermute | solution.py:28
  92.6 4.2 %copy-start.8 = (bf16[1024,1024]{1,0:T(8,128)(2,1)}, bf16[1024,1024]{1,0:T(8,128)(2,1)S(1)}, u32[]{:S(2)}) copy-start(bf16[1024,1024]{1,0:T(8,128)(2,1)S(1)} %bitcast_dynamic-update-slice_fusion.5) | copy-start | bytes 6291460
  92.7 1.4 copy-start.7
  97.3 18.6 %collective-permute-start.9 = (bf16[8,32768]{1,0:T(8,128)(2,1)S(1)}, bf16[8,32768]{1,0:T(8,128)(2,1)S(1)}, u32[]{:S(2)}, u32[]{:S(2)}) collective-permute-start(bf16[8,32768]{1,0:T(8,128)(2,1)S(1)} %maximum_select_fusion.2), channel_id=1, source_target_pairs={{0,1},{1,0},{2,3},{3,2},{4,5},{5,4},{6,7},{7,6},{8,9},{9,8},{10,11... | collective-permute-start | bytes 1572872 | tf_op jit(solution)/shard_map/ppermute | solution.py:25
  107.2 21.9 %all-to-all-start = ((bf16[16,128,64]{1,2,0:T(8,128)(2,1)}), bf16[16,128,64]{1,2,0:T(8,128)(2,1)S(1)}, u32[]{:S(2)}, u32[]{:S(2)}) async-start(bf16[16,128,64]{1,2,0:T(8,128)(2,1)} %bitcast.107), calls=%async_computation | async-start | bytes 524288 | tf_op jit(solution)/shard_map/all_to_all | solution.py:165
  130.5 11.7 %copy-start.11 = (pred[384]{0:T(512)(128)(4,1)S(1)}, pred[384]{0:T(512)(128)(4,1)}, u32[]{:S(2)}) copy-start(pred[384]{0:T(512)(128)(4,1)} %constant.113) | copy-start | bytes 1156
  142.2 2.9 %copy-start.4 = (f32[768,1024]{1,0:T(8,128)S(1)}, f32[768,1024]{1,0:T(8,128)}, u32[]{:S(2)}) copy-start(f32[768,1024]{1,0:T(8,128)} %get-tuple-element.12) | copy-start | bytes 9437188
  148.4 4.5 %copy-start.2 = (f32[16,32768]{1,0:T(8,128)S(1)}, f32[16,32768]{1,0:T(8,128)}, u32[]{:S(2)}) copy-start(f32[16,32768]{1,0:T(8,128)} %reshape.176) | copy-start | bytes 6291460
  149.9 3.0 %collective-permute-start.12 = (bf16[8,32768]{1,0:T(8,128)(2,1)S(1)}, bf16[8,32768]{1,0:T(8,128)(2,1)S(1)}, u32[]{:S(2)}, u32[]{:S(2)}) collective-permute-start(bf16[8,32768]{1,0:T(8,128)(2,1)S(1)} %dynamic-slice_convert_fusion), channel_id=1, source_target_pairs={{0,1},{1,0},{2,3},{3,2},{4,5},{5,4},{6,7},{7,6},{8,9},{9,8},{10,11... | collective-permute-start | bytes 1572872 | tf_op jit(solution)/shard_map/ppermute | solution.py:25
  151.5 2.8 %copy-start.3 = (f32[768,1024]{1,0:T(8,128)S(1)}, f32[768,1024]{1,0:T(8,128)}, u32[]{:S(2)}) copy-start(f32[768,1024]{1,0:T(8,128)} %get-tuple-element.13) | copy-start | bytes 9437188
  153.1 8.0 %collective-permute-start.13 = (bf16[4,32768]{1,0:T(4,128)(2,1)S(1)}, bf16[4,32768]{1,0:T(4,128)(2,1)S(1)}, u32[]{:S(2)}, u32[]{:S(2)}) collective-permute-start(bf16[4,32768]{1,0:T(4,128)(2,1)S(1)} %dynamic-slice_convert_fusion.1), channel_id=1, source_target_pairs={{0,2},{2,0},{4,6},{6,4},{8,10},{10,8},{12,14},{14,12},{1,3},{3,1},... | collective-permute-start | bytes 786440 | tf_op jit(solution)/shard_map/ppermute | solution.py:28
  161.4 4.2 %collective-permute-start.14 = (bf16[2,32768]{1,0:T(2,128)(2,1)S(1)}, bf16[2,32768]{1,0:T(2,128)(2,1)S(1)}, u32[]{:S(2)}, u32[]{:S(2)}) collective-permute-start(bf16[2,32768]{1,0:T(2,128)(2,1)S(1)} %dynamic-slice_convert_fusion.2), channel_id=1, source_target_pairs={{0,4},{2,6},{4,0},{6,2},{8,12},{10,14},{12,8},{14,10},{1,5},{3,7},... | collective-permute-start | bytes 393224 | tf_op jit(solution)/shard_map/ppermute | solution.py:28
  163.0 12.6 %copy-start.1 = (f32[1,384,1024]{2,1,0:T(8,128)}, f32[1,384,1024]{2,1,0:T(8,128)S(1)}, u32[]{:S(2)}) copy-start(f32[1,384,1024]{2,1,0:T(8,128)S(1)} %bitcast_dynamic-update-slice_fusion.1) | copy-start | bytes 4718596
  165.9 4.9 %collective-permute-start.15 = (bf16[1,32768]{1,0:T(2,128)(2,1)S(1)}, bf16[1,32768]{1,0:T(2,128)(2,1)S(1)}, u32[]{:S(2)}, u32[]{:S(2)}) collective-permute-start(bf16[1,32768]{1,0:T(2,128)(2,1)S(1)} %dynamic-slice_convert_fusion.3), channel_id=1, source_target_pairs={{0,8},{2,10},{4,12},{6,14},{8,0},{10,2},{12,4},{14,6},{1,9},{3,11}... | collective-permute-start | bytes 196616 | tf_op jit(solution)/shard_map/ppermute | solution.py:28
  167.1 8.5 %copy-start = (f32[1,384,1024]{2,1,0:T(8,128)}, f32[1,384,1024]{2,1,0:T(8,128)S(1)}, u32[]{:S(2)}) copy-start(f32[1,384,1024]{2,1,0:T(8,128)S(1)} %bitcast_dynamic-update-slice_fusion) | copy-start | bytes 4718596
  171.0 10.1 %collective-permute-start.16 = (bf16[1,32768]{1,0:T(2,128)(2,1)S(1)}, bf16[1,32768]{1,0:T(2,128)(2,1)S(1)}, u32[]{:S(2)}, u32[]{:S(2)}) collective-permute-start(bf16[1,32768]{1,0:T(2,128)(2,1)S(1)} %add_convert_fusion), channel_id=1, source_target_pairs={{0,8},{2,10},{4,12},{6,14},{8,0},{10,2},{12,4},{14,6},{1,9},{3,11}... | collective-permute-start | bytes 196616 | tf_op jit(solution)/shard_map/ppermute | solution.py:28
  175.6 13.1 %copy-start.10 = (bf16[128,1024]{1,0:T(8,128)(2,1)S(1)}, bf16[128,1024]{1,0:T(8,128)(2,1)}, u32[]{:S(2)}) copy-start(bf16[128,1024]{1,0:T(8,128)(2,1)} %get-tuple-element.10) | copy-start | bytes 786436
  181.7 14.3 %collective-permute-start.17 = (bf16[2,32768]{1,0:T(2,128)(2,1)S(1)}, bf16[2,32768]{1,0:T(2,128)(2,1)S(1)}, u32[]{:S(2)}, u32[]{:S(2)}) collective-permute-start(bf16[2,32768]{1,0:T(2,128)(2,1)S(1)} %broadcast_select_fusion.2), channel_id=1, source_target_pairs={{0,4},{2,6},{4,0},{6,2},{8,12},{10,14},{12,8},{14,10},{1,5},{3,7},... | collective-permute-start | bytes 393224 | tf_op jit(solution)/shard_map/ppermute | solution.py:28
  184.0 44.5 %collective-permute-start.10 = (bf16[2,256,1024]{2,1,0:T(8,128)(2,1)S(1)}, bf16[2,256,1024]{2,1,0:T(8,128)(2,1)}, u32[]{:S(2)}, u32[]{:S(2)}) collective-permute-start(bf16[2,256,1024]{2,1,0:T(8,128)(2,1)S(1)} %pad_maximum_fusion.3), channel_id=1, source_target_pairs={{0,1},{1,2},{2,3},{3,4},{4,5},{5,6},{6,7},{7,8},{8,9},{9,10},{10,1... | collective-permute-start | bytes 3145736 | tf_op jit(solution)/shard_map/ppermute | solution.py:61
  186.2 42.4 %collective-permute-start.11 = (bf16[2,256,1024]{2,1,0:T(8,128)(2,1)S(1)}, bf16[2,256,1024]{2,1,0:T(8,128)(2,1)}, u32[]{:S(2)}, u32[]{:S(2)}) collective-permute-start(bf16[2,256,1024]{2,1,0:T(8,128)(2,1)S(1)} %pad_maximum_fusion.3), channel_id=1, source_target_pairs={{1,0},{2,1},{3,2},{4,3},{5,4},{6,5},{7,6},{8,7},{9,8},{10,9},{11,1... | collective-permute-start | bytes 3145736 | tf_op jit(solution)/shard_map/ppermute | solution.py:62
  189.6 28.6 %all-to-all-start.1 = ((bf16[1,128,16,64]{1,3,0,2:T(8,128)(2,1)}), bf16[1,128,16,64]{1,3,0,2:T(8,128)(2,1)S(1)}, u32[]{:S(2)}, u32[]{:S(2)}) async-start(bf16[1,128,16,64]{1,3,0,2:T(8,128)(2,1)} %bitcast.35), calls=%async_computation.1 | async-start | bytes 524288 | tf_op jit(solution)/shard_map/all_to_all | solution.py:205
  196.4 22.0 %collective-permute-start.18 = (bf16[4,32768]{1,0:T(4,128)(2,1)S(1)}, bf16[4,32768]{1,0:T(4,128)(2,1)S(1)}, u32[]{:S(2)}, u32[]{:S(2)}) collective-permute-start(bf16[4,32768]{1,0:T(4,128)(2,1)S(1)} %maximum_select_fusion.5), channel_id=1, source_target_pairs={{0,2},{2,0},{4,6},{6,4},{8,10},{10,8},{12,14},{14,12},{1,3},{3,1},... | collective-permute-start | bytes 786440 | tf_op jit(solution)/shard_map/ppermute | solution.py:28
  218.9 9.0 %collective-permute-start.19 = (bf16[8,32768]{1,0:T(8,128)(2,1)S(1)}, bf16[8,32768]{1,0:T(8,128)(2,1)S(1)}, u32[]{:S(2)}, u32[]{:S(2)}) collective-permute-start(bf16[8,32768]{1,0:T(8,128)(2,1)S(1)} %maximum_select_fusion.3), channel_id=1, source_target_pairs={{0,1},{1,0},{2,3},{3,2},{4,5},{5,4},{6,7},{7,6},{8,9},{9,8},{10,11... | collective-permute-start | bytes 1572872 | tf_op jit(solution)/shard_map/ppermute | solution.py:25
Sparse Core Ops, SparseCore 0:
  10.2 86.0 all-gather.2
  98.4 59.9 all-gather.4
